TPU v7x, 32 devices: a whole 2x2x4 slice. The times are simulated.
32 devices in a mesh: gx: 8 (over y, x, core), gy: 4 (over z).
Axes of the slice: x: 2, y: 2, z: 4, core: 2. Of those that a mesh axis runs over, the one named last changes fastest.
Arguments:
- coords: float32 [8, 65536], P(None, ('gx', 'gy')), may hold values from -6 to 6
- inv_scale: float32 [8], replicated, may hold values from 0.3 to 0.8
- noise: float32 [65536], P(('gx', 'gy')), may hold values from 0.3 to 1
- right_side: float32 [16, 65536], P(None, ('gx', 'gy')), may hold values from -20 to 20
- basis: float32 [128, 65536], P(None, ('gx', 'gy')), may hold values from -0.125 to 0.125
- level_gain: float32 [5, 65536], P(None, ('gx', 'gy')), may hold values from 0.5 to 2
- coupling: float32 [5, 128, 128], replicated, may hold values from -0.5 to 0.5
- order: int32 [32, 2048], P(('gx', 'gy')), may hold values from 0 to 2047, each once within a row
- pairs: int32 [32, 2, 4], P(('gx', 'gy')), may hold values from 0 to 7
Outputs:
- solution: float32 [16, 65536], P(None, ('gx', 'gy'))
- residual: float32 [16, 65536], P(None, ('gx', 'gy'))
Inputs may be any that keep to these rules, and one draw needn't show every extreme that they name: Each row of order is a permutation of 0 .. 2047. `pairs`: every entry names a tile of its own leaf.
All inputs are finite; a program needn't handle non-finite values.
Results may differ from a plain program's by a relative error of at most 0.0003.
Values sent between devices are 32-bit elements; how exact they have to be, the bound alone decides.
No kernel may reach another device: no remote copies, remote signals or barrier semaphores. Data moves between devices by JAX's collectives and lax.ppermute only.
A program may use at most 64 MiB of HBM per device.

v0:
```python
import math

import jax
import jax.numpy as jnp
from jax import lax
from jax.sharding import PartitionSpec as P

TILE_POINTS = 256
ITERATIONS = 2


near_weight = 0.25
highest = lax.Precision.HIGHEST


def swapped(value, axis, bit):
    mask = 2**bit
    pairs = [(source, source ^ mask) for source in range(lax.axis_size(axis))]
    return lax.ppermute(value, axis, pairs)


def tile_near(tile_coords, tile_vec, pair_rows, pair_cols):
    width = tile_coords.shape[2]
    union = jnp.concatenate([tile_coords[:, pair_rows], tile_coords[:, pair_cols]], axis=2)
    gram = jnp.einsum("fgi,fgj->gij", union, union, precision=highest)
    square = jnp.sum(union * union, axis=0)
    dist = square[:, :, None] + square[:, None, :] - 2.0 * gram
    kern = near_weight * jnp.exp(-0.5 * dist)
    union_vec = jnp.concatenate([tile_vec[:, pair_rows], tile_vec[:, pair_cols]], axis=2)
    result = jnp.einsum("gij,cgj->cgi", kern, union_vec, precision=highest)
    tile_ids = jnp.arange(tile_coords.shape[1], dtype=jnp.int32)
    row_hot = (pair_rows[:, None] == tile_ids[None, :]).astype(jnp.float32)
    col_hot = (pair_cols[:, None] == tile_ids[None, :]).astype(jnp.float32)
    added = jnp.einsum("cgi,gt->cti", result[:, :, :width], row_hot, precision=highest)
    return added + jnp.einsum("cgi,gt->cti", result[:, :, width:], col_hot, precision=highest)


def near_field(tile_coords, tile_vec, pair_rows, pair_cols):
    group = math.gcd(pair_rows.shape[0], 4)
    rows = pair_rows.reshape(-1, group)
    cols = pair_cols.reshape(-1, group)

    def accumulate(total, picked):
        return (total + tile_near(tile_coords, tile_vec, picked[0], picked[1]), None)

    total, unused = lax.scan(accumulate, jnp.zeros(tile_vec.shape, jnp.float32), (rows, cols))
    return total


def tree_sums(proj):
    low_count = lax.axis_size("gy").bit_length() - 1
    high_count = lax.axis_size("gx").bit_length() - 1
    running = proj
    for bit in range(low_count):
        partner = swapped(running[bit:], "gy", bit)
        running = jnp.concatenate([running[:bit], running[bit:] + partner], axis=0)
    for bit in range(high_count):
        level = low_count + bit
        partner = swapped(running[level:], "gx", bit)
        running = jnp.concatenate([running[:level], running[level:] + partner], axis=0)
    return running


def per_device(coords, inv_scale, noise, right_side, basis, level_gain, coupling, order, pairs):
    perm = order[0]
    points = right_side.shape[1]
    columns = right_side.shape[0]
    tiles = points // TILE_POINTS
    levels = level_gain.shape[0]
    tile_coords = (coords * inv_scale[:, None])[:, perm].reshape(
        coords.shape[0], tiles, TILE_POINTS
    )
    noise_t = noise[perm]
    gain_t = level_gain[:, perm]
    basis_t = basis[:, perm]
    rhs_t = right_side[:, perm]
    pair_rows = pairs[0, 0]
    pair_cols = pairs[0, 1]
    scales = 2.0 ** ((1.0 - jnp.arange(levels, dtype=jnp.float32)) / 2.0)
    solution = jnp.zeros_like(rhs_t)
    residual = rhs_t
    direction = rhs_t

    def squares(values):
        return lax.psum(jnp.sum(values * values, axis=1), ("gx", "gy"))

    norm_now = squares(residual)
    for step in range(ITERATIONS):
        proj = jnp.einsum("lp,cp,rp->lcr", gain_t, direction, basis_t, precision=highest)
        nodesum = tree_sums(proj)
        coupled = jnp.einsum("lcr,lrs->lcs", nodesum, coupling, precision=highest)
        coupled = (
            jnp.einsum("lcs,lrs->lcr", coupled, coupling, precision=highest) * scales[:, None, None]
        )
        back = jnp.einsum("lcr,rp->lcp", coupled, basis_t, precision=highest)
        far = jnp.sum(back * gain_t[:, None, :], axis=0)
        near = near_field(
            tile_coords, direction.reshape(columns, tiles, TILE_POINTS), pair_rows, pair_cols
        )
        image = noise_t[None, :] * direction + far + near.reshape(columns, points)
        curve = lax.psum(jnp.sum(direction * image, axis=1), ("gx", "gy"))
        alpha = norm_now / curve
        solution = solution + alpha[:, None] * direction
        residual = residual - alpha[:, None] * image
        if step + 1 < ITERATIONS:
            norm_next = squares(residual)
            direction = residual + (norm_next / norm_now)[:, None] * direction
            norm_now = norm_next
    inverse = jnp.zeros_like(perm).at[perm].set(jnp.arange(points, dtype=jnp.int32))
    return (solution[:, inverse], residual[:, inverse])


def solution(mesh):
    return jax.shard_map(
        per_device,
        mesh=mesh,
        in_specs=(
            P(None, ("gx", "gy")),
            P(),
            P(("gx", "gy")),
            P(None, ("gx", "gy")),
            P(None, ("gx", "gy")),
            P(None, ("gx", "gy")),
            P(),
            P(("gx", "gy"), None),
            P(("gx", "gy"), None, None),
        ),
        out_specs=(P(None, ("gx", "gy")), P(None, ("gx", "gy"))),
        check_vma=False,
    )
```

profile of v0, /device:TPU:0, one launch (start us, length us, event | category | flops | bytes accessed | tf_op | source)
XLA Modules:
  0.0 244.1 jit_solution(13138407150953133568)
XLA Ops:
  0.6 0.8 compare_select_fusion
  1.4 1.2 copy.84
  2.7 5.5 %gather_fusion = f32[2048,16]{1,0:T(8,128)S(1)} fusion(f32[16,2048]{0,1:T(8,128)S(1)} %copy.84, s32[2048]{0:T(1024)S(1)} %broadcast_clamp_fusion), kind=kCustom, calls=%fused_computation | custom fusion | bytes 270336 | tf_op jit(solution)/shard_map/gather | solution.py:76
  8.4 1.6 copy.89
  10.0 5.5 %gather_fusion.3 = f32[2048,128]{1,0:T(8,128)S(1)} fusion(f32[128,2048]{0,1:T(8,128)S(1)} %copy.89, s32[2048]{0:T(1024)S(1)} %broadcast_clamp_fusion), kind=kCustom, calls=%fused_computation.3 | custom fusion | bytes 2105344 | tf_op jit(solution)/shard_map/gather | solution.py:75
  15.5 1.4 copy.87
  16.9 6.7 %gather_fusion.2 = f32[2048,5]{1,0:T(8,128)S(1)} fusion(f32[5,2048]{0,1:T(8,128)} %copy.87, s32[2048]{0:T(1024)S(1)} %broadcast_clamp_fusion), kind=kCustom, calls=%fused_computation.2 | custom fusion | bytes 90112 | tf_op jit(solution)/shard_map/gather | solution.py:74
  23.9 0.9 convolution_bitcast_fusion.1
  24.8 3.1 %collective-permute-start = (f32[5,16,128]{2,1,0:T(8,128)S(1)}, f32[5,16,128]{2,1,0:T(8,128)S(1)}, u32[]{:S(2)}, u32[]{:S(2)}) collective-permute-start(f32[5,16,128]{2,1,0:T(8,128)S(1)} %convolution_bitcast_fusion.1), channel_id=1, source_target_pairs={{0,1},{1,0},{2,3},{3,2},{4,5},{5,4},{6,7},{7,6},{8,9},{9,8},{10,11... | collective-permute-start | bytes 122888 | tf_op jit(solution)/shard_map/ppermute | solution.py:19
  28.0 1.3 copy.93
  29.3 8.8 %gather_fusion.6 = f32[2048,8]{1,0:T(8,128)} fusion(f32[8,2048]{0,1:T(8,128)} %copy.93, s32[2048]{0:T(1024)S(1)} %broadcast_clamp_fusion), kind=kCustom, calls=%fused_computation.6 | custom fusion | bytes 139264 | tf_op jit(solution)/shard_map/gather | solution.py:70
  38.1 1.5 copy.94
  39.6 0.6 gather_fusion.8
  40.8 0.6 gather_fusion.5
  41.3 0.6 gather_fusion.4
  41.9 3.5 %fusion.52 = f32[4,512,512]{2,1,0:T(8,128)S(1)} fusion(f32[8,4,256]{2,0,1:T(8,128)S(1)} %bitcast.181, f32[8,4,256]{2,0,1:T(8,128)S(1)} %bitcast.183), kind=kOutput, calls=%fused_computation.91 | convolution fusion | flops 100679680 | bytes 4259840 | tf_op jit(solution)/shard_map/while/body/eval_jaxpr/fgi,fgj->gij/dot_general | solution.py:25
  45.4 1.9 copy-done.2
  47.3 4.4 %fusion.14 = f32[16,4,512]{2,0,1:T(8,128)S(1)} fusion(f32[4,512,512]{2,1,0:T(8,128)S(1)} %fusion.52, f32[4,512]{1,0:T(4,128)S(1)} %multiply_reduce_fusion.1, f32[16,4,256]{2,0,1:T(8,128)S(1)} %bitcast.186, f32[16,4,256]{2,0,1:T(8,128)S(1)} %bitcast.187), kind=kOutput, calls=%fused_computation.33 | convolution fusion | flops 206602240 | bytes 4464640 | tf_op jit(solution)/shard_map/while/body/eval_jaxpr/gij,cgj->cgi/dot_general | solution.py:30
  51.8 2.6 %collective-permute-start.1 = (f32[4,16,128]{2,1,0:T(8,128)S(1)}, f32[4,16,128]{2,1,0:T(8,128)S(1)}, u32[]{:S(2)}, u32[]{:S(2)}) collective-permute-start(f32[4,16,128]{2,1,0:T(8,128)S(1)} %slice.127), channel_id=1, source_target_pairs={{0,2},{1,3},{2,0},{3,1},{4,6},{5,7},{6,4},{7,5},{8,10},{9,11},{10,... | collective-permute-start | bytes 98312 | tf_op jit(solution)/shard_map/ppermute | solution.py:19
  54.8 1.9 collective-permute-done.1
  56.9 1.1 collective-permute-done.2
  58.0 1.8 collective-permute-start.3
  59.8 11.8 %gather_fusion.1 = f32[2048]{0:T(1024)S(1)} fusion(f32[2048]{0:T(1024)S(1)} %copy-done.1, s32[2048]{0:T(1024)S(1)} %broadcast_clamp_fusion), kind=kCustom, calls=%fused_computation.1 | custom fusion | bytes 24576 | tf_op jit(solution)/shard_map/gather | solution.py:73
  71.9 8.2 %scatter_custom_fusion = s32[2048]{0:T(1024)S(1)} fusion(s32[2048]{0:T(1024)S(1)} %bitcast.189, s32[2048]{0:T(1024)S(1)} %iota.18, s32[]{:T(128)} %constant.28.clone.1), kind=kCustom, calls=%fused_computation.124 | custom fusion | bytes 8196 | tf_op jit(solution)/shard_map/scatter | solution.py:109
  80.2 1.6 collective-permute-start.4
  81.8 2.1 collective-permute-done.4
  84.3 0.6 convolution_multiply_fusion.3
  84.9 1.3 fusion.12
  86.8 39.3 %all-reduce = (f32[16]{0:T(128)S(1)}, f32[16]{0:T(128)S(1)}) all-reduce(f32[16]{0:T(128)S(1)} %fusion.41, f32[16]{0:T(128)S(1)} %get-tuple-element.58), channel_id=1, replica_groups=mesh['gx'=8,'gy'=4] {'gx','gy'}, use_global_device_ids=true, to_apply=%region_1.0 | all-reduce | flops 32 | bytes 256 | tf_op jit(solution)/shard_map/psum | solution.py:85
  126.3 40.1 %psum.30 = f32[16]{0:T(128)S(1)} all-reduce(f32[16]{0:T(128)S(1)} %multiply_reduce_fusion), channel_id=1, replica_groups=mesh['gx'=8,'gy'=4] {'gx','gy'}, use_global_device_ids=true, to_apply=%region_7.8 | all-reduce | flops 16 | bytes 128 | tf_op jit(solution)/shard_map/psum | solution.py:85
  166.6 0.9 convolution_bitcast_fusion
  167.4 1.6 collective-permute-start.5
  169.2 0.6 gather_fusion.10
  170.3 1.2 collective-permute-done.5
  171.5 2.4 collective-permute-start.6
  173.9 6.0 %fusion.15 = f32[16,4,512]{2,0,1:T(8,128)S(1)} fusion(f32[4,512,512]{2,1,0:T(8,128)} %copy-done.2, f32[4,512]{1,0:T(4,128)S(1)} %multiply_reduce_fusion.1, f32[16,4,256]{2,0,1:T(8,128)S(1)} %bitcast.184, f32[16,4,256]{2,0,1:T(8,128)S(1)} %bitcast.185), kind=kOutput, calls=%fused_computation.34 | convolution fusion | flops 206602240 | bytes 4464640 | tf_op jit(solution)/shard_map/while/body/eval_jaxpr/gij,cgj->cgi/dot_general | solution.py:30
  180.0 1.2 collective-permute-done.7
  181.2 2.7 %collective-permute-start.8 = (f32[2,16,128]{2,1,0:T(8,128)S(1)}, f32[2,16,128]{2,1,0:T(8,128)S(1)}, u32[]{:S(2)}, u32[]{:S(2)}) collective-permute-start(f32[2,16,128]{2,1,0:T(8,128)S(1)} %slice.136), channel_id=1, source_target_pairs={{0,8},{4,12},{8,0},{12,4},{16,24},{20,28},{24,16},{28,20},{1,9},{5... | collective-permute-start | bytes 49160 | tf_op jit(solution)/shard_map/ppermute | solution.py:19
  184.2 1.4 collective-permute-done.8
  185.6 2.0 collective-permute-start.9
  187.6 1.6 collective-permute-done.9
  189.6 0.6 convolution_multiply_fusion.2
  190.3 1.3 fusion.13
  192.1 38.3 %psum.31 = f32[16]{0:T(128)S(1)} all-reduce(f32[16]{0:T(128)S(1)} %get-tuple-element.60), channel_id=1, replica_groups=mesh['gx'=8,'gy'=4] {'gx','gy'}, use_global_device_ids=true, to_apply=%region_10.11 | all-reduce | flops 16 | bytes 128 | tf_op jit(solution)/shard_map/psum | solution.py:101
  230.9 5.5 %gather_fusion.12 = f32[2048,16]{1,0:T(8,128)S(1)} fusion(f32[16,2048]{0,1:T(8,128)S(1)} %copy.103, s32[2048]{0:T(1024)S(1)} %fusion.70), kind=kCustom, calls=%fused_computation.12 | custom fusion | bytes 270336 | tf_op jit(solution)/shard_map/gather | solution.py:110
  236.4 1.0 copy.105
  237.7 5.5 %gather_fusion.11 = f32[2048,16]{1,0:T(8,128)S(1)} fusion(f32[16,2048]{0,1:T(8,128)S(1)} %copy.102, s32[2048]{0:T(1024)S(1)} %fusion.70), kind=kCustom, calls=%fused_computation.11 | custom fusion | bytes 270336 | tf_op jit(solution)/shard_map/gather | solution.py:110
  243.1 1.0 copy.104
  (80 shorter events, 6.6 us)
Async XLA Ops:
  0.6 83.3 %copy-start = (f32[5,128,128]{2,1,0:T(8,128)S(1)}, f32[5,128,128]{2,1,0:T(8,128)}, u32[]{:S(2)}) copy-start(f32[5,128,128]{2,1,0:T(8,128)} %param.15) | copy-start | bytes 983044
  10.0 5.5 %copy-start.3 = (f32[5,2048]{1,0:T(8,128)S(1)}, f32[5,2048]{1,0:T(8,128)}, u32[]{:S(2)}) copy-start(f32[5,2048]{1,0:T(8,128)} %param.14) | copy-start | bytes 122884
  10.0 17.9 %copy-start.5 = (s32[1,2,4]{2,1,0:T(2,128)S(1)}, s32[1,2,4]{2,1,0:T(2,128)}, u32[]{:S(2)}) copy-start(s32[1,2,4]{2,1,0:T(2,128)} %param.17) | copy-start | bytes 100
  10.0 17.9 %copy-start.4 = (f32[8,2048]{1,0:T(8,128)S(1)}, f32[8,2048]{1,0:T(8,128)}, u32[]{:S(2)}) copy-start(f32[8,2048]{1,0:T(8,128)} %param.9) | copy-start | bytes 196612
  10.0 17.8 %copy-start.6 = (f32[8]{0:T(128)S(1)}, f32[8]{0:T(128)}, u32[]{:S(2)}) copy-start(f32[8]{0:T(128)} %param.10) | copy-start | bytes 100
  24.8 27.0 %collective-permute-start = (f32[5,16,128]{2,1,0:T(8,128)S(1)}, f32[5,16,128]{2,1,0:T(8,128)S(1)}, u32[]{:S(2)}, u32[]{:S(2)}) collective-permute-start(f32[5,16,128]{2,1,0:T(8,128)S(1)} %convolution_bitcast_fusion.1), channel_id=1, source_target_pairs={{0,1},{1,0},{2,3},{3,2},{4,5},{5,4},{6,7},{7,6},{8,9},{9,8},{10,11... | collective-permute-start | bytes 122888 | tf_op jit(solution)/shard_map/ppermute | solution.py:19
  45.4 1.9 copy-start.2
  45.4 14.4 %copy-start.1 = (f32[2048]{0:T(1024)S(1)}, f32[2048]{0:T(1024)}, u32[]{:S(2)}) copy-start(f32[2048]{0:T(1024)} %param.11) | copy-start | bytes 24580
  51.8 4.9 %collective-permute-start.1 = (f32[4,16,128]{2,1,0:T(8,128)S(1)}, f32[4,16,128]{2,1,0:T(8,128)S(1)}, u32[]{:S(2)}, u32[]{:S(2)}) collective-permute-start(f32[4,16,128]{2,1,0:T(8,128)S(1)} %slice.127), channel_id=1, source_target_pairs={{0,2},{1,3},{2,0},{3,1},{4,6},{5,7},{6,4},{7,5},{8,10},{9,11},{10,... | collective-permute-start | bytes 98312 | tf_op jit(solution)/shard_map/ppermute | solution.py:19
  56.7 1.3 collective-permute-start.2
  58.0 22.2 %collective-permute-start.3 = (f32[2,16,128]{2,1,0:T(8,128)S(1)}, f32[2,16,128]{2,1,0:T(8,128)S(1)}, u32[]{:S(2)}, u32[]{:S(2)}) collective-permute-start(f32[2,16,128]{2,1,0:T(8,128)S(1)} %slice.129), channel_id=1, source_target_pairs={{0,8},{4,12},{8,0},{12,4},{16,24},{20,28},{24,16},{28,20},{1,9},{5... | collective-permute-start | bytes 49160 | tf_op jit(solution)/shard_map/ppermute | solution.py:19
  80.2 3.7 %collective-permute-start.4 = (f32[1,16,128]{2,1,0:T(8,128)S(1)}, f32[1,16,128]{2,1,0:T(8,128)S(1)}, u32[]{:S(2)}, u32[]{:S(2)}) collective-permute-start(f32[1,16,128]{2,1,0:T(8,128)S(1)} %slice.130), channel_id=1, source_target_pairs={{0,16},{4,20},{8,24},{12,28},{16,0},{20,4},{24,8},{28,12},{1,17},{... | collective-permute-start | bytes 24584 | tf_op jit(solution)/shard_map/ppermute | solution.py:19
  167.4 4.1 %collective-permute-start.5 = (f32[5,16,128]{2,1,0:T(8,128)S(1)}, f32[5,16,128]{2,1,0:T(8,128)S(1)}, u32[]{:S(2)}, u32[]{:S(2)}) collective-permute-start(f32[5,16,128]{2,1,0:T(8,128)S(1)} %convolution_bitcast_fusion), channel_id=1, source_target_pairs={{0,1},{1,0},{2,3},{3,2},{4,5},{5,4},{6,7},{7,6},{8,9},{9,8},{10,11... | collective-permute-start | bytes 122888 | tf_op jit(solution)/shard_map/ppermute | solution.py:19
  171.5 8.4 %collective-permute-start.6 = (f32[4,16,128]{2,1,0:T(8,128)S(1)}, f32[4,16,128]{2,1,0:T(8,128)S(1)}, u32[]{:S(2)}, u32[]{:S(2)}) collective-permute-start(f32[4,16,128]{2,1,0:T(8,128)S(1)} %slice.134), channel_id=1, source_target_pairs={{0,2},{1,3},{2,0},{3,1},{4,6},{5,7},{6,4},{7,5},{8,10},{9,11},{10,... | collective-permute-start | bytes 98312 | tf_op jit(solution)/shard_map/ppermute | solution.py:19
  179.9 1.3 collective-permute-start.7
  181.2 4.4 %collective-permute-start.8 = (f32[2,16,128]{2,1,0:T(8,128)S(1)}, f32[2,16,128]{2,1,0:T(8,128)S(1)}, u32[]{:S(2)}, u32[]{:S(2)}) collective-permute-start(f32[2,16,128]{2,1,0:T(8,128)S(1)} %slice.136), channel_id=1, source_target_pairs={{0,8},{4,12},{8,0},{12,4},{16,24},{20,28},{24,16},{28,20},{1,9},{5... | collective-permute-start | bytes 49160 | tf_op jit(solution)/shard_map/ppermute | solution.py:19
  185.6 3.7 %collective-permute-start.9 = (f32[1,16,128]{2,1,0:T(8,128)S(1)}, f32[1,16,128]{2,1,0:T(8,128)S(1)}, u32[]{:S(2)}, u32[]{:S(2)}) collective-permute-start(f32[1,16,128]{2,1,0:T(8,128)S(1)} %slice.137), channel_id=1, source_target_pairs={{0,16},{4,20},{8,24},{12,28},{16,0},{20,4},{24,8},{28,12},{1,17},{... | collective-permute-start | bytes 24584 | tf_op jit(solution)/shard_map/ppermute | solution.py:19
where the time goes:
time: 245 us; the launch traced here: 244 us
  blocking collectives  118 us (48%)
  local copies, waits for them, and re-layouts  73.5 us (30%)
  matrix products  21.7 us (9%)
  starting transfers between devices  17.9 us (7%)
  waiting for transfers between devices  10.5 us (4%)
    psum x2, blocking collectives, squares(): return lax.psum(jnp.sum(values * values, axis=1), ('gx', 'gy'))  79.4 us
    psum x1, blocking collectives, per_device(): curve = lax.psum(jnp.sum(direction * image, axis=1), ('gx', 'gy'))  38.3 us
    ppermute x10, starting transfers between devices, swapped(): return lax.ppermute(value, axis, pairs)  17.9 us
    gather x1, local copies, waits for them, and re-layouts, per_device(): noise_t = noise[perm]  11.8 us
    gather x2, local copies, waits for them, and re-layouts, per_device(): return (solution[:, inverse], residual[:, inverse])  10.9 us
    ppermute x10, waiting for transfers between devices, swapped(): return lax.ppermute(value, axis, pairs)  10.5 us
    dot_general x2, matrix products, tile_near(): result = jnp.einsum('gij,cgj->cgi', kern, union_vec, precision=highest)  10.4 us
    gather x1, local copies, waits for them, and re-layouts, per_device(): (coords * inv_scale[:, None])[:, perm]  8.79 us
  transfers between devices with their start and end apart: 10, of which 7 were waited for; matrix products, arithmetic and copies ran while one was open for 21% of the time, Pallas kernels for 0%

commit v1 on v0

--- a/solution.py
+++ b/solution.py
@@ -61,12 +61,21 @@
     return running
 
 
+def butterfly(value):
+    for bit in range(lax.axis_size("gy").bit_length() - 1):
+        value = value + swapped(value, "gy", bit)
+    for bit in range(lax.axis_size("gx").bit_length() - 1):
+        value = value + swapped(value, "gx", bit)
+    return value
+
+
 def per_device(coords, inv_scale, noise, right_side, basis, level_gain, coupling, order, pairs):
     perm = order[0]
     points = right_side.shape[1]
     columns = right_side.shape[0]
     tiles = points // TILE_POINTS
     levels = level_gain.shape[0]
+    rank = basis.shape[0]
     tile_coords = (coords * inv_scale[:, None])[:, perm].reshape(
         coords.shape[0], tiles, TILE_POINTS
     )
@@ -81,13 +90,24 @@
     residual = rhs_t
     direction = rhs_t
 
-    def squares(values):
-        return lax.psum(jnp.sum(values * values, axis=1), ("gx", "gy"))
+    def sums_with_norm(values):
+        proj = jnp.einsum("lp,cp,rp->lcr", gain_t, values, basis_t, precision=highest)
+        norm = jnp.sum(values * values, axis=1)
+        extra = jnp.broadcast_to(norm[None, :, None], (1, columns, rank))
+        running = tree_sums(jnp.concatenate([proj, extra], axis=0))
+        return running[:levels], running[levels, :, 0]
 
-    norm_now = squares(residual)
+    nodesum = None
+    norm_now = None
     for step in range(ITERATIONS):
-        proj = jnp.einsum("lp,cp,rp->lcr", gain_t, direction, basis_t, precision=highest)
-        nodesum = tree_sums(proj)
+        if step == 0:
+            nodesum, norm_now = sums_with_norm(residual)
+        else:
+            residual_sum, norm_next = sums_with_norm(residual)
+            ratio = norm_next / norm_now
+            direction = residual + ratio[:, None] * direction
+            nodesum = residual_sum + ratio[None, :, None] * nodesum
+            norm_now = norm_next
         coupled = jnp.einsum("lcr,lrs->lcs", nodesum, coupling, precision=highest)
         coupled = (
             jnp.einsum("lcs,lrs->lcr", coupled, coupling, precision=highest) * scales[:, None, None]
@@ -98,14 +118,10 @@
             tile_coords, direction.reshape(columns, tiles, TILE_POINTS), pair_rows, pair_cols
         )
         image = noise_t[None, :] * direction + far + near.reshape(columns, points)
-        curve = lax.psum(jnp.sum(direction * image, axis=1), ("gx", "gy"))
+        curve = butterfly(jnp.sum(direction * image, axis=1))
         alpha = norm_now / curve
         solution = solution + alpha[:, None] * direction
         residual = residual - alpha[:, None] * image
-        if step + 1 < ITERATIONS:
-            norm_next = squares(residual)
-            direction = residual + (norm_next / norm_now)[:, None] * direction
-            norm_now = norm_next
     inverse = jnp.zeros_like(perm).at[perm].set(jnp.arange(points, dtype=jnp.int32))
     return (solution[:, inverse], residual[:, inverse])
 

time: 245 us -> 164 us (0.67)
  blocking collectives: 118 us -> 0 us
  waiting for transfers between devices: 10.5 us -> 41.8 us
  starting transfers between devices: 17.9 us -> 22.2 us
  matrix products: 21.7 us -> 25.1 us
    psum x3 -> x0, blocking collectives: 118 us -> none  [the longest x2 79.4 us: squares(): return lax.psum(jnp.sum(values * values, axis=1), ('gx', 'gy'))]
    ppermute x10 -> x20, waiting for transfers between devices: 10.5 us -> 41.8 us  [swapped(): return lax.ppermute(value, axis, pairs)]
    ppermute x10 -> x20, starting transfers between devices: 17.9 us -> 22.2 us  [swapped(): return lax.ppermute(value, axis, pairs)]
    unnamed x24 -> x22, local copies, waits for them, and re-layouts: 8.24 us -> 6.33 us
  transfers between devices with their start and end apart: 10 -> 20, of which waited for: 7 -> 17; matrix products, arithmetic and copies ran while one was open for 21% -> 28% of each run, Pallas kernels for 0% -> 0%
where the time goes in v1:
time: 164 us
  local copies, waits for them, and re-layouts  71.7 us (44%)
  waiting for transfers between devices  41.8 us (25%)
  matrix products  25.1 us (15%)
  starting transfers between devices  22.2 us (14%)
  other arithmetic  1.91 us (1%)
    ppermute x20, waiting for transfers between devices, swapped(): return lax.ppermute(value, axis, pairs)  41.8 us
    ppermute x20, starting transfers between devices, swapped(): return lax.ppermute(value, axis, pairs)  22.2 us
    dot_general x2, matrix products, tile_near(): result = jnp.einsum('gij,cgj->cgi', kern, union_vec, precision=highest)  12.2 us
    gather x1, local copies, waits for them, and re-layouts, per_device(): noise_t = noise[perm]  11.8 us
    gather x2, local copies, waits for them, and re-layouts, per_device(): return (solution[:, inverse], residual[:, inverse])  10.9 us
    gather x1, local copies, waits for them, and re-layouts, per_device(): (coords * inv_scale[:, None])[:, perm]  8.8 us
    scatter x1, local copies, waits for them, and re-layouts, per_device(): jnp.zeros_like(perm).at[perm].set(jnp.arange(points, dtype=jnp.int32))  8.05 us
    gather x3, local copies, waits for them, and re-layouts, per_device(): gain_t = level_gain[:, perm]  7.34 us
  transfers between devices with their start and end apart: 20, of which 17 were waited for; matrix products, arithmetic and copies ran while one was open for 28% of the time, Pallas kernels for 0%

profile of v1, /device:TPU:0, one launch (start us, length us, event | category | flops | bytes accessed | tf_op | source)
XLA Modules:
  0.0 163.8 jit_solution(17979123866666533587)
XLA Ops:
  1.4 1.2 copy.84
  2.7 5.5 %gather_fusion = f32[2048,16]{1,0:T(8,128)S(1)} fusion(f32[16,2048]{0,1:T(8,128)S(1)} %copy.84, s32[2048]{0:T(1024)S(1)} %broadcast_clamp_fusion), kind=kCustom, calls=%fused_computation | custom fusion | bytes 270336 | tf_op jit(solution)/shard_map/gather | solution.py:85
  8.4 1.6 copy.88
  10.0 5.5 %gather_fusion.2 = f32[2048,128]{1,0:T(8,128)S(1)} fusion(f32[128,2048]{0,1:T(8,128)S(1)} %copy.88, s32[2048]{0:T(1024)S(1)} %broadcast_clamp_fusion), kind=kCustom, calls=%fused_computation.2 | custom fusion | bytes 2105344 | tf_op jit(solution)/shard_map/gather | solution.py:84
  15.5 1.3 copy.86
  16.9 6.7 %gather_fusion.1 = f32[2048,5]{1,0:T(8,128)S(1)} fusion(f32[5,2048]{0,1:T(8,128)} %copy.86, s32[2048]{0:T(1024)S(1)} %broadcast_clamp_fusion), kind=kCustom, calls=%fused_computation.1 | custom fusion | bytes 90112 | tf_op jit(solution)/shard_map/gather | solution.py:83
  24.0 0.9 convolution_bitcast_fusion.1
  25.0 3.0 %collective-permute-start = (f32[6,16,128]{2,1,0:T(8,128)S(1)}, f32[6,16,128]{2,1,0:T(8,128)S(1)}, u32[]{:S(2)}, u32[]{:S(2)}) collective-permute-start(f32[6,16,128]{2,1,0:T(8,128)S(1)} %pad_maximum_fusion.2), channel_id=1, source_target_pairs={{0,1},{1,0},{2,3},{3,2},{4,5},{5,4},{6,7},{7,6},{8,9},{9,8},{10,11... | collective-permute-start | bytes 147464 | tf_op jit(solution)/shard_map/ppermute | solution.py:19
  28.1 1.3 copy.93
  29.4 8.8 %gather_fusion.6 = f32[2048,8]{1,0:T(8,128)} fusion(f32[8,2048]{0,1:T(8,128)} %copy.93, s32[2048]{0:T(1024)S(1)} %broadcast_clamp_fusion), kind=kCustom, calls=%fused_computation.6 | custom fusion | bytes 139264 | tf_op jit(solution)/shard_map/gather | solution.py:79
  38.2 1.5 copy.94
  40.9 5.0 %fusion.52 = f32[4,512,512]{2,1,0:T(8,128)} fusion(f32[8,4,256]{2,0,1:T(8,128)S(1)} %bitcast.173, f32[8,4,256]{2,0,1:T(8,128)S(1)} %bitcast.171), kind=kOutput, calls=%fused_computation.91 | convolution fusion | flops 100679680 | bytes 4259840 | tf_op jit(solution)/shard_map/while/body/eval_jaxpr/fgi,fgj->gij/dot_general | solution.py:25
  47.1 6.0 %fusion.14 = f32[16,4,512]{2,0,1:T(8,128)S(1)} fusion(f32[4,512,512]{2,1,0:T(8,128)} %fusion.52, f32[4,512]{1,0:T(4,128)S(1)} %multiply_reduce_fusion.1, f32[16,4,256]{2,0,1:T(8,128)S(1)} %bitcast.178, f32[16,4,256]{2,0,1:T(8,128)S(1)} %bitcast.177), kind=kOutput, calls=%fused_computation.33 | convolution fusion | flops 206602240 | bytes 4464640 | tf_op jit(solution)/shard_map/while/body/eval_jaxpr/gij,cgj->cgi/dot_general | solution.py:30
  53.1 2.7 %collective-permute-start.1 = (f32[5,16,128]{2,1,0:T(8,128)S(1)}, f32[5,16,128]{2,1,0:T(8,128)S(1)}, u32[]{:S(2)}, u32[]{:S(2)}) collective-permute-start(f32[5,16,128]{2,1,0:T(8,128)S(1)} %slice.142), channel_id=1, source_target_pairs={{0,2},{1,3},{2,0},{3,1},{4,6},{5,7},{6,4},{7,5},{8,10},{9,11},{10,... | collective-permute-start | bytes 122888 | tf_op jit(solution)/shard_map/ppermute | solution.py:19
  55.8 2.3 %collective-permute-done.1 = f32[5,16,128]{2,1,0:T(8,128)S(1)} collective-permute-done((f32[5,16,128]{2,1,0:T(8,128)S(1)}, f32[5,16,128]{2,1,0:T(8,128)S(1)}, u32[]{:S(2)}, u32[]{:S(2)}) %collective-permute-start.1) | collective-permute-done | bytes 40992 | tf_op jit(solution)/shard_map/ppermute | solution.py:19
  58.2 1.2 collective-permute-done.2
  59.4 1.9 %collective-permute-start.3 = (f32[3,16,128]{2,1,0:T(8,128)S(1)}, f32[3,16,128]{2,1,0:T(8,128)S(1)}, u32[]{:S(2)}, u32[]{:S(2)}) collective-permute-start(f32[3,16,128]{2,1,0:T(8,128)S(1)} %slice.144), channel_id=1, source_target_pairs={{0,8},{4,12},{8,0},{12,4},{16,24},{20,28},{24,16},{28,20},{1,9},{5... | collective-permute-start | bytes 73736 | tf_op jit(solution)/shard_map/ppermute | solution.py:19
  61.6 1.7 %collective-permute-done.3 = f32[3,16,128]{2,1,0:T(8,128)S(1)} collective-permute-done((f32[3,16,128]{2,1,0:T(8,128)S(1)}, f32[3,16,128]{2,1,0:T(8,128)S(1)}, u32[]{:S(2)}, u32[]{:S(2)}) %collective-permute-start.3) | collective-permute-done | bytes 24608 | tf_op jit(solution)/shard_map/ppermute | solution.py:19
  63.3 1.9 %collective-permute-start.4 = (f32[2,16,128]{2,1,0:T(8,128)S(1)}, f32[2,16,128]{2,1,0:T(8,128)S(1)}, u32[]{:S(2)}, u32[]{:S(2)}) collective-permute-start(f32[2,16,128]{2,1,0:T(8,128)S(1)} %slice.145), channel_id=1, source_target_pairs={{0,16},{4,20},{8,24},{12,28},{16,0},{20,4},{24,8},{28,12},{1,17},{... | collective-permute-start | bytes 49160 | tf_op jit(solution)/shard_map/ppermute | solution.py:19
  65.6 11.8 %gather_fusion.3 = f32[2048]{0:T(1024)S(1)} fusion(f32[2048]{0:T(1024)S(1)} %copy-done.1, s32[2048]{0:T(1024)S(1)} %broadcast_clamp_fusion), kind=kCustom, calls=%fused_computation.3 | custom fusion | bytes 24576 | tf_op jit(solution)/shard_map/gather | solution.py:82
  78.4 1.3 fusion.12
  80.5 3.4 %collective-permute-done.5 = f32[16]{0:T(128)S(1)} collective-permute-done((f32[16]{0:T(128)S(1)}, f32[16]{0:T(128)S(1)}, u32[]{:S(2)}, u32[]{:S(2)}) %collective-permute-start.5) | collective-permute-done | bytes 96 | tf_op jit(solution)/shard_map/ppermute | solution.py:19
  83.9 2.3 %collective-permute-start.6 = (f32[16]{0:T(128)S(1)}, f32[16]{0:T(128)S(1)}, u32[]{:S(2)}, u32[]{:S(2)}) collective-permute-start(f32[16]{0:T(128)S(1)} %add.223), channel_id=1, source_target_pairs={{0,2},{1,3},{2,0},{3,1},{4,6},{5,7},{6,4},{7,5},{8,10},{9,11},{10,... | collective-permute-start | bytes 200 | tf_op jit(solution)/shard_map/ppermute | solution.py:19
  86.1 2.2 %collective-permute-done.6 = f32[16]{0:T(128)S(1)} collective-permute-done((f32[16]{0:T(128)S(1)}, f32[16]{0:T(128)S(1)}, u32[]{:S(2)}, u32[]{:S(2)}) %collective-permute-start.6) | collective-permute-done | bytes 96 | tf_op jit(solution)/shard_map/ppermute | solution.py:19
  88.3 1.1 collective-permute-done.7
  89.4 1.5 collective-permute-start.8
  91.0 1.9 %collective-permute-done.8 = f32[16]{0:T(128)S(1)} collective-permute-done((f32[16]{0:T(128)S(1)}, f32[16]{0:T(128)S(1)}, u32[]{:S(2)}, u32[]{:S(2)}) %collective-permute-start.8) | collective-permute-done | bytes 96 | tf_op jit(solution)/shard_map/ppermute | solution.py:19
  93.2 3.3 %collective-permute-done.9 = f32[16]{0:T(128)S(1)} collective-permute-done((f32[16]{0:T(128)S(1)}, f32[16]{0:T(128)S(1)}, u32[]{:S(2)}, u32[]{:S(2)}) %collective-permute-start.9) | collective-permute-done | bytes 96 | tf_op jit(solution)/shard_map/ppermute | solution.py:19
  98.0 3.9 %collective-permute-done.10 = f32[6,16,128]{2,1,0:T(8,128)S(1)} collective-permute-done((f32[6,16,128]{2,1,0:T(8,128)S(1)}, f32[6,16,128]{2,1,0:T(8,128)S(1)}, u32[]{:S(2)}, u32[]{:S(2)}) %collective-permute-start.10) | collective-permute-done | bytes 49184 | tf_op jit(solution)/shard_map/ppermute | solution.py:19
  102.0 2.3 %collective-permute-start.11 = (f32[5,16,128]{2,1,0:T(8,128)S(1)}, f32[5,16,128]{2,1,0:T(8,128)S(1)}, u32[]{:S(2)}, u32[]{:S(2)}) collective-permute-start(f32[5,16,128]{2,1,0:T(8,128)S(1)} %slice.150), channel_id=1, source_target_pairs={{0,2},{1,3},{2,0},{3,1},{4,6},{5,7},{6,4},{7,5},{8,10},{9,11},{10,... | collective-permute-start | bytes 122888 | tf_op jit(solution)/shard_map/ppermute | solution.py:19
  104.3 2.7 %collective-permute-done.11 = f32[5,16,128]{2,1,0:T(8,128)S(1)} collective-permute-done((f32[5,16,128]{2,1,0:T(8,128)S(1)}, f32[5,16,128]{2,1,0:T(8,128)S(1)}, u32[]{:S(2)}, u32[]{:S(2)}) %collective-permute-start.11) | collective-permute-done | bytes 40992 | tf_op jit(solution)/shard_map/ppermute | solution.py:19
  107.1 1.2 collective-permute-done.12
  108.3 1.6 collective-permute-start.13
  109.8 2.3 %collective-permute-done.13 = f32[3,16,128]{2,1,0:T(8,128)S(1)} collective-permute-done((f32[3,16,128]{2,1,0:T(8,128)S(1)}, f32[3,16,128]{2,1,0:T(8,128)S(1)}, u32[]{:S(2)}, u32[]{:S(2)}) %collective-permute-start.13) | collective-permute-done | bytes 24608 | tf_op jit(solution)/shard_map/ppermute | solution.py:19
  112.4 3.6 %collective-permute-done.14 = f32[2,16,128]{2,1,0:T(8,128)S(1)} collective-permute-done((f32[2,16,128]{2,1,0:T(8,128)S(1)}, f32[2,16,128]{2,1,0:T(8,128)S(1)}, u32[]{:S(2)}, u32[]{:S(2)}) %collective-permute-start.14) | collective-permute-done | bytes 16416 | tf_op jit(solution)/shard_map/ppermute | solution.py:19
  117.4 6.2 %fusion.15 = f32[16,4,512]{2,0,1:T(8,128)S(1)} fusion(f32[4,512,512]{2,1,0:T(8,128)} %fusion.52, f32[4,512]{1,0:T(4,128)S(1)} %multiply_reduce_fusion.1, f32[16,4,256]{2,0,1:T(8,128)S(1)} %bitcast.176, f32[16,4,256]{2,0,1:T(8,128)S(1)} %bitcast.175), kind=kOutput, calls=%fused_computation.34 | convolution fusion | flops 206602240 | bytes 4464640 | tf_op jit(solution)/shard_map/while/body/eval_jaxpr/gij,cgj->cgi/dot_general | solution.py:30
  125.0 1.3 fusion.13
  127.0 3.4 %collective-permute-done.15 = f32[16]{0:T(128)S(1)} collective-permute-done((f32[16]{0:T(128)S(1)}, f32[16]{0:T(128)S(1)}, u32[]{:S(2)}, u32[]{:S(2)}) %collective-permute-start.15) | collective-permute-done | bytes 96 | tf_op jit(solution)/shard_map/ppermute | solution.py:19
  130.4 2.2 %collective-permute-start.16 = (f32[16]{0:T(128)S(1)}, f32[16]{0:T(128)S(1)}, u32[]{:S(2)}, u32[]{:S(2)}) collective-permute-start(f32[16]{0:T(128)S(1)} %add.241), channel_id=1, source_target_pairs={{0,2},{1,3},{2,0},{3,1},{4,6},{5,7},{6,4},{7,5},{8,10},{9,11},{10,... | collective-permute-start | bytes 200 | tf_op jit(solution)/shard_map/ppermute | solution.py:19
  132.6 2.2 %collective-permute-done.16 = f32[16]{0:T(128)S(1)} collective-permute-done((f32[16]{0:T(128)S(1)}, f32[16]{0:T(128)S(1)}, u32[]{:S(2)}, u32[]{:S(2)}) %collective-permute-start.16) | collective-permute-done | bytes 96 | tf_op jit(solution)/shard_map/ppermute | solution.py:19
  134.8 8.0 %scatter_custom_fusion = s32[2048]{0:T(1024)S(1)} fusion(s32[2048]{0:T(1024)S(1)} %bitcast.180, s32[2048]{0:T(1024)S(1)} %iota.18, s32[]{:T(128)} %constant.28.clone.1), kind=kCustom, calls=%fused_computation.125 | custom fusion | bytes 8196 | tf_op jit(solution)/shard_map/scatter | solution.py:125
  142.9 1.6 collective-permute-start.18
  144.5 2.0 %collective-permute-done.18 = f32[16]{0:T(128)S(1)} collective-permute-done((f32[16]{0:T(128)S(1)}, f32[16]{0:T(128)S(1)}, u32[]{:S(2)}, u32[]{:S(2)}) %collective-permute-start.18) | collective-permute-done | bytes 96 | tf_op jit(solution)/shard_map/ppermute | solution.py:19
  146.8 3.3 %collective-permute-done.19 = f32[16]{0:T(128)S(1)} collective-permute-done((f32[16]{0:T(128)S(1)}, f32[16]{0:T(128)S(1)}, u32[]{:S(2)}, u32[]{:S(2)}) %collective-permute-start.19) | collective-permute-done | bytes 96 | tf_op jit(solution)/shard_map/ppermute | solution.py:19
  150.6 5.5 %gather_fusion.12 = f32[2048,16]{1,0:T(8,128)S(1)} fusion(f32[16,2048]{0,1:T(8,128)S(1)} %copy.103, s32[2048]{0:T(1024)S(1)} %fusion.61), kind=kCustom, calls=%fused_computation.12 | custom fusion | bytes 270336 | tf_op jit(solution)/shard_map/gather | solution.py:126
  156.0 1.0 copy.105
  157.3 5.5 %gather_fusion.11 = f32[2048,16]{1,0:T(8,128)S(1)} fusion(f32[16,2048]{0,1:T(8,128)S(1)} %copy.102, s32[2048]{0:T(1024)S(1)} %fusion.61), kind=kCustom, calls=%fused_computation.11 | custom fusion | bytes 270336 | tf_op jit(solution)/shard_map/gather | solution.py:126
  162.8 1.0 copy.104
  (108 shorter events, 13.3 us)
Async XLA Ops:
  0.6 76.8 %copy-start = (f32[5,128,128]{2,1,0:T(8,128)S(1)}, f32[5,128,128]{2,1,0:T(8,128)}, u32[]{:S(2)}) copy-start(f32[5,128,128]{2,1,0:T(8,128)} %param.15) | copy-start | bytes 983044
  10.0 5.5 %copy-start.2 = (f32[5,2048]{1,0:T(8,128)S(1)}, f32[5,2048]{1,0:T(8,128)}, u32[]{:S(2)}) copy-start(f32[5,2048]{1,0:T(8,128)} %param.14) | copy-start | bytes 122884
  15.5 12.5 %copy-start.3 = (f32[8,2048]{1,0:T(8,128)S(1)}, f32[8,2048]{1,0:T(8,128)}, u32[]{:S(2)}) copy-start(f32[8,2048]{1,0:T(8,128)} %param.9) | copy-start | bytes 196612
  15.5 12.5 %copy-start.5 = (f32[8]{0:T(128)S(1)}, f32[8]{0:T(128)}, u32[]{:S(2)}) copy-start(f32[8]{0:T(128)} %param.10) | copy-start | bytes 100
  15.5 24.2 %copy-start.4 = (s32[1,2,4]{2,1,0:T(2,128)S(1)}, s32[1,2,4]{2,1,0:T(2,128)}, u32[]{:S(2)}) copy-start(s32[1,2,4]{2,1,0:T(2,128)} %param.17) | copy-start | bytes 100
  25.0 28.1 %collective-permute-start = (f32[6,16,128]{2,1,0:T(8,128)S(1)}, f32[6,16,128]{2,1,0:T(8,128)S(1)}, u32[]{:S(2)}, u32[]{:S(2)}) collective-permute-start(f32[6,16,128]{2,1,0:T(8,128)S(1)} %pad_maximum_fusion.2), channel_id=1, source_target_pairs={{0,1},{1,0},{2,3},{3,2},{4,5},{5,4},{6,7},{7,6},{8,9},{9,8},{10,11... | collective-permute-start | bytes 147464 | tf_op jit(solution)/shard_map/ppermute | solution.py:19
  47.1 18.6 %copy-start.1 = (f32[2048]{0:T(1024)S(1)}, f32[2048]{0:T(1024)}, u32[]{:S(2)}) copy-start(f32[2048]{0:T(1024)} %param.11) | copy-start | bytes 24580
  53.1 5.0 %collective-permute-start.1 = (f32[5,16,128]{2,1,0:T(8,128)S(1)}, f32[5,16,128]{2,1,0:T(8,128)S(1)}, u32[]{:S(2)}, u32[]{:S(2)}) collective-permute-start(f32[5,16,128]{2,1,0:T(8,128)S(1)} %slice.142), channel_id=1, source_target_pairs={{0,2},{1,3},{2,0},{3,1},{4,6},{5,7},{6,4},{7,5},{8,10},{9,11},{10,... | collective-permute-start | bytes 122888 | tf_op jit(solution)/shard_map/ppermute | solution.py:19
  58.1 1.3 collective-permute-start.2
  59.4 3.9 %collective-permute-start.3 = (f32[3,16,128]{2,1,0:T(8,128)S(1)}, f32[3,16,128]{2,1,0:T(8,128)S(1)}, u32[]{:S(2)}, u32[]{:S(2)}) collective-permute-start(f32[3,16,128]{2,1,0:T(8,128)S(1)} %slice.144), channel_id=1, source_target_pairs={{0,8},{4,12},{8,0},{12,4},{16,24},{20,28},{24,16},{28,20},{1,9},{5... | collective-permute-start | bytes 73736 | tf_op jit(solution)/shard_map/ppermute | solution.py:19
  63.3 14.1 %collective-permute-start.4 = (f32[2,16,128]{2,1,0:T(8,128)S(1)}, f32[2,16,128]{2,1,0:T(8,128)S(1)}, u32[]{:S(2)}, u32[]{:S(2)}) collective-permute-start(f32[2,16,128]{2,1,0:T(8,128)S(1)} %slice.145), channel_id=1, source_target_pairs={{0,16},{4,20},{8,24},{12,28},{16,0},{20,4},{24,8},{28,12},{1,17},{... | collective-permute-start | bytes 49160 | tf_op jit(solution)/shard_map/ppermute | solution.py:19
  80.3 3.6 %collective-permute-start.5 = (f32[16]{0:T(128)S(1)}, f32[16]{0:T(128)S(1)}, u32[]{:S(2)}, u32[]{:S(2)}) collective-permute-start(f32[16]{0:T(128)S(1)} %get-tuple-element.62), channel_id=1, source_target_pairs={{0,1},{1,0},{2,3},{3,2},{4,5},{5,4},{6,7},{7,6},{8,9},{9,8},{10,11... | collective-permute-start | bytes 200 | tf_op jit(solution)/shard_map/ppermute | solution.py:19
  83.9 4.4 %collective-permute-start.6 = (f32[16]{0:T(128)S(1)}, f32[16]{0:T(128)S(1)}, u32[]{:S(2)}, u32[]{:S(2)}) collective-permute-start(f32[16]{0:T(128)S(1)} %add.223), channel_id=1, source_target_pairs={{0,2},{1,3},{2,0},{3,1},{4,6},{5,7},{6,4},{7,5},{8,10},{9,11},{10,... | collective-permute-start | bytes 200 | tf_op jit(solution)/shard_map/ppermute | solution.py:19
  88.3 1.1 collective-permute-start.7
  89.4 3.5 %collective-permute-start.8 = (f32[16]{0:T(128)S(1)}, f32[16]{0:T(128)S(1)}, u32[]{:S(2)}, u32[]{:S(2)}) collective-permute-start(f32[16]{0:T(128)S(1)} %add.225), channel_id=1, source_target_pairs={{0,8},{4,12},{8,0},{12,4},{16,24},{20,28},{24,16},{28,20},{1,9},{5... | collective-permute-start | bytes 200 | tf_op jit(solution)/shard_map/ppermute | solution.py:19
  93.0 3.5 %collective-permute-start.9 = (f32[16]{0:T(128)S(1)}, f32[16]{0:T(128)S(1)}, u32[]{:S(2)}, u32[]{:S(2)}) collective-permute-start(f32[16]{0:T(128)S(1)} %add.226), channel_id=1, source_target_pairs={{0,16},{4,20},{8,24},{12,28},{16,0},{20,4},{24,8},{28,12},{1,17},{... | collective-permute-start | bytes 200 | tf_op jit(solution)/shard_map/ppermute | solution.py:19
  97.8 4.1 %collective-permute-start.10 = (f32[6,16,128]{2,1,0:T(8,128)S(1)}, f32[6,16,128]{2,1,0:T(8,128)S(1)}, u32[]{:S(2)}, u32[]{:S(2)}) collective-permute-start(f32[6,16,128]{2,1,0:T(8,128)S(1)} %pad_maximum_fusion.3), channel_id=1, source_target_pairs={{0,1},{1,0},{2,3},{3,2},{4,5},{5,4},{6,7},{7,6},{8,9},{9,8},{10,11... | collective-permute-start | bytes 147464 | tf_op jit(solution)/shard_map/ppermute | solution.py:19
  102.0 5.0 %collective-permute-start.11 = (f32[5,16,128]{2,1,0:T(8,128)S(1)}, f32[5,16,128]{2,1,0:T(8,128)S(1)}, u32[]{:S(2)}, u32[]{:S(2)}) collective-permute-start(f32[5,16,128]{2,1,0:T(8,128)S(1)} %slice.150), channel_id=1, source_target_pairs={{0,2},{1,3},{2,0},{3,1},{4,6},{5,7},{6,4},{7,5},{8,10},{9,11},{10,... | collective-permute-start | bytes 122888 | tf_op jit(solution)/shard_map/ppermute | solution.py:19
  107.0 1.3 collective-permute-start.12
  108.3 3.9 %collective-permute-start.13 = (f32[3,16,128]{2,1,0:T(8,128)S(1)}, f32[3,16,128]{2,1,0:T(8,128)S(1)}, u32[]{:S(2)}, u32[]{:S(2)}) collective-permute-start(f32[3,16,128]{2,1,0:T(8,128)S(1)} %slice.152), channel_id=1, source_target_pairs={{0,8},{4,12},{8,0},{12,4},{16,24},{20,28},{24,16},{28,20},{1,9},{5... | collective-permute-start | bytes 73736 | tf_op jit(solution)/shard_map/ppermute | solution.py:19
  112.2 3.8 %collective-permute-start.14 = (f32[2,16,128]{2,1,0:T(8,128)S(1)}, f32[2,16,128]{2,1,0:T(8,128)S(1)}, u32[]{:S(2)}, u32[]{:S(2)}) collective-permute-start(f32[2,16,128]{2,1,0:T(8,128)S(1)} %slice.153), channel_id=1, source_target_pairs={{0,16},{4,20},{8,24},{12,28},{16,0},{20,4},{24,8},{28,12},{1,17},{... | collective-permute-start | bytes 49160 | tf_op jit(solution)/shard_map/ppermute | solution.py:19
  126.8 3.6 %collective-permute-start.15 = (f32[16]{0:T(128)S(1)}, f32[16]{0:T(128)S(1)}, u32[]{:S(2)}, u32[]{:S(2)}) collective-permute-start(f32[16]{0:T(128)S(1)} %get-tuple-element.64), channel_id=1, source_target_pairs={{0,1},{1,0},{2,3},{3,2},{4,5},{5,4},{6,7},{7,6},{8,9},{9,8},{10,11... | collective-permute-start | bytes 200 | tf_op jit(solution)/shard_map/ppermute | solution.py:19
  130.4 4.4 %collective-permute-start.16 = (f32[16]{0:T(128)S(1)}, f32[16]{0:T(128)S(1)}, u32[]{:S(2)}, u32[]{:S(2)}) collective-permute-start(f32[16]{0:T(128)S(1)} %add.241), channel_id=1, source_target_pairs={{0,2},{1,3},{2,0},{3,1},{4,6},{5,7},{6,4},{7,5},{8,10},{9,11},{10,... | collective-permute-start | bytes 200 | tf_op jit(solution)/shard_map/ppermute | solution.py:19
  134.8 8.1 %collective-permute-start.17 = (f32[16]{0:T(128)S(1)}, f32[16]{0:T(128)S(1)}, u32[]{:S(2)}, u32[]{:S(2)}) collective-permute-start(f32[16]{0:T(128)S(1)} %add.242), channel_id=1, source_target_pairs={{0,4},{4,0},{8,12},{12,8},{16,20},{20,16},{24,28},{28,24},{1,5},{5... | collective-permute-start | bytes 200 | tf_op jit(solution)/shard_map/ppermute | solution.py:19
  142.9 3.6 %collective-permute-start.18 = (f32[16]{0:T(128)S(1)}, f32[16]{0:T(128)S(1)}, u32[]{:S(2)}, u32[]{:S(2)}) collective-permute-start(f32[16]{0:T(128)S(1)} %add.243), channel_id=1, source_target_pairs={{0,8},{4,12},{8,0},{12,4},{16,24},{20,28},{24,16},{28,20},{1,9},{5... | collective-permute-start | bytes 200 | tf_op jit(solution)/shard_map/ppermute | solution.py:19
  146.5 3.5 %collective-permute-start.19 = (f32[16]{0:T(128)S(1)}, f32[16]{0:T(128)S(1)}, u32[]{:S(2)}, u32[]{:S(2)}) collective-permute-start(f32[16]{0:T(128)S(1)} %add.244), channel_id=1, source_target_pairs={{0,16},{4,20},{8,24},{12,28},{16,0},{20,4},{24,8},{28,12},{1,17},{... | collective-permute-start | bytes 200 | tf_op jit(solution)/shard_map/ppermute | solution.py:19

commit v2 on v1

v2 whole, which is shorter than its diff:
```python
import math

import jax
import jax.numpy as jnp
from jax import lax
from jax.sharding import PartitionSpec as P

TILE_POINTS = 256
ITERATIONS = 2


near_weight = 0.25
highest = lax.Precision.HIGHEST


def swapped(value, axis, bit):
    mask = 2**bit
    pairs = [(source, source ^ mask) for source in range(lax.axis_size(axis))]
    return lax.ppermute(value, axis, pairs)


def near_kernels(tile_coords, pair_rows, pair_cols):
    union = jnp.concatenate([tile_coords[:, pair_rows], tile_coords[:, pair_cols]], axis=2)
    gram = jnp.einsum("fgi,fgj->gij", union, union, precision=highest)
    square = jnp.sum(union * union, axis=0)
    dist = square[:, :, None] + square[:, None, :] - 2.0 * gram
    return near_weight * jnp.exp(-0.5 * dist)


def near_apply(kern, tile_vec, pair_rows, pair_cols):
    width = tile_vec.shape[2]
    union_vec = jnp.concatenate([tile_vec[:, pair_rows], tile_vec[:, pair_cols]], axis=2)
    result = jnp.einsum("gij,cgj->cgi", kern, union_vec, precision=highest)
    tile_ids = jnp.arange(tile_vec.shape[1], dtype=jnp.int32)
    row_hot = (pair_rows[:, None] == tile_ids[None, :]).astype(jnp.float32)
    col_hot = (pair_cols[:, None] == tile_ids[None, :]).astype(jnp.float32)
    added = jnp.einsum("cgi,gt->cti", result[:, :, :width], row_hot, precision=highest)
    return added + jnp.einsum("cgi,gt->cti", result[:, :, width:], col_hot, precision=highest)


def tree_sums(proj):
    low_count = lax.axis_size("gy").bit_length() - 1
    high_count = lax.axis_size("gx").bit_length() - 1
    running = proj
    for bit in range(low_count):
        partner = swapped(running[bit:], "gy", bit)
        running = jnp.concatenate([running[:bit], running[bit:] + partner], axis=0)
    for bit in range(high_count):
        level = low_count + bit
        partner = swapped(running[level:], "gx", bit)
        running = jnp.concatenate([running[:level], running[level:] + partner], axis=0)
    return running


def butterfly(value):
    for bit in range(lax.axis_size("gy").bit_length() - 1):
        value = value + swapped(value, "gy", bit)
    for bit in range(lax.axis_size("gx").bit_length() - 1):
        value = value + swapped(value, "gx", bit)
    return value


def per_device(coords, inv_scale, noise, right_side, basis, level_gain, coupling, order, pairs):
    perm = order[0]
    columns, points = right_side.shape
    tiles = points // TILE_POINTS
    levels = level_gain.shape[0]
    rank = basis.shape[0]
    pair_rows = pairs[0, 0]
    pair_cols = pairs[0, 1]
    inverse = jnp.zeros_like(perm).at[perm].set(jnp.arange(points, dtype=jnp.int32))
    tile_coords = (coords * inv_scale[:, None])[:, perm].reshape(
        coords.shape[0], tiles, TILE_POINTS
    )
    kern = near_kernels(tile_coords, pair_rows, pair_cols)
    scales = 2.0 ** ((1.0 - jnp.arange(levels, dtype=jnp.float32)) / 2.0)

    def near_of(values):
        tile_vec = values[:, perm].reshape(columns, tiles, TILE_POINTS)
        near_t = near_apply(kern, tile_vec, pair_rows, pair_cols).reshape(columns, points)
        return near_t[:, inverse]

    def sums_with_norm(values):
        proj = jnp.einsum("lp,cp,rp->lcr", level_gain, values, basis, precision=highest)
        norm = jnp.sum(values * values, axis=1)
        extra = jnp.broadcast_to(norm[None, :, None], (1, columns, rank))
        running = tree_sums(jnp.concatenate([proj, extra], axis=0))
        return running[:levels], running[levels, :, 0]

    solution = jnp.zeros_like(right_side)
    residual = right_side
    direction = right_side
    for step in range(ITERATIONS):
        if step == 0:
            nodesum, norm_now = sums_with_norm(residual)
            near = near_of(direction)
        else:
            residual_sum, norm_next = sums_with_norm(residual)
            residual_near = near_of(residual)
            ratio = norm_next / norm_now
            direction = residual + ratio[:, None] * direction
            nodesum = residual_sum + ratio[None, :, None] * nodesum
            near = residual_near + ratio[:, None] * near
            norm_now = norm_next
        coupled = jnp.einsum("lcr,lrs->lcs", nodesum, coupling, precision=highest)
        coupled = (
            jnp.einsum("lcs,lrs->lcr", coupled, coupling, precision=highest) * scales[:, None, None]
        )
        back = jnp.einsum("lcr,rp->lcp", coupled, basis, precision=highest)
        far = jnp.sum(back * level_gain[:, None, :], axis=0)
        image = noise[None, :] * direction + far + near
        curve = butterfly(jnp.sum(direction * image, axis=1))
        alpha = norm_now / curve
        solution = solution + alpha[:, None] * direction
        residual = residual - alpha[:, None] * image
    return (solution, residual)


def solution(mesh):
    return jax.shard_map(
        per_device,
        mesh=mesh,
        in_specs=(
            P(None, ("gx", "gy")),
            P(),
            P(("gx", "gy")),
            P(None, ("gx", "gy")),
            P(None, ("gx", "gy")),
            P(None, ("gx", "gy")),
            P(),
            P(("gx", "gy"), None),
            P(("gx", "gy"), None, None),
        ),
        out_specs=(P(None, ("gx", "gy")), P(None, ("gx", "gy"))),
        check_vma=False,
    )
```

time: 164 us -> 145 us (0.88)
  local copies, waits for them, and re-layouts: 71.7 us -> 59.4 us
  waiting for transfers between devices: 41.8 us -> 30.8 us
  other arithmetic: 1.91 us -> 4.5 us
    ppermute x20, waiting for transfers between devices: 41.8 us -> 30.8 us  [swapped(): return lax.ppermute(value, axis, pairs)]
    gather x16 -> x12, local copies, waits for them, and re-layouts: 44.6 us -> 36.8 us  [the longest x4 18.2 us: near_of(): return near_t[:, inverse]]
    unnamed x22 -> x13, local copies, waits for them, and re-layouts: 6.33 us -> 0.52 us
    reshape x0 -> x4, local copies, waits for them, and re-layouts: none -> 3.74 us  [the longest x2 3.04 us: near_of(): tile_vec = values[:, perm].reshape(columns, tiles, TILE_POINTS)]
  transfers between devices with their start and end apart: 20 -> 20, of which waited for: 17 -> 14; matrix products, arithmetic and copies ran while one was open for 28% -> 55% of each run, Pallas kernels for 0% -> 0%
where the time goes in v2:
time: 145 us; the launch traced here: 144 us
  local copies, waits for them, and re-layouts  59.4 us (41%)
  waiting for transfers between devices  30.8 us (21%)
  matrix products  25.2 us (17%)
  starting transfers between devices  23.4 us (16%)
  other arithmetic  4.5 us (3%)
    ppermute x20, waiting for transfers between devices, swapped(): return lax.ppermute(value, axis, pairs)  30.8 us
    ppermute x20, starting transfers between devices, swapped(): return lax.ppermute(value, axis, pairs)  23.4 us
    gather x4, local copies, waits for them, and re-layouts, near_of(): return near_t[:, inverse]  18.2 us
    gather x2, local copies, waits for them, and re-layouts, near_of(): tile_vec = values[:, perm].reshape(columns, tiles, TILE_POINTS)  15.2 us
    dot_general x2, matrix products, near_apply(): result = jnp.einsum('gij,cgj->cgi', kern, union_vec, precision=highest)  12 us
    scatter x1, local copies, waits for them, and re-layouts, per_device(): jnp.zeros_like(perm).at[perm].set(jnp.arange(points, dtype=jnp.int32))  8.23 us
    gather x1, local copies, waits for them, and re-layouts, per_device(): (coords * inv_scale[:, None])[:, perm]  7.6 us
    dot_general x1, matrix products, near_kernels(): gram = jnp.einsum('fgi,fgj->gij', union, union, precision=highest)  5.02 us
  transfers between devices with their start and end apart: 20, of which 14 were waited for; matrix products, arithmetic and copies ran while one was open for 55% of the time, Pallas kernels for 0%

profile of v2, /device:TPU:0, one launch (start us, length us, event | category | flops | bytes accessed | tf_op | source)
XLA Modules:
  0.0 144.2 jit_solution(9048735715033511115)
XLA Ops:
  0.7 1.1 multiply_reduce_fusion.3
  1.9 2.2 %convolution_bitcast_fusion.1 = f32[5,16,128]{2,1,0:T(8,128)S(1)} fusion(f32[128,2048]{1,0:T(8,128)S(1)} %copy-done, f32[2048,5]{0,1:T(8,128)} %bitcast.108, f32[2048,16]{0,1:T(8,128)} %bitcast.101), kind=kOutput, calls=%fused_computation.36 | convolution fusion | flops 251822080 | bytes 1261568 | tf_op jit(solution)/shard_map/lp,cp,rp->lcr/dot_general | solution.py:84
  4.2 3.0 %collective-permute-start = (f32[6,16,128]{2,1,0:T(8,128)S(1)}, f32[6,16,128]{2,1,0:T(8,128)S(1)}, u32[]{:S(2)}, u32[]{:S(2)}) collective-permute-start(f32[6,16,128]{2,1,0:T(8,128)S(1)} %pad_maximum_fusion.2), channel_id=1, source_target_pairs={{0,1},{1,0},{2,3},{3,2},{4,5},{5,4},{6,7},{7,6},{8,9},{9,8},{10,11... | collective-permute-start | bytes 147464 | tf_op jit(solution)/shard_map/ppermute | solution.py:19
  7.2 0.9 broadcast_multiply_fusion
  8.5 0.7 compare_select_fusion
  9.2 7.6 %gather_fusion.3 = f32[2048,8]{1,0:T(8,128)} fusion(f32[8,2048]{0,1:T(8,128)S(1)} %copy.88, s32[2048]{0:T(1024)S(1)} %broadcast_clamp_fusion), kind=kCustom, calls=%fused_computation.3 | custom fusion | bytes 139264 | tf_op jit(solution)/shard_map/gather | solution.py:72
  16.8 1.5 %copy.89 = f32[8,8,256]{2,0,1:T(8,128)S(1)} copy(f32[8,8,256]{0,2,1:T(8,128)} %bitcast.107) | data formatting | bytes 131072 | tf_op jit(solution)/shard_map/reshape | solution.py:72
  19.5 5.0 %fusion.43 = f32[4,512,512]{2,1,0:T(8,128)} fusion(f32[8,4,256]{2,0,1:T(8,128)S(1)} %bitcast.110, f32[8,4,256]{2,0,1:T(8,128)S(1)} %bitcast.112), kind=kOutput, calls=%fused_computation.77 | convolution fusion | flops 100679680 | bytes 4259840 | tf_op jit(solution)/shard_map/fgi,fgj->gij/dot_general | solution.py:24
  24.9 7.6 %gather_fusion = f32[2048,16]{1,0:T(8,128)} fusion(f32[16,2048]{0,1:T(8,128)S(1)} %copy.85, s32[2048]{0:T(1024)S(1)} %broadcast_clamp_fusion), kind=kCustom, calls=%fused_computation | custom fusion | bytes 270336 | tf_op jit(solution)/shard_map/gather | solution.py:79
  32.5 1.5 %copy.86 = f32[16,8,256]{2,0,1:T(8,128)S(1)} copy(f32[16,8,256]{0,2,1:T(8,128)} %bitcast.106) | data formatting | bytes 262144 | tf_op jit(solution)/shard_map/reshape | solution.py:79
  35.1 6.0 %fusion.16 = f32[16,4,512]{2,0,1:T(8,128)S(1)} fusion(f32[4,512,512]{2,1,0:T(8,128)} %fusion.43, f32[4,512]{1,0:T(4,128)S(1)} %multiply_reduce_fusion.4, f32[16,4,256]{2,0,1:T(8,128)S(1)} %bitcast.116, f32[16,4,256]{2,0,1:T(8,128)S(1)} %bitcast.117), kind=kOutput, calls=%fused_computation.33 | convolution fusion | flops 206602240 | bytes 4464640 | tf_op jit(solution)/shard_map/gij,cgj->cgi/dot_general | solution.py:33
  41.2 2.7 %collective-permute-start.1 = (f32[5,16,128]{2,1,0:T(8,128)S(1)}, f32[5,16,128]{2,1,0:T(8,128)S(1)}, u32[]{:S(2)}, u32[]{:S(2)}) collective-permute-start(f32[5,16,128]{2,1,0:T(8,128)S(1)} %slice.134), channel_id=1, source_target_pairs={{0,2},{1,3},{2,0},{3,1},{4,6},{5,7},{6,4},{7,5},{8,10},{9,11},{10,... | collective-permute-start | bytes 122888 | tf_op jit(solution)/shard_map/ppermute | solution.py:19
  44.2 2.0 %collective-permute-done.1 = f32[5,16,128]{2,1,0:T(8,128)S(1)} collective-permute-done((f32[5,16,128]{2,1,0:T(8,128)S(1)}, f32[5,16,128]{2,1,0:T(8,128)S(1)}, u32[]{:S(2)}, u32[]{:S(2)}) %collective-permute-start.1) | collective-permute-done | bytes 40992 | tf_op jit(solution)/shard_map/ppermute | solution.py:19
  46.6 8.2 %scatter_custom_fusion = s32[2048]{0:T(1024)S(1)} fusion(s32[2048]{0:T(1024)S(1)} %bitcast.119, s32[2048]{0:T(1024)S(1)} %iota.16, s32[]{:T(128)} %constant.4.clone.1), kind=kCustom, calls=%fused_computation.111 | custom fusion | bytes 8196 | tf_op jit(solution)/shard_map/scatter | solution.py:71
  54.9 1.9 %collective-permute-start.3 = (f32[3,16,128]{2,1,0:T(8,128)S(1)}, f32[3,16,128]{2,1,0:T(8,128)S(1)}, u32[]{:S(2)}, u32[]{:S(2)}) collective-permute-start(f32[3,16,128]{2,1,0:T(8,128)S(1)} %slice.136), channel_id=1, source_target_pairs={{0,8},{4,12},{8,0},{12,4},{16,24},{20,28},{24,16},{28,20},{1,9},{5... | collective-permute-start | bytes 73736 | tf_op jit(solution)/shard_map/ppermute | solution.py:19
  56.8 2.0 %collective-permute-done.3 = f32[3,16,128]{2,1,0:T(8,128)S(1)} collective-permute-done((f32[3,16,128]{2,1,0:T(8,128)S(1)}, f32[3,16,128]{2,1,0:T(8,128)S(1)}, u32[]{:S(2)}, u32[]{:S(2)}) %collective-permute-start.3) | collective-permute-done | bytes 24608 | tf_op jit(solution)/shard_map/ppermute | solution.py:19
  58.8 1.9 %collective-permute-start.4 = (f32[2,16,128]{2,1,0:T(8,128)S(1)}, f32[2,16,128]{2,1,0:T(8,128)S(1)}, u32[]{:S(2)}, u32[]{:S(2)}) collective-permute-start(f32[2,16,128]{2,1,0:T(8,128)S(1)} %slice.137), channel_id=1, source_target_pairs={{0,16},{4,20},{8,24},{12,28},{16,0},{20,4},{24,8},{28,12},{1,17},{... | collective-permute-start | bytes 49160 | tf_op jit(solution)/shard_map/ppermute | solution.py:19
  61.1 7.6 %gather_fusion.6 = f32[2048,16]{1,0:T(8,128)} fusion(f32[16,2048]{0,1:T(8,128)S(1)} %bitcast.103, s32[2048]{0:T(1024)S(1)} %fusion.52), kind=kCustom, calls=%fused_computation.6 | custom fusion | bytes 270336 | tf_op jit(solution)/shard_map/gather | solution.py:81
  68.7 1.5 %copy.94 = f32[2048,16]{0,1:T(8,128)S(1)} copy(f32[2048,16]{1,0:T(8,128)} %gather_fusion.6) | data formatting | bytes 262144 | tf_op jit(solution)/shard_map/gather | solution.py:81
  71.2 0.8 fusion.12
  72.4 3.4 %collective-permute-done.5 = f32[16]{0:T(128)S(1)} collective-permute-done((f32[16]{0:T(128)S(1)}, f32[16]{0:T(128)S(1)}, u32[]{:S(2)}, u32[]{:S(2)}) %collective-permute-start.5) | collective-permute-done | bytes 96 | tf_op jit(solution)/shard_map/ppermute | solution.py:19
  75.7 2.3 %collective-permute-start.6 = (f32[16]{0:T(128)S(1)}, f32[16]{0:T(128)S(1)}, u32[]{:S(2)}, u32[]{:S(2)}) collective-permute-start(f32[16]{0:T(128)S(1)} %add.166), channel_id=1, source_target_pairs={{0,2},{1,3},{2,0},{3,1},{4,6},{5,7},{6,4},{7,5},{8,10},{9,11},{10,... | collective-permute-start | bytes 200 | tf_op jit(solution)/shard_map/ppermute | solution.py:19
  78.0 2.2 %collective-permute-done.6 = f32[16]{0:T(128)S(1)} collective-permute-done((f32[16]{0:T(128)S(1)}, f32[16]{0:T(128)S(1)}, u32[]{:S(2)}, u32[]{:S(2)}) %collective-permute-start.6) | collective-permute-done | bytes 96 | tf_op jit(solution)/shard_map/ppermute | solution.py:19
  80.2 1.1 collective-permute-done.7
  81.3 1.5 %collective-permute-start.8 = (f32[16]{0:T(128)S(1)}, f32[16]{0:T(128)S(1)}, u32[]{:S(2)}, u32[]{:S(2)}) collective-permute-start(f32[16]{0:T(128)S(1)} %add.168), channel_id=1, source_target_pairs={{0,8},{4,12},{8,0},{12,4},{16,24},{20,28},{24,16},{28,20},{1,9},{5... | collective-permute-start | bytes 200 | tf_op jit(solution)/shard_map/ppermute | solution.py:19
  82.8 2.0 %collective-permute-done.8 = f32[16]{0:T(128)S(1)} collective-permute-done((f32[16]{0:T(128)S(1)}, f32[16]{0:T(128)S(1)}, u32[]{:S(2)}, u32[]{:S(2)}) %collective-permute-start.8) | collective-permute-done | bytes 96 | tf_op jit(solution)/shard_map/ppermute | solution.py:19
  85.1 3.3 %collective-permute-done.9 = f32[16]{0:T(128)S(1)} collective-permute-done((f32[16]{0:T(128)S(1)}, f32[16]{0:T(128)S(1)}, u32[]{:S(2)}, u32[]{:S(2)}) %collective-permute-start.9) | collective-permute-done | bytes 96 | tf_op jit(solution)/shard_map/ppermute | solution.py:19
  88.6 1.2 convolution_bitcast_fusion
  90.4 7.6 %gather_fusion.7 = f32[2048,16]{1,0:T(8,128)} fusion(f32[16,2048]{0,1:T(8,128)S(1)} %copy.95, s32[2048]{0:T(1024)S(1)} %broadcast_clamp_fusion), kind=kCustom, calls=%fused_computation.7 | custom fusion | bytes 270336 | tf_op jit(solution)/shard_map/gather | solution.py:79
  98.0 1.5 %copy.96 = f32[16,8,256]{2,0,1:T(8,128)S(1)} copy(f32[16,8,256]{0,2,1:T(8,128)} %bitcast.105) | data formatting | bytes 262144 | tf_op jit(solution)/shard_map/reshape | solution.py:79
  100.7 2.7 %collective-permute-start.11 = (f32[5,16,128]{2,1,0:T(8,128)S(1)}, f32[5,16,128]{2,1,0:T(8,128)S(1)}, u32[]{:S(2)}, u32[]{:S(2)}) collective-permute-start(f32[5,16,128]{2,1,0:T(8,128)S(1)} %slice.142), channel_id=1, source_target_pairs={{0,2},{1,3},{2,0},{3,1},{4,6},{5,7},{6,4},{7,5},{8,10},{9,11},{10,... | collective-permute-start | bytes 122888 | tf_op jit(solution)/shard_map/ppermute | solution.py:19
  103.4 6.0 %fusion.17 = f32[16,4,512]{2,0,1:T(8,128)S(1)} fusion(f32[4,512,512]{2,1,0:T(8,128)} %fusion.43, f32[4,512]{1,0:T(4,128)S(1)} %multiply_reduce_fusion.4, f32[16,4,256]{2,0,1:T(8,128)S(1)} %bitcast.114, f32[16,4,256]{2,0,1:T(8,128)S(1)} %bitcast.115), kind=kOutput, calls=%fused_computation.34 | convolution fusion | flops 206602240 | bytes 4464640 | tf_op jit(solution)/shard_map/gij,cgj->cgi/dot_general | solution.py:33
  109.5 1.2 collective-permute-done.12
  110.7 1.5 %collective-permute-start.13 = (f32[3,16,128]{2,1,0:T(8,128)S(1)}, f32[3,16,128]{2,1,0:T(8,128)S(1)}, u32[]{:S(2)}, u32[]{:S(2)}) collective-permute-start(f32[3,16,128]{2,1,0:T(8,128)S(1)} %slice.144), channel_id=1, source_target_pairs={{0,8},{4,12},{8,0},{12,4},{16,24},{20,28},{24,16},{28,20},{1,9},{5... | collective-permute-start | bytes 73736 | tf_op jit(solution)/shard_map/ppermute | solution.py:19
  112.6 2.0 %collective-permute-done.13 = f32[3,16,128]{2,1,0:T(8,128)S(1)} collective-permute-done((f32[3,16,128]{2,1,0:T(8,128)S(1)}, f32[3,16,128]{2,1,0:T(8,128)S(1)}, u32[]{:S(2)}, u32[]{:S(2)}) %collective-permute-start.13) | collective-permute-done | bytes 24608 | tf_op jit(solution)/shard_map/ppermute | solution.py:19
  115.8 7.6 %gather_fusion.10 = f32[2048,16]{1,0:T(8,128)} fusion(f32[16,2048]{0,1:T(8,128)S(1)} %bitcast.102, s32[2048]{0:T(1024)S(1)} %fusion.52), kind=kCustom, calls=%fused_computation.10 | custom fusion | bytes 270336 | tf_op jit(solution)/shard_map/gather | solution.py:81
  123.4 1.5 %copy.101 = f32[2048,16]{0,1:T(8,128)S(1)} copy(f32[2048,16]{1,0:T(8,128)} %gather_fusion.10) | data formatting | bytes 262144 | tf_op jit(solution)/shard_map/gather | solution.py:81
  125.5 0.6 convolution_multiply_fusion.2
  126.1 0.8 fusion.13
  127.1 1.6 %collective-permute-start.15 = (f32[16]{0:T(128)S(1)}, f32[16]{0:T(128)S(1)}, u32[]{:S(2)}, u32[]{:S(2)}) collective-permute-start(f32[16]{0:T(128)S(1)} %multiply_reduce_fusion), channel_id=1, source_target_pairs={{0,1},{1,0},{2,3},{3,2},{4,5},{5,4},{6,7},{7,6},{8,9},{9,8},{10,11... | collective-permute-start | bytes 200 | tf_op jit(solution)/shard_map/ppermute | solution.py:19
  128.7 2.0 %collective-permute-done.15 = f32[16]{0:T(128)S(1)} collective-permute-done((f32[16]{0:T(128)S(1)}, f32[16]{0:T(128)S(1)}, u32[]{:S(2)}, u32[]{:S(2)}) %collective-permute-start.15) | collective-permute-done | bytes 96 | tf_op jit(solution)/shard_map/ppermute | solution.py:19
  130.7 4.4 %collective-permute-done.16 = f32[16]{0:T(128)S(1)} collective-permute-done((f32[16]{0:T(128)S(1)}, f32[16]{0:T(128)S(1)}, u32[]{:S(2)}, u32[]{:S(2)}) %collective-permute-start.16) | collective-permute-done | bytes 96 | tf_op jit(solution)/shard_map/ppermute | solution.py:19
  135.2 1.1 collective-permute-done.17
  136.3 1.5 %collective-permute-start.18 = (f32[16]{0:T(128)S(1)}, f32[16]{0:T(128)S(1)}, u32[]{:S(2)}, u32[]{:S(2)}) collective-permute-start(f32[16]{0:T(128)S(1)} %add.185), channel_id=1, source_target_pairs={{0,8},{4,12},{8,0},{12,4},{16,24},{20,28},{24,16},{28,20},{1,9},{5... | collective-permute-start | bytes 200 | tf_op jit(solution)/shard_map/ppermute | solution.py:19
  137.8 2.1 %collective-permute-done.18 = f32[16]{0:T(128)S(1)} collective-permute-done((f32[16]{0:T(128)S(1)}, f32[16]{0:T(128)S(1)}, u32[]{:S(2)}, u32[]{:S(2)}) %collective-permute-start.18) | collective-permute-done | bytes 96 | tf_op jit(solution)/shard_map/ppermute | solution.py:19
  139.8 1.5 %collective-permute-start.19 = (f32[16]{0:T(128)S(1)}, f32[16]{0:T(128)S(1)}, u32[]{:S(2)}, u32[]{:S(2)}) collective-permute-start(f32[16]{0:T(128)S(1)} %add.186), channel_id=1, source_target_pairs={{0,16},{4,20},{8,24},{12,28},{16,0},{20,4},{24,8},{28,12},{1,17},{... | collective-permute-start | bytes 200 | tf_op jit(solution)/shard_map/ppermute | solution.py:19
  141.4 2.0 %collective-permute-done.19 = f32[16]{0:T(128)S(1)} collective-permute-done((f32[16]{0:T(128)S(1)}, f32[16]{0:T(128)S(1)}, u32[]{:S(2)}, u32[]{:S(2)}) %collective-permute-start.19) | collective-permute-done | bytes 96 | tf_op jit(solution)/shard_map/ppermute | solution.py:19
  143.4 0.8 multiply_subtract_fusion
  (96 shorter events, 10.4 us)
Async XLA Ops:
  0.6 1.3 copy-start
  0.6 17.7 %copy-start.5 = (s32[1,2,4]{2,1,0:T(2,128)S(1)}, s32[1,2,4]{2,1,0:T(2,128)}, u32[]{:S(2)}) copy-start(s32[1,2,4]{2,1,0:T(2,128)} %param.17) | copy-start | bytes 100
  1.9 22.6 %copy-start.1 = (f32[16,2048]{1,0:T(8,128)S(1)}, f32[16,2048]{1,0:T(8,128)}, u32[]{:S(2)}) copy-start(f32[16,2048]{1,0:T(8,128)} %param.12) | copy-start | bytes 393220
  4.2 37.0 %collective-permute-start = (f32[6,16,128]{2,1,0:T(8,128)S(1)}, f32[6,16,128]{2,1,0:T(8,128)S(1)}, u32[]{:S(2)}, u32[]{:S(2)}) collective-permute-start(f32[6,16,128]{2,1,0:T(8,128)S(1)} %pad_maximum_fusion.2), channel_id=1, source_target_pairs={{0,1},{1,0},{2,3},{3,2},{4,5},{5,4},{6,7},{7,6},{8,9},{9,8},{10,11... | collective-permute-start | bytes 147464 | tf_op jit(solution)/shard_map/ppermute | solution.py:19
  41.1 29.1 %copy-start.2 = (f32[5,128,128]{2,1,0:T(8,128)S(1)}, f32[5,128,128]{2,1,0:T(8,128)}, u32[]{:S(2)}) copy-start(f32[5,128,128]{2,1,0:T(8,128)} %param.15) | copy-start | bytes 983044
  41.1 30.1 %copy-start.3 = (f32[5,2048]{1,0:T(8,128)S(1)}, f32[5,2048]{1,0:T(8,128)}, u32[]{:S(2)}) copy-start(f32[5,2048]{1,0:T(8,128)} %param.14) | copy-start | bytes 122884
  41.1 30.9 %copy-start.4 = (f32[2048]{0:T(1024)S(1)}, f32[2048]{0:T(1024)}, u32[]{:S(2)}) copy-start(f32[2048]{0:T(1024)} %param.11) | copy-start | bytes 24580
  41.2 5.0 %collective-permute-start.1 = (f32[5,16,128]{2,1,0:T(8,128)S(1)}, f32[5,16,128]{2,1,0:T(8,128)S(1)}, u32[]{:S(2)}, u32[]{:S(2)}) collective-permute-start(f32[5,16,128]{2,1,0:T(8,128)S(1)} %slice.134), channel_id=1, source_target_pairs={{0,2},{1,3},{2,0},{3,1},{4,6},{5,7},{6,4},{7,5},{8,10},{9,11},{10,... | collective-permute-start | bytes 122888 | tf_op jit(solution)/shard_map/ppermute | solution.py:19
  46.2 8.7 %collective-permute-start.2 = (f32[4,16,128]{2,1,0:T(8,128)S(1)}, f32[4,16,128]{2,1,0:T(8,128)S(1)}, u32[]{:S(2)}, u32[]{:S(2)}) collective-permute-start(f32[4,16,128]{2,1,0:T(8,128)S(1)} %slice.135), channel_id=1, source_target_pairs={{0,4},{4,0},{8,12},{12,8},{16,20},{20,16},{24,28},{28,24},{1,5},{5... | collective-permute-start | bytes 98312 | tf_op jit(solution)/shard_map/ppermute | solution.py:19
  54.9 3.9 %collective-permute-start.3 = (f32[3,16,128]{2,1,0:T(8,128)S(1)}, f32[3,16,128]{2,1,0:T(8,128)S(1)}, u32[]{:S(2)}, u32[]{:S(2)}) collective-permute-start(f32[3,16,128]{2,1,0:T(8,128)S(1)} %slice.136), channel_id=1, source_target_pairs={{0,8},{4,12},{8,0},{12,4},{16,24},{20,28},{24,16},{28,20},{1,9},{5... | collective-permute-start | bytes 73736 | tf_op jit(solution)/shard_map/ppermute | solution.py:19
  58.8 11.4 %collective-permute-start.4 = (f32[2,16,128]{2,1,0:T(8,128)S(1)}, f32[2,16,128]{2,1,0:T(8,128)S(1)}, u32[]{:S(2)}, u32[]{:S(2)}) collective-permute-start(f32[2,16,128]{2,1,0:T(8,128)S(1)} %slice.137), channel_id=1, source_target_pairs={{0,16},{4,20},{8,24},{12,28},{16,0},{20,4},{24,8},{28,12},{1,17},{... | collective-permute-start | bytes 49160 | tf_op jit(solution)/shard_map/ppermute | solution.py:19
  72.1 3.6 %collective-permute-start.5 = (f32[16]{0:T(128)S(1)}, f32[16]{0:T(128)S(1)}, u32[]{:S(2)}, u32[]{:S(2)}) collective-permute-start(f32[16]{0:T(128)S(1)} %multiply_reduce_fusion.2), channel_id=1, source_target_pairs={{0,1},{1,0},{2,3},{3,2},{4,5},{5,4},{6,7},{7,6},{8,9},{9,8},{10,11... | collective-permute-start | bytes 200 | tf_op jit(solution)/shard_map/ppermute | solution.py:19
  75.7 4.4 %collective-permute-start.6 = (f32[16]{0:T(128)S(1)}, f32[16]{0:T(128)S(1)}, u32[]{:S(2)}, u32[]{:S(2)}) collective-permute-start(f32[16]{0:T(128)S(1)} %add.166), channel_id=1, source_target_pairs={{0,2},{1,3},{2,0},{3,1},{4,6},{5,7},{6,4},{7,5},{8,10},{9,11},{10,... | collective-permute-start | bytes 200 | tf_op jit(solution)/shard_map/ppermute | solution.py:19
  80.2 1.1 collective-permute-start.7
  81.3 3.5 %collective-permute-start.8 = (f32[16]{0:T(128)S(1)}, f32[16]{0:T(128)S(1)}, u32[]{:S(2)}, u32[]{:S(2)}) collective-permute-start(f32[16]{0:T(128)S(1)} %add.168), channel_id=1, source_target_pairs={{0,8},{4,12},{8,0},{12,4},{16,24},{20,28},{24,16},{28,20},{1,9},{5... | collective-permute-start | bytes 200 | tf_op jit(solution)/shard_map/ppermute | solution.py:19
  84.9 3.5 %collective-permute-start.9 = (f32[16]{0:T(128)S(1)}, f32[16]{0:T(128)S(1)}, u32[]{:S(2)}, u32[]{:S(2)}) collective-permute-start(f32[16]{0:T(128)S(1)} %add.169), channel_id=1, source_target_pairs={{0,16},{4,20},{8,24},{12,28},{16,0},{20,4},{24,8},{28,12},{1,17},{... | collective-permute-start | bytes 200 | tf_op jit(solution)/shard_map/ppermute | solution.py:19
  89.9 10.8 %collective-permute-start.10 = (f32[6,16,128]{2,1,0:T(8,128)S(1)}, f32[6,16,128]{2,1,0:T(8,128)S(1)}, u32[]{:S(2)}, u32[]{:S(2)}) collective-permute-start(f32[6,16,128]{2,1,0:T(8,128)S(1)} %pad_maximum_fusion.3), channel_id=1, source_target_pairs={{0,1},{1,0},{2,3},{3,2},{4,5},{5,4},{6,7},{7,6},{8,9},{9,8},{10,11... | collective-permute-start | bytes 147464 | tf_op jit(solution)/shard_map/ppermute | solution.py:19
  100.7 8.7 %collective-permute-start.11 = (f32[5,16,128]{2,1,0:T(8,128)S(1)}, f32[5,16,128]{2,1,0:T(8,128)S(1)}, u32[]{:S(2)}, u32[]{:S(2)}) collective-permute-start(f32[5,16,128]{2,1,0:T(8,128)S(1)} %slice.142), channel_id=1, source_target_pairs={{0,2},{1,3},{2,0},{3,1},{4,6},{5,7},{6,4},{7,5},{8,10},{9,11},{10,... | collective-permute-start | bytes 122888 | tf_op jit(solution)/shard_map/ppermute | solution.py:19
  109.4 1.3 collective-permute-start.12
  110.7 3.9 %collective-permute-start.13 = (f32[3,16,128]{2,1,0:T(8,128)S(1)}, f32[3,16,128]{2,1,0:T(8,128)S(1)}, u32[]{:S(2)}, u32[]{:S(2)}) collective-permute-start(f32[3,16,128]{2,1,0:T(8,128)S(1)} %slice.144), channel_id=1, source_target_pairs={{0,8},{4,12},{8,0},{12,4},{16,24},{20,28},{24,16},{28,20},{1,9},{5... | collective-permute-start | bytes 73736 | tf_op jit(solution)/shard_map/ppermute | solution.py:19
  114.6 10.4 %collective-permute-start.14 = (f32[2,16,128]{2,1,0:T(8,128)S(1)}, f32[2,16,128]{2,1,0:T(8,128)S(1)}, u32[]{:S(2)}, u32[]{:S(2)}) collective-permute-start(f32[2,16,128]{2,1,0:T(8,128)S(1)} %slice.145), channel_id=1, source_target_pairs={{0,16},{4,20},{8,24},{12,28},{16,0},{20,4},{24,8},{28,12},{1,17},{... | collective-permute-start | bytes 49160 | tf_op jit(solution)/shard_map/ppermute | solution.py:19
  127.1 3.6 %collective-permute-start.15 = (f32[16]{0:T(128)S(1)}, f32[16]{0:T(128)S(1)}, u32[]{:S(2)}, u32[]{:S(2)}) collective-permute-start(f32[16]{0:T(128)S(1)} %multiply_reduce_fusion), channel_id=1, source_target_pairs={{0,1},{1,0},{2,3},{3,2},{4,5},{5,4},{6,7},{7,6},{8,9},{9,8},{10,11... | collective-permute-start | bytes 200 | tf_op jit(solution)/shard_map/ppermute | solution.py:19
  130.7 4.4 %collective-permute-start.16 = (f32[16]{0:T(128)S(1)}, f32[16]{0:T(128)S(1)}, u32[]{:S(2)}, u32[]{:S(2)}) collective-permute-start(f32[16]{0:T(128)S(1)} %add.183), channel_id=1, source_target_pairs={{0,2},{1,3},{2,0},{3,1},{4,6},{5,7},{6,4},{7,5},{8,10},{9,11},{10,... | collective-permute-start | bytes 200 | tf_op jit(solution)/shard_map/ppermute | solution.py:19
  135.2 1.1 collective-permute-start.17
  136.3 3.5 %collective-permute-start.18 = (f32[16]{0:T(128)S(1)}, f32[16]{0:T(128)S(1)}, u32[]{:S(2)}, u32[]{:S(2)}) collective-permute-start(f32[16]{0:T(128)S(1)} %add.185), channel_id=1, source_target_pairs={{0,8},{4,12},{8,0},{12,4},{16,24},{20,28},{24,16},{28,20},{1,9},{5... | collective-permute-start | bytes 200 | tf_op jit(solution)/shard_map/ppermute | solution.py:19
  139.8 3.5 %collective-permute-start.19 = (f32[16]{0:T(128)S(1)}, f32[16]{0:T(128)S(1)}, u32[]{:S(2)}, u32[]{:S(2)}) collective-permute-start(f32[16]{0:T(128)S(1)} %add.186), channel_id=1, source_target_pairs={{0,16},{4,20},{8,24},{12,28},{16,0},{20,4},{24,8},{28,12},{1,17},{... | collective-permute-start | bytes 200 | tf_op jit(solution)/shard_map/ppermute | solution.py:19

commit v3 on v2

--- a/solution.py
+++ b/solution.py
@@ -63,22 +63,22 @@
 def per_device(coords, inv_scale, noise, right_side, basis, level_gain, coupling, order, pairs):
     perm = order[0]
     columns, points = right_side.shape
+    features = coords.shape[0]
     tiles = points // TILE_POINTS
     levels = level_gain.shape[0]
     rank = basis.shape[0]
     pair_rows = pairs[0, 0]
     pair_cols = pairs[0, 1]
-    inverse = jnp.zeros_like(perm).at[perm].set(jnp.arange(points, dtype=jnp.int32))
-    tile_coords = (coords * inv_scale[:, None])[:, perm].reshape(
-        coords.shape[0], tiles, TILE_POINTS
-    )
+    position = jnp.arange(points, dtype=jnp.int32)
+    inverse = jnp.sum(jnp.where(perm[:, None] == position[None, :], position[:, None], 0), axis=0)
+    stacked = jnp.concatenate([coords * inv_scale[:, None], right_side], axis=0)[:, perm]
+    tile_coords = stacked[:features].reshape(features, tiles, TILE_POINTS)
     kern = near_kernels(tile_coords, pair_rows, pair_cols)
     scales = 2.0 ** ((1.0 - jnp.arange(levels, dtype=jnp.float32)) / 2.0)
 
-    def near_of(values):
-        tile_vec = values[:, perm].reshape(columns, tiles, TILE_POINTS)
-        near_t = near_apply(kern, tile_vec, pair_rows, pair_cols).reshape(columns, points)
-        return near_t[:, inverse]
+    def near_tiles(values_t):
+        tile_vec = values_t.reshape(columns, tiles, TILE_POINTS)
+        return near_apply(kern, tile_vec, pair_rows, pair_cols).reshape(columns, points)
 
     def sums_with_norm(values):
         proj = jnp.einsum("lp,cp,rp->lcr", level_gain, values, basis, precision=highest)
@@ -90,17 +90,24 @@
     solution = jnp.zeros_like(right_side)
     residual = right_side
     direction = right_side
+    direction_t = stacked[features:]
     for step in range(ITERATIONS):
         if step == 0:
             nodesum, norm_now = sums_with_norm(residual)
-            near = near_of(direction)
+            near_t = near_tiles(direction_t)
+            late_t, nodesum = lax.optimization_barrier((near_t, nodesum))
+            near = late_t[:, inverse]
         else:
             residual_sum, norm_next = sums_with_norm(residual)
-            residual_near = near_of(residual)
+            residual_t = residual[:, perm]
+            residual_near_t = near_tiles(residual_t)
+            late_t, residual_sum = lax.optimization_barrier((residual_near_t, residual_sum))
             ratio = norm_next / norm_now
             direction = residual + ratio[:, None] * direction
+            direction_t = residual_t + ratio[:, None] * direction_t
             nodesum = residual_sum + ratio[None, :, None] * nodesum
-            near = residual_near + ratio[:, None] * near
+            near_t = residual_near_t + ratio[:, None] * near_t
+            near = late_t[:, inverse] + ratio[:, None] * near
             norm_now = norm_next
         coupled = jnp.einsum("lcr,lrs->lcs", nodesum, coupling, precision=highest)
         coupled = (
@@ -108,11 +115,12 @@
         )
         back = jnp.einsum("lcr,rp->lcp", coupled, basis, precision=highest)
         far = jnp.sum(back * level_gain[:, None, :], axis=0)
-        image = noise[None, :] * direction + far + near
-        curve = butterfly(jnp.sum(direction * image, axis=1))
+        base = noise[None, :] * direction + far
+        local = jnp.sum(direction * base, axis=1) + jnp.sum(direction_t * near_t, axis=1)
+        curve = butterfly(local)
         alpha = norm_now / curve
         solution = solution + alpha[:, None] * direction
-        residual = residual - alpha[:, None] * image
+        residual = residual - alpha[:, None] * (base + near)
     return (solution, residual)
 
 

time: 145 us -> 127 us (0.88)
  local copies, waits for them, and re-layouts: 59.4 us -> 41.7 us
  waiting for transfers between devices: 30.8 us -> 26.4 us
  other arithmetic: 4.5 us -> 7.29 us
  starting transfers between devices: 23.4 us -> 24.9 us
    scatter x1 -> x0, local copies, waits for them, and re-layouts: 8.23 us -> none  [per_device(): jnp.zeros_like(perm).at[perm].set(jnp.arange(points, dtype=jnp.int32))]
    reshape x5 -> x2, local copies, waits for them, and re-layouts: 5.26 us -> 0.03 us  [near_tiles(): tile_vec = values_t.reshape(columns, tiles, TILE_POINTS)]
    gather x7 -> x8, local copies, waits for them, and re-layouts: 41 us -> 36.4 us  [the longest x2 9.1 us: per_device(): jnp.concatenate([coords * inv_scale[:, None], right_side], axis=0)[:, perm]]
    ppermute x20, waiting for transfers between devices: 30.8 us -> 26.4 us  [swapped(): return lax.ppermute(value, axis, pairs)]
    reduce_sum x2 -> x4, other arithmetic: 0.37 us -> 2.25 us  [the longest x1 1.73 us: per_device(): jnp.sum(jnp.where(perm[:, None] == position[None, :], position[:, None],...]
    ppermute x20, starting transfers between devices: 23.4 us -> 24.9 us  [swapped(): return lax.ppermute(value, axis, pairs)]
  transfers between devices with their start and end apart: 20 -> 20, of which waited for: 14 -> 15; matrix products, arithmetic and copies ran while one was open for 55% -> 51% of each run, Pallas kernels for 0% -> 0%
where the time goes in v3:
time: 127 us
  local copies, waits for them, and re-layouts  41.7 us (33%)
  waiting for transfers between devices  26.4 us (21%)
  matrix products  25.3 us (20%)
  starting transfers between devices  24.9 us (20%)
  other arithmetic  7.29 us (6%)
    ppermute x20, waiting for transfers between devices, swapped(): return lax.ppermute(value, axis, pairs)  26.4 us
    ppermute x20, starting transfers between devices, swapped(): return lax.ppermute(value, axis, pairs)  24.9 us
    dot_general x2, matrix products, near_apply(): result = jnp.einsum('gij,cgj->cgi', kern, union_vec, precision=highest)  12.2 us
    gather x2, local copies, waits for them, and re-layouts, per_device(): jnp.concatenate([coords * inv_scale[:, None], right_side], axis=0)[:, perm]  9.1 us
    gather x2, local copies, waits for them, and re-layouts, per_device(): residual_t = residual[:, perm]  9.1 us
    gather x2, local copies, waits for them, and re-layouts, per_device(): near = late_t[:, inverse] + ratio[:, None] * near  9.09 us
    gather x2, local copies, waits for them, and re-layouts, per_device(): near = late_t[:, inverse]  9.09 us
    dot_general x1, matrix products, near_kernels(): gram = jnp.einsum('fgi,fgj->gij', union, union, precision=highest)  5.01 us
  transfers between devices with their start and end apart: 20, of which 15 were waited for; matrix products, arithmetic and copies ran while one was open for 51% of the time, Pallas kernels for 0%

profile of v3, /device:TPU:0, one launch (start us, length us, event | category | flops | bytes accessed | tf_op | source)
XLA Modules:
  0.0 126.6 jit_solution(10770004315815871603)
XLA Ops:
  0.7 1.1 multiply_reduce_fusion.4
  1.9 2.1 %convolution_bitcast_fusion.1 = f32[5,16,128]{2,1,0:T(8,128)S(1)} fusion(f32[128,2048]{1,0:T(8,128)S(1)} %copy-done, f32[2048,5]{0,1:T(8,128)} %bitcast.119, f32[2048,16]{0,1:T(8,128)} %bitcast.107), kind=kOutput, calls=%fused_computation.34 | convolution fusion | flops 251822080 | bytes 1261568 | tf_op jit(solution)/shard_map/lp,cp,rp->lcr/dot_general | solution.py:84
  4.1 3.0 %collective-permute-start = (f32[6,16,128]{2,1,0:T(8,128)S(1)}, f32[6,16,128]{2,1,0:T(8,128)S(1)}, u32[]{:S(2)}, u32[]{:S(2)}) collective-permute-start(f32[6,16,128]{2,1,0:T(8,128)S(1)} %pad_maximum_fusion.3), channel_id=1, source_target_pairs={{0,1},{1,0},{2,3},{3,2},{4,5},{5,4},{6,7},{7,6},{8,9},{9,8},{10,11... | collective-permute-start | bytes 147464 | tf_op jit(solution)/shard_map/ppermute | solution.py:19
  7.2 0.9 broadcast_multiply_fusion
  8.1 0.9 pad_maximum_fusion
  9.3 0.7 compare_select_fusion.1
  10.1 7.6 %gather_fusion = f32[2048,24]{1,0:T(8,128)} fusion(f32[24,2048]{0,1:T(8,128)S(1)} %copy.121, s32[2048]{0:T(1024)S(1)} %broadcast_clamp_fusion.1), kind=kCustom, calls=%fused_computation | custom fusion | bytes 401408 | tf_op jit(solution)/shard_map/gather | solution.py:74
  17.7 1.5 %copy.122 = f32[2048,24]{0,1:T(8,128)S(1)} copy(f32[2048,24]{1,0:T(8,128)} %gather_fusion) | data formatting | bytes 393216 | tf_op jit(solution)/shard_map/gather | solution.py:74
  20.4 5.0 %fusion.47 = f32[4,512,512]{2,1,0:T(8,128)} fusion(f32[8,4,256]{2,0,1:T(8,128)S(1)} %bitcast.128, f32[8,4,256]{2,0,1:T(8,128)S(1)} %bitcast.130), kind=kOutput, calls=%fused_computation.86 | convolution fusion | flops 100679680 | bytes 4259840 | tf_op jit(solution)/shard_map/fgi,fgj->gij/dot_general | solution.py:24
  26.6 6.1 %fusion.14 = f32[16,4,512]{2,0,1:T(8,128)S(1)} fusion(f32[4,512,512]{2,1,0:T(8,128)} %fusion.47, f32[4,512]{1,0:T(4,128)S(1)} %multiply_reduce_fusion.5, f32[16,4,256]{2,0,1:T(8,128)S(1)} %bitcast.136, f32[16,4,256]{2,0,1:T(8,128)S(1)} %bitcast.137), kind=kOutput, calls=%fused_computation.31 | convolution fusion | flops 206602240 | bytes 4464640 | tf_op jit(solution)/shard_map/gij,cgj->cgi/dot_general | solution.py:33
  32.7 1.7 %select_reduce_fusion = s32[2048]{0:T(1024)S(1)} fusion(s32[2048]{0:T(1024)S(1)} %bitcast.140), kind=kLoop, calls=%fused_computation.10 | loop fusion | flops 12580864 | bytes 16384 | tf_op jit(solution)/shard_map/reduce_sum | solution.py:73
  34.5 2.7 %collective-permute-start.1 = (f32[5,16,128]{2,1,0:T(8,128)S(1)}, f32[5,16,128]{2,1,0:T(8,128)S(1)}, u32[]{:S(2)}, u32[]{:S(2)}) collective-permute-start(f32[5,16,128]{2,1,0:T(8,128)S(1)} %slice.140), channel_id=1, source_target_pairs={{0,2},{1,3},{2,0},{3,1},{4,6},{5,7},{6,4},{7,5},{8,10},{9,11},{10,... | collective-permute-start | bytes 122888 | tf_op jit(solution)/shard_map/ppermute | solution.py:19
  37.5 2.0 %collective-permute-done.1 = f32[5,16,128]{2,1,0:T(8,128)S(1)} collective-permute-done((f32[5,16,128]{2,1,0:T(8,128)S(1)}, f32[5,16,128]{2,1,0:T(8,128)S(1)}, u32[]{:S(2)}, u32[]{:S(2)}) %collective-permute-start.1) | collective-permute-done | bytes 40992 | tf_op jit(solution)/shard_map/ppermute | solution.py:19
  39.9 0.8 collective-permute-done.2
  40.8 1.9 %collective-permute-start.3 = (f32[3,16,128]{2,1,0:T(8,128)S(1)}, f32[3,16,128]{2,1,0:T(8,128)S(1)}, u32[]{:S(2)}, u32[]{:S(2)}) collective-permute-start(f32[3,16,128]{2,1,0:T(8,128)S(1)} %slice.142), channel_id=1, source_target_pairs={{0,8},{4,12},{8,0},{12,4},{16,24},{20,28},{24,16},{28,20},{1,9},{5... | collective-permute-start | bytes 73736 | tf_op jit(solution)/shard_map/ppermute | solution.py:19
  42.8 1.9 %collective-permute-done.3 = f32[3,16,128]{2,1,0:T(8,128)S(1)} collective-permute-done((f32[3,16,128]{2,1,0:T(8,128)S(1)}, f32[3,16,128]{2,1,0:T(8,128)S(1)}, u32[]{:S(2)}, u32[]{:S(2)}) %collective-permute-start.3) | collective-permute-done | bytes 24608 | tf_op jit(solution)/shard_map/ppermute | solution.py:19
  44.7 1.9 %collective-permute-start.4 = (f32[2,16,128]{2,1,0:T(8,128)S(1)}, f32[2,16,128]{2,1,0:T(8,128)S(1)}, u32[]{:S(2)}, u32[]{:S(2)}) collective-permute-start(f32[2,16,128]{2,1,0:T(8,128)S(1)} %slice.143), channel_id=1, source_target_pairs={{0,16},{4,20},{8,24},{12,28},{16,0},{20,4},{24,8},{28,12},{1,17},{... | collective-permute-start | bytes 49160 | tf_op jit(solution)/shard_map/ppermute | solution.py:19
  46.6 1.9 %collective-permute-done.4 = f32[2,16,128]{2,1,0:T(8,128)S(1)} collective-permute-done((f32[2,16,128]{2,1,0:T(8,128)S(1)}, f32[2,16,128]{2,1,0:T(8,128)S(1)}, u32[]{:S(2)}, u32[]{:S(2)}) %collective-permute-start.4) | collective-permute-done | bytes 16416 | tf_op jit(solution)/shard_map/ppermute | solution.py:19
  48.9 0.6 convolution_multiply_fusion.3
  49.5 0.8 fusion.12
  50.6 3.4 %collective-permute-done.5 = f32[16]{0:T(128)S(1)} collective-permute-done((f32[16]{0:T(128)S(1)}, f32[16]{0:T(128)S(1)}, u32[]{:S(2)}, u32[]{:S(2)}) %collective-permute-start.5) | collective-permute-done | bytes 96 | tf_op jit(solution)/shard_map/ppermute | solution.py:19
  54.0 2.6 %collective-permute-start.6 = (f32[16]{0:T(128)S(1)}, f32[16]{0:T(128)S(1)}, u32[]{:S(2)}, u32[]{:S(2)}) collective-permute-start(f32[16]{0:T(128)S(1)} %add.182), channel_id=1, source_target_pairs={{0,2},{1,3},{2,0},{3,1},{4,6},{5,7},{6,4},{7,5},{8,10},{9,11},{10,... | collective-permute-start | bytes 200 | tf_op jit(solution)/shard_map/ppermute | solution.py:19
  56.7 1.7 %collective-permute-done.6 = f32[16]{0:T(128)S(1)} collective-permute-done((f32[16]{0:T(128)S(1)}, f32[16]{0:T(128)S(1)}, u32[]{:S(2)}, u32[]{:S(2)}) %collective-permute-start.6) | collective-permute-done | bytes 96 | tf_op jit(solution)/shard_map/ppermute | solution.py:19
  58.8 0.8 collective-permute-done.7
  59.6 1.8 %collective-permute-start.8 = (f32[16]{0:T(128)S(1)}, f32[16]{0:T(128)S(1)}, u32[]{:S(2)}, u32[]{:S(2)}) collective-permute-start(f32[16]{0:T(128)S(1)} %add.184), channel_id=1, source_target_pairs={{0,8},{4,12},{8,0},{12,4},{16,24},{20,28},{24,16},{28,20},{1,9},{5... | collective-permute-start | bytes 200 | tf_op jit(solution)/shard_map/ppermute | solution.py:19
  61.4 7.6 %gather_fusion.5 = f32[2048,16]{1,0:T(8,128)} fusion(f32[16,2048]{0,1:T(8,128)S(1)} %copy.127, s32[2048]{0:T(1024)S(1)} %broadcast_clamp_fusion), kind=kCustom, calls=%fused_computation.5 | custom fusion | bytes 270336 | tf_op jit(solution)/shard_map/gather | solution.py:99
  69.0 1.6 %collective-permute-start.9 = (f32[16]{0:T(128)S(1)}, f32[16]{0:T(128)S(1)}, u32[]{:S(2)}, u32[]{:S(2)}) collective-permute-start(f32[16]{0:T(128)S(1)} %add.185), channel_id=1, source_target_pairs={{0,16},{4,20},{8,24},{12,28},{16,0},{20,4},{24,8},{28,12},{1,17},{... | collective-permute-start | bytes 200 | tf_op jit(solution)/shard_map/ppermute | solution.py:19
  70.6 1.5 %copy.128 = f32[2048,16]{0,1:T(8,128)S(1)} copy(f32[2048,16]{1,0:T(8,128)} %gather_fusion.5) | data formatting | bytes 262144 | tf_op jit(solution)/shard_map/gather | solution.py:99
  72.8 1.2 convolution_bitcast_fusion
  74.6 7.6 %gather_fusion.6 = f32[2048,16]{1,0:T(8,128)} fusion(f32[16,2048]{0,1:T(8,128)S(1)} %copy.129, s32[2048]{0:T(1024)S(1)} %broadcast_clamp_fusion.1), kind=kCustom, calls=%fused_computation.6 | custom fusion | bytes 270336 | tf_op jit(solution)/shard_map/gather | solution.py:102
  82.2 1.5 %copy.130 = f32[2048,16]{0,1:T(8,128)S(1)} copy(f32[2048,16]{1,0:T(8,128)} %gather_fusion.6) | data formatting | bytes 262144 | tf_op jit(solution)/shard_map/gather | solution.py:102
  84.9 2.7 %collective-permute-start.11 = (f32[5,16,128]{2,1,0:T(8,128)S(1)}, f32[5,16,128]{2,1,0:T(8,128)S(1)}, u32[]{:S(2)}, u32[]{:S(2)}) collective-permute-start(f32[5,16,128]{2,1,0:T(8,128)S(1)} %slice.150), channel_id=1, source_target_pairs={{0,2},{1,3},{2,0},{3,1},{4,6},{5,7},{6,4},{7,5},{8,10},{9,11},{10,... | collective-permute-start | bytes 122888 | tf_op jit(solution)/shard_map/ppermute | solution.py:19
  87.5 6.1 %fusion.15 = f32[16,4,512]{2,0,1:T(8,128)S(1)} fusion(f32[4,512,512]{2,1,0:T(8,128)} %fusion.47, f32[4,512]{1,0:T(4,128)S(1)} %multiply_reduce_fusion.5, f32[16,4,256]{2,0,1:T(8,128)S(1)} %bitcast.134, f32[16,4,256]{2,0,1:T(8,128)S(1)} %bitcast.135), kind=kOutput, calls=%fused_computation.32 | convolution fusion | flops 206602240 | bytes 4464640 | tf_op jit(solution)/shard_map/gij,cgj->cgi/dot_general | solution.py:33
  93.8 1.2 collective-permute-done.12
  95.0 0.6 collective-permute-start.13
  95.9 3.0 %collective-permute-done.13 = f32[3,16,128]{2,1,0:T(8,128)S(1)} collective-permute-done((f32[3,16,128]{2,1,0:T(8,128)S(1)}, f32[3,16,128]{2,1,0:T(8,128)S(1)}, u32[]{:S(2)}, u32[]{:S(2)}) %collective-permute-start.13) | collective-permute-done | bytes 24608 | tf_op jit(solution)/shard_map/ppermute | solution.py:19
  98.9 1.6 %collective-permute-start.14 = (f32[2,16,128]{2,1,0:T(8,128)S(1)}, f32[2,16,128]{2,1,0:T(8,128)S(1)}, u32[]{:S(2)}, u32[]{:S(2)}) collective-permute-start(f32[2,16,128]{2,1,0:T(8,128)S(1)} %slice.153), channel_id=1, source_target_pairs={{0,16},{4,20},{8,24},{12,28},{16,0},{20,4},{24,8},{28,12},{1,17},{... | collective-permute-start | bytes 49160 | tf_op jit(solution)/shard_map/ppermute | solution.py:19
  100.8 1.8 %collective-permute-done.14 = f32[2,16,128]{2,1,0:T(8,128)S(1)} collective-permute-done((f32[2,16,128]{2,1,0:T(8,128)S(1)}, f32[2,16,128]{2,1,0:T(8,128)S(1)}, u32[]{:S(2)}, u32[]{:S(2)}) %collective-permute-start.14) | collective-permute-done | bytes 16416 | tf_op jit(solution)/shard_map/ppermute | solution.py:19
  103.2 0.6 convolution_multiply_fusion.2
  103.9 0.8 fusion.13
  104.9 1.6 %collective-permute-start.15 = (f32[16]{0:T(128)S(1)}, f32[16]{0:T(128)S(1)}, u32[]{:S(2)}, u32[]{:S(2)}) collective-permute-start(f32[16]{0:T(128)S(1)} %add.201), channel_id=1, source_target_pairs={{0,1},{1,0},{2,3},{3,2},{4,5},{5,4},{6,7},{7,6},{8,9},{9,8},{10,11... | collective-permute-start | bytes 200 | tf_op jit(solution)/shard_map/ppermute | solution.py:19
  106.5 2.0 %collective-permute-done.15 = f32[16]{0:T(128)S(1)} collective-permute-done((f32[16]{0:T(128)S(1)}, f32[16]{0:T(128)S(1)}, u32[]{:S(2)}, u32[]{:S(2)}) %collective-permute-start.15) | collective-permute-done | bytes 96 | tf_op jit(solution)/shard_map/ppermute | solution.py:19
  108.8 4.1 %collective-permute-done.16 = f32[16]{0:T(128)S(1)} collective-permute-done((f32[16]{0:T(128)S(1)}, f32[16]{0:T(128)S(1)}, u32[]{:S(2)}, u32[]{:S(2)}) %collective-permute-start.16) | collective-permute-done | bytes 96 | tf_op jit(solution)/shard_map/ppermute | solution.py:19
  113.3 0.8 collective-permute-done.17
  114.6 7.6 %gather_fusion.9 = f32[2048,16]{1,0:T(8,128)} fusion(f32[16,2048]{0,1:T(8,128)S(1)} %copy.135, s32[2048]{0:T(1024)S(1)} %broadcast_clamp_fusion), kind=kCustom, calls=%fused_computation.9 | custom fusion | bytes 270336 | tf_op jit(solution)/shard_map/gather | solution.py:110
  122.2 1.6 %collective-permute-start.19 = (f32[16]{0:T(128)S(1)}, f32[16]{0:T(128)S(1)}, u32[]{:S(2)}, u32[]{:S(2)}) collective-permute-start(f32[16]{0:T(128)S(1)} %add.205), channel_id=1, source_target_pairs={{0,16},{4,20},{8,24},{12,28},{16,0},{20,4},{24,8},{28,12},{1,17},{... | collective-permute-start | bytes 200 | tf_op jit(solution)/shard_map/ppermute | solution.py:19
  123.8 1.5 %copy.136 = f32[2048,16]{0,1:T(8,128)S(1)} copy(f32[2048,16]{1,0:T(8,128)} %gather_fusion.9) | data formatting | bytes 262144 | tf_op jit(solution)/shard_map/gather | solution.py:110
  125.8 0.8 fusion.36
  (106 shorter events, 10.7 us)
Async XLA Ops:
  0.6 1.3 %copy-start = (f32[128,2048]{1,0:T(8,128)S(1)}, f32[128,2048]{1,0:T(8,128)}, u32[]{:S(2)}) copy-start(f32[128,2048]{1,0:T(8,128)} %param.13) | copy-start | bytes 3145732
  0.6 18.6 %copy-start.6 = (s32[1,2,4]{2,1,0:T(2,128)S(1)}, s32[1,2,4]{2,1,0:T(2,128)}, u32[]{:S(2)}) copy-start(s32[1,2,4]{2,1,0:T(2,128)} %param.17) | copy-start | bytes 100
  4.1 30.3 %collective-permute-start = (f32[6,16,128]{2,1,0:T(8,128)S(1)}, f32[6,16,128]{2,1,0:T(8,128)S(1)}, u32[]{:S(2)}, u32[]{:S(2)}) collective-permute-start(f32[6,16,128]{2,1,0:T(8,128)S(1)} %pad_maximum_fusion.3), channel_id=1, source_target_pairs={{0,1},{1,0},{2,3},{3,2},{4,5},{5,4},{6,7},{7,6},{8,9},{9,8},{10,11... | collective-permute-start | bytes 147464 | tf_op jit(solution)/shard_map/ppermute | solution.py:19
  25.4 7.3 %copy-start.5 = (s32[1,2048]{1,0:T(1,128)S(1)}, s32[1,2048]{1,0:T(1,128)}, u32[]{:S(2)}) copy-start(s32[1,2048]{1,0:T(1,128)} %param.16) | copy-start | bytes 24580
  26.6 21.9 %copy-start.2 = (f32[5,128,128]{2,1,0:T(8,128)S(1)}, f32[5,128,128]{2,1,0:T(8,128)}, u32[]{:S(2)}) copy-start(f32[5,128,128]{2,1,0:T(8,128)} %param.15) | copy-start | bytes 983044
  26.6 22.9 %copy-start.3 = (f32[5,2048]{1,0:T(8,128)S(1)}, f32[5,2048]{1,0:T(8,128)}, u32[]{:S(2)}) copy-start(f32[5,2048]{1,0:T(8,128)} %param.14) | copy-start | bytes 122884
  26.6 23.7 %copy-start.1 = (f32[16,2048]{1,0:T(8,128)S(1)}, f32[16,2048]{1,0:T(8,128)}, u32[]{:S(2)}) copy-start(f32[16,2048]{1,0:T(8,128)} %param.12) | copy-start | bytes 393220
  26.6 23.7 %copy-start.4 = (f32[2048]{0:T(1024)S(1)}, f32[2048]{0:T(1024)}, u32[]{:S(2)}) copy-start(f32[2048]{0:T(1024)} %param.11) | copy-start | bytes 24580
  34.5 5.0 %collective-permute-start.1 = (f32[5,16,128]{2,1,0:T(8,128)S(1)}, f32[5,16,128]{2,1,0:T(8,128)S(1)}, u32[]{:S(2)}, u32[]{:S(2)}) collective-permute-start(f32[5,16,128]{2,1,0:T(8,128)S(1)} %slice.140), channel_id=1, source_target_pairs={{0,2},{1,3},{2,0},{3,1},{4,6},{5,7},{6,4},{7,5},{8,10},{9,11},{10,... | collective-permute-start | bytes 122888 | tf_op jit(solution)/shard_map/ppermute | solution.py:19
  39.5 1.3 %collective-permute-start.2 = (f32[4,16,128]{2,1,0:T(8,128)S(1)}, f32[4,16,128]{2,1,0:T(8,128)S(1)}, u32[]{:S(2)}, u32[]{:S(2)}) collective-permute-start(f32[4,16,128]{2,1,0:T(8,128)S(1)} %slice.141), channel_id=1, source_target_pairs={{0,4},{4,0},{8,12},{12,8},{16,20},{20,16},{24,28},{28,24},{1,5},{5... | collective-permute-start | bytes 98312 | tf_op jit(solution)/shard_map/ppermute | solution.py:19
  40.8 3.9 %collective-permute-start.3 = (f32[3,16,128]{2,1,0:T(8,128)S(1)}, f32[3,16,128]{2,1,0:T(8,128)S(1)}, u32[]{:S(2)}, u32[]{:S(2)}) collective-permute-start(f32[3,16,128]{2,1,0:T(8,128)S(1)} %slice.142), channel_id=1, source_target_pairs={{0,8},{4,12},{8,0},{12,4},{16,24},{20,28},{24,16},{28,20},{1,9},{5... | collective-permute-start | bytes 73736 | tf_op jit(solution)/shard_map/ppermute | solution.py:19
  44.7 3.8 %collective-permute-start.4 = (f32[2,16,128]{2,1,0:T(8,128)S(1)}, f32[2,16,128]{2,1,0:T(8,128)S(1)}, u32[]{:S(2)}, u32[]{:S(2)}) collective-permute-start(f32[2,16,128]{2,1,0:T(8,128)S(1)} %slice.143), channel_id=1, source_target_pairs={{0,16},{4,20},{8,24},{12,28},{16,0},{20,4},{24,8},{28,12},{1,17},{... | collective-permute-start | bytes 49160 | tf_op jit(solution)/shard_map/ppermute | solution.py:19
  50.4 3.6 %collective-permute-start.5 = (f32[16]{0:T(128)S(1)}, f32[16]{0:T(128)S(1)}, u32[]{:S(2)}, u32[]{:S(2)}) collective-permute-start(f32[16]{0:T(128)S(1)} %add.181), channel_id=1, source_target_pairs={{0,1},{1,0},{2,3},{3,2},{4,5},{5,4},{6,7},{7,6},{8,9},{9,8},{10,11... | collective-permute-start | bytes 200 | tf_op jit(solution)/shard_map/ppermute | solution.py:19
  54.0 4.4 %collective-permute-start.6 = (f32[16]{0:T(128)S(1)}, f32[16]{0:T(128)S(1)}, u32[]{:S(2)}, u32[]{:S(2)}) collective-permute-start(f32[16]{0:T(128)S(1)} %add.182), channel_id=1, source_target_pairs={{0,2},{1,3},{2,0},{3,1},{4,6},{5,7},{6,4},{7,5},{8,10},{9,11},{10,... | collective-permute-start | bytes 200 | tf_op jit(solution)/shard_map/ppermute | solution.py:19
  58.5 1.1 collective-permute-start.7
  59.6 9.4 %collective-permute-start.8 = (f32[16]{0:T(128)S(1)}, f32[16]{0:T(128)S(1)}, u32[]{:S(2)}, u32[]{:S(2)}) collective-permute-start(f32[16]{0:T(128)S(1)} %add.184), channel_id=1, source_target_pairs={{0,8},{4,12},{8,0},{12,4},{16,24},{20,28},{24,16},{28,20},{1,9},{5... | collective-permute-start | bytes 200 | tf_op jit(solution)/shard_map/ppermute | solution.py:19
  69.0 3.6 %collective-permute-start.9 = (f32[16]{0:T(128)S(1)}, f32[16]{0:T(128)S(1)}, u32[]{:S(2)}, u32[]{:S(2)}) collective-permute-start(f32[16]{0:T(128)S(1)} %add.185), channel_id=1, source_target_pairs={{0,16},{4,20},{8,24},{12,28},{16,0},{20,4},{24,8},{28,12},{1,17},{... | collective-permute-start | bytes 200 | tf_op jit(solution)/shard_map/ppermute | solution.py:19
  74.1 10.8 %collective-permute-start.10 = (f32[6,16,128]{2,1,0:T(8,128)S(1)}, f32[6,16,128]{2,1,0:T(8,128)S(1)}, u32[]{:S(2)}, u32[]{:S(2)}) collective-permute-start(f32[6,16,128]{2,1,0:T(8,128)S(1)} %pad_maximum_fusion.4), channel_id=1, source_target_pairs={{0,1},{1,0},{2,3},{3,2},{4,5},{5,4},{6,7},{7,6},{8,9},{9,8},{10,11... | collective-permute-start | bytes 147464 | tf_op jit(solution)/shard_map/ppermute | solution.py:19
  84.9 8.8 %collective-permute-start.11 = (f32[5,16,128]{2,1,0:T(8,128)S(1)}, f32[5,16,128]{2,1,0:T(8,128)S(1)}, u32[]{:S(2)}, u32[]{:S(2)}) collective-permute-start(f32[5,16,128]{2,1,0:T(8,128)S(1)} %slice.150), channel_id=1, source_target_pairs={{0,2},{1,3},{2,0},{3,1},{4,6},{5,7},{6,4},{7,5},{8,10},{9,11},{10,... | collective-permute-start | bytes 122888 | tf_op jit(solution)/shard_map/ppermute | solution.py:19
  93.7 1.3 %collective-permute-start.12 = (f32[4,16,128]{2,1,0:T(8,128)S(1)}, f32[4,16,128]{2,1,0:T(8,128)S(1)}, u32[]{:S(2)}, u32[]{:S(2)}) collective-permute-start(f32[4,16,128]{2,1,0:T(8,128)S(1)} %slice.151), channel_id=1, source_target_pairs={{0,4},{4,0},{8,12},{12,8},{16,20},{20,16},{24,28},{28,24},{1,5},{5... | collective-permute-start | bytes 98312 | tf_op jit(solution)/shard_map/ppermute | solution.py:19
  95.0 3.9 %collective-permute-start.13 = (f32[3,16,128]{2,1,0:T(8,128)S(1)}, f32[3,16,128]{2,1,0:T(8,128)S(1)}, u32[]{:S(2)}, u32[]{:S(2)}) collective-permute-start(f32[3,16,128]{2,1,0:T(8,128)S(1)} %slice.152), channel_id=1, source_target_pairs={{0,8},{4,12},{8,0},{12,4},{16,24},{20,28},{24,16},{28,20},{1,9},{5... | collective-permute-start | bytes 73736 | tf_op jit(solution)/shard_map/ppermute | solution.py:19
  98.9 3.8 %collective-permute-start.14 = (f32[2,16,128]{2,1,0:T(8,128)S(1)}, f32[2,16,128]{2,1,0:T(8,128)S(1)}, u32[]{:S(2)}, u32[]{:S(2)}) collective-permute-start(f32[2,16,128]{2,1,0:T(8,128)S(1)} %slice.153), channel_id=1, source_target_pairs={{0,16},{4,20},{8,24},{12,28},{16,0},{20,4},{24,8},{28,12},{1,17},{... | collective-permute-start | bytes 49160 | tf_op jit(solution)/shard_map/ppermute | solution.py:19
  104.9 3.6 %collective-permute-start.15 = (f32[16]{0:T(128)S(1)}, f32[16]{0:T(128)S(1)}, u32[]{:S(2)}, u32[]{:S(2)}) collective-permute-start(f32[16]{0:T(128)S(1)} %add.201), channel_id=1, source_target_pairs={{0,1},{1,0},{2,3},{3,2},{4,5},{5,4},{6,7},{7,6},{8,9},{9,8},{10,11... | collective-permute-start | bytes 200 | tf_op jit(solution)/shard_map/ppermute | solution.py:19
  108.5 4.4 %collective-permute-start.16 = (f32[16]{0:T(128)S(1)}, f32[16]{0:T(128)S(1)}, u32[]{:S(2)}, u32[]{:S(2)}) collective-permute-start(f32[16]{0:T(128)S(1)} %add.202), channel_id=1, source_target_pairs={{0,2},{1,3},{2,0},{3,1},{4,6},{5,7},{6,4},{7,5},{8,10},{9,11},{10,... | collective-permute-start | bytes 200 | tf_op jit(solution)/shard_map/ppermute | solution.py:19
  112.9 1.1 collective-permute-start.17
  114.1 8.1 %collective-permute-start.18 = (f32[16]{0:T(128)S(1)}, f32[16]{0:T(128)S(1)}, u32[]{:S(2)}, u32[]{:S(2)}) collective-permute-start(f32[16]{0:T(128)S(1)} %add.204), channel_id=1, source_target_pairs={{0,8},{4,12},{8,0},{12,4},{16,24},{20,28},{24,16},{28,20},{1,9},{5... | collective-permute-start | bytes 200 | tf_op jit(solution)/shard_map/ppermute | solution.py:19
  122.2 3.6 %collective-permute-start.19 = (f32[16]{0:T(128)S(1)}, f32[16]{0:T(128)S(1)}, u32[]{:S(2)}, u32[]{:S(2)}) collective-permute-start(f32[16]{0:T(128)S(1)} %add.205), channel_id=1, source_target_pairs={{0,16},{4,20},{8,24},{12,28},{16,0},{20,4},{24,8},{28,12},{1,17},{... | collective-permute-start | bytes 200 | tf_op jit(solution)/shard_map/ppermute | solution.py:19

commit v4 on v3

--- a/solution.py
+++ b/solution.py
@@ -38,6 +38,19 @@
     return added + jnp.einsum("cgi,gt->cti", result[:, :, width:], col_hot, precision=highest)
 
 
+def pieces(values):
+    high = lax.reduce_precision(values, exponent_bits=8, mantissa_bits=7)
+    rest = values - high
+    middle = lax.reduce_precision(rest, exponent_bits=8, mantissa_bits=7)
+    return jnp.concatenate([high, middle, rest - middle], axis=0).astype(jnp.bfloat16)
+
+
+def select(values, hot, spec):
+    count = values.shape[0]
+    out = jnp.einsum(spec, pieces(values), hot, preferred_element_type=jnp.float32)
+    return (out[:count] + out[count : 2 * count]) + out[2 * count :]
+
+
 def tree_sums(proj):
     low_count = lax.axis_size("gy").bit_length() - 1
     high_count = lax.axis_size("gx").bit_length() - 1
@@ -70,15 +83,15 @@
     pair_rows = pairs[0, 0]
     pair_cols = pairs[0, 1]
     position = jnp.arange(points, dtype=jnp.int32)
-    inverse = jnp.sum(jnp.where(perm[:, None] == position[None, :], position[:, None], 0), axis=0)
-    stacked = jnp.concatenate([coords * inv_scale[:, None], right_side], axis=0)[:, perm]
-    tile_coords = stacked[:features].reshape(features, tiles, TILE_POINTS)
-    kern = near_kernels(tile_coords, pair_rows, pair_cols)
+    hot = (perm[:, None] == position[None, :]).astype(jnp.bfloat16)
+    hot = hot.reshape(tiles, TILE_POINTS, points)
+    stacked = select(jnp.concatenate([coords * inv_scale[:, None], right_side], axis=0), hot, "cp,ktp->ckt")
+    tile_coords = stacked[:features]
+    kern = lax.optimization_barrier(near_kernels(tile_coords, pair_rows, pair_cols))
     scales = 2.0 ** ((1.0 - jnp.arange(levels, dtype=jnp.float32)) / 2.0)
 
     def near_tiles(values_t):
-        tile_vec = values_t.reshape(columns, tiles, TILE_POINTS)
-        return near_apply(kern, tile_vec, pair_rows, pair_cols).reshape(columns, points)
+        return near_apply(kern, values_t, pair_rows, pair_cols)
 
     def sums_with_norm(values):
         proj = jnp.einsum("lp,cp,rp->lcr", level_gain, values, basis, precision=highest)
@@ -96,18 +109,18 @@
             nodesum, norm_now = sums_with_norm(residual)
             near_t = near_tiles(direction_t)
             late_t, nodesum = lax.optimization_barrier((near_t, nodesum))
-            near = late_t[:, inverse]
+            near = select(late_t, hot, "ckt,ktp->cp")
         else:
             residual_sum, norm_next = sums_with_norm(residual)
-            residual_t = residual[:, perm]
+            residual_t = select(residual, hot, "cp,ktp->ckt")
             residual_near_t = near_tiles(residual_t)
             late_t, residual_sum = lax.optimization_barrier((residual_near_t, residual_sum))
             ratio = norm_next / norm_now
             direction = residual + ratio[:, None] * direction
-            direction_t = residual_t + ratio[:, None] * direction_t
+            direction_t = residual_t + ratio[:, None, None] * direction_t
             nodesum = residual_sum + ratio[None, :, None] * nodesum
-            near_t = residual_near_t + ratio[:, None] * near_t
-            near = late_t[:, inverse] + ratio[:, None] * near
+            near_t = residual_near_t + ratio[:, None, None] * near_t
+            near = select(late_t, hot, "ckt,ktp->cp") + ratio[:, None] * near
             norm_now = norm_next
         coupled = jnp.einsum("lcr,lrs->lcs", nodesum, coupling, precision=highest)
         coupled = (
@@ -116,7 +129,7 @@
         back = jnp.einsum("lcr,rp->lcp", coupled, basis, precision=highest)
         far = jnp.sum(back * level_gain[:, None, :], axis=0)
         base = noise[None, :] * direction + far
-        local = jnp.sum(direction * base, axis=1) + jnp.sum(direction_t * near_t, axis=1)
+        local = jnp.sum(direction * base, axis=1) + jnp.sum(direction_t * near_t, axis=(1, 2))
         curve = butterfly(local)
         alpha = norm_now / curve
         solution = solution + alpha[:, None] * direction

time: 127 us -> 104 us (0.82)
  local copies, waits for them, and re-layouts: 41.7 us -> 4.38 us
  matrix products: 25.3 us -> 35.8 us
  waiting for transfers between devices: 26.4 us -> 31.1 us
    gather x8 -> x0, local copies, waits for them, and re-layouts: 36.4 us -> none  [the longest x2 9.1 us: per_device(): jnp.concatenate([coords * inv_scale[:, None], right_side], axis=0)[:, perm]]
    dot_general x0 -> x4, matrix products: none -> 13.9 us  [select(): jnp.einsum(spec, pieces(values), hot, preferred_element_type=jnp.float32)]
    ppermute x20, waiting for transfers between devices: 26.4 us -> 31.1 us  [swapped(): return lax.ppermute(value, axis, pairs)]
    dot_general x2, matrix products: 12.2 us -> 9.46 us  [near_apply(): result = jnp.einsum('gij,cgj->cgi', kern, union_vec, precision=highest)]
    reduce_sum x4, other arithmetic: 2.25 us -> 0.79 us  [the longest x2 0.44 us: per_device(): jnp.sum(direction_t * near_t, axis=(1, 2))]
    unnamed x0 -> x1, other arithmetic: none -> 1.36 us
  transfers between devices with their start and end apart: 20 -> 20, of which waited for: 15 -> 15; matrix products, arithmetic and copies ran while one was open for 51% -> 35% of each run, Pallas kernels for 0% -> 0%
where the time goes in v4:
time: 104 us
  matrix products  35.8 us (34%)
  waiting for transfers between devices  31.1 us (30%)
  starting transfers between devices  25 us (24%)
  other arithmetic  6.66 us (6%)
  local copies, waits for them, and re-layouts  4.38 us (4%)
  between operations  1.11 us (1%)
    ppermute x20, waiting for transfers between devices, swapped(): return lax.ppermute(value, axis, pairs)  31.1 us
    ppermute x20, starting transfers between devices, swapped(): return lax.ppermute(value, axis, pairs)  25 us
    dot_general x4, matrix products, select(): jnp.einsum(spec, pieces(values), hot, preferred_element_type=jnp.float32)  13.9 us
    dot_general x2, matrix products, near_apply(): result = jnp.einsum('gij,cgj->cgi', kern, union_vec, precision=highest)  9.46 us
    dot_general x1, matrix products, near_kernels(): gram = jnp.einsum('fgi,fgj->gij', union, union, precision=highest)  4.29 us
    dot_general x2, matrix products, sums_with_norm(): jnp.einsum('lp,cp,rp->lcr', level_gain, values, basis, precision=highest)  3.32 us
  transfers between devices with their start and end apart: 20, of which 15 were waited for; matrix products, arithmetic and copies ran while one was open for 35% of the time, Pallas kernels for 0%

profile of v4, /device:TPU:0, one launch (start us, length us, event | category | flops | bytes accessed | tf_op | source)
XLA Modules:
  0.0 104.0 jit_solution(7367354261586986132)
XLA Ops:
  0.6 1.1 %multiply_reduce_fusion.5 = f32[16]{0:T(128)S(1)} fusion(f32[16,2048]{1,0:T(8,128)} %param.12), kind=kLoop, calls=%fused_computation.113 | loop fusion | flops 65520 | bytes 131136 | tf_op jit(solution)/shard_map/reduce_sum | solution.py:98
  1.9 2.1 %convolution_bitcast_fusion.3 = f32[5,16,128]{2,1,0:T(8,128)S(1)} fusion(f32[128,2048]{1,0:T(8,128)S(1)} %copy-done, f32[2048,5]{0,1:T(8,128)} %bitcast.81, f32[2048,16]{0,1:T(8,128)} %bitcast.79), kind=kOutput, calls=%fused_computation.25 | convolution fusion | flops 251822080 | bytes 1261568 | tf_op jit(solution)/shard_map/lp,cp,rp->lcr/dot_general | solution.py:97
  4.1 3.0 %collective-permute-start = (f32[6,16,128]{2,1,0:T(8,128)S(1)}, f32[6,16,128]{2,1,0:T(8,128)S(1)}, u32[]{:S(2)}, u32[]{:S(2)}) collective-permute-start(f32[6,16,128]{2,1,0:T(8,128)S(1)} %pad_maximum_fusion.3), channel_id=1, source_target_pairs={{0,1},{1,0},{2,3},{3,2},{4,5},{5,4},{6,7},{7,6},{8,9},{9,8},{10,11... | collective-permute-start | bytes 147464 | tf_op jit(solution)/shard_map/ppermute | solution.py:19
  7.7 1.4 %reduce.9 = s32[2048]{0:T(1024)S(1)} reduce(s32[1,2048]{1,0:T(1,128)} %param.16, s32[]{:T(128)} %broadcast.141), dimensions={0}, to_apply=%param.16.reduce_sub_computation.3 | reduce | bytes 16388 | tf_op args[7]
  9.1 0.9 broadcast_multiply_fusion
  10.0 1.0 reduce-precision_convert_fusion.1
  10.9 3.5 %fusion.3 = f32[72,8,256]{2,0,1:T(8,128)S(1)} fusion(s32[8,256]{1,0:T(8,128)S(1)} %eq.29, bf16[24,2048]{1,0:T(8,128)(2,1)S(1)} %get-tuple-element.22, bf16[24,2048]{1,0:T(8,128)(2,1)S(1)} %get-tuple-element.21, bf16[24,2048]{1,0:T(8,128)(2,1)S(1)} %get-tuple-element.20), kind=kOutput, calls=%fused_computation.10 | convolution fusion | flops 609058816 | bytes 892928 | tf_op jit(solution)/shard_map/cp,ktp->ckt/dot_general | solution.py:50
  16.2 0.6 gather_fusion
  16.8 4.3 %exponential_multiply_fusion = f32[4,512,512]{2,1,0:T(8,128)S(1)} fusion(f32[4,512]{1,0:T(4,128)S(1)} %multiply_reduce_fusion.6, f32[8,4,256]{2,0,1:T(8,128)S(1)} %bitcast.88, f32[8,4,256]{2,0,1:T(8,128)S(1)} %bitcast.90), kind=kOutput, calls=%fused_computation.15 | convolution fusion | flops 105922560 | bytes 4268032 | tf_op jit(solution)/shard_map/fgi,fgj->gij/dot_general | solution.py:24
  21.2 3.6 %convolution_bitcast_fusion.1 = f32[16,4,512]{2,0,1:T(8,128)S(1)} fusion(f32[4,512,512]{2,1,0:T(8,128)S(1)} %exponential_multiply_fusion, f32[16,4,256]{2,0,1:T(8,128)S(1)} %bitcast.85, f32[16,4,256]{2,0,1:T(8,128)S(1)} %bitcast.86), kind=kOutput, calls=%fused_computation.23 | convolution fusion | flops 201359360 | bytes 4456448 | tf_op jit(solution)/shard_map/gij,cgj->cgi/dot_general | solution.py:33
  24.9 2.7 %collective-permute-start.1 = (f32[5,16,128]{2,1,0:T(8,128)S(1)}, f32[5,16,128]{2,1,0:T(8,128)S(1)}, u32[]{:S(2)}, u32[]{:S(2)}) collective-permute-start(f32[5,16,128]{2,1,0:T(8,128)S(1)} %slice.180), channel_id=1, source_target_pairs={{0,2},{1,3},{2,0},{3,1},{4,6},{5,7},{6,4},{7,5},{8,10},{9,11},{10,... | collective-permute-start | bytes 122888 | tf_op jit(solution)/shard_map/ppermute | solution.py:19
  27.8 2.0 %collective-permute-done.1 = f32[5,16,128]{2,1,0:T(8,128)S(1)} collective-permute-done((f32[5,16,128]{2,1,0:T(8,128)S(1)}, f32[5,16,128]{2,1,0:T(8,128)S(1)}, u32[]{:S(2)}, u32[]{:S(2)}) %collective-permute-start.1) | collective-permute-done | bytes 40992 | tf_op jit(solution)/shard_map/ppermute | solution.py:19
  30.2 0.9 collective-permute-done.2
  31.1 2.1 %collective-permute-start.3 = (f32[3,16,128]{2,1,0:T(8,128)S(1)}, f32[3,16,128]{2,1,0:T(8,128)S(1)}, u32[]{:S(2)}, u32[]{:S(2)}) collective-permute-start(f32[3,16,128]{2,1,0:T(8,128)S(1)} %slice.182), channel_id=1, source_target_pairs={{0,8},{4,12},{8,0},{12,4},{16,24},{20,28},{24,16},{28,20},{1,9},{5... | collective-permute-start | bytes 73736 | tf_op jit(solution)/shard_map/ppermute | solution.py:19
  33.4 1.8 %collective-permute-done.3 = f32[3,16,128]{2,1,0:T(8,128)S(1)} collective-permute-done((f32[3,16,128]{2,1,0:T(8,128)S(1)}, f32[3,16,128]{2,1,0:T(8,128)S(1)}, u32[]{:S(2)}, u32[]{:S(2)}) %collective-permute-start.3) | collective-permute-done | bytes 24608 | tf_op jit(solution)/shard_map/ppermute | solution.py:19
  35.2 1.9 %collective-permute-start.4 = (f32[2,16,128]{2,1,0:T(8,128)S(1)}, f32[2,16,128]{2,1,0:T(8,128)S(1)}, u32[]{:S(2)}, u32[]{:S(2)}) collective-permute-start(f32[2,16,128]{2,1,0:T(8,128)S(1)} %slice.183), channel_id=1, source_target_pairs={{0,16},{4,20},{8,24},{12,28},{16,0},{20,4},{24,8},{28,12},{1,17},{... | collective-permute-start | bytes 49160 | tf_op jit(solution)/shard_map/ppermute | solution.py:19
  37.1 1.9 %collective-permute-done.4 = f32[2,16,128]{2,1,0:T(8,128)S(1)} collective-permute-done((f32[2,16,128]{2,1,0:T(8,128)S(1)}, f32[2,16,128]{2,1,0:T(8,128)S(1)}, u32[]{:S(2)}, u32[]{:S(2)}) %collective-permute-start.4) | collective-permute-done | bytes 16416 | tf_op jit(solution)/shard_map/ppermute | solution.py:19
  39.4 0.6 convolution_multiply_fusion.3
  40.0 0.8 fusion.10
  41.2 3.4 %collective-permute-done.5 = f32[16]{0:T(128)S(1)} collective-permute-done((f32[16]{0:T(128)S(1)}, f32[16]{0:T(128)S(1)}, u32[]{:S(2)}, u32[]{:S(2)}) %collective-permute-start.5) | collective-permute-done | bytes 96 | tf_op jit(solution)/shard_map/ppermute | solution.py:19
  44.6 2.6 %collective-permute-start.6 = (f32[16]{0:T(128)S(1)}, f32[16]{0:T(128)S(1)}, u32[]{:S(2)}, u32[]{:S(2)}) collective-permute-start(f32[16]{0:T(128)S(1)} %add.185), channel_id=1, source_target_pairs={{0,2},{1,3},{2,0},{3,1},{4,6},{5,7},{6,4},{7,5},{8,10},{9,11},{10,... | collective-permute-start | bytes 200 | tf_op jit(solution)/shard_map/ppermute | solution.py:19
  47.2 1.8 %collective-permute-done.6 = f32[16]{0:T(128)S(1)} collective-permute-done((f32[16]{0:T(128)S(1)}, f32[16]{0:T(128)S(1)}, u32[]{:S(2)}, u32[]{:S(2)}) %collective-permute-start.6) | collective-permute-done | bytes 96 | tf_op jit(solution)/shard_map/ppermute | solution.py:19
  49.1 1.1 %collective-permute-done.7 = f32[16]{0:T(128)S(1)} collective-permute-done((f32[16]{0:T(128)S(1)}, f32[16]{0:T(128)S(1)}, u32[]{:S(2)}, u32[]{:S(2)}) %collective-permute-start.7) | collective-permute-done | bytes 96 | tf_op jit(solution)/shard_map/ppermute | solution.py:19
  50.1 1.8 %collective-permute-start.8 = (f32[16]{0:T(128)S(1)}, f32[16]{0:T(128)S(1)}, u32[]{:S(2)}, u32[]{:S(2)}) collective-permute-start(f32[16]{0:T(128)S(1)} %add.187), channel_id=1, source_target_pairs={{0,8},{4,12},{8,0},{12,4},{16,24},{20,28},{24,16},{28,20},{1,9},{5... | collective-permute-start | bytes 200 | tf_op jit(solution)/shard_map/ppermute | solution.py:19
  52.0 3.5 %fusion.8 = f32[48,2048]{1,0:T(8,128)S(1)} fusion(s32[8,256]{1,0:T(8,128)S(1)} %eq.29, bf16[16,8,256]{2,0,1:T(8,128)(2,1)S(1)} %get-tuple-element.32, bf16[16,8,256]{2,0,1:T(8,128)(2,1)S(1)} %get-tuple-element.33, bf16[16,8,256]{2,0,1:T(8,128)(2,1)S(1)} %get-tuple-element.31), kind=kOutput, calls=%fused_computation.18 | convolution fusion | flops 407437312 | bytes 598016 | tf_op jit(solution)/shard_map/ckt,ktp->cp/dot_general | solution.py:50
  55.4 1.6 %collective-permute-start.9 = (f32[16]{0:T(128)S(1)}, f32[16]{0:T(128)S(1)}, u32[]{:S(2)}, u32[]{:S(2)}) collective-permute-start(f32[16]{0:T(128)S(1)} %add.188), channel_id=1, source_target_pairs={{0,16},{4,20},{8,24},{12,28},{16,0},{20,4},{24,8},{28,12},{1,17},{... | collective-permute-start | bytes 200 | tf_op jit(solution)/shard_map/ppermute | solution.py:19
  57.1 1.9 %collective-permute-done.9 = f32[16]{0:T(128)S(1)} collective-permute-done((f32[16]{0:T(128)S(1)}, f32[16]{0:T(128)S(1)}, u32[]{:S(2)}, u32[]{:S(2)}) %collective-permute-start.9) | collective-permute-done | bytes 96 | tf_op jit(solution)/shard_map/ppermute | solution.py:19
  59.3 1.2 %convolution_bitcast_fusion.2 = f32[5,16,128]{2,1,0:T(8,128)S(1)} fusion(f32[128,2048]{1,0:T(8,128)S(1)} %copy-done, f32[2048,16]{0,1:T(8,128)S(1)} %bitcast.80, f32[2048,5]{0,1:T(8,128)S(1)} %bitcast.82), kind=kOutput, calls=%fused_computation.24 | convolution fusion | flops 251822080 | bytes 1261568 | tf_op jit(solution)/shard_map/lp,cp,rp->lcr/dot_general | solution.py:97
  60.7 3.5 %fusion.1 = f32[48,8,256]{2,0,1:T(8,128)S(1)} fusion(s32[8,256]{1,0:T(8,128)S(1)} %eq.29, bf16[16,2048]{1,0:T(8,128)(2,1)S(1)} %get-tuple-element.29, bf16[16,2048]{1,0:T(8,128)(2,1)S(1)} %get-tuple-element.28, bf16[16,2048]{1,0:T(8,128)(2,1)S(1)} %get-tuple-element.14), kind=kOutput, calls=%fused_computation.8 | convolution fusion | flops 407437312 | bytes 598016 | tf_op jit(solution)/shard_map/cp,ktp->ckt/dot_general | solution.py:50
  64.3 0.6 gather_fusion.5
  64.8 0.6 gather_fusion.4
  65.4 2.7 %collective-permute-start.11 = (f32[5,16,128]{2,1,0:T(8,128)S(1)}, f32[5,16,128]{2,1,0:T(8,128)S(1)}, u32[]{:S(2)}, u32[]{:S(2)}) collective-permute-start(f32[5,16,128]{2,1,0:T(8,128)S(1)} %slice.196), channel_id=1, source_target_pairs={{0,2},{1,3},{2,0},{3,1},{4,6},{5,7},{6,4},{7,5},{8,10},{9,11},{10,... | collective-permute-start | bytes 122888 | tf_op jit(solution)/shard_map/ppermute | solution.py:19
  68.1 5.9 %convolution_bitcast_fusion = f32[16,4,512]{2,0,1:T(8,128)S(1)} fusion(f32[4,512,512]{2,1,0:T(8,128)} %copy-done.1, f32[16,4,256]{2,0,1:T(8,128)S(1)} %bitcast.83, f32[16,4,256]{2,0,1:T(8,128)S(1)} %bitcast.84), kind=kOutput, calls=%fused_computation.22 | convolution fusion | flops 201359360 | bytes 4456448 | tf_op jit(solution)/shard_map/gij,cgj->cgi/dot_general | solution.py:33
  74.1 1.2 %collective-permute-done.12 = f32[4,16,128]{2,1,0:T(8,128)S(1)} collective-permute-done((f32[4,16,128]{2,1,0:T(8,128)S(1)}, f32[4,16,128]{2,1,0:T(8,128)S(1)}, u32[]{:S(2)}, u32[]{:S(2)}) %collective-permute-start.12) | collective-permute-done | bytes 32800 | tf_op jit(solution)/shard_map/ppermute | solution.py:19
  75.3 0.6 collective-permute-start.13
  76.2 3.0 %collective-permute-done.13 = f32[3,16,128]{2,1,0:T(8,128)S(1)} collective-permute-done((f32[3,16,128]{2,1,0:T(8,128)S(1)}, f32[3,16,128]{2,1,0:T(8,128)S(1)}, u32[]{:S(2)}, u32[]{:S(2)}) %collective-permute-start.13) | collective-permute-done | bytes 24608 | tf_op jit(solution)/shard_map/ppermute | solution.py:19
  79.2 1.6 %collective-permute-start.14 = (f32[2,16,128]{2,1,0:T(8,128)S(1)}, f32[2,16,128]{2,1,0:T(8,128)S(1)}, u32[]{:S(2)}, u32[]{:S(2)}) collective-permute-start(f32[2,16,128]{2,1,0:T(8,128)S(1)} %slice.199), channel_id=1, source_target_pairs={{0,16},{4,20},{8,24},{12,28},{16,0},{20,4},{24,8},{28,12},{1,17},{... | collective-permute-start | bytes 49160 | tf_op jit(solution)/shard_map/ppermute | solution.py:19
  81.1 1.9 %collective-permute-done.14 = f32[2,16,128]{2,1,0:T(8,128)S(1)} collective-permute-done((f32[2,16,128]{2,1,0:T(8,128)S(1)}, f32[2,16,128]{2,1,0:T(8,128)S(1)}, u32[]{:S(2)}, u32[]{:S(2)}) %collective-permute-start.14) | collective-permute-done | bytes 16416 | tf_op jit(solution)/shard_map/ppermute | solution.py:19
  83.8 0.6 convolution_multiply_fusion.2
  84.4 0.8 fusion.11
  85.4 1.6 %collective-permute-start.15 = (f32[16]{0:T(128)S(1)}, f32[16]{0:T(128)S(1)}, u32[]{:S(2)}, u32[]{:S(2)}) collective-permute-start(f32[16]{0:T(128)S(1)} %add.207), channel_id=1, source_target_pairs={{0,1},{1,0},{2,3},{3,2},{4,5},{5,4},{6,7},{7,6},{8,9},{9,8},{10,11... | collective-permute-start | bytes 200 | tf_op jit(solution)/shard_map/ppermute | solution.py:19
  87.0 2.0 %collective-permute-done.15 = f32[16]{0:T(128)S(1)} collective-permute-done((f32[16]{0:T(128)S(1)}, f32[16]{0:T(128)S(1)}, u32[]{:S(2)}, u32[]{:S(2)}) %collective-permute-start.15) | collective-permute-done | bytes 96 | tf_op jit(solution)/shard_map/ppermute | solution.py:19
  89.4 4.1 %collective-permute-done.16 = f32[16]{0:T(128)S(1)} collective-permute-done((f32[16]{0:T(128)S(1)}, f32[16]{0:T(128)S(1)}, u32[]{:S(2)}, u32[]{:S(2)}) %collective-permute-start.16) | collective-permute-done | bytes 96 | tf_op jit(solution)/shard_map/ppermute | solution.py:19
  93.5 1.1 %collective-permute-done.17 = f32[16]{0:T(128)S(1)} collective-permute-done((f32[16]{0:T(128)S(1)}, f32[16]{0:T(128)S(1)}, u32[]{:S(2)}, u32[]{:S(2)}) %collective-permute-start.17) | collective-permute-done | bytes 96 | tf_op jit(solution)/shard_map/ppermute | solution.py:19
  95.2 3.0 %collective-permute-done.18 = f32[16]{0:T(128)S(1)} collective-permute-done((f32[16]{0:T(128)S(1)}, f32[16]{0:T(128)S(1)}, u32[]{:S(2)}, u32[]{:S(2)}) %collective-permute-start.18) | collective-permute-done | bytes 96 | tf_op jit(solution)/shard_map/ppermute | solution.py:19
  98.2 1.5 %collective-permute-start.19 = (f32[16]{0:T(128)S(1)}, f32[16]{0:T(128)S(1)}, u32[]{:S(2)}, u32[]{:S(2)}) collective-permute-start(f32[16]{0:T(128)S(1)} %add.211), channel_id=1, source_target_pairs={{0,16},{4,20},{8,24},{12,28},{16,0},{20,4},{24,8},{28,12},{1,17},{... | collective-permute-start | bytes 200 | tf_op jit(solution)/shard_map/ppermute | solution.py:19
  99.7 3.5 %fusion.9 = f32[48,2048]{1,0:T(8,128)S(1)} fusion(s32[8,256]{1,0:T(8,128)S(1)} %eq.29, bf16[16,8,256]{2,0,1:T(8,128)(2,1)S(1)} %get-tuple-element.24, bf16[16,8,256]{2,0,1:T(8,128)(2,1)S(1)} %get-tuple-element.25, bf16[16,8,256]{2,0,1:T(8,128)(2,1)S(1)} %get-tuple-element.23), kind=kOutput, calls=%fused_computation.19 | convolution fusion | flops 407437312 | bytes 598016 | tf_op jit(solution)/shard_map/ckt,ktp->cp/dot_general | solution.py:50
  103.2 0.8 fusion.49
  (98 shorter events, 7.6 us)
Async XLA Ops:
  0.6 1.3 %copy-start = (f32[128,2048]{1,0:T(8,128)S(1)}, f32[128,2048]{1,0:T(8,128)}, u32[]{:S(2)}) copy-start(f32[128,2048]{1,0:T(8,128)} %param.13) | copy-start | bytes 3145732
  4.1 20.7 %collective-permute-start = (f32[6,16,128]{2,1,0:T(8,128)S(1)}, f32[6,16,128]{2,1,0:T(8,128)S(1)}, u32[]{:S(2)}, u32[]{:S(2)}) collective-permute-start(f32[6,16,128]{2,1,0:T(8,128)S(1)} %pad_maximum_fusion.3), channel_id=1, source_target_pairs={{0,1},{1,0},{2,3},{3,2},{4,5},{5,4},{6,7},{7,6},{8,9},{9,8},{10,11... | collective-permute-start | bytes 147464 | tf_op jit(solution)/shard_map/ppermute | solution.py:19
  10.0 4.6 %copy-start.6 = (s32[1,2,4]{2,1,0:T(2,128)S(1)}, s32[1,2,4]{2,1,0:T(2,128)}, u32[]{:S(2)}) copy-start(s32[1,2,4]{2,1,0:T(2,128)} %param.17) | copy-start | bytes 100
  21.1 19.7 %copy-start.1 = (f32[4,512,512]{2,1,0:T(8,128)}, f32[4,512,512]{2,1,0:T(8,128)S(1)}, u32[]{:S(2)}) copy-start(f32[4,512,512]{2,1,0:T(8,128)S(1)} %exponential_multiply_fusion) | copy-start | bytes 12582916
  21.1 17.9 %copy-start.3 = (f32[5,128,128]{2,1,0:T(8,128)S(1)}, f32[5,128,128]{2,1,0:T(8,128)}, u32[]{:S(2)}) copy-start(f32[5,128,128]{2,1,0:T(8,128)} %param.15) | copy-start | bytes 983044
  21.2 18.9 %copy-start.4 = (f32[5,2048]{1,0:T(8,128)S(1)}, f32[5,2048]{1,0:T(8,128)}, u32[]{:S(2)}) copy-start(f32[5,2048]{1,0:T(8,128)} %param.14) | copy-start | bytes 122884
  21.2 19.6 %copy-start.2 = (f32[16,2048]{1,0:T(8,128)S(1)}, f32[16,2048]{1,0:T(8,128)}, u32[]{:S(2)}) copy-start(f32[16,2048]{1,0:T(8,128)} %param.12) | copy-start | bytes 393220
  21.2 19.6 %copy-start.5 = (f32[2048]{0:T(1024)S(1)}, f32[2048]{0:T(1024)}, u32[]{:S(2)}) copy-start(f32[2048]{0:T(1024)} %param.11) | copy-start | bytes 24580
  24.9 5.0 %collective-permute-start.1 = (f32[5,16,128]{2,1,0:T(8,128)S(1)}, f32[5,16,128]{2,1,0:T(8,128)S(1)}, u32[]{:S(2)}, u32[]{:S(2)}) collective-permute-start(f32[5,16,128]{2,1,0:T(8,128)S(1)} %slice.180), channel_id=1, source_target_pairs={{0,2},{1,3},{2,0},{3,1},{4,6},{5,7},{6,4},{7,5},{8,10},{9,11},{10,... | collective-permute-start | bytes 122888 | tf_op jit(solution)/shard_map/ppermute | solution.py:19
  29.8 1.3 %collective-permute-start.2 = (f32[4,16,128]{2,1,0:T(8,128)S(1)}, f32[4,16,128]{2,1,0:T(8,128)S(1)}, u32[]{:S(2)}, u32[]{:S(2)}) collective-permute-start(f32[4,16,128]{2,1,0:T(8,128)S(1)} %slice.181), channel_id=1, source_target_pairs={{0,4},{4,0},{8,12},{12,8},{16,20},{20,16},{24,28},{28,24},{1,5},{5... | collective-permute-start | bytes 98312 | tf_op jit(solution)/shard_map/ppermute | solution.py:19
  31.1 4.1 %collective-permute-start.3 = (f32[3,16,128]{2,1,0:T(8,128)S(1)}, f32[3,16,128]{2,1,0:T(8,128)S(1)}, u32[]{:S(2)}, u32[]{:S(2)}) collective-permute-start(f32[3,16,128]{2,1,0:T(8,128)S(1)} %slice.182), channel_id=1, source_target_pairs={{0,8},{4,12},{8,0},{12,4},{16,24},{20,28},{24,16},{28,20},{1,9},{5... | collective-permute-start | bytes 73736 | tf_op jit(solution)/shard_map/ppermute | solution.py:19
  35.2 3.8 %collective-permute-start.4 = (f32[2,16,128]{2,1,0:T(8,128)S(1)}, f32[2,16,128]{2,1,0:T(8,128)S(1)}, u32[]{:S(2)}, u32[]{:S(2)}) collective-permute-start(f32[2,16,128]{2,1,0:T(8,128)S(1)} %slice.183), channel_id=1, source_target_pairs={{0,16},{4,20},{8,24},{12,28},{16,0},{20,4},{24,8},{28,12},{1,17},{... | collective-permute-start | bytes 49160 | tf_op jit(solution)/shard_map/ppermute | solution.py:19
  41.0 3.6 %collective-permute-start.5 = (f32[16]{0:T(128)S(1)}, f32[16]{0:T(128)S(1)}, u32[]{:S(2)}, u32[]{:S(2)}) collective-permute-start(f32[16]{0:T(128)S(1)} %add.184), channel_id=1, source_target_pairs={{0,1},{1,0},{2,3},{3,2},{4,5},{5,4},{6,7},{7,6},{8,9},{9,8},{10,11... | collective-permute-start | bytes 200 | tf_op jit(solution)/shard_map/ppermute | solution.py:19
  44.6 4.4 %collective-permute-start.6 = (f32[16]{0:T(128)S(1)}, f32[16]{0:T(128)S(1)}, u32[]{:S(2)}, u32[]{:S(2)}) collective-permute-start(f32[16]{0:T(128)S(1)} %add.185), channel_id=1, source_target_pairs={{0,2},{1,3},{2,0},{3,1},{4,6},{5,7},{6,4},{7,5},{8,10},{9,11},{10,... | collective-permute-start | bytes 200 | tf_op jit(solution)/shard_map/ppermute | solution.py:19
  49.0 1.1 %collective-permute-start.7 = (f32[16]{0:T(128)S(1)}, f32[16]{0:T(128)S(1)}, u32[]{:S(2)}, u32[]{:S(2)}) collective-permute-start(f32[16]{0:T(128)S(1)} %add.186), channel_id=1, source_target_pairs={{0,4},{4,0},{8,12},{12,8},{16,20},{20,16},{24,28},{28,24},{1,5},{5... | collective-permute-start | bytes 200 | tf_op jit(solution)/shard_map/ppermute | solution.py:19
  50.1 5.3 %collective-permute-start.8 = (f32[16]{0:T(128)S(1)}, f32[16]{0:T(128)S(1)}, u32[]{:S(2)}, u32[]{:S(2)}) collective-permute-start(f32[16]{0:T(128)S(1)} %add.187), channel_id=1, source_target_pairs={{0,8},{4,12},{8,0},{12,4},{16,24},{20,28},{24,16},{28,20},{1,9},{5... | collective-permute-start | bytes 200 | tf_op jit(solution)/shard_map/ppermute | solution.py:19
  55.4 3.6 %collective-permute-start.9 = (f32[16]{0:T(128)S(1)}, f32[16]{0:T(128)S(1)}, u32[]{:S(2)}, u32[]{:S(2)}) collective-permute-start(f32[16]{0:T(128)S(1)} %add.188), channel_id=1, source_target_pairs={{0,16},{4,20},{8,24},{12,28},{16,0},{20,4},{24,8},{28,12},{1,17},{... | collective-permute-start | bytes 200 | tf_op jit(solution)/shard_map/ppermute | solution.py:19
  60.6 4.8 %collective-permute-start.10 = (f32[6,16,128]{2,1,0:T(8,128)S(1)}, f32[6,16,128]{2,1,0:T(8,128)S(1)}, u32[]{:S(2)}, u32[]{:S(2)}) collective-permute-start(f32[6,16,128]{2,1,0:T(8,128)S(1)} %pad_maximum_fusion.4), channel_id=1, source_target_pairs={{0,1},{1,0},{2,3},{3,2},{4,5},{5,4},{6,7},{7,6},{8,9},{9,8},{10,11... | collective-permute-start | bytes 147464 | tf_op jit(solution)/shard_map/ppermute | solution.py:19
  65.4 8.6 %collective-permute-start.11 = (f32[5,16,128]{2,1,0:T(8,128)S(1)}, f32[5,16,128]{2,1,0:T(8,128)S(1)}, u32[]{:S(2)}, u32[]{:S(2)}) collective-permute-start(f32[5,16,128]{2,1,0:T(8,128)S(1)} %slice.196), channel_id=1, source_target_pairs={{0,2},{1,3},{2,0},{3,1},{4,6},{5,7},{6,4},{7,5},{8,10},{9,11},{10,... | collective-permute-start | bytes 122888 | tf_op jit(solution)/shard_map/ppermute | solution.py:19
  74.0 1.3 %collective-permute-start.12 = (f32[4,16,128]{2,1,0:T(8,128)S(1)}, f32[4,16,128]{2,1,0:T(8,128)S(1)}, u32[]{:S(2)}, u32[]{:S(2)}) collective-permute-start(f32[4,16,128]{2,1,0:T(8,128)S(1)} %slice.197), channel_id=1, source_target_pairs={{0,4},{4,0},{8,12},{12,8},{16,20},{20,16},{24,28},{28,24},{1,5},{5... | collective-permute-start | bytes 98312 | tf_op jit(solution)/shard_map/ppermute | solution.py:19
  75.3 3.9 %collective-permute-start.13 = (f32[3,16,128]{2,1,0:T(8,128)S(1)}, f32[3,16,128]{2,1,0:T(8,128)S(1)}, u32[]{:S(2)}, u32[]{:S(2)}) collective-permute-start(f32[3,16,128]{2,1,0:T(8,128)S(1)} %slice.198), channel_id=1, source_target_pairs={{0,8},{4,12},{8,0},{12,4},{16,24},{20,28},{24,16},{28,20},{1,9},{5... | collective-permute-start | bytes 73736 | tf_op jit(solution)/shard_map/ppermute | solution.py:19
  79.2 3.8 %collective-permute-start.14 = (f32[2,16,128]{2,1,0:T(8,128)S(1)}, f32[2,16,128]{2,1,0:T(8,128)S(1)}, u32[]{:S(2)}, u32[]{:S(2)}) collective-permute-start(f32[2,16,128]{2,1,0:T(8,128)S(1)} %slice.199), channel_id=1, source_target_pairs={{0,16},{4,20},{8,24},{12,28},{16,0},{20,4},{24,8},{28,12},{1,17},{... | collective-permute-start | bytes 49160 | tf_op jit(solution)/shard_map/ppermute | solution.py:19
  85.4 3.6 %collective-permute-start.15 = (f32[16]{0:T(128)S(1)}, f32[16]{0:T(128)S(1)}, u32[]{:S(2)}, u32[]{:S(2)}) collective-permute-start(f32[16]{0:T(128)S(1)} %add.207), channel_id=1, source_target_pairs={{0,1},{1,0},{2,3},{3,2},{4,5},{5,4},{6,7},{7,6},{8,9},{9,8},{10,11... | collective-permute-start | bytes 200 | tf_op jit(solution)/shard_map/ppermute | solution.py:19
  89.0 4.4 %collective-permute-start.16 = (f32[16]{0:T(128)S(1)}, f32[16]{0:T(128)S(1)}, u32[]{:S(2)}, u32[]{:S(2)}) collective-permute-start(f32[16]{0:T(128)S(1)} %add.208), channel_id=1, source_target_pairs={{0,2},{1,3},{2,0},{3,1},{4,6},{5,7},{6,4},{7,5},{8,10},{9,11},{10,... | collective-permute-start | bytes 200 | tf_op jit(solution)/shard_map/ppermute | solution.py:19
  93.5 1.1 %collective-permute-start.17 = (f32[16]{0:T(128)S(1)}, f32[16]{0:T(128)S(1)}, u32[]{:S(2)}, u32[]{:S(2)}) collective-permute-start(f32[16]{0:T(128)S(1)} %add.209), channel_id=1, source_target_pairs={{0,4},{4,0},{8,12},{12,8},{16,20},{20,16},{24,28},{28,24},{1,5},{5... | collective-permute-start | bytes 200 | tf_op jit(solution)/shard_map/ppermute | solution.py:19
  94.6 3.5 %collective-permute-start.18 = (f32[16]{0:T(128)S(1)}, f32[16]{0:T(128)S(1)}, u32[]{:S(2)}, u32[]{:S(2)}) collective-permute-start(f32[16]{0:T(128)S(1)} %add.210), channel_id=1, source_target_pairs={{0,8},{4,12},{8,0},{12,4},{16,24},{20,28},{24,16},{28,20},{1,9},{5... | collective-permute-start | bytes 200 | tf_op jit(solution)/shard_map/ppermute | solution.py:19
  98.2 5.0 %collective-permute-start.19 = (f32[16]{0:T(128)S(1)}, f32[16]{0:T(128)S(1)}, u32[]{:S(2)}, u32[]{:S(2)}) collective-permute-start(f32[16]{0:T(128)S(1)} %add.211), channel_id=1, source_target_pairs={{0,16},{4,20},{8,24},{12,28},{16,0},{20,4},{24,8},{28,12},{1,17},{... | collective-permute-start | bytes 200 | tf_op jit(solution)/shard_map/ppermute | solution.py:19

commit v5 on v4

--- a/solution.py
+++ b/solution.py
@@ -20,34 +20,40 @@
 
 
 def near_kernels(tile_coords, pair_rows, pair_cols):
-    union = jnp.concatenate([tile_coords[:, pair_rows], tile_coords[:, pair_cols]], axis=2)
-    gram = jnp.einsum("fgi,fgj->gij", union, union, precision=highest)
-    square = jnp.sum(union * union, axis=0)
+    union = jnp.concatenate([tile_coords[pair_rows], tile_coords[pair_cols]], axis=2)
+    gram = jnp.einsum("gfi,gfj->gij", union, union, precision=highest)
+    square = jnp.sum(union * union, axis=1)
     dist = square[:, :, None] + square[:, None, :] - 2.0 * gram
     return near_weight * jnp.exp(-0.5 * dist)
 
 
 def near_apply(kern, tile_vec, pair_rows, pair_cols):
     width = tile_vec.shape[2]
-    union_vec = jnp.concatenate([tile_vec[:, pair_rows], tile_vec[:, pair_cols]], axis=2)
-    result = jnp.einsum("gij,cgj->cgi", kern, union_vec, precision=highest)
-    tile_ids = jnp.arange(tile_vec.shape[1], dtype=jnp.int32)
+    union_vec = jnp.concatenate([tile_vec[pair_rows], tile_vec[pair_cols]], axis=2)
+    result = jnp.einsum("gij,gcj->gci", kern, union_vec, precision=highest)
+    tile_ids = jnp.arange(tile_vec.shape[0], dtype=jnp.int32)
     row_hot = (pair_rows[:, None] == tile_ids[None, :]).astype(jnp.float32)
     col_hot = (pair_cols[:, None] == tile_ids[None, :]).astype(jnp.float32)
-    added = jnp.einsum("cgi,gt->cti", result[:, :, :width], row_hot, precision=highest)
-    return added + jnp.einsum("cgi,gt->cti", result[:, :, width:], col_hot, precision=highest)
+    added = jnp.einsum("gci,gk->kci", result[:, :, :width], row_hot, precision=highest)
+    return added + jnp.einsum("gci,gk->kci", result[:, :, width:], col_hot, precision=highest)
 
 
-def pieces(values):
+def pieces(values, axis):
     high = lax.reduce_precision(values, exponent_bits=8, mantissa_bits=7)
     rest = values - high
     middle = lax.reduce_precision(rest, exponent_bits=8, mantissa_bits=7)
-    return jnp.concatenate([high, middle, rest - middle], axis=0).astype(jnp.bfloat16)
+    return jnp.concatenate([high, middle, rest - middle], axis=axis).astype(jnp.bfloat16)
 
 
-def select(values, hot, spec):
+def to_tiles(values, hot):
     count = values.shape[0]
-    out = jnp.einsum(spec, pieces(values), hot, preferred_element_type=jnp.float32)
+    out = jnp.einsum("cp,ktp->kct", pieces(values, 0), hot, preferred_element_type=jnp.float32)
+    return (out[:, :count] + out[:, count : 2 * count]) + out[:, 2 * count :]
+
+
+def to_points(values_t, hot):
+    count = values_t.shape[1]
+    out = jnp.einsum("kct,ktp->cp", pieces(values_t, 1), hot, preferred_element_type=jnp.float32)
     return (out[:count] + out[count : 2 * count]) + out[2 * count :]
 
 
@@ -74,7 +80,7 @@
 
 
 def per_device(coords, inv_scale, noise, right_side, basis, level_gain, coupling, order, pairs):
-    perm = order[0]
+    perm = order.reshape(order.shape[1])
     columns, points = right_side.shape
     features = coords.shape[0]
     tiles = points // TILE_POINTS
@@ -85,8 +91,8 @@
     position = jnp.arange(points, dtype=jnp.int32)
     hot = (perm[:, None] == position[None, :]).astype(jnp.bfloat16)
     hot = hot.reshape(tiles, TILE_POINTS, points)
-    stacked = select(jnp.concatenate([coords * inv_scale[:, None], right_side], axis=0), hot, "cp,ktp->ckt")
-    tile_coords = stacked[:features]
+    stacked = to_tiles(jnp.concatenate([coords * inv_scale[:, None], right_side], axis=0), hot)
+    tile_coords = stacked[:, :features]
     kern = lax.optimization_barrier(near_kernels(tile_coords, pair_rows, pair_cols))
     scales = 2.0 ** ((1.0 - jnp.arange(levels, dtype=jnp.float32)) / 2.0)
 
@@ -103,24 +109,24 @@
     solution = jnp.zeros_like(right_side)
     residual = right_side
     direction = right_side
-    direction_t = stacked[features:]
+    direction_t = stacked[:, features:]
     for step in range(ITERATIONS):
         if step == 0:
             nodesum, norm_now = sums_with_norm(residual)
             near_t = near_tiles(direction_t)
             late_t, nodesum = lax.optimization_barrier((near_t, nodesum))
-            near = select(late_t, hot, "ckt,ktp->cp")
+            near = to_points(late_t, hot)
         else:
             residual_sum, norm_next = sums_with_norm(residual)
-            residual_t = select(residual, hot, "cp,ktp->ckt")
+            residual_t = to_tiles(residual, hot)
             residual_near_t = near_tiles(residual_t)
             late_t, residual_sum = lax.optimization_barrier((residual_near_t, residual_sum))
             ratio = norm_next / norm_now
             direction = residual + ratio[:, None] * direction
-            direction_t = residual_t + ratio[:, None, None] * direction_t
+            direction_t = residual_t + ratio[None, :, None] * direction_t
             nodesum = residual_sum + ratio[None, :, None] * nodesum
-            near_t = residual_near_t + ratio[:, None, None] * near_t
-            near = select(late_t, hot, "ckt,ktp->cp") + ratio[:, None] * near
+            near_t = residual_near_t + ratio[None, :, None] * near_t
+            near = to_points(late_t, hot) + ratio[:, None] * near
             norm_now = norm_next
         coupled = jnp.einsum("lcr,lrs->lcs", nodesum, coupling, precision=highest)
         coupled = (
@@ -129,7 +135,7 @@
         back = jnp.einsum("lcr,rp->lcp", coupled, basis, precision=highest)
         far = jnp.sum(back * level_gain[:, None, :], axis=0)
         base = noise[None, :] * direction + far
-        local = jnp.sum(direction * base, axis=1) + jnp.sum(direction_t * near_t, axis=(1, 2))
+        local = jnp.sum(direction * base, axis=1) + jnp.sum(direction_t * near_t, axis=(0, 2))
         curve = butterfly(local)
         alpha = norm_now / curve
         solution = solution + alpha[:, None] * direction

time: 104 us -> 104 us (level)
  no operation moved by 1% of the time
where the time goes in v5:
time: 104 us
  matrix products  35.8 us (34%)
  waiting for transfers between devices  31.1 us (30%)
  starting transfers between devices  25 us (24%)
  other arithmetic  6.66 us (6%)
  local copies, waits for them, and re-layouts  4.38 us (4%)
  between operations  1.13 us (1%)
    ppermute x20, waiting for transfers between devices, swapped(): return lax.ppermute(value, axis, pairs)  31.1 us
    ppermute x20, starting transfers between devices, swapped(): return lax.ppermute(value, axis, pairs)  25 us
    dot_general x2, matrix products, near_apply(): result = jnp.einsum('gij,gcj->gci', kern, union_vec, precision=highest)  9.46 us
    dot_general x2, matrix products, to_tiles(): jnp.einsum('cp,ktp->kct', pieces(values, 0), hot, preferred_element_type=...  6.97 us
    dot_general x2, matrix products, to_points(): jnp.einsum('kct,ktp->cp', pieces(values_t, 1), hot, preferred_element_typ...  6.92 us
    dot_general x1, matrix products, near_kernels(): gram = jnp.einsum('gfi,gfj->gij', union, union, precision=highest)  4.29 us
    dot_general x2, matrix products, sums_with_norm(): jnp.einsum('lp,cp,rp->lcr', level_gain, values, basis, precision=highest)  3.32 us
  transfers between devices with their start and end apart: 20, of which 15 were waited for; matrix products, arithmetic and copies ran while one was open for 35% of the time, Pallas kernels for 0%

profile of v5, /device:TPU:0, one launch (start us, length us, event | category | flops | bytes accessed | tf_op | source)
XLA Modules:
  0.0 104.0 jit_solution(1697512577307781847)
XLA Ops:
  0.6 1.1 %multiply_reduce_fusion.5 = f32[16]{0:T(128)S(1)} fusion(f32[16,2048]{1,0:T(8,128)} %param.12), kind=kLoop, calls=%fused_computation.113 | loop fusion | flops 65520 | bytes 131136 | tf_op jit(solution)/shard_map/reduce_sum | solution.py:104
  1.9 2.1 %convolution_bitcast_fusion.1 = f32[5,16,128]{2,1,0:T(8,128)S(1)} fusion(f32[128,2048]{1,0:T(8,128)S(1)} %copy-done, f32[2048,5]{0,1:T(8,128)} %bitcast.71, f32[2048,16]{0,1:T(8,128)} %bitcast.69), kind=kOutput, calls=%fused_computation.25 | convolution fusion | flops 251822080 | bytes 1261568 | tf_op jit(solution)/shard_map/lp,cp,rp->lcr/dot_general | solution.py:103
  4.1 3.0 %collective-permute-start = (f32[6,16,128]{2,1,0:T(8,128)S(1)}, f32[6,16,128]{2,1,0:T(8,128)S(1)}, u32[]{:S(2)}, u32[]{:S(2)}) collective-permute-start(f32[6,16,128]{2,1,0:T(8,128)S(1)} %pad_maximum_fusion.1), channel_id=1, source_target_pairs={{0,1},{1,0},{2,3},{3,2},{4,5},{5,4},{6,7},{7,6},{8,9},{9,8},{10,11... | collective-permute-start | bytes 147464 | tf_op jit(solution)/shard_map/ppermute | solution.py:19
  7.7 1.4 %reduce.9 = s32[2048]{0:T(1024)S(1)} reduce(s32[1,2048]{1,0:T(1,128)} %param.16, s32[]{:T(128)} %broadcast.141), dimensions={0}, to_apply=%param.16.reduce_sub_computation.3 | reduce | bytes 16388 | tf_op args[7]
  9.1 0.9 broadcast_multiply_fusion
  10.0 1.0 reduce-precision_convert_fusion.1
  10.9 3.5 %fusion.10 = f32[8,72,256]{2,1,0:T(8,128)S(1)} fusion(s32[8,256]{1,0:T(8,128)S(1)} %eq.29, bf16[24,2048]{1,0:T(8,128)(2,1)S(1)} %get-tuple-element.22, bf16[24,2048]{1,0:T(8,128)(2,1)S(1)} %get-tuple-element.21, bf16[24,2048]{1,0:T(8,128)(2,1)S(1)} %get-tuple-element.20), kind=kOutput, calls=%fused_computation.20 | convolution fusion | flops 609058816 | bytes 892928 | tf_op jit(solution)/shard_map/cp,ktp->kct/dot_general | solution.py:50
  15.7 0.6 gather_fusion.1
  16.2 0.6 gather_fusion
  16.9 4.3 %exponential_multiply_fusion = f32[4,512,512]{2,1,0:T(8,128)S(1)} fusion(f32[4,8,512]{2,1,0:T(8,128)S(1)} %constant_dynamic-update-slice_fusion, f32[4,512]{1,0:T(4,128)S(1)} %multiply_reduce_fusion.6), kind=kOutput, calls=%fused_computation.15 | convolution fusion | flops 105906176 | bytes 4268032 | tf_op jit(solution)/shard_map/gfi,gfj->gij/dot_general | solution.py:24
  21.2 3.6 %fusion.52 = f32[4,16,512]{2,1,0:T(8,128)S(1)} fusion(f32[4,512,512]{2,1,0:T(8,128)S(1)} %exponential_multiply_fusion, f32[4,16,256]{2,1,0:T(8,128)S(1)} %gather_fusion.1, f32[4,16,256]{2,1,0:T(8,128)S(1)} %gather_fusion), kind=kOutput, calls=%fused_computation.93 | convolution fusion | flops 201359360 | bytes 4456448 | tf_op jit(solution)/shard_map/gij,gcj->gci/dot_general | solution.py:33
  24.9 2.7 %collective-permute-start.1 = (f32[5,16,128]{2,1,0:T(8,128)S(1)}, f32[5,16,128]{2,1,0:T(8,128)S(1)}, u32[]{:S(2)}, u32[]{:S(2)}) collective-permute-start(f32[5,16,128]{2,1,0:T(8,128)S(1)} %slice.180), channel_id=1, source_target_pairs={{0,2},{1,3},{2,0},{3,1},{4,6},{5,7},{6,4},{7,5},{8,10},{9,11},{10,... | collective-permute-start | bytes 122888 | tf_op jit(solution)/shard_map/ppermute | solution.py:19
  27.9 2.0 %collective-permute-done.1 = f32[5,16,128]{2,1,0:T(8,128)S(1)} collective-permute-done((f32[5,16,128]{2,1,0:T(8,128)S(1)}, f32[5,16,128]{2,1,0:T(8,128)S(1)}, u32[]{:S(2)}, u32[]{:S(2)}) %collective-permute-start.1) | collective-permute-done | bytes 40992 | tf_op jit(solution)/shard_map/ppermute | solution.py:19
  30.3 0.9 collective-permute-done.2
  31.1 2.1 %collective-permute-start.3 = (f32[3,16,128]{2,1,0:T(8,128)S(1)}, f32[3,16,128]{2,1,0:T(8,128)S(1)}, u32[]{:S(2)}, u32[]{:S(2)}) collective-permute-start(f32[3,16,128]{2,1,0:T(8,128)S(1)} %slice.182), channel_id=1, source_target_pairs={{0,8},{4,12},{8,0},{12,4},{16,24},{20,28},{24,16},{28,20},{1,9},{5... | collective-permute-start | bytes 73736 | tf_op jit(solution)/shard_map/ppermute | solution.py:19
  33.4 1.8 %collective-permute-done.3 = f32[3,16,128]{2,1,0:T(8,128)S(1)} collective-permute-done((f32[3,16,128]{2,1,0:T(8,128)S(1)}, f32[3,16,128]{2,1,0:T(8,128)S(1)}, u32[]{:S(2)}, u32[]{:S(2)}) %collective-permute-start.3) | collective-permute-done | bytes 24608 | tf_op jit(solution)/shard_map/ppermute | solution.py:19
  35.2 1.9 %collective-permute-start.4 = (f32[2,16,128]{2,1,0:T(8,128)S(1)}, f32[2,16,128]{2,1,0:T(8,128)S(1)}, u32[]{:S(2)}, u32[]{:S(2)}) collective-permute-start(f32[2,16,128]{2,1,0:T(8,128)S(1)} %slice.183), channel_id=1, source_target_pairs={{0,16},{4,20},{8,24},{12,28},{16,0},{20,4},{24,8},{28,12},{1,17},{... | collective-permute-start | bytes 49160 | tf_op jit(solution)/shard_map/ppermute | solution.py:19
  37.2 1.9 %collective-permute-done.4 = f32[2,16,128]{2,1,0:T(8,128)S(1)} collective-permute-done((f32[2,16,128]{2,1,0:T(8,128)S(1)}, f32[2,16,128]{2,1,0:T(8,128)S(1)}, u32[]{:S(2)}, u32[]{:S(2)}) %collective-permute-start.4) | collective-permute-done | bytes 16416 | tf_op jit(solution)/shard_map/ppermute | solution.py:19
  39.4 0.6 convolution_multiply_fusion.3
  40.0 0.8 fusion.11
  41.2 3.4 %collective-permute-done.5 = f32[16]{0:T(128)S(1)} collective-permute-done((f32[16]{0:T(128)S(1)}, f32[16]{0:T(128)S(1)}, u32[]{:S(2)}, u32[]{:S(2)}) %collective-permute-start.5) | collective-permute-done | bytes 96 | tf_op jit(solution)/shard_map/ppermute | solution.py:19
  44.6 2.6 %collective-permute-start.6 = (f32[16]{0:T(128)S(1)}, f32[16]{0:T(128)S(1)}, u32[]{:S(2)}, u32[]{:S(2)}) collective-permute-start(f32[16]{0:T(128)S(1)} %add.178), channel_id=1, source_target_pairs={{0,2},{1,3},{2,0},{3,1},{4,6},{5,7},{6,4},{7,5},{8,10},{9,11},{10,... | collective-permute-start | bytes 200 | tf_op jit(solution)/shard_map/ppermute | solution.py:19
  47.2 1.8 %collective-permute-done.6 = f32[16]{0:T(128)S(1)} collective-permute-done((f32[16]{0:T(128)S(1)}, f32[16]{0:T(128)S(1)}, u32[]{:S(2)}, u32[]{:S(2)}) %collective-permute-start.6) | collective-permute-done | bytes 96 | tf_op jit(solution)/shard_map/ppermute | solution.py:19
  49.1 1.1 %collective-permute-done.7 = f32[16]{0:T(128)S(1)} collective-permute-done((f32[16]{0:T(128)S(1)}, f32[16]{0:T(128)S(1)}, u32[]{:S(2)}, u32[]{:S(2)}) %collective-permute-start.7) | collective-permute-done | bytes 96 | tf_op jit(solution)/shard_map/ppermute | solution.py:19
  50.2 1.8 %collective-permute-start.8 = (f32[16]{0:T(128)S(1)}, f32[16]{0:T(128)S(1)}, u32[]{:S(2)}, u32[]{:S(2)}) collective-permute-start(f32[16]{0:T(128)S(1)} %add.180), channel_id=1, source_target_pairs={{0,8},{4,12},{8,0},{12,4},{16,24},{20,28},{24,16},{28,20},{1,9},{5... | collective-permute-start | bytes 200 | tf_op jit(solution)/shard_map/ppermute | solution.py:19
  52.0 3.5 %fusion.8 = f32[48,2048]{1,0:T(8,128)S(1)} fusion(s32[8,256]{1,0:T(8,128)S(1)} %eq.29, bf16[8,16,256]{2,1,0:T(8,128)(2,1)S(1)} %get-tuple-element.32, bf16[8,16,256]{2,1,0:T(8,128)(2,1)S(1)} %get-tuple-element.33, bf16[8,16,256]{2,1,0:T(8,128)(2,1)S(1)} %get-tuple-element.31), kind=kOutput, calls=%fused_computation.18 | convolution fusion | flops 407437312 | bytes 598016 | tf_op jit(solution)/shard_map/kct,ktp->cp/dot_general | solution.py:56
  55.5 1.6 %collective-permute-start.9 = (f32[16]{0:T(128)S(1)}, f32[16]{0:T(128)S(1)}, u32[]{:S(2)}, u32[]{:S(2)}) collective-permute-start(f32[16]{0:T(128)S(1)} %add.181), channel_id=1, source_target_pairs={{0,16},{4,20},{8,24},{12,28},{16,0},{20,4},{24,8},{28,12},{1,17},{... | collective-permute-start | bytes 200 | tf_op jit(solution)/shard_map/ppermute | solution.py:19
  57.2 1.9 %collective-permute-done.9 = f32[16]{0:T(128)S(1)} collective-permute-done((f32[16]{0:T(128)S(1)}, f32[16]{0:T(128)S(1)}, u32[]{:S(2)}, u32[]{:S(2)}) %collective-permute-start.9) | collective-permute-done | bytes 96 | tf_op jit(solution)/shard_map/ppermute | solution.py:19
  59.3 1.2 %convolution_bitcast_fusion = f32[5,16,128]{2,1,0:T(8,128)S(1)} fusion(f32[128,2048]{1,0:T(8,128)S(1)} %copy-done, f32[2048,16]{0,1:T(8,128)S(1)} %bitcast.70, f32[2048,5]{0,1:T(8,128)S(1)} %bitcast.72), kind=kOutput, calls=%fused_computation.24 | convolution fusion | flops 251822080 | bytes 1261568 | tf_op jit(solution)/shard_map/lp,cp,rp->lcr/dot_general | solution.py:103
  60.8 3.5 %fusion.13 = f32[8,48,256]{2,1,0:T(8,128)S(1)} fusion(s32[8,256]{1,0:T(8,128)S(1)} %eq.29, bf16[16,2048]{1,0:T(8,128)(2,1)S(1)} %get-tuple-element.29, bf16[16,2048]{1,0:T(8,128)(2,1)S(1)} %get-tuple-element.28, bf16[16,2048]{1,0:T(8,128)(2,1)S(1)} %get-tuple-element.14), kind=kOutput, calls=%fused_computation.23 | convolution fusion | flops 407437312 | bytes 598016 | tf_op jit(solution)/shard_map/cp,ktp->kct/dot_general | solution.py:50
  64.3 0.6 gather_fusion.5
  65.4 2.6 %collective-permute-start.11 = (f32[5,16,128]{2,1,0:T(8,128)S(1)}, f32[5,16,128]{2,1,0:T(8,128)S(1)}, u32[]{:S(2)}, u32[]{:S(2)}) collective-permute-start(f32[5,16,128]{2,1,0:T(8,128)S(1)} %slice.196), channel_id=1, source_target_pairs={{0,2},{1,3},{2,0},{3,1},{4,6},{5,7},{6,4},{7,5},{8,10},{9,11},{10,... | collective-permute-start | bytes 122888 | tf_op jit(solution)/shard_map/ppermute | solution.py:19
  68.1 5.9 %fusion.56 = f32[4,16,512]{2,1,0:T(8,128)S(1)} fusion(f32[4,512,512]{2,1,0:T(8,128)} %copy-done.1, f32[4,16,256]{2,1,0:T(8,128)S(1)} %gather_fusion.5, f32[4,16,256]{2,1,0:T(8,128)S(1)} %gather_fusion.4), kind=kOutput, calls=%fused_computation.97 | convolution fusion | flops 201359360 | bytes 4456448 | tf_op jit(solution)/shard_map/gij,gcj->gci/dot_general | solution.py:33
  74.1 1.2 %collective-permute-done.12 = f32[4,16,128]{2,1,0:T(8,128)S(1)} collective-permute-done((f32[4,16,128]{2,1,0:T(8,128)S(1)}, f32[4,16,128]{2,1,0:T(8,128)S(1)}, u32[]{:S(2)}, u32[]{:S(2)}) %collective-permute-start.12) | collective-permute-done | bytes 32800 | tf_op jit(solution)/shard_map/ppermute | solution.py:19
  75.3 0.6 collective-permute-start.13
  76.2 3.0 %collective-permute-done.13 = f32[3,16,128]{2,1,0:T(8,128)S(1)} collective-permute-done((f32[3,16,128]{2,1,0:T(8,128)S(1)}, f32[3,16,128]{2,1,0:T(8,128)S(1)}, u32[]{:S(2)}, u32[]{:S(2)}) %collective-permute-start.13) | collective-permute-done | bytes 24608 | tf_op jit(solution)/shard_map/ppermute | solution.py:19
  79.2 1.6 %collective-permute-start.14 = (f32[2,16,128]{2,1,0:T(8,128)S(1)}, f32[2,16,128]{2,1,0:T(8,128)S(1)}, u32[]{:S(2)}, u32[]{:S(2)}) collective-permute-start(f32[2,16,128]{2,1,0:T(8,128)S(1)} %slice.199), channel_id=1, source_target_pairs={{0,16},{4,20},{8,24},{12,28},{16,0},{20,4},{24,8},{28,12},{1,17},{... | collective-permute-start | bytes 49160 | tf_op jit(solution)/shard_map/ppermute | solution.py:19
  81.1 1.9 %collective-permute-done.14 = f32[2,16,128]{2,1,0:T(8,128)S(1)} collective-permute-done((f32[2,16,128]{2,1,0:T(8,128)S(1)}, f32[2,16,128]{2,1,0:T(8,128)S(1)}, u32[]{:S(2)}, u32[]{:S(2)}) %collective-permute-start.14) | collective-permute-done | bytes 16416 | tf_op jit(solution)/shard_map/ppermute | solution.py:19
  83.8 0.6 convolution_multiply_fusion.2
  84.4 0.8 fusion.12
  85.4 1.6 %collective-permute-start.15 = (f32[16]{0:T(128)S(1)}, f32[16]{0:T(128)S(1)}, u32[]{:S(2)}, u32[]{:S(2)}) collective-permute-start(f32[16]{0:T(128)S(1)} %add.199), channel_id=1, source_target_pairs={{0,1},{1,0},{2,3},{3,2},{4,5},{5,4},{6,7},{7,6},{8,9},{9,8},{10,11... | collective-permute-start | bytes 200 | tf_op jit(solution)/shard_map/ppermute | solution.py:19
  87.0 2.0 %collective-permute-done.15 = f32[16]{0:T(128)S(1)} collective-permute-done((f32[16]{0:T(128)S(1)}, f32[16]{0:T(128)S(1)}, u32[]{:S(2)}, u32[]{:S(2)}) %collective-permute-start.15) | collective-permute-done | bytes 96 | tf_op jit(solution)/shard_map/ppermute | solution.py:19
  89.4 4.1 %collective-permute-done.16 = f32[16]{0:T(128)S(1)} collective-permute-done((f32[16]{0:T(128)S(1)}, f32[16]{0:T(128)S(1)}, u32[]{:S(2)}, u32[]{:S(2)}) %collective-permute-start.16) | collective-permute-done | bytes 96 | tf_op jit(solution)/shard_map/ppermute | solution.py:19
  93.5 1.1 %collective-permute-done.17 = f32[16]{0:T(128)S(1)} collective-permute-done((f32[16]{0:T(128)S(1)}, f32[16]{0:T(128)S(1)}, u32[]{:S(2)}, u32[]{:S(2)}) %collective-permute-start.17) | collective-permute-done | bytes 96 | tf_op jit(solution)/shard_map/ppermute | solution.py:19
  95.2 3.0 %collective-permute-done.18 = f32[16]{0:T(128)S(1)} collective-permute-done((f32[16]{0:T(128)S(1)}, f32[16]{0:T(128)S(1)}, u32[]{:S(2)}, u32[]{:S(2)}) %collective-permute-start.18) | collective-permute-done | bytes 96 | tf_op jit(solution)/shard_map/ppermute | solution.py:19
  98.2 1.5 %collective-permute-start.19 = (f32[16]{0:T(128)S(1)}, f32[16]{0:T(128)S(1)}, u32[]{:S(2)}, u32[]{:S(2)}) collective-permute-start(f32[16]{0:T(128)S(1)} %add.203), channel_id=1, source_target_pairs={{0,16},{4,20},{8,24},{12,28},{16,0},{20,4},{24,8},{28,12},{1,17},{... | collective-permute-start | bytes 200 | tf_op jit(solution)/shard_map/ppermute | solution.py:19
  99.7 3.5 %fusion.9 = f32[48,2048]{1,0:T(8,128)S(1)} fusion(s32[8,256]{1,0:T(8,128)S(1)} %eq.29, bf16[8,16,256]{2,1,0:T(8,128)(2,1)S(1)} %get-tuple-element.24, bf16[8,16,256]{2,1,0:T(8,128)(2,1)S(1)} %get-tuple-element.25, bf16[8,16,256]{2,1,0:T(8,128)(2,1)S(1)} %get-tuple-element.23), kind=kOutput, calls=%fused_computation.19 | convolution fusion | flops 407437312 | bytes 598016 | tf_op jit(solution)/shard_map/kct,ktp->cp/dot_general | solution.py:56
  103.2 0.8 fusion.51
  (100 shorter events, 7.6 us)
Async XLA Ops:
  0.6 1.3 %copy-start = (f32[128,2048]{1,0:T(8,128)S(1)}, f32[128,2048]{1,0:T(8,128)}, u32[]{:S(2)}) copy-start(f32[128,2048]{1,0:T(8,128)} %param.13) | copy-start | bytes 3145732
  4.1 20.7 %collective-permute-start = (f32[6,16,128]{2,1,0:T(8,128)S(1)}, f32[6,16,128]{2,1,0:T(8,128)S(1)}, u32[]{:S(2)}, u32[]{:S(2)}) collective-permute-start(f32[6,16,128]{2,1,0:T(8,128)S(1)} %pad_maximum_fusion.1), channel_id=1, source_target_pairs={{0,1},{1,0},{2,3},{3,2},{4,5},{5,4},{6,7},{7,6},{8,9},{9,8},{10,11... | collective-permute-start | bytes 147464 | tf_op jit(solution)/shard_map/ppermute | solution.py:19
  10.0 4.5 %copy-start.6 = (s32[1,2,4]{2,1,0:T(2,128)S(1)}, s32[1,2,4]{2,1,0:T(2,128)}, u32[]{:S(2)}) copy-start(s32[1,2,4]{2,1,0:T(2,128)} %param.17) | copy-start | bytes 100
  21.2 19.7 %copy-start.1 = (f32[4,512,512]{2,1,0:T(8,128)}, f32[4,512,512]{2,1,0:T(8,128)S(1)}, u32[]{:S(2)}) copy-start(f32[4,512,512]{2,1,0:T(8,128)S(1)} %exponential_multiply_fusion) | copy-start | bytes 12582916
  21.2 17.9 %copy-start.3 = (f32[5,128,128]{2,1,0:T(8,128)S(1)}, f32[5,128,128]{2,1,0:T(8,128)}, u32[]{:S(2)}) copy-start(f32[5,128,128]{2,1,0:T(8,128)} %param.15) | copy-start | bytes 983044
  21.2 18.9 %copy-start.4 = (f32[5,2048]{1,0:T(8,128)S(1)}, f32[5,2048]{1,0:T(8,128)}, u32[]{:S(2)}) copy-start(f32[5,2048]{1,0:T(8,128)} %param.14) | copy-start | bytes 122884
  21.2 19.6 %copy-start.2 = (f32[16,2048]{1,0:T(8,128)S(1)}, f32[16,2048]{1,0:T(8,128)}, u32[]{:S(2)}) copy-start(f32[16,2048]{1,0:T(8,128)} %param.12) | copy-start | bytes 393220
  21.2 19.6 %copy-start.5 = (f32[2048]{0:T(1024)S(1)}, f32[2048]{0:T(1024)}, u32[]{:S(2)}) copy-start(f32[2048]{0:T(1024)} %param.11) | copy-start | bytes 24580
  24.9 5.0 %collective-permute-start.1 = (f32[5,16,128]{2,1,0:T(8,128)S(1)}, f32[5,16,128]{2,1,0:T(8,128)S(1)}, u32[]{:S(2)}, u32[]{:S(2)}) collective-permute-start(f32[5,16,128]{2,1,0:T(8,128)S(1)} %slice.180), channel_id=1, source_target_pairs={{0,2},{1,3},{2,0},{3,1},{4,6},{5,7},{6,4},{7,5},{8,10},{9,11},{10,... | collective-permute-start | bytes 122888 | tf_op jit(solution)/shard_map/ppermute | solution.py:19
  29.9 1.3 %collective-permute-start.2 = (f32[4,16,128]{2,1,0:T(8,128)S(1)}, f32[4,16,128]{2,1,0:T(8,128)S(1)}, u32[]{:S(2)}, u32[]{:S(2)}) collective-permute-start(f32[4,16,128]{2,1,0:T(8,128)S(1)} %slice.181), channel_id=1, source_target_pairs={{0,4},{4,0},{8,12},{12,8},{16,20},{20,16},{24,28},{28,24},{1,5},{5... | collective-permute-start | bytes 98312 | tf_op jit(solution)/shard_map/ppermute | solution.py:19
  31.1 4.1 %collective-permute-start.3 = (f32[3,16,128]{2,1,0:T(8,128)S(1)}, f32[3,16,128]{2,1,0:T(8,128)S(1)}, u32[]{:S(2)}, u32[]{:S(2)}) collective-permute-start(f32[3,16,128]{2,1,0:T(8,128)S(1)} %slice.182), channel_id=1, source_target_pairs={{0,8},{4,12},{8,0},{12,4},{16,24},{20,28},{24,16},{28,20},{1,9},{5... | collective-permute-start | bytes 73736 | tf_op jit(solution)/shard_map/ppermute | solution.py:19
  35.2 3.8 %collective-permute-start.4 = (f32[2,16,128]{2,1,0:T(8,128)S(1)}, f32[2,16,128]{2,1,0:T(8,128)S(1)}, u32[]{:S(2)}, u32[]{:S(2)}) collective-permute-start(f32[2,16,128]{2,1,0:T(8,128)S(1)} %slice.183), channel_id=1, source_target_pairs={{0,16},{4,20},{8,24},{12,28},{16,0},{20,4},{24,8},{28,12},{1,17},{... | collective-permute-start | bytes 49160 | tf_op jit(solution)/shard_map/ppermute | solution.py:19
  41.0 3.6 %collective-permute-start.5 = (f32[16]{0:T(128)S(1)}, f32[16]{0:T(128)S(1)}, u32[]{:S(2)}, u32[]{:S(2)}) collective-permute-start(f32[16]{0:T(128)S(1)} %add.177), channel_id=1, source_target_pairs={{0,1},{1,0},{2,3},{3,2},{4,5},{5,4},{6,7},{7,6},{8,9},{9,8},{10,11... | collective-permute-start | bytes 200 | tf_op jit(solution)/shard_map/ppermute | solution.py:19
  44.6 4.4 %collective-permute-start.6 = (f32[16]{0:T(128)S(1)}, f32[16]{0:T(128)S(1)}, u32[]{:S(2)}, u32[]{:S(2)}) collective-permute-start(f32[16]{0:T(128)S(1)} %add.178), channel_id=1, source_target_pairs={{0,2},{1,3},{2,0},{3,1},{4,6},{5,7},{6,4},{7,5},{8,10},{9,11},{10,... | collective-permute-start | bytes 200 | tf_op jit(solution)/shard_map/ppermute | solution.py:19
  49.0 1.1 %collective-permute-start.7 = (f32[16]{0:T(128)S(1)}, f32[16]{0:T(128)S(1)}, u32[]{:S(2)}, u32[]{:S(2)}) collective-permute-start(f32[16]{0:T(128)S(1)} %add.179), channel_id=1, source_target_pairs={{0,4},{4,0},{8,12},{12,8},{16,20},{20,16},{24,28},{28,24},{1,5},{5... | collective-permute-start | bytes 200 | tf_op jit(solution)/shard_map/ppermute | solution.py:19
  50.2 5.3 %collective-permute-start.8 = (f32[16]{0:T(128)S(1)}, f32[16]{0:T(128)S(1)}, u32[]{:S(2)}, u32[]{:S(2)}) collective-permute-start(f32[16]{0:T(128)S(1)} %add.180), channel_id=1, source_target_pairs={{0,8},{4,12},{8,0},{12,4},{16,24},{20,28},{24,16},{28,20},{1,9},{5... | collective-permute-start | bytes 200 | tf_op jit(solution)/shard_map/ppermute | solution.py:19
  55.5 3.6 %collective-permute-start.9 = (f32[16]{0:T(128)S(1)}, f32[16]{0:T(128)S(1)}, u32[]{:S(2)}, u32[]{:S(2)}) collective-permute-start(f32[16]{0:T(128)S(1)} %add.181), channel_id=1, source_target_pairs={{0,16},{4,20},{8,24},{12,28},{16,0},{20,4},{24,8},{28,12},{1,17},{... | collective-permute-start | bytes 200 | tf_op jit(solution)/shard_map/ppermute | solution.py:19
  60.6 4.8 %collective-permute-start.10 = (f32[6,16,128]{2,1,0:T(8,128)S(1)}, f32[6,16,128]{2,1,0:T(8,128)S(1)}, u32[]{:S(2)}, u32[]{:S(2)}) collective-permute-start(f32[6,16,128]{2,1,0:T(8,128)S(1)} %pad_maximum_fusion.2), channel_id=1, source_target_pairs={{0,1},{1,0},{2,3},{3,2},{4,5},{5,4},{6,7},{7,6},{8,9},{9,8},{10,11... | collective-permute-start | bytes 147464 | tf_op jit(solution)/shard_map/ppermute | solution.py:19
  65.4 8.5 %collective-permute-start.11 = (f32[5,16,128]{2,1,0:T(8,128)S(1)}, f32[5,16,128]{2,1,0:T(8,128)S(1)}, u32[]{:S(2)}, u32[]{:S(2)}) collective-permute-start(f32[5,16,128]{2,1,0:T(8,128)S(1)} %slice.196), channel_id=1, source_target_pairs={{0,2},{1,3},{2,0},{3,1},{4,6},{5,7},{6,4},{7,5},{8,10},{9,11},{10,... | collective-permute-start | bytes 122888 | tf_op jit(solution)/shard_map/ppermute | solution.py:19
  74.0 1.3 %collective-permute-start.12 = (f32[4,16,128]{2,1,0:T(8,128)S(1)}, f32[4,16,128]{2,1,0:T(8,128)S(1)}, u32[]{:S(2)}, u32[]{:S(2)}) collective-permute-start(f32[4,16,128]{2,1,0:T(8,128)S(1)} %slice.197), channel_id=1, source_target_pairs={{0,4},{4,0},{8,12},{12,8},{16,20},{20,16},{24,28},{28,24},{1,5},{5... | collective-permute-start | bytes 98312 | tf_op jit(solution)/shard_map/ppermute | solution.py:19
  75.3 3.9 %collective-permute-start.13 = (f32[3,16,128]{2,1,0:T(8,128)S(1)}, f32[3,16,128]{2,1,0:T(8,128)S(1)}, u32[]{:S(2)}, u32[]{:S(2)}) collective-permute-start(f32[3,16,128]{2,1,0:T(8,128)S(1)} %slice.198), channel_id=1, source_target_pairs={{0,8},{4,12},{8,0},{12,4},{16,24},{20,28},{24,16},{28,20},{1,9},{5... | collective-permute-start | bytes 73736 | tf_op jit(solution)/shard_map/ppermute | solution.py:19
  79.2 3.8 %collective-permute-start.14 = (f32[2,16,128]{2,1,0:T(8,128)S(1)}, f32[2,16,128]{2,1,0:T(8,128)S(1)}, u32[]{:S(2)}, u32[]{:S(2)}) collective-permute-start(f32[2,16,128]{2,1,0:T(8,128)S(1)} %slice.199), channel_id=1, source_target_pairs={{0,16},{4,20},{8,24},{12,28},{16,0},{20,4},{24,8},{28,12},{1,17},{... | collective-permute-start | bytes 49160 | tf_op jit(solution)/shard_map/ppermute | solution.py:19
  85.4 3.6 %collective-permute-start.15 = (f32[16]{0:T(128)S(1)}, f32[16]{0:T(128)S(1)}, u32[]{:S(2)}, u32[]{:S(2)}) collective-permute-start(f32[16]{0:T(128)S(1)} %add.199), channel_id=1, source_target_pairs={{0,1},{1,0},{2,3},{3,2},{4,5},{5,4},{6,7},{7,6},{8,9},{9,8},{10,11... | collective-permute-start | bytes 200 | tf_op jit(solution)/shard_map/ppermute | solution.py:19
  89.0 4.4 %collective-permute-start.16 = (f32[16]{0:T(128)S(1)}, f32[16]{0:T(128)S(1)}, u32[]{:S(2)}, u32[]{:S(2)}) collective-permute-start(f32[16]{0:T(128)S(1)} %add.200), channel_id=1, source_target_pairs={{0,2},{1,3},{2,0},{3,1},{4,6},{5,7},{6,4},{7,5},{8,10},{9,11},{10,... | collective-permute-start | bytes 200 | tf_op jit(solution)/shard_map/ppermute | solution.py:19
  93.5 1.1 %collective-permute-start.17 = (f32[16]{0:T(128)S(1)}, f32[16]{0:T(128)S(1)}, u32[]{:S(2)}, u32[]{:S(2)}) collective-permute-start(f32[16]{0:T(128)S(1)} %add.201), channel_id=1, source_target_pairs={{0,4},{4,0},{8,12},{12,8},{16,20},{20,16},{24,28},{28,24},{1,5},{5... | collective-permute-start | bytes 200 | tf_op jit(solution)/shard_map/ppermute | solution.py:19
  94.6 3.5 %collective-permute-start.18 = (f32[16]{0:T(128)S(1)}, f32[16]{0:T(128)S(1)}, u32[]{:S(2)}, u32[]{:S(2)}) collective-permute-start(f32[16]{0:T(128)S(1)} %add.202), channel_id=1, source_target_pairs={{0,8},{4,12},{8,0},{12,4},{16,24},{20,28},{24,16},{28,20},{1,9},{5... | collective-permute-start | bytes 200 | tf_op jit(solution)/shard_map/ppermute | solution.py:19
  98.2 5.0 %collective-permute-start.19 = (f32[16]{0:T(128)S(1)}, f32[16]{0:T(128)S(1)}, u32[]{:S(2)}, u32[]{:S(2)}) collective-permute-start(f32[16]{0:T(128)S(1)} %add.203), channel_id=1, source_target_pairs={{0,16},{4,20},{8,24},{12,28},{16,0},{20,4},{24,8},{28,12},{1,17},{... | collective-permute-start | bytes 200 | tf_op jit(solution)/shard_map/ppermute | solution.py:19

commit v6 on v5

--- a/solution.py
+++ b/solution.py
@@ -57,18 +57,23 @@
     return (out[:count] + out[count : 2 * count]) + out[2 * count :]
 
 
-def tree_sums(proj):
+def tree_sums(proj, stages, state):
     low_count = lax.axis_size("gy").bit_length() - 1
     high_count = lax.axis_size("gx").bit_length() - 1
+    rounds = [("gy", bit, bit) for bit in range(low_count)]
+    rounds += [("gx", bit, low_count + bit) for bit in range(high_count)]
     running = proj
-    for bit in range(low_count):
-        partner = swapped(running[bit:], "gy", bit)
-        running = jnp.concatenate([running[:bit], running[bit:] + partner], axis=0)
-    for bit in range(high_count):
-        level = low_count + bit
-        partner = swapped(running[level:], "gx", bit)
+    for index, (axis, bit, level) in enumerate(rounds):
+        partner = swapped(running[level:], axis, bit)
+        if index < len(stages):
+            state, running = lax.optimization_barrier((state, running))
+            state = stages[index](state)
         running = jnp.concatenate([running[:level], running[level:] + partner], axis=0)
-    return running
+        if index < len(stages):
+            running, state = lax.optimization_barrier((running, state))
+    for stage in stages[len(rounds) :]:
+        state = stage(state)
+    return running, state
 
 
 def butterfly(value):
@@ -91,35 +96,51 @@
     position = jnp.arange(points, dtype=jnp.int32)
     hot = (perm[:, None] == position[None, :]).astype(jnp.bfloat16)
     hot = hot.reshape(tiles, TILE_POINTS, points)
-    stacked = to_tiles(jnp.concatenate([coords * inv_scale[:, None], right_side], axis=0), hot)
-    tile_coords = stacked[:, :features]
-    kern = lax.optimization_barrier(near_kernels(tile_coords, pair_rows, pair_cols))
     scales = 2.0 ** ((1.0 - jnp.arange(levels, dtype=jnp.float32)) / 2.0)
 
-    def near_tiles(values_t):
-        return near_apply(kern, values_t, pair_rows, pair_cols)
-
-    def sums_with_norm(values):
+    def sums_with_norm(values, stages, state):
         proj = jnp.einsum("lp,cp,rp->lcr", level_gain, values, basis, precision=highest)
         norm = jnp.sum(values * values, axis=1)
         extra = jnp.broadcast_to(norm[None, :, None], (1, columns, rank))
-        running = tree_sums(jnp.concatenate([proj, extra], axis=0))
-        return running[:levels], running[levels, :, 0]
+        running, state = tree_sums(jnp.concatenate([proj, extra], axis=0), stages, state)
+        return running[:levels], running[levels, :, 0], state
+
+    def permute_inputs(unused):
+        stacked = to_tiles(jnp.concatenate([coords * inv_scale[:, None], right_side], axis=0), hot)
+        return stacked[:, :features], stacked[:, features:]
+
+    def kernel_blocks(state):
+        tile_coords, direction_t = state
+        return near_kernels(tile_coords, pair_rows, pair_cols), direction_t
+
+    def first_near(state):
+        kern, direction_t = state
+        return kern, direction_t, near_apply(kern, direction_t, pair_rows, pair_cols)
+
+    def permute_residual(state):
+        kern, values = state
+        return kern, to_tiles(values, hot)
+
+    def residual_near(state):
+        kern, values_t = state
+        return values_t, near_apply(kern, values_t, pair_rows, pair_cols)
 
     solution = jnp.zeros_like(right_side)
     residual = right_side
     direction = right_side
-    direction_t = stacked[:, features:]
     for step in range(ITERATIONS):
         if step == 0:
-            nodesum, norm_now = sums_with_norm(residual)
-            near_t = near_tiles(direction_t)
+            stages = [permute_inputs, kernel_blocks, first_near]
+            nodesum, norm_now, (kern, direction_t, near_t) = sums_with_norm(
+                residual, stages, jnp.zeros((), jnp.float32)
+            )
             late_t, nodesum = lax.optimization_barrier((near_t, nodesum))
             near = to_points(late_t, hot)
         else:
-            residual_sum, norm_next = sums_with_norm(residual)
-            residual_t = to_tiles(residual, hot)
-            residual_near_t = near_tiles(residual_t)
+            stages = [permute_residual, residual_near]
+            residual_sum, norm_next, (residual_t, residual_near_t) = sums_with_norm(
+                residual, stages, (kern, residual)
+            )
             late_t, residual_sum = lax.optimization_barrier((residual_near_t, residual_sum))
             ratio = norm_next / norm_now
             direction = residual + ratio[:, None] * direction

time: 104 us -> 105 us (level)
  matrix products: 35.8 us -> 39.3 us
  starting transfers between devices: 25 us -> 21.9 us
  waiting for transfers between devices: 31.1 us -> 29.5 us
    ppermute x20, starting transfers between devices: 25 us -> 21.9 us  [swapped(): return lax.ppermute(value, axis, pairs)]
    dot_general x2, matrix products: 9.46 us -> 11.3 us  [near_apply(): result = jnp.einsum('gij,gcj->gci', kern, union_vec, precision=highest)]
    ppermute x20, waiting for transfers between devices: 31.1 us -> 29.5 us  [swapped(): return lax.ppermute(value, axis, pairs)]
    dot_general x1, matrix products: 4.29 us -> 5.77 us  [near_kernels(): gram = jnp.einsum('gfi,gfj->gij', union, union, precision=highest)]
  transfers between devices with their start and end apart: 20 -> 20, of which waited for: 15 -> 13; matrix products, arithmetic and copies ran while one was open for 35% -> 37% of each run, Pallas kernels for 0% -> 0%
where the time goes in v6:
time: 105 us
  matrix products  39.3 us (37%)
  waiting for transfers between devices  29.5 us (28%)
  starting transfers between devices  21.9 us (21%)
  other arithmetic  7.5 us (7%)
  local copies, waits for them, and re-layouts  5.14 us (5%)
  between operations  1.15 us (1%)
    ppermute x20, waiting for transfers between devices, swapped(): return lax.ppermute(value, axis, pairs)  29.5 us
    ppermute x20, starting transfers between devices, swapped(): return lax.ppermute(value, axis, pairs)  21.9 us
    dot_general x2, matrix products, near_apply(): result = jnp.einsum('gij,gcj->gci', kern, union_vec, precision=highest)  11.3 us
    dot_general x2, matrix products, to_tiles(): jnp.einsum('cp,ktp->kct', pieces(values, 0), hot, preferred_element_type=...  7.19 us
    dot_general x2, matrix products, to_points(): jnp.einsum('kct,ktp->cp', pieces(values_t, 1), hot, preferred_element_typ...  6.92 us
    dot_general x1, matrix products, near_kernels(): gram = jnp.einsum('gfi,gfj->gij', union, union, precision=highest)  5.77 us
    dot_general x2, matrix products, sums_with_norm(): jnp.einsum('lp,cp,rp->lcr', level_gain, values, basis, precision=highest)  3.32 us
  transfers between devices with their start and end apart: 20, of which 13 were waited for; matrix products, arithmetic and copies ran while one was open for 37% of the time, Pallas kernels for 0%

profile of v6, /device:TPU:0, one launch (start us, length us, event | category | flops | bytes accessed | tf_op | source)
XLA Modules:
  0.0 104.6 jit_solution(6173062643606308151)
XLA Ops:
  0.6 1.1 %multiply_reduce_fusion.5 = f32[16]{0:T(128)S(1)} fusion(f32[16,2048]{1,0:T(8,128)} %param.12), kind=kLoop, calls=%fused_computation.113 | loop fusion | flops 65520 | bytes 131136 | tf_op jit(solution)/shard_map/reduce_sum | solution.py:103
  1.9 2.1 %convolution_bitcast_fusion.1 = f32[5,16,128]{2,1,0:T(8,128)S(1)} fusion(f32[128,2048]{1,0:T(8,128)S(1)} %copy-done, f32[2048,5]{0,1:T(8,128)} %bitcast.71, f32[2048,16]{0,1:T(8,128)} %bitcast.69), kind=kOutput, calls=%fused_computation.25 | convolution fusion | flops 251822080 | bytes 1261568 | tf_op jit(solution)/shard_map/lp,cp,rp->lcr/dot_general | solution.py:102
  4.1 3.0 %collective-permute-start = (f32[6,16,128]{2,1,0:T(8,128)S(1)}, f32[6,16,128]{2,1,0:T(8,128)S(1)}, u32[]{:S(2)}, u32[]{:S(2)}) collective-permute-start(f32[6,16,128]{2,1,0:T(8,128)S(1)} %pad_maximum_fusion.1), channel_id=1, source_target_pairs={{0,1},{1,0},{2,3},{3,2},{4,5},{5,4},{6,7},{7,6},{8,9},{9,8},{10,11... | collective-permute-start | bytes 147464 | tf_op jit(solution)/shard_map/ppermute | solution.py:19
  7.2 0.8 fusion.83
  7.9 0.8 slice_bitcast_fusion.1
  9.2 1.4 %reduce.9 = s32[2048]{0:T(1024)S(1)} reduce(s32[1,2048]{1,0:T(1,128)} %param.16, s32[]{:T(128)} %broadcast.125), dimensions={0}, to_apply=%param.16.reduce_sub_computation.3 | reduce | bytes 16388 | tf_op args[7]
  10.6 0.9 broadcast_multiply_fusion
  11.5 0.9 reduce-precision_convert_fusion.1
  12.4 3.5 %fusion.10 = f32[8,72,256]{2,1,0:T(8,128)S(1)} fusion(s32[8,256]{1,0:T(8,128)S(1)} %eq.25, bf16[24,2048]{1,0:T(8,128)(2,1)S(1)} %get-tuple-element.76, bf16[24,2048]{1,0:T(8,128)(2,1)S(1)} %get-tuple-element.75, bf16[24,2048]{1,0:T(8,128)(2,1)S(1)} %get-tuple-element.74), kind=kOutput, calls=%fused_computation.20 | convolution fusion | flops 609058816 | bytes 892928 | tf_op jit(solution)/shard_map/cp,ktp->kct/dot_general | solution.py:50
  16.1 0.6 gather_fusion.1
  17.2 2.7 %collective-permute-start.1 = (f32[5,16,128]{2,1,0:T(8,128)S(1)}, f32[5,16,128]{2,1,0:T(8,128)S(1)}, u32[]{:S(2)}, u32[]{:S(2)}) collective-permute-start(f32[5,16,128]{2,1,0:T(8,128)S(1)} %slice.141), channel_id=1, source_target_pairs={{0,2},{1,3},{2,0},{3,1},{4,6},{5,7},{6,4},{7,5},{8,10},{9,11},{10,... | collective-permute-start | bytes 122888 | tf_op jit(solution)/shard_map/ppermute | solution.py:19
  19.9 5.8 %exponential_multiply_fusion = f32[4,512,512]{2,1,0:T(8,128)} fusion(f32[4,8,512]{2,1,0:T(8,128)S(1)} %constant_dynamic-update-slice_fusion, f32[4,512]{1,0:T(4,128)S(1)} %multiply_reduce_fusion.6), kind=kOutput, calls=%fused_computation.15 | convolution fusion | flops 105906176 | bytes 4268032 | tf_op jit(solution)/shard_map/gfi,gfj->gij/dot_general | solution.py:24
  25.7 0.6 gather_fusion.3
  26.3 0.6 gather_fusion.2
  27.0 5.7 %fusion.52 = f32[4,16,512]{2,1,0:T(8,128)S(1)} fusion(f32[4,512,512]{2,1,0:T(8,128)} %exponential_multiply_fusion, f32[4,16,256]{2,1,0:T(8,128)S(1)} %gather_fusion.3, f32[4,16,256]{2,1,0:T(8,128)S(1)} %gather_fusion.2), kind=kOutput, calls=%fused_computation.93 | convolution fusion | flops 201359360 | bytes 4456448 | tf_op jit(solution)/shard_map/gij,gcj->gci/dot_general | solution.py:33
  33.4 1.6 %collective-permute-start.3 = (f32[3,16,128]{2,1,0:T(8,128)S(1)}, f32[3,16,128]{2,1,0:T(8,128)S(1)}, u32[]{:S(2)}, u32[]{:S(2)}) collective-permute-start(f32[3,16,128]{2,1,0:T(8,128)S(1)} %slice.149), channel_id=1, source_target_pairs={{0,8},{4,12},{8,0},{12,4},{16,24},{20,28},{24,16},{28,20},{1,9},{5... | collective-permute-start | bytes 73736 | tf_op jit(solution)/shard_map/ppermute | solution.py:19
  35.0 2.3 %collective-permute-done.3 = f32[3,16,128]{2,1,0:T(8,128)S(1)} collective-permute-done((f32[3,16,128]{2,1,0:T(8,128)S(1)}, f32[3,16,128]{2,1,0:T(8,128)S(1)}, u32[]{:S(2)}, u32[]{:S(2)}) %collective-permute-start.3) | collective-permute-done | bytes 24608 | tf_op jit(solution)/shard_map/ppermute | solution.py:19
  37.3 1.6 %collective-permute-start.4 = (f32[2,16,128]{2,1,0:T(8,128)S(1)}, f32[2,16,128]{2,1,0:T(8,128)S(1)}, u32[]{:S(2)}, u32[]{:S(2)}) collective-permute-start(f32[2,16,128]{2,1,0:T(8,128)S(1)} %slice.196), channel_id=1, source_target_pairs={{0,16},{4,20},{8,24},{12,28},{16,0},{20,4},{24,8},{28,12},{1,17},{... | collective-permute-start | bytes 49160 | tf_op jit(solution)/shard_map/ppermute | solution.py:19
  39.1 2.1 %collective-permute-done.4 = f32[2,16,128]{2,1,0:T(8,128)S(1)} collective-permute-done((f32[2,16,128]{2,1,0:T(8,128)S(1)}, f32[2,16,128]{2,1,0:T(8,128)S(1)}, u32[]{:S(2)}, u32[]{:S(2)}) %collective-permute-start.4) | collective-permute-done | bytes 16416 | tf_op jit(solution)/shard_map/ppermute | solution.py:19
  41.5 0.6 convolution_multiply_fusion.3
  42.2 0.8 fusion.11
  43.6 3.1 %collective-permute-done.5 = f32[16]{0:T(128)S(1)} collective-permute-done((f32[16]{0:T(128)S(1)}, f32[16]{0:T(128)S(1)}, u32[]{:S(2)}, u32[]{:S(2)}) %collective-permute-start.5) | collective-permute-done | bytes 96 | tf_op jit(solution)/shard_map/ppermute | solution.py:19
  47.0 4.1 %collective-permute-done.6 = f32[16]{0:T(128)S(1)} collective-permute-done((f32[16]{0:T(128)S(1)}, f32[16]{0:T(128)S(1)}, u32[]{:S(2)}, u32[]{:S(2)}) %collective-permute-start.6) | collective-permute-done | bytes 96 | tf_op jit(solution)/shard_map/ppermute | solution.py:19
  51.2 1.1 %collective-permute-done.7 = f32[16]{0:T(128)S(1)} collective-permute-done((f32[16]{0:T(128)S(1)}, f32[16]{0:T(128)S(1)}, u32[]{:S(2)}, u32[]{:S(2)}) %collective-permute-start.7) | collective-permute-done | bytes 96 | tf_op jit(solution)/shard_map/ppermute | solution.py:19
  52.3 1.5 %collective-permute-start.8 = (f32[16]{0:T(128)S(1)}, f32[16]{0:T(128)S(1)}, u32[]{:S(2)}, u32[]{:S(2)}) collective-permute-start(f32[16]{0:T(128)S(1)} %add.180), channel_id=1, source_target_pairs={{0,8},{4,12},{8,0},{12,4},{16,24},{20,28},{24,16},{28,20},{1,9},{5... | collective-permute-start | bytes 200 | tf_op jit(solution)/shard_map/ppermute | solution.py:19
  53.8 3.5 %fusion.8 = f32[48,2048]{1,0:T(8,128)S(1)} fusion(s32[8,256]{1,0:T(8,128)S(1)} %eq.25, bf16[8,16,256]{2,1,0:T(8,128)(2,1)S(1)} %get-tuple-element.86, bf16[8,16,256]{2,1,0:T(8,128)(2,1)S(1)} %get-tuple-element.87, bf16[8,16,256]{2,1,0:T(8,128)(2,1)S(1)} %get-tuple-element.85), kind=kOutput, calls=%fused_computation.18 | convolution fusion | flops 407437312 | bytes 598016 | tf_op jit(solution)/shard_map/kct,ktp->cp/dot_general | solution.py:56
  57.2 1.6 %collective-permute-start.9 = (f32[16]{0:T(128)S(1)}, f32[16]{0:T(128)S(1)}, u32[]{:S(2)}, u32[]{:S(2)}) collective-permute-start(f32[16]{0:T(128)S(1)} %add.181), channel_id=1, source_target_pairs={{0,16},{4,20},{8,24},{12,28},{16,0},{20,4},{24,8},{28,12},{1,17},{... | collective-permute-start | bytes 200 | tf_op jit(solution)/shard_map/ppermute | solution.py:19
  58.9 1.9 %collective-permute-done.9 = f32[16]{0:T(128)S(1)} collective-permute-done((f32[16]{0:T(128)S(1)}, f32[16]{0:T(128)S(1)}, u32[]{:S(2)}, u32[]{:S(2)}) %collective-permute-start.9) | collective-permute-done | bytes 96 | tf_op jit(solution)/shard_map/ppermute | solution.py:19
  61.1 1.2 %convolution_bitcast_fusion = f32[5,16,128]{2,1,0:T(8,128)S(1)} fusion(f32[128,2048]{1,0:T(8,128)S(1)} %copy-done, f32[2048,16]{0,1:T(8,128)S(1)} %bitcast.70, f32[2048,5]{0,1:T(8,128)S(1)} %bitcast.72), kind=kOutput, calls=%fused_computation.24 | convolution fusion | flops 251822080 | bytes 1261568 | tf_op jit(solution)/shard_map/lp,cp,rp->lcr/dot_general | solution.py:102
  62.8 3.7 %fusion.13 = f32[8,48,256]{2,1,0:T(8,128)S(1)} fusion(s32[8,256]{1,0:T(8,128)S(1)} %eq.25, bf16[16,2048]{1,0:T(8,128)(2,1)S(1)} %get-tuple-element.83, bf16[16,2048]{1,0:T(8,128)(2,1)S(1)} %get-tuple-element.84, bf16[16,2048]{1,0:T(8,128)(2,1)S(1)} %get-tuple-element.82), kind=kOutput, calls=%fused_computation.23 | convolution fusion | flops 407437312 | bytes 598016 | tf_op jit(solution)/shard_map/cp,ktp->kct/dot_general | solution.py:50
  66.6 0.6 gather_fusion.5
  67.2 0.6 gather_fusion.4
  68.1 5.7 %fusion.56 = f32[4,16,512]{2,1,0:T(8,128)S(1)} fusion(f32[4,512,512]{2,1,0:T(8,128)} %exponential_multiply_fusion, f32[4,16,256]{2,1,0:T(8,128)S(1)} %gather_fusion.5, f32[4,16,256]{2,1,0:T(8,128)S(1)} %gather_fusion.4), kind=kOutput, calls=%fused_computation.97 | convolution fusion | flops 201359360 | bytes 4456448 | tf_op jit(solution)/shard_map/gij,gcj->gci/dot_general | solution.py:33
  74.7 1.2 %collective-permute-done.12 = f32[4,16,128]{2,1,0:T(8,128)S(1)} collective-permute-done((f32[4,16,128]{2,1,0:T(8,128)S(1)}, f32[4,16,128]{2,1,0:T(8,128)S(1)}, u32[]{:S(2)}, u32[]{:S(2)}) %collective-permute-start.12) | collective-permute-done | bytes 32800 | tf_op jit(solution)/shard_map/ppermute | solution.py:19
  76.4 3.4 %collective-permute-done.13 = f32[3,16,128]{2,1,0:T(8,128)S(1)} collective-permute-done((f32[3,16,128]{2,1,0:T(8,128)S(1)}, f32[3,16,128]{2,1,0:T(8,128)S(1)}, u32[]{:S(2)}, u32[]{:S(2)}) %collective-permute-start.13) | collective-permute-done | bytes 24608 | tf_op jit(solution)/shard_map/ppermute | solution.py:19
  79.8 1.6 %collective-permute-start.14 = (f32[2,16,128]{2,1,0:T(8,128)S(1)}, f32[2,16,128]{2,1,0:T(8,128)S(1)}, u32[]{:S(2)}, u32[]{:S(2)}) collective-permute-start(f32[2,16,128]{2,1,0:T(8,128)S(1)} %slice.207), channel_id=1, source_target_pairs={{0,16},{4,20},{8,24},{12,28},{16,0},{20,4},{24,8},{28,12},{1,17},{... | collective-permute-start | bytes 49160 | tf_op jit(solution)/shard_map/ppermute | solution.py:19
  81.4 2.2 %collective-permute-done.14 = f32[2,16,128]{2,1,0:T(8,128)S(1)} collective-permute-done((f32[2,16,128]{2,1,0:T(8,128)S(1)}, f32[2,16,128]{2,1,0:T(8,128)S(1)}, u32[]{:S(2)}, u32[]{:S(2)}) %collective-permute-start.14) | collective-permute-done | bytes 16416 | tf_op jit(solution)/shard_map/ppermute | solution.py:19
  84.4 0.6 convolution_multiply_fusion.2
  85.0 0.8 fusion.12
  86.0 1.6 %collective-permute-start.15 = (f32[16]{0:T(128)S(1)}, f32[16]{0:T(128)S(1)}, u32[]{:S(2)}, u32[]{:S(2)}) collective-permute-start(f32[16]{0:T(128)S(1)} %add.199), channel_id=1, source_target_pairs={{0,1},{1,0},{2,3},{3,2},{4,5},{5,4},{6,7},{7,6},{8,9},{9,8},{10,11... | collective-permute-start | bytes 200 | tf_op jit(solution)/shard_map/ppermute | solution.py:19
  87.6 2.0 %collective-permute-done.15 = f32[16]{0:T(128)S(1)} collective-permute-done((f32[16]{0:T(128)S(1)}, f32[16]{0:T(128)S(1)}, u32[]{:S(2)}, u32[]{:S(2)}) %collective-permute-start.15) | collective-permute-done | bytes 96 | tf_op jit(solution)/shard_map/ppermute | solution.py:19
  89.6 2.6 %collective-permute-start.16 = (f32[16]{0:T(128)S(1)}, f32[16]{0:T(128)S(1)}, u32[]{:S(2)}, u32[]{:S(2)}) collective-permute-start(f32[16]{0:T(128)S(1)} %add.200), channel_id=1, source_target_pairs={{0,2},{1,3},{2,0},{3,1},{4,6},{5,7},{6,4},{7,5},{8,10},{9,11},{10,... | collective-permute-start | bytes 200 | tf_op jit(solution)/shard_map/ppermute | solution.py:19
  92.2 1.8 %collective-permute-done.16 = f32[16]{0:T(128)S(1)} collective-permute-done((f32[16]{0:T(128)S(1)}, f32[16]{0:T(128)S(1)}, u32[]{:S(2)}, u32[]{:S(2)}) %collective-permute-start.16) | collective-permute-done | bytes 96 | tf_op jit(solution)/shard_map/ppermute | solution.py:19
  94.1 1.1 %collective-permute-done.17 = f32[16]{0:T(128)S(1)} collective-permute-done((f32[16]{0:T(128)S(1)}, f32[16]{0:T(128)S(1)}, u32[]{:S(2)}, u32[]{:S(2)}) %collective-permute-start.17) | collective-permute-done | bytes 96 | tf_op jit(solution)/shard_map/ppermute | solution.py:19
  95.6 3.1 %collective-permute-done.18 = f32[16]{0:T(128)S(1)} collective-permute-done((f32[16]{0:T(128)S(1)}, f32[16]{0:T(128)S(1)}, u32[]{:S(2)}, u32[]{:S(2)}) %collective-permute-start.18) | collective-permute-done | bytes 96 | tf_op jit(solution)/shard_map/ppermute | solution.py:19
  98.7 1.5 %collective-permute-start.19 = (f32[16]{0:T(128)S(1)}, f32[16]{0:T(128)S(1)}, u32[]{:S(2)}, u32[]{:S(2)}) collective-permute-start(f32[16]{0:T(128)S(1)} %add.203), channel_id=1, source_target_pairs={{0,16},{4,20},{8,24},{12,28},{16,0},{20,4},{24,8},{28,12},{1,17},{... | collective-permute-start | bytes 200 | tf_op jit(solution)/shard_map/ppermute | solution.py:19
  100.2 3.5 %fusion.9 = f32[48,2048]{1,0:T(8,128)S(1)} fusion(s32[8,256]{1,0:T(8,128)S(1)} %eq.25, bf16[8,16,256]{2,1,0:T(8,128)(2,1)S(1)} %get-tuple-element.78, bf16[8,16,256]{2,1,0:T(8,128)(2,1)S(1)} %get-tuple-element.79, bf16[8,16,256]{2,1,0:T(8,128)(2,1)S(1)} %get-tuple-element.77), kind=kOutput, calls=%fused_computation.19 | convolution fusion | flops 407437312 | bytes 598016 | tf_op jit(solution)/shard_map/kct,ktp->cp/dot_general | solution.py:56
  103.7 0.8 fusion.51
  (104 shorter events, 7.9 us)
Async XLA Ops:
  0.6 1.3 %copy-start = (f32[128,2048]{1,0:T(8,128)S(1)}, f32[128,2048]{1,0:T(8,128)}, u32[]{:S(2)}) copy-start(f32[128,2048]{1,0:T(8,128)} %param.13) | copy-start | bytes 3145732
  4.1 11.9 %collective-permute-start = (f32[6,16,128]{2,1,0:T(8,128)S(1)}, f32[6,16,128]{2,1,0:T(8,128)S(1)}, u32[]{:S(2)}, u32[]{:S(2)}) collective-permute-start(f32[6,16,128]{2,1,0:T(8,128)S(1)} %pad_maximum_fusion.1), channel_id=1, source_target_pairs={{0,1},{1,0},{2,3},{3,2},{4,5},{5,4},{6,7},{7,6},{8,9},{9,8},{10,11... | collective-permute-start | bytes 147464 | tf_op jit(solution)/shard_map/ppermute | solution.py:19
  17.2 8.4 %collective-permute-start.1 = (f32[5,16,128]{2,1,0:T(8,128)S(1)}, f32[5,16,128]{2,1,0:T(8,128)S(1)}, u32[]{:S(2)}, u32[]{:S(2)}) collective-permute-start(f32[5,16,128]{2,1,0:T(8,128)S(1)} %slice.141), channel_id=1, source_target_pairs={{0,2},{1,3},{2,0},{3,1},{4,6},{5,7},{6,4},{7,5},{8,10},{9,11},{10,... | collective-permute-start | bytes 122888 | tf_op jit(solution)/shard_map/ppermute | solution.py:19
  25.7 15.5 %copy-start.2 = (f32[5,128,128]{2,1,0:T(8,128)S(1)}, f32[5,128,128]{2,1,0:T(8,128)}, u32[]{:S(2)}) copy-start(f32[5,128,128]{2,1,0:T(8,128)} %param.15) | copy-start | bytes 983044
  25.7 16.5 %copy-start.3 = (f32[5,2048]{1,0:T(8,128)S(1)}, f32[5,2048]{1,0:T(8,128)}, u32[]{:S(2)}) copy-start(f32[5,2048]{1,0:T(8,128)} %param.14) | copy-start | bytes 122884
  26.8 16.1 %copy-start.1 = (f32[16,2048]{1,0:T(8,128)S(1)}, f32[16,2048]{1,0:T(8,128)}, u32[]{:S(2)}) copy-start(f32[16,2048]{1,0:T(8,128)} %param.12) | copy-start | bytes 393220
  26.9 16.1 %copy-start.4 = (f32[2048]{0:T(1024)S(1)}, f32[2048]{0:T(1024)}, u32[]{:S(2)}) copy-start(f32[2048]{0:T(1024)} %param.11) | copy-start | bytes 24580
  26.9 6.5 %collective-permute-start.2 = (f32[4,16,128]{2,1,0:T(8,128)S(1)}, f32[4,16,128]{2,1,0:T(8,128)S(1)}, u32[]{:S(2)}, u32[]{:S(2)}) collective-permute-start(f32[4,16,128]{2,1,0:T(8,128)S(1)} %slice.146), channel_id=1, source_target_pairs={{0,4},{4,0},{8,12},{12,8},{16,20},{20,16},{24,28},{28,24},{1,5},{5... | collective-permute-start | bytes 98312 | tf_op jit(solution)/shard_map/ppermute | solution.py:19
  33.4 3.9 %collective-permute-start.3 = (f32[3,16,128]{2,1,0:T(8,128)S(1)}, f32[3,16,128]{2,1,0:T(8,128)S(1)}, u32[]{:S(2)}, u32[]{:S(2)}) collective-permute-start(f32[3,16,128]{2,1,0:T(8,128)S(1)} %slice.149), channel_id=1, source_target_pairs={{0,8},{4,12},{8,0},{12,4},{16,24},{20,28},{24,16},{28,20},{1,9},{5... | collective-permute-start | bytes 73736 | tf_op jit(solution)/shard_map/ppermute | solution.py:19
  37.3 3.8 %collective-permute-start.4 = (f32[2,16,128]{2,1,0:T(8,128)S(1)}, f32[2,16,128]{2,1,0:T(8,128)S(1)}, u32[]{:S(2)}, u32[]{:S(2)}) collective-permute-start(f32[2,16,128]{2,1,0:T(8,128)S(1)} %slice.196), channel_id=1, source_target_pairs={{0,16},{4,20},{8,24},{12,28},{16,0},{20,4},{24,8},{28,12},{1,17},{... | collective-permute-start | bytes 49160 | tf_op jit(solution)/shard_map/ppermute | solution.py:19
  43.1 3.6 %collective-permute-start.5 = (f32[16]{0:T(128)S(1)}, f32[16]{0:T(128)S(1)}, u32[]{:S(2)}, u32[]{:S(2)}) collective-permute-start(f32[16]{0:T(128)S(1)} %add.177), channel_id=1, source_target_pairs={{0,1},{1,0},{2,3},{3,2},{4,5},{5,4},{6,7},{7,6},{8,9},{9,8},{10,11... | collective-permute-start | bytes 200 | tf_op jit(solution)/shard_map/ppermute | solution.py:19
  46.7 4.4 %collective-permute-start.6 = (f32[16]{0:T(128)S(1)}, f32[16]{0:T(128)S(1)}, u32[]{:S(2)}, u32[]{:S(2)}) collective-permute-start(f32[16]{0:T(128)S(1)} %add.178), channel_id=1, source_target_pairs={{0,2},{1,3},{2,0},{3,1},{4,6},{5,7},{6,4},{7,5},{8,10},{9,11},{10,... | collective-permute-start | bytes 200 | tf_op jit(solution)/shard_map/ppermute | solution.py:19
  51.1 1.1 %collective-permute-start.7 = (f32[16]{0:T(128)S(1)}, f32[16]{0:T(128)S(1)}, u32[]{:S(2)}, u32[]{:S(2)}) collective-permute-start(f32[16]{0:T(128)S(1)} %add.179), channel_id=1, source_target_pairs={{0,4},{4,0},{8,12},{12,8},{16,20},{20,16},{24,28},{28,24},{1,5},{5... | collective-permute-start | bytes 200 | tf_op jit(solution)/shard_map/ppermute | solution.py:19
  52.3 5.0 %collective-permute-start.8 = (f32[16]{0:T(128)S(1)}, f32[16]{0:T(128)S(1)}, u32[]{:S(2)}, u32[]{:S(2)}) collective-permute-start(f32[16]{0:T(128)S(1)} %add.180), channel_id=1, source_target_pairs={{0,8},{4,12},{8,0},{12,4},{16,24},{20,28},{24,16},{28,20},{1,9},{5... | collective-permute-start | bytes 200 | tf_op jit(solution)/shard_map/ppermute | solution.py:19
  57.2 3.6 %collective-permute-start.9 = (f32[16]{0:T(128)S(1)}, f32[16]{0:T(128)S(1)}, u32[]{:S(2)}, u32[]{:S(2)}) collective-permute-start(f32[16]{0:T(128)S(1)} %add.181), channel_id=1, source_target_pairs={{0,16},{4,20},{8,24},{12,28},{16,0},{20,4},{24,8},{28,12},{1,17},{... | collective-permute-start | bytes 200 | tf_op jit(solution)/shard_map/ppermute | solution.py:19
  62.3 4.2 %collective-permute-start.10 = (f32[6,16,128]{2,1,0:T(8,128)S(1)}, f32[6,16,128]{2,1,0:T(8,128)S(1)}, u32[]{:S(2)}, u32[]{:S(2)}) collective-permute-start(f32[6,16,128]{2,1,0:T(8,128)S(1)} %pad_maximum_fusion.4), channel_id=1, source_target_pairs={{0,1},{1,0},{2,3},{3,2},{4,5},{5,4},{6,7},{7,6},{8,9},{9,8},{10,11... | collective-permute-start | bytes 147464 | tf_op jit(solution)/shard_map/ppermute | solution.py:19
  67.7 6.8 %collective-permute-start.11 = (f32[5,16,128]{2,1,0:T(8,128)S(1)}, f32[5,16,128]{2,1,0:T(8,128)S(1)}, u32[]{:S(2)}, u32[]{:S(2)}) collective-permute-start(f32[5,16,128]{2,1,0:T(8,128)S(1)} %slice.163), channel_id=1, source_target_pairs={{0,2},{1,3},{2,0},{3,1},{4,6},{5,7},{6,4},{7,5},{8,10},{9,11},{10,... | collective-permute-start | bytes 122888 | tf_op jit(solution)/shard_map/ppermute | solution.py:19
  74.6 1.3 %collective-permute-start.12 = (f32[4,16,128]{2,1,0:T(8,128)S(1)}, f32[4,16,128]{2,1,0:T(8,128)S(1)}, u32[]{:S(2)}, u32[]{:S(2)}) collective-permute-start(f32[4,16,128]{2,1,0:T(8,128)S(1)} %slice.166), channel_id=1, source_target_pairs={{0,4},{4,0},{8,12},{12,8},{16,20},{20,16},{24,28},{28,24},{1,5},{5... | collective-permute-start | bytes 98312 | tf_op jit(solution)/shard_map/ppermute | solution.py:19
  75.9 3.9 %collective-permute-start.13 = (f32[3,16,128]{2,1,0:T(8,128)S(1)}, f32[3,16,128]{2,1,0:T(8,128)S(1)}, u32[]{:S(2)}, u32[]{:S(2)}) collective-permute-start(f32[3,16,128]{2,1,0:T(8,128)S(1)} %slice.206), channel_id=1, source_target_pairs={{0,8},{4,12},{8,0},{12,4},{16,24},{20,28},{24,16},{28,20},{1,9},{5... | collective-permute-start | bytes 73736 | tf_op jit(solution)/shard_map/ppermute | solution.py:19
  79.8 3.8 %collective-permute-start.14 = (f32[2,16,128]{2,1,0:T(8,128)S(1)}, f32[2,16,128]{2,1,0:T(8,128)S(1)}, u32[]{:S(2)}, u32[]{:S(2)}) collective-permute-start(f32[2,16,128]{2,1,0:T(8,128)S(1)} %slice.207), channel_id=1, source_target_pairs={{0,16},{4,20},{8,24},{12,28},{16,0},{20,4},{24,8},{28,12},{1,17},{... | collective-permute-start | bytes 49160 | tf_op jit(solution)/shard_map/ppermute | solution.py:19
  86.0 3.6 %collective-permute-start.15 = (f32[16]{0:T(128)S(1)}, f32[16]{0:T(128)S(1)}, u32[]{:S(2)}, u32[]{:S(2)}) collective-permute-start(f32[16]{0:T(128)S(1)} %add.199), channel_id=1, source_target_pairs={{0,1},{1,0},{2,3},{3,2},{4,5},{5,4},{6,7},{7,6},{8,9},{9,8},{10,11... | collective-permute-start | bytes 200 | tf_op jit(solution)/shard_map/ppermute | solution.py:19
  89.6 4.4 %collective-permute-start.16 = (f32[16]{0:T(128)S(1)}, f32[16]{0:T(128)S(1)}, u32[]{:S(2)}, u32[]{:S(2)}) collective-permute-start(f32[16]{0:T(128)S(1)} %add.200), channel_id=1, source_target_pairs={{0,2},{1,3},{2,0},{3,1},{4,6},{5,7},{6,4},{7,5},{8,10},{9,11},{10,... | collective-permute-start | bytes 200 | tf_op jit(solution)/shard_map/ppermute | solution.py:19
  94.1 1.1 %collective-permute-start.17 = (f32[16]{0:T(128)S(1)}, f32[16]{0:T(128)S(1)}, u32[]{:S(2)}, u32[]{:S(2)}) collective-permute-start(f32[16]{0:T(128)S(1)} %add.201), channel_id=1, source_target_pairs={{0,4},{4,0},{8,12},{12,8},{16,20},{20,16},{24,28},{28,24},{1,5},{5... | collective-permute-start | bytes 200 | tf_op jit(solution)/shard_map/ppermute | solution.py:19
  95.2 3.5 %collective-permute-start.18 = (f32[16]{0:T(128)S(1)}, f32[16]{0:T(128)S(1)}, u32[]{:S(2)}, u32[]{:S(2)}) collective-permute-start(f32[16]{0:T(128)S(1)} %add.202), channel_id=1, source_target_pairs={{0,8},{4,12},{8,0},{12,4},{16,24},{20,28},{24,16},{28,20},{1,9},{5... | collective-permute-start | bytes 200 | tf_op jit(solution)/shard_map/ppermute | solution.py:19
  98.7 5.0 %collective-permute-start.19 = (f32[16]{0:T(128)S(1)}, f32[16]{0:T(128)S(1)}, u32[]{:S(2)}, u32[]{:S(2)}) collective-permute-start(f32[16]{0:T(128)S(1)} %add.203), channel_id=1, source_target_pairs={{0,16},{4,20},{8,24},{12,28},{16,0},{20,4},{24,8},{28,12},{1,17},{... | collective-permute-start | bytes 200 | tf_op jit(solution)/shard_map/ppermute | solution.py:19

commit v7 on v5

--- a/solution.py
+++ b/solution.py
@@ -19,8 +19,17 @@
     return lax.ppermute(value, axis, pairs)
 
 
+def pair_union(tiled, pair_rows, pair_cols):
+    unions = []
+    for pair in range(pair_rows.shape[0]):
+        row = lax.dynamic_index_in_dim(tiled, pair_rows[pair], axis=0, keepdims=False)
+        col = lax.dynamic_index_in_dim(tiled, pair_cols[pair], axis=0, keepdims=False)
+        unions.append(jnp.concatenate([row, col], axis=1))
+    return jnp.stack(unions, axis=0)
+
+
 def near_kernels(tile_coords, pair_rows, pair_cols):
-    union = jnp.concatenate([tile_coords[pair_rows], tile_coords[pair_cols]], axis=2)
+    union = pair_union(tile_coords, pair_rows, pair_cols)
     gram = jnp.einsum("gfi,gfj->gij", union, union, precision=highest)
     square = jnp.sum(union * union, axis=1)
     dist = square[:, :, None] + square[:, None, :] - 2.0 * gram
@@ -29,8 +38,8 @@
 
 def near_apply(kern, tile_vec, pair_rows, pair_cols):
     width = tile_vec.shape[2]
-    union_vec = jnp.concatenate([tile_vec[pair_rows], tile_vec[pair_cols]], axis=2)
-    result = jnp.einsum("gij,gcj->gci", kern, union_vec, precision=highest)
+    union_vec = pair_union(tile_vec, pair_rows, pair_cols)
+    result = jnp.einsum("gij,gcj->gci", kern, union_vec, precision=lax.Precision.HIGH)
     tile_ids = jnp.arange(tile_vec.shape[0], dtype=jnp.int32)
     row_hot = (pair_rows[:, None] == tile_ids[None, :]).astype(jnp.float32)
     col_hot = (pair_cols[:, None] == tile_ids[None, :]).astype(jnp.float32)
@@ -80,7 +89,6 @@
 
 
 def per_device(coords, inv_scale, noise, right_side, basis, level_gain, coupling, order, pairs):
-    perm = order.reshape(order.shape[1])
     columns, points = right_side.shape
     features = coords.shape[0]
     tiles = points // TILE_POINTS
@@ -89,7 +97,7 @@
     pair_rows = pairs[0, 0]
     pair_cols = pairs[0, 1]
     position = jnp.arange(points, dtype=jnp.int32)
-    hot = (perm[:, None] == position[None, :]).astype(jnp.bfloat16)
+    hot = (jnp.transpose(order) == position[None, :]).astype(jnp.bfloat16)
     hot = hot.reshape(tiles, TILE_POINTS, points)
     stacked = to_tiles(jnp.concatenate([coords * inv_scale[:, None], right_side], axis=0), hot)
     tile_coords = stacked[:, :features]

time: 104 us -> 113 us (1.087)
  between operations: 1.13 us -> 16 us
  matrix products: 35.8 us -> 30.2 us
  local copies, waits for them, and re-layouts: 4.38 us -> 2.79 us
    dot_general x2, matrix products: 9.46 us -> 3.48 us  [near_apply(): jnp.einsum('gij,gcj->gci', kern, union_vec, precision=lax.Precision.HIGH)]
    gather x6 -> x0, local copies, waits for them, and re-layouts: 3.31 us -> none  [the longest x2 1.11 us: near_apply(): tile_vec[pair_rows]]
    slice x0 -> x1, local copies, waits for them, and re-layouts: none -> 1.64 us  [pair_union(): pair_rows[pair]]
  transfers between devices with their start and end apart: 20 -> 20, of which waited for: 15 -> 17; matrix products, arithmetic and copies ran while one was open for 35% -> 26% of each run, Pallas kernels for 0% -> 0%
where the time goes in v7:
time: 113 us; the launch traced here: 112 us
  waiting for transfers between devices  30.9 us (27%)
  matrix products  30.2 us (27%)
  starting transfers between devices  25.9 us (23%)
  between operations  16 us (14%)
  other arithmetic  6.67 us (6%)
  local copies, waits for them, and re-layouts  2.79 us (2%)
    ppermute x20, waiting for transfers between devices, swapped(): return lax.ppermute(value, axis, pairs)  30.9 us
    ppermute x20, starting transfers between devices, swapped(): return lax.ppermute(value, axis, pairs)  25.9 us
    dot_general x2, matrix products, to_tiles(): jnp.einsum('cp,ktp->kct', pieces(values, 0), hot, preferred_element_type=...  6.97 us
    dot_general x2, matrix products, to_points(): jnp.einsum('kct,ktp->cp', pieces(values_t, 1), hot, preferred_element_typ...  6.92 us
    dot_general x1, matrix products, near_kernels(): gram = jnp.einsum('gfi,gfj->gij', union, union, precision=highest)  4.26 us
    dot_general x2, matrix products, near_apply(): jnp.einsum('gij,gcj->gci', kern, union_vec, precision=lax.Precision.HIGH)  3.48 us
    dot_general x2, matrix products, sums_with_norm(): jnp.einsum('lp,cp,rp->lcr', level_gain, values, basis, precision=highest)  3.32 us
  transfers between devices with their start and end apart: 20, of which 17 were waited for; matrix products, arithmetic and copies ran while one was open for 26% of the time, Pallas kernels for 0%

profile of v7, /device:TPU:0, one launch (start us, length us, event | category | flops | bytes accessed | tf_op | source)
XLA Modules:
  0.0 112.4 jit_solution(6589119356031927775)
XLA Ops:
  0.6 1.1 multiply_reduce_fusion.5
  1.9 2.1 %convolution_bitcast_fusion.1 = f32[5,16,128]{2,1,0:T(8,128)S(1)} fusion(f32[128,2048]{1,0:T(8,128)S(1)} %copy-done, f32[2048,5]{0,1:T(8,128)} %bitcast.141, f32[2048,16]{0,1:T(8,128)} %bitcast.139), kind=kOutput, calls=%fused_computation.19 | convolution fusion | flops 251822080 | bytes 1261568 | tf_op jit(solution)/shard_map/lp,cp,rp->lcr/dot_general | solution.py:111
  4.1 3.0 %collective-permute-start = (f32[6,16,128]{2,1,0:T(8,128)S(1)}, f32[6,16,128]{2,1,0:T(8,128)S(1)}, u32[]{:S(2)}, u32[]{:S(2)}) collective-permute-start(f32[6,16,128]{2,1,0:T(8,128)S(1)} %pad_maximum_fusion.2), channel_id=1, source_target_pairs={{0,1},{1,0},{2,3},{3,2},{4,5},{5,4},{6,7},{7,6},{8,9},{9,8},{10,11... | collective-permute-start | bytes 147464 | tf_op jit(solution)/shard_map/ppermute | solution.py:19
  7.2 1.6 %fusion.101 = (s32[1,1,1]{2,1,0:T(1,128)}, s32[1,1,1]{2,1,0:T(1,128)}, s32[1,1,1]{2,1,0:T(1,128)}, s32[1,1,1]{2,1,0:T(1,128)}, s32[1,1,1]{2,1,0:T(1,128)}, /*ind...) fusion(s32[1,2,4]{2,1,0:T(2,128)} %param.17), kind=kLoop, calls=%fused_computation.218 | loop fusion | bytes 64 | tf_op jit(solution)/shard_map/slice | solution.py:25
  18.8 0.5 broadcast.85
  19.3 1.4 %reduce.9 = s32[2048]{0:T(1024)S(1)} reduce(s32[1,2048]{1,0:T(1,128)} %param.16, s32[]{:T(128)} %broadcast.85), dimensions={0}, to_apply=%param.16.reduce_sub_computation.3 | reduce | bytes 16388 | tf_op args[7]
  20.7 0.9 broadcast_multiply_fusion
  21.6 0.9 reduce-precision_convert_fusion.1
  22.5 3.5 %fusion.10 = f32[8,72,256]{2,1,0:T(8,128)S(1)} fusion(s32[8,256]{1,0:T(8,128)S(1)} %eq.29, bf16[24,2048]{1,0:T(8,128)(2,1)S(1)} %get-tuple-element.22, bf16[24,2048]{1,0:T(8,128)(2,1)S(1)} %get-tuple-element.21, bf16[24,2048]{1,0:T(8,128)(2,1)S(1)} %get-tuple-element.20), kind=kOutput, calls=%fused_computation.14 | convolution fusion | flops 609058816 | bytes 892928 | tf_op jit(solution)/shard_map/cp,ktp->kct/dot_general | solution.py:59
  31.2 4.3 %exponential_multiply_fusion = f32[4,512,512]{2,1,0:T(8,128)S(1)} fusion(f32[4,512]{1,0:T(4,128)S(1)} %multiply_reduce_fusion.6, f32[1,8,512]{2,1,0:T(8,128)S(1)} %get-tuple-element.77, f32[1,8,512]{2,1,0:T(8,128)S(1)} %get-tuple-element.76, f32[1,8,512]{2,1,0:T(8,128)S(1)} %get-tuple-element.75, f32[1,8,512]{2,1,0:T(8,128)S(1)} %get-tuple-element.74), kind=kOutput, calls=%fused_computation.9 | convolution fusion | flops 105955328 | bytes 4268032 | tf_op jit(solution)/shard_map/gfi,gfj->gij/dot_general | solution.py:33
  35.6 1.7 %fusion.52 = f32[4,16,512]{2,1,0:T(8,128)S(1)} fusion(f32[4,512,512]{2,1,0:T(8,128)S(1)} %exponential_multiply_fusion, f32[1,16,512]{2,1,0:T(8,128)S(1)} %get-tuple-element.81, f32[1,16,512]{2,1,0:T(8,128)S(1)} %get-tuple-element.80, f32[1,16,512]{2,1,0:T(8,128)S(1)} %get-tuple-element.79, f32[1,16,512]{2,1,0:T(8,128)S(1)} %get-tuple-element.78), kind=kOutput, calls=%fused_computation.87 | convolution fusion | flops 100761600 | bytes 4456448 | tf_op jit(solution)/shard_map/gij,gcj->gci/dot_general | solution.py:42
  37.4 2.7 %collective-permute-start.1 = (f32[5,16,128]{2,1,0:T(8,128)S(1)}, f32[5,16,128]{2,1,0:T(8,128)S(1)}, u32[]{:S(2)}, u32[]{:S(2)}) collective-permute-start(f32[5,16,128]{2,1,0:T(8,128)S(1)} %slice.232), channel_id=1, source_target_pairs={{0,2},{1,3},{2,0},{3,1},{4,6},{5,7},{6,4},{7,5},{8,10},{9,11},{10,... | collective-permute-start | bytes 122888 | tf_op jit(solution)/shard_map/ppermute | solution.py:19
  40.4 2.0 %collective-permute-done.1 = f32[5,16,128]{2,1,0:T(8,128)S(1)} collective-permute-done((f32[5,16,128]{2,1,0:T(8,128)S(1)}, f32[5,16,128]{2,1,0:T(8,128)S(1)}, u32[]{:S(2)}, u32[]{:S(2)}) %collective-permute-start.1) | collective-permute-done | bytes 40992 | tf_op jit(solution)/shard_map/ppermute | solution.py:19
  42.8 0.9 collective-permute-done.2
  43.6 1.9 %collective-permute-start.3 = (f32[3,16,128]{2,1,0:T(8,128)S(1)}, f32[3,16,128]{2,1,0:T(8,128)S(1)}, u32[]{:S(2)}, u32[]{:S(2)}) collective-permute-start(f32[3,16,128]{2,1,0:T(8,128)S(1)} %slice.234), channel_id=1, source_target_pairs={{0,8},{4,12},{8,0},{12,4},{16,24},{20,28},{24,16},{28,20},{1,9},{5... | collective-permute-start | bytes 73736 | tf_op jit(solution)/shard_map/ppermute | solution.py:19
  45.7 1.8 %collective-permute-done.3 = f32[3,16,128]{2,1,0:T(8,128)S(1)} collective-permute-done((f32[3,16,128]{2,1,0:T(8,128)S(1)}, f32[3,16,128]{2,1,0:T(8,128)S(1)}, u32[]{:S(2)}, u32[]{:S(2)}) %collective-permute-start.3) | collective-permute-done | bytes 24608 | tf_op jit(solution)/shard_map/ppermute | solution.py:19
  47.6 1.9 %collective-permute-start.4 = (f32[2,16,128]{2,1,0:T(8,128)S(1)}, f32[2,16,128]{2,1,0:T(8,128)S(1)}, u32[]{:S(2)}, u32[]{:S(2)}) collective-permute-start(f32[2,16,128]{2,1,0:T(8,128)S(1)} %slice.235), channel_id=1, source_target_pairs={{0,16},{4,20},{8,24},{12,28},{16,0},{20,4},{24,8},{28,12},{1,17},{... | collective-permute-start | bytes 49160 | tf_op jit(solution)/shard_map/ppermute | solution.py:19
  49.5 1.9 %collective-permute-done.4 = f32[2,16,128]{2,1,0:T(8,128)S(1)} collective-permute-done((f32[2,16,128]{2,1,0:T(8,128)S(1)}, f32[2,16,128]{2,1,0:T(8,128)S(1)}, u32[]{:S(2)}, u32[]{:S(2)}) %collective-permute-start.4) | collective-permute-done | bytes 16416 | tf_op jit(solution)/shard_map/ppermute | solution.py:19
  51.7 0.6 convolution_multiply_fusion.3
  52.4 1.0 fusion.11
  53.7 3.4 %collective-permute-done.5 = f32[16]{0:T(128)S(1)} collective-permute-done((f32[16]{0:T(128)S(1)}, f32[16]{0:T(128)S(1)}, u32[]{:S(2)}, u32[]{:S(2)}) %collective-permute-start.5) | collective-permute-done | bytes 96 | tf_op jit(solution)/shard_map/ppermute | solution.py:19
  57.1 2.6 %collective-permute-start.6 = (f32[16]{0:T(128)S(1)}, f32[16]{0:T(128)S(1)}, u32[]{:S(2)}, u32[]{:S(2)}) collective-permute-start(f32[16]{0:T(128)S(1)} %add.202), channel_id=1, source_target_pairs={{0,2},{1,3},{2,0},{3,1},{4,6},{5,7},{6,4},{7,5},{8,10},{9,11},{10,... | collective-permute-start | bytes 200 | tf_op jit(solution)/shard_map/ppermute | solution.py:19
  59.7 1.8 %collective-permute-done.6 = f32[16]{0:T(128)S(1)} collective-permute-done((f32[16]{0:T(128)S(1)}, f32[16]{0:T(128)S(1)}, u32[]{:S(2)}, u32[]{:S(2)}) %collective-permute-start.6) | collective-permute-done | bytes 96 | tf_op jit(solution)/shard_map/ppermute | solution.py:19
  61.6 1.1 collective-permute-done.7
  62.7 1.8 %collective-permute-start.8 = (f32[16]{0:T(128)S(1)}, f32[16]{0:T(128)S(1)}, u32[]{:S(2)}, u32[]{:S(2)}) collective-permute-start(f32[16]{0:T(128)S(1)} %add.204), channel_id=1, source_target_pairs={{0,8},{4,12},{8,0},{12,4},{16,24},{20,28},{24,16},{28,20},{1,9},{5... | collective-permute-start | bytes 200 | tf_op jit(solution)/shard_map/ppermute | solution.py:19
  64.5 3.5 %fusion.8 = f32[48,2048]{1,0:T(8,128)S(1)} fusion(s32[8,256]{1,0:T(8,128)S(1)} %eq.29, bf16[8,16,256]{2,1,0:T(8,128)(2,1)S(1)} %get-tuple-element.40, bf16[8,16,256]{2,1,0:T(8,128)(2,1)S(1)} %get-tuple-element.41, bf16[8,16,256]{2,1,0:T(8,128)(2,1)S(1)} %get-tuple-element.39), kind=kOutput, calls=%fused_computation.12 | convolution fusion | flops 407437312 | bytes 598016 | tf_op jit(solution)/shard_map/kct,ktp->cp/dot_general | solution.py:65
  68.0 1.6 %collective-permute-start.9 = (f32[16]{0:T(128)S(1)}, f32[16]{0:T(128)S(1)}, u32[]{:S(2)}, u32[]{:S(2)}) collective-permute-start(f32[16]{0:T(128)S(1)} %add.205), channel_id=1, source_target_pairs={{0,16},{4,20},{8,24},{12,28},{16,0},{20,4},{24,8},{28,12},{1,17},{... | collective-permute-start | bytes 200 | tf_op jit(solution)/shard_map/ppermute | solution.py:19
  69.7 1.9 %collective-permute-done.9 = f32[16]{0:T(128)S(1)} collective-permute-done((f32[16]{0:T(128)S(1)}, f32[16]{0:T(128)S(1)}, u32[]{:S(2)}, u32[]{:S(2)}) %collective-permute-start.9) | collective-permute-done | bytes 96 | tf_op jit(solution)/shard_map/ppermute | solution.py:19
  71.8 1.2 %convolution_bitcast_fusion = f32[5,16,128]{2,1,0:T(8,128)S(1)} fusion(f32[128,2048]{1,0:T(8,128)S(1)} %copy-done, f32[2048,16]{0,1:T(8,128)S(1)} %bitcast.140, f32[2048,5]{0,1:T(8,128)S(1)} %bitcast.142), kind=kOutput, calls=%fused_computation.18 | convolution fusion | flops 251822080 | bytes 1261568 | tf_op jit(solution)/shard_map/lp,cp,rp->lcr/dot_general | solution.py:111
  73.3 3.5 %fusion.13 = f32[8,48,256]{2,1,0:T(8,128)S(1)} fusion(s32[8,256]{1,0:T(8,128)S(1)} %eq.29, bf16[16,2048]{1,0:T(8,128)(2,1)S(1)} %get-tuple-element.37, bf16[16,2048]{1,0:T(8,128)(2,1)S(1)} %get-tuple-element.36, bf16[16,2048]{1,0:T(8,128)(2,1)S(1)} %get-tuple-element.14), kind=kOutput, calls=%fused_computation.17 | convolution fusion | flops 407437312 | bytes 598016 | tf_op jit(solution)/shard_map/cp,ktp->kct/dot_general | solution.py:59
  77.2 2.4 %collective-permute-start.11 = (f32[5,16,128]{2,1,0:T(8,128)S(1)}, f32[5,16,128]{2,1,0:T(8,128)S(1)}, u32[]{:S(2)}, u32[]{:S(2)}) collective-permute-start(f32[5,16,128]{2,1,0:T(8,128)S(1)} %slice.248), channel_id=1, source_target_pairs={{0,2},{1,3},{2,0},{3,1},{4,6},{5,7},{6,4},{7,5},{8,10},{9,11},{10,... | collective-permute-start | bytes 122888 | tf_op jit(solution)/shard_map/ppermute | solution.py:19
  79.6 1.7 %fusion.60 = f32[4,16,512]{2,1,0:T(8,128)S(1)} fusion(f32[4,512,512]{2,1,0:T(8,128)S(1)} %exponential_multiply_fusion, f32[1,16,512]{2,1,0:T(8,128)S(1)} %maximum_bitcast_fusion.11, f32[1,16,512]{2,1,0:T(8,128)S(1)} %maximum_bitcast_fusion.10, f32[1,16,512]{2,1,0:T(8,128)S(1)} %maximum_bitcast_fusion.9, f32[1,16,512]{2,1,0:T(8,128)S(1)} %maximum_bitcast_fusion.8), kind=kOutput, calls=%fused_computation.95 | convolution fusion | flops 100761600 | bytes 4456448 | tf_op jit(solution)/shard_map/gij,gcj->gci/dot_general | solution.py:42
  81.3 0.9 collective-permute-done.11
  82.3 1.2 %collective-permute-done.12 = f32[4,16,128]{2,1,0:T(8,128)S(1)} collective-permute-done((f32[4,16,128]{2,1,0:T(8,128)S(1)}, f32[4,16,128]{2,1,0:T(8,128)S(1)}, u32[]{:S(2)}, u32[]{:S(2)}) %collective-permute-start.12) | collective-permute-done | bytes 32800 | tf_op jit(solution)/shard_map/ppermute | solution.py:19
  84.1 3.3 %collective-permute-done.13 = f32[3,16,128]{2,1,0:T(8,128)S(1)} collective-permute-done((f32[3,16,128]{2,1,0:T(8,128)S(1)}, f32[3,16,128]{2,1,0:T(8,128)S(1)}, u32[]{:S(2)}, u32[]{:S(2)}) %collective-permute-start.13) | collective-permute-done | bytes 24608 | tf_op jit(solution)/shard_map/ppermute | solution.py:19
  87.4 1.6 %collective-permute-start.14 = (f32[2,16,128]{2,1,0:T(8,128)S(1)}, f32[2,16,128]{2,1,0:T(8,128)S(1)}, u32[]{:S(2)}, u32[]{:S(2)}) collective-permute-start(f32[2,16,128]{2,1,0:T(8,128)S(1)} %slice.251), channel_id=1, source_target_pairs={{0,16},{4,20},{8,24},{12,28},{16,0},{20,4},{24,8},{28,12},{1,17},{... | collective-permute-start | bytes 49160 | tf_op jit(solution)/shard_map/ppermute | solution.py:19
  89.3 1.9 %collective-permute-done.14 = f32[2,16,128]{2,1,0:T(8,128)S(1)} collective-permute-done((f32[2,16,128]{2,1,0:T(8,128)S(1)}, f32[2,16,128]{2,1,0:T(8,128)S(1)}, u32[]{:S(2)}, u32[]{:S(2)}) %collective-permute-start.14) | collective-permute-done | bytes 16416 | tf_op jit(solution)/shard_map/ppermute | solution.py:19
  92.0 0.6 convolution_multiply_fusion.2
  92.6 1.0 fusion.12
  93.8 1.6 %collective-permute-start.15 = (f32[16]{0:T(128)S(1)}, f32[16]{0:T(128)S(1)}, u32[]{:S(2)}, u32[]{:S(2)}) collective-permute-start(f32[16]{0:T(128)S(1)} %add.223), channel_id=1, source_target_pairs={{0,1},{1,0},{2,3},{3,2},{4,5},{5,4},{6,7},{7,6},{8,9},{9,8},{10,11... | collective-permute-start | bytes 200 | tf_op jit(solution)/shard_map/ppermute | solution.py:19
  95.5 2.0 %collective-permute-done.15 = f32[16]{0:T(128)S(1)} collective-permute-done((f32[16]{0:T(128)S(1)}, f32[16]{0:T(128)S(1)}, u32[]{:S(2)}, u32[]{:S(2)}) %collective-permute-start.15) | collective-permute-done | bytes 96 | tf_op jit(solution)/shard_map/ppermute | solution.py:19
  97.5 2.3 %collective-permute-start.16 = (f32[16]{0:T(128)S(1)}, f32[16]{0:T(128)S(1)}, u32[]{:S(2)}, u32[]{:S(2)}) collective-permute-start(f32[16]{0:T(128)S(1)} %add.224), channel_id=1, source_target_pairs={{0,2},{1,3},{2,0},{3,1},{4,6},{5,7},{6,4},{7,5},{8,10},{9,11},{10,... | collective-permute-start | bytes 200 | tf_op jit(solution)/shard_map/ppermute | solution.py:19
  99.8 2.1 %collective-permute-done.16 = f32[16]{0:T(128)S(1)} collective-permute-done((f32[16]{0:T(128)S(1)}, f32[16]{0:T(128)S(1)}, u32[]{:S(2)}, u32[]{:S(2)}) %collective-permute-start.16) | collective-permute-done | bytes 96 | tf_op jit(solution)/shard_map/ppermute | solution.py:19
  101.9 1.1 collective-permute-done.17
  103.3 3.3 %collective-permute-done.18 = f32[16]{0:T(128)S(1)} collective-permute-done((f32[16]{0:T(128)S(1)}, f32[16]{0:T(128)S(1)}, u32[]{:S(2)}, u32[]{:S(2)}) %collective-permute-start.18) | collective-permute-done | bytes 96 | tf_op jit(solution)/shard_map/ppermute | solution.py:19
  106.6 1.5 %collective-permute-start.19 = (f32[16]{0:T(128)S(1)}, f32[16]{0:T(128)S(1)}, u32[]{:S(2)}, u32[]{:S(2)}) collective-permute-start(f32[16]{0:T(128)S(1)} %add.227), channel_id=1, source_target_pairs={{0,16},{4,20},{8,24},{12,28},{16,0},{20,4},{24,8},{28,12},{1,17},{... | collective-permute-start | bytes 200 | tf_op jit(solution)/shard_map/ppermute | solution.py:19
  108.1 3.5 %fusion.9 = f32[48,2048]{1,0:T(8,128)S(1)} fusion(s32[8,256]{1,0:T(8,128)S(1)} %eq.29, bf16[8,16,256]{2,1,0:T(8,128)(2,1)S(1)} %get-tuple-element.24, bf16[8,16,256]{2,1,0:T(8,128)(2,1)S(1)} %get-tuple-element.25, bf16[8,16,256]{2,1,0:T(8,128)(2,1)S(1)} %get-tuple-element.23), kind=kOutput, calls=%fused_computation.13 | convolution fusion | flops 407437312 | bytes 598016 | tf_op jit(solution)/shard_map/kct,ktp->cp/dot_general | solution.py:65
  111.6 0.8 fusion.51
  (100 shorter events, 5.5 us)
Async XLA Ops:
  0.6 1.3 %copy-start = (f32[128,2048]{1,0:T(8,128)S(1)}, f32[128,2048]{1,0:T(8,128)}, u32[]{:S(2)}) copy-start(f32[128,2048]{1,0:T(8,128)} %param.13) | copy-start | bytes 3145732
  4.1 33.2 %collective-permute-start = (f32[6,16,128]{2,1,0:T(8,128)S(1)}, f32[6,16,128]{2,1,0:T(8,128)S(1)}, u32[]{:S(2)}, u32[]{:S(2)}) collective-permute-start(f32[6,16,128]{2,1,0:T(8,128)S(1)} %pad_maximum_fusion.2), channel_id=1, source_target_pairs={{0,1},{1,0},{2,3},{3,2},{4,5},{5,4},{6,7},{7,6},{8,9},{9,8},{10,11... | collective-permute-start | bytes 147464 | tf_op jit(solution)/shard_map/ppermute | solution.py:19
  31.2 6.1 %copy-start.5 = (s32[1,2,4]{2,1,0:T(2,128)S(1)}, s32[1,2,4]{2,1,0:T(2,128)}, u32[]{:S(2)}) copy-start(s32[1,2,4]{2,1,0:T(2,128)} %param.17) | copy-start | bytes 100
  35.5 15.9 %copy-start.2 = (f32[5,128,128]{2,1,0:T(8,128)S(1)}, f32[5,128,128]{2,1,0:T(8,128)}, u32[]{:S(2)}) copy-start(f32[5,128,128]{2,1,0:T(8,128)} %param.15) | copy-start | bytes 983044
  35.5 16.9 %copy-start.3 = (f32[5,2048]{1,0:T(8,128)S(1)}, f32[5,2048]{1,0:T(8,128)}, u32[]{:S(2)}) copy-start(f32[5,2048]{1,0:T(8,128)} %param.14) | copy-start | bytes 122884
  35.5 17.8 %copy-start.1 = (f32[16,2048]{1,0:T(8,128)S(1)}, f32[16,2048]{1,0:T(8,128)}, u32[]{:S(2)}) copy-start(f32[16,2048]{1,0:T(8,128)} %param.12) | copy-start | bytes 393220
  35.5 17.8 %copy-start.4 = (f32[2048]{0:T(1024)S(1)}, f32[2048]{0:T(1024)}, u32[]{:S(2)}) copy-start(f32[2048]{0:T(1024)} %param.11) | copy-start | bytes 24580
  37.4 5.0 %collective-permute-start.1 = (f32[5,16,128]{2,1,0:T(8,128)S(1)}, f32[5,16,128]{2,1,0:T(8,128)S(1)}, u32[]{:S(2)}, u32[]{:S(2)}) collective-permute-start(f32[5,16,128]{2,1,0:T(8,128)S(1)} %slice.232), channel_id=1, source_target_pairs={{0,2},{1,3},{2,0},{3,1},{4,6},{5,7},{6,4},{7,5},{8,10},{9,11},{10,... | collective-permute-start | bytes 122888 | tf_op jit(solution)/shard_map/ppermute | solution.py:19
  42.4 1.3 %collective-permute-start.2 = (f32[4,16,128]{2,1,0:T(8,128)S(1)}, f32[4,16,128]{2,1,0:T(8,128)S(1)}, u32[]{:S(2)}, u32[]{:S(2)}) collective-permute-start(f32[4,16,128]{2,1,0:T(8,128)S(1)} %slice.233), channel_id=1, source_target_pairs={{0,4},{4,0},{8,12},{12,8},{16,20},{20,16},{24,28},{28,24},{1,5},{5... | collective-permute-start | bytes 98312 | tf_op jit(solution)/shard_map/ppermute | solution.py:19
  43.6 3.9 %collective-permute-start.3 = (f32[3,16,128]{2,1,0:T(8,128)S(1)}, f32[3,16,128]{2,1,0:T(8,128)S(1)}, u32[]{:S(2)}, u32[]{:S(2)}) collective-permute-start(f32[3,16,128]{2,1,0:T(8,128)S(1)} %slice.234), channel_id=1, source_target_pairs={{0,8},{4,12},{8,0},{12,4},{16,24},{20,28},{24,16},{28,20},{1,9},{5... | collective-permute-start | bytes 73736 | tf_op jit(solution)/shard_map/ppermute | solution.py:19
  47.6 3.8 %collective-permute-start.4 = (f32[2,16,128]{2,1,0:T(8,128)S(1)}, f32[2,16,128]{2,1,0:T(8,128)S(1)}, u32[]{:S(2)}, u32[]{:S(2)}) collective-permute-start(f32[2,16,128]{2,1,0:T(8,128)S(1)} %slice.235), channel_id=1, source_target_pairs={{0,16},{4,20},{8,24},{12,28},{16,0},{20,4},{24,8},{28,12},{1,17},{... | collective-permute-start | bytes 49160 | tf_op jit(solution)/shard_map/ppermute | solution.py:19
  53.5 3.6 %collective-permute-start.5 = (f32[16]{0:T(128)S(1)}, f32[16]{0:T(128)S(1)}, u32[]{:S(2)}, u32[]{:S(2)}) collective-permute-start(f32[16]{0:T(128)S(1)} %add.201), channel_id=1, source_target_pairs={{0,1},{1,0},{2,3},{3,2},{4,5},{5,4},{6,7},{7,6},{8,9},{9,8},{10,11... | collective-permute-start | bytes 200 | tf_op jit(solution)/shard_map/ppermute | solution.py:19
  57.1 4.4 %collective-permute-start.6 = (f32[16]{0:T(128)S(1)}, f32[16]{0:T(128)S(1)}, u32[]{:S(2)}, u32[]{:S(2)}) collective-permute-start(f32[16]{0:T(128)S(1)} %add.202), channel_id=1, source_target_pairs={{0,2},{1,3},{2,0},{3,1},{4,6},{5,7},{6,4},{7,5},{8,10},{9,11},{10,... | collective-permute-start | bytes 200 | tf_op jit(solution)/shard_map/ppermute | solution.py:19
  61.6 1.1 collective-permute-start.7
  62.7 5.3 %collective-permute-start.8 = (f32[16]{0:T(128)S(1)}, f32[16]{0:T(128)S(1)}, u32[]{:S(2)}, u32[]{:S(2)}) collective-permute-start(f32[16]{0:T(128)S(1)} %add.204), channel_id=1, source_target_pairs={{0,8},{4,12},{8,0},{12,4},{16,24},{20,28},{24,16},{28,20},{1,9},{5... | collective-permute-start | bytes 200 | tf_op jit(solution)/shard_map/ppermute | solution.py:19
  68.0 3.6 %collective-permute-start.9 = (f32[16]{0:T(128)S(1)}, f32[16]{0:T(128)S(1)}, u32[]{:S(2)}, u32[]{:S(2)}) collective-permute-start(f32[16]{0:T(128)S(1)} %add.205), channel_id=1, source_target_pairs={{0,16},{4,20},{8,24},{12,28},{16,0},{20,4},{24,8},{28,12},{1,17},{... | collective-permute-start | bytes 200 | tf_op jit(solution)/shard_map/ppermute | solution.py:19
  73.1 4.1 %collective-permute-start.10 = (f32[6,16,128]{2,1,0:T(8,128)S(1)}, f32[6,16,128]{2,1,0:T(8,128)S(1)}, u32[]{:S(2)}, u32[]{:S(2)}) collective-permute-start(f32[6,16,128]{2,1,0:T(8,128)S(1)} %pad_maximum_fusion.3), channel_id=1, source_target_pairs={{0,1},{1,0},{2,3},{3,2},{4,5},{5,4},{6,7},{7,6},{8,9},{9,8},{10,11... | collective-permute-start | bytes 147464 | tf_op jit(solution)/shard_map/ppermute | solution.py:19
  77.2 5.0 %collective-permute-start.11 = (f32[5,16,128]{2,1,0:T(8,128)S(1)}, f32[5,16,128]{2,1,0:T(8,128)S(1)}, u32[]{:S(2)}, u32[]{:S(2)}) collective-permute-start(f32[5,16,128]{2,1,0:T(8,128)S(1)} %slice.248), channel_id=1, source_target_pairs={{0,2},{1,3},{2,0},{3,1},{4,6},{5,7},{6,4},{7,5},{8,10},{9,11},{10,... | collective-permute-start | bytes 122888 | tf_op jit(solution)/shard_map/ppermute | solution.py:19
  82.2 1.3 %collective-permute-start.12 = (f32[4,16,128]{2,1,0:T(8,128)S(1)}, f32[4,16,128]{2,1,0:T(8,128)S(1)}, u32[]{:S(2)}, u32[]{:S(2)}) collective-permute-start(f32[4,16,128]{2,1,0:T(8,128)S(1)} %slice.249), channel_id=1, source_target_pairs={{0,4},{4,0},{8,12},{12,8},{16,20},{20,16},{24,28},{28,24},{1,5},{5... | collective-permute-start | bytes 98312 | tf_op jit(solution)/shard_map/ppermute | solution.py:19
  83.5 3.9 %collective-permute-start.13 = (f32[3,16,128]{2,1,0:T(8,128)S(1)}, f32[3,16,128]{2,1,0:T(8,128)S(1)}, u32[]{:S(2)}, u32[]{:S(2)}) collective-permute-start(f32[3,16,128]{2,1,0:T(8,128)S(1)} %slice.250), channel_id=1, source_target_pairs={{0,8},{4,12},{8,0},{12,4},{16,24},{20,28},{24,16},{28,20},{1,9},{5... | collective-permute-start | bytes 73736 | tf_op jit(solution)/shard_map/ppermute | solution.py:19
  87.4 3.8 %collective-permute-start.14 = (f32[2,16,128]{2,1,0:T(8,128)S(1)}, f32[2,16,128]{2,1,0:T(8,128)S(1)}, u32[]{:S(2)}, u32[]{:S(2)}) collective-permute-start(f32[2,16,128]{2,1,0:T(8,128)S(1)} %slice.251), channel_id=1, source_target_pairs={{0,16},{4,20},{8,24},{12,28},{16,0},{20,4},{24,8},{28,12},{1,17},{... | collective-permute-start | bytes 49160 | tf_op jit(solution)/shard_map/ppermute | solution.py:19
  93.8 3.6 %collective-permute-start.15 = (f32[16]{0:T(128)S(1)}, f32[16]{0:T(128)S(1)}, u32[]{:S(2)}, u32[]{:S(2)}) collective-permute-start(f32[16]{0:T(128)S(1)} %add.223), channel_id=1, source_target_pairs={{0,1},{1,0},{2,3},{3,2},{4,5},{5,4},{6,7},{7,6},{8,9},{9,8},{10,11... | collective-permute-start | bytes 200 | tf_op jit(solution)/shard_map/ppermute | solution.py:19
  97.5 4.4 %collective-permute-start.16 = (f32[16]{0:T(128)S(1)}, f32[16]{0:T(128)S(1)}, u32[]{:S(2)}, u32[]{:S(2)}) collective-permute-start(f32[16]{0:T(128)S(1)} %add.224), channel_id=1, source_target_pairs={{0,2},{1,3},{2,0},{3,1},{4,6},{5,7},{6,4},{7,5},{8,10},{9,11},{10,... | collective-permute-start | bytes 200 | tf_op jit(solution)/shard_map/ppermute | solution.py:19
  101.9 1.1 collective-permute-start.17
  103.0 3.5 %collective-permute-start.18 = (f32[16]{0:T(128)S(1)}, f32[16]{0:T(128)S(1)}, u32[]{:S(2)}, u32[]{:S(2)}) collective-permute-start(f32[16]{0:T(128)S(1)} %add.226), channel_id=1, source_target_pairs={{0,8},{4,12},{8,0},{12,4},{16,24},{20,28},{24,16},{28,20},{1,9},{5... | collective-permute-start | bytes 200 | tf_op jit(solution)/shard_map/ppermute | solution.py:19
  106.6 5.0 %collective-permute-start.19 = (f32[16]{0:T(128)S(1)}, f32[16]{0:T(128)S(1)}, u32[]{:S(2)}, u32[]{:S(2)}) collective-permute-start(f32[16]{0:T(128)S(1)} %add.227), channel_id=1, source_target_pairs={{0,16},{4,20},{8,24},{12,28},{16,0},{20,4},{24,8},{28,12},{1,17},{... | collective-permute-start | bytes 200 | tf_op jit(solution)/shard_map/ppermute | solution.py:19

commit v8 on v5

v8 whole, which is shorter than its diff:
```python
import math

import jax
import jax.numpy as jnp
from jax import lax
from jax.sharding import PartitionSpec as P

TILE_POINTS = 256
ITERATIONS = 2


near_weight = 0.25
highest = lax.Precision.HIGHEST


def swapped(value, axis, bit):
    mask = 2**bit
    pairs = [(source, source ^ mask) for source in range(lax.axis_size(axis))]
    return lax.ppermute(value, axis, pairs)


def near_kernels(union):
    gram = jnp.einsum("gfi,gfj->gij", union, union, precision=highest)
    square = jnp.sum(union * union, axis=1)
    dist = square[:, :, None] + square[:, None, :] - 2.0 * gram
    return near_weight * jnp.exp(-0.5 * dist)


def near_apply(kern, union_vec):
    return jnp.einsum("gij,gcj->gci", kern, union_vec, precision=lax.Precision.HIGH)


def pieces(values, axis):
    high = lax.reduce_precision(values, exponent_bits=8, mantissa_bits=7)
    rest = values - high
    middle = lax.reduce_precision(rest, exponent_bits=8, mantissa_bits=7)
    return jnp.concatenate([high, middle, rest - middle], axis=axis).astype(jnp.bfloat16)


def to_union(values, hot):
    count = values.shape[0]
    out = jnp.einsum("cp,gip->gci", pieces(values, 0), hot, preferred_element_type=jnp.float32)
    return (out[:, :count] + out[:, count : 2 * count]) + out[:, 2 * count :]


def from_union(values_u, hot):
    count = values_u.shape[1]
    out = jnp.einsum("gci,gip->cp", pieces(values_u, 1), hot, preferred_element_type=jnp.float32)
    return (out[:count] + out[count : 2 * count]) + out[2 * count :]


def tree_sums(proj):
    low_count = lax.axis_size("gy").bit_length() - 1
    high_count = lax.axis_size("gx").bit_length() - 1
    running = proj
    for bit in range(low_count):
        partner = swapped(running[bit:], "gy", bit)
        running = jnp.concatenate([running[:bit], running[bit:] + partner], axis=0)
    for bit in range(high_count):
        level = low_count + bit
        partner = swapped(running[level:], "gx", bit)
        running = jnp.concatenate([running[:level], running[level:] + partner], axis=0)
    return running


def butterfly(value):
    for bit in range(lax.axis_size("gy").bit_length() - 1):
        value = value + swapped(value, "gy", bit)
    for bit in range(lax.axis_size("gx").bit_length() - 1):
        value = value + swapped(value, "gx", bit)
    return value


def per_device(coords, inv_scale, noise, right_side, basis, level_gain, coupling, order, pairs):
    columns, points = right_side.shape
    features = coords.shape[0]
    tiles = points // TILE_POINTS
    levels = level_gain.shape[0]
    rank = basis.shape[0]
    order_tiles = order.reshape(tiles, TILE_POINTS)
    union_order = jnp.concatenate([order_tiles[pairs[0, 0]], order_tiles[pairs[0, 1]]], axis=1)
    position = jnp.arange(points, dtype=jnp.int32)
    hot = (union_order[:, :, None] == position[None, None, :]).astype(jnp.bfloat16)
    stacked = to_union(jnp.concatenate([coords * inv_scale[:, None], right_side], axis=0), hot)
    kern = lax.optimization_barrier(near_kernels(stacked[:, :features]))
    scales = 2.0 ** ((1.0 - jnp.arange(levels, dtype=jnp.float32)) / 2.0)

    def near_of_union(values_u):
        return near_apply(kern, values_u)

    def sums_with_norm(values):
        proj = jnp.einsum("lp,cp,rp->lcr", level_gain, values, basis, precision=highest)
        norm = jnp.sum(values * values, axis=1)
        extra = jnp.broadcast_to(norm[None, :, None], (1, columns, rank))
        running = tree_sums(jnp.concatenate([proj, extra], axis=0))
        return running[:levels], running[levels, :, 0]

    solution = jnp.zeros_like(right_side)
    residual = right_side
    direction = right_side
    direction_u = stacked[:, features:]
    for step in range(ITERATIONS):
        if step == 0:
            nodesum, norm_now = sums_with_norm(residual)
            near_u = near_of_union(direction_u)
            late_u, nodesum = lax.optimization_barrier((near_u, nodesum))
            near = from_union(late_u, hot)
        else:
            residual_sum, norm_next = sums_with_norm(residual)
            residual_u = to_union(residual, hot)
            residual_near_u = near_of_union(residual_u)
            late_u, residual_sum = lax.optimization_barrier((residual_near_u, residual_sum))
            ratio = norm_next / norm_now
            direction = residual + ratio[:, None] * direction
            direction_u = residual_u + ratio[None, :, None] * direction_u
            nodesum = residual_sum + ratio[None, :, None] * nodesum
            near_u = residual_near_u + ratio[None, :, None] * near_u
            near = from_union(late_u, hot) + ratio[:, None] * near
            norm_now = norm_next
        coupled = jnp.einsum("lcr,lrs->lcs", nodesum, coupling, precision=highest)
        coupled = (
            jnp.einsum("lcs,lrs->lcr", coupled, coupling, precision=highest) * scales[:, None, None]
        )
        back = jnp.einsum("lcr,rp->lcp", coupled, basis, precision=highest)
        far = jnp.sum(back * level_gain[:, None, :], axis=0)
        base = noise[None, :] * direction + far
        local = jnp.sum(direction * base, axis=1) + jnp.sum(direction_u * near_u, axis=(0, 2))
        curve = butterfly(local)
        alpha = norm_now / curve
        solution = solution + alpha[:, None] * direction
        residual = residual - alpha[:, None] * (base + near)
    return (solution, residual)


def solution(mesh):
    return jax.shard_map(
        per_device,
        mesh=mesh,
        in_specs=(
            P(None, ("gx", "gy")),
            P(),
            P(("gx", "gy")),
            P(None, ("gx", "gy")),
            P(None, ("gx", "gy")),
            P(None, ("gx", "gy")),
            P(),
            P(("gx", "gy"), None),
            P(("gx", "gy"), None, None),
        ),
        out_specs=(P(None, ("gx", "gy")), P(None, ("gx", "gy"))),
        check_vma=False,
    )
```

time: 104 us -> 96.6 us (0.929)
  matrix products: 35.8 us -> 29 us
  waiting for transfers between devices: 31.1 us -> 33.4 us
  local copies, waits for them, and re-layouts: 4.38 us -> 2.13 us
    dot_general x10 -> x6, matrix products: 24.6 us -> 17.8 us  [the longest x2 7.14 us: from_union(): jnp.einsum('gci,gip->cp', pieces(values_u, 1), hot, preferred_element_typ...]
    ppermute x20, waiting for transfers between devices: 31.1 us -> 33.4 us  [swapped(): return lax.ppermute(value, axis, pairs)]
    gather x6 -> x2, local copies, waits for them, and re-layouts: 3.31 us -> 1.12 us  [the longest x1 0.56 us: per_device(): order_tiles[pairs[0, 1]]]
  transfers between devices with their start and end apart: 20 -> 20, of which waited for: 15 -> 15; matrix products, arithmetic and copies ran while one was open for 35% -> 27% of each run, Pallas kernels for 0% -> 0%
where the time goes in v8:
time: 96.6 us; the launch traced here: 96.3 us
  waiting for transfers between devices  33.4 us (35%)
  matrix products  29 us (30%)
  starting transfers between devices  24 us (25%)
  other arithmetic  6.94 us (7%)
  local copies, waits for them, and re-layouts  2.13 us (2%)
    ppermute x20, waiting for transfers between devices, swapped(): return lax.ppermute(value, axis, pairs)  33.4 us
    ppermute x20, starting transfers between devices, swapped(): return lax.ppermute(value, axis, pairs)  24 us
    dot_general x2, matrix products, from_union(): jnp.einsum('gci,gip->cp', pieces(values_u, 1), hot, preferred_element_typ...  7.14 us
    dot_general x2, matrix products, to_union(): jnp.einsum('cp,gip->gci', pieces(values, 0), hot, preferred_element_type=...  6.98 us
    dot_general x1, matrix products, near_kernels(): gram = jnp.einsum('gfi,gfj->gij', union, union, precision=highest)  4.26 us
    dot_general x2, matrix products, near_apply(): jnp.einsum('gij,gcj->gci', kern, union_vec, precision=lax.Precision.HIGH)  3.71 us
    dot_general x2, matrix products, sums_with_norm(): jnp.einsum('lp,cp,rp->lcr', level_gain, values, basis, precision=highest)  3.32 us
  transfers between devices with their start and end apart: 20, of which 15 were waited for; matrix products, arithmetic and copies ran while one was open for 27% of the time, Pallas kernels for 0%

profile of v8, /device:TPU:0, one launch (start us, length us, event | category | flops | bytes accessed | tf_op | source)
XLA Modules:
  0.0 96.3 jit_solution(11670717418553119238)
XLA Ops:
  0.6 1.1 %multiply_reduce_fusion.5 = f32[16]{0:T(128)S(1)} fusion(f32[16,2048]{1,0:T(8,128)} %param.12), kind=kLoop, calls=%fused_computation.99 | loop fusion | flops 65520 | bytes 131136 | tf_op jit(solution)/shard_map/reduce_sum | solution.py:93
  1.9 2.1 %convolution_bitcast_fusion.1 = f32[5,16,128]{2,1,0:T(8,128)S(1)} fusion(f32[128,2048]{1,0:T(8,128)S(1)} %copy-done, f32[2048,5]{0,1:T(8,128)} %bitcast.57, f32[2048,16]{0,1:T(8,128)} %bitcast.55), kind=kOutput, calls=%fused_computation.21 | convolution fusion | flops 251822080 | bytes 1261568 | tf_op jit(solution)/shard_map/lp,cp,rp->lcr/dot_general | solution.py:92
  4.1 3.0 %collective-permute-start = (f32[6,16,128]{2,1,0:T(8,128)S(1)}, f32[6,16,128]{2,1,0:T(8,128)S(1)}, u32[]{:S(2)}, u32[]{:S(2)}) collective-permute-start(f32[6,16,128]{2,1,0:T(8,128)S(1)} %pad_maximum_fusion.1), channel_id=1, source_target_pairs={{0,1},{1,0},{2,3},{3,2},{4,5},{5,4},{6,7},{7,6},{8,9},{9,8},{10,11... | collective-permute-start | bytes 147464 | tf_op jit(solution)/shard_map/ppermute | solution.py:19
  7.2 0.8 fusion.59
  7.9 0.5 broadcast.129
  8.4 1.4 %reduce.9 = s32[2048]{0:T(1024)S(1)} reduce(s32[1,2048]{1,0:T(1,128)} %param.16, s32[]{:T(128)} %broadcast.129), dimensions={0}, to_apply=%param.16.reduce_sub_computation.3 | reduce | bytes 16388 | tf_op args[7]
  9.8 0.6 gather_fusion.1
  10.4 0.6 gather_fusion
  11.0 0.9 broadcast_multiply_fusion
  11.9 0.9 reduce-precision_convert_fusion.1
  12.8 3.5 %fusion.10 = f32[4,72,512]{2,1,0:T(8,128)S(1)} fusion(s32[4,512]{1,0:T(4,128)S(1)} %pad_add_fusion, bf16[24,2048]{1,0:T(8,128)(2,1)S(1)} %get-tuple-element.18, bf16[24,2048]{1,0:T(8,128)(2,1)S(1)} %get-tuple-element.17, bf16[24,2048]{1,0:T(8,128)(2,1)S(1)} %get-tuple-element.16), kind=kOutput, calls=%fused_computation.16 | convolution fusion | flops 609058816 | bytes 892928 | tf_op jit(solution)/shard_map/cp,gip->gci/dot_general | solution.py:42
  16.4 2.7 %collective-permute-start.1 = (f32[5,16,128]{2,1,0:T(8,128)S(1)}, f32[5,16,128]{2,1,0:T(8,128)S(1)}, u32[]{:S(2)}, u32[]{:S(2)}) collective-permute-start(f32[5,16,128]{2,1,0:T(8,128)S(1)} %slice.156), channel_id=1, source_target_pairs={{0,2},{1,3},{2,0},{3,1},{4,6},{5,7},{6,4},{7,5},{8,10},{9,11},{10,... | collective-permute-start | bytes 122888 | tf_op jit(solution)/shard_map/ppermute | solution.py:19
  19.1 2.3 %collective-permute-done.1 = f32[5,16,128]{2,1,0:T(8,128)S(1)} collective-permute-done((f32[5,16,128]{2,1,0:T(8,128)S(1)}, f32[5,16,128]{2,1,0:T(8,128)S(1)}, u32[]{:S(2)}, u32[]{:S(2)}) %collective-permute-start.1) | collective-permute-done | bytes 40992 | tf_op jit(solution)/shard_map/ppermute | solution.py:19
  21.5 4.3 %exponential_multiply_fusion = f32[4,512,512]{2,1,0:T(8,128)S(1)} fusion(f32[4,512]{1,0:T(4,128)S(1)} %multiply_reduce_fusion.6, f32[4,24,512]{2,1,0:T(8,128)S(1)} %slice_add_fusion), kind=kOutput, calls=%fused_computation.11 | convolution fusion | flops 105906176 | bytes 4276224 | tf_op jit(solution)/shard_map/gfi,gfj->gij/dot_general | solution.py:23
  25.8 1.9 %collective-permute-start.3 = (f32[3,16,128]{2,1,0:T(8,128)S(1)}, f32[3,16,128]{2,1,0:T(8,128)S(1)}, u32[]{:S(2)}, u32[]{:S(2)}) collective-permute-start(f32[3,16,128]{2,1,0:T(8,128)S(1)} %slice.158), channel_id=1, source_target_pairs={{0,8},{4,12},{8,0},{12,4},{16,24},{20,28},{24,16},{28,20},{1,9},{5... | collective-permute-start | bytes 73736 | tf_op jit(solution)/shard_map/ppermute | solution.py:19
  27.7 1.8 %multiply_reduce_fusion.3 = (f32[16]{0:T(128)S(1)}, f32[4,16,512]{2,1,0:T(8,128)S(1)}) fusion(f32[4,24,512]{2,1,0:T(8,128)S(1)} %slice_add_fusion, f32[4,512,512]{2,1,0:T(8,128)S(1)} %exponential_multiply_fusion), kind=kOutput, calls=%fused_computation.96 | convolution fusion | flops 100728816 | bytes 4587584 | tf_op jit(solution)/shard_map/gij,gcj->gci/dot_general | solution.py:30
  29.7 1.9 %collective-permute-start.4 = (f32[2,16,128]{2,1,0:T(8,128)S(1)}, f32[2,16,128]{2,1,0:T(8,128)S(1)}, u32[]{:S(2)}, u32[]{:S(2)}) collective-permute-start(f32[2,16,128]{2,1,0:T(8,128)S(1)} %slice.159), channel_id=1, source_target_pairs={{0,16},{4,20},{8,24},{12,28},{16,0},{20,4},{24,8},{28,12},{1,17},{... | collective-permute-start | bytes 49160 | tf_op jit(solution)/shard_map/ppermute | solution.py:19
  31.7 1.9 %collective-permute-done.4 = f32[2,16,128]{2,1,0:T(8,128)S(1)} collective-permute-done((f32[2,16,128]{2,1,0:T(8,128)S(1)}, f32[2,16,128]{2,1,0:T(8,128)S(1)}, u32[]{:S(2)}, u32[]{:S(2)}) %collective-permute-start.4) | collective-permute-done | bytes 16416 | tf_op jit(solution)/shard_map/ppermute | solution.py:19
  33.9 0.6 convolution_multiply_fusion.3
  34.6 0.8 fusion.11
  35.7 3.4 %collective-permute-done.5 = f32[16]{0:T(128)S(1)} collective-permute-done((f32[16]{0:T(128)S(1)}, f32[16]{0:T(128)S(1)}, u32[]{:S(2)}, u32[]{:S(2)}) %collective-permute-start.5) | collective-permute-done | bytes 96 | tf_op jit(solution)/shard_map/ppermute | solution.py:19
  39.1 2.6 %collective-permute-start.6 = (f32[16]{0:T(128)S(1)}, f32[16]{0:T(128)S(1)}, u32[]{:S(2)}, u32[]{:S(2)}) collective-permute-start(f32[16]{0:T(128)S(1)} %add.167), channel_id=1, source_target_pairs={{0,2},{1,3},{2,0},{3,1},{4,6},{5,7},{6,4},{7,5},{8,10},{9,11},{10,... | collective-permute-start | bytes 200 | tf_op jit(solution)/shard_map/ppermute | solution.py:19
  41.7 1.8 %collective-permute-done.6 = f32[16]{0:T(128)S(1)} collective-permute-done((f32[16]{0:T(128)S(1)}, f32[16]{0:T(128)S(1)}, u32[]{:S(2)}, u32[]{:S(2)}) %collective-permute-start.6) | collective-permute-done | bytes 96 | tf_op jit(solution)/shard_map/ppermute | solution.py:19
  43.6 1.1 %collective-permute-done.7 = f32[16]{0:T(128)S(1)} collective-permute-done((f32[16]{0:T(128)S(1)}, f32[16]{0:T(128)S(1)}, u32[]{:S(2)}, u32[]{:S(2)}) %collective-permute-start.7) | collective-permute-done | bytes 96 | tf_op jit(solution)/shard_map/ppermute | solution.py:19
  44.7 1.8 %collective-permute-start.8 = (f32[16]{0:T(128)S(1)}, f32[16]{0:T(128)S(1)}, u32[]{:S(2)}, u32[]{:S(2)}) collective-permute-start(f32[16]{0:T(128)S(1)} %add.169), channel_id=1, source_target_pairs={{0,8},{4,12},{8,0},{12,4},{16,24},{20,28},{24,16},{28,20},{1,9},{5... | collective-permute-start | bytes 200 | tf_op jit(solution)/shard_map/ppermute | solution.py:19
  46.5 3.5 %fusion.8 = f32[48,2048]{1,0:T(8,128)S(1)} fusion(s32[4,512]{1,0:T(4,128)S(1)} %pad_add_fusion, bf16[4,16,512]{2,1,0:T(8,128)(2,1)S(1)} %get-tuple-element.26, bf16[4,16,512]{2,1,0:T(8,128)(2,1)S(1)} %get-tuple-element.27, bf16[4,16,512]{2,1,0:T(8,128)(2,1)S(1)} %get-tuple-element.25), kind=kOutput, calls=%fused_computation.14 | convolution fusion | flops 407437312 | bytes 598016 | tf_op jit(solution)/shard_map/gci,gip->cp/dot_general | solution.py:48
  50.0 1.6 %collective-permute-start.9 = (f32[16]{0:T(128)S(1)}, f32[16]{0:T(128)S(1)}, u32[]{:S(2)}, u32[]{:S(2)}) collective-permute-start(f32[16]{0:T(128)S(1)} %add.170), channel_id=1, source_target_pairs={{0,16},{4,20},{8,24},{12,28},{16,0},{20,4},{24,8},{28,12},{1,17},{... | collective-permute-start | bytes 200 | tf_op jit(solution)/shard_map/ppermute | solution.py:19
  51.7 1.9 %collective-permute-done.9 = f32[16]{0:T(128)S(1)} collective-permute-done((f32[16]{0:T(128)S(1)}, f32[16]{0:T(128)S(1)}, u32[]{:S(2)}, u32[]{:S(2)}) %collective-permute-start.9) | collective-permute-done | bytes 96 | tf_op jit(solution)/shard_map/ppermute | solution.py:19
  53.8 1.2 %convolution_bitcast_fusion = f32[5,16,128]{2,1,0:T(8,128)S(1)} fusion(f32[128,2048]{1,0:T(8,128)S(1)} %copy-done, f32[2048,16]{0,1:T(8,128)S(1)} %bitcast.56, f32[2048,5]{0,1:T(8,128)S(1)} %bitcast.58), kind=kOutput, calls=%fused_computation.20 | convolution fusion | flops 251822080 | bytes 1261568 | tf_op jit(solution)/shard_map/lp,cp,rp->lcr/dot_general | solution.py:92
  55.3 3.9 %collective-permute-done.10 = f32[6,16,128]{2,1,0:T(8,128)S(1)} collective-permute-done((f32[6,16,128]{2,1,0:T(8,128)S(1)}, f32[6,16,128]{2,1,0:T(8,128)S(1)}, u32[]{:S(2)}, u32[]{:S(2)}) %collective-permute-start.10) | collective-permute-done | bytes 49184 | tf_op jit(solution)/shard_map/ppermute | solution.py:19
  59.2 2.5 %collective-permute-start.11 = (f32[5,16,128]{2,1,0:T(8,128)S(1)}, f32[5,16,128]{2,1,0:T(8,128)S(1)}, u32[]{:S(2)}, u32[]{:S(2)}) collective-permute-start(f32[5,16,128]{2,1,0:T(8,128)S(1)} %slice.170), channel_id=1, source_target_pairs={{0,2},{1,3},{2,0},{3,1},{4,6},{5,7},{6,4},{7,5},{8,10},{9,11},{10,... | collective-permute-start | bytes 122888 | tf_op jit(solution)/shard_map/ppermute | solution.py:19
  61.7 2.5 %collective-permute-done.11 = f32[5,16,128]{2,1,0:T(8,128)S(1)} collective-permute-done((f32[5,16,128]{2,1,0:T(8,128)S(1)}, f32[5,16,128]{2,1,0:T(8,128)S(1)}, u32[]{:S(2)}, u32[]{:S(2)}) %collective-permute-start.11) | collective-permute-done | bytes 40992 | tf_op jit(solution)/shard_map/ppermute | solution.py:19
  64.3 1.2 %collective-permute-done.12 = f32[4,16,128]{2,1,0:T(8,128)S(1)} collective-permute-done((f32[4,16,128]{2,1,0:T(8,128)S(1)}, f32[4,16,128]{2,1,0:T(8,128)S(1)}, u32[]{:S(2)}, u32[]{:S(2)}) %collective-permute-start.12) | collective-permute-done | bytes 32800 | tf_op jit(solution)/shard_map/ppermute | solution.py:19
  65.8 3.6 %collective-permute-done.13 = f32[3,16,128]{2,1,0:T(8,128)S(1)} collective-permute-done((f32[3,16,128]{2,1,0:T(8,128)S(1)}, f32[3,16,128]{2,1,0:T(8,128)S(1)}, u32[]{:S(2)}, u32[]{:S(2)}) %collective-permute-start.13) | collective-permute-done | bytes 24608 | tf_op jit(solution)/shard_map/ppermute | solution.py:19
  69.4 1.6 %collective-permute-start.14 = (f32[2,16,128]{2,1,0:T(8,128)S(1)}, f32[2,16,128]{2,1,0:T(8,128)S(1)}, u32[]{:S(2)}, u32[]{:S(2)}) collective-permute-start(f32[2,16,128]{2,1,0:T(8,128)S(1)} %slice.173), channel_id=1, source_target_pairs={{0,16},{4,20},{8,24},{12,28},{16,0},{20,4},{24,8},{28,12},{1,17},{... | collective-permute-start | bytes 49160 | tf_op jit(solution)/shard_map/ppermute | solution.py:19
  71.0 3.5 %fusion.13 = f32[4,48,512]{2,1,0:T(8,128)S(1)} fusion(s32[4,512]{1,0:T(4,128)S(1)} %pad_add_fusion, bf16[16,2048]{1,0:T(8,128)(2,1)S(1)} %get-tuple-element.23, bf16[16,2048]{1,0:T(8,128)(2,1)S(1)} %get-tuple-element.22, bf16[16,2048]{1,0:T(8,128)(2,1)S(1)} %get-tuple-element.12), kind=kOutput, calls=%fused_computation.19 | convolution fusion | flops 407437312 | bytes 598016 | tf_op jit(solution)/shard_map/cp,gip->gci/dot_general | solution.py:42
  74.7 1.9 %multiply_reduce_fusion = (f32[16]{0:T(128)S(1)}, f32[4,16,512]{2,1,0:T(8,128)S(1)}) fusion(f32[4,16,512]{2,1,0:T(8,128)S(1)} %get-tuple-element.7, f32[4,24,512]{2,1,0:T(8,128)S(1)} %slice_add_fusion, f32[16]{0:T(128)S(1)} %get-tuple-element.10, f32[4,48,512]{2,1,0:T(8,128)S(1)} %fusion.13, f32[4,512,512]{2,1,0:T(8,128)S(1)} %exponential_multiply_fusion), kind=kOutput, calls=%fused_computation.90 | convolution fusion | flops 100990960 | bytes 5374528 | tf_op jit(solution)/shard_map/gij,gcj->gci/dot_general | solution.py:30
  76.9 0.6 convolution_multiply_fusion.2
  77.6 0.8 fusion.12
  78.7 3.4 %collective-permute-done.15 = f32[16]{0:T(128)S(1)} collective-permute-done((f32[16]{0:T(128)S(1)}, f32[16]{0:T(128)S(1)}, u32[]{:S(2)}, u32[]{:S(2)}) %collective-permute-start.15) | collective-permute-done | bytes 96 | tf_op jit(solution)/shard_map/ppermute | solution.py:19
  82.2 2.4 %collective-permute-start.16 = (f32[16]{0:T(128)S(1)}, f32[16]{0:T(128)S(1)}, u32[]{:S(2)}, u32[]{:S(2)}) collective-permute-start(f32[16]{0:T(128)S(1)} %add.188), channel_id=1, source_target_pairs={{0,2},{1,3},{2,0},{3,1},{4,6},{5,7},{6,4},{7,5},{8,10},{9,11},{10,... | collective-permute-start | bytes 200 | tf_op jit(solution)/shard_map/ppermute | solution.py:19
  84.6 2.0 %collective-permute-done.16 = f32[16]{0:T(128)S(1)} collective-permute-done((f32[16]{0:T(128)S(1)}, f32[16]{0:T(128)S(1)}, u32[]{:S(2)}, u32[]{:S(2)}) %collective-permute-start.16) | collective-permute-done | bytes 96 | tf_op jit(solution)/shard_map/ppermute | solution.py:19
  86.6 1.1 %collective-permute-done.17 = f32[16]{0:T(128)S(1)} collective-permute-done((f32[16]{0:T(128)S(1)}, f32[16]{0:T(128)S(1)}, u32[]{:S(2)}, u32[]{:S(2)}) %collective-permute-start.17) | collective-permute-done | bytes 96 | tf_op jit(solution)/shard_map/ppermute | solution.py:19
  87.7 0.5 collective-permute-start.18
  88.3 3.0 %collective-permute-done.18 = f32[16]{0:T(128)S(1)} collective-permute-done((f32[16]{0:T(128)S(1)}, f32[16]{0:T(128)S(1)}, u32[]{:S(2)}, u32[]{:S(2)}) %collective-permute-start.18) | collective-permute-done | bytes 96 | tf_op jit(solution)/shard_map/ppermute | solution.py:19
  91.3 0.5 collective-permute-start.19
  91.8 3.7 %fusion.9 = f32[48,2048]{1,0:T(8,128)S(1)} fusion(s32[4,512]{1,0:T(4,128)S(1)} %pad_add_fusion, bf16[4,16,512]{2,1,0:T(8,128)(2,1)S(1)} %get-tuple-element.20, bf16[4,16,512]{2,1,0:T(8,128)(2,1)S(1)} %get-tuple-element.21, bf16[4,16,512]{2,1,0:T(8,128)(2,1)S(1)} %get-tuple-element.19), kind=kOutput, calls=%fused_computation.15 | convolution fusion | flops 407437312 | bytes 598016 | tf_op jit(solution)/shard_map/gci,gip->cp/dot_general | solution.py:48
  95.5 0.8 fusion.51
  (79 shorter events, 3.4 us)
Async XLA Ops:
  0.6 1.3 %copy-start = (f32[128,2048]{1,0:T(8,128)S(1)}, f32[128,2048]{1,0:T(8,128)}, u32[]{:S(2)}) copy-start(f32[128,2048]{1,0:T(8,128)} %param.13) | copy-start | bytes 3145732
  4.1 12.3 %collective-permute-start = (f32[6,16,128]{2,1,0:T(8,128)S(1)}, f32[6,16,128]{2,1,0:T(8,128)S(1)}, u32[]{:S(2)}, u32[]{:S(2)}) collective-permute-start(f32[6,16,128]{2,1,0:T(8,128)S(1)} %pad_maximum_fusion.1), channel_id=1, source_target_pairs={{0,1},{1,0},{2,3},{3,2},{4,5},{5,4},{6,7},{7,6},{8,9},{9,8},{10,11... | collective-permute-start | bytes 147464 | tf_op jit(solution)/shard_map/ppermute | solution.py:19
  16.4 5.0 %collective-permute-start.1 = (f32[5,16,128]{2,1,0:T(8,128)S(1)}, f32[5,16,128]{2,1,0:T(8,128)S(1)}, u32[]{:S(2)}, u32[]{:S(2)}) collective-permute-start(f32[5,16,128]{2,1,0:T(8,128)S(1)} %slice.156), channel_id=1, source_target_pairs={{0,2},{1,3},{2,0},{3,1},{4,6},{5,7},{6,4},{7,5},{8,10},{9,11},{10,... | collective-permute-start | bytes 122888 | tf_op jit(solution)/shard_map/ppermute | solution.py:19
  21.4 12.2 %copy-start.2 = (f32[5,128,128]{2,1,0:T(8,128)S(1)}, f32[5,128,128]{2,1,0:T(8,128)}, u32[]{:S(2)}) copy-start(f32[5,128,128]{2,1,0:T(8,128)} %param.15) | copy-start | bytes 983044
  21.4 4.4 %collective-permute-start.2 = (f32[4,16,128]{2,1,0:T(8,128)S(1)}, f32[4,16,128]{2,1,0:T(8,128)S(1)}, u32[]{:S(2)}, u32[]{:S(2)}) collective-permute-start(f32[4,16,128]{2,1,0:T(8,128)S(1)} %slice.157), channel_id=1, source_target_pairs={{0,4},{4,0},{8,12},{12,8},{16,20},{20,16},{24,28},{28,24},{1,5},{5... | collective-permute-start | bytes 98312 | tf_op jit(solution)/shard_map/ppermute | solution.py:19
  25.8 8.8 %copy-start.3 = (f32[5,2048]{1,0:T(8,128)S(1)}, f32[5,2048]{1,0:T(8,128)}, u32[]{:S(2)}) copy-start(f32[5,2048]{1,0:T(8,128)} %param.14) | copy-start | bytes 122884
  25.8 9.6 %copy-start.1 = (f32[16,2048]{1,0:T(8,128)S(1)}, f32[16,2048]{1,0:T(8,128)}, u32[]{:S(2)}) copy-start(f32[16,2048]{1,0:T(8,128)} %param.12) | copy-start | bytes 393220
  25.8 9.5 %copy-start.4 = (f32[2048]{0:T(1024)S(1)}, f32[2048]{0:T(1024)}, u32[]{:S(2)}) copy-start(f32[2048]{0:T(1024)} %param.11) | copy-start | bytes 24580
  25.8 3.9 %collective-permute-start.3 = (f32[3,16,128]{2,1,0:T(8,128)S(1)}, f32[3,16,128]{2,1,0:T(8,128)S(1)}, u32[]{:S(2)}, u32[]{:S(2)}) collective-permute-start(f32[3,16,128]{2,1,0:T(8,128)S(1)} %slice.158), channel_id=1, source_target_pairs={{0,8},{4,12},{8,0},{12,4},{16,24},{20,28},{24,16},{28,20},{1,9},{5... | collective-permute-start | bytes 73736 | tf_op jit(solution)/shard_map/ppermute | solution.py:19
  29.7 3.8 %collective-permute-start.4 = (f32[2,16,128]{2,1,0:T(8,128)S(1)}, f32[2,16,128]{2,1,0:T(8,128)S(1)}, u32[]{:S(2)}, u32[]{:S(2)}) collective-permute-start(f32[2,16,128]{2,1,0:T(8,128)S(1)} %slice.159), channel_id=1, source_target_pairs={{0,16},{4,20},{8,24},{12,28},{16,0},{20,4},{24,8},{28,12},{1,17},{... | collective-permute-start | bytes 49160 | tf_op jit(solution)/shard_map/ppermute | solution.py:19
  35.5 3.6 %collective-permute-start.5 = (f32[16]{0:T(128)S(1)}, f32[16]{0:T(128)S(1)}, u32[]{:S(2)}, u32[]{:S(2)}) collective-permute-start(f32[16]{0:T(128)S(1)} %add.166), channel_id=1, source_target_pairs={{0,1},{1,0},{2,3},{3,2},{4,5},{5,4},{6,7},{7,6},{8,9},{9,8},{10,11... | collective-permute-start | bytes 200 | tf_op jit(solution)/shard_map/ppermute | solution.py:19
  39.1 4.4 %collective-permute-start.6 = (f32[16]{0:T(128)S(1)}, f32[16]{0:T(128)S(1)}, u32[]{:S(2)}, u32[]{:S(2)}) collective-permute-start(f32[16]{0:T(128)S(1)} %add.167), channel_id=1, source_target_pairs={{0,2},{1,3},{2,0},{3,1},{4,6},{5,7},{6,4},{7,5},{8,10},{9,11},{10,... | collective-permute-start | bytes 200 | tf_op jit(solution)/shard_map/ppermute | solution.py:19
  43.5 1.1 %collective-permute-start.7 = (f32[16]{0:T(128)S(1)}, f32[16]{0:T(128)S(1)}, u32[]{:S(2)}, u32[]{:S(2)}) collective-permute-start(f32[16]{0:T(128)S(1)} %add.168), channel_id=1, source_target_pairs={{0,4},{4,0},{8,12},{12,8},{16,20},{20,16},{24,28},{28,24},{1,5},{5... | collective-permute-start | bytes 200 | tf_op jit(solution)/shard_map/ppermute | solution.py:19
  44.7 5.3 %collective-permute-start.8 = (f32[16]{0:T(128)S(1)}, f32[16]{0:T(128)S(1)}, u32[]{:S(2)}, u32[]{:S(2)}) collective-permute-start(f32[16]{0:T(128)S(1)} %add.169), channel_id=1, source_target_pairs={{0,8},{4,12},{8,0},{12,4},{16,24},{20,28},{24,16},{28,20},{1,9},{5... | collective-permute-start | bytes 200 | tf_op jit(solution)/shard_map/ppermute | solution.py:19
  50.0 3.6 %collective-permute-start.9 = (f32[16]{0:T(128)S(1)}, f32[16]{0:T(128)S(1)}, u32[]{:S(2)}, u32[]{:S(2)}) collective-permute-start(f32[16]{0:T(128)S(1)} %add.170), channel_id=1, source_target_pairs={{0,16},{4,20},{8,24},{12,28},{16,0},{20,4},{24,8},{28,12},{1,17},{... | collective-permute-start | bytes 200 | tf_op jit(solution)/shard_map/ppermute | solution.py:19
  55.1 4.1 %collective-permute-start.10 = (f32[6,16,128]{2,1,0:T(8,128)S(1)}, f32[6,16,128]{2,1,0:T(8,128)S(1)}, u32[]{:S(2)}, u32[]{:S(2)}) collective-permute-start(f32[6,16,128]{2,1,0:T(8,128)S(1)} %pad_maximum_fusion.2), channel_id=1, source_target_pairs={{0,1},{1,0},{2,3},{3,2},{4,5},{5,4},{6,7},{7,6},{8,9},{9,8},{10,11... | collective-permute-start | bytes 147464 | tf_op jit(solution)/shard_map/ppermute | solution.py:19
  59.2 5.0 %collective-permute-start.11 = (f32[5,16,128]{2,1,0:T(8,128)S(1)}, f32[5,16,128]{2,1,0:T(8,128)S(1)}, u32[]{:S(2)}, u32[]{:S(2)}) collective-permute-start(f32[5,16,128]{2,1,0:T(8,128)S(1)} %slice.170), channel_id=1, source_target_pairs={{0,2},{1,3},{2,0},{3,1},{4,6},{5,7},{6,4},{7,5},{8,10},{9,11},{10,... | collective-permute-start | bytes 122888 | tf_op jit(solution)/shard_map/ppermute | solution.py:19
  64.2 1.3 %collective-permute-start.12 = (f32[4,16,128]{2,1,0:T(8,128)S(1)}, f32[4,16,128]{2,1,0:T(8,128)S(1)}, u32[]{:S(2)}, u32[]{:S(2)}) collective-permute-start(f32[4,16,128]{2,1,0:T(8,128)S(1)} %slice.171), channel_id=1, source_target_pairs={{0,4},{4,0},{8,12},{12,8},{16,20},{20,16},{24,28},{28,24},{1,5},{5... | collective-permute-start | bytes 98312 | tf_op jit(solution)/shard_map/ppermute | solution.py:19
  65.5 3.9 %collective-permute-start.13 = (f32[3,16,128]{2,1,0:T(8,128)S(1)}, f32[3,16,128]{2,1,0:T(8,128)S(1)}, u32[]{:S(2)}, u32[]{:S(2)}) collective-permute-start(f32[3,16,128]{2,1,0:T(8,128)S(1)} %slice.172), channel_id=1, source_target_pairs={{0,8},{4,12},{8,0},{12,4},{16,24},{20,28},{24,16},{28,20},{1,9},{5... | collective-permute-start | bytes 73736 | tf_op jit(solution)/shard_map/ppermute | solution.py:19
  69.4 5.1 %collective-permute-start.14 = (f32[2,16,128]{2,1,0:T(8,128)S(1)}, f32[2,16,128]{2,1,0:T(8,128)S(1)}, u32[]{:S(2)}, u32[]{:S(2)}) collective-permute-start(f32[2,16,128]{2,1,0:T(8,128)S(1)} %slice.173), channel_id=1, source_target_pairs={{0,16},{4,20},{8,24},{12,28},{16,0},{20,4},{24,8},{28,12},{1,17},{... | collective-permute-start | bytes 49160 | tf_op jit(solution)/shard_map/ppermute | solution.py:19
  78.6 3.6 %collective-permute-start.15 = (f32[16]{0:T(128)S(1)}, f32[16]{0:T(128)S(1)}, u32[]{:S(2)}, u32[]{:S(2)}) collective-permute-start(f32[16]{0:T(128)S(1)} %add.187), channel_id=1, source_target_pairs={{0,1},{1,0},{2,3},{3,2},{4,5},{5,4},{6,7},{7,6},{8,9},{9,8},{10,11... | collective-permute-start | bytes 200 | tf_op jit(solution)/shard_map/ppermute | solution.py:19
  82.2 4.4 %collective-permute-start.16 = (f32[16]{0:T(128)S(1)}, f32[16]{0:T(128)S(1)}, u32[]{:S(2)}, u32[]{:S(2)}) collective-permute-start(f32[16]{0:T(128)S(1)} %add.188), channel_id=1, source_target_pairs={{0,2},{1,3},{2,0},{3,1},{4,6},{5,7},{6,4},{7,5},{8,10},{9,11},{10,... | collective-permute-start | bytes 200 | tf_op jit(solution)/shard_map/ppermute | solution.py:19
  86.6 1.1 %collective-permute-start.17 = (f32[16]{0:T(128)S(1)}, f32[16]{0:T(128)S(1)}, u32[]{:S(2)}, u32[]{:S(2)}) collective-permute-start(f32[16]{0:T(128)S(1)} %add.189), channel_id=1, source_target_pairs={{0,4},{4,0},{8,12},{12,8},{16,20},{20,16},{24,28},{28,24},{1,5},{5... | collective-permute-start | bytes 200 | tf_op jit(solution)/shard_map/ppermute | solution.py:19
  87.7 3.5 %collective-permute-start.18 = (f32[16]{0:T(128)S(1)}, f32[16]{0:T(128)S(1)}, u32[]{:S(2)}, u32[]{:S(2)}) collective-permute-start(f32[16]{0:T(128)S(1)} %add.190), channel_id=1, source_target_pairs={{0,8},{4,12},{8,0},{12,4},{16,24},{20,28},{24,16},{28,20},{1,9},{5... | collective-permute-start | bytes 200 | tf_op jit(solution)/shard_map/ppermute | solution.py:19
  91.3 4.2 %collective-permute-start.19 = (f32[16]{0:T(128)S(1)}, f32[16]{0:T(128)S(1)}, u32[]{:S(2)}, u32[]{:S(2)}) collective-permute-start(f32[16]{0:T(128)S(1)} %add.191), channel_id=1, source_target_pairs={{0,16},{4,20},{8,24},{12,28},{16,0},{20,4},{24,8},{28,12},{1,17},{... | collective-permute-start | bytes 200 | tf_op jit(solution)/shard_map/ppermute | solution.py:19

commit v9 on v8

--- a/solution.py
+++ b/solution.py
@@ -86,7 +86,7 @@
     scales = 2.0 ** ((1.0 - jnp.arange(levels, dtype=jnp.float32)) / 2.0)
 
     def near_of_union(values_u):
-        return near_apply(kern, values_u)
+        return lax.optimization_barrier(near_apply(kern, values_u))
 
     def sums_with_norm(values):
         proj = jnp.einsum("lp,cp,rp->lcr", level_gain, values, basis, precision=highest)

time: 96.6 us -> 94.3 us (0.976)
  starting transfers between devices: 24 us -> 19.9 us
  waiting for transfers between devices: 33.4 us -> 35.1 us
    ppermute x20, starting transfers between devices: 24 us -> 19.9 us  [swapped(): return lax.ppermute(value, axis, pairs)]
    ppermute x20, waiting for transfers between devices: 33.4 us -> 35.1 us  [swapped(): return lax.ppermute(value, axis, pairs)]
  transfers between devices with their start and end apart: 20 -> 20, of which waited for: 15 -> 14; matrix products, arithmetic and copies ran while one was open for 27% -> 30% of each run, Pallas kernels for 0% -> 0%
where the time goes in v9:
time: 94.3 us; the launch traced here: 94.1 us
  waiting for transfers between devices  35.1 us (37%)
  matrix products  28.7 us (30%)
  starting transfers between devices  19.9 us (21%)
  other arithmetic  7.29 us (8%)
  local copies, waits for them, and re-layouts  2.12 us (2%)
  between operations  0.98 us (1%)
    ppermute x20, waiting for transfers between devices, swapped(): return lax.ppermute(value, axis, pairs)  35.1 us
    ppermute x20, starting transfers between devices, swapped(): return lax.ppermute(value, axis, pairs)  19.9 us
    dot_general x2, matrix products, from_union(): jnp.einsum('gci,gip->cp', pieces(values_u, 1), hot, preferred_element_typ...  7.13 us
    dot_general x2, matrix products, to_union(): jnp.einsum('cp,gip->gci', pieces(values, 0), hot, preferred_element_type=...  6.97 us
    dot_general x1, matrix products, near_kernels(): gram = jnp.einsum('gfi,gfj->gij', union, union, precision=highest)  4.27 us
    dot_general x2, matrix products, near_apply(): jnp.einsum('gij,gcj->gci', kern, union_vec, precision=lax.Precision.HIGH)  3.47 us
    dot_general x2, matrix products, sums_with_norm(): jnp.einsum('lp,cp,rp->lcr', level_gain, values, basis, precision=highest)  3.32 us
  transfers between devices with their start and end apart: 20, of which 14 were waited for; matrix products, arithmetic and copies ran while one was open for 30% of the time, Pallas kernels for 0%

profile of v9, /device:TPU:0, one launch (start us, length us, event | category | flops | bytes accessed | tf_op | source)
XLA Modules:
  0.0 94.1 jit_solution(10030720567755921767)
XLA Ops:
  0.6 1.1 %multiply_reduce_fusion.5 = f32[16]{0:T(128)S(1)} fusion(f32[16,2048]{1,0:T(8,128)} %param.12), kind=kLoop, calls=%fused_computation.99 | loop fusion | flops 65520 | bytes 131136 | tf_op jit(solution)/shard_map/reduce_sum | solution.py:93
  1.9 2.1 %convolution_bitcast_fusion.1 = f32[5,16,128]{2,1,0:T(8,128)S(1)} fusion(f32[128,2048]{1,0:T(8,128)S(1)} %copy-done, f32[2048,5]{0,1:T(8,128)} %bitcast.57, f32[2048,16]{0,1:T(8,128)} %bitcast.55), kind=kOutput, calls=%fused_computation.21 | convolution fusion | flops 251822080 | bytes 1261568 | tf_op jit(solution)/shard_map/lp,cp,rp->lcr/dot_general | solution.py:92
  4.1 3.0 %collective-permute-start = (f32[6,16,128]{2,1,0:T(8,128)S(1)}, f32[6,16,128]{2,1,0:T(8,128)S(1)}, u32[]{:S(2)}, u32[]{:S(2)}) collective-permute-start(f32[6,16,128]{2,1,0:T(8,128)S(1)} %pad_maximum_fusion.1), channel_id=1, source_target_pairs={{0,1},{1,0},{2,3},{3,2},{4,5},{5,4},{6,7},{7,6},{8,9},{9,8},{10,11... | collective-permute-start | bytes 147464 | tf_op jit(solution)/shard_map/ppermute | solution.py:19
  7.2 0.5 broadcast.129
  7.7 1.4 %reduce.9 = s32[2048]{0:T(1024)S(1)} reduce(s32[1,2048]{1,0:T(1,128)} %param.16, s32[]{:T(128)} %broadcast.129), dimensions={0}, to_apply=%param.16.reduce_sub_computation.3 | reduce | bytes 16388 | tf_op args[7]
  9.1 0.8 fusion.59
  9.8 0.6 gather_fusion.1
  10.4 0.6 gather_fusion
  11.0 0.9 broadcast_multiply_fusion
  11.9 0.9 %reduce-precision_convert_fusion.1 = (bf16[24,2048]{1,0:T(8,128)(2,1)S(1)}, bf16[24,2048]{1,0:T(8,128)(2,1)S(1)}, bf16[24,2048]{1,0:T(8,128)(2,1)S(1)}) fusion(f32[16,2048]{1,0:T(8,128)} %param.12, f32[8,2048]{1,0:T(8,128)S(1)} %broadcast_multiply_fusion), kind=kLoop, calls=%fused_computation.44 | loop fusion | flops 393216 | bytes 491520 | tf_op jit(solution)/shard_map/convert.9
  12.8 3.5 %fusion.10 = f32[4,72,512]{2,1,0:T(8,128)S(1)} fusion(s32[4,512]{1,0:T(4,128)S(1)} %pad_add_fusion, bf16[24,2048]{1,0:T(8,128)(2,1)S(1)} %get-tuple-element.18, bf16[24,2048]{1,0:T(8,128)(2,1)S(1)} %get-tuple-element.17, bf16[24,2048]{1,0:T(8,128)(2,1)S(1)} %get-tuple-element.16), kind=kOutput, calls=%fused_computation.16 | convolution fusion | flops 609058816 | bytes 892928 | tf_op jit(solution)/shard_map/cp,gip->gci/dot_general | solution.py:42
  16.5 2.7 %collective-permute-start.1 = (f32[5,16,128]{2,1,0:T(8,128)S(1)}, f32[5,16,128]{2,1,0:T(8,128)S(1)}, u32[]{:S(2)}, u32[]{:S(2)}) collective-permute-start(f32[5,16,128]{2,1,0:T(8,128)S(1)} %slice.156), channel_id=1, source_target_pairs={{0,2},{1,3},{2,0},{3,1},{4,6},{5,7},{6,4},{7,5},{8,10},{9,11},{10,... | collective-permute-start | bytes 122888 | tf_op jit(solution)/shard_map/ppermute | solution.py:19
  19.1 4.3 %exponential_multiply_fusion = f32[4,512,512]{2,1,0:T(8,128)S(1)} fusion(f32[4,512]{1,0:T(4,128)S(1)} %multiply_reduce_fusion.6, f32[4,24,512]{2,1,0:T(8,128)S(1)} %slice_add_fusion), kind=kOutput, calls=%fused_computation.11 | convolution fusion | flops 105906176 | bytes 4276224 | tf_op jit(solution)/shard_map/gfi,gfj->gij/dot_general | solution.py:23
  23.5 1.7 %fusion.52 = f32[4,16,512]{2,1,0:T(8,128)S(1)} fusion(f32[4,512,512]{2,1,0:T(8,128)S(1)} %exponential_multiply_fusion, f32[4,24,512]{2,1,0:T(8,128)S(1)} %slice_add_fusion), kind=kOutput, calls=%fused_computation.100 | convolution fusion | flops 100663296 | bytes 4456448 | tf_op jit(solution)/shard_map/gij,gcj->gci/dot_general | solution.py:30
  25.3 1.6 %collective-permute-start.3 = (f32[3,16,128]{2,1,0:T(8,128)S(1)}, f32[3,16,128]{2,1,0:T(8,128)S(1)}, u32[]{:S(2)}, u32[]{:S(2)}) collective-permute-start(f32[3,16,128]{2,1,0:T(8,128)S(1)} %slice.158), channel_id=1, source_target_pairs={{0,8},{4,12},{8,0},{12,4},{16,24},{20,28},{24,16},{28,20},{1,9},{5... | collective-permute-start | bytes 73736 | tf_op jit(solution)/shard_map/ppermute | solution.py:19
  27.0 2.2 %collective-permute-done.3 = f32[3,16,128]{2,1,0:T(8,128)S(1)} collective-permute-done((f32[3,16,128]{2,1,0:T(8,128)S(1)}, f32[3,16,128]{2,1,0:T(8,128)S(1)}, u32[]{:S(2)}, u32[]{:S(2)}) %collective-permute-start.3) | collective-permute-done | bytes 24608 | tf_op jit(solution)/shard_map/ppermute | solution.py:19
  29.2 1.6 %collective-permute-start.4 = (f32[2,16,128]{2,1,0:T(8,128)S(1)}, f32[2,16,128]{2,1,0:T(8,128)S(1)}, u32[]{:S(2)}, u32[]{:S(2)}) collective-permute-start(f32[2,16,128]{2,1,0:T(8,128)S(1)} %slice.159), channel_id=1, source_target_pairs={{0,16},{4,20},{8,24},{12,28},{16,0},{20,4},{24,8},{28,12},{1,17},{... | collective-permute-start | bytes 49160 | tf_op jit(solution)/shard_map/ppermute | solution.py:19
  30.8 2.2 %collective-permute-done.4 = f32[2,16,128]{2,1,0:T(8,128)S(1)} collective-permute-done((f32[2,16,128]{2,1,0:T(8,128)S(1)}, f32[2,16,128]{2,1,0:T(8,128)S(1)}, u32[]{:S(2)}, u32[]{:S(2)}) %collective-permute-start.4) | collective-permute-done | bytes 16416 | tf_op jit(solution)/shard_map/ppermute | solution.py:19
  33.4 0.6 convolution_multiply_fusion.3
  34.0 0.8 fusion.11
  35.0 0.5 collective-permute-start.5
  35.5 3.1 %collective-permute-done.5 = f32[16]{0:T(128)S(1)} collective-permute-done((f32[16]{0:T(128)S(1)}, f32[16]{0:T(128)S(1)}, u32[]{:S(2)}, u32[]{:S(2)}) %collective-permute-start.5) | collective-permute-done | bytes 96 | tf_op jit(solution)/shard_map/ppermute | solution.py:19
  38.6 0.6 collective-permute-start.6
  39.1 3.9 %collective-permute-done.6 = f32[16]{0:T(128)S(1)} collective-permute-done((f32[16]{0:T(128)S(1)}, f32[16]{0:T(128)S(1)}, u32[]{:S(2)}, u32[]{:S(2)}) %collective-permute-start.6) | collective-permute-done | bytes 96 | tf_op jit(solution)/shard_map/ppermute | solution.py:19
  43.1 1.1 %collective-permute-done.7 = f32[16]{0:T(128)S(1)} collective-permute-done((f32[16]{0:T(128)S(1)}, f32[16]{0:T(128)S(1)}, u32[]{:S(2)}, u32[]{:S(2)}) %collective-permute-start.7) | collective-permute-done | bytes 96 | tf_op jit(solution)/shard_map/ppermute | solution.py:19
  44.2 1.5 %collective-permute-start.8 = (f32[16]{0:T(128)S(1)}, f32[16]{0:T(128)S(1)}, u32[]{:S(2)}, u32[]{:S(2)}) collective-permute-start(f32[16]{0:T(128)S(1)} %add.169), channel_id=1, source_target_pairs={{0,8},{4,12},{8,0},{12,4},{16,24},{20,28},{24,16},{28,20},{1,9},{5... | collective-permute-start | bytes 200 | tf_op jit(solution)/shard_map/ppermute | solution.py:19
  45.7 3.5 %fusion.8 = f32[48,2048]{1,0:T(8,128)S(1)} fusion(s32[4,512]{1,0:T(4,128)S(1)} %pad_add_fusion, bf16[4,16,512]{2,1,0:T(8,128)(2,1)S(1)} %get-tuple-element.26, bf16[4,16,512]{2,1,0:T(8,128)(2,1)S(1)} %get-tuple-element.27, bf16[4,16,512]{2,1,0:T(8,128)(2,1)S(1)} %get-tuple-element.25), kind=kOutput, calls=%fused_computation.14 | convolution fusion | flops 407437312 | bytes 598016 | tf_op jit(solution)/shard_map/gci,gip->cp/dot_general | solution.py:48
  49.1 1.6 %collective-permute-start.9 = (f32[16]{0:T(128)S(1)}, f32[16]{0:T(128)S(1)}, u32[]{:S(2)}, u32[]{:S(2)}) collective-permute-start(f32[16]{0:T(128)S(1)} %add.170), channel_id=1, source_target_pairs={{0,16},{4,20},{8,24},{12,28},{16,0},{20,4},{24,8},{28,12},{1,17},{... | collective-permute-start | bytes 200 | tf_op jit(solution)/shard_map/ppermute | solution.py:19
  50.8 1.9 %collective-permute-done.9 = f32[16]{0:T(128)S(1)} collective-permute-done((f32[16]{0:T(128)S(1)}, f32[16]{0:T(128)S(1)}, u32[]{:S(2)}, u32[]{:S(2)}) %collective-permute-start.9) | collective-permute-done | bytes 96 | tf_op jit(solution)/shard_map/ppermute | solution.py:19
  53.0 1.2 %convolution_bitcast_fusion = f32[5,16,128]{2,1,0:T(8,128)S(1)} fusion(f32[128,2048]{1,0:T(8,128)S(1)} %copy-done, f32[2048,16]{0,1:T(8,128)S(1)} %bitcast.56, f32[2048,5]{0,1:T(8,128)S(1)} %bitcast.58), kind=kOutput, calls=%fused_computation.20 | convolution fusion | flops 251822080 | bytes 1261568 | tf_op jit(solution)/shard_map/lp,cp,rp->lcr/dot_general | solution.py:92
  54.7 3.6 %collective-permute-done.10 = f32[6,16,128]{2,1,0:T(8,128)S(1)} collective-permute-done((f32[6,16,128]{2,1,0:T(8,128)S(1)}, f32[6,16,128]{2,1,0:T(8,128)S(1)}, u32[]{:S(2)}, u32[]{:S(2)}) %collective-permute-start.10) | collective-permute-done | bytes 49184 | tf_op jit(solution)/shard_map/ppermute | solution.py:19
  58.4 0.6 collective-permute-start.11
  59.0 4.7 %collective-permute-done.11 = f32[5,16,128]{2,1,0:T(8,128)S(1)} collective-permute-done((f32[5,16,128]{2,1,0:T(8,128)S(1)}, f32[5,16,128]{2,1,0:T(8,128)S(1)}, u32[]{:S(2)}, u32[]{:S(2)}) %collective-permute-start.11) | collective-permute-done | bytes 40992 | tf_op jit(solution)/shard_map/ppermute | solution.py:19
  63.8 1.2 %collective-permute-done.12 = f32[4,16,128]{2,1,0:T(8,128)S(1)} collective-permute-done((f32[4,16,128]{2,1,0:T(8,128)S(1)}, f32[4,16,128]{2,1,0:T(8,128)S(1)}, u32[]{:S(2)}, u32[]{:S(2)}) %collective-permute-start.12) | collective-permute-done | bytes 32800 | tf_op jit(solution)/shard_map/ppermute | solution.py:19
  65.0 0.6 collective-permute-start.13
  65.6 3.5 %fusion.13 = f32[4,48,512]{2,1,0:T(8,128)S(1)} fusion(s32[4,512]{1,0:T(4,128)S(1)} %pad_add_fusion, bf16[16,2048]{1,0:T(8,128)(2,1)S(1)} %get-tuple-element.23, bf16[16,2048]{1,0:T(8,128)(2,1)S(1)} %get-tuple-element.22, bf16[16,2048]{1,0:T(8,128)(2,1)S(1)} %get-tuple-element.12), kind=kOutput, calls=%fused_computation.19 | convolution fusion | flops 407437312 | bytes 598016 | tf_op jit(solution)/shard_map/cp,gip->gci/dot_general | solution.py:42
  69.1 1.6 %collective-permute-start.14 = (f32[2,16,128]{2,1,0:T(8,128)S(1)}, f32[2,16,128]{2,1,0:T(8,128)S(1)}, u32[]{:S(2)}, u32[]{:S(2)}) collective-permute-start(f32[2,16,128]{2,1,0:T(8,128)S(1)} %slice.173), channel_id=1, source_target_pairs={{0,16},{4,20},{8,24},{12,28},{16,0},{20,4},{24,8},{28,12},{1,17},{... | collective-permute-start | bytes 49160 | tf_op jit(solution)/shard_map/ppermute | solution.py:19
  70.7 1.7 %fusion.67 = f32[4,16,512]{2,1,0:T(8,128)S(1)} fusion(f32[4,512,512]{2,1,0:T(8,128)S(1)} %exponential_multiply_fusion, f32[4,48,512]{2,1,0:T(8,128)S(1)} %fusion.13), kind=kOutput, calls=%fused_computation.152 | convolution fusion | flops 100728832 | bytes 4718592 | tf_op jit(solution)/shard_map/gij,gcj->gci/dot_general | solution.py:30
  73.7 0.6 convolution_multiply_fusion.2
  74.3 0.8 fusion.12
  75.5 3.4 %collective-permute-done.15 = f32[16]{0:T(128)S(1)} collective-permute-done((f32[16]{0:T(128)S(1)}, f32[16]{0:T(128)S(1)}, u32[]{:S(2)}, u32[]{:S(2)}) %collective-permute-start.15) | collective-permute-done | bytes 96 | tf_op jit(solution)/shard_map/ppermute | solution.py:19
  79.1 4.2 %collective-permute-done.16 = f32[16]{0:T(128)S(1)} collective-permute-done((f32[16]{0:T(128)S(1)}, f32[16]{0:T(128)S(1)}, u32[]{:S(2)}, u32[]{:S(2)}) %collective-permute-start.16) | collective-permute-done | bytes 96 | tf_op jit(solution)/shard_map/ppermute | solution.py:19
  83.3 1.1 %collective-permute-done.17 = f32[16]{0:T(128)S(1)} collective-permute-done((f32[16]{0:T(128)S(1)}, f32[16]{0:T(128)S(1)}, u32[]{:S(2)}, u32[]{:S(2)}) %collective-permute-start.17) | collective-permute-done | bytes 96 | tf_op jit(solution)/shard_map/ppermute | solution.py:19
  84.5 1.5 %collective-permute-start.18 = (f32[16]{0:T(128)S(1)}, f32[16]{0:T(128)S(1)}, u32[]{:S(2)}, u32[]{:S(2)}) collective-permute-start(f32[16]{0:T(128)S(1)} %add.190), channel_id=1, source_target_pairs={{0,8},{4,12},{8,0},{12,4},{16,24},{20,28},{24,16},{28,20},{1,9},{5... | collective-permute-start | bytes 200 | tf_op jit(solution)/shard_map/ppermute | solution.py:19
  86.0 2.0 %collective-permute-done.18 = f32[16]{0:T(128)S(1)} collective-permute-done((f32[16]{0:T(128)S(1)}, f32[16]{0:T(128)S(1)}, u32[]{:S(2)}, u32[]{:S(2)}) %collective-permute-start.18) | collective-permute-done | bytes 96 | tf_op jit(solution)/shard_map/ppermute | solution.py:19
  88.0 1.5 %collective-permute-start.19 = (f32[16]{0:T(128)S(1)}, f32[16]{0:T(128)S(1)}, u32[]{:S(2)}, u32[]{:S(2)}) collective-permute-start(f32[16]{0:T(128)S(1)} %add.191), channel_id=1, source_target_pairs={{0,16},{4,20},{8,24},{12,28},{16,0},{20,4},{24,8},{28,12},{1,17},{... | collective-permute-start | bytes 200 | tf_op jit(solution)/shard_map/ppermute | solution.py:19
  89.5 3.7 %fusion.9 = f32[48,2048]{1,0:T(8,128)S(1)} fusion(s32[4,512]{1,0:T(4,128)S(1)} %pad_add_fusion, bf16[4,16,512]{2,1,0:T(8,128)(2,1)S(1)} %get-tuple-element.20, bf16[4,16,512]{2,1,0:T(8,128)(2,1)S(1)} %get-tuple-element.21, bf16[4,16,512]{2,1,0:T(8,128)(2,1)S(1)} %get-tuple-element.19), kind=kOutput, calls=%fused_computation.15 | convolution fusion | flops 407437312 | bytes 598016 | tf_op jit(solution)/shard_map/gci,gip->cp/dot_general | solution.py:48
  93.2 0.8 fusion.51
  (81 shorter events, 4.2 us)
Async XLA Ops:
  0.6 1.3 %copy-start = (f32[128,2048]{1,0:T(8,128)S(1)}, f32[128,2048]{1,0:T(8,128)}, u32[]{:S(2)}) copy-start(f32[128,2048]{1,0:T(8,128)} %param.13) | copy-start | bytes 3145732
  4.1 12.3 %collective-permute-start = (f32[6,16,128]{2,1,0:T(8,128)S(1)}, f32[6,16,128]{2,1,0:T(8,128)S(1)}, u32[]{:S(2)}, u32[]{:S(2)}) collective-permute-start(f32[6,16,128]{2,1,0:T(8,128)S(1)} %pad_maximum_fusion.1), channel_id=1, source_target_pairs={{0,1},{1,0},{2,3},{3,2},{4,5},{5,4},{6,7},{7,6},{8,9},{9,8},{10,11... | collective-permute-start | bytes 147464 | tf_op jit(solution)/shard_map/ppermute | solution.py:19
  16.5 7.0 %collective-permute-start.1 = (f32[5,16,128]{2,1,0:T(8,128)S(1)}, f32[5,16,128]{2,1,0:T(8,128)S(1)}, u32[]{:S(2)}, u32[]{:S(2)}) collective-permute-start(f32[5,16,128]{2,1,0:T(8,128)S(1)} %slice.156), channel_id=1, source_target_pairs={{0,2},{1,3},{2,0},{3,1},{4,6},{5,7},{6,4},{7,5},{8,10},{9,11},{10,... | collective-permute-start | bytes 122888 | tf_op jit(solution)/shard_map/ppermute | solution.py:19
  23.4 9.7 %copy-start.2 = (f32[5,128,128]{2,1,0:T(8,128)S(1)}, f32[5,128,128]{2,1,0:T(8,128)}, u32[]{:S(2)}) copy-start(f32[5,128,128]{2,1,0:T(8,128)} %param.15) | copy-start | bytes 983044
  23.4 10.7 %copy-start.3 = (f32[5,2048]{1,0:T(8,128)S(1)}, f32[5,2048]{1,0:T(8,128)}, u32[]{:S(2)}) copy-start(f32[5,2048]{1,0:T(8,128)} %param.14) | copy-start | bytes 122884
  23.4 11.4 %copy-start.1 = (f32[16,2048]{1,0:T(8,128)S(1)}, f32[16,2048]{1,0:T(8,128)}, u32[]{:S(2)}) copy-start(f32[16,2048]{1,0:T(8,128)} %param.12) | copy-start | bytes 393220
  23.4 11.4 %copy-start.4 = (f32[2048]{0:T(1024)S(1)}, f32[2048]{0:T(1024)}, u32[]{:S(2)}) copy-start(f32[2048]{0:T(1024)} %param.11) | copy-start | bytes 24580
  23.5 1.8 %collective-permute-start.2 = (f32[4,16,128]{2,1,0:T(8,128)S(1)}, f32[4,16,128]{2,1,0:T(8,128)S(1)}, u32[]{:S(2)}, u32[]{:S(2)}) collective-permute-start(f32[4,16,128]{2,1,0:T(8,128)S(1)} %slice.157), channel_id=1, source_target_pairs={{0,4},{4,0},{8,12},{12,8},{16,20},{20,16},{24,28},{28,24},{1,5},{5... | collective-permute-start | bytes 98312 | tf_op jit(solution)/shard_map/ppermute | solution.py:19
  25.3 3.9 %collective-permute-start.3 = (f32[3,16,128]{2,1,0:T(8,128)S(1)}, f32[3,16,128]{2,1,0:T(8,128)S(1)}, u32[]{:S(2)}, u32[]{:S(2)}) collective-permute-start(f32[3,16,128]{2,1,0:T(8,128)S(1)} %slice.158), channel_id=1, source_target_pairs={{0,8},{4,12},{8,0},{12,4},{16,24},{20,28},{24,16},{28,20},{1,9},{5... | collective-permute-start | bytes 73736 | tf_op jit(solution)/shard_map/ppermute | solution.py:19
  29.2 3.8 %collective-permute-start.4 = (f32[2,16,128]{2,1,0:T(8,128)S(1)}, f32[2,16,128]{2,1,0:T(8,128)S(1)}, u32[]{:S(2)}, u32[]{:S(2)}) collective-permute-start(f32[2,16,128]{2,1,0:T(8,128)S(1)} %slice.159), channel_id=1, source_target_pairs={{0,16},{4,20},{8,24},{12,28},{16,0},{20,4},{24,8},{28,12},{1,17},{... | collective-permute-start | bytes 49160 | tf_op jit(solution)/shard_map/ppermute | solution.py:19
  35.0 3.6 %collective-permute-start.5 = (f32[16]{0:T(128)S(1)}, f32[16]{0:T(128)S(1)}, u32[]{:S(2)}, u32[]{:S(2)}) collective-permute-start(f32[16]{0:T(128)S(1)} %add.166), channel_id=1, source_target_pairs={{0,1},{1,0},{2,3},{3,2},{4,5},{5,4},{6,7},{7,6},{8,9},{9,8},{10,11... | collective-permute-start | bytes 200 | tf_op jit(solution)/shard_map/ppermute | solution.py:19
  38.6 4.4 %collective-permute-start.6 = (f32[16]{0:T(128)S(1)}, f32[16]{0:T(128)S(1)}, u32[]{:S(2)}, u32[]{:S(2)}) collective-permute-start(f32[16]{0:T(128)S(1)} %add.167), channel_id=1, source_target_pairs={{0,2},{1,3},{2,0},{3,1},{4,6},{5,7},{6,4},{7,5},{8,10},{9,11},{10,... | collective-permute-start | bytes 200 | tf_op jit(solution)/shard_map/ppermute | solution.py:19
  43.0 1.1 %collective-permute-start.7 = (f32[16]{0:T(128)S(1)}, f32[16]{0:T(128)S(1)}, u32[]{:S(2)}, u32[]{:S(2)}) collective-permute-start(f32[16]{0:T(128)S(1)} %add.168), channel_id=1, source_target_pairs={{0,4},{4,0},{8,12},{12,8},{16,20},{20,16},{24,28},{28,24},{1,5},{5... | collective-permute-start | bytes 200 | tf_op jit(solution)/shard_map/ppermute | solution.py:19
  44.2 5.0 %collective-permute-start.8 = (f32[16]{0:T(128)S(1)}, f32[16]{0:T(128)S(1)}, u32[]{:S(2)}, u32[]{:S(2)}) collective-permute-start(f32[16]{0:T(128)S(1)} %add.169), channel_id=1, source_target_pairs={{0,8},{4,12},{8,0},{12,4},{16,24},{20,28},{24,16},{28,20},{1,9},{5... | collective-permute-start | bytes 200 | tf_op jit(solution)/shard_map/ppermute | solution.py:19
  49.1 3.6 %collective-permute-start.9 = (f32[16]{0:T(128)S(1)}, f32[16]{0:T(128)S(1)}, u32[]{:S(2)}, u32[]{:S(2)}) collective-permute-start(f32[16]{0:T(128)S(1)} %add.170), channel_id=1, source_target_pairs={{0,16},{4,20},{8,24},{12,28},{16,0},{20,4},{24,8},{28,12},{1,17},{... | collective-permute-start | bytes 200 | tf_op jit(solution)/shard_map/ppermute | solution.py:19
  54.3 4.1 %collective-permute-start.10 = (f32[6,16,128]{2,1,0:T(8,128)S(1)}, f32[6,16,128]{2,1,0:T(8,128)S(1)}, u32[]{:S(2)}, u32[]{:S(2)}) collective-permute-start(f32[6,16,128]{2,1,0:T(8,128)S(1)} %pad_maximum_fusion.2), channel_id=1, source_target_pairs={{0,1},{1,0},{2,3},{3,2},{4,5},{5,4},{6,7},{7,6},{8,9},{9,8},{10,11... | collective-permute-start | bytes 147464 | tf_op jit(solution)/shard_map/ppermute | solution.py:19
  58.4 5.3 %collective-permute-start.11 = (f32[5,16,128]{2,1,0:T(8,128)S(1)}, f32[5,16,128]{2,1,0:T(8,128)S(1)}, u32[]{:S(2)}, u32[]{:S(2)}) collective-permute-start(f32[5,16,128]{2,1,0:T(8,128)S(1)} %slice.170), channel_id=1, source_target_pairs={{0,2},{1,3},{2,0},{3,1},{4,6},{5,7},{6,4},{7,5},{8,10},{9,11},{10,... | collective-permute-start | bytes 122888 | tf_op jit(solution)/shard_map/ppermute | solution.py:19
  63.7 1.3 %collective-permute-start.12 = (f32[4,16,128]{2,1,0:T(8,128)S(1)}, f32[4,16,128]{2,1,0:T(8,128)S(1)}, u32[]{:S(2)}, u32[]{:S(2)}) collective-permute-start(f32[4,16,128]{2,1,0:T(8,128)S(1)} %slice.171), channel_id=1, source_target_pairs={{0,4},{4,0},{8,12},{12,8},{16,20},{20,16},{24,28},{28,24},{1,5},{5... | collective-permute-start | bytes 98312 | tf_op jit(solution)/shard_map/ppermute | solution.py:19
  65.0 4.1 %collective-permute-start.13 = (f32[3,16,128]{2,1,0:T(8,128)S(1)}, f32[3,16,128]{2,1,0:T(8,128)S(1)}, u32[]{:S(2)}, u32[]{:S(2)}) collective-permute-start(f32[3,16,128]{2,1,0:T(8,128)S(1)} %slice.172), channel_id=1, source_target_pairs={{0,8},{4,12},{8,0},{12,4},{16,24},{20,28},{24,16},{28,20},{1,9},{5... | collective-permute-start | bytes 73736 | tf_op jit(solution)/shard_map/ppermute | solution.py:19
  69.1 3.8 %collective-permute-start.14 = (f32[2,16,128]{2,1,0:T(8,128)S(1)}, f32[2,16,128]{2,1,0:T(8,128)S(1)}, u32[]{:S(2)}, u32[]{:S(2)}) collective-permute-start(f32[2,16,128]{2,1,0:T(8,128)S(1)} %slice.173), channel_id=1, source_target_pairs={{0,16},{4,20},{8,24},{12,28},{16,0},{20,4},{24,8},{28,12},{1,17},{... | collective-permute-start | bytes 49160 | tf_op jit(solution)/shard_map/ppermute | solution.py:19
  75.3 3.6 %collective-permute-start.15 = (f32[16]{0:T(128)S(1)}, f32[16]{0:T(128)S(1)}, u32[]{:S(2)}, u32[]{:S(2)}) collective-permute-start(f32[16]{0:T(128)S(1)} %add.187), channel_id=1, source_target_pairs={{0,1},{1,0},{2,3},{3,2},{4,5},{5,4},{6,7},{7,6},{8,9},{9,8},{10,11... | collective-permute-start | bytes 200 | tf_op jit(solution)/shard_map/ppermute | solution.py:19
  78.9 4.4 %collective-permute-start.16 = (f32[16]{0:T(128)S(1)}, f32[16]{0:T(128)S(1)}, u32[]{:S(2)}, u32[]{:S(2)}) collective-permute-start(f32[16]{0:T(128)S(1)} %add.188), channel_id=1, source_target_pairs={{0,2},{1,3},{2,0},{3,1},{4,6},{5,7},{6,4},{7,5},{8,10},{9,11},{10,... | collective-permute-start | bytes 200 | tf_op jit(solution)/shard_map/ppermute | solution.py:19
  83.3 1.1 %collective-permute-start.17 = (f32[16]{0:T(128)S(1)}, f32[16]{0:T(128)S(1)}, u32[]{:S(2)}, u32[]{:S(2)}) collective-permute-start(f32[16]{0:T(128)S(1)} %add.189), channel_id=1, source_target_pairs={{0,4},{4,0},{8,12},{12,8},{16,20},{20,16},{24,28},{28,24},{1,5},{5... | collective-permute-start | bytes 200 | tf_op jit(solution)/shard_map/ppermute | solution.py:19
  84.5 3.5 %collective-permute-start.18 = (f32[16]{0:T(128)S(1)}, f32[16]{0:T(128)S(1)}, u32[]{:S(2)}, u32[]{:S(2)}) collective-permute-start(f32[16]{0:T(128)S(1)} %add.190), channel_id=1, source_target_pairs={{0,8},{4,12},{8,0},{12,4},{16,24},{20,28},{24,16},{28,20},{1,9},{5... | collective-permute-start | bytes 200 | tf_op jit(solution)/shard_map/ppermute | solution.py:19
  88.0 5.2 %collective-permute-start.19 = (f32[16]{0:T(128)S(1)}, f32[16]{0:T(128)S(1)}, u32[]{:S(2)}, u32[]{:S(2)}) collective-permute-start(f32[16]{0:T(128)S(1)} %add.191), channel_id=1, source_target_pairs={{0,16},{4,20},{8,24},{12,28},{16,0},{20,4},{24,8},{28,12},{1,17},{... | collective-permute-start | bytes 200 | tf_op jit(solution)/shard_map/ppermute | solution.py:19

commit v10 on v9

--- a/solution.py
+++ b/solution.py
@@ -19,8 +19,18 @@
     return lax.ppermute(value, axis, pairs)
 
 
+def split3(values):
+    high = lax.reduce_precision(values, exponent_bits=8, mantissa_bits=7)
+    rest = values - high
+    middle = lax.reduce_precision(rest, exponent_bits=8, mantissa_bits=7)
+    return high, middle, rest - middle
+
+
 def near_kernels(union):
-    gram = jnp.einsum("gfi,gfj->gij", union, union, precision=highest)
+    high, middle, low = split3(union)
+    left = jnp.concatenate([high, high, middle, high, low, middle], axis=1).astype(jnp.bfloat16)
+    right = jnp.concatenate([high, middle, high, low, high, middle], axis=1).astype(jnp.bfloat16)
+    gram = jnp.einsum("gfi,gfj->gij", left, right, preferred_element_type=jnp.float32)
     square = jnp.sum(union * union, axis=1)
     dist = square[:, :, None] + square[:, None, :] - 2.0 * gram
     return near_weight * jnp.exp(-0.5 * dist)
@@ -31,10 +41,7 @@
 
 
 def pieces(values, axis):
-    high = lax.reduce_precision(values, exponent_bits=8, mantissa_bits=7)
-    rest = values - high
-    middle = lax.reduce_precision(rest, exponent_bits=8, mantissa_bits=7)
-    return jnp.concatenate([high, middle, rest - middle], axis=axis).astype(jnp.bfloat16)
+    return jnp.concatenate(split3(values), axis=axis).astype(jnp.bfloat16)
 
 
 def to_union(values, hot):
@@ -81,8 +88,8 @@
     union_order = jnp.concatenate([order_tiles[pairs[0, 0]], order_tiles[pairs[0, 1]]], axis=1)
     position = jnp.arange(points, dtype=jnp.int32)
     hot = (union_order[:, :, None] == position[None, None, :]).astype(jnp.bfloat16)
-    stacked = to_union(jnp.concatenate([coords * inv_scale[:, None], right_side], axis=0), hot)
-    kern = lax.optimization_barrier(near_kernels(stacked[:, :features]))
+    stacked = to_union(jnp.concatenate([coords, right_side], axis=0), hot)
+    kern = lax.optimization_barrier(near_kernels(stacked[:, :features] * inv_scale[None, :, None]))
     scales = 2.0 ** ((1.0 - jnp.arange(levels, dtype=jnp.float32)) / 2.0)
 
     def near_of_union(values_u):

time: 94.3 us -> 91.4 us (0.969)
  starting transfers between devices: 19.9 us -> 26.7 us
  waiting for transfers between devices: 35.1 us -> 28.8 us
  matrix products: 28.7 us -> 26 us
  other arithmetic: 7.29 us -> 5.69 us
    ppermute x20, starting transfers between devices: 19.9 us -> 26.7 us  [swapped(): return lax.ppermute(value, axis, pairs)]
    ppermute x20, waiting for transfers between devices: 35.1 us -> 28.8 us  [swapped(): return lax.ppermute(value, axis, pairs)]
    dot_general x1, matrix products: 4.27 us -> 1.59 us  [near_kernels(): jnp.einsum('gfi,gfj->gij', left, right, preferred_element_type=jnp.float32)]
  transfers between devices with their start and end apart: 20 -> 20, of which waited for: 14 -> 15; matrix products, arithmetic and copies ran while one was open for 30% -> 26% of each run, Pallas kernels for 0% -> 0%
where the time goes in v10:
time: 91.4 us; the launch traced here: 91.2 us
  waiting for transfers between devices  28.8 us (32%)
  starting transfers between devices  26.7 us (29%)
  matrix products  26 us (28%)
  other arithmetic  5.69 us (6%)
  local copies, waits for them, and re-layouts  2.95 us (3%)
  between operations  1.01 us (1%)
    ppermute x20, waiting for transfers between devices, swapped(): return lax.ppermute(value, axis, pairs)  28.8 us
    ppermute x20, starting transfers between devices, swapped(): return lax.ppermute(value, axis, pairs)  26.7 us
    dot_general x2, matrix products, to_union(): jnp.einsum('cp,gip->gci', pieces(values, 0), hot, preferred_element_type=...  6.97 us
    dot_general x2, matrix products, from_union(): jnp.einsum('gci,gip->cp', pieces(values_u, 1), hot, preferred_element_typ...  6.92 us
    dot_general x2, matrix products, near_apply(): jnp.einsum('gij,gcj->gci', kern, union_vec, precision=lax.Precision.HIGH)  3.68 us
    dot_general x2, matrix products, sums_with_norm(): jnp.einsum('lp,cp,rp->lcr', level_gain, values, basis, precision=highest)  3.32 us
  transfers between devices with their start and end apart: 20, of which 15 were waited for; matrix products, arithmetic and copies ran while one was open for 26% of the time, Pallas kernels for 0%

profile of v10, /device:TPU:0, one launch (start us, length us, event | category | flops | bytes accessed | tf_op | source)
XLA Modules:
  0.0 91.2 jit_solution(9751757185605262023)
XLA Ops:
  0.6 0.9 %constant_dynamic-update-slice_fusion.1 = f32[24,2048]{1,0:T(8,128)S(1)} fusion(f32[8,2048]{1,0:T(8,128)} %param.9), kind=kLoop, calls=%fused_computation.121 | loop fusion | bytes 131072
  1.6 1.0 %multiply_reduce_fusion.5 = (f32[16]{0:T(128)S(1)}, f32[24,2048]{1,0:T(8,128)S(1)}) fusion(f32[16,2048]{1,0:T(8,128)} %param.12, f32[24,2048]{1,0:T(8,128)S(1)} %constant_dynamic-update-slice_fusion.1), kind=kLoop, calls=%fused_computation.98 | loop fusion | flops 65520 | bytes 262656 | tf_op jit(solution)/shard_map/reduce_sum | solution.py:100
  2.6 2.1 %convolution_bitcast_fusion.1 = f32[5,16,128]{2,1,0:T(8,128)S(1)} fusion(f32[128,2048]{1,0:T(8,128)S(1)} %copy-done, f32[2048,5]{0,1:T(8,128)} %bitcast.59, f32[2048,16]{0,1:T(8,128)} %bitcast.57), kind=kOutput, calls=%fused_computation.21 | convolution fusion | flops 251822080 | bytes 1261568 | tf_op jit(solution)/shard_map/lp,cp,rp->lcr/dot_general | solution.py:99
  4.8 3.1 %collective-permute-start = (f32[6,16,128]{2,1,0:T(8,128)S(1)}, f32[6,16,128]{2,1,0:T(8,128)S(1)}, u32[]{:S(2)}, u32[]{:S(2)}) collective-permute-start(f32[6,16,128]{2,1,0:T(8,128)S(1)} %pad_maximum_fusion), channel_id=1, source_target_pairs={{0,1},{1,0},{2,3},{3,2},{4,5},{5,4},{6,7},{7,6},{8,9},{9,8},{10,11... | collective-permute-start | bytes 147464 | tf_op jit(solution)/shard_map/ppermute | solution.py:19
  7.9 0.5 broadcast.129
  8.4 1.4 %reduce.9 = s32[2048]{0:T(1024)S(1)} reduce(s32[1,2048]{1,0:T(1,128)} %param.16, s32[]{:T(128)} %broadcast.129), dimensions={0}, to_apply=%param.16.reduce_sub_computation.3 | reduce | bytes 16388 | tf_op args[7]
  9.8 0.8 fusion.59
  10.6 0.6 gather_fusion.1
  11.1 0.6 gather_fusion
  11.8 3.5 %fusion.10 = f32[4,72,512]{2,1,0:T(8,128)S(1)} fusion(s32[4,512]{1,0:T(4,128)S(1)} %pad_add_fusion, bf16[24,2048]{1,0:T(8,128)(2,1)S(1)} %get-tuple-element.23, bf16[24,2048]{1,0:T(8,128)(2,1)S(1)} %get-tuple-element.24, bf16[24,2048]{1,0:T(8,128)(2,1)S(1)} %get-tuple-element.22), kind=kOutput, calls=%fused_computation.16 | convolution fusion | flops 609058816 | bytes 892928 | tf_op jit(solution)/shard_map/cp,gip->gci/dot_general | solution.py:49
  15.8 2.7 %collective-permute-start.1 = (f32[5,16,128]{2,1,0:T(8,128)S(1)}, f32[5,16,128]{2,1,0:T(8,128)S(1)}, u32[]{:S(2)}, u32[]{:S(2)}) collective-permute-start(f32[5,16,128]{2,1,0:T(8,128)S(1)} %slice.156), channel_id=1, source_target_pairs={{0,2},{1,3},{2,0},{3,1},{4,6},{5,7},{6,4},{7,5},{8,10},{9,11},{10,... | collective-permute-start | bytes 122888 | tf_op jit(solution)/shard_map/ppermute | solution.py:19
  18.4 1.6 %exponential_multiply_fusion = f32[4,512,512]{2,1,0:T(8,128)S(1)} fusion(bf16[4,48,512]{2,1,0:T(8,128)(2,1)S(1)} %get-tuple-element.41, bf16[4,48,512]{2,1,0:T(8,128)(2,1)S(1)} %get-tuple-element.40, f32[4,512]{1,0:T(4,128)S(1)} %multiply_reduce_fusion.6), kind=kOutput, calls=%fused_computation.11 | convolution fusion | flops 105906176 | bytes 4595712 | tf_op jit(solution)/shard_map/gfi,gfj->gij/dot_general | solution.py:33
  20.1 0.7 collective-permute-done.1
  20.8 1.7 %fusion.52 = f32[4,16,512]{2,1,0:T(8,128)S(1)} fusion(f32[4,512,512]{2,1,0:T(8,128)S(1)} %exponential_multiply_fusion, f32[4,24,512]{2,1,0:T(8,128)S(1)} %slice_add_fusion), kind=kOutput, calls=%fused_computation.99 | convolution fusion | flops 100663296 | bytes 4456448 | tf_op jit(solution)/shard_map/gij,gcj->gci/dot_general | solution.py:40
  22.6 1.9 %collective-permute-start.3 = (f32[3,16,128]{2,1,0:T(8,128)S(1)}, f32[3,16,128]{2,1,0:T(8,128)S(1)}, u32[]{:S(2)}, u32[]{:S(2)}) collective-permute-start(f32[3,16,128]{2,1,0:T(8,128)S(1)} %slice.158), channel_id=1, source_target_pairs={{0,8},{4,12},{8,0},{12,4},{16,24},{20,28},{24,16},{28,20},{1,9},{5... | collective-permute-start | bytes 73736 | tf_op jit(solution)/shard_map/ppermute | solution.py:19
  24.6 1.9 %collective-permute-done.3 = f32[3,16,128]{2,1,0:T(8,128)S(1)} collective-permute-done((f32[3,16,128]{2,1,0:T(8,128)S(1)}, f32[3,16,128]{2,1,0:T(8,128)S(1)}, u32[]{:S(2)}, u32[]{:S(2)}) %collective-permute-start.3) | collective-permute-done | bytes 24608 | tf_op jit(solution)/shard_map/ppermute | solution.py:19
  26.5 1.9 %collective-permute-start.4 = (f32[2,16,128]{2,1,0:T(8,128)S(1)}, f32[2,16,128]{2,1,0:T(8,128)S(1)}, u32[]{:S(2)}, u32[]{:S(2)}) collective-permute-start(f32[2,16,128]{2,1,0:T(8,128)S(1)} %slice.159), channel_id=1, source_target_pairs={{0,16},{4,20},{8,24},{12,28},{16,0},{20,4},{24,8},{28,12},{1,17},{... | collective-permute-start | bytes 49160 | tf_op jit(solution)/shard_map/ppermute | solution.py:19
  28.4 1.9 %collective-permute-done.4 = f32[2,16,128]{2,1,0:T(8,128)S(1)} collective-permute-done((f32[2,16,128]{2,1,0:T(8,128)S(1)}, f32[2,16,128]{2,1,0:T(8,128)S(1)}, u32[]{:S(2)}, u32[]{:S(2)}) %collective-permute-start.4) | collective-permute-done | bytes 16416 | tf_op jit(solution)/shard_map/ppermute | solution.py:19
  30.7 0.6 convolution_multiply_fusion.3
  31.3 0.8 fusion.11
  32.5 3.4 %collective-permute-done.5 = f32[16]{0:T(128)S(1)} collective-permute-done((f32[16]{0:T(128)S(1)}, f32[16]{0:T(128)S(1)}, u32[]{:S(2)}, u32[]{:S(2)}) %collective-permute-start.5) | collective-permute-done | bytes 96 | tf_op jit(solution)/shard_map/ppermute | solution.py:19
  35.9 2.6 %collective-permute-start.6 = (f32[16]{0:T(128)S(1)}, f32[16]{0:T(128)S(1)}, u32[]{:S(2)}, u32[]{:S(2)}) collective-permute-start(f32[16]{0:T(128)S(1)} %add.167), channel_id=1, source_target_pairs={{0,2},{1,3},{2,0},{3,1},{4,6},{5,7},{6,4},{7,5},{8,10},{9,11},{10,... | collective-permute-start | bytes 200 | tf_op jit(solution)/shard_map/ppermute | solution.py:19
  38.5 1.8 %collective-permute-done.6 = f32[16]{0:T(128)S(1)} collective-permute-done((f32[16]{0:T(128)S(1)}, f32[16]{0:T(128)S(1)}, u32[]{:S(2)}, u32[]{:S(2)}) %collective-permute-start.6) | collective-permute-done | bytes 96 | tf_op jit(solution)/shard_map/ppermute | solution.py:19
  40.4 1.1 %collective-permute-done.7 = f32[16]{0:T(128)S(1)} collective-permute-done((f32[16]{0:T(128)S(1)}, f32[16]{0:T(128)S(1)}, u32[]{:S(2)}, u32[]{:S(2)}) %collective-permute-start.7) | collective-permute-done | bytes 96 | tf_op jit(solution)/shard_map/ppermute | solution.py:19
  41.5 1.8 %collective-permute-start.8 = (f32[16]{0:T(128)S(1)}, f32[16]{0:T(128)S(1)}, u32[]{:S(2)}, u32[]{:S(2)}) collective-permute-start(f32[16]{0:T(128)S(1)} %add.169), channel_id=1, source_target_pairs={{0,8},{4,12},{8,0},{12,4},{16,24},{20,28},{24,16},{28,20},{1,9},{5... | collective-permute-start | bytes 200 | tf_op jit(solution)/shard_map/ppermute | solution.py:19
  43.3 3.5 %fusion.8 = f32[48,2048]{1,0:T(8,128)S(1)} fusion(s32[4,512]{1,0:T(4,128)S(1)} %pad_add_fusion, bf16[4,16,512]{2,1,0:T(8,128)(2,1)S(1)} %get-tuple-element.32, bf16[4,16,512]{2,1,0:T(8,128)(2,1)S(1)} %get-tuple-element.33, bf16[4,16,512]{2,1,0:T(8,128)(2,1)S(1)} %get-tuple-element.31), kind=kOutput, calls=%fused_computation.14 | convolution fusion | flops 407437312 | bytes 598016 | tf_op jit(solution)/shard_map/gci,gip->cp/dot_general | solution.py:55
  46.8 1.6 %collective-permute-start.9 = (f32[16]{0:T(128)S(1)}, f32[16]{0:T(128)S(1)}, u32[]{:S(2)}, u32[]{:S(2)}) collective-permute-start(f32[16]{0:T(128)S(1)} %add.170), channel_id=1, source_target_pairs={{0,16},{4,20},{8,24},{12,28},{16,0},{20,4},{24,8},{28,12},{1,17},{... | collective-permute-start | bytes 200 | tf_op jit(solution)/shard_map/ppermute | solution.py:19
  48.5 1.9 %collective-permute-done.9 = f32[16]{0:T(128)S(1)} collective-permute-done((f32[16]{0:T(128)S(1)}, f32[16]{0:T(128)S(1)}, u32[]{:S(2)}, u32[]{:S(2)}) %collective-permute-start.9) | collective-permute-done | bytes 96 | tf_op jit(solution)/shard_map/ppermute | solution.py:19
  50.6 1.2 %convolution_bitcast_fusion = f32[5,16,128]{2,1,0:T(8,128)S(1)} fusion(f32[128,2048]{1,0:T(8,128)S(1)} %copy-done, f32[2048,16]{0,1:T(8,128)S(1)} %bitcast.58, f32[2048,5]{0,1:T(8,128)S(1)} %bitcast.60), kind=kOutput, calls=%fused_computation.20 | convolution fusion | flops 251822080 | bytes 1261568 | tf_op jit(solution)/shard_map/lp,cp,rp->lcr/dot_general | solution.py:99
  52.1 3.9 %collective-permute-done.10 = f32[6,16,128]{2,1,0:T(8,128)S(1)} collective-permute-done((f32[6,16,128]{2,1,0:T(8,128)S(1)}, f32[6,16,128]{2,1,0:T(8,128)S(1)}, u32[]{:S(2)}, u32[]{:S(2)}) %collective-permute-start.10) | collective-permute-done | bytes 49184 | tf_op jit(solution)/shard_map/ppermute | solution.py:19
  56.0 2.5 %collective-permute-start.11 = (f32[5,16,128]{2,1,0:T(8,128)S(1)}, f32[5,16,128]{2,1,0:T(8,128)S(1)}, u32[]{:S(2)}, u32[]{:S(2)}) collective-permute-start(f32[5,16,128]{2,1,0:T(8,128)S(1)} %slice.170), channel_id=1, source_target_pairs={{0,2},{1,3},{2,0},{3,1},{4,6},{5,7},{6,4},{7,5},{8,10},{9,11},{10,... | collective-permute-start | bytes 122888 | tf_op jit(solution)/shard_map/ppermute | solution.py:19
  58.5 2.5 %collective-permute-done.11 = f32[5,16,128]{2,1,0:T(8,128)S(1)} collective-permute-done((f32[5,16,128]{2,1,0:T(8,128)S(1)}, f32[5,16,128]{2,1,0:T(8,128)S(1)}, u32[]{:S(2)}, u32[]{:S(2)}) %collective-permute-start.11) | collective-permute-done | bytes 40992 | tf_op jit(solution)/shard_map/ppermute | solution.py:19
  61.1 1.2 %collective-permute-done.12 = f32[4,16,128]{2,1,0:T(8,128)S(1)} collective-permute-done((f32[4,16,128]{2,1,0:T(8,128)S(1)}, f32[4,16,128]{2,1,0:T(8,128)S(1)}, u32[]{:S(2)}, u32[]{:S(2)}) %collective-permute-start.12) | collective-permute-done | bytes 32800 | tf_op jit(solution)/shard_map/ppermute | solution.py:19
  62.6 3.5 %fusion.13 = f32[4,48,512]{2,1,0:T(8,128)S(1)} fusion(s32[4,512]{1,0:T(4,128)S(1)} %pad_add_fusion, bf16[16,2048]{1,0:T(8,128)(2,1)S(1)} %get-tuple-element.29, bf16[16,2048]{1,0:T(8,128)(2,1)S(1)} %get-tuple-element.28, bf16[16,2048]{1,0:T(8,128)(2,1)S(1)} %get-tuple-element.12), kind=kOutput, calls=%fused_computation.19 | convolution fusion | flops 407437312 | bytes 598016 | tf_op jit(solution)/shard_map/cp,gip->gci/dot_general | solution.py:49
  66.2 1.8 %collective-permute-start.14 = (f32[2,16,128]{2,1,0:T(8,128)S(1)}, f32[2,16,128]{2,1,0:T(8,128)S(1)}, u32[]{:S(2)}, u32[]{:S(2)}) collective-permute-start(f32[2,16,128]{2,1,0:T(8,128)S(1)} %slice.173), channel_id=1, source_target_pairs={{0,16},{4,20},{8,24},{12,28},{16,0},{20,4},{24,8},{28,12},{1,17},{... | collective-permute-start | bytes 49160 | tf_op jit(solution)/shard_map/ppermute | solution.py:19
  68.0 2.0 %fusion.67 = f32[4,16,512]{2,1,0:T(8,128)S(1)} fusion(f32[4,512,512]{2,1,0:T(8,128)S(1)} %exponential_multiply_fusion, f32[4,48,512]{2,1,0:T(8,128)S(1)} %fusion.13), kind=kOutput, calls=%fused_computation.169 | convolution fusion | flops 100728832 | bytes 4718592 | tf_op jit(solution)/shard_map/gij,gcj->gci/dot_general | solution.py:40
  70.4 0.4 fusion.55
  70.8 0.6 convolution_multiply_fusion.2
  71.4 0.8 fusion.12
  72.6 3.4 %collective-permute-done.15 = f32[16]{0:T(128)S(1)} collective-permute-done((f32[16]{0:T(128)S(1)}, f32[16]{0:T(128)S(1)}, u32[]{:S(2)}, u32[]{:S(2)}) %collective-permute-start.15) | collective-permute-done | bytes 96 | tf_op jit(solution)/shard_map/ppermute | solution.py:19
  76.0 2.5 %collective-permute-start.16 = (f32[16]{0:T(128)S(1)}, f32[16]{0:T(128)S(1)}, u32[]{:S(2)}, u32[]{:S(2)}) collective-permute-start(f32[16]{0:T(128)S(1)} %add.188), channel_id=1, source_target_pairs={{0,2},{1,3},{2,0},{3,1},{4,6},{5,7},{6,4},{7,5},{8,10},{9,11},{10,... | collective-permute-start | bytes 200 | tf_op jit(solution)/shard_map/ppermute | solution.py:19
  78.5 2.0 %collective-permute-done.16 = f32[16]{0:T(128)S(1)} collective-permute-done((f32[16]{0:T(128)S(1)}, f32[16]{0:T(128)S(1)}, u32[]{:S(2)}, u32[]{:S(2)}) %collective-permute-start.16) | collective-permute-done | bytes 96 | tf_op jit(solution)/shard_map/ppermute | solution.py:19
  80.5 1.1 %collective-permute-done.17 = f32[16]{0:T(128)S(1)} collective-permute-done((f32[16]{0:T(128)S(1)}, f32[16]{0:T(128)S(1)}, u32[]{:S(2)}, u32[]{:S(2)}) %collective-permute-start.17) | collective-permute-done | bytes 96 | tf_op jit(solution)/shard_map/ppermute | solution.py:19
  81.6 1.7 %collective-permute-start.18 = (f32[16]{0:T(128)S(1)}, f32[16]{0:T(128)S(1)}, u32[]{:S(2)}, u32[]{:S(2)}) collective-permute-start(f32[16]{0:T(128)S(1)} %add.190), channel_id=1, source_target_pairs={{0,8},{4,12},{8,0},{12,4},{16,24},{20,28},{24,16},{28,20},{1,9},{5... | collective-permute-start | bytes 200 | tf_op jit(solution)/shard_map/ppermute | solution.py:19
  83.3 1.8 %collective-permute-done.18 = f32[16]{0:T(128)S(1)} collective-permute-done((f32[16]{0:T(128)S(1)}, f32[16]{0:T(128)S(1)}, u32[]{:S(2)}, u32[]{:S(2)}) %collective-permute-start.18) | collective-permute-done | bytes 96 | tf_op jit(solution)/shard_map/ppermute | solution.py:19
  85.1 1.7 %collective-permute-start.19 = (f32[16]{0:T(128)S(1)}, f32[16]{0:T(128)S(1)}, u32[]{:S(2)}, u32[]{:S(2)}) collective-permute-start(f32[16]{0:T(128)S(1)} %add.191), channel_id=1, source_target_pairs={{0,16},{4,20},{8,24},{12,28},{16,0},{20,4},{24,8},{28,12},{1,17},{... | collective-permute-start | bytes 200 | tf_op jit(solution)/shard_map/ppermute | solution.py:19
  86.9 3.5 %fusion.9 = f32[48,2048]{1,0:T(8,128)S(1)} fusion(s32[4,512]{1,0:T(4,128)S(1)} %pad_add_fusion, bf16[4,16,512]{2,1,0:T(8,128)(2,1)S(1)} %get-tuple-element.26, bf16[4,16,512]{2,1,0:T(8,128)(2,1)S(1)} %get-tuple-element.27, bf16[4,16,512]{2,1,0:T(8,128)(2,1)S(1)} %get-tuple-element.25), kind=kOutput, calls=%fused_computation.15 | convolution fusion | flops 407437312 | bytes 598016 | tf_op jit(solution)/shard_map/gci,gip->cp/dot_general | solution.py:55
  90.4 0.8 fusion.51
  (92 shorter events, 3.6 us)
Async XLA Ops:
  0.6 2.0 %copy-start = (f32[128,2048]{1,0:T(8,128)S(1)}, f32[128,2048]{1,0:T(8,128)}, u32[]{:S(2)}) copy-start(f32[128,2048]{1,0:T(8,128)} %param.13) | copy-start | bytes 3145732
  4.8 10.5 %copy-start.5 = (f32[8]{0:T(128)S(1)}, f32[8]{0:T(128)}, u32[]{:S(2)}) copy-start(f32[8]{0:T(128)} %param.10) | copy-start | bytes 100
  4.8 10.9 %collective-permute-start = (f32[6,16,128]{2,1,0:T(8,128)S(1)}, f32[6,16,128]{2,1,0:T(8,128)S(1)}, u32[]{:S(2)}, u32[]{:S(2)}) collective-permute-start(f32[6,16,128]{2,1,0:T(8,128)S(1)} %pad_maximum_fusion), channel_id=1, source_target_pairs={{0,1},{1,0},{2,3},{3,2},{4,5},{5,4},{6,7},{7,6},{8,9},{9,8},{10,11... | collective-permute-start | bytes 147464 | tf_op jit(solution)/shard_map/ppermute | solution.py:19
  15.8 5.0 %collective-permute-start.1 = (f32[5,16,128]{2,1,0:T(8,128)S(1)}, f32[5,16,128]{2,1,0:T(8,128)S(1)}, u32[]{:S(2)}, u32[]{:S(2)}) collective-permute-start(f32[5,16,128]{2,1,0:T(8,128)S(1)} %slice.156), channel_id=1, source_target_pairs={{0,2},{1,3},{2,0},{3,1},{4,6},{5,7},{6,4},{7,5},{8,10},{9,11},{10,... | collective-permute-start | bytes 122888 | tf_op jit(solution)/shard_map/ppermute | solution.py:19
  20.0 10.3 %copy-start.1 = (f32[5,128,128]{2,1,0:T(8,128)S(1)}, f32[5,128,128]{2,1,0:T(8,128)}, u32[]{:S(2)}) copy-start(f32[5,128,128]{2,1,0:T(8,128)} %param.15) | copy-start | bytes 983044
  20.1 11.3 %copy-start.3 = (f32[5,2048]{1,0:T(8,128)S(1)}, f32[5,2048]{1,0:T(8,128)}, u32[]{:S(2)}) copy-start(f32[5,2048]{1,0:T(8,128)} %param.14) | copy-start | bytes 122884
  20.1 12.0 %copy-start.2 = (f32[16,2048]{1,0:T(8,128)S(1)}, f32[16,2048]{1,0:T(8,128)}, u32[]{:S(2)}) copy-start(f32[16,2048]{1,0:T(8,128)} %param.12) | copy-start | bytes 393220
  20.1 12.0 %copy-start.4 = (f32[2048]{0:T(1024)S(1)}, f32[2048]{0:T(1024)}, u32[]{:S(2)}) copy-start(f32[2048]{0:T(1024)} %param.11) | copy-start | bytes 24580
  20.8 1.8 %collective-permute-start.2 = (f32[4,16,128]{2,1,0:T(8,128)S(1)}, f32[4,16,128]{2,1,0:T(8,128)S(1)}, u32[]{:S(2)}, u32[]{:S(2)}) collective-permute-start(f32[4,16,128]{2,1,0:T(8,128)S(1)} %slice.157), channel_id=1, source_target_pairs={{0,4},{4,0},{8,12},{12,8},{16,20},{20,16},{24,28},{28,24},{1,5},{5... | collective-permute-start | bytes 98312 | tf_op jit(solution)/shard_map/ppermute | solution.py:19
  22.6 3.9 %collective-permute-start.3 = (f32[3,16,128]{2,1,0:T(8,128)S(1)}, f32[3,16,128]{2,1,0:T(8,128)S(1)}, u32[]{:S(2)}, u32[]{:S(2)}) collective-permute-start(f32[3,16,128]{2,1,0:T(8,128)S(1)} %slice.158), channel_id=1, source_target_pairs={{0,8},{4,12},{8,0},{12,4},{16,24},{20,28},{24,16},{28,20},{1,9},{5... | collective-permute-start | bytes 73736 | tf_op jit(solution)/shard_map/ppermute | solution.py:19
  26.5 3.8 %collective-permute-start.4 = (f32[2,16,128]{2,1,0:T(8,128)S(1)}, f32[2,16,128]{2,1,0:T(8,128)S(1)}, u32[]{:S(2)}, u32[]{:S(2)}) collective-permute-start(f32[2,16,128]{2,1,0:T(8,128)S(1)} %slice.159), channel_id=1, source_target_pairs={{0,16},{4,20},{8,24},{12,28},{16,0},{20,4},{24,8},{28,12},{1,17},{... | collective-permute-start | bytes 49160 | tf_op jit(solution)/shard_map/ppermute | solution.py:19
  32.3 3.6 %collective-permute-start.5 = (f32[16]{0:T(128)S(1)}, f32[16]{0:T(128)S(1)}, u32[]{:S(2)}, u32[]{:S(2)}) collective-permute-start(f32[16]{0:T(128)S(1)} %add.166), channel_id=1, source_target_pairs={{0,1},{1,0},{2,3},{3,2},{4,5},{5,4},{6,7},{7,6},{8,9},{9,8},{10,11... | collective-permute-start | bytes 200 | tf_op jit(solution)/shard_map/ppermute | solution.py:19
  35.9 4.4 %collective-permute-start.6 = (f32[16]{0:T(128)S(1)}, f32[16]{0:T(128)S(1)}, u32[]{:S(2)}, u32[]{:S(2)}) collective-permute-start(f32[16]{0:T(128)S(1)} %add.167), channel_id=1, source_target_pairs={{0,2},{1,3},{2,0},{3,1},{4,6},{5,7},{6,4},{7,5},{8,10},{9,11},{10,... | collective-permute-start | bytes 200 | tf_op jit(solution)/shard_map/ppermute | solution.py:19
  40.3 1.1 %collective-permute-start.7 = (f32[16]{0:T(128)S(1)}, f32[16]{0:T(128)S(1)}, u32[]{:S(2)}, u32[]{:S(2)}) collective-permute-start(f32[16]{0:T(128)S(1)} %add.168), channel_id=1, source_target_pairs={{0,4},{4,0},{8,12},{12,8},{16,20},{20,16},{24,28},{28,24},{1,5},{5... | collective-permute-start | bytes 200 | tf_op jit(solution)/shard_map/ppermute | solution.py:19
  41.5 5.3 %collective-permute-start.8 = (f32[16]{0:T(128)S(1)}, f32[16]{0:T(128)S(1)}, u32[]{:S(2)}, u32[]{:S(2)}) collective-permute-start(f32[16]{0:T(128)S(1)} %add.169), channel_id=1, source_target_pairs={{0,8},{4,12},{8,0},{12,4},{16,24},{20,28},{24,16},{28,20},{1,9},{5... | collective-permute-start | bytes 200 | tf_op jit(solution)/shard_map/ppermute | solution.py:19
  46.8 3.6 %collective-permute-start.9 = (f32[16]{0:T(128)S(1)}, f32[16]{0:T(128)S(1)}, u32[]{:S(2)}, u32[]{:S(2)}) collective-permute-start(f32[16]{0:T(128)S(1)} %add.170), channel_id=1, source_target_pairs={{0,16},{4,20},{8,24},{12,28},{16,0},{20,4},{24,8},{28,12},{1,17},{... | collective-permute-start | bytes 200 | tf_op jit(solution)/shard_map/ppermute | solution.py:19
  51.9 4.1 %collective-permute-start.10 = (f32[6,16,128]{2,1,0:T(8,128)S(1)}, f32[6,16,128]{2,1,0:T(8,128)S(1)}, u32[]{:S(2)}, u32[]{:S(2)}) collective-permute-start(f32[6,16,128]{2,1,0:T(8,128)S(1)} %pad_maximum_fusion.1), channel_id=1, source_target_pairs={{0,1},{1,0},{2,3},{3,2},{4,5},{5,4},{6,7},{7,6},{8,9},{9,8},{10,11... | collective-permute-start | bytes 147464 | tf_op jit(solution)/shard_map/ppermute | solution.py:19
  56.0 5.0 %collective-permute-start.11 = (f32[5,16,128]{2,1,0:T(8,128)S(1)}, f32[5,16,128]{2,1,0:T(8,128)S(1)}, u32[]{:S(2)}, u32[]{:S(2)}) collective-permute-start(f32[5,16,128]{2,1,0:T(8,128)S(1)} %slice.170), channel_id=1, source_target_pairs={{0,2},{1,3},{2,0},{3,1},{4,6},{5,7},{6,4},{7,5},{8,10},{9,11},{10,... | collective-permute-start | bytes 122888 | tf_op jit(solution)/shard_map/ppermute | solution.py:19
  61.0 1.3 %collective-permute-start.12 = (f32[4,16,128]{2,1,0:T(8,128)S(1)}, f32[4,16,128]{2,1,0:T(8,128)S(1)}, u32[]{:S(2)}, u32[]{:S(2)}) collective-permute-start(f32[4,16,128]{2,1,0:T(8,128)S(1)} %slice.171), channel_id=1, source_target_pairs={{0,4},{4,0},{8,12},{12,8},{16,20},{20,16},{24,28},{28,24},{1,5},{5... | collective-permute-start | bytes 98312 | tf_op jit(solution)/shard_map/ppermute | solution.py:19
  62.3 3.9 %collective-permute-start.13 = (f32[3,16,128]{2,1,0:T(8,128)S(1)}, f32[3,16,128]{2,1,0:T(8,128)S(1)}, u32[]{:S(2)}, u32[]{:S(2)}) collective-permute-start(f32[3,16,128]{2,1,0:T(8,128)S(1)} %slice.172), channel_id=1, source_target_pairs={{0,8},{4,12},{8,0},{12,4},{16,24},{20,28},{24,16},{28,20},{1,9},{5... | collective-permute-start | bytes 73736 | tf_op jit(solution)/shard_map/ppermute | solution.py:19
  66.2 3.8 %collective-permute-start.14 = (f32[2,16,128]{2,1,0:T(8,128)S(1)}, f32[2,16,128]{2,1,0:T(8,128)S(1)}, u32[]{:S(2)}, u32[]{:S(2)}) collective-permute-start(f32[2,16,128]{2,1,0:T(8,128)S(1)} %slice.173), channel_id=1, source_target_pairs={{0,16},{4,20},{8,24},{12,28},{16,0},{20,4},{24,8},{28,12},{1,17},{... | collective-permute-start | bytes 49160 | tf_op jit(solution)/shard_map/ppermute | solution.py:19
  72.4 3.6 %collective-permute-start.15 = (f32[16]{0:T(128)S(1)}, f32[16]{0:T(128)S(1)}, u32[]{:S(2)}, u32[]{:S(2)}) collective-permute-start(f32[16]{0:T(128)S(1)} %add.187), channel_id=1, source_target_pairs={{0,1},{1,0},{2,3},{3,2},{4,5},{5,4},{6,7},{7,6},{8,9},{9,8},{10,11... | collective-permute-start | bytes 200 | tf_op jit(solution)/shard_map/ppermute | solution.py:19
  76.0 4.4 %collective-permute-start.16 = (f32[16]{0:T(128)S(1)}, f32[16]{0:T(128)S(1)}, u32[]{:S(2)}, u32[]{:S(2)}) collective-permute-start(f32[16]{0:T(128)S(1)} %add.188), channel_id=1, source_target_pairs={{0,2},{1,3},{2,0},{3,1},{4,6},{5,7},{6,4},{7,5},{8,10},{9,11},{10,... | collective-permute-start | bytes 200 | tf_op jit(solution)/shard_map/ppermute | solution.py:19
  80.5 1.1 %collective-permute-start.17 = (f32[16]{0:T(128)S(1)}, f32[16]{0:T(128)S(1)}, u32[]{:S(2)}, u32[]{:S(2)}) collective-permute-start(f32[16]{0:T(128)S(1)} %add.189), channel_id=1, source_target_pairs={{0,4},{4,0},{8,12},{12,8},{16,20},{20,16},{24,28},{28,24},{1,5},{5... | collective-permute-start | bytes 200 | tf_op jit(solution)/shard_map/ppermute | solution.py:19
  81.6 3.5 %collective-permute-start.18 = (f32[16]{0:T(128)S(1)}, f32[16]{0:T(128)S(1)}, u32[]{:S(2)}, u32[]{:S(2)}) collective-permute-start(f32[16]{0:T(128)S(1)} %add.190), channel_id=1, source_target_pairs={{0,8},{4,12},{8,0},{12,4},{16,24},{20,28},{24,16},{28,20},{1,9},{5... | collective-permute-start | bytes 200 | tf_op jit(solution)/shard_map/ppermute | solution.py:19
  85.1 5.2 %collective-permute-start.19 = (f32[16]{0:T(128)S(1)}, f32[16]{0:T(128)S(1)}, u32[]{:S(2)}, u32[]{:S(2)}) collective-permute-start(f32[16]{0:T(128)S(1)} %add.191), channel_id=1, source_target_pairs={{0,16},{4,20},{8,24},{12,28},{16,0},{20,4},{24,8},{28,12},{1,17},{... | collective-permute-start | bytes 200 | tf_op jit(solution)/shard_map/ppermute | solution.py:19

commit v11 on v10

--- a/solution.py
+++ b/solution.py
@@ -70,12 +70,20 @@
     return running
 
 
-def butterfly(value):
-    for bit in range(lax.axis_size("gy").bit_length() - 1):
-        value = value + swapped(value, "gy", bit)
-    for bit in range(lax.axis_size("gx").bit_length() - 1):
-        value = value + swapped(value, "gx", bit)
-    return value
+def butterfly(value, stages, state):
+    rounds = [("gy", bit) for bit in range(lax.axis_size("gy").bit_length() - 1)]
+    rounds += [("gx", bit) for bit in range(lax.axis_size("gx").bit_length() - 1)]
+    for index, (axis, bit) in enumerate(rounds):
+        partner = swapped(value, axis, bit)
+        if index < len(stages):
+            state, value = lax.optimization_barrier((state, value))
+            state = stages[index](state)
+        value = value + partner
+        if index < len(stages):
+            value, state = lax.optimization_barrier((value, state))
+    for stage in stages[len(rounds) :]:
+        state = stage(state)
+    return value, state
 
 
 def per_device(coords, inv_scale, noise, right_side, basis, level_gain, coupling, order, pairs):
@@ -95,25 +103,38 @@
     def near_of_union(values_u):
         return lax.optimization_barrier(near_apply(kern, values_u))
 
-    def sums_with_norm(values):
-        proj = jnp.einsum("lp,cp,rp->lcr", level_gain, values, basis, precision=highest)
+    def project(values):
+        return jnp.einsum("lp,cp,rp->lcr", level_gain, values, basis, precision=highest)
+
+    def sums_with_norm(values, proj):
         norm = jnp.sum(values * values, axis=1)
         extra = jnp.broadcast_to(norm[None, :, None], (1, columns, rank))
         running = tree_sums(jnp.concatenate([proj, extra], axis=0))
         return running[:levels], running[levels, :, 0]
 
+    half = union_order.shape[0] // 2
+
+    def unpermute_first(state):
+        late, near, extra = state
+        return late, from_union(late[:half], hot[:half]) + extra, extra
+
+    def unpermute_second(state):
+        late, near, extra = state
+        return late, near + from_union(late[half:], hot[half:]), extra
+
     solution = jnp.zeros_like(right_side)
     residual = right_side
     direction = right_side
     direction_u = stacked[:, features:]
+    residual_proj = project(residual)
     for step in range(ITERATIONS):
         if step == 0:
-            nodesum, norm_now = sums_with_norm(residual)
+            nodesum, norm_now = sums_with_norm(residual, residual_proj)
             near_u = near_of_union(direction_u)
             late_u, nodesum = lax.optimization_barrier((near_u, nodesum))
-            near = from_union(late_u, hot)
+            carried = jnp.zeros_like(right_side)
         else:
-            residual_sum, norm_next = sums_with_norm(residual)
+            residual_sum, norm_next = sums_with_norm(residual, residual_proj)
             residual_u = to_union(residual, hot)
             residual_near_u = near_of_union(residual_u)
             late_u, residual_sum = lax.optimization_barrier((residual_near_u, residual_sum))
@@ -122,7 +143,7 @@
             direction_u = residual_u + ratio[None, :, None] * direction_u
             nodesum = residual_sum + ratio[None, :, None] * nodesum
             near_u = residual_near_u + ratio[None, :, None] * near_u
-            near = from_union(late_u, hot) + ratio[:, None] * near
+            carried = ratio[:, None] * near
             norm_now = norm_next
         coupled = jnp.einsum("lcr,lrs->lcs", nodesum, coupling, precision=highest)
         coupled = (
@@ -132,10 +153,19 @@
         far = jnp.sum(back * level_gain[:, None, :], axis=0)
         base = noise[None, :] * direction + far
         local = jnp.sum(direction * base, axis=1) + jnp.sum(direction_u * near_u, axis=(0, 2))
-        curve = butterfly(local)
+        def project_image(state, base=base):
+            late, near, extra = state
+            return late, near, project(base + near)
+
+        stages = [unpermute_first, unpermute_second]
+        if step + 1 < ITERATIONS:
+            stages.append(project_image)
+        curve, (late_u, near, image_proj) = butterfly(local, stages, (late_u, carried, carried))
         alpha = norm_now / curve
         solution = solution + alpha[:, None] * direction
         residual = residual - alpha[:, None] * (base + near)
+        if step + 1 < ITERATIONS:
+            residual_proj = residual_proj - alpha[None, :, None] * image_proj
     return (solution, residual)
 
 

time: 91.4 us -> 91.2 us (level)
  other arithmetic: 5.69 us -> 8.59 us
  waiting for transfers between devices: 28.8 us -> 26.5 us
    eq x0 -> x1, other arithmetic: none -> 2.65 us  [per_device(): union_order[:, :, None] == position[None, None, :]]
    ppermute x20, waiting for transfers between devices: 28.8 us -> 26.5 us  [swapped(): return lax.ppermute(value, axis, pairs)]
    dot_general x2 -> x4, matrix products: 6.92 us -> 5.96 us  [from_union(): jnp.einsum('gci,gip->cp', pieces(values_u, 1), hot, preferred_element_typ...]
  transfers between devices with their start and end apart: 20 -> 20, of which waited for: 15 -> 16; matrix products, arithmetic and copies ran while one was open for 26% -> 29% of each run, Pallas kernels for 0% -> 0%
where the time goes in v11:
time: 91.2 us; the launch traced here: 90.9 us
  starting transfers between devices  26.7 us (29%)
  waiting for transfers between devices  26.5 us (29%)
  matrix products  25.1 us (28%)
  other arithmetic  8.59 us (9%)
  local copies, waits for them, and re-layouts  2.96 us (3%)
  between operations  1.08 us (1%)
    ppermute x20, starting transfers between devices, swapped(): return lax.ppermute(value, axis, pairs)  26.7 us
    ppermute x20, waiting for transfers between devices, swapped(): return lax.ppermute(value, axis, pairs)  26.5 us
    dot_general x2, matrix products, to_union(): jnp.einsum('cp,gip->gci', pieces(values, 0), hot, preferred_element_type=...  6.97 us
    dot_general x4, matrix products, from_union(): jnp.einsum('gci,gip->cp', pieces(values_u, 1), hot, preferred_element_typ...  5.96 us
    dot_general x2, matrix products, near_apply(): jnp.einsum('gij,gcj->gci', kern, union_vec, precision=lax.Precision.HIGH)  3.68 us
    dot_general x2, matrix products, project(): jnp.einsum('lp,cp,rp->lcr', level_gain, values, basis, precision=highest)  3.32 us
    eq x1, other arithmetic, per_device(): union_order[:, :, None] == position[None, None, :]  2.65 us
  transfers between devices with their start and end apart: 20, of which 16 were waited for; matrix products, arithmetic and copies ran while one was open for 29% of the time, Pallas kernels for 0%

profile of v11, /device:TPU:0, one launch (start us, length us, event | category | flops | bytes accessed | tf_op | source)
XLA Modules:
  0.0 90.9 jit_solution(18101113712978530539)
XLA Ops:
  0.6 0.9 %constant_dynamic-update-slice_fusion.1 = f32[24,2048]{1,0:T(8,128)S(1)} fusion(f32[8,2048]{1,0:T(8,128)} %param.9), kind=kLoop, calls=%fused_computation.155 | loop fusion | bytes 131072
  1.6 1.0 %multiply_reduce_fusion.5 = (f32[16]{0:T(128)S(1)}, f32[24,2048]{1,0:T(8,128)S(1)}) fusion(f32[16,2048]{1,0:T(8,128)} %param.12, f32[24,2048]{1,0:T(8,128)S(1)} %constant_dynamic-update-slice_fusion.1), kind=kLoop, calls=%fused_computation.90 | loop fusion | flops 65520 | bytes 262656 | tf_op jit(solution)/shard_map/reduce_sum | solution.py:110
  2.6 2.1 %convolution_bitcast_fusion.1 = f32[5,16,128]{2,1,0:T(8,128)S(1)} fusion(f32[128,2048]{1,0:T(8,128)S(1)} %copy-done, f32[2048,5]{0,1:T(8,128)} %bitcast.63, f32[2048,16]{0,1:T(8,128)} %bitcast.62), kind=kOutput, calls=%fused_computation.27 | convolution fusion | flops 251822080 | bytes 1261568 | tf_op jit(solution)/shard_map/lp,cp,rp->lcr/dot_general | solution.py:107
  4.8 3.1 %collective-permute-start = (f32[6,16,128]{2,1,0:T(8,128)S(1)}, f32[6,16,128]{2,1,0:T(8,128)S(1)}, u32[]{:S(2)}, u32[]{:S(2)}) collective-permute-start(f32[6,16,128]{2,1,0:T(8,128)S(1)} %pad_maximum_fusion), channel_id=1, source_target_pairs={{0,1},{1,0},{2,3},{3,2},{4,5},{5,4},{6,7},{7,6},{8,9},{9,8},{10,11... | collective-permute-start | bytes 147464 | tf_op jit(solution)/shard_map/ppermute | solution.py:19
  7.9 0.8 fusion.85
  9.2 1.4 %reduce.9 = s32[2048]{0:T(1024)S(1)} reduce(s32[1,2048]{1,0:T(1,128)} %param.16, s32[]{:T(128)} %broadcast.130), dimensions={0}, to_apply=%param.16.reduce_sub_computation.3 | reduce | bytes 16388 | tf_op args[7]
  10.6 0.6 gather_fusion.1
  11.8 3.5 %fusion.24 = f32[4,72,512]{2,1,0:T(8,128)S(1)} fusion(s32[4,512]{1,0:T(4,128)S(1)} %pad_add_fusion, bf16[24,2048]{1,0:T(8,128)(2,1)S(1)} %get-tuple-element.77, bf16[24,2048]{1,0:T(8,128)(2,1)S(1)} %get-tuple-element.78, bf16[24,2048]{1,0:T(8,128)(2,1)S(1)} %get-tuple-element.76), kind=kOutput, calls=%fused_computation.22 | convolution fusion | flops 609058816 | bytes 892928 | tf_op jit(solution)/shard_map/cp,gip->gci/dot_general | solution.py:49
  15.5 2.6 %iota_compare_fusion = pred[4,512,2048]{2,1,0:T(32,128)(4,1)S(1)} fusion(s32[4,512]{1,0:T(4,128)S(1)} %pad_add_fusion), kind=kLoop, calls=%fused_computation.2 | loop fusion | flops 4194304 | bytes 4202496 | tf_op jit(solution)/shard_map/eq | solution.py:98
  18.4 2.7 %collective-permute-start.1 = (f32[5,16,128]{2,1,0:T(8,128)S(1)}, f32[5,16,128]{2,1,0:T(8,128)S(1)}, u32[]{:S(2)}, u32[]{:S(2)}) collective-permute-start(f32[5,16,128]{2,1,0:T(8,128)S(1)} %slice.206), channel_id=1, source_target_pairs={{0,2},{1,3},{2,0},{3,1},{4,6},{5,7},{6,4},{7,5},{8,10},{9,11},{10,... | collective-permute-start | bytes 122888 | tf_op jit(solution)/shard_map/ppermute | solution.py:19
  21.1 1.6 %exponential_multiply_fusion = f32[4,512,512]{2,1,0:T(8,128)S(1)} fusion(bf16[4,48,512]{2,1,0:T(8,128)(2,1)S(1)} %get-tuple-element.101, bf16[4,48,512]{2,1,0:T(8,128)(2,1)S(1)} %get-tuple-element.100, f32[4,512]{1,0:T(4,128)S(1)} %multiply_reduce_fusion.6), kind=kOutput, calls=%fused_computation.15 | convolution fusion | flops 105906176 | bytes 4595712 | tf_op jit(solution)/shard_map/gfi,gfj->gij/dot_general | solution.py:33
  22.8 0.7 collective-permute-done.1
  23.5 1.7 %fusion.54 = f32[4,16,512]{2,1,0:T(8,128)S(1)} fusion(f32[4,512,512]{2,1,0:T(8,128)S(1)} %exponential_multiply_fusion, f32[4,24,512]{2,1,0:T(8,128)S(1)} %slice_add_fusion), kind=kOutput, calls=%fused_computation.91 | convolution fusion | flops 100663296 | bytes 4456448 | tf_op jit(solution)/shard_map/gij,gcj->gci/dot_general | solution.py:40
  25.3 1.9 %collective-permute-start.3 = (f32[3,16,128]{2,1,0:T(8,128)S(1)}, f32[3,16,128]{2,1,0:T(8,128)S(1)}, u32[]{:S(2)}, u32[]{:S(2)}) collective-permute-start(f32[3,16,128]{2,1,0:T(8,128)S(1)} %slice.208), channel_id=1, source_target_pairs={{0,8},{4,12},{8,0},{12,4},{16,24},{20,28},{24,16},{28,20},{1,9},{5... | collective-permute-start | bytes 73736 | tf_op jit(solution)/shard_map/ppermute | solution.py:19
  27.3 1.9 %collective-permute-done.3 = f32[3,16,128]{2,1,0:T(8,128)S(1)} collective-permute-done((f32[3,16,128]{2,1,0:T(8,128)S(1)}, f32[3,16,128]{2,1,0:T(8,128)S(1)}, u32[]{:S(2)}, u32[]{:S(2)}) %collective-permute-start.3) | collective-permute-done | bytes 24608 | tf_op jit(solution)/shard_map/ppermute | solution.py:19
  29.2 1.9 %collective-permute-start.4 = (f32[2,16,128]{2,1,0:T(8,128)S(1)}, f32[2,16,128]{2,1,0:T(8,128)S(1)}, u32[]{:S(2)}, u32[]{:S(2)}) collective-permute-start(f32[2,16,128]{2,1,0:T(8,128)S(1)} %slice.209), channel_id=1, source_target_pairs={{0,16},{4,20},{8,24},{12,28},{16,0},{20,4},{24,8},{28,12},{1,17},{... | collective-permute-start | bytes 49160 | tf_op jit(solution)/shard_map/ppermute | solution.py:19
  31.1 1.9 %collective-permute-done.4 = f32[2,16,128]{2,1,0:T(8,128)S(1)} collective-permute-done((f32[2,16,128]{2,1,0:T(8,128)S(1)}, f32[2,16,128]{2,1,0:T(8,128)S(1)}, u32[]{:S(2)}, u32[]{:S(2)}) %collective-permute-start.4) | collective-permute-done | bytes 16416 | tf_op jit(solution)/shard_map/ppermute | solution.py:19
  33.4 0.6 convolution_multiply_fusion.3
  34.0 0.8 fusion.25
  35.1 1.5 %fusion.12 = f32[48,2048]{1,0:T(8,128)S(1)} fusion(pred[4,512,2048]{2,1,0:T(32,128)(4,1)S(1)} %iota_compare_fusion, bf16[2,16,512]{2,1,0:T(8,128)(2,1)S(1)} %get-tuple-element.92, bf16[2,16,512]{2,1,0:T(8,128)(2,1)S(1)} %get-tuple-element.93, bf16[2,16,512]{2,1,0:T(8,128)(2,1)S(1)} %get-tuple-element.91), kind=kOutput, calls=%fused_computation.18 | convolution fusion | flops 201621504 | bytes 2588672 | tf_op jit(solution)/shard_map/gci,gip->cp/dot_general | solution.py:55
  36.7 1.8 %collective-permute-done.5 = f32[16]{0:T(128)S(1)} collective-permute-done((f32[16]{0:T(128)S(1)}, f32[16]{0:T(128)S(1)}, u32[]{:S(2)}, u32[]{:S(2)}) %collective-permute-start.5) | collective-permute-done | bytes 96 | tf_op jit(solution)/shard_map/ppermute | solution.py:19
  38.6 2.6 %collective-permute-start.6 = (f32[16]{0:T(128)S(1)}, f32[16]{0:T(128)S(1)}, u32[]{:S(2)}, u32[]{:S(2)}) collective-permute-start(f32[16]{0:T(128)S(1)} %add.193), channel_id=1, source_target_pairs={{0,2},{1,3},{2,0},{3,1},{4,6},{5,7},{6,4},{7,5},{8,10},{9,11},{10,... | collective-permute-start | bytes 200 | tf_op jit(solution)/shard_map/ppermute | solution.py:19
  41.2 1.5 %fusion.18 = f32[48,2048]{1,0:T(8,128)S(1)} fusion(pred[4,512,2048]{2,1,0:T(32,128)(4,1)S(1)} %iota_compare_fusion, bf16[2,16,512]{2,1,0:T(8,128)(2,1)S(1)} %get-tuple-element.89, bf16[2,16,512]{2,1,0:T(8,128)(2,1)S(1)} %get-tuple-element.90, bf16[2,16,512]{2,1,0:T(8,128)(2,1)S(1)} %get-tuple-element.88), kind=kOutput, calls=%fused_computation.20 | convolution fusion | flops 201621504 | bytes 2588672 | tf_op jit(solution)/shard_map/gci,gip->cp/dot_general | solution.py:55
  43.0 1.2 %convolution_bitcast_fusion = f32[5,16,128]{2,1,0:T(8,128)S(1)} fusion(f32[128,2048]{1,0:T(8,128)S(1)} %copy-done, f32[2048,16]{0,1:T(8,128)S(1)} %add_bitcast_fusion, f32[2048,5]{0,1:T(8,128)S(1)} %bitcast.64), kind=kOutput, calls=%fused_computation.26 | convolution fusion | flops 251822080 | bytes 1261568 | tf_op jit(solution)/shard_map/lp,cp,rp->lcr/dot_general | solution.py:107
  44.2 1.9 %collective-permute-start.8 = (f32[16]{0:T(128)S(1)}, f32[16]{0:T(128)S(1)}, u32[]{:S(2)}, u32[]{:S(2)}) collective-permute-start(f32[16]{0:T(128)S(1)} %add.201), channel_id=1, source_target_pairs={{0,8},{4,12},{8,0},{12,4},{16,24},{20,28},{24,16},{28,20},{1,9},{5... | collective-permute-start | bytes 200 | tf_op jit(solution)/shard_map/ppermute | solution.py:19
  46.1 1.7 %collective-permute-done.8 = f32[16]{0:T(128)S(1)} collective-permute-done((f32[16]{0:T(128)S(1)}, f32[16]{0:T(128)S(1)}, u32[]{:S(2)}, u32[]{:S(2)}) %collective-permute-start.8) | collective-permute-done | bytes 96 | tf_op jit(solution)/shard_map/ppermute | solution.py:19
  47.9 1.8 %collective-permute-start.9 = (f32[16]{0:T(128)S(1)}, f32[16]{0:T(128)S(1)}, u32[]{:S(2)}, u32[]{:S(2)}) collective-permute-start(f32[16]{0:T(128)S(1)} %add.204), channel_id=1, source_target_pairs={{0,16},{4,20},{8,24},{12,28},{16,0},{20,4},{24,8},{28,12},{1,17},{... | collective-permute-start | bytes 200 | tf_op jit(solution)/shard_map/ppermute | solution.py:19
  49.8 1.6 %collective-permute-done.9 = f32[16]{0:T(128)S(1)} collective-permute-done((f32[16]{0:T(128)S(1)}, f32[16]{0:T(128)S(1)}, u32[]{:S(2)}, u32[]{:S(2)}) %collective-permute-start.9) | collective-permute-done | bytes 96 | tf_op jit(solution)/shard_map/ppermute | solution.py:19
  52.1 3.8 %collective-permute-done.10 = f32[6,16,128]{2,1,0:T(8,128)S(1)} collective-permute-done((f32[6,16,128]{2,1,0:T(8,128)S(1)}, f32[6,16,128]{2,1,0:T(8,128)S(1)}, u32[]{:S(2)}, u32[]{:S(2)}) %collective-permute-start.10) | collective-permute-done | bytes 49184 | tf_op jit(solution)/shard_map/ppermute | solution.py:19
  55.9 2.7 %collective-permute-start.11 = (f32[5,16,128]{2,1,0:T(8,128)S(1)}, f32[5,16,128]{2,1,0:T(8,128)S(1)}, u32[]{:S(2)}, u32[]{:S(2)}) collective-permute-start(f32[5,16,128]{2,1,0:T(8,128)S(1)} %slice.225), channel_id=1, source_target_pairs={{0,2},{1,3},{2,0},{3,1},{4,6},{5,7},{6,4},{7,5},{8,10},{9,11},{10,... | collective-permute-start | bytes 122888 | tf_op jit(solution)/shard_map/ppermute | solution.py:19
  58.6 2.5 %collective-permute-done.11 = f32[5,16,128]{2,1,0:T(8,128)S(1)} collective-permute-done((f32[5,16,128]{2,1,0:T(8,128)S(1)}, f32[5,16,128]{2,1,0:T(8,128)S(1)}, u32[]{:S(2)}, u32[]{:S(2)}) %collective-permute-start.11) | collective-permute-done | bytes 40992 | tf_op jit(solution)/shard_map/ppermute | solution.py:19
  61.1 1.2 %collective-permute-done.12 = f32[4,16,128]{2,1,0:T(8,128)S(1)} collective-permute-done((f32[4,16,128]{2,1,0:T(8,128)S(1)}, f32[4,16,128]{2,1,0:T(8,128)S(1)}, u32[]{:S(2)}, u32[]{:S(2)}) %collective-permute-start.12) | collective-permute-done | bytes 32800 | tf_op jit(solution)/shard_map/ppermute | solution.py:19
  62.3 1.8 %collective-permute-start.13 = (f32[3,16,128]{2,1,0:T(8,128)S(1)}, f32[3,16,128]{2,1,0:T(8,128)S(1)}, u32[]{:S(2)}, u32[]{:S(2)}) collective-permute-start(f32[3,16,128]{2,1,0:T(8,128)S(1)} %slice.227), channel_id=1, source_target_pairs={{0,8},{4,12},{8,0},{12,4},{16,24},{20,28},{24,16},{28,20},{1,9},{5... | collective-permute-start | bytes 73736 | tf_op jit(solution)/shard_map/ppermute | solution.py:19
  64.1 3.5 %fusion.27 = f32[4,48,512]{2,1,0:T(8,128)S(1)} fusion(s32[4,512]{1,0:T(4,128)S(1)} %pad_add_fusion, bf16[16,2048]{1,0:T(8,128)(2,1)S(1)} %get-tuple-element.86, bf16[16,2048]{1,0:T(8,128)(2,1)S(1)} %get-tuple-element.85, bf16[16,2048]{1,0:T(8,128)(2,1)S(1)} %get-tuple-element.66), kind=kOutput, calls=%fused_computation.25 | convolution fusion | flops 407437312 | bytes 598016 | tf_op jit(solution)/shard_map/cp,gip->gci/dot_general | solution.py:49
  67.6 1.6 %collective-permute-start.14 = (f32[2,16,128]{2,1,0:T(8,128)S(1)}, f32[2,16,128]{2,1,0:T(8,128)S(1)}, u32[]{:S(2)}, u32[]{:S(2)}) collective-permute-start(f32[2,16,128]{2,1,0:T(8,128)S(1)} %slice.228), channel_id=1, source_target_pairs={{0,16},{4,20},{8,24},{12,28},{16,0},{20,4},{24,8},{28,12},{1,17},{... | collective-permute-start | bytes 49160 | tf_op jit(solution)/shard_map/ppermute | solution.py:19
  69.2 1.9 %fusion.95 = f32[4,16,512]{2,1,0:T(8,128)S(1)} fusion(f32[4,512,512]{2,1,0:T(8,128)S(1)} %exponential_multiply_fusion, f32[4,48,512]{2,1,0:T(8,128)S(1)} %fusion.27), kind=kOutput, calls=%fused_computation.205 | convolution fusion | flops 100728832 | bytes 4718592 | tf_op jit(solution)/shard_map/gij,gcj->gci/dot_general | solution.py:40
  72.2 0.6 convolution_multiply_fusion.2
  72.8 0.8 fusion.26
  74.0 1.5 %fusion.15 = f32[48,2048]{1,0:T(8,128)S(1)} fusion(pred[4,512,2048]{2,1,0:T(32,128)(4,1)S(1)} %iota_compare_fusion, bf16[2,16,512]{2,1,0:T(8,128)(2,1)S(1)} %get-tuple-element.83, bf16[2,16,512]{2,1,0:T(8,128)(2,1)S(1)} %get-tuple-element.84, bf16[2,16,512]{2,1,0:T(8,128)(2,1)S(1)} %get-tuple-element.82), kind=kOutput, calls=%fused_computation.19 | convolution fusion | flops 201621504 | bytes 2588672 | tf_op jit(solution)/shard_map/gci,gip->cp/dot_general | solution.py:55
  75.6 1.9 %collective-permute-done.15 = f32[16]{0:T(128)S(1)} collective-permute-done((f32[16]{0:T(128)S(1)}, f32[16]{0:T(128)S(1)}, u32[]{:S(2)}, u32[]{:S(2)}) %collective-permute-start.15) | collective-permute-done | bytes 96 | tf_op jit(solution)/shard_map/ppermute | solution.py:19
  77.4 2.2 %collective-permute-start.16 = (f32[16]{0:T(128)S(1)}, f32[16]{0:T(128)S(1)}, u32[]{:S(2)}, u32[]{:S(2)}) collective-permute-start(f32[16]{0:T(128)S(1)} %add.220), channel_id=1, source_target_pairs={{0,2},{1,3},{2,0},{3,1},{4,6},{5,7},{6,4},{7,5},{8,10},{9,11},{10,... | collective-permute-start | bytes 200 | tf_op jit(solution)/shard_map/ppermute | solution.py:19
  79.7 1.5 %fusion.21 = f32[48,2048]{1,0:T(8,128)S(1)} fusion(pred[4,512,2048]{2,1,0:T(32,128)(4,1)S(1)} %iota_compare_fusion, bf16[2,16,512]{2,1,0:T(8,128)(2,1)S(1)} %get-tuple-element.80, bf16[2,16,512]{2,1,0:T(8,128)(2,1)S(1)} %get-tuple-element.81, bf16[2,16,512]{2,1,0:T(8,128)(2,1)S(1)} %get-tuple-element.79), kind=kOutput, calls=%fused_computation.21 | convolution fusion | flops 201621504 | bytes 2588672 | tf_op jit(solution)/shard_map/gci,gip->cp/dot_general | solution.py:55
  81.2 0.7 collective-permute-done.16
  81.9 1.1 %collective-permute-done.17 = f32[16]{0:T(128)S(1)} collective-permute-done((f32[16]{0:T(128)S(1)}, f32[16]{0:T(128)S(1)}, u32[]{:S(2)}, u32[]{:S(2)}) %collective-permute-start.17) | collective-permute-done | bytes 96 | tf_op jit(solution)/shard_map/ppermute | solution.py:19
  83.3 3.2 %collective-permute-done.18 = f32[16]{0:T(128)S(1)} collective-permute-done((f32[16]{0:T(128)S(1)}, f32[16]{0:T(128)S(1)}, u32[]{:S(2)}, u32[]{:S(2)}) %collective-permute-start.18) | collective-permute-done | bytes 96 | tf_op jit(solution)/shard_map/ppermute | solution.py:19
  86.6 1.5 %collective-permute-start.19 = (f32[16]{0:T(128)S(1)}, f32[16]{0:T(128)S(1)}, u32[]{:S(2)}, u32[]{:S(2)}) collective-permute-start(f32[16]{0:T(128)S(1)} %add.229), channel_id=1, source_target_pairs={{0,16},{4,20},{8,24},{12,28},{16,0},{20,4},{24,8},{28,12},{1,17},{... | collective-permute-start | bytes 200 | tf_op jit(solution)/shard_map/ppermute | solution.py:19
  88.1 2.0 %collective-permute-done.19 = f32[16]{0:T(128)S(1)} collective-permute-done((f32[16]{0:T(128)S(1)}, f32[16]{0:T(128)S(1)}, u32[]{:S(2)}, u32[]{:S(2)}) %collective-permute-start.19) | collective-permute-done | bytes 96 | tf_op jit(solution)/shard_map/ppermute | solution.py:19
  90.1 0.8 multiply_subtract_fusion
  (104 shorter events, 5.9 us)
Async XLA Ops:
  0.6 2.0 %copy-start = (f32[128,2048]{1,0:T(8,128)S(1)}, f32[128,2048]{1,0:T(8,128)}, u32[]{:S(2)}) copy-start(f32[128,2048]{1,0:T(8,128)} %param.13) | copy-start | bytes 3145732
  4.8 10.5 %copy-start.5 = (f32[8]{0:T(128)S(1)}, f32[8]{0:T(128)}, u32[]{:S(2)}) copy-start(f32[8]{0:T(128)} %param.10) | copy-start | bytes 100
  4.8 13.6 %collective-permute-start = (f32[6,16,128]{2,1,0:T(8,128)S(1)}, f32[6,16,128]{2,1,0:T(8,128)S(1)}, u32[]{:S(2)}, u32[]{:S(2)}) collective-permute-start(f32[6,16,128]{2,1,0:T(8,128)S(1)} %pad_maximum_fusion), channel_id=1, source_target_pairs={{0,1},{1,0},{2,3},{3,2},{4,5},{5,4},{6,7},{7,6},{8,9},{9,8},{10,11... | collective-permute-start | bytes 147464 | tf_op jit(solution)/shard_map/ppermute | solution.py:19
  18.4 5.0 %collective-permute-start.1 = (f32[5,16,128]{2,1,0:T(8,128)S(1)}, f32[5,16,128]{2,1,0:T(8,128)S(1)}, u32[]{:S(2)}, u32[]{:S(2)}) collective-permute-start(f32[5,16,128]{2,1,0:T(8,128)S(1)} %slice.206), channel_id=1, source_target_pairs={{0,2},{1,3},{2,0},{3,1},{4,6},{5,7},{6,4},{7,5},{8,10},{9,11},{10,... | collective-permute-start | bytes 122888 | tf_op jit(solution)/shard_map/ppermute | solution.py:19
  22.7 10.3 %copy-start.2 = (f32[5,128,128]{2,1,0:T(8,128)S(1)}, f32[5,128,128]{2,1,0:T(8,128)}, u32[]{:S(2)}) copy-start(f32[5,128,128]{2,1,0:T(8,128)} %param.15) | copy-start | bytes 983044
  22.7 11.3 %copy-start.3 = (f32[5,2048]{1,0:T(8,128)S(1)}, f32[5,2048]{1,0:T(8,128)}, u32[]{:S(2)}) copy-start(f32[5,2048]{1,0:T(8,128)} %param.14) | copy-start | bytes 122884
  22.7 12.1 %copy-start.1 = (f32[16,2048]{1,0:T(8,128)S(1)}, f32[16,2048]{1,0:T(8,128)}, u32[]{:S(2)}) copy-start(f32[16,2048]{1,0:T(8,128)} %param.12) | copy-start | bytes 393220
  22.7 12.0 %copy-start.4 = (f32[2048]{0:T(1024)S(1)}, f32[2048]{0:T(1024)}, u32[]{:S(2)}) copy-start(f32[2048]{0:T(1024)} %param.11) | copy-start | bytes 24580
  23.4 1.8 %collective-permute-start.2 = (f32[4,16,128]{2,1,0:T(8,128)S(1)}, f32[4,16,128]{2,1,0:T(8,128)S(1)}, u32[]{:S(2)}, u32[]{:S(2)}) collective-permute-start(f32[4,16,128]{2,1,0:T(8,128)S(1)} %slice.207), channel_id=1, source_target_pairs={{0,4},{4,0},{8,12},{12,8},{16,20},{20,16},{24,28},{28,24},{1,5},{5... | collective-permute-start | bytes 98312 | tf_op jit(solution)/shard_map/ppermute | solution.py:19
  25.3 3.9 %collective-permute-start.3 = (f32[3,16,128]{2,1,0:T(8,128)S(1)}, f32[3,16,128]{2,1,0:T(8,128)S(1)}, u32[]{:S(2)}, u32[]{:S(2)}) collective-permute-start(f32[3,16,128]{2,1,0:T(8,128)S(1)} %slice.208), channel_id=1, source_target_pairs={{0,8},{4,12},{8,0},{12,4},{16,24},{20,28},{24,16},{28,20},{1,9},{5... | collective-permute-start | bytes 73736 | tf_op jit(solution)/shard_map/ppermute | solution.py:19
  29.2 3.8 %collective-permute-start.4 = (f32[2,16,128]{2,1,0:T(8,128)S(1)}, f32[2,16,128]{2,1,0:T(8,128)S(1)}, u32[]{:S(2)}, u32[]{:S(2)}) collective-permute-start(f32[2,16,128]{2,1,0:T(8,128)S(1)} %slice.209), channel_id=1, source_target_pairs={{0,16},{4,20},{8,24},{12,28},{16,0},{20,4},{24,8},{28,12},{1,17},{... | collective-permute-start | bytes 49160 | tf_op jit(solution)/shard_map/ppermute | solution.py:19
  34.9 3.6 %collective-permute-start.5 = (f32[16]{0:T(128)S(1)}, f32[16]{0:T(128)S(1)}, u32[]{:S(2)}, u32[]{:S(2)}) collective-permute-start(f32[16]{0:T(128)S(1)} %add.192), channel_id=1, source_target_pairs={{0,1},{1,0},{2,3},{3,2},{4,5},{5,4},{6,7},{7,6},{8,9},{9,8},{10,11... | collective-permute-start | bytes 200 | tf_op jit(solution)/shard_map/ppermute | solution.py:19
  38.6 4.4 %collective-permute-start.6 = (f32[16]{0:T(128)S(1)}, f32[16]{0:T(128)S(1)}, u32[]{:S(2)}, u32[]{:S(2)}) collective-permute-start(f32[16]{0:T(128)S(1)} %add.193), channel_id=1, source_target_pairs={{0,2},{1,3},{2,0},{3,1},{4,6},{5,7},{6,4},{7,5},{8,10},{9,11},{10,... | collective-permute-start | bytes 200 | tf_op jit(solution)/shard_map/ppermute | solution.py:19
  43.0 1.2 %collective-permute-start.7 = (f32[16]{0:T(128)S(1)}, f32[16]{0:T(128)S(1)}, u32[]{:S(2)}, u32[]{:S(2)}) collective-permute-start(f32[16]{0:T(128)S(1)} %add.197), channel_id=1, source_target_pairs={{0,4},{4,0},{8,12},{12,8},{16,20},{20,16},{24,28},{28,24},{1,5},{5... | collective-permute-start | bytes 200 | tf_op jit(solution)/shard_map/ppermute | solution.py:19
  44.2 3.6 %collective-permute-start.8 = (f32[16]{0:T(128)S(1)}, f32[16]{0:T(128)S(1)}, u32[]{:S(2)}, u32[]{:S(2)}) collective-permute-start(f32[16]{0:T(128)S(1)} %add.201), channel_id=1, source_target_pairs={{0,8},{4,12},{8,0},{12,4},{16,24},{20,28},{24,16},{28,20},{1,9},{5... | collective-permute-start | bytes 200 | tf_op jit(solution)/shard_map/ppermute | solution.py:19
  47.9 3.5 %collective-permute-start.9 = (f32[16]{0:T(128)S(1)}, f32[16]{0:T(128)S(1)}, u32[]{:S(2)}, u32[]{:S(2)}) collective-permute-start(f32[16]{0:T(128)S(1)} %add.204), channel_id=1, source_target_pairs={{0,16},{4,20},{8,24},{12,28},{16,0},{20,4},{24,8},{28,12},{1,17},{... | collective-permute-start | bytes 200 | tf_op jit(solution)/shard_map/ppermute | solution.py:19
  51.8 4.1 %collective-permute-start.10 = (f32[6,16,128]{2,1,0:T(8,128)S(1)}, f32[6,16,128]{2,1,0:T(8,128)S(1)}, u32[]{:S(2)}, u32[]{:S(2)}) collective-permute-start(f32[6,16,128]{2,1,0:T(8,128)S(1)} %pad_maximum_fusion.1), channel_id=1, source_target_pairs={{0,1},{1,0},{2,3},{3,2},{4,5},{5,4},{6,7},{7,6},{8,9},{9,8},{10,11... | collective-permute-start | bytes 147464 | tf_op jit(solution)/shard_map/ppermute | solution.py:19
  55.9 5.1 %collective-permute-start.11 = (f32[5,16,128]{2,1,0:T(8,128)S(1)}, f32[5,16,128]{2,1,0:T(8,128)S(1)}, u32[]{:S(2)}, u32[]{:S(2)}) collective-permute-start(f32[5,16,128]{2,1,0:T(8,128)S(1)} %slice.225), channel_id=1, source_target_pairs={{0,2},{1,3},{2,0},{3,1},{4,6},{5,7},{6,4},{7,5},{8,10},{9,11},{10,... | collective-permute-start | bytes 122888 | tf_op jit(solution)/shard_map/ppermute | solution.py:19
  61.1 1.3 %collective-permute-start.12 = (f32[4,16,128]{2,1,0:T(8,128)S(1)}, f32[4,16,128]{2,1,0:T(8,128)S(1)}, u32[]{:S(2)}, u32[]{:S(2)}) collective-permute-start(f32[4,16,128]{2,1,0:T(8,128)S(1)} %slice.226), channel_id=1, source_target_pairs={{0,4},{4,0},{8,12},{12,8},{16,20},{20,16},{24,28},{28,24},{1,5},{5... | collective-permute-start | bytes 98312 | tf_op jit(solution)/shard_map/ppermute | solution.py:19
  62.3 5.3 %collective-permute-start.13 = (f32[3,16,128]{2,1,0:T(8,128)S(1)}, f32[3,16,128]{2,1,0:T(8,128)S(1)}, u32[]{:S(2)}, u32[]{:S(2)}) collective-permute-start(f32[3,16,128]{2,1,0:T(8,128)S(1)} %slice.227), channel_id=1, source_target_pairs={{0,8},{4,12},{8,0},{12,4},{16,24},{20,28},{24,16},{28,20},{1,9},{5... | collective-permute-start | bytes 73736 | tf_op jit(solution)/shard_map/ppermute | solution.py:19
  67.6 3.8 %collective-permute-start.14 = (f32[2,16,128]{2,1,0:T(8,128)S(1)}, f32[2,16,128]{2,1,0:T(8,128)S(1)}, u32[]{:S(2)}, u32[]{:S(2)}) collective-permute-start(f32[2,16,128]{2,1,0:T(8,128)S(1)} %slice.228), channel_id=1, source_target_pairs={{0,16},{4,20},{8,24},{12,28},{16,0},{20,4},{24,8},{28,12},{1,17},{... | collective-permute-start | bytes 49160 | tf_op jit(solution)/shard_map/ppermute | solution.py:19
  73.8 3.6 %collective-permute-start.15 = (f32[16]{0:T(128)S(1)}, f32[16]{0:T(128)S(1)}, u32[]{:S(2)}, u32[]{:S(2)}) collective-permute-start(f32[16]{0:T(128)S(1)} %add.219), channel_id=1, source_target_pairs={{0,1},{1,0},{2,3},{3,2},{4,5},{5,4},{6,7},{7,6},{8,9},{9,8},{10,11... | collective-permute-start | bytes 200 | tf_op jit(solution)/shard_map/ppermute | solution.py:19
  77.4 4.4 %collective-permute-start.16 = (f32[16]{0:T(128)S(1)}, f32[16]{0:T(128)S(1)}, u32[]{:S(2)}, u32[]{:S(2)}) collective-permute-start(f32[16]{0:T(128)S(1)} %add.220), channel_id=1, source_target_pairs={{0,2},{1,3},{2,0},{3,1},{4,6},{5,7},{6,4},{7,5},{8,10},{9,11},{10,... | collective-permute-start | bytes 200 | tf_op jit(solution)/shard_map/ppermute | solution.py:19
  81.9 1.1 %collective-permute-start.17 = (f32[16]{0:T(128)S(1)}, f32[16]{0:T(128)S(1)}, u32[]{:S(2)}, u32[]{:S(2)}) collective-permute-start(f32[16]{0:T(128)S(1)} %add.224), channel_id=1, source_target_pairs={{0,4},{4,0},{8,12},{12,8},{16,20},{20,16},{24,28},{28,24},{1,5},{5... | collective-permute-start | bytes 200 | tf_op jit(solution)/shard_map/ppermute | solution.py:19
  83.0 3.5 %collective-permute-start.18 = (f32[16]{0:T(128)S(1)}, f32[16]{0:T(128)S(1)}, u32[]{:S(2)}, u32[]{:S(2)}) collective-permute-start(f32[16]{0:T(128)S(1)} %add.228), channel_id=1, source_target_pairs={{0,8},{4,12},{8,0},{12,4},{16,24},{20,28},{24,16},{28,20},{1,9},{5... | collective-permute-start | bytes 200 | tf_op jit(solution)/shard_map/ppermute | solution.py:19
  86.6 3.5 %collective-permute-start.19 = (f32[16]{0:T(128)S(1)}, f32[16]{0:T(128)S(1)}, u32[]{:S(2)}, u32[]{:S(2)}) collective-permute-start(f32[16]{0:T(128)S(1)} %add.229), channel_id=1, source_target_pairs={{0,16},{4,20},{8,24},{12,28},{16,0},{20,4},{24,8},{28,12},{1,17},{... | collective-permute-start | bytes 200 | tf_op jit(solution)/shard_map/ppermute | solution.py:19

commit v12 on v11

--- a/solution.py
+++ b/solution.py
@@ -113,14 +113,16 @@
         return running[:levels], running[levels, :, 0]
 
     half = union_order.shape[0] // 2
+    hot_first = (union_order[:half, :, None] == position[None, None, :]).astype(jnp.bfloat16)
+    hot_second = (union_order[half:, :, None] == position[None, None, :]).astype(jnp.bfloat16)
 
     def unpermute_first(state):
         late, near, extra = state
-        return late, from_union(late[:half], hot[:half]) + extra, extra
+        return late, from_union(late[:half], hot_first) + extra, extra
 
     def unpermute_second(state):
         late, near, extra = state
-        return late, near + from_union(late[half:], hot[half:]), extra
+        return late, near + from_union(late[half:], hot_second), extra
 
     solution = jnp.zeros_like(right_side)
     residual = right_side

time: 91.2 us -> 89.9 us (0.986)
  other arithmetic: 8.59 us -> 5.92 us
  matrix products: 25.1 us -> 26.4 us
    eq x1 -> x0, other arithmetic: 2.65 us -> none  [per_device(): union_order[:, :, None] == position[None, None, :]]
    dot_general x4, matrix products: 5.96 us -> 7.26 us  [from_union(): jnp.einsum('gci,gip->cp', pieces(values_u, 1), hot, preferred_element_typ...]
  transfers between devices with their start and end apart: 20 -> 20, of which waited for: 16 -> 16; matrix products, arithmetic and copies ran while one was open for 29% -> 28% of each run, Pallas kernels for 0% -> 0%
where the time goes in v12:
time: 89.9 us; the launch traced here: 89.7 us
  waiting for transfers between devices  27 us (30%)
  matrix products  26.4 us (29%)
  starting transfers between devices  26.3 us (29%)
  other arithmetic  5.92 us (7%)
  local copies, waits for them, and re-layouts  2.99 us (3%)
  between operations  1.08 us (1%)
    ppermute x20, waiting for transfers between devices, swapped(): return lax.ppermute(value, axis, pairs)  27 us
    ppermute x20, starting transfers between devices, swapped(): return lax.ppermute(value, axis, pairs)  26.3 us
    dot_general x4, matrix products, from_union(): jnp.einsum('gci,gip->cp', pieces(values_u, 1), hot, preferred_element_typ...  7.26 us
    dot_general x2, matrix products, to_union(): jnp.einsum('cp,gip->gci', pieces(values, 0), hot, preferred_element_type=...  6.98 us
    dot_general x2, matrix products, near_apply(): jnp.einsum('gij,gcj->gci', kern, union_vec, precision=lax.Precision.HIGH)  3.68 us
    dot_general x2, matrix products, project(): jnp.einsum('lp,cp,rp->lcr', level_gain, values, basis, precision=highest)  3.32 us
  transfers between devices with their start and end apart: 20, of which 16 were waited for; matrix products, arithmetic and copies ran while one was open for 28% of the time, Pallas kernels for 0%

profile of v12, /device:TPU:0, one launch (start us, length us, event | category | flops | bytes accessed | tf_op | source)
XLA Modules:
  0.0 89.7 jit_solution(11404762154333893834)
XLA Ops:
  0.6 0.9 %constant_dynamic-update-slice_fusion.3 = f32[24,2048]{1,0:T(8,128)S(1)} fusion(f32[8,2048]{1,0:T(8,128)} %param.9), kind=kLoop, calls=%fused_computation.159 | loop fusion | bytes 131072
  1.6 1.0 %multiply_reduce_fusion.5 = (f32[16]{0:T(128)S(1)}, f32[24,2048]{1,0:T(8,128)S(1)}) fusion(f32[16,2048]{1,0:T(8,128)} %param.12, f32[24,2048]{1,0:T(8,128)S(1)} %constant_dynamic-update-slice_fusion.3), kind=kLoop, calls=%fused_computation.92 | loop fusion | flops 65520 | bytes 262656 | tf_op jit(solution)/shard_map/reduce_sum | solution.py:110
  2.6 2.1 %convolution_bitcast_fusion.1 = f32[5,16,128]{2,1,0:T(8,128)S(1)} fusion(f32[128,2048]{1,0:T(8,128)S(1)} %copy-done, f32[2048,5]{0,1:T(8,128)} %bitcast.63, f32[2048,16]{0,1:T(8,128)} %bitcast.62), kind=kOutput, calls=%fused_computation.29 | convolution fusion | flops 251822080 | bytes 1261568 | tf_op jit(solution)/shard_map/lp,cp,rp->lcr/dot_general | solution.py:107
  4.8 3.1 %collective-permute-start = (f32[6,16,128]{2,1,0:T(8,128)S(1)}, f32[6,16,128]{2,1,0:T(8,128)S(1)}, u32[]{:S(2)}, u32[]{:S(2)}) collective-permute-start(f32[6,16,128]{2,1,0:T(8,128)S(1)} %pad_maximum_fusion), channel_id=1, source_target_pairs={{0,1},{1,0},{2,3},{3,2},{4,5},{5,4},{6,7},{7,6},{8,9},{9,8},{10,11... | collective-permute-start | bytes 147464 | tf_op jit(solution)/shard_map/ppermute | solution.py:19
  7.9 0.8 fusion.78
  9.2 1.4 %reduce.9 = s32[2048]{0:T(1024)S(1)} reduce(s32[1,2048]{1,0:T(1,128)} %param.16, s32[]{:T(128)} %broadcast.132), dimensions={0}, to_apply=%param.16.reduce_sub_computation.3 | reduce | bytes 16388 | tf_op args[7]
  10.6 0.6 gather_fusion.1
  11.8 3.5 %fusion.16 = f32[4,72,512]{2,1,0:T(8,128)S(1)} fusion(s32[4,512]{1,0:T(4,128)S(1)} %constant_dynamic-update-slice_fusion, bf16[24,2048]{1,0:T(8,128)(2,1)S(1)} %get-tuple-element.77, bf16[24,2048]{1,0:T(8,128)(2,1)S(1)} %get-tuple-element.78, bf16[24,2048]{1,0:T(8,128)(2,1)S(1)} %get-tuple-element.76), kind=kOutput, calls=%fused_computation.24 | convolution fusion | flops 609058816 | bytes 892928 | tf_op jit(solution)/shard_map/cp,gip->gci/dot_general | solution.py:49
  15.8 1.6 %exponential_multiply_fusion = f32[4,512,512]{2,1,0:T(8,128)S(1)} fusion(bf16[4,48,512]{2,1,0:T(8,128)(2,1)S(1)} %get-tuple-element.101, bf16[4,48,512]{2,1,0:T(8,128)(2,1)S(1)} %get-tuple-element.100, f32[4,512]{1,0:T(4,128)S(1)} %multiply_reduce_fusion.6), kind=kOutput, calls=%fused_computation.17 | convolution fusion | flops 105906176 | bytes 4595712 | tf_op jit(solution)/shard_map/gfi,gfj->gij/dot_general | solution.py:33
  17.5 2.7 %collective-permute-start.1 = (f32[5,16,128]{2,1,0:T(8,128)S(1)}, f32[5,16,128]{2,1,0:T(8,128)S(1)}, u32[]{:S(2)}, u32[]{:S(2)}) collective-permute-start(f32[5,16,128]{2,1,0:T(8,128)S(1)} %slice.204), channel_id=1, source_target_pairs={{0,2},{1,3},{2,0},{3,1},{4,6},{5,7},{6,4},{7,5},{8,10},{9,11},{10,... | collective-permute-start | bytes 122888 | tf_op jit(solution)/shard_map/ppermute | solution.py:19
  20.1 1.7 %fusion.46 = f32[4,16,512]{2,1,0:T(8,128)S(1)} fusion(f32[4,512,512]{2,1,0:T(8,128)S(1)} %exponential_multiply_fusion, f32[4,24,512]{2,1,0:T(8,128)S(1)} %slice_add_fusion), kind=kOutput, calls=%fused_computation.93 | convolution fusion | flops 100663296 | bytes 4456448 | tf_op jit(solution)/shard_map/gij,gcj->gci/dot_general | solution.py:40
  21.9 0.6 collective-permute-done.1
  22.5 1.2 %collective-permute-done.2 = f32[4,16,128]{2,1,0:T(8,128)S(1)} collective-permute-done((f32[4,16,128]{2,1,0:T(8,128)S(1)}, f32[4,16,128]{2,1,0:T(8,128)S(1)}, u32[]{:S(2)}, u32[]{:S(2)}) %collective-permute-start.2) | collective-permute-done | bytes 32800 | tf_op jit(solution)/shard_map/ppermute | solution.py:19
  23.7 1.9 %collective-permute-start.3 = (f32[3,16,128]{2,1,0:T(8,128)S(1)}, f32[3,16,128]{2,1,0:T(8,128)S(1)}, u32[]{:S(2)}, u32[]{:S(2)}) collective-permute-start(f32[3,16,128]{2,1,0:T(8,128)S(1)} %slice.206), channel_id=1, source_target_pairs={{0,8},{4,12},{8,0},{12,4},{16,24},{20,28},{24,16},{28,20},{1,9},{5... | collective-permute-start | bytes 73736 | tf_op jit(solution)/shard_map/ppermute | solution.py:19
  25.8 1.9 %collective-permute-done.3 = f32[3,16,128]{2,1,0:T(8,128)S(1)} collective-permute-done((f32[3,16,128]{2,1,0:T(8,128)S(1)}, f32[3,16,128]{2,1,0:T(8,128)S(1)}, u32[]{:S(2)}, u32[]{:S(2)}) %collective-permute-start.3) | collective-permute-done | bytes 24608 | tf_op jit(solution)/shard_map/ppermute | solution.py:19
  27.6 1.9 %collective-permute-start.4 = (f32[2,16,128]{2,1,0:T(8,128)S(1)}, f32[2,16,128]{2,1,0:T(8,128)S(1)}, u32[]{:S(2)}, u32[]{:S(2)}) collective-permute-start(f32[2,16,128]{2,1,0:T(8,128)S(1)} %slice.207), channel_id=1, source_target_pairs={{0,16},{4,20},{8,24},{12,28},{16,0},{20,4},{24,8},{28,12},{1,17},{... | collective-permute-start | bytes 49160 | tf_op jit(solution)/shard_map/ppermute | solution.py:19
  29.6 1.9 %collective-permute-done.4 = f32[2,16,128]{2,1,0:T(8,128)S(1)} collective-permute-done((f32[2,16,128]{2,1,0:T(8,128)S(1)}, f32[2,16,128]{2,1,0:T(8,128)S(1)}, u32[]{:S(2)}, u32[]{:S(2)}) %collective-permute-start.4) | collective-permute-done | bytes 16416 | tf_op jit(solution)/shard_map/ppermute | solution.py:19
  31.8 0.6 convolution_multiply_fusion.3
  32.5 0.8 fusion.17
  33.6 1.8 %fusion.12 = f32[48,2048]{1,0:T(8,128)S(1)} fusion(s32[2,512]{1,0:T(2,128)S(1)} %get-tuple-element.105, bf16[2,16,512]{2,1,0:T(8,128)(2,1)S(1)} %get-tuple-element.92, bf16[2,16,512]{2,1,0:T(8,128)(2,1)S(1)} %get-tuple-element.93, bf16[2,16,512]{2,1,0:T(8,128)(2,1)S(1)} %get-tuple-element.91), kind=kOutput, calls=%fused_computation.20 | convolution fusion | flops 203718656 | bytes 495616 | tf_op jit(solution)/shard_map/gci,gip->cp/dot_general | solution.py:55
  35.5 1.5 %collective-permute-done.5 = f32[16]{0:T(128)S(1)} collective-permute-done((f32[16]{0:T(128)S(1)}, f32[16]{0:T(128)S(1)}, u32[]{:S(2)}, u32[]{:S(2)}) %collective-permute-start.5) | collective-permute-done | bytes 96 | tf_op jit(solution)/shard_map/ppermute | solution.py:19
  37.0 2.6 %collective-permute-start.6 = (f32[16]{0:T(128)S(1)}, f32[16]{0:T(128)S(1)}, u32[]{:S(2)}, u32[]{:S(2)}) collective-permute-start(f32[16]{0:T(128)S(1)} %add.193), channel_id=1, source_target_pairs={{0,2},{1,3},{2,0},{3,1},{4,6},{5,7},{6,4},{7,5},{8,10},{9,11},{10,... | collective-permute-start | bytes 200 | tf_op jit(solution)/shard_map/ppermute | solution.py:19
  39.6 1.8 %fusion.14 = f32[48,2048]{1,0:T(8,128)S(1)} fusion(s32[2,512]{1,0:T(2,128)S(1)} %get-tuple-element.104, bf16[2,16,512]{2,1,0:T(8,128)(2,1)S(1)} %get-tuple-element.89, bf16[2,16,512]{2,1,0:T(8,128)(2,1)S(1)} %get-tuple-element.90, bf16[2,16,512]{2,1,0:T(8,128)(2,1)S(1)} %get-tuple-element.88), kind=kOutput, calls=%fused_computation.22 | convolution fusion | flops 203718656 | bytes 495616 | tf_op jit(solution)/shard_map/gci,gip->cp/dot_general | solution.py:55
  41.6 1.2 %convolution_bitcast_fusion = f32[5,16,128]{2,1,0:T(8,128)S(1)} fusion(f32[128,2048]{1,0:T(8,128)S(1)} %copy-done, f32[2048,16]{0,1:T(8,128)S(1)} %add_bitcast_fusion, f32[2048,5]{0,1:T(8,128)S(1)} %bitcast.64), kind=kOutput, calls=%fused_computation.28 | convolution fusion | flops 251822080 | bytes 1261568 | tf_op jit(solution)/shard_map/lp,cp,rp->lcr/dot_general | solution.py:107
  42.8 1.8 %collective-permute-start.8 = (f32[16]{0:T(128)S(1)}, f32[16]{0:T(128)S(1)}, u32[]{:S(2)}, u32[]{:S(2)}) collective-permute-start(f32[16]{0:T(128)S(1)} %add.201), channel_id=1, source_target_pairs={{0,8},{4,12},{8,0},{12,4},{16,24},{20,28},{24,16},{28,20},{1,9},{5... | collective-permute-start | bytes 200 | tf_op jit(solution)/shard_map/ppermute | solution.py:19
  44.6 1.8 %collective-permute-done.8 = f32[16]{0:T(128)S(1)} collective-permute-done((f32[16]{0:T(128)S(1)}, f32[16]{0:T(128)S(1)}, u32[]{:S(2)}, u32[]{:S(2)}) %collective-permute-start.8) | collective-permute-done | bytes 96 | tf_op jit(solution)/shard_map/ppermute | solution.py:19
  46.4 1.7 %collective-permute-start.9 = (f32[16]{0:T(128)S(1)}, f32[16]{0:T(128)S(1)}, u32[]{:S(2)}, u32[]{:S(2)}) collective-permute-start(f32[16]{0:T(128)S(1)} %add.204), channel_id=1, source_target_pairs={{0,16},{4,20},{8,24},{12,28},{16,0},{20,4},{24,8},{28,12},{1,17},{... | collective-permute-start | bytes 200 | tf_op jit(solution)/shard_map/ppermute | solution.py:19
  48.3 1.7 %collective-permute-done.9 = f32[16]{0:T(128)S(1)} collective-permute-done((f32[16]{0:T(128)S(1)}, f32[16]{0:T(128)S(1)}, u32[]{:S(2)}, u32[]{:S(2)}) %collective-permute-start.9) | collective-permute-done | bytes 96 | tf_op jit(solution)/shard_map/ppermute | solution.py:19
  50.9 3.6 %collective-permute-done.10 = f32[6,16,128]{2,1,0:T(8,128)S(1)} collective-permute-done((f32[6,16,128]{2,1,0:T(8,128)S(1)}, f32[6,16,128]{2,1,0:T(8,128)S(1)}, u32[]{:S(2)}, u32[]{:S(2)}) %collective-permute-start.10) | collective-permute-done | bytes 49184 | tf_op jit(solution)/shard_map/ppermute | solution.py:19
  54.5 2.5 %collective-permute-start.11 = (f32[5,16,128]{2,1,0:T(8,128)S(1)}, f32[5,16,128]{2,1,0:T(8,128)S(1)}, u32[]{:S(2)}, u32[]{:S(2)}) collective-permute-start(f32[5,16,128]{2,1,0:T(8,128)S(1)} %slice.223), channel_id=1, source_target_pairs={{0,2},{1,3},{2,0},{3,1},{4,6},{5,7},{6,4},{7,5},{8,10},{9,11},{10,... | collective-permute-start | bytes 122888 | tf_op jit(solution)/shard_map/ppermute | solution.py:19
  57.0 2.8 %collective-permute-done.11 = f32[5,16,128]{2,1,0:T(8,128)S(1)} collective-permute-done((f32[5,16,128]{2,1,0:T(8,128)S(1)}, f32[5,16,128]{2,1,0:T(8,128)S(1)}, u32[]{:S(2)}, u32[]{:S(2)}) %collective-permute-start.11) | collective-permute-done | bytes 40992 | tf_op jit(solution)/shard_map/ppermute | solution.py:19
  59.9 1.2 %collective-permute-done.12 = f32[4,16,128]{2,1,0:T(8,128)S(1)} collective-permute-done((f32[4,16,128]{2,1,0:T(8,128)S(1)}, f32[4,16,128]{2,1,0:T(8,128)S(1)}, u32[]{:S(2)}, u32[]{:S(2)}) %collective-permute-start.12) | collective-permute-done | bytes 32800 | tf_op jit(solution)/shard_map/ppermute | solution.py:19
  61.1 1.7 %collective-permute-start.13 = (f32[3,16,128]{2,1,0:T(8,128)S(1)}, f32[3,16,128]{2,1,0:T(8,128)S(1)}, u32[]{:S(2)}, u32[]{:S(2)}) collective-permute-start(f32[3,16,128]{2,1,0:T(8,128)S(1)} %slice.225), channel_id=1, source_target_pairs={{0,8},{4,12},{8,0},{12,4},{16,24},{20,28},{24,16},{28,20},{1,9},{5... | collective-permute-start | bytes 73736 | tf_op jit(solution)/shard_map/ppermute | solution.py:19
  62.9 3.5 %fusion.19 = f32[4,48,512]{2,1,0:T(8,128)S(1)} fusion(s32[4,512]{1,0:T(4,128)S(1)} %constant_dynamic-update-slice_fusion, bf16[16,2048]{1,0:T(8,128)(2,1)S(1)} %get-tuple-element.86, bf16[16,2048]{1,0:T(8,128)(2,1)S(1)} %get-tuple-element.85, bf16[16,2048]{1,0:T(8,128)(2,1)S(1)} %get-tuple-element.66), kind=kOutput, calls=%fused_computation.27 | convolution fusion | flops 407437312 | bytes 598016 | tf_op jit(solution)/shard_map/cp,gip->gci/dot_general | solution.py:49
  66.4 1.6 %collective-permute-start.14 = (f32[2,16,128]{2,1,0:T(8,128)S(1)}, f32[2,16,128]{2,1,0:T(8,128)S(1)}, u32[]{:S(2)}, u32[]{:S(2)}) collective-permute-start(f32[2,16,128]{2,1,0:T(8,128)S(1)} %slice.226), channel_id=1, source_target_pairs={{0,16},{4,20},{8,24},{12,28},{16,0},{20,4},{24,8},{28,12},{1,17},{... | collective-permute-start | bytes 49160 | tf_op jit(solution)/shard_map/ppermute | solution.py:19
  68.0 2.0 %fusion.87 = f32[4,16,512]{2,1,0:T(8,128)S(1)} fusion(f32[4,512,512]{2,1,0:T(8,128)S(1)} %exponential_multiply_fusion, f32[4,48,512]{2,1,0:T(8,128)S(1)} %fusion.19), kind=kOutput, calls=%fused_computation.208 | convolution fusion | flops 100728832 | bytes 4718592 | tf_op jit(solution)/shard_map/gij,gcj->gci/dot_general | solution.py:40
  71.0 0.6 convolution_multiply_fusion.2
  71.6 0.8 fusion.18
  72.8 1.8 %fusion.13 = f32[48,2048]{1,0:T(8,128)S(1)} fusion(s32[2,512]{1,0:T(2,128)S(1)} %get-tuple-element.105, bf16[2,16,512]{2,1,0:T(8,128)(2,1)S(1)} %get-tuple-element.83, bf16[2,16,512]{2,1,0:T(8,128)(2,1)S(1)} %get-tuple-element.84, bf16[2,16,512]{2,1,0:T(8,128)(2,1)S(1)} %get-tuple-element.82), kind=kOutput, calls=%fused_computation.21 | convolution fusion | flops 203718656 | bytes 495616 | tf_op jit(solution)/shard_map/gci,gip->cp/dot_general | solution.py:55
  74.7 1.5 %collective-permute-done.15 = f32[16]{0:T(128)S(1)} collective-permute-done((f32[16]{0:T(128)S(1)}, f32[16]{0:T(128)S(1)}, u32[]{:S(2)}, u32[]{:S(2)}) %collective-permute-start.15) | collective-permute-done | bytes 96 | tf_op jit(solution)/shard_map/ppermute | solution.py:19
  76.2 1.9 %collective-permute-start.16 = (f32[16]{0:T(128)S(1)}, f32[16]{0:T(128)S(1)}, u32[]{:S(2)}, u32[]{:S(2)}) collective-permute-start(f32[16]{0:T(128)S(1)} %add.220), channel_id=1, source_target_pairs={{0,2},{1,3},{2,0},{3,1},{4,6},{5,7},{6,4},{7,5},{8,10},{9,11},{10,... | collective-permute-start | bytes 200 | tf_op jit(solution)/shard_map/ppermute | solution.py:19
  78.1 1.8 %fusion.15 = f32[48,2048]{1,0:T(8,128)S(1)} fusion(s32[2,512]{1,0:T(2,128)S(1)} %get-tuple-element.104, bf16[2,16,512]{2,1,0:T(8,128)(2,1)S(1)} %get-tuple-element.80, bf16[2,16,512]{2,1,0:T(8,128)(2,1)S(1)} %get-tuple-element.81, bf16[2,16,512]{2,1,0:T(8,128)(2,1)S(1)} %get-tuple-element.79), kind=kOutput, calls=%fused_computation.23 | convolution fusion | flops 203718656 | bytes 495616 | tf_op jit(solution)/shard_map/gci,gip->cp/dot_general | solution.py:55
  80.0 0.7 collective-permute-done.16
  80.6 1.1 %collective-permute-done.17 = f32[16]{0:T(128)S(1)} collective-permute-done((f32[16]{0:T(128)S(1)}, f32[16]{0:T(128)S(1)}, u32[]{:S(2)}, u32[]{:S(2)}) %collective-permute-start.17) | collective-permute-done | bytes 96 | tf_op jit(solution)/shard_map/ppermute | solution.py:19
  82.1 3.2 %collective-permute-done.18 = f32[16]{0:T(128)S(1)} collective-permute-done((f32[16]{0:T(128)S(1)}, f32[16]{0:T(128)S(1)}, u32[]{:S(2)}, u32[]{:S(2)}) %collective-permute-start.18) | collective-permute-done | bytes 96 | tf_op jit(solution)/shard_map/ppermute | solution.py:19
  85.3 1.5 %collective-permute-start.19 = (f32[16]{0:T(128)S(1)}, f32[16]{0:T(128)S(1)}, u32[]{:S(2)}, u32[]{:S(2)}) collective-permute-start(f32[16]{0:T(128)S(1)} %add.229), channel_id=1, source_target_pairs={{0,16},{4,20},{8,24},{12,28},{16,0},{20,4},{24,8},{28,12},{1,17},{... | collective-permute-start | bytes 200 | tf_op jit(solution)/shard_map/ppermute | solution.py:19
  86.8 2.0 %collective-permute-done.19 = f32[16]{0:T(128)S(1)} collective-permute-done((f32[16]{0:T(128)S(1)}, f32[16]{0:T(128)S(1)}, u32[]{:S(2)}, u32[]{:S(2)}) %collective-permute-start.19) | collective-permute-done | bytes 96 | tf_op jit(solution)/shard_map/ppermute | solution.py:19
  88.9 0.8 multiply_subtract_fusion
  (105 shorter events, 6.0 us)
Async XLA Ops:
  0.6 2.0 %copy-start = (f32[128,2048]{1,0:T(8,128)S(1)}, f32[128,2048]{1,0:T(8,128)}, u32[]{:S(2)}) copy-start(f32[128,2048]{1,0:T(8,128)} %param.13) | copy-start | bytes 3145732
  4.8 10.5 %copy-start.5 = (f32[8]{0:T(128)S(1)}, f32[8]{0:T(128)}, u32[]{:S(2)}) copy-start(f32[8]{0:T(128)} %param.10) | copy-start | bytes 100
  4.8 12.6 %collective-permute-start = (f32[6,16,128]{2,1,0:T(8,128)S(1)}, f32[6,16,128]{2,1,0:T(8,128)S(1)}, u32[]{:S(2)}, u32[]{:S(2)}) collective-permute-start(f32[6,16,128]{2,1,0:T(8,128)S(1)} %pad_maximum_fusion), channel_id=1, source_target_pairs={{0,1},{1,0},{2,3},{3,2},{4,5},{5,4},{6,7},{7,6},{8,9},{9,8},{10,11... | collective-permute-start | bytes 147464 | tf_op jit(solution)/shard_map/ppermute | solution.py:19
  17.4 14.1 %copy-start.2 = (f32[5,128,128]{2,1,0:T(8,128)S(1)}, f32[5,128,128]{2,1,0:T(8,128)}, u32[]{:S(2)}) copy-start(f32[5,128,128]{2,1,0:T(8,128)} %param.15) | copy-start | bytes 983044
  17.4 15.1 %copy-start.3 = (f32[5,2048]{1,0:T(8,128)S(1)}, f32[5,2048]{1,0:T(8,128)}, u32[]{:S(2)}) copy-start(f32[5,2048]{1,0:T(8,128)} %param.14) | copy-start | bytes 122884
  17.4 15.8 %copy-start.1 = (f32[16,2048]{1,0:T(8,128)S(1)}, f32[16,2048]{1,0:T(8,128)}, u32[]{:S(2)}) copy-start(f32[16,2048]{1,0:T(8,128)} %param.12) | copy-start | bytes 393220
  17.4 15.8 %copy-start.4 = (f32[2048]{0:T(1024)S(1)}, f32[2048]{0:T(1024)}, u32[]{:S(2)}) copy-start(f32[2048]{0:T(1024)} %param.11) | copy-start | bytes 24580
  17.5 5.0 %collective-permute-start.1 = (f32[5,16,128]{2,1,0:T(8,128)S(1)}, f32[5,16,128]{2,1,0:T(8,128)S(1)}, u32[]{:S(2)}, u32[]{:S(2)}) collective-permute-start(f32[5,16,128]{2,1,0:T(8,128)S(1)} %slice.204), channel_id=1, source_target_pairs={{0,2},{1,3},{2,0},{3,1},{4,6},{5,7},{6,4},{7,5},{8,10},{9,11},{10,... | collective-permute-start | bytes 122888 | tf_op jit(solution)/shard_map/ppermute | solution.py:19
  22.4 1.3 %collective-permute-start.2 = (f32[4,16,128]{2,1,0:T(8,128)S(1)}, f32[4,16,128]{2,1,0:T(8,128)S(1)}, u32[]{:S(2)}, u32[]{:S(2)}) collective-permute-start(f32[4,16,128]{2,1,0:T(8,128)S(1)} %slice.205), channel_id=1, source_target_pairs={{0,4},{4,0},{8,12},{12,8},{16,20},{20,16},{24,28},{28,24},{1,5},{5... | collective-permute-start | bytes 98312 | tf_op jit(solution)/shard_map/ppermute | solution.py:19
  23.7 3.9 %collective-permute-start.3 = (f32[3,16,128]{2,1,0:T(8,128)S(1)}, f32[3,16,128]{2,1,0:T(8,128)S(1)}, u32[]{:S(2)}, u32[]{:S(2)}) collective-permute-start(f32[3,16,128]{2,1,0:T(8,128)S(1)} %slice.206), channel_id=1, source_target_pairs={{0,8},{4,12},{8,0},{12,4},{16,24},{20,28},{24,16},{28,20},{1,9},{5... | collective-permute-start | bytes 73736 | tf_op jit(solution)/shard_map/ppermute | solution.py:19
  27.6 3.8 %collective-permute-start.4 = (f32[2,16,128]{2,1,0:T(8,128)S(1)}, f32[2,16,128]{2,1,0:T(8,128)S(1)}, u32[]{:S(2)}, u32[]{:S(2)}) collective-permute-start(f32[2,16,128]{2,1,0:T(8,128)S(1)} %slice.207), channel_id=1, source_target_pairs={{0,16},{4,20},{8,24},{12,28},{16,0},{20,4},{24,8},{28,12},{1,17},{... | collective-permute-start | bytes 49160 | tf_op jit(solution)/shard_map/ppermute | solution.py:19
  33.4 3.6 %collective-permute-start.5 = (f32[16]{0:T(128)S(1)}, f32[16]{0:T(128)S(1)}, u32[]{:S(2)}, u32[]{:S(2)}) collective-permute-start(f32[16]{0:T(128)S(1)} %add.192), channel_id=1, source_target_pairs={{0,1},{1,0},{2,3},{3,2},{4,5},{5,4},{6,7},{7,6},{8,9},{9,8},{10,11... | collective-permute-start | bytes 200 | tf_op jit(solution)/shard_map/ppermute | solution.py:19
  37.0 4.5 %collective-permute-start.6 = (f32[16]{0:T(128)S(1)}, f32[16]{0:T(128)S(1)}, u32[]{:S(2)}, u32[]{:S(2)}) collective-permute-start(f32[16]{0:T(128)S(1)} %add.193), channel_id=1, source_target_pairs={{0,2},{1,3},{2,0},{3,1},{4,6},{5,7},{6,4},{7,5},{8,10},{9,11},{10,... | collective-permute-start | bytes 200 | tf_op jit(solution)/shard_map/ppermute | solution.py:19
  41.5 1.3 %collective-permute-start.7 = (f32[16]{0:T(128)S(1)}, f32[16]{0:T(128)S(1)}, u32[]{:S(2)}, u32[]{:S(2)}) collective-permute-start(f32[16]{0:T(128)S(1)} %add.197), channel_id=1, source_target_pairs={{0,4},{4,0},{8,12},{12,8},{16,20},{20,16},{24,28},{28,24},{1,5},{5... | collective-permute-start | bytes 200 | tf_op jit(solution)/shard_map/ppermute | solution.py:19
  42.8 3.6 %collective-permute-start.8 = (f32[16]{0:T(128)S(1)}, f32[16]{0:T(128)S(1)}, u32[]{:S(2)}, u32[]{:S(2)}) collective-permute-start(f32[16]{0:T(128)S(1)} %add.201), channel_id=1, source_target_pairs={{0,8},{4,12},{8,0},{12,4},{16,24},{20,28},{24,16},{28,20},{1,9},{5... | collective-permute-start | bytes 200 | tf_op jit(solution)/shard_map/ppermute | solution.py:19
  46.4 3.5 %collective-permute-start.9 = (f32[16]{0:T(128)S(1)}, f32[16]{0:T(128)S(1)}, u32[]{:S(2)}, u32[]{:S(2)}) collective-permute-start(f32[16]{0:T(128)S(1)} %add.204), channel_id=1, source_target_pairs={{0,16},{4,20},{8,24},{12,28},{16,0},{20,4},{24,8},{28,12},{1,17},{... | collective-permute-start | bytes 200 | tf_op jit(solution)/shard_map/ppermute | solution.py:19
  50.4 4.1 %collective-permute-start.10 = (f32[6,16,128]{2,1,0:T(8,128)S(1)}, f32[6,16,128]{2,1,0:T(8,128)S(1)}, u32[]{:S(2)}, u32[]{:S(2)}) collective-permute-start(f32[6,16,128]{2,1,0:T(8,128)S(1)} %pad_maximum_fusion.1), channel_id=1, source_target_pairs={{0,1},{1,0},{2,3},{3,2},{4,5},{5,4},{6,7},{7,6},{8,9},{9,8},{10,11... | collective-permute-start | bytes 147464 | tf_op jit(solution)/shard_map/ppermute | solution.py:19
  54.5 5.3 %collective-permute-start.11 = (f32[5,16,128]{2,1,0:T(8,128)S(1)}, f32[5,16,128]{2,1,0:T(8,128)S(1)}, u32[]{:S(2)}, u32[]{:S(2)}) collective-permute-start(f32[5,16,128]{2,1,0:T(8,128)S(1)} %slice.223), channel_id=1, source_target_pairs={{0,2},{1,3},{2,0},{3,1},{4,6},{5,7},{6,4},{7,5},{8,10},{9,11},{10,... | collective-permute-start | bytes 122888 | tf_op jit(solution)/shard_map/ppermute | solution.py:19
  59.8 1.3 %collective-permute-start.12 = (f32[4,16,128]{2,1,0:T(8,128)S(1)}, f32[4,16,128]{2,1,0:T(8,128)S(1)}, u32[]{:S(2)}, u32[]{:S(2)}) collective-permute-start(f32[4,16,128]{2,1,0:T(8,128)S(1)} %slice.224), channel_id=1, source_target_pairs={{0,4},{4,0},{8,12},{12,8},{16,20},{20,16},{24,28},{28,24},{1,5},{5... | collective-permute-start | bytes 98312 | tf_op jit(solution)/shard_map/ppermute | solution.py:19
  61.1 5.2 %collective-permute-start.13 = (f32[3,16,128]{2,1,0:T(8,128)S(1)}, f32[3,16,128]{2,1,0:T(8,128)S(1)}, u32[]{:S(2)}, u32[]{:S(2)}) collective-permute-start(f32[3,16,128]{2,1,0:T(8,128)S(1)} %slice.225), channel_id=1, source_target_pairs={{0,8},{4,12},{8,0},{12,4},{16,24},{20,28},{24,16},{28,20},{1,9},{5... | collective-permute-start | bytes 73736 | tf_op jit(solution)/shard_map/ppermute | solution.py:19
  66.4 3.8 %collective-permute-start.14 = (f32[2,16,128]{2,1,0:T(8,128)S(1)}, f32[2,16,128]{2,1,0:T(8,128)S(1)}, u32[]{:S(2)}, u32[]{:S(2)}) collective-permute-start(f32[2,16,128]{2,1,0:T(8,128)S(1)} %slice.226), channel_id=1, source_target_pairs={{0,16},{4,20},{8,24},{12,28},{16,0},{20,4},{24,8},{28,12},{1,17},{... | collective-permute-start | bytes 49160 | tf_op jit(solution)/shard_map/ppermute | solution.py:19
  72.6 3.6 %collective-permute-start.15 = (f32[16]{0:T(128)S(1)}, f32[16]{0:T(128)S(1)}, u32[]{:S(2)}, u32[]{:S(2)}) collective-permute-start(f32[16]{0:T(128)S(1)} %add.219), channel_id=1, source_target_pairs={{0,1},{1,0},{2,3},{3,2},{4,5},{5,4},{6,7},{7,6},{8,9},{9,8},{10,11... | collective-permute-start | bytes 200 | tf_op jit(solution)/shard_map/ppermute | solution.py:19
  76.2 4.4 %collective-permute-start.16 = (f32[16]{0:T(128)S(1)}, f32[16]{0:T(128)S(1)}, u32[]{:S(2)}, u32[]{:S(2)}) collective-permute-start(f32[16]{0:T(128)S(1)} %add.220), channel_id=1, source_target_pairs={{0,2},{1,3},{2,0},{3,1},{4,6},{5,7},{6,4},{7,5},{8,10},{9,11},{10,... | collective-permute-start | bytes 200 | tf_op jit(solution)/shard_map/ppermute | solution.py:19
  80.6 1.1 %collective-permute-start.17 = (f32[16]{0:T(128)S(1)}, f32[16]{0:T(128)S(1)}, u32[]{:S(2)}, u32[]{:S(2)}) collective-permute-start(f32[16]{0:T(128)S(1)} %add.224), channel_id=1, source_target_pairs={{0,4},{4,0},{8,12},{12,8},{16,20},{20,16},{24,28},{28,24},{1,5},{5... | collective-permute-start | bytes 200 | tf_op jit(solution)/shard_map/ppermute | solution.py:19
  81.8 3.5 %collective-permute-start.18 = (f32[16]{0:T(128)S(1)}, f32[16]{0:T(128)S(1)}, u32[]{:S(2)}, u32[]{:S(2)}) collective-permute-start(f32[16]{0:T(128)S(1)} %add.228), channel_id=1, source_target_pairs={{0,8},{4,12},{8,0},{12,4},{16,24},{20,28},{24,16},{28,20},{1,9},{5... | collective-permute-start | bytes 200 | tf_op jit(solution)/shard_map/ppermute | solution.py:19
  85.3 3.5 %collective-permute-start.19 = (f32[16]{0:T(128)S(1)}, f32[16]{0:T(128)S(1)}, u32[]{:S(2)}, u32[]{:S(2)}) collective-permute-start(f32[16]{0:T(128)S(1)} %add.229), channel_id=1, source_target_pairs={{0,16},{4,20},{8,24},{12,28},{16,0},{20,4},{24,8},{28,12},{1,17},{... | collective-permute-start | bytes 200 | tf_op jit(solution)/shard_map/ppermute | solution.py:19

commit v13 on v12

--- a/solution.py
+++ b/solution.py
@@ -56,18 +56,25 @@
     return (out[:count] + out[count : 2 * count]) + out[2 * count :]
 
 
-def tree_sums(proj):
+def tree_sums(proj, stages, state):
     low_count = lax.axis_size("gy").bit_length() - 1
     high_count = lax.axis_size("gx").bit_length() - 1
+    rounds = [("gy", bit, bit) for bit in range(low_count)]
+    rounds += [("gx", bit, low_count + bit) for bit in range(high_count)]
     running = proj
-    for bit in range(low_count):
-        partner = swapped(running[bit:], "gy", bit)
-        running = jnp.concatenate([running[:bit], running[bit:] + partner], axis=0)
-    for bit in range(high_count):
-        level = low_count + bit
-        partner = swapped(running[level:], "gx", bit)
+    for index, (axis, bit, level) in enumerate(rounds):
+        partner = swapped(running[level:], axis, bit)
+        stage = stages[index] if index < len(stages) else None
+        if stage is not None:
+            state, running = lax.optimization_barrier((state, running))
+            state = stage(state)
         running = jnp.concatenate([running[:level], running[level:] + partner], axis=0)
-    return running
+        if stage is not None:
+            running, state = lax.optimization_barrier((running, state))
+    for stage in stages[len(rounds) :]:
+        if stage is not None:
+            state = stage(state)
+    return running, state
 
 
 def butterfly(value, stages, state):
@@ -106,11 +113,24 @@
     def project(values):
         return jnp.einsum("lp,cp,rp->lcr", level_gain, values, basis, precision=highest)
 
-    def sums_with_norm(values, proj):
+    def sums_with_norm(values, proj, stages, state):
         norm = jnp.sum(values * values, axis=1)
         extra = jnp.broadcast_to(norm[None, :, None], (1, columns, rank))
-        running = tree_sums(jnp.concatenate([proj, extra], axis=0))
-        return running[:levels], running[levels, :, 0]
+        running, state = tree_sums(jnp.concatenate([proj, extra], axis=0), stages, state)
+        return running[:levels], running[levels, :, 0], state
+
+    def permute_first(state):
+        values, first, second = state
+        return values, to_union(values, hot_first), second
+
+    def permute_second(state):
+        values, first, second = state
+        return values, first, to_union(values, hot_second)
+
+    def near_of_halves(state):
+        values, first, second = state
+        values_u = jnp.concatenate([first, second], axis=0)
+        return values_u, near_of_union(values_u), second
 
     half = union_order.shape[0] // 2
     hot_first = (union_order[:half, :, None] == position[None, None, :]).astype(jnp.bfloat16)
@@ -131,14 +151,16 @@
     residual_proj = project(residual)
     for step in range(ITERATIONS):
         if step == 0:
-            nodesum, norm_now = sums_with_norm(residual, residual_proj)
+            nodesum, norm_now, unused = sums_with_norm(residual, residual_proj, [], ())
             near_u = near_of_union(direction_u)
             late_u, nodesum = lax.optimization_barrier((near_u, nodesum))
             carried = jnp.zeros_like(right_side)
         else:
-            residual_sum, norm_next = sums_with_norm(residual, residual_proj)
-            residual_u = to_union(residual, hot)
-            residual_near_u = near_of_union(residual_u)
+            empty = jnp.zeros((half,) + direction_u.shape[1:], jnp.float32)
+            stages = [permute_first, permute_second, None, near_of_halves]
+            residual_sum, norm_next, (residual_u, residual_near_u, unused) = sums_with_norm(
+                residual, residual_proj, stages, (residual, empty, empty)
+            )
             late_u, residual_sum = lax.optimization_barrier((residual_near_u, residual_sum))
             ratio = norm_next / norm_now
             direction = residual + ratio[:, None] * direction

time: 89.9 us -> 88.6 us (0.986)
  waiting for transfers between devices: 27 us -> 23.2 us
  starting transfers between devices: 26.3 us -> 28.2 us
    ppermute x20, waiting for transfers between devices: 27 us -> 23.2 us  [swapped(): return lax.ppermute(value, axis, pairs)]
    ppermute x20, starting transfers between devices: 26.3 us -> 28.2 us  [swapped(): return lax.ppermute(value, axis, pairs)]
    dot_general x2 -> x3, matrix products: 6.98 us -> 7.1 us  [to_union(): jnp.einsum('cp,gip->gci', pieces(values, 0), hot, preferred_element_type=...]
  transfers between devices with their start and end apart: 20 -> 20, of which waited for: 16 -> 17; matrix products, arithmetic and copies ran while one was open for 28% -> 29% of each run, Pallas kernels for 0% -> 0%
where the time goes in v13:
time: 88.6 us; the launch traced here: 88.3 us
  starting transfers between devices  28.2 us (32%)
  matrix products  26.8 us (30%)
  waiting for transfers between devices  23.2 us (26%)
  other arithmetic  5.99 us (7%)
  local copies, waits for them, and re-layouts  3 us (3%)
  between operations  1.14 us (1%)
    ppermute x20, starting transfers between devices, swapped(): return lax.ppermute(value, axis, pairs)  28.2 us
    ppermute x20, waiting for transfers between devices, swapped(): return lax.ppermute(value, axis, pairs)  23.2 us
    dot_general x4, matrix products, from_union(): jnp.einsum('gci,gip->cp', pieces(values_u, 1), hot, preferred_element_typ...  7.26 us
    dot_general x3, matrix products, to_union(): jnp.einsum('cp,gip->gci', pieces(values, 0), hot, preferred_element_type=...  7.1 us
    dot_general x2, matrix products, near_apply(): jnp.einsum('gij,gcj->gci', kern, union_vec, precision=lax.Precision.HIGH)  3.91 us
    dot_general x2, matrix products, project(): jnp.einsum('lp,cp,rp->lcr', level_gain, values, basis, precision=highest)  3.33 us
  transfers between devices with their start and end apart: 20, of which 17 were waited for; matrix products, arithmetic and copies ran while one was open for 29% of the time, Pallas kernels for 0%

profile of v13, /device:TPU:0, one launch (start us, length us, event | category | flops | bytes accessed | tf_op | source)
XLA Modules:
  0.0 88.3 jit_solution(836177687058742627)
XLA Ops:
  0.6 0.9 %constant_dynamic-update-slice_fusion.3 = f32[24,2048]{1,0:T(8,128)S(1)} fusion(f32[8,2048]{1,0:T(8,128)} %param.9), kind=kLoop, calls=%fused_computation.176 | loop fusion | bytes 131072
  1.6 1.0 %multiply_reduce_fusion.5 = (f32[16]{0:T(128)S(1)}, f32[24,2048]{1,0:T(8,128)S(1)}) fusion(f32[16,2048]{1,0:T(8,128)} %param.12, f32[24,2048]{1,0:T(8,128)S(1)} %constant_dynamic-update-slice_fusion.3), kind=kLoop, calls=%fused_computation.103 | loop fusion | flops 65520 | bytes 262656 | tf_op jit(solution)/shard_map/reduce_sum | solution.py:117
  2.6 2.1 %convolution_bitcast_fusion.1 = f32[5,16,128]{2,1,0:T(8,128)S(1)} fusion(f32[128,2048]{1,0:T(8,128)S(1)} %copy-done, f32[2048,5]{0,1:T(8,128)} %bitcast.69, f32[2048,16]{0,1:T(8,128)} %bitcast.68), kind=kOutput, calls=%fused_computation.32 | convolution fusion | flops 251822080 | bytes 1261568 | tf_op jit(solution)/shard_map/lp,cp,rp->lcr/dot_general | solution.py:114
  4.8 3.1 %collective-permute-start = (f32[6,16,128]{2,1,0:T(8,128)S(1)}, f32[6,16,128]{2,1,0:T(8,128)S(1)}, u32[]{:S(2)}, u32[]{:S(2)}) collective-permute-start(f32[6,16,128]{2,1,0:T(8,128)S(1)} %pad_maximum_fusion), channel_id=1, source_target_pairs={{0,1},{1,0},{2,3},{3,2},{4,5},{5,4},{6,7},{7,6},{8,9},{9,8},{10,11... | collective-permute-start | bytes 147464 | tf_op jit(solution)/shard_map/ppermute | solution.py:19
  8.4 1.4 %reduce.9 = s32[2048]{0:T(1024)S(1)} reduce(s32[1,2048]{1,0:T(1,128)} %param.16, s32[]{:T(128)} %broadcast.116), dimensions={0}, to_apply=%param.16.reduce_sub_computation.3 | reduce | bytes 16388 | tf_op args[7]
  9.8 0.8 fusion.86
  11.8 3.5 %fusion.18 = f32[4,72,512]{2,1,0:T(8,128)S(1)} fusion(s32[4,512]{1,0:T(4,128)S(1)} %constant_dynamic-update-slice_fusion, bf16[24,2048]{1,0:T(8,128)(2,1)S(1)} %get-tuple-element.111, bf16[24,2048]{1,0:T(8,128)(2,1)S(1)} %get-tuple-element.112, bf16[24,2048]{1,0:T(8,128)(2,1)S(1)} %get-tuple-element.110), kind=kOutput, calls=%fused_computation.26 | convolution fusion | flops 609058816 | bytes 892928 | tf_op jit(solution)/shard_map/cp,gip->gci/dot_general | solution.py:49
  15.8 1.6 %exponential_multiply_fusion = f32[4,512,512]{2,1,0:T(8,128)S(1)} fusion(bf16[4,48,512]{2,1,0:T(8,128)(2,1)S(1)} %get-tuple-element.138, bf16[4,48,512]{2,1,0:T(8,128)(2,1)S(1)} %get-tuple-element.137, f32[4,512]{1,0:T(4,128)S(1)} %multiply_reduce_fusion.6), kind=kOutput, calls=%fused_computation.19 | convolution fusion | flops 105906176 | bytes 4595712 | tf_op jit(solution)/shard_map/gfi,gfj->gij/dot_general | solution.py:33
  17.5 2.7 %collective-permute-start.1 = (f32[5,16,128]{2,1,0:T(8,128)S(1)}, f32[5,16,128]{2,1,0:T(8,128)S(1)}, u32[]{:S(2)}, u32[]{:S(2)}) collective-permute-start(f32[5,16,128]{2,1,0:T(8,128)S(1)} %slice.222), channel_id=1, source_target_pairs={{0,2},{1,3},{2,0},{3,1},{4,6},{5,7},{6,4},{7,5},{8,10},{9,11},{10,... | collective-permute-start | bytes 122888 | tf_op jit(solution)/shard_map/ppermute | solution.py:19
  20.1 1.8 %fusion.54 = f32[4,16,512]{2,1,0:T(8,128)S(1)} fusion(f32[4,512,512]{2,1,0:T(8,128)S(1)} %exponential_multiply_fusion, f32[4,24,512]{2,1,0:T(8,128)S(1)} %slice_add_fusion), kind=kOutput, calls=%fused_computation.104 | convolution fusion | flops 100663296 | bytes 4456448 | tf_op jit(solution)/shard_map/gij,gcj->gci/dot_general | solution.py:40
  22.5 1.2 %collective-permute-done.2 = f32[4,16,128]{2,1,0:T(8,128)S(1)} collective-permute-done((f32[4,16,128]{2,1,0:T(8,128)S(1)}, f32[4,16,128]{2,1,0:T(8,128)S(1)}, u32[]{:S(2)}, u32[]{:S(2)}) %collective-permute-start.2) | collective-permute-done | bytes 32800 | tf_op jit(solution)/shard_map/ppermute | solution.py:19
  23.7 1.9 %collective-permute-start.3 = (f32[3,16,128]{2,1,0:T(8,128)S(1)}, f32[3,16,128]{2,1,0:T(8,128)S(1)}, u32[]{:S(2)}, u32[]{:S(2)}) collective-permute-start(f32[3,16,128]{2,1,0:T(8,128)S(1)} %slice.224), channel_id=1, source_target_pairs={{0,8},{4,12},{8,0},{12,4},{16,24},{20,28},{24,16},{28,20},{1,9},{5... | collective-permute-start | bytes 73736 | tf_op jit(solution)/shard_map/ppermute | solution.py:19
  25.8 1.9 %collective-permute-done.3 = f32[3,16,128]{2,1,0:T(8,128)S(1)} collective-permute-done((f32[3,16,128]{2,1,0:T(8,128)S(1)}, f32[3,16,128]{2,1,0:T(8,128)S(1)}, u32[]{:S(2)}, u32[]{:S(2)}) %collective-permute-start.3) | collective-permute-done | bytes 24608 | tf_op jit(solution)/shard_map/ppermute | solution.py:19
  27.6 1.9 %collective-permute-start.4 = (f32[2,16,128]{2,1,0:T(8,128)S(1)}, f32[2,16,128]{2,1,0:T(8,128)S(1)}, u32[]{:S(2)}, u32[]{:S(2)}) collective-permute-start(f32[2,16,128]{2,1,0:T(8,128)S(1)} %slice.225), channel_id=1, source_target_pairs={{0,16},{4,20},{8,24},{12,28},{16,0},{20,4},{24,8},{28,12},{1,17},{... | collective-permute-start | bytes 49160 | tf_op jit(solution)/shard_map/ppermute | solution.py:19
  29.6 1.9 %collective-permute-done.4 = f32[2,16,128]{2,1,0:T(8,128)S(1)} collective-permute-done((f32[2,16,128]{2,1,0:T(8,128)S(1)}, f32[2,16,128]{2,1,0:T(8,128)S(1)}, u32[]{:S(2)}, u32[]{:S(2)}) %collective-permute-start.4) | collective-permute-done | bytes 16416 | tf_op jit(solution)/shard_map/ppermute | solution.py:19
  31.8 0.6 convolution_multiply_fusion.3
  32.5 0.8 fusion.19
  33.6 1.8 %fusion.14 = f32[48,2048]{1,0:T(8,128)S(1)} fusion(s32[2,512]{1,0:T(2,128)S(1)} %get-tuple-element.142, bf16[2,16,512]{2,1,0:T(8,128)(2,1)S(1)} %get-tuple-element.129, bf16[2,16,512]{2,1,0:T(8,128)(2,1)S(1)} %get-tuple-element.130, bf16[2,16,512]{2,1,0:T(8,128)(2,1)S(1)} %get-tuple-element.128), kind=kOutput, calls=%fused_computation.22 | convolution fusion | flops 203718656 | bytes 495616 | tf_op jit(solution)/shard_map/gci,gip->cp/dot_general | solution.py:55
  35.5 1.5 %collective-permute-done.5 = f32[16]{0:T(128)S(1)} collective-permute-done((f32[16]{0:T(128)S(1)}, f32[16]{0:T(128)S(1)}, u32[]{:S(2)}, u32[]{:S(2)}) %collective-permute-start.5) | collective-permute-done | bytes 96 | tf_op jit(solution)/shard_map/ppermute | solution.py:19
  37.0 2.6 %collective-permute-start.6 = (f32[16]{0:T(128)S(1)}, f32[16]{0:T(128)S(1)}, u32[]{:S(2)}, u32[]{:S(2)}) collective-permute-start(f32[16]{0:T(128)S(1)} %add.199), channel_id=1, source_target_pairs={{0,2},{1,3},{2,0},{3,1},{4,6},{5,7},{6,4},{7,5},{8,10},{9,11},{10,... | collective-permute-start | bytes 200 | tf_op jit(solution)/shard_map/ppermute | solution.py:19
  39.6 1.8 %fusion.16 = f32[48,2048]{1,0:T(8,128)S(1)} fusion(s32[2,512]{1,0:T(2,128)S(1)} %get-tuple-element.141, bf16[2,16,512]{2,1,0:T(8,128)(2,1)S(1)} %get-tuple-element.126, bf16[2,16,512]{2,1,0:T(8,128)(2,1)S(1)} %get-tuple-element.127, bf16[2,16,512]{2,1,0:T(8,128)(2,1)S(1)} %get-tuple-element.125), kind=kOutput, calls=%fused_computation.24 | convolution fusion | flops 203718656 | bytes 495616 | tf_op jit(solution)/shard_map/gci,gip->cp/dot_general | solution.py:55
  41.6 1.2 %convolution_bitcast_fusion = f32[5,16,128]{2,1,0:T(8,128)S(1)} fusion(f32[128,2048]{1,0:T(8,128)S(1)} %copy-done, f32[2048,16]{0,1:T(8,128)S(1)} %add_bitcast_fusion, f32[2048,5]{0,1:T(8,128)S(1)} %bitcast.70), kind=kOutput, calls=%fused_computation.31 | convolution fusion | flops 251822080 | bytes 1261568 | tf_op jit(solution)/shard_map/lp,cp,rp->lcr/dot_general | solution.py:114
  42.8 1.8 %collective-permute-start.8 = (f32[16]{0:T(128)S(1)}, f32[16]{0:T(128)S(1)}, u32[]{:S(2)}, u32[]{:S(2)}) collective-permute-start(f32[16]{0:T(128)S(1)} %add.207), channel_id=1, source_target_pairs={{0,8},{4,12},{8,0},{12,4},{16,24},{20,28},{24,16},{28,20},{1,9},{5... | collective-permute-start | bytes 200 | tf_op jit(solution)/shard_map/ppermute | solution.py:19
  44.6 1.8 %collective-permute-done.8 = f32[16]{0:T(128)S(1)} collective-permute-done((f32[16]{0:T(128)S(1)}, f32[16]{0:T(128)S(1)}, u32[]{:S(2)}, u32[]{:S(2)}) %collective-permute-start.8) | collective-permute-done | bytes 96 | tf_op jit(solution)/shard_map/ppermute | solution.py:19
  46.4 1.7 %collective-permute-start.9 = (f32[16]{0:T(128)S(1)}, f32[16]{0:T(128)S(1)}, u32[]{:S(2)}, u32[]{:S(2)}) collective-permute-start(f32[16]{0:T(128)S(1)} %add.210), channel_id=1, source_target_pairs={{0,16},{4,20},{8,24},{12,28},{16,0},{20,4},{24,8},{28,12},{1,17},{... | collective-permute-start | bytes 200 | tf_op jit(solution)/shard_map/ppermute | solution.py:19
  48.3 1.7 %collective-permute-done.9 = f32[16]{0:T(128)S(1)} collective-permute-done((f32[16]{0:T(128)S(1)}, f32[16]{0:T(128)S(1)}, u32[]{:S(2)}, u32[]{:S(2)}) %collective-permute-start.9) | collective-permute-done | bytes 96 | tf_op jit(solution)/shard_map/ppermute | solution.py:19
  50.9 1.8 %fusion.21 = f32[2,48,512]{2,1,0:T(8,128)S(1)} fusion(s32[2,512]{1,0:T(2,128)S(1)} %get-tuple-element.142, bf16[16,2048]{1,0:T(8,128)(2,1)S(1)} %get-tuple-element.123, bf16[16,2048]{1,0:T(8,128)(2,1)S(1)} %get-tuple-element.124, bf16[16,2048]{1,0:T(8,128)(2,1)S(1)} %get-tuple-element.122), kind=kOutput, calls=%fused_computation.29 | convolution fusion | flops 204013568 | bytes 397312 | tf_op jit(solution)/shard_map/cp,gip->gci/dot_general | solution.py:49
  52.7 1.7 %collective-permute-done.10 = f32[6,16,128]{2,1,0:T(8,128)S(1)} collective-permute-done((f32[6,16,128]{2,1,0:T(8,128)S(1)}, f32[6,16,128]{2,1,0:T(8,128)S(1)}, u32[]{:S(2)}, u32[]{:S(2)}) %collective-permute-start.10) | collective-permute-done | bytes 49184 | tf_op jit(solution)/shard_map/ppermute | solution.py:19
  54.5 2.5 %collective-permute-start.11 = (f32[5,16,128]{2,1,0:T(8,128)S(1)}, f32[5,16,128]{2,1,0:T(8,128)S(1)}, u32[]{:S(2)}, u32[]{:S(2)}) collective-permute-start(f32[5,16,128]{2,1,0:T(8,128)S(1)} %slice.197), channel_id=1, source_target_pairs={{0,2},{1,3},{2,0},{3,1},{4,6},{5,7},{6,4},{7,5},{8,10},{9,11},{10,... | collective-permute-start | bytes 122888 | tf_op jit(solution)/shard_map/ppermute | solution.py:19
  57.0 1.8 %fusion.22 = f32[2,48,512]{2,1,0:T(8,128)S(1)} fusion(s32[2,512]{1,0:T(2,128)S(1)} %get-tuple-element.141, bf16[16,2048]{1,0:T(8,128)(2,1)S(1)} %get-tuple-element.120, bf16[16,2048]{1,0:T(8,128)(2,1)S(1)} %get-tuple-element.121, bf16[16,2048]{1,0:T(8,128)(2,1)S(1)} %get-tuple-element.119), kind=kOutput, calls=%fused_computation.30 | convolution fusion | flops 204013568 | bytes 397312 | tf_op jit(solution)/shard_map/cp,gip->gci/dot_general | solution.py:49
  58.9 0.9 %collective-permute-done.11 = f32[5,16,128]{2,1,0:T(8,128)S(1)} collective-permute-done((f32[5,16,128]{2,1,0:T(8,128)S(1)}, f32[5,16,128]{2,1,0:T(8,128)S(1)}, u32[]{:S(2)}, u32[]{:S(2)}) %collective-permute-start.11) | collective-permute-done | bytes 40992 | tf_op jit(solution)/shard_map/ppermute | solution.py:19
  59.9 1.2 %collective-permute-done.12 = f32[4,16,128]{2,1,0:T(8,128)S(1)} collective-permute-done((f32[4,16,128]{2,1,0:T(8,128)S(1)}, f32[4,16,128]{2,1,0:T(8,128)S(1)}, u32[]{:S(2)}, u32[]{:S(2)}) %collective-permute-start.12) | collective-permute-done | bytes 32800 | tf_op jit(solution)/shard_map/ppermute | solution.py:19
  61.1 1.7 %collective-permute-start.13 = (f32[3,16,128]{2,1,0:T(8,128)S(1)}, f32[3,16,128]{2,1,0:T(8,128)S(1)}, u32[]{:S(2)}, u32[]{:S(2)}) collective-permute-start(f32[3,16,128]{2,1,0:T(8,128)S(1)} %slice.247), channel_id=1, source_target_pairs={{0,8},{4,12},{8,0},{12,4},{16,24},{20,28},{24,16},{28,20},{1,9},{5... | collective-permute-start | bytes 73736 | tf_op jit(solution)/shard_map/ppermute | solution.py:19
  62.9 2.1 %fusion.98 = f32[4,16,512]{2,1,0:T(8,128)S(1)} fusion(f32[4,16,512]{2,1,0:T(8,128)S(1)} %constant_dynamic-update-slice_fusion.16, f32[4,512,512]{2,1,0:T(8,128)S(1)} %exponential_multiply_fusion), kind=kOutput, calls=%fused_computation.226 | convolution fusion | flops 100663296 | bytes 4456448 | tf_op jit(solution)/shard_map/gij,gcj->gci/dot_general | solution.py:40
  65.0 1.8 %collective-permute-start.14 = (f32[2,16,128]{2,1,0:T(8,128)S(1)}, f32[2,16,128]{2,1,0:T(8,128)S(1)}, u32[]{:S(2)}, u32[]{:S(2)}) collective-permute-start(f32[2,16,128]{2,1,0:T(8,128)S(1)} %slice.206), channel_id=1, source_target_pairs={{0,16},{4,20},{8,24},{12,28},{16,0},{20,4},{24,8},{28,12},{1,17},{... | collective-permute-start | bytes 49160 | tf_op jit(solution)/shard_map/ppermute | solution.py:19
  66.8 2.0 %collective-permute-done.14 = f32[2,16,128]{2,1,0:T(8,128)S(1)} collective-permute-done((f32[2,16,128]{2,1,0:T(8,128)S(1)}, f32[2,16,128]{2,1,0:T(8,128)S(1)}, u32[]{:S(2)}, u32[]{:S(2)}) %collective-permute-start.14) | collective-permute-done | bytes 16416 | tf_op jit(solution)/shard_map/ppermute | solution.py:19
  69.4 0.6 convolution_multiply_fusion.2
  70.0 0.8 fusion.20
  71.5 1.8 %fusion.15 = f32[48,2048]{1,0:T(8,128)S(1)} fusion(s32[2,512]{1,0:T(2,128)S(1)} %get-tuple-element.142, bf16[2,16,512]{2,1,0:T(8,128)(2,1)S(1)} %get-tuple-element.117, bf16[2,16,512]{2,1,0:T(8,128)(2,1)S(1)} %get-tuple-element.118, bf16[2,16,512]{2,1,0:T(8,128)(2,1)S(1)} %get-tuple-element.116), kind=kOutput, calls=%fused_computation.23 | convolution fusion | flops 203718656 | bytes 495616 | tf_op jit(solution)/shard_map/gci,gip->cp/dot_general | solution.py:55
  73.4 1.5 %collective-permute-done.15 = f32[16]{0:T(128)S(1)} collective-permute-done((f32[16]{0:T(128)S(1)}, f32[16]{0:T(128)S(1)}, u32[]{:S(2)}, u32[]{:S(2)}) %collective-permute-start.15) | collective-permute-done | bytes 96 | tf_op jit(solution)/shard_map/ppermute | solution.py:19
  74.9 2.1 %collective-permute-start.16 = (f32[16]{0:T(128)S(1)}, f32[16]{0:T(128)S(1)}, u32[]{:S(2)}, u32[]{:S(2)}) collective-permute-start(f32[16]{0:T(128)S(1)} %add.228), channel_id=1, source_target_pairs={{0,2},{1,3},{2,0},{3,1},{4,6},{5,7},{6,4},{7,5},{8,10},{9,11},{10,... | collective-permute-start | bytes 200 | tf_op jit(solution)/shard_map/ppermute | solution.py:19
  77.0 1.8 %fusion.17 = f32[48,2048]{1,0:T(8,128)S(1)} fusion(s32[2,512]{1,0:T(2,128)S(1)} %get-tuple-element.141, bf16[2,16,512]{2,1,0:T(8,128)(2,1)S(1)} %get-tuple-element.114, bf16[2,16,512]{2,1,0:T(8,128)(2,1)S(1)} %get-tuple-element.115, bf16[2,16,512]{2,1,0:T(8,128)(2,1)S(1)} %get-tuple-element.113), kind=kOutput, calls=%fused_computation.25 | convolution fusion | flops 203718656 | bytes 495616 | tf_op jit(solution)/shard_map/gci,gip->cp/dot_general | solution.py:55
  79.3 1.1 %collective-permute-done.17 = f32[16]{0:T(128)S(1)} collective-permute-done((f32[16]{0:T(128)S(1)}, f32[16]{0:T(128)S(1)}, u32[]{:S(2)}, u32[]{:S(2)}) %collective-permute-start.17) | collective-permute-done | bytes 96 | tf_op jit(solution)/shard_map/ppermute | solution.py:19
  80.4 1.7 %collective-permute-start.18 = (f32[16]{0:T(128)S(1)}, f32[16]{0:T(128)S(1)}, u32[]{:S(2)}, u32[]{:S(2)}) collective-permute-start(f32[16]{0:T(128)S(1)} %add.236), channel_id=1, source_target_pairs={{0,8},{4,12},{8,0},{12,4},{16,24},{20,28},{24,16},{28,20},{1,9},{5... | collective-permute-start | bytes 200 | tf_op jit(solution)/shard_map/ppermute | solution.py:19
  82.1 1.9 %collective-permute-done.18 = f32[16]{0:T(128)S(1)} collective-permute-done((f32[16]{0:T(128)S(1)}, f32[16]{0:T(128)S(1)}, u32[]{:S(2)}, u32[]{:S(2)}) %collective-permute-start.18) | collective-permute-done | bytes 96 | tf_op jit(solution)/shard_map/ppermute | solution.py:19
  84.0 1.7 %collective-permute-start.19 = (f32[16]{0:T(128)S(1)}, f32[16]{0:T(128)S(1)}, u32[]{:S(2)}, u32[]{:S(2)}) collective-permute-start(f32[16]{0:T(128)S(1)} %add.237), channel_id=1, source_target_pairs={{0,16},{4,20},{8,24},{12,28},{16,0},{20,4},{24,8},{28,12},{1,17},{... | collective-permute-start | bytes 200 | tf_op jit(solution)/shard_map/ppermute | solution.py:19
  85.7 1.8 %collective-permute-done.19 = f32[16]{0:T(128)S(1)} collective-permute-done((f32[16]{0:T(128)S(1)}, f32[16]{0:T(128)S(1)}, u32[]{:S(2)}, u32[]{:S(2)}) %collective-permute-start.19) | collective-permute-done | bytes 96 | tf_op jit(solution)/shard_map/ppermute | solution.py:19
  87.5 0.8 multiply_subtract_fusion
  (116 shorter events, 7.0 us)
Async XLA Ops:
  0.6 2.0 %copy-start = (f32[128,2048]{1,0:T(8,128)S(1)}, f32[128,2048]{1,0:T(8,128)}, u32[]{:S(2)}) copy-start(f32[128,2048]{1,0:T(8,128)} %param.13) | copy-start | bytes 3145732
  4.8 10.5 %copy-start.5 = (f32[8]{0:T(128)S(1)}, f32[8]{0:T(128)}, u32[]{:S(2)}) copy-start(f32[8]{0:T(128)} %param.10) | copy-start | bytes 100
  4.8 12.6 %collective-permute-start = (f32[6,16,128]{2,1,0:T(8,128)S(1)}, f32[6,16,128]{2,1,0:T(8,128)S(1)}, u32[]{:S(2)}, u32[]{:S(2)}) collective-permute-start(f32[6,16,128]{2,1,0:T(8,128)S(1)} %pad_maximum_fusion), channel_id=1, source_target_pairs={{0,1},{1,0},{2,3},{3,2},{4,5},{5,4},{6,7},{7,6},{8,9},{9,8},{10,11... | collective-permute-start | bytes 147464 | tf_op jit(solution)/shard_map/ppermute | solution.py:19
  17.4 14.1 %copy-start.2 = (f32[5,128,128]{2,1,0:T(8,128)S(1)}, f32[5,128,128]{2,1,0:T(8,128)}, u32[]{:S(2)}) copy-start(f32[5,128,128]{2,1,0:T(8,128)} %param.15) | copy-start | bytes 983044
  17.4 15.1 %copy-start.3 = (f32[5,2048]{1,0:T(8,128)S(1)}, f32[5,2048]{1,0:T(8,128)}, u32[]{:S(2)}) copy-start(f32[5,2048]{1,0:T(8,128)} %param.14) | copy-start | bytes 122884
  17.4 15.8 %copy-start.1 = (f32[16,2048]{1,0:T(8,128)S(1)}, f32[16,2048]{1,0:T(8,128)}, u32[]{:S(2)}) copy-start(f32[16,2048]{1,0:T(8,128)} %param.12) | copy-start | bytes 393220
  17.4 15.8 %copy-start.4 = (f32[2048]{0:T(1024)S(1)}, f32[2048]{0:T(1024)}, u32[]{:S(2)}) copy-start(f32[2048]{0:T(1024)} %param.11) | copy-start | bytes 24580
  17.5 5.0 %collective-permute-start.1 = (f32[5,16,128]{2,1,0:T(8,128)S(1)}, f32[5,16,128]{2,1,0:T(8,128)S(1)}, u32[]{:S(2)}, u32[]{:S(2)}) collective-permute-start(f32[5,16,128]{2,1,0:T(8,128)S(1)} %slice.222), channel_id=1, source_target_pairs={{0,2},{1,3},{2,0},{3,1},{4,6},{5,7},{6,4},{7,5},{8,10},{9,11},{10,... | collective-permute-start | bytes 122888 | tf_op jit(solution)/shard_map/ppermute | solution.py:19
  22.4 1.3 %collective-permute-start.2 = (f32[4,16,128]{2,1,0:T(8,128)S(1)}, f32[4,16,128]{2,1,0:T(8,128)S(1)}, u32[]{:S(2)}, u32[]{:S(2)}) collective-permute-start(f32[4,16,128]{2,1,0:T(8,128)S(1)} %slice.223), channel_id=1, source_target_pairs={{0,4},{4,0},{8,12},{12,8},{16,20},{20,16},{24,28},{28,24},{1,5},{5... | collective-permute-start | bytes 98312 | tf_op jit(solution)/shard_map/ppermute | solution.py:19
  23.7 3.9 %collective-permute-start.3 = (f32[3,16,128]{2,1,0:T(8,128)S(1)}, f32[3,16,128]{2,1,0:T(8,128)S(1)}, u32[]{:S(2)}, u32[]{:S(2)}) collective-permute-start(f32[3,16,128]{2,1,0:T(8,128)S(1)} %slice.224), channel_id=1, source_target_pairs={{0,8},{4,12},{8,0},{12,4},{16,24},{20,28},{24,16},{28,20},{1,9},{5... | collective-permute-start | bytes 73736 | tf_op jit(solution)/shard_map/ppermute | solution.py:19
  27.6 3.8 %collective-permute-start.4 = (f32[2,16,128]{2,1,0:T(8,128)S(1)}, f32[2,16,128]{2,1,0:T(8,128)S(1)}, u32[]{:S(2)}, u32[]{:S(2)}) collective-permute-start(f32[2,16,128]{2,1,0:T(8,128)S(1)} %slice.225), channel_id=1, source_target_pairs={{0,16},{4,20},{8,24},{12,28},{16,0},{20,4},{24,8},{28,12},{1,17},{... | collective-permute-start | bytes 49160 | tf_op jit(solution)/shard_map/ppermute | solution.py:19
  33.4 3.6 %collective-permute-start.5 = (f32[16]{0:T(128)S(1)}, f32[16]{0:T(128)S(1)}, u32[]{:S(2)}, u32[]{:S(2)}) collective-permute-start(f32[16]{0:T(128)S(1)} %add.198), channel_id=1, source_target_pairs={{0,1},{1,0},{2,3},{3,2},{4,5},{5,4},{6,7},{7,6},{8,9},{9,8},{10,11... | collective-permute-start | bytes 200 | tf_op jit(solution)/shard_map/ppermute | solution.py:19
  37.0 4.5 %collective-permute-start.6 = (f32[16]{0:T(128)S(1)}, f32[16]{0:T(128)S(1)}, u32[]{:S(2)}, u32[]{:S(2)}) collective-permute-start(f32[16]{0:T(128)S(1)} %add.199), channel_id=1, source_target_pairs={{0,2},{1,3},{2,0},{3,1},{4,6},{5,7},{6,4},{7,5},{8,10},{9,11},{10,... | collective-permute-start | bytes 200 | tf_op jit(solution)/shard_map/ppermute | solution.py:19
  41.5 1.3 %collective-permute-start.7 = (f32[16]{0:T(128)S(1)}, f32[16]{0:T(128)S(1)}, u32[]{:S(2)}, u32[]{:S(2)}) collective-permute-start(f32[16]{0:T(128)S(1)} %add.203), channel_id=1, source_target_pairs={{0,4},{4,0},{8,12},{12,8},{16,20},{20,16},{24,28},{28,24},{1,5},{5... | collective-permute-start | bytes 200 | tf_op jit(solution)/shard_map/ppermute | solution.py:19
  42.8 3.6 %collective-permute-start.8 = (f32[16]{0:T(128)S(1)}, f32[16]{0:T(128)S(1)}, u32[]{:S(2)}, u32[]{:S(2)}) collective-permute-start(f32[16]{0:T(128)S(1)} %add.207), channel_id=1, source_target_pairs={{0,8},{4,12},{8,0},{12,4},{16,24},{20,28},{24,16},{28,20},{1,9},{5... | collective-permute-start | bytes 200 | tf_op jit(solution)/shard_map/ppermute | solution.py:19
  46.4 3.5 %collective-permute-start.9 = (f32[16]{0:T(128)S(1)}, f32[16]{0:T(128)S(1)}, u32[]{:S(2)}, u32[]{:S(2)}) collective-permute-start(f32[16]{0:T(128)S(1)} %add.210), channel_id=1, source_target_pairs={{0,16},{4,20},{8,24},{12,28},{16,0},{20,4},{24,8},{28,12},{1,17},{... | collective-permute-start | bytes 200 | tf_op jit(solution)/shard_map/ppermute | solution.py:19
  50.3 4.1 %collective-permute-start.10 = (f32[6,16,128]{2,1,0:T(8,128)S(1)}, f32[6,16,128]{2,1,0:T(8,128)S(1)}, u32[]{:S(2)}, u32[]{:S(2)}) collective-permute-start(f32[6,16,128]{2,1,0:T(8,128)S(1)} %pad_maximum_fusion.1), channel_id=1, source_target_pairs={{0,1},{1,0},{2,3},{3,2},{4,5},{5,4},{6,7},{7,6},{8,9},{9,8},{10,11... | collective-permute-start | bytes 147464 | tf_op jit(solution)/shard_map/ppermute | solution.py:19
  54.5 5.3 %collective-permute-start.11 = (f32[5,16,128]{2,1,0:T(8,128)S(1)}, f32[5,16,128]{2,1,0:T(8,128)S(1)}, u32[]{:S(2)}, u32[]{:S(2)}) collective-permute-start(f32[5,16,128]{2,1,0:T(8,128)S(1)} %slice.197), channel_id=1, source_target_pairs={{0,2},{1,3},{2,0},{3,1},{4,6},{5,7},{6,4},{7,5},{8,10},{9,11},{10,... | collective-permute-start | bytes 122888 | tf_op jit(solution)/shard_map/ppermute | solution.py:19
  59.8 1.3 %collective-permute-start.12 = (f32[4,16,128]{2,1,0:T(8,128)S(1)}, f32[4,16,128]{2,1,0:T(8,128)S(1)}, u32[]{:S(2)}, u32[]{:S(2)}) collective-permute-start(f32[4,16,128]{2,1,0:T(8,128)S(1)} %slice.202), channel_id=1, source_target_pairs={{0,4},{4,0},{8,12},{12,8},{16,20},{20,16},{24,28},{28,24},{1,5},{5... | collective-permute-start | bytes 98312 | tf_op jit(solution)/shard_map/ppermute | solution.py:19
  61.1 3.9 %collective-permute-start.13 = (f32[3,16,128]{2,1,0:T(8,128)S(1)}, f32[3,16,128]{2,1,0:T(8,128)S(1)}, u32[]{:S(2)}, u32[]{:S(2)}) collective-permute-start(f32[3,16,128]{2,1,0:T(8,128)S(1)} %slice.247), channel_id=1, source_target_pairs={{0,8},{4,12},{8,0},{12,4},{16,24},{20,28},{24,16},{28,20},{1,9},{5... | collective-permute-start | bytes 73736 | tf_op jit(solution)/shard_map/ppermute | solution.py:19
  65.0 3.8 %collective-permute-start.14 = (f32[2,16,128]{2,1,0:T(8,128)S(1)}, f32[2,16,128]{2,1,0:T(8,128)S(1)}, u32[]{:S(2)}, u32[]{:S(2)}) collective-permute-start(f32[2,16,128]{2,1,0:T(8,128)S(1)} %slice.206), channel_id=1, source_target_pairs={{0,16},{4,20},{8,24},{12,28},{16,0},{20,4},{24,8},{28,12},{1,17},{... | collective-permute-start | bytes 49160 | tf_op jit(solution)/shard_map/ppermute | solution.py:19
  71.2 3.6 %collective-permute-start.15 = (f32[16]{0:T(128)S(1)}, f32[16]{0:T(128)S(1)}, u32[]{:S(2)}, u32[]{:S(2)}) collective-permute-start(f32[16]{0:T(128)S(1)} %add.227), channel_id=1, source_target_pairs={{0,1},{1,0},{2,3},{3,2},{4,5},{5,4},{6,7},{7,6},{8,9},{9,8},{10,11... | collective-permute-start | bytes 200 | tf_op jit(solution)/shard_map/ppermute | solution.py:19
  74.9 4.4 %collective-permute-start.16 = (f32[16]{0:T(128)S(1)}, f32[16]{0:T(128)S(1)}, u32[]{:S(2)}, u32[]{:S(2)}) collective-permute-start(f32[16]{0:T(128)S(1)} %add.228), channel_id=1, source_target_pairs={{0,2},{1,3},{2,0},{3,1},{4,6},{5,7},{6,4},{7,5},{8,10},{9,11},{10,... | collective-permute-start | bytes 200 | tf_op jit(solution)/shard_map/ppermute | solution.py:19
  79.3 1.1 %collective-permute-start.17 = (f32[16]{0:T(128)S(1)}, f32[16]{0:T(128)S(1)}, u32[]{:S(2)}, u32[]{:S(2)}) collective-permute-start(f32[16]{0:T(128)S(1)} %add.232), channel_id=1, source_target_pairs={{0,4},{4,0},{8,12},{12,8},{16,20},{20,16},{24,28},{28,24},{1,5},{5... | collective-permute-start | bytes 200 | tf_op jit(solution)/shard_map/ppermute | solution.py:19
  80.4 3.5 %collective-permute-start.18 = (f32[16]{0:T(128)S(1)}, f32[16]{0:T(128)S(1)}, u32[]{:S(2)}, u32[]{:S(2)}) collective-permute-start(f32[16]{0:T(128)S(1)} %add.236), channel_id=1, source_target_pairs={{0,8},{4,12},{8,0},{12,4},{16,24},{20,28},{24,16},{28,20},{1,9},{5... | collective-permute-start | bytes 200 | tf_op jit(solution)/shard_map/ppermute | solution.py:19
  84.0 3.5 %collective-permute-start.19 = (f32[16]{0:T(128)S(1)}, f32[16]{0:T(128)S(1)}, u32[]{:S(2)}, u32[]{:S(2)}) collective-permute-start(f32[16]{0:T(128)S(1)} %add.237), channel_id=1, source_target_pairs={{0,16},{4,20},{8,24},{12,28},{16,0},{20,4},{24,8},{28,12},{1,17},{... | collective-permute-start | bytes 200 | tf_op jit(solution)/shard_map/ppermute | solution.py:19

commit v14 on v13

--- a/solution.py
+++ b/solution.py
@@ -103,12 +103,8 @@
     union_order = jnp.concatenate([order_tiles[pairs[0, 0]], order_tiles[pairs[0, 1]]], axis=1)
     position = jnp.arange(points, dtype=jnp.int32)
     hot = (union_order[:, :, None] == position[None, None, :]).astype(jnp.bfloat16)
-    stacked = to_union(jnp.concatenate([coords, right_side], axis=0), hot)
-    kern = lax.optimization_barrier(near_kernels(stacked[:, :features] * inv_scale[None, :, None]))
     scales = 2.0 ** ((1.0 - jnp.arange(levels, dtype=jnp.float32)) / 2.0)
 
-    def near_of_union(values_u):
-        return lax.optimization_barrier(near_apply(kern, values_u))
 
     def project(values):
         return jnp.einsum("lp,cp,rp->lcr", level_gain, values, basis, precision=highest)
@@ -130,7 +126,7 @@
     def near_of_halves(state):
         values, first, second = state
         values_u = jnp.concatenate([first, second], axis=0)
-        return values_u, near_of_union(values_u), second
+        return values_u, lax.optimization_barrier(near_apply(kern, values_u)), second
 
     half = union_order.shape[0] // 2
     hot_first = (union_order[:half, :, None] == position[None, None, :]).astype(jnp.bfloat16)
@@ -144,15 +140,28 @@
         late, near, extra = state
         return late, near + from_union(late[half:], hot_second), extra
 
+    def permute_inputs(unused):
+        stacked = to_union(jnp.concatenate([coords, right_side], axis=0), hot)
+        return stacked[:, :features] * inv_scale[None, :, None], stacked[:, features:]
+
+    def kernel_blocks(state):
+        union_coords, direction_u = state
+        return near_kernels(union_coords), direction_u
+
+    def first_near(state):
+        kern, direction_u = state
+        return kern, direction_u, lax.optimization_barrier(near_apply(kern, direction_u))
+
     solution = jnp.zeros_like(right_side)
     residual = right_side
     direction = right_side
-    direction_u = stacked[:, features:]
     residual_proj = project(residual)
     for step in range(ITERATIONS):
         if step == 0:
-            nodesum, norm_now, unused = sums_with_norm(residual, residual_proj, [], ())
-            near_u = near_of_union(direction_u)
+            stages = [permute_inputs, kernel_blocks, None, first_near]
+            nodesum, norm_now, (kern, direction_u, near_u) = sums_with_norm(
+                residual, residual_proj, stages, jnp.zeros((), jnp.float32)
+            )
             late_u, nodesum = lax.optimization_barrier((near_u, nodesum))
             carried = jnp.zeros_like(right_side)
         else:

time: 88.6 us -> 86.7 us (0.979)
  waiting for transfers between devices: 23.2 us -> 21.5 us
    ppermute x20, waiting for transfers between devices: 23.2 us -> 21.5 us  [swapped(): return lax.ppermute(value, axis, pairs)]
    concatenate x0 -> x1, other arithmetic: none -> 1.03 us  [permute_inputs(): stacked = to_union(jnp.concatenate([coords, right_side], axis=0), hot)]
    reduce_sum x2 -> x1, other arithmetic: 1.24 us -> 0.21 us  [sums_with_norm(): norm = jnp.sum(values * values, axis=1)]
  transfers between devices with their start and end apart: 20 -> 20, of which waited for: 17 -> 17; matrix products, arithmetic and copies ran while one was open for 29% -> 30% of each run, Pallas kernels for 0% -> 0%
where the time goes in v14:
time: 86.7 us; the launch traced here: 86.4 us
  starting transfers between devices  28.2 us (33%)
  matrix products  26.8 us (31%)
  waiting for transfers between devices  21.5 us (25%)
  other arithmetic  5.8 us (7%)
  local copies, waits for them, and re-layouts  3.01 us (3%)
  between operations  1.2 us (1%)
    ppermute x20, starting transfers between devices, swapped(): return lax.ppermute(value, axis, pairs)  28.2 us
    ppermute x20, waiting for transfers between devices, swapped(): return lax.ppermute(value, axis, pairs)  21.5 us
    dot_general x4, matrix products, from_union(): jnp.einsum('gci,gip->cp', pieces(values_u, 1), hot, preferred_element_typ...  7.26 us
    dot_general x3, matrix products, to_union(): jnp.einsum('cp,gip->gci', pieces(values, 0), hot, preferred_element_type=...  7.1 us
    dot_general x2, matrix products, near_apply(): jnp.einsum('gij,gcj->gci', kern, union_vec, precision=lax.Precision.HIGH)  3.91 us
    dot_general x2, matrix products, project(): jnp.einsum('lp,cp,rp->lcr', level_gain, values, basis, precision=highest)  3.33 us
  transfers between devices with their start and end apart: 20, of which 17 were waited for; matrix products, arithmetic and copies ran while one was open for 30% of the time, Pallas kernels for 0%

profile of v14, /device:TPU:0, one launch (start us, length us, event | category | flops | bytes accessed | tf_op | source)
XLA Modules:
  0.0 86.4 jit_solution(8866152805940277721)
XLA Ops:
  0.6 0.9 %constant_dynamic-update-slice_fusion.3 = f32[24,2048]{1,0:T(8,128)S(1)} fusion(f32[8,2048]{1,0:T(8,128)} %param.9), kind=kLoop, calls=%fused_computation.175 | loop fusion | bytes 131072
  1.6 1.0 %constant_dynamic-update-slice_fusion.2 = (f32[24,2048]{1,0:T(8,128)S(1)}, f32[16]{0:T(128)S(1)}) fusion(f32[24,2048]{1,0:T(8,128)S(1)} %constant_dynamic-update-slice_fusion.3, f32[16,2048]{1,0:T(8,128)} %param.12), kind=kLoop, calls=%fused_computation.174 | loop fusion | flops 65520 | bytes 262656 | tf_op jit(solution)/shard_map/concatenate | solution.py:144
  2.6 2.1 %convolution_bitcast_fusion.1 = f32[5,16,128]{2,1,0:T(8,128)S(1)} fusion(f32[128,2048]{1,0:T(8,128)S(1)} %copy-done, f32[2048,5]{0,1:T(8,128)} %bitcast.70, f32[2048,16]{0,1:T(8,128)} %bitcast.69), kind=kOutput, calls=%fused_computation.32 | convolution fusion | flops 251822080 | bytes 1261568 | tf_op jit(solution)/shard_map/lp,cp,rp->lcr/dot_general | solution.py:110
  4.8 3.1 %collective-permute-start = (f32[6,16,128]{2,1,0:T(8,128)S(1)}, f32[6,16,128]{2,1,0:T(8,128)S(1)}, u32[]{:S(2)}, u32[]{:S(2)}) collective-permute-start(f32[6,16,128]{2,1,0:T(8,128)S(1)} %pad_maximum_fusion), channel_id=1, source_target_pairs={{0,1},{1,0},{2,3},{3,2},{4,5},{5,4},{6,7},{7,6},{8,9},{9,8},{10,11... | collective-permute-start | bytes 147464 | tf_op jit(solution)/shard_map/ppermute | solution.py:19
  8.4 1.4 %reduce.9 = s32[2048]{0:T(1024)S(1)} reduce(s32[1,2048]{1,0:T(1,128)} %param.16, s32[]{:T(128)} %broadcast.100), dimensions={0}, to_apply=%param.16.reduce_sub_computation.3 | reduce | bytes 16388 | tf_op args[7]
  9.8 0.8 fusion.84
  10.6 0.6 gather_fusion
  11.8 3.5 %fusion.18 = f32[4,72,512]{2,1,0:T(8,128)S(1)} fusion(s32[4,512]{1,0:T(4,128)S(1)} %constant_dynamic-update-slice_fusion, bf16[24,2048]{1,0:T(8,128)(2,1)S(1)} %get-tuple-element.143, bf16[24,2048]{1,0:T(8,128)(2,1)S(1)} %get-tuple-element.144, bf16[24,2048]{1,0:T(8,128)(2,1)S(1)} %get-tuple-element.142), kind=kOutput, calls=%fused_computation.26 | convolution fusion | flops 609058816 | bytes 892928 | tf_op jit(solution)/shard_map/cp,gip->gci/dot_general | solution.py:49
  15.5 2.7 %collective-permute-start.1 = (f32[5,16,128]{2,1,0:T(8,128)S(1)}, f32[5,16,128]{2,1,0:T(8,128)S(1)}, u32[]{:S(2)}, u32[]{:S(2)}) collective-permute-start(f32[5,16,128]{2,1,0:T(8,128)S(1)} %slice.178), channel_id=1, source_target_pairs={{0,2},{1,3},{2,0},{3,1},{4,6},{5,7},{6,4},{7,5},{8,10},{9,11},{10,... | collective-permute-start | bytes 122888 | tf_op jit(solution)/shard_map/ppermute | solution.py:19
  18.3 1.6 %exponential_multiply_fusion = f32[4,512,512]{2,1,0:T(8,128)S(1)} fusion(bf16[4,48,512]{2,1,0:T(8,128)(2,1)S(1)} %get-tuple-element.172, bf16[4,48,512]{2,1,0:T(8,128)(2,1)S(1)} %get-tuple-element.171, f32[4,512]{1,0:T(4,128)S(1)} %multiply_reduce_fusion.6), kind=kOutput, calls=%fused_computation.19 | convolution fusion | flops 105906176 | bytes 4595712 | tf_op jit(solution)/shard_map/gfi,gfj->gij/dot_general | solution.py:33
  20.6 1.2 %collective-permute-done.2 = f32[4,16,128]{2,1,0:T(8,128)S(1)} collective-permute-done((f32[4,16,128]{2,1,0:T(8,128)S(1)}, f32[4,16,128]{2,1,0:T(8,128)S(1)}, u32[]{:S(2)}, u32[]{:S(2)}) %collective-permute-start.2) | collective-permute-done | bytes 32800 | tf_op jit(solution)/shard_map/ppermute | solution.py:19
  21.8 1.9 %collective-permute-start.3 = (f32[3,16,128]{2,1,0:T(8,128)S(1)}, f32[3,16,128]{2,1,0:T(8,128)S(1)}, u32[]{:S(2)}, u32[]{:S(2)}) collective-permute-start(f32[3,16,128]{2,1,0:T(8,128)S(1)} %slice.233), channel_id=1, source_target_pairs={{0,8},{4,12},{8,0},{12,4},{16,24},{20,28},{24,16},{28,20},{1,9},{5... | collective-permute-start | bytes 73736 | tf_op jit(solution)/shard_map/ppermute | solution.py:19
  23.7 1.8 %fusion.95 = f32[4,16,512]{2,1,0:T(8,128)S(1)} fusion(f32[4,16,512]{2,1,0:T(8,128)S(1)} %slice.232, f32[4,512,512]{2,1,0:T(8,128)S(1)} %exponential_multiply_fusion), kind=kOutput, calls=%fused_computation.219 | convolution fusion | flops 100663296 | bytes 4456448 | tf_op jit(solution)/shard_map/gij,gcj->gci/dot_general | solution.py:40
  25.7 1.9 %collective-permute-start.4 = (f32[2,16,128]{2,1,0:T(8,128)S(1)}, f32[2,16,128]{2,1,0:T(8,128)S(1)}, u32[]{:S(2)}, u32[]{:S(2)}) collective-permute-start(f32[2,16,128]{2,1,0:T(8,128)S(1)} %slice.184), channel_id=1, source_target_pairs={{0,16},{4,20},{8,24},{12,28},{16,0},{20,4},{24,8},{28,12},{1,17},{... | collective-permute-start | bytes 49160 | tf_op jit(solution)/shard_map/ppermute | solution.py:19
  27.8 1.8 %collective-permute-done.4 = f32[2,16,128]{2,1,0:T(8,128)S(1)} collective-permute-done((f32[2,16,128]{2,1,0:T(8,128)S(1)}, f32[2,16,128]{2,1,0:T(8,128)S(1)}, u32[]{:S(2)}, u32[]{:S(2)}) %collective-permute-start.4) | collective-permute-done | bytes 16416 | tf_op jit(solution)/shard_map/ppermute | solution.py:19
  29.9 0.6 convolution_multiply_fusion.3
  30.5 0.8 fusion.19
  31.7 1.8 %fusion.14 = f32[48,2048]{1,0:T(8,128)S(1)} fusion(s32[2,512]{1,0:T(2,128)S(1)} %get-tuple-element.176, bf16[2,16,512]{2,1,0:T(8,128)(2,1)S(1)} %get-tuple-element.161, bf16[2,16,512]{2,1,0:T(8,128)(2,1)S(1)} %get-tuple-element.162, bf16[2,16,512]{2,1,0:T(8,128)(2,1)S(1)} %get-tuple-element.160), kind=kOutput, calls=%fused_computation.22 | convolution fusion | flops 203718656 | bytes 495616 | tf_op jit(solution)/shard_map/gci,gip->cp/dot_general | solution.py:55
  33.6 1.5 %collective-permute-done.5 = f32[16]{0:T(128)S(1)} collective-permute-done((f32[16]{0:T(128)S(1)}, f32[16]{0:T(128)S(1)}, u32[]{:S(2)}, u32[]{:S(2)}) %collective-permute-start.5) | collective-permute-done | bytes 96 | tf_op jit(solution)/shard_map/ppermute | solution.py:19
  35.1 2.6 %collective-permute-start.6 = (f32[16]{0:T(128)S(1)}, f32[16]{0:T(128)S(1)}, u32[]{:S(2)}, u32[]{:S(2)}) collective-permute-start(f32[16]{0:T(128)S(1)} %add.199), channel_id=1, source_target_pairs={{0,2},{1,3},{2,0},{3,1},{4,6},{5,7},{6,4},{7,5},{8,10},{9,11},{10,... | collective-permute-start | bytes 200 | tf_op jit(solution)/shard_map/ppermute | solution.py:19
  37.7 1.8 %fusion.16 = f32[48,2048]{1,0:T(8,128)S(1)} fusion(s32[2,512]{1,0:T(2,128)S(1)} %get-tuple-element.175, bf16[2,16,512]{2,1,0:T(8,128)(2,1)S(1)} %get-tuple-element.158, bf16[2,16,512]{2,1,0:T(8,128)(2,1)S(1)} %get-tuple-element.159, bf16[2,16,512]{2,1,0:T(8,128)(2,1)S(1)} %get-tuple-element.157), kind=kOutput, calls=%fused_computation.24 | convolution fusion | flops 203718656 | bytes 495616 | tf_op jit(solution)/shard_map/gci,gip->cp/dot_general | solution.py:55
  39.7 1.2 %convolution_bitcast_fusion = f32[5,16,128]{2,1,0:T(8,128)S(1)} fusion(f32[128,2048]{1,0:T(8,128)S(1)} %copy-done, f32[2048,16]{0,1:T(8,128)S(1)} %add_bitcast_fusion, f32[2048,5]{0,1:T(8,128)S(1)} %bitcast.71), kind=kOutput, calls=%fused_computation.31 | convolution fusion | flops 251822080 | bytes 1261568 | tf_op jit(solution)/shard_map/lp,cp,rp->lcr/dot_general | solution.py:110
  40.9 1.7 %collective-permute-start.8 = (f32[16]{0:T(128)S(1)}, f32[16]{0:T(128)S(1)}, u32[]{:S(2)}, u32[]{:S(2)}) collective-permute-start(f32[16]{0:T(128)S(1)} %add.207), channel_id=1, source_target_pairs={{0,8},{4,12},{8,0},{12,4},{16,24},{20,28},{24,16},{28,20},{1,9},{5... | collective-permute-start | bytes 200 | tf_op jit(solution)/shard_map/ppermute | solution.py:19
  42.7 1.9 %collective-permute-done.8 = f32[16]{0:T(128)S(1)} collective-permute-done((f32[16]{0:T(128)S(1)}, f32[16]{0:T(128)S(1)}, u32[]{:S(2)}, u32[]{:S(2)}) %collective-permute-start.8) | collective-permute-done | bytes 96 | tf_op jit(solution)/shard_map/ppermute | solution.py:19
  44.5 1.7 %collective-permute-start.9 = (f32[16]{0:T(128)S(1)}, f32[16]{0:T(128)S(1)}, u32[]{:S(2)}, u32[]{:S(2)}) collective-permute-start(f32[16]{0:T(128)S(1)} %add.210), channel_id=1, source_target_pairs={{0,16},{4,20},{8,24},{12,28},{16,0},{20,4},{24,8},{28,12},{1,17},{... | collective-permute-start | bytes 200 | tf_op jit(solution)/shard_map/ppermute | solution.py:19
  46.3 1.7 %collective-permute-done.9 = f32[16]{0:T(128)S(1)} collective-permute-done((f32[16]{0:T(128)S(1)}, f32[16]{0:T(128)S(1)}, u32[]{:S(2)}, u32[]{:S(2)}) %collective-permute-start.9) | collective-permute-done | bytes 96 | tf_op jit(solution)/shard_map/ppermute | solution.py:19
  49.0 1.8 %fusion.21 = f32[2,48,512]{2,1,0:T(8,128)S(1)} fusion(s32[2,512]{1,0:T(2,128)S(1)} %get-tuple-element.176, bf16[16,2048]{1,0:T(8,128)(2,1)S(1)} %get-tuple-element.155, bf16[16,2048]{1,0:T(8,128)(2,1)S(1)} %get-tuple-element.156, bf16[16,2048]{1,0:T(8,128)(2,1)S(1)} %get-tuple-element.154), kind=kOutput, calls=%fused_computation.29 | convolution fusion | flops 204013568 | bytes 397312 | tf_op jit(solution)/shard_map/cp,gip->gci/dot_general | solution.py:49
  50.8 1.7 %collective-permute-done.10 = f32[6,16,128]{2,1,0:T(8,128)S(1)} collective-permute-done((f32[6,16,128]{2,1,0:T(8,128)S(1)}, f32[6,16,128]{2,1,0:T(8,128)S(1)}, u32[]{:S(2)}, u32[]{:S(2)}) %collective-permute-start.10) | collective-permute-done | bytes 49184 | tf_op jit(solution)/shard_map/ppermute | solution.py:19
  52.6 2.5 %collective-permute-start.11 = (f32[5,16,128]{2,1,0:T(8,128)S(1)}, f32[5,16,128]{2,1,0:T(8,128)S(1)}, u32[]{:S(2)}, u32[]{:S(2)}) collective-permute-start(f32[5,16,128]{2,1,0:T(8,128)S(1)} %slice.203), channel_id=1, source_target_pairs={{0,2},{1,3},{2,0},{3,1},{4,6},{5,7},{6,4},{7,5},{8,10},{9,11},{10,... | collective-permute-start | bytes 122888 | tf_op jit(solution)/shard_map/ppermute | solution.py:19
  55.1 1.8 %fusion.22 = f32[2,48,512]{2,1,0:T(8,128)S(1)} fusion(s32[2,512]{1,0:T(2,128)S(1)} %get-tuple-element.175, bf16[16,2048]{1,0:T(8,128)(2,1)S(1)} %get-tuple-element.152, bf16[16,2048]{1,0:T(8,128)(2,1)S(1)} %get-tuple-element.153, bf16[16,2048]{1,0:T(8,128)(2,1)S(1)} %get-tuple-element.151), kind=kOutput, calls=%fused_computation.30 | convolution fusion | flops 204013568 | bytes 397312 | tf_op jit(solution)/shard_map/cp,gip->gci/dot_general | solution.py:49
  57.0 0.9 %collective-permute-done.11 = f32[5,16,128]{2,1,0:T(8,128)S(1)} collective-permute-done((f32[5,16,128]{2,1,0:T(8,128)S(1)}, f32[5,16,128]{2,1,0:T(8,128)S(1)}, u32[]{:S(2)}, u32[]{:S(2)}) %collective-permute-start.11) | collective-permute-done | bytes 40992 | tf_op jit(solution)/shard_map/ppermute | solution.py:19
  58.0 1.2 %collective-permute-done.12 = f32[4,16,128]{2,1,0:T(8,128)S(1)} collective-permute-done((f32[4,16,128]{2,1,0:T(8,128)S(1)}, f32[4,16,128]{2,1,0:T(8,128)S(1)}, u32[]{:S(2)}, u32[]{:S(2)}) %collective-permute-start.12) | collective-permute-done | bytes 32800 | tf_op jit(solution)/shard_map/ppermute | solution.py:19
  59.2 1.7 %collective-permute-start.13 = (f32[3,16,128]{2,1,0:T(8,128)S(1)}, f32[3,16,128]{2,1,0:T(8,128)S(1)}, u32[]{:S(2)}, u32[]{:S(2)}) collective-permute-start(f32[3,16,128]{2,1,0:T(8,128)S(1)} %slice.249), channel_id=1, source_target_pairs={{0,8},{4,12},{8,0},{12,4},{16,24},{20,28},{24,16},{28,20},{1,9},{5... | collective-permute-start | bytes 73736 | tf_op jit(solution)/shard_map/ppermute | solution.py:19
  61.0 2.1 %fusion.97 = f32[4,16,512]{2,1,0:T(8,128)S(1)} fusion(f32[4,16,512]{2,1,0:T(8,128)S(1)} %constant_dynamic-update-slice_fusion.16, f32[4,512,512]{2,1,0:T(8,128)S(1)} %exponential_multiply_fusion), kind=kOutput, calls=%fused_computation.221 | convolution fusion | flops 100663296 | bytes 4456448 | tf_op jit(solution)/shard_map/gij,gcj->gci/dot_general | solution.py:40
  63.1 1.8 %collective-permute-start.14 = (f32[2,16,128]{2,1,0:T(8,128)S(1)}, f32[2,16,128]{2,1,0:T(8,128)S(1)}, u32[]{:S(2)}, u32[]{:S(2)}) collective-permute-start(f32[2,16,128]{2,1,0:T(8,128)S(1)} %slice.212), channel_id=1, source_target_pairs={{0,16},{4,20},{8,24},{12,28},{16,0},{20,4},{24,8},{28,12},{1,17},{... | collective-permute-start | bytes 49160 | tf_op jit(solution)/shard_map/ppermute | solution.py:19
  64.9 2.0 %collective-permute-done.14 = f32[2,16,128]{2,1,0:T(8,128)S(1)} collective-permute-done((f32[2,16,128]{2,1,0:T(8,128)S(1)}, f32[2,16,128]{2,1,0:T(8,128)S(1)}, u32[]{:S(2)}, u32[]{:S(2)}) %collective-permute-start.14) | collective-permute-done | bytes 16416 | tf_op jit(solution)/shard_map/ppermute | solution.py:19
  67.5 0.6 convolution_multiply_fusion.2
  68.1 0.8 fusion.20
  69.6 1.8 %fusion.15 = f32[48,2048]{1,0:T(8,128)S(1)} fusion(s32[2,512]{1,0:T(2,128)S(1)} %get-tuple-element.176, bf16[2,16,512]{2,1,0:T(8,128)(2,1)S(1)} %get-tuple-element.149, bf16[2,16,512]{2,1,0:T(8,128)(2,1)S(1)} %get-tuple-element.150, bf16[2,16,512]{2,1,0:T(8,128)(2,1)S(1)} %get-tuple-element.148), kind=kOutput, calls=%fused_computation.23 | convolution fusion | flops 203718656 | bytes 495616 | tf_op jit(solution)/shard_map/gci,gip->cp/dot_general | solution.py:55
  71.4 1.5 %collective-permute-done.15 = f32[16]{0:T(128)S(1)} collective-permute-done((f32[16]{0:T(128)S(1)}, f32[16]{0:T(128)S(1)}, u32[]{:S(2)}, u32[]{:S(2)}) %collective-permute-start.15) | collective-permute-done | bytes 96 | tf_op jit(solution)/shard_map/ppermute | solution.py:19
  72.9 2.1 %collective-permute-start.16 = (f32[16]{0:T(128)S(1)}, f32[16]{0:T(128)S(1)}, u32[]{:S(2)}, u32[]{:S(2)}) collective-permute-start(f32[16]{0:T(128)S(1)} %add.228), channel_id=1, source_target_pairs={{0,2},{1,3},{2,0},{3,1},{4,6},{5,7},{6,4},{7,5},{8,10},{9,11},{10,... | collective-permute-start | bytes 200 | tf_op jit(solution)/shard_map/ppermute | solution.py:19
  75.1 1.8 %fusion.17 = f32[48,2048]{1,0:T(8,128)S(1)} fusion(s32[2,512]{1,0:T(2,128)S(1)} %get-tuple-element.175, bf16[2,16,512]{2,1,0:T(8,128)(2,1)S(1)} %get-tuple-element.146, bf16[2,16,512]{2,1,0:T(8,128)(2,1)S(1)} %get-tuple-element.147, bf16[2,16,512]{2,1,0:T(8,128)(2,1)S(1)} %get-tuple-element.145), kind=kOutput, calls=%fused_computation.25 | convolution fusion | flops 203718656 | bytes 495616 | tf_op jit(solution)/shard_map/gci,gip->cp/dot_general | solution.py:55
  77.4 1.1 %collective-permute-done.17 = f32[16]{0:T(128)S(1)} collective-permute-done((f32[16]{0:T(128)S(1)}, f32[16]{0:T(128)S(1)}, u32[]{:S(2)}, u32[]{:S(2)}) %collective-permute-start.17) | collective-permute-done | bytes 96 | tf_op jit(solution)/shard_map/ppermute | solution.py:19
  78.5 1.7 %collective-permute-start.18 = (f32[16]{0:T(128)S(1)}, f32[16]{0:T(128)S(1)}, u32[]{:S(2)}, u32[]{:S(2)}) collective-permute-start(f32[16]{0:T(128)S(1)} %add.236), channel_id=1, source_target_pairs={{0,8},{4,12},{8,0},{12,4},{16,24},{20,28},{24,16},{28,20},{1,9},{5... | collective-permute-start | bytes 200 | tf_op jit(solution)/shard_map/ppermute | solution.py:19
  80.2 1.9 %collective-permute-done.18 = f32[16]{0:T(128)S(1)} collective-permute-done((f32[16]{0:T(128)S(1)}, f32[16]{0:T(128)S(1)}, u32[]{:S(2)}, u32[]{:S(2)}) %collective-permute-start.18) | collective-permute-done | bytes 96 | tf_op jit(solution)/shard_map/ppermute | solution.py:19
  82.1 1.7 %collective-permute-start.19 = (f32[16]{0:T(128)S(1)}, f32[16]{0:T(128)S(1)}, u32[]{:S(2)}, u32[]{:S(2)}) collective-permute-start(f32[16]{0:T(128)S(1)} %add.237), channel_id=1, source_target_pairs={{0,16},{4,20},{8,24},{12,28},{16,0},{20,4},{24,8},{28,12},{1,17},{... | collective-permute-start | bytes 200 | tf_op jit(solution)/shard_map/ppermute | solution.py:19
  83.7 1.9 %collective-permute-done.19 = f32[16]{0:T(128)S(1)} collective-permute-done((f32[16]{0:T(128)S(1)}, f32[16]{0:T(128)S(1)}, u32[]{:S(2)}, u32[]{:S(2)}) %collective-permute-start.19) | collective-permute-done | bytes 96 | tf_op jit(solution)/shard_map/ppermute | solution.py:19
  85.6 0.8 multiply_subtract_fusion
  (123 shorter events, 6.4 us)
Async XLA Ops:
  0.6 2.0 %copy-start = (f32[128,2048]{1,0:T(8,128)S(1)}, f32[128,2048]{1,0:T(8,128)}, u32[]{:S(2)}) copy-start(f32[128,2048]{1,0:T(8,128)} %param.13) | copy-start | bytes 3145732
  4.8 10.5 %copy-start.5 = (f32[8]{0:T(128)S(1)}, f32[8]{0:T(128)}, u32[]{:S(2)}) copy-start(f32[8]{0:T(128)} %param.10) | copy-start | bytes 100
  4.8 10.6 %collective-permute-start = (f32[6,16,128]{2,1,0:T(8,128)S(1)}, f32[6,16,128]{2,1,0:T(8,128)S(1)}, u32[]{:S(2)}, u32[]{:S(2)}) collective-permute-start(f32[6,16,128]{2,1,0:T(8,128)S(1)} %pad_maximum_fusion), channel_id=1, source_target_pairs={{0,1},{1,0},{2,3},{3,2},{4,5},{5,4},{6,7},{7,6},{8,9},{9,8},{10,11... | collective-permute-start | bytes 147464 | tf_op jit(solution)/shard_map/ppermute | solution.py:19
  15.5 5.0 %collective-permute-start.1 = (f32[5,16,128]{2,1,0:T(8,128)S(1)}, f32[5,16,128]{2,1,0:T(8,128)S(1)}, u32[]{:S(2)}, u32[]{:S(2)}) collective-permute-start(f32[5,16,128]{2,1,0:T(8,128)S(1)} %slice.178), channel_id=1, source_target_pairs={{0,2},{1,3},{2,0},{3,1},{4,6},{5,7},{6,4},{7,5},{8,10},{9,11},{10,... | collective-permute-start | bytes 122888 | tf_op jit(solution)/shard_map/ppermute | solution.py:19
  19.9 9.6 %copy-start.2 = (f32[5,128,128]{2,1,0:T(8,128)S(1)}, f32[5,128,128]{2,1,0:T(8,128)}, u32[]{:S(2)}) copy-start(f32[5,128,128]{2,1,0:T(8,128)} %param.15) | copy-start | bytes 983044
  19.9 10.6 %copy-start.3 = (f32[5,2048]{1,0:T(8,128)S(1)}, f32[5,2048]{1,0:T(8,128)}, u32[]{:S(2)}) copy-start(f32[5,2048]{1,0:T(8,128)} %param.14) | copy-start | bytes 122884
  19.9 11.4 %copy-start.1 = (f32[16,2048]{1,0:T(8,128)S(1)}, f32[16,2048]{1,0:T(8,128)}, u32[]{:S(2)}) copy-start(f32[16,2048]{1,0:T(8,128)} %param.12) | copy-start | bytes 393220
  20.0 11.4 %copy-start.4 = (f32[2048]{0:T(1024)S(1)}, f32[2048]{0:T(1024)}, u32[]{:S(2)}) copy-start(f32[2048]{0:T(1024)} %param.11) | copy-start | bytes 24580
  20.5 1.3 %collective-permute-start.2 = (f32[4,16,128]{2,1,0:T(8,128)S(1)}, f32[4,16,128]{2,1,0:T(8,128)S(1)}, u32[]{:S(2)}, u32[]{:S(2)}) collective-permute-start(f32[4,16,128]{2,1,0:T(8,128)S(1)} %slice.180), channel_id=1, source_target_pairs={{0,4},{4,0},{8,12},{12,8},{16,20},{20,16},{24,28},{28,24},{1,5},{5... | collective-permute-start | bytes 98312 | tf_op jit(solution)/shard_map/ppermute | solution.py:19
  21.8 3.9 %collective-permute-start.3 = (f32[3,16,128]{2,1,0:T(8,128)S(1)}, f32[3,16,128]{2,1,0:T(8,128)S(1)}, u32[]{:S(2)}, u32[]{:S(2)}) collective-permute-start(f32[3,16,128]{2,1,0:T(8,128)S(1)} %slice.233), channel_id=1, source_target_pairs={{0,8},{4,12},{8,0},{12,4},{16,24},{20,28},{24,16},{28,20},{1,9},{5... | collective-permute-start | bytes 73736 | tf_op jit(solution)/shard_map/ppermute | solution.py:19
  25.7 3.8 %collective-permute-start.4 = (f32[2,16,128]{2,1,0:T(8,128)S(1)}, f32[2,16,128]{2,1,0:T(8,128)S(1)}, u32[]{:S(2)}, u32[]{:S(2)}) collective-permute-start(f32[2,16,128]{2,1,0:T(8,128)S(1)} %slice.184), channel_id=1, source_target_pairs={{0,16},{4,20},{8,24},{12,28},{16,0},{20,4},{24,8},{28,12},{1,17},{... | collective-permute-start | bytes 49160 | tf_op jit(solution)/shard_map/ppermute | solution.py:19
  31.5 3.6 %collective-permute-start.5 = (f32[16]{0:T(128)S(1)}, f32[16]{0:T(128)S(1)}, u32[]{:S(2)}, u32[]{:S(2)}) collective-permute-start(f32[16]{0:T(128)S(1)} %add.198), channel_id=1, source_target_pairs={{0,1},{1,0},{2,3},{3,2},{4,5},{5,4},{6,7},{7,6},{8,9},{9,8},{10,11... | collective-permute-start | bytes 200 | tf_op jit(solution)/shard_map/ppermute | solution.py:19
  35.1 4.5 %collective-permute-start.6 = (f32[16]{0:T(128)S(1)}, f32[16]{0:T(128)S(1)}, u32[]{:S(2)}, u32[]{:S(2)}) collective-permute-start(f32[16]{0:T(128)S(1)} %add.199), channel_id=1, source_target_pairs={{0,2},{1,3},{2,0},{3,1},{4,6},{5,7},{6,4},{7,5},{8,10},{9,11},{10,... | collective-permute-start | bytes 200 | tf_op jit(solution)/shard_map/ppermute | solution.py:19
  39.6 1.3 %collective-permute-start.7 = (f32[16]{0:T(128)S(1)}, f32[16]{0:T(128)S(1)}, u32[]{:S(2)}, u32[]{:S(2)}) collective-permute-start(f32[16]{0:T(128)S(1)} %add.203), channel_id=1, source_target_pairs={{0,4},{4,0},{8,12},{12,8},{16,20},{20,16},{24,28},{28,24},{1,5},{5... | collective-permute-start | bytes 200 | tf_op jit(solution)/shard_map/ppermute | solution.py:19
  40.9 3.6 %collective-permute-start.8 = (f32[16]{0:T(128)S(1)}, f32[16]{0:T(128)S(1)}, u32[]{:S(2)}, u32[]{:S(2)}) collective-permute-start(f32[16]{0:T(128)S(1)} %add.207), channel_id=1, source_target_pairs={{0,8},{4,12},{8,0},{12,4},{16,24},{20,28},{24,16},{28,20},{1,9},{5... | collective-permute-start | bytes 200 | tf_op jit(solution)/shard_map/ppermute | solution.py:19
  44.5 3.5 %collective-permute-start.9 = (f32[16]{0:T(128)S(1)}, f32[16]{0:T(128)S(1)}, u32[]{:S(2)}, u32[]{:S(2)}) collective-permute-start(f32[16]{0:T(128)S(1)} %add.210), channel_id=1, source_target_pairs={{0,16},{4,20},{8,24},{12,28},{16,0},{20,4},{24,8},{28,12},{1,17},{... | collective-permute-start | bytes 200 | tf_op jit(solution)/shard_map/ppermute | solution.py:19
  48.4 4.1 %collective-permute-start.10 = (f32[6,16,128]{2,1,0:T(8,128)S(1)}, f32[6,16,128]{2,1,0:T(8,128)S(1)}, u32[]{:S(2)}, u32[]{:S(2)}) collective-permute-start(f32[6,16,128]{2,1,0:T(8,128)S(1)} %pad_maximum_fusion.4), channel_id=1, source_target_pairs={{0,1},{1,0},{2,3},{3,2},{4,5},{5,4},{6,7},{7,6},{8,9},{9,8},{10,11... | collective-permute-start | bytes 147464 | tf_op jit(solution)/shard_map/ppermute | solution.py:19
  52.6 5.3 %collective-permute-start.11 = (f32[5,16,128]{2,1,0:T(8,128)S(1)}, f32[5,16,128]{2,1,0:T(8,128)S(1)}, u32[]{:S(2)}, u32[]{:S(2)}) collective-permute-start(f32[5,16,128]{2,1,0:T(8,128)S(1)} %slice.203), channel_id=1, source_target_pairs={{0,2},{1,3},{2,0},{3,1},{4,6},{5,7},{6,4},{7,5},{8,10},{9,11},{10,... | collective-permute-start | bytes 122888 | tf_op jit(solution)/shard_map/ppermute | solution.py:19
  57.9 1.3 %collective-permute-start.12 = (f32[4,16,128]{2,1,0:T(8,128)S(1)}, f32[4,16,128]{2,1,0:T(8,128)S(1)}, u32[]{:S(2)}, u32[]{:S(2)}) collective-permute-start(f32[4,16,128]{2,1,0:T(8,128)S(1)} %slice.208), channel_id=1, source_target_pairs={{0,4},{4,0},{8,12},{12,8},{16,20},{20,16},{24,28},{28,24},{1,5},{5... | collective-permute-start | bytes 98312 | tf_op jit(solution)/shard_map/ppermute | solution.py:19
  59.2 3.9 %collective-permute-start.13 = (f32[3,16,128]{2,1,0:T(8,128)S(1)}, f32[3,16,128]{2,1,0:T(8,128)S(1)}, u32[]{:S(2)}, u32[]{:S(2)}) collective-permute-start(f32[3,16,128]{2,1,0:T(8,128)S(1)} %slice.249), channel_id=1, source_target_pairs={{0,8},{4,12},{8,0},{12,4},{16,24},{20,28},{24,16},{28,20},{1,9},{5... | collective-permute-start | bytes 73736 | tf_op jit(solution)/shard_map/ppermute | solution.py:19
  63.1 3.8 %collective-permute-start.14 = (f32[2,16,128]{2,1,0:T(8,128)S(1)}, f32[2,16,128]{2,1,0:T(8,128)S(1)}, u32[]{:S(2)}, u32[]{:S(2)}) collective-permute-start(f32[2,16,128]{2,1,0:T(8,128)S(1)} %slice.212), channel_id=1, source_target_pairs={{0,16},{4,20},{8,24},{12,28},{16,0},{20,4},{24,8},{28,12},{1,17},{... | collective-permute-start | bytes 49160 | tf_op jit(solution)/shard_map/ppermute | solution.py:19
  69.3 3.6 %collective-permute-start.15 = (f32[16]{0:T(128)S(1)}, f32[16]{0:T(128)S(1)}, u32[]{:S(2)}, u32[]{:S(2)}) collective-permute-start(f32[16]{0:T(128)S(1)} %add.227), channel_id=1, source_target_pairs={{0,1},{1,0},{2,3},{3,2},{4,5},{5,4},{6,7},{7,6},{8,9},{9,8},{10,11... | collective-permute-start | bytes 200 | tf_op jit(solution)/shard_map/ppermute | solution.py:19
  72.9 4.4 %collective-permute-start.16 = (f32[16]{0:T(128)S(1)}, f32[16]{0:T(128)S(1)}, u32[]{:S(2)}, u32[]{:S(2)}) collective-permute-start(f32[16]{0:T(128)S(1)} %add.228), channel_id=1, source_target_pairs={{0,2},{1,3},{2,0},{3,1},{4,6},{5,7},{6,4},{7,5},{8,10},{9,11},{10,... | collective-permute-start | bytes 200 | tf_op jit(solution)/shard_map/ppermute | solution.py:19
  77.4 1.1 %collective-permute-start.17 = (f32[16]{0:T(128)S(1)}, f32[16]{0:T(128)S(1)}, u32[]{:S(2)}, u32[]{:S(2)}) collective-permute-start(f32[16]{0:T(128)S(1)} %add.232), channel_id=1, source_target_pairs={{0,4},{4,0},{8,12},{12,8},{16,20},{20,16},{24,28},{28,24},{1,5},{5... | collective-permute-start | bytes 200 | tf_op jit(solution)/shard_map/ppermute | solution.py:19
  78.5 3.5 %collective-permute-start.18 = (f32[16]{0:T(128)S(1)}, f32[16]{0:T(128)S(1)}, u32[]{:S(2)}, u32[]{:S(2)}) collective-permute-start(f32[16]{0:T(128)S(1)} %add.236), channel_id=1, source_target_pairs={{0,8},{4,12},{8,0},{12,4},{16,24},{20,28},{24,16},{28,20},{1,9},{5... | collective-permute-start | bytes 200 | tf_op jit(solution)/shard_map/ppermute | solution.py:19
  82.1 3.5 %collective-permute-start.19 = (f32[16]{0:T(128)S(1)}, f32[16]{0:T(128)S(1)}, u32[]{:S(2)}, u32[]{:S(2)}) collective-permute-start(f32[16]{0:T(128)S(1)} %add.237), channel_id=1, source_target_pairs={{0,16},{4,20},{8,24},{12,28},{16,0},{20,4},{24,8},{28,12},{1,17},{... | collective-permute-start | bytes 200 | tf_op jit(solution)/shard_map/ppermute | solution.py:19

commit v15 on v14

--- a/solution.py
+++ b/solution.py
@@ -140,8 +140,8 @@
         late, near, extra = state
         return late, near + from_union(late[half:], hot_second), extra
 
-    def permute_inputs(unused):
-        stacked = to_union(jnp.concatenate([coords, right_side], axis=0), hot)
+    def permute_inputs(state):
+        stacked = to_union(jnp.concatenate(state, axis=0), hot)
         return stacked[:, :features] * inv_scale[None, :, None], stacked[:, features:]
 
     def kernel_blocks(state):
@@ -158,9 +158,9 @@
     residual_proj = project(residual)
     for step in range(ITERATIONS):
         if step == 0:
-            stages = [permute_inputs, kernel_blocks, None, first_near]
+            stages = [None, permute_inputs, kernel_blocks, first_near]
             nodesum, norm_now, (kern, direction_u, near_u) = sums_with_norm(
-                residual, residual_proj, stages, jnp.zeros((), jnp.float32)
+                residual, residual_proj, stages, (coords, right_side)
             )
             late_u, nodesum = lax.optimization_barrier((near_u, nodesum))
             carried = jnp.zeros_like(right_side)

time: 86.7 us -> 86.1 us (level)
  starting transfers between devices: 28.2 us -> 20.5 us
  waiting for transfers between devices: 21.5 us -> 27.4 us
  local copies, waits for them, and re-layouts: 3.01 us -> 4.01 us
    ppermute x20, starting transfers between devices: 28.2 us -> 20.5 us  [swapped(): return lax.ppermute(value, axis, pairs)]
    ppermute x20, waiting for transfers between devices: 21.5 us -> 27.4 us  [swapped(): return lax.ppermute(value, axis, pairs)]
    reduce_sum x1 -> x2, other arithmetic: 0.21 us -> 1.33 us  [sums_with_norm(): norm = jnp.sum(values * values, axis=1)]
    concatenate x1 -> x0, other arithmetic: 1.03 us -> none  [permute_inputs(): stacked = to_union(jnp.concatenate([coords, right_side], axis=0), hot)]
    concatenate x0 -> x1, local copies, waits for them, and re-layouts: none -> 0.93 us  [permute_inputs(): stacked = to_union(jnp.concatenate(state, axis=0), hot)]
  transfers between devices with their start and end apart: 20 -> 20, of which waited for: 17 -> 16; matrix products, arithmetic and copies ran while one was open for 30% -> 32% of each run, Pallas kernels for 0% -> 0%
where the time goes in v15:
time: 86.1 us; the launch traced here: 85.8 us
  waiting for transfers between devices  27.4 us (32%)
  matrix products  26.8 us (31%)
  starting transfers between devices  20.5 us (24%)
  other arithmetic  5.9 us (7%)
  local copies, waits for them, and re-layouts  4.01 us (5%)
  between operations  1.22 us (1%)
    ppermute x20, waiting for transfers between devices, swapped(): return lax.ppermute(value, axis, pairs)  27.4 us
    ppermute x20, starting transfers between devices, swapped(): return lax.ppermute(value, axis, pairs)  20.5 us
    dot_general x4, matrix products, from_union(): jnp.einsum('gci,gip->cp', pieces(values_u, 1), hot, preferred_element_typ...  7.27 us
    dot_general x3, matrix products, to_union(): jnp.einsum('cp,gip->gci', pieces(values, 0), hot, preferred_element_type=...  7.1 us
    dot_general x2, matrix products, near_apply(): jnp.einsum('gij,gcj->gci', kern, union_vec, precision=lax.Precision.HIGH)  3.91 us
    dot_general x2, matrix products, project(): jnp.einsum('lp,cp,rp->lcr', level_gain, values, basis, precision=highest)  3.33 us
  transfers between devices with their start and end apart: 20, of which 16 were waited for; matrix products, arithmetic and copies ran while one was open for 32% of the time, Pallas kernels for 0%

profile of v15, /device:TPU:0, one launch (start us, length us, event | category | flops | bytes accessed | tf_op | source)
XLA Modules:
  0.0 85.8 jit_solution(516710789227271017)
XLA Ops:
  0.6 1.1 %multiply_reduce_fusion.5 = f32[16]{0:T(128)S(1)} fusion(f32[16,2048]{1,0:T(8,128)} %param.12), kind=kLoop, calls=%fused_computation.103 | loop fusion | flops 65520 | bytes 131136 | tf_op jit(solution)/shard_map/reduce_sum | solution.py:113
  1.9 2.1 %convolution_bitcast_fusion.1 = f32[5,16,128]{2,1,0:T(8,128)S(1)} fusion(f32[128,2048]{1,0:T(8,128)S(1)} %copy-done, f32[2048,5]{0,1:T(8,128)} %bitcast.70, f32[2048,16]{0,1:T(8,128)} %bitcast.69), kind=kOutput, calls=%fused_computation.32 | convolution fusion | flops 251822080 | bytes 1261568 | tf_op jit(solution)/shard_map/lp,cp,rp->lcr/dot_general | solution.py:110
  4.1 3.0 %collective-permute-start = (f32[6,16,128]{2,1,0:T(8,128)S(1)}, f32[6,16,128]{2,1,0:T(8,128)S(1)}, u32[]{:S(2)}, u32[]{:S(2)}) collective-permute-start(f32[6,16,128]{2,1,0:T(8,128)S(1)} %pad_maximum_fusion), channel_id=1, source_target_pairs={{0,1},{1,0},{2,3},{3,2},{4,5},{5,4},{6,7},{7,6},{8,9},{9,8},{10,11... | collective-permute-start | bytes 147464 | tf_op jit(solution)/shard_map/ppermute | solution.py:19
  7.7 1.4 %reduce.9 = s32[2048]{0:T(1024)S(1)} reduce(s32[1,2048]{1,0:T(1,128)} %param.16, s32[]{:T(128)} %broadcast.100), dimensions={0}, to_apply=%param.16.reduce_sub_computation.3 | reduce | bytes 16388 | tf_op args[7]
  9.1 0.8 fusion.84
  9.8 0.6 gather_fusion
  10.4 0.6 gather_fusion.1
  11.0 2.7 %collective-permute-start.1 = (f32[5,16,128]{2,1,0:T(8,128)S(1)}, f32[5,16,128]{2,1,0:T(8,128)S(1)}, u32[]{:S(2)}, u32[]{:S(2)}) collective-permute-start(f32[5,16,128]{2,1,0:T(8,128)S(1)} %slice.231), channel_id=1, source_target_pairs={{0,2},{1,3},{2,0},{3,1},{4,6},{5,7},{6,4},{7,5},{8,10},{9,11},{10,... | collective-permute-start | bytes 122888 | tf_op jit(solution)/shard_map/ppermute | solution.py:19
  13.7 0.8 constant_dynamic-update-slice_fusion.3
  14.5 0.9 %constant_dynamic-update-slice_fusion.2 = f32[24,2048]{1,0:T(8,128)S(1)} fusion(f32[24,2048]{1,0:T(8,128)S(1)} %constant_dynamic-update-slice_fusion.3, f32[16,2048]{1,0:T(8,128)} %param.12), kind=kLoop, calls=%fused_computation.174 | loop fusion | bytes 262144 | tf_op jit(solution)/shard_map/concatenate | solution.py:144
  15.5 3.5 %fusion.18 = f32[4,72,512]{2,1,0:T(8,128)S(1)} fusion(s32[4,512]{1,0:T(4,128)S(1)} %constant_dynamic-update-slice_fusion, bf16[24,2048]{1,0:T(8,128)(2,1)S(1)} %get-tuple-element.147, bf16[24,2048]{1,0:T(8,128)(2,1)S(1)} %get-tuple-element.148, bf16[24,2048]{1,0:T(8,128)(2,1)S(1)} %get-tuple-element.146), kind=kOutput, calls=%fused_computation.26 | convolution fusion | flops 609058816 | bytes 892928 | tf_op jit(solution)/shard_map/cp,gip->gci/dot_general | solution.py:49
  19.5 1.6 %exponential_multiply_fusion = f32[4,512,512]{2,1,0:T(8,128)S(1)} fusion(bf16[4,48,512]{2,1,0:T(8,128)(2,1)S(1)} %get-tuple-element.174, bf16[4,48,512]{2,1,0:T(8,128)(2,1)S(1)} %get-tuple-element.173, f32[4,512]{1,0:T(4,128)S(1)} %multiply_reduce_fusion.6), kind=kOutput, calls=%fused_computation.19 | convolution fusion | flops 105906176 | bytes 4595712 | tf_op jit(solution)/shard_map/gfi,gfj->gij/dot_general | solution.py:33
  21.2 1.6 %collective-permute-start.3 = (f32[3,16,128]{2,1,0:T(8,128)S(1)}, f32[3,16,128]{2,1,0:T(8,128)S(1)}, u32[]{:S(2)}, u32[]{:S(2)}) collective-permute-start(f32[3,16,128]{2,1,0:T(8,128)S(1)} %slice.186), channel_id=1, source_target_pairs={{0,8},{4,12},{8,0},{12,4},{16,24},{20,28},{24,16},{28,20},{1,9},{5... | collective-permute-start | bytes 73736 | tf_op jit(solution)/shard_map/ppermute | solution.py:19
  22.8 1.8 %fusion.96 = f32[4,16,512]{2,1,0:T(8,128)S(1)} fusion(f32[4,16,512]{2,1,0:T(8,128)S(1)} %slice.236, f32[4,512,512]{2,1,0:T(8,128)S(1)} %exponential_multiply_fusion), kind=kOutput, calls=%fused_computation.220 | convolution fusion | flops 100663296 | bytes 4456448 | tf_op jit(solution)/shard_map/gij,gcj->gci/dot_general | solution.py:40
  25.1 1.6 %collective-permute-start.4 = (f32[2,16,128]{2,1,0:T(8,128)S(1)}, f32[2,16,128]{2,1,0:T(8,128)S(1)}, u32[]{:S(2)}, u32[]{:S(2)}) collective-permute-start(f32[2,16,128]{2,1,0:T(8,128)S(1)} %slice.187), channel_id=1, source_target_pairs={{0,16},{4,20},{8,24},{12,28},{16,0},{20,4},{24,8},{28,12},{1,17},{... | collective-permute-start | bytes 49160 | tf_op jit(solution)/shard_map/ppermute | solution.py:19
  26.9 2.1 %collective-permute-done.4 = f32[2,16,128]{2,1,0:T(8,128)S(1)} collective-permute-done((f32[2,16,128]{2,1,0:T(8,128)S(1)}, f32[2,16,128]{2,1,0:T(8,128)S(1)}, u32[]{:S(2)}, u32[]{:S(2)}) %collective-permute-start.4) | collective-permute-done | bytes 16416 | tf_op jit(solution)/shard_map/ppermute | solution.py:19
  29.3 0.6 convolution_multiply_fusion.3
  30.0 0.8 fusion.19
  31.4 1.8 %fusion.14 = f32[48,2048]{1,0:T(8,128)S(1)} fusion(s32[2,512]{1,0:T(2,128)S(1)} %get-tuple-element.178, bf16[2,16,512]{2,1,0:T(8,128)(2,1)S(1)} %get-tuple-element.165, bf16[2,16,512]{2,1,0:T(8,128)(2,1)S(1)} %get-tuple-element.166, bf16[2,16,512]{2,1,0:T(8,128)(2,1)S(1)} %get-tuple-element.164), kind=kOutput, calls=%fused_computation.22 | convolution fusion | flops 203718656 | bytes 495616 | tf_op jit(solution)/shard_map/gci,gip->cp/dot_general | solution.py:55
  33.3 1.2 %collective-permute-done.5 = f32[16]{0:T(128)S(1)} collective-permute-done((f32[16]{0:T(128)S(1)}, f32[16]{0:T(128)S(1)}, u32[]{:S(2)}, u32[]{:S(2)}) %collective-permute-start.5) | collective-permute-done | bytes 96 | tf_op jit(solution)/shard_map/ppermute | solution.py:19
  34.9 1.8 %fusion.16 = f32[48,2048]{1,0:T(8,128)S(1)} fusion(s32[2,512]{1,0:T(2,128)S(1)} %get-tuple-element.177, bf16[2,16,512]{2,1,0:T(8,128)(2,1)S(1)} %get-tuple-element.162, bf16[2,16,512]{2,1,0:T(8,128)(2,1)S(1)} %get-tuple-element.163, bf16[2,16,512]{2,1,0:T(8,128)(2,1)S(1)} %get-tuple-element.161), kind=kOutput, calls=%fused_computation.24 | convolution fusion | flops 203718656 | bytes 495616 | tf_op jit(solution)/shard_map/gci,gip->cp/dot_general | solution.py:55
  36.7 2.2 %collective-permute-done.6 = f32[16]{0:T(128)S(1)} collective-permute-done((f32[16]{0:T(128)S(1)}, f32[16]{0:T(128)S(1)}, u32[]{:S(2)}, u32[]{:S(2)}) %collective-permute-start.6) | collective-permute-done | bytes 96 | tf_op jit(solution)/shard_map/ppermute | solution.py:19
  39.0 1.2 %convolution_bitcast_fusion = f32[5,16,128]{2,1,0:T(8,128)S(1)} fusion(f32[128,2048]{1,0:T(8,128)S(1)} %copy-done, f32[2048,16]{0,1:T(8,128)S(1)} %add_bitcast_fusion, f32[2048,5]{0,1:T(8,128)S(1)} %bitcast.71), kind=kOutput, calls=%fused_computation.31 | convolution fusion | flops 251822080 | bytes 1261568 | tf_op jit(solution)/shard_map/lp,cp,rp->lcr/dot_general | solution.py:110
  40.2 1.6 %collective-permute-start.8 = (f32[16]{0:T(128)S(1)}, f32[16]{0:T(128)S(1)}, u32[]{:S(2)}, u32[]{:S(2)}) collective-permute-start(f32[16]{0:T(128)S(1)} %add.207), channel_id=1, source_target_pairs={{0,8},{4,12},{8,0},{12,4},{16,24},{20,28},{24,16},{28,20},{1,9},{5... | collective-permute-start | bytes 200 | tf_op jit(solution)/shard_map/ppermute | solution.py:19
  41.8 2.1 %collective-permute-done.8 = f32[16]{0:T(128)S(1)} collective-permute-done((f32[16]{0:T(128)S(1)}, f32[16]{0:T(128)S(1)}, u32[]{:S(2)}, u32[]{:S(2)}) %collective-permute-start.8) | collective-permute-done | bytes 96 | tf_op jit(solution)/shard_map/ppermute | solution.py:19
  43.8 1.5 %collective-permute-start.9 = (f32[16]{0:T(128)S(1)}, f32[16]{0:T(128)S(1)}, u32[]{:S(2)}, u32[]{:S(2)}) collective-permute-start(f32[16]{0:T(128)S(1)} %add.210), channel_id=1, source_target_pairs={{0,16},{4,20},{8,24},{12,28},{16,0},{20,4},{24,8},{28,12},{1,17},{... | collective-permute-start | bytes 200 | tf_op jit(solution)/shard_map/ppermute | solution.py:19
  45.5 1.9 %collective-permute-done.9 = f32[16]{0:T(128)S(1)} collective-permute-done((f32[16]{0:T(128)S(1)}, f32[16]{0:T(128)S(1)}, u32[]{:S(2)}, u32[]{:S(2)}) %collective-permute-start.9) | collective-permute-done | bytes 96 | tf_op jit(solution)/shard_map/ppermute | solution.py:19
  48.2 1.8 %fusion.21 = f32[2,48,512]{2,1,0:T(8,128)S(1)} fusion(s32[2,512]{1,0:T(2,128)S(1)} %get-tuple-element.178, bf16[16,2048]{1,0:T(8,128)(2,1)S(1)} %get-tuple-element.159, bf16[16,2048]{1,0:T(8,128)(2,1)S(1)} %get-tuple-element.160, bf16[16,2048]{1,0:T(8,128)(2,1)S(1)} %get-tuple-element.158), kind=kOutput, calls=%fused_computation.29 | convolution fusion | flops 204013568 | bytes 397312 | tf_op jit(solution)/shard_map/cp,gip->gci/dot_general | solution.py:49
  50.1 1.8 %collective-permute-done.10 = f32[6,16,128]{2,1,0:T(8,128)S(1)} collective-permute-done((f32[6,16,128]{2,1,0:T(8,128)S(1)}, f32[6,16,128]{2,1,0:T(8,128)S(1)}, u32[]{:S(2)}, u32[]{:S(2)}) %collective-permute-start.10) | collective-permute-done | bytes 49184 | tf_op jit(solution)/shard_map/ppermute | solution.py:19
  52.4 1.8 %fusion.22 = f32[2,48,512]{2,1,0:T(8,128)S(1)} fusion(s32[2,512]{1,0:T(2,128)S(1)} %get-tuple-element.177, bf16[16,2048]{1,0:T(8,128)(2,1)S(1)} %get-tuple-element.156, bf16[16,2048]{1,0:T(8,128)(2,1)S(1)} %get-tuple-element.157, bf16[16,2048]{1,0:T(8,128)(2,1)S(1)} %get-tuple-element.155), kind=kOutput, calls=%fused_computation.30 | convolution fusion | flops 204013568 | bytes 397312 | tf_op jit(solution)/shard_map/cp,gip->gci/dot_general | solution.py:49
  54.3 3.0 %collective-permute-done.11 = f32[5,16,128]{2,1,0:T(8,128)S(1)} collective-permute-done((f32[5,16,128]{2,1,0:T(8,128)S(1)}, f32[5,16,128]{2,1,0:T(8,128)S(1)}, u32[]{:S(2)}, u32[]{:S(2)}) %collective-permute-start.11) | collective-permute-done | bytes 40992 | tf_op jit(solution)/shard_map/ppermute | solution.py:19
  57.4 1.2 %collective-permute-done.12 = f32[4,16,128]{2,1,0:T(8,128)S(1)} collective-permute-done((f32[4,16,128]{2,1,0:T(8,128)S(1)}, f32[4,16,128]{2,1,0:T(8,128)S(1)}, u32[]{:S(2)}, u32[]{:S(2)}) %collective-permute-start.12) | collective-permute-done | bytes 32800 | tf_op jit(solution)/shard_map/ppermute | solution.py:19
  58.6 1.6 %collective-permute-start.13 = (f32[3,16,128]{2,1,0:T(8,128)S(1)}, f32[3,16,128]{2,1,0:T(8,128)S(1)}, u32[]{:S(2)}, u32[]{:S(2)}) collective-permute-start(f32[3,16,128]{2,1,0:T(8,128)S(1)} %slice.252), channel_id=1, source_target_pairs={{0,8},{4,12},{8,0},{12,4},{16,24},{20,28},{24,16},{28,20},{1,9},{5... | collective-permute-start | bytes 73736 | tf_op jit(solution)/shard_map/ppermute | solution.py:19
  60.2 2.1 %fusion.98 = f32[4,16,512]{2,1,0:T(8,128)S(1)} fusion(f32[4,16,512]{2,1,0:T(8,128)S(1)} %constant_dynamic-update-slice_fusion.16, f32[4,512,512]{2,1,0:T(8,128)S(1)} %exponential_multiply_fusion), kind=kOutput, calls=%fused_computation.222 | convolution fusion | flops 100663296 | bytes 4456448 | tf_op jit(solution)/shard_map/gij,gcj->gci/dot_general | solution.py:40
  62.5 1.6 %collective-permute-start.14 = (f32[2,16,128]{2,1,0:T(8,128)S(1)}, f32[2,16,128]{2,1,0:T(8,128)S(1)}, u32[]{:S(2)}, u32[]{:S(2)}) collective-permute-start(f32[2,16,128]{2,1,0:T(8,128)S(1)} %slice.215), channel_id=1, source_target_pairs={{0,16},{4,20},{8,24},{12,28},{16,0},{20,4},{24,8},{28,12},{1,17},{... | collective-permute-start | bytes 49160 | tf_op jit(solution)/shard_map/ppermute | solution.py:19
  64.1 2.2 %collective-permute-done.14 = f32[2,16,128]{2,1,0:T(8,128)S(1)} collective-permute-done((f32[2,16,128]{2,1,0:T(8,128)S(1)}, f32[2,16,128]{2,1,0:T(8,128)S(1)}, u32[]{:S(2)}, u32[]{:S(2)}) %collective-permute-start.14) | collective-permute-done | bytes 16416 | tf_op jit(solution)/shard_map/ppermute | solution.py:19
  66.9 0.6 convolution_multiply_fusion.2
  67.5 0.8 fusion.20
  69.2 1.8 %fusion.15 = f32[48,2048]{1,0:T(8,128)S(1)} fusion(s32[2,512]{1,0:T(2,128)S(1)} %get-tuple-element.178, bf16[2,16,512]{2,1,0:T(8,128)(2,1)S(1)} %get-tuple-element.153, bf16[2,16,512]{2,1,0:T(8,128)(2,1)S(1)} %get-tuple-element.154, bf16[2,16,512]{2,1,0:T(8,128)(2,1)S(1)} %get-tuple-element.152), kind=kOutput, calls=%fused_computation.23 | convolution fusion | flops 203718656 | bytes 495616 | tf_op jit(solution)/shard_map/gci,gip->cp/dot_general | solution.py:55
  71.1 1.3 %collective-permute-done.15 = f32[16]{0:T(128)S(1)} collective-permute-done((f32[16]{0:T(128)S(1)}, f32[16]{0:T(128)S(1)}, u32[]{:S(2)}, u32[]{:S(2)}) %collective-permute-start.15) | collective-permute-done | bytes 96 | tf_op jit(solution)/shard_map/ppermute | solution.py:19
  72.4 1.8 %fusion.17 = f32[48,2048]{1,0:T(8,128)S(1)} fusion(s32[2,512]{1,0:T(2,128)S(1)} %get-tuple-element.177, bf16[2,16,512]{2,1,0:T(8,128)(2,1)S(1)} %get-tuple-element.150, bf16[2,16,512]{2,1,0:T(8,128)(2,1)S(1)} %get-tuple-element.151, bf16[2,16,512]{2,1,0:T(8,128)(2,1)S(1)} %get-tuple-element.149), kind=kOutput, calls=%fused_computation.25 | convolution fusion | flops 203718656 | bytes 495616 | tf_op jit(solution)/shard_map/gci,gip->cp/dot_general | solution.py:55
  74.2 2.5 %collective-permute-done.16 = f32[16]{0:T(128)S(1)} collective-permute-done((f32[16]{0:T(128)S(1)}, f32[16]{0:T(128)S(1)}, u32[]{:S(2)}, u32[]{:S(2)}) %collective-permute-start.16) | collective-permute-done | bytes 96 | tf_op jit(solution)/shard_map/ppermute | solution.py:19
  76.8 1.1 %collective-permute-done.17 = f32[16]{0:T(128)S(1)} collective-permute-done((f32[16]{0:T(128)S(1)}, f32[16]{0:T(128)S(1)}, u32[]{:S(2)}, u32[]{:S(2)}) %collective-permute-start.17) | collective-permute-done | bytes 96 | tf_op jit(solution)/shard_map/ppermute | solution.py:19
  77.9 1.5 %collective-permute-start.18 = (f32[16]{0:T(128)S(1)}, f32[16]{0:T(128)S(1)}, u32[]{:S(2)}, u32[]{:S(2)}) collective-permute-start(f32[16]{0:T(128)S(1)} %add.236), channel_id=1, source_target_pairs={{0,8},{4,12},{8,0},{12,4},{16,24},{20,28},{24,16},{28,20},{1,9},{5... | collective-permute-start | bytes 200 | tf_op jit(solution)/shard_map/ppermute | solution.py:19
  79.4 2.1 %collective-permute-done.18 = f32[16]{0:T(128)S(1)} collective-permute-done((f32[16]{0:T(128)S(1)}, f32[16]{0:T(128)S(1)}, u32[]{:S(2)}, u32[]{:S(2)}) %collective-permute-start.18) | collective-permute-done | bytes 96 | tf_op jit(solution)/shard_map/ppermute | solution.py:19
  81.4 1.5 %collective-permute-start.19 = (f32[16]{0:T(128)S(1)}, f32[16]{0:T(128)S(1)}, u32[]{:S(2)}, u32[]{:S(2)}) collective-permute-start(f32[16]{0:T(128)S(1)} %add.237), channel_id=1, source_target_pairs={{0,16},{4,20},{8,24},{12,28},{16,0},{20,4},{24,8},{28,12},{1,17},{... | collective-permute-start | bytes 200 | tf_op jit(solution)/shard_map/ppermute | solution.py:19
  83.0 2.0 %collective-permute-done.19 = f32[16]{0:T(128)S(1)} collective-permute-done((f32[16]{0:T(128)S(1)}, f32[16]{0:T(128)S(1)}, u32[]{:S(2)}, u32[]{:S(2)}) %collective-permute-start.19) | collective-permute-done | bytes 96 | tf_op jit(solution)/shard_map/ppermute | solution.py:19
  85.0 0.8 multiply_subtract_fusion
  (124 shorter events, 6.9 us)
Async XLA Ops:
  0.6 1.3 %copy-start = (f32[128,2048]{1,0:T(8,128)S(1)}, f32[128,2048]{1,0:T(8,128)}, u32[]{:S(2)}) copy-start(f32[128,2048]{1,0:T(8,128)} %param.13) | copy-start | bytes 3145732
  4.1 6.9 %collective-permute-start = (f32[6,16,128]{2,1,0:T(8,128)S(1)}, f32[6,16,128]{2,1,0:T(8,128)S(1)}, u32[]{:S(2)}, u32[]{:S(2)}) collective-permute-start(f32[6,16,128]{2,1,0:T(8,128)S(1)} %pad_maximum_fusion), channel_id=1, source_target_pairs={{0,1},{1,0},{2,3},{3,2},{4,5},{5,4},{6,7},{7,6},{8,9},{9,8},{10,11... | collective-permute-start | bytes 147464 | tf_op jit(solution)/shard_map/ppermute | solution.py:19
  11.0 8.1 %collective-permute-start.1 = (f32[5,16,128]{2,1,0:T(8,128)S(1)}, f32[5,16,128]{2,1,0:T(8,128)S(1)}, u32[]{:S(2)}, u32[]{:S(2)}) collective-permute-start(f32[5,16,128]{2,1,0:T(8,128)S(1)} %slice.231), channel_id=1, source_target_pairs={{0,2},{1,3},{2,0},{3,1},{4,6},{5,7},{6,4},{7,5},{8,10},{9,11},{10,... | collective-permute-start | bytes 122888 | tf_op jit(solution)/shard_map/ppermute | solution.py:19
  14.5 4.5 %copy-start.5 = (f32[8]{0:T(128)S(1)}, f32[8]{0:T(128)}, u32[]{:S(2)}) copy-start(f32[8]{0:T(128)} %param.10) | copy-start | bytes 100
  19.3 1.9 %collective-permute-start.2 = (f32[4,16,128]{2,1,0:T(8,128)S(1)}, f32[4,16,128]{2,1,0:T(8,128)S(1)}, u32[]{:S(2)}, u32[]{:S(2)}) collective-permute-start(f32[4,16,128]{2,1,0:T(8,128)S(1)} %slice.183), channel_id=1, source_target_pairs={{0,4},{4,0},{8,12},{12,8},{16,20},{20,16},{24,28},{28,24},{1,5},{5... | collective-permute-start | bytes 98312 | tf_op jit(solution)/shard_map/ppermute | solution.py:19
  21.1 7.8 %copy-start.2 = (f32[5,128,128]{2,1,0:T(8,128)S(1)}, f32[5,128,128]{2,1,0:T(8,128)}, u32[]{:S(2)}) copy-start(f32[5,128,128]{2,1,0:T(8,128)} %param.15) | copy-start | bytes 983044
  21.1 8.8 %copy-start.3 = (f32[5,2048]{1,0:T(8,128)S(1)}, f32[5,2048]{1,0:T(8,128)}, u32[]{:S(2)}) copy-start(f32[5,2048]{1,0:T(8,128)} %param.14) | copy-start | bytes 122884
  21.1 9.6 %copy-start.1 = (f32[16,2048]{1,0:T(8,128)S(1)}, f32[16,2048]{1,0:T(8,128)}, u32[]{:S(2)}) copy-start(f32[16,2048]{1,0:T(8,128)} %param.12) | copy-start | bytes 393220
  21.2 9.6 %copy-start.4 = (f32[2048]{0:T(1024)S(1)}, f32[2048]{0:T(1024)}, u32[]{:S(2)}) copy-start(f32[2048]{0:T(1024)} %param.11) | copy-start | bytes 24580
  21.2 3.9 %collective-permute-start.3 = (f32[3,16,128]{2,1,0:T(8,128)S(1)}, f32[3,16,128]{2,1,0:T(8,128)S(1)}, u32[]{:S(2)}, u32[]{:S(2)}) collective-permute-start(f32[3,16,128]{2,1,0:T(8,128)S(1)} %slice.186), channel_id=1, source_target_pairs={{0,8},{4,12},{8,0},{12,4},{16,24},{20,28},{24,16},{28,20},{1,9},{5... | collective-permute-start | bytes 73736 | tf_op jit(solution)/shard_map/ppermute | solution.py:19
  25.1 3.8 %collective-permute-start.4 = (f32[2,16,128]{2,1,0:T(8,128)S(1)}, f32[2,16,128]{2,1,0:T(8,128)S(1)}, u32[]{:S(2)}, u32[]{:S(2)}) collective-permute-start(f32[2,16,128]{2,1,0:T(8,128)S(1)} %slice.187), channel_id=1, source_target_pairs={{0,16},{4,20},{8,24},{12,28},{16,0},{20,4},{24,8},{28,12},{1,17},{... | collective-permute-start | bytes 49160 | tf_op jit(solution)/shard_map/ppermute | solution.py:19
  30.9 3.6 %collective-permute-start.5 = (f32[16]{0:T(128)S(1)}, f32[16]{0:T(128)S(1)}, u32[]{:S(2)}, u32[]{:S(2)}) collective-permute-start(f32[16]{0:T(128)S(1)} %add.198), channel_id=1, source_target_pairs={{0,1},{1,0},{2,3},{3,2},{4,5},{5,4},{6,7},{7,6},{8,9},{9,8},{10,11... | collective-permute-start | bytes 200 | tf_op jit(solution)/shard_map/ppermute | solution.py:19
  34.5 4.4 %collective-permute-start.6 = (f32[16]{0:T(128)S(1)}, f32[16]{0:T(128)S(1)}, u32[]{:S(2)}, u32[]{:S(2)}) collective-permute-start(f32[16]{0:T(128)S(1)} %add.199), channel_id=1, source_target_pairs={{0,2},{1,3},{2,0},{3,1},{4,6},{5,7},{6,4},{7,5},{8,10},{9,11},{10,... | collective-permute-start | bytes 200 | tf_op jit(solution)/shard_map/ppermute | solution.py:19
  39.0 1.2 %collective-permute-start.7 = (f32[16]{0:T(128)S(1)}, f32[16]{0:T(128)S(1)}, u32[]{:S(2)}, u32[]{:S(2)}) collective-permute-start(f32[16]{0:T(128)S(1)} %add.203), channel_id=1, source_target_pairs={{0,4},{4,0},{8,12},{12,8},{16,20},{20,16},{24,28},{28,24},{1,5},{5... | collective-permute-start | bytes 200 | tf_op jit(solution)/shard_map/ppermute | solution.py:19
  40.2 3.6 %collective-permute-start.8 = (f32[16]{0:T(128)S(1)}, f32[16]{0:T(128)S(1)}, u32[]{:S(2)}, u32[]{:S(2)}) collective-permute-start(f32[16]{0:T(128)S(1)} %add.207), channel_id=1, source_target_pairs={{0,8},{4,12},{8,0},{12,4},{16,24},{20,28},{24,16},{28,20},{1,9},{5... | collective-permute-start | bytes 200 | tf_op jit(solution)/shard_map/ppermute | solution.py:19
  43.8 3.5 %collective-permute-start.9 = (f32[16]{0:T(128)S(1)}, f32[16]{0:T(128)S(1)}, u32[]{:S(2)}, u32[]{:S(2)}) collective-permute-start(f32[16]{0:T(128)S(1)} %add.210), channel_id=1, source_target_pairs={{0,16},{4,20},{8,24},{12,28},{16,0},{20,4},{24,8},{28,12},{1,17},{... | collective-permute-start | bytes 200 | tf_op jit(solution)/shard_map/ppermute | solution.py:19
  47.7 4.1 %collective-permute-start.10 = (f32[6,16,128]{2,1,0:T(8,128)S(1)}, f32[6,16,128]{2,1,0:T(8,128)S(1)}, u32[]{:S(2)}, u32[]{:S(2)}) collective-permute-start(f32[6,16,128]{2,1,0:T(8,128)S(1)} %pad_maximum_fusion.4), channel_id=1, source_target_pairs={{0,1},{1,0},{2,3},{3,2},{4,5},{5,4},{6,7},{7,6},{8,9},{9,8},{10,11... | collective-permute-start | bytes 147464 | tf_op jit(solution)/shard_map/ppermute | solution.py:19
  51.9 5.4 %collective-permute-start.11 = (f32[5,16,128]{2,1,0:T(8,128)S(1)}, f32[5,16,128]{2,1,0:T(8,128)S(1)}, u32[]{:S(2)}, u32[]{:S(2)}) collective-permute-start(f32[5,16,128]{2,1,0:T(8,128)S(1)} %slice.206), channel_id=1, source_target_pairs={{0,2},{1,3},{2,0},{3,1},{4,6},{5,7},{6,4},{7,5},{8,10},{9,11},{10,... | collective-permute-start | bytes 122888 | tf_op jit(solution)/shard_map/ppermute | solution.py:19
  57.3 1.3 %collective-permute-start.12 = (f32[4,16,128]{2,1,0:T(8,128)S(1)}, f32[4,16,128]{2,1,0:T(8,128)S(1)}, u32[]{:S(2)}, u32[]{:S(2)}) collective-permute-start(f32[4,16,128]{2,1,0:T(8,128)S(1)} %slice.211), channel_id=1, source_target_pairs={{0,4},{4,0},{8,12},{12,8},{16,20},{20,16},{24,28},{28,24},{1,5},{5... | collective-permute-start | bytes 98312 | tf_op jit(solution)/shard_map/ppermute | solution.py:19
  58.6 3.9 %collective-permute-start.13 = (f32[3,16,128]{2,1,0:T(8,128)S(1)}, f32[3,16,128]{2,1,0:T(8,128)S(1)}, u32[]{:S(2)}, u32[]{:S(2)}) collective-permute-start(f32[3,16,128]{2,1,0:T(8,128)S(1)} %slice.252), channel_id=1, source_target_pairs={{0,8},{4,12},{8,0},{12,4},{16,24},{20,28},{24,16},{28,20},{1,9},{5... | collective-permute-start | bytes 73736 | tf_op jit(solution)/shard_map/ppermute | solution.py:19
  62.5 3.8 %collective-permute-start.14 = (f32[2,16,128]{2,1,0:T(8,128)S(1)}, f32[2,16,128]{2,1,0:T(8,128)S(1)}, u32[]{:S(2)}, u32[]{:S(2)}) collective-permute-start(f32[2,16,128]{2,1,0:T(8,128)S(1)} %slice.215), channel_id=1, source_target_pairs={{0,16},{4,20},{8,24},{12,28},{16,0},{20,4},{24,8},{28,12},{1,17},{... | collective-permute-start | bytes 49160 | tf_op jit(solution)/shard_map/ppermute | solution.py:19
  68.7 3.6 %collective-permute-start.15 = (f32[16]{0:T(128)S(1)}, f32[16]{0:T(128)S(1)}, u32[]{:S(2)}, u32[]{:S(2)}) collective-permute-start(f32[16]{0:T(128)S(1)} %add.227), channel_id=1, source_target_pairs={{0,1},{1,0},{2,3},{3,2},{4,5},{5,4},{6,7},{7,6},{8,9},{9,8},{10,11... | collective-permute-start | bytes 200 | tf_op jit(solution)/shard_map/ppermute | solution.py:19
  72.3 4.4 %collective-permute-start.16 = (f32[16]{0:T(128)S(1)}, f32[16]{0:T(128)S(1)}, u32[]{:S(2)}, u32[]{:S(2)}) collective-permute-start(f32[16]{0:T(128)S(1)} %add.228), channel_id=1, source_target_pairs={{0,2},{1,3},{2,0},{3,1},{4,6},{5,7},{6,4},{7,5},{8,10},{9,11},{10,... | collective-permute-start | bytes 200 | tf_op jit(solution)/shard_map/ppermute | solution.py:19
  76.8 1.1 %collective-permute-start.17 = (f32[16]{0:T(128)S(1)}, f32[16]{0:T(128)S(1)}, u32[]{:S(2)}, u32[]{:S(2)}) collective-permute-start(f32[16]{0:T(128)S(1)} %add.232), channel_id=1, source_target_pairs={{0,4},{4,0},{8,12},{12,8},{16,20},{20,16},{24,28},{28,24},{1,5},{5... | collective-permute-start | bytes 200 | tf_op jit(solution)/shard_map/ppermute | solution.py:19
  77.9 3.5 %collective-permute-start.18 = (f32[16]{0:T(128)S(1)}, f32[16]{0:T(128)S(1)}, u32[]{:S(2)}, u32[]{:S(2)}) collective-permute-start(f32[16]{0:T(128)S(1)} %add.236), channel_id=1, source_target_pairs={{0,8},{4,12},{8,0},{12,4},{16,24},{20,28},{24,16},{28,20},{1,9},{5... | collective-permute-start | bytes 200 | tf_op jit(solution)/shard_map/ppermute | solution.py:19
  81.4 3.5 %collective-permute-start.19 = (f32[16]{0:T(128)S(1)}, f32[16]{0:T(128)S(1)}, u32[]{:S(2)}, u32[]{:S(2)}) collective-permute-start(f32[16]{0:T(128)S(1)} %add.237), channel_id=1, source_target_pairs={{0,16},{4,20},{8,24},{12,28},{16,0},{20,4},{24,8},{28,12},{1,17},{... | collective-permute-start | bytes 200 | tf_op jit(solution)/shard_map/ppermute | solution.py:19

commit v16 on v15

--- a/solution.py
+++ b/solution.py
@@ -158,7 +158,7 @@
     residual_proj = project(residual)
     for step in range(ITERATIONS):
         if step == 0:
-            stages = [None, permute_inputs, kernel_blocks, first_near]
+            stages = [None, permute_inputs, None, kernel_blocks, first_near]
             nodesum, norm_now, (kern, direction_u, near_u) = sums_with_norm(
                 residual, residual_proj, stages, (coords, right_side)
             )

time: 86.1 us -> 85.6 us (level)
  transfers between devices with their start and end apart: 20 -> 20, of which waited for: 16 -> 17; matrix products, arithmetic and copies ran while one was open for 32% -> 32% of each run, Pallas kernels for 0% -> 0%
where the time goes in v16:
time: 85.6 us; the launch traced here: 85.3 us
  matrix products  26.8 us (31%)
  waiting for transfers between devices  26.8 us (31%)
  starting transfers between devices  20.6 us (24%)
  other arithmetic  5.9 us (7%)
  local copies, waits for them, and re-layouts  4.03 us (5%)
  between operations  1.2 us (1%)
    ppermute x20, waiting for transfers between devices, swapped(): return lax.ppermute(value, axis, pairs)  26.8 us
    ppermute x20, starting transfers between devices, swapped(): return lax.ppermute(value, axis, pairs)  20.6 us
    dot_general x4, matrix products, from_union(): jnp.einsum('gci,gip->cp', pieces(values_u, 1), hot, preferred_element_typ...  7.27 us
    dot_general x3, matrix products, to_union(): jnp.einsum('cp,gip->gci', pieces(values, 0), hot, preferred_element_type=...  7.1 us
    dot_general x2, matrix products, near_apply(): jnp.einsum('gij,gcj->gci', kern, union_vec, precision=lax.Precision.HIGH)  3.91 us
    dot_general x2, matrix products, project(): jnp.einsum('lp,cp,rp->lcr', level_gain, values, basis, precision=highest)  3.33 us
  transfers between devices with their start and end apart: 20, of which 17 were waited for; matrix products, arithmetic and copies ran while one was open for 32% of the time, Pallas kernels for 0%

profile of v16, /device:TPU:0, one launch (start us, length us, event | category | flops | bytes accessed | tf_op | source)
XLA Modules:
  0.0 85.3 jit_solution(8861756891603191484)
XLA Ops:
  0.6 1.1 %multiply_reduce_fusion.5 = f32[16]{0:T(128)S(1)} fusion(f32[16,2048]{1,0:T(8,128)} %param.12), kind=kLoop, calls=%fused_computation.103 | loop fusion | flops 65520 | bytes 131136 | tf_op jit(solution)/shard_map/reduce_sum | solution.py:113
  1.9 2.1 %convolution_bitcast_fusion.1 = f32[5,16,128]{2,1,0:T(8,128)S(1)} fusion(f32[128,2048]{1,0:T(8,128)S(1)} %copy-done, f32[2048,5]{0,1:T(8,128)} %bitcast.70, f32[2048,16]{0,1:T(8,128)} %bitcast.69), kind=kOutput, calls=%fused_computation.32 | convolution fusion | flops 251822080 | bytes 1261568 | tf_op jit(solution)/shard_map/lp,cp,rp->lcr/dot_general | solution.py:110
  4.1 3.0 %collective-permute-start = (f32[6,16,128]{2,1,0:T(8,128)S(1)}, f32[6,16,128]{2,1,0:T(8,128)S(1)}, u32[]{:S(2)}, u32[]{:S(2)}) collective-permute-start(f32[6,16,128]{2,1,0:T(8,128)S(1)} %pad_maximum_fusion), channel_id=1, source_target_pairs={{0,1},{1,0},{2,3},{3,2},{4,5},{5,4},{6,7},{7,6},{8,9},{9,8},{10,11... | collective-permute-start | bytes 147464 | tf_op jit(solution)/shard_map/ppermute | solution.py:19
  7.7 1.4 %reduce.9 = s32[2048]{0:T(1024)S(1)} reduce(s32[1,2048]{1,0:T(1,128)} %param.16, s32[]{:T(128)} %broadcast.100), dimensions={0}, to_apply=%param.16.reduce_sub_computation.3 | reduce | bytes 16388 | tf_op args[7]
  9.1 0.8 fusion.84
  9.8 0.6 gather_fusion
  10.4 0.6 gather_fusion.1
  11.0 2.7 %collective-permute-start.1 = (f32[5,16,128]{2,1,0:T(8,128)S(1)}, f32[5,16,128]{2,1,0:T(8,128)S(1)}, u32[]{:S(2)}, u32[]{:S(2)}) collective-permute-start(f32[5,16,128]{2,1,0:T(8,128)S(1)} %slice.231), channel_id=1, source_target_pairs={{0,2},{1,3},{2,0},{3,1},{4,6},{5,7},{6,4},{7,5},{8,10},{9,11},{10,... | collective-permute-start | bytes 122888 | tf_op jit(solution)/shard_map/ppermute | solution.py:19
  13.7 0.8 constant_dynamic-update-slice_fusion.3
  14.5 0.9 %constant_dynamic-update-slice_fusion.2 = f32[24,2048]{1,0:T(8,128)S(1)} fusion(f32[24,2048]{1,0:T(8,128)S(1)} %constant_dynamic-update-slice_fusion.3, f32[16,2048]{1,0:T(8,128)} %param.12), kind=kLoop, calls=%fused_computation.174 | loop fusion | bytes 262144 | tf_op jit(solution)/shard_map/concatenate | solution.py:144
  15.5 3.5 %fusion.18 = f32[4,72,512]{2,1,0:T(8,128)S(1)} fusion(s32[4,512]{1,0:T(4,128)S(1)} %constant_dynamic-update-slice_fusion, bf16[24,2048]{1,0:T(8,128)(2,1)S(1)} %get-tuple-element.147, bf16[24,2048]{1,0:T(8,128)(2,1)S(1)} %get-tuple-element.148, bf16[24,2048]{1,0:T(8,128)(2,1)S(1)} %get-tuple-element.146), kind=kOutput, calls=%fused_computation.26 | convolution fusion | flops 609058816 | bytes 892928 | tf_op jit(solution)/shard_map/cp,gip->gci/dot_general | solution.py:49
  19.3 1.2 %collective-permute-done.2 = f32[4,16,128]{2,1,0:T(8,128)S(1)} collective-permute-done((f32[4,16,128]{2,1,0:T(8,128)S(1)}, f32[4,16,128]{2,1,0:T(8,128)S(1)}, u32[]{:S(2)}, u32[]{:S(2)}) %collective-permute-start.2) | collective-permute-done | bytes 32800 | tf_op jit(solution)/shard_map/ppermute | solution.py:19
  20.6 1.6 %collective-permute-start.3 = (f32[3,16,128]{2,1,0:T(8,128)S(1)}, f32[3,16,128]{2,1,0:T(8,128)S(1)}, u32[]{:S(2)}, u32[]{:S(2)}) collective-permute-start(f32[3,16,128]{2,1,0:T(8,128)S(1)} %slice.237), channel_id=1, source_target_pairs={{0,8},{4,12},{8,0},{12,4},{16,24},{20,28},{24,16},{28,20},{1,9},{5... | collective-permute-start | bytes 73736 | tf_op jit(solution)/shard_map/ppermute | solution.py:19
  22.3 1.6 %exponential_multiply_fusion = f32[4,512,512]{2,1,0:T(8,128)S(1)} fusion(bf16[4,48,512]{2,1,0:T(8,128)(2,1)S(1)} %get-tuple-element.174, bf16[4,48,512]{2,1,0:T(8,128)(2,1)S(1)} %get-tuple-element.173, f32[4,512]{1,0:T(4,128)S(1)} %multiply_reduce_fusion.6), kind=kOutput, calls=%fused_computation.19 | convolution fusion | flops 105906176 | bytes 4595712 | tf_op jit(solution)/shard_map/gfi,gfj->gij/dot_general | solution.py:33
  24.5 1.6 %collective-permute-start.4 = (f32[2,16,128]{2,1,0:T(8,128)S(1)}, f32[2,16,128]{2,1,0:T(8,128)S(1)}, u32[]{:S(2)}, u32[]{:S(2)}) collective-permute-start(f32[2,16,128]{2,1,0:T(8,128)S(1)} %slice.188), channel_id=1, source_target_pairs={{0,16},{4,20},{8,24},{12,28},{16,0},{20,4},{24,8},{28,12},{1,17},{... | collective-permute-start | bytes 49160 | tf_op jit(solution)/shard_map/ppermute | solution.py:19
  26.1 1.8 %fusion.96 = f32[4,16,512]{2,1,0:T(8,128)S(1)} fusion(f32[4,16,512]{2,1,0:T(8,128)S(1)} %slice.236, f32[4,512,512]{2,1,0:T(8,128)S(1)} %exponential_multiply_fusion), kind=kOutput, calls=%fused_computation.220 | convolution fusion | flops 100663296 | bytes 4456448 | tf_op jit(solution)/shard_map/gij,gcj->gci/dot_general | solution.py:40
  28.7 0.6 convolution_multiply_fusion.3
  29.3 0.8 fusion.19
  30.9 1.8 %fusion.14 = f32[48,2048]{1,0:T(8,128)S(1)} fusion(s32[2,512]{1,0:T(2,128)S(1)} %get-tuple-element.178, bf16[2,16,512]{2,1,0:T(8,128)(2,1)S(1)} %get-tuple-element.165, bf16[2,16,512]{2,1,0:T(8,128)(2,1)S(1)} %get-tuple-element.166, bf16[2,16,512]{2,1,0:T(8,128)(2,1)S(1)} %get-tuple-element.164), kind=kOutput, calls=%fused_computation.22 | convolution fusion | flops 203718656 | bytes 495616 | tf_op jit(solution)/shard_map/gci,gip->cp/dot_general | solution.py:55
  32.8 1.2 %collective-permute-done.5 = f32[16]{0:T(128)S(1)} collective-permute-done((f32[16]{0:T(128)S(1)}, f32[16]{0:T(128)S(1)}, u32[]{:S(2)}, u32[]{:S(2)}) %collective-permute-start.5) | collective-permute-done | bytes 96 | tf_op jit(solution)/shard_map/ppermute | solution.py:19
  34.3 1.8 %fusion.16 = f32[48,2048]{1,0:T(8,128)S(1)} fusion(s32[2,512]{1,0:T(2,128)S(1)} %get-tuple-element.177, bf16[2,16,512]{2,1,0:T(8,128)(2,1)S(1)} %get-tuple-element.162, bf16[2,16,512]{2,1,0:T(8,128)(2,1)S(1)} %get-tuple-element.163, bf16[2,16,512]{2,1,0:T(8,128)(2,1)S(1)} %get-tuple-element.161), kind=kOutput, calls=%fused_computation.24 | convolution fusion | flops 203718656 | bytes 495616 | tf_op jit(solution)/shard_map/gci,gip->cp/dot_general | solution.py:55
  36.2 2.2 %collective-permute-done.6 = f32[16]{0:T(128)S(1)} collective-permute-done((f32[16]{0:T(128)S(1)}, f32[16]{0:T(128)S(1)}, u32[]{:S(2)}, u32[]{:S(2)}) %collective-permute-start.6) | collective-permute-done | bytes 96 | tf_op jit(solution)/shard_map/ppermute | solution.py:19
  38.5 1.2 %convolution_bitcast_fusion = f32[5,16,128]{2,1,0:T(8,128)S(1)} fusion(f32[128,2048]{1,0:T(8,128)S(1)} %copy-done, f32[2048,16]{0,1:T(8,128)S(1)} %add_bitcast_fusion, f32[2048,5]{0,1:T(8,128)S(1)} %bitcast.71), kind=kOutput, calls=%fused_computation.31 | convolution fusion | flops 251822080 | bytes 1261568 | tf_op jit(solution)/shard_map/lp,cp,rp->lcr/dot_general | solution.py:110
  39.7 1.6 %collective-permute-start.8 = (f32[16]{0:T(128)S(1)}, f32[16]{0:T(128)S(1)}, u32[]{:S(2)}, u32[]{:S(2)}) collective-permute-start(f32[16]{0:T(128)S(1)} %add.207), channel_id=1, source_target_pairs={{0,8},{4,12},{8,0},{12,4},{16,24},{20,28},{24,16},{28,20},{1,9},{5... | collective-permute-start | bytes 200 | tf_op jit(solution)/shard_map/ppermute | solution.py:19
  41.2 2.1 %collective-permute-done.8 = f32[16]{0:T(128)S(1)} collective-permute-done((f32[16]{0:T(128)S(1)}, f32[16]{0:T(128)S(1)}, u32[]{:S(2)}, u32[]{:S(2)}) %collective-permute-start.8) | collective-permute-done | bytes 96 | tf_op jit(solution)/shard_map/ppermute | solution.py:19
  43.3 1.5 %collective-permute-start.9 = (f32[16]{0:T(128)S(1)}, f32[16]{0:T(128)S(1)}, u32[]{:S(2)}, u32[]{:S(2)}) collective-permute-start(f32[16]{0:T(128)S(1)} %add.210), channel_id=1, source_target_pairs={{0,16},{4,20},{8,24},{12,28},{16,0},{20,4},{24,8},{28,12},{1,17},{... | collective-permute-start | bytes 200 | tf_op jit(solution)/shard_map/ppermute | solution.py:19
  44.9 1.9 %collective-permute-done.9 = f32[16]{0:T(128)S(1)} collective-permute-done((f32[16]{0:T(128)S(1)}, f32[16]{0:T(128)S(1)}, u32[]{:S(2)}, u32[]{:S(2)}) %collective-permute-start.9) | collective-permute-done | bytes 96 | tf_op jit(solution)/shard_map/ppermute | solution.py:19
  47.7 1.8 %fusion.21 = f32[2,48,512]{2,1,0:T(8,128)S(1)} fusion(s32[2,512]{1,0:T(2,128)S(1)} %get-tuple-element.178, bf16[16,2048]{1,0:T(8,128)(2,1)S(1)} %get-tuple-element.159, bf16[16,2048]{1,0:T(8,128)(2,1)S(1)} %get-tuple-element.160, bf16[16,2048]{1,0:T(8,128)(2,1)S(1)} %get-tuple-element.158), kind=kOutput, calls=%fused_computation.29 | convolution fusion | flops 204013568 | bytes 397312 | tf_op jit(solution)/shard_map/cp,gip->gci/dot_general | solution.py:49
  49.5 1.7 %collective-permute-done.10 = f32[6,16,128]{2,1,0:T(8,128)S(1)} collective-permute-done((f32[6,16,128]{2,1,0:T(8,128)S(1)}, f32[6,16,128]{2,1,0:T(8,128)S(1)}, u32[]{:S(2)}, u32[]{:S(2)}) %collective-permute-start.10) | collective-permute-done | bytes 49184 | tf_op jit(solution)/shard_map/ppermute | solution.py:19
  51.9 1.8 %fusion.22 = f32[2,48,512]{2,1,0:T(8,128)S(1)} fusion(s32[2,512]{1,0:T(2,128)S(1)} %get-tuple-element.177, bf16[16,2048]{1,0:T(8,128)(2,1)S(1)} %get-tuple-element.156, bf16[16,2048]{1,0:T(8,128)(2,1)S(1)} %get-tuple-element.157, bf16[16,2048]{1,0:T(8,128)(2,1)S(1)} %get-tuple-element.155), kind=kOutput, calls=%fused_computation.30 | convolution fusion | flops 204013568 | bytes 397312 | tf_op jit(solution)/shard_map/cp,gip->gci/dot_general | solution.py:49
  53.7 3.0 %collective-permute-done.11 = f32[5,16,128]{2,1,0:T(8,128)S(1)} collective-permute-done((f32[5,16,128]{2,1,0:T(8,128)S(1)}, f32[5,16,128]{2,1,0:T(8,128)S(1)}, u32[]{:S(2)}, u32[]{:S(2)}) %collective-permute-start.11) | collective-permute-done | bytes 40992 | tf_op jit(solution)/shard_map/ppermute | solution.py:19
  56.8 1.2 %collective-permute-done.12 = f32[4,16,128]{2,1,0:T(8,128)S(1)} collective-permute-done((f32[4,16,128]{2,1,0:T(8,128)S(1)}, f32[4,16,128]{2,1,0:T(8,128)S(1)}, u32[]{:S(2)}, u32[]{:S(2)}) %collective-permute-start.12) | collective-permute-done | bytes 32800 | tf_op jit(solution)/shard_map/ppermute | solution.py:19
  58.1 1.6 %collective-permute-start.13 = (f32[3,16,128]{2,1,0:T(8,128)S(1)}, f32[3,16,128]{2,1,0:T(8,128)S(1)}, u32[]{:S(2)}, u32[]{:S(2)}) collective-permute-start(f32[3,16,128]{2,1,0:T(8,128)S(1)} %slice.252), channel_id=1, source_target_pairs={{0,8},{4,12},{8,0},{12,4},{16,24},{20,28},{24,16},{28,20},{1,9},{5... | collective-permute-start | bytes 73736 | tf_op jit(solution)/shard_map/ppermute | solution.py:19
  59.6 2.1 %fusion.98 = f32[4,16,512]{2,1,0:T(8,128)S(1)} fusion(f32[4,16,512]{2,1,0:T(8,128)S(1)} %constant_dynamic-update-slice_fusion.16, f32[4,512,512]{2,1,0:T(8,128)S(1)} %exponential_multiply_fusion), kind=kOutput, calls=%fused_computation.222 | convolution fusion | flops 100663296 | bytes 4456448 | tf_op jit(solution)/shard_map/gij,gcj->gci/dot_general | solution.py:40
  62.0 1.6 %collective-permute-start.14 = (f32[2,16,128]{2,1,0:T(8,128)S(1)}, f32[2,16,128]{2,1,0:T(8,128)S(1)}, u32[]{:S(2)}, u32[]{:S(2)}) collective-permute-start(f32[2,16,128]{2,1,0:T(8,128)S(1)} %slice.215), channel_id=1, source_target_pairs={{0,16},{4,20},{8,24},{12,28},{16,0},{20,4},{24,8},{28,12},{1,17},{... | collective-permute-start | bytes 49160 | tf_op jit(solution)/shard_map/ppermute | solution.py:19
  63.6 2.2 %collective-permute-done.14 = f32[2,16,128]{2,1,0:T(8,128)S(1)} collective-permute-done((f32[2,16,128]{2,1,0:T(8,128)S(1)}, f32[2,16,128]{2,1,0:T(8,128)S(1)}, u32[]{:S(2)}, u32[]{:S(2)}) %collective-permute-start.14) | collective-permute-done | bytes 16416 | tf_op jit(solution)/shard_map/ppermute | solution.py:19
  66.3 0.6 convolution_multiply_fusion.2
  67.0 0.8 fusion.20
  68.7 1.8 %fusion.15 = f32[48,2048]{1,0:T(8,128)S(1)} fusion(s32[2,512]{1,0:T(2,128)S(1)} %get-tuple-element.178, bf16[2,16,512]{2,1,0:T(8,128)(2,1)S(1)} %get-tuple-element.153, bf16[2,16,512]{2,1,0:T(8,128)(2,1)S(1)} %get-tuple-element.154, bf16[2,16,512]{2,1,0:T(8,128)(2,1)S(1)} %get-tuple-element.152), kind=kOutput, calls=%fused_computation.23 | convolution fusion | flops 203718656 | bytes 495616 | tf_op jit(solution)/shard_map/gci,gip->cp/dot_general | solution.py:55
  70.5 1.3 %collective-permute-done.15 = f32[16]{0:T(128)S(1)} collective-permute-done((f32[16]{0:T(128)S(1)}, f32[16]{0:T(128)S(1)}, u32[]{:S(2)}, u32[]{:S(2)}) %collective-permute-start.15) | collective-permute-done | bytes 96 | tf_op jit(solution)/shard_map/ppermute | solution.py:19
  71.8 1.8 %fusion.17 = f32[48,2048]{1,0:T(8,128)S(1)} fusion(s32[2,512]{1,0:T(2,128)S(1)} %get-tuple-element.177, bf16[2,16,512]{2,1,0:T(8,128)(2,1)S(1)} %get-tuple-element.150, bf16[2,16,512]{2,1,0:T(8,128)(2,1)S(1)} %get-tuple-element.151, bf16[2,16,512]{2,1,0:T(8,128)(2,1)S(1)} %get-tuple-element.149), kind=kOutput, calls=%fused_computation.25 | convolution fusion | flops 203718656 | bytes 495616 | tf_op jit(solution)/shard_map/gci,gip->cp/dot_general | solution.py:55
  73.7 2.5 %collective-permute-done.16 = f32[16]{0:T(128)S(1)} collective-permute-done((f32[16]{0:T(128)S(1)}, f32[16]{0:T(128)S(1)}, u32[]{:S(2)}, u32[]{:S(2)}) %collective-permute-start.16) | collective-permute-done | bytes 96 | tf_op jit(solution)/shard_map/ppermute | solution.py:19
  76.2 1.1 %collective-permute-done.17 = f32[16]{0:T(128)S(1)} collective-permute-done((f32[16]{0:T(128)S(1)}, f32[16]{0:T(128)S(1)}, u32[]{:S(2)}, u32[]{:S(2)}) %collective-permute-start.17) | collective-permute-done | bytes 96 | tf_op jit(solution)/shard_map/ppermute | solution.py:19
  77.3 1.5 %collective-permute-start.18 = (f32[16]{0:T(128)S(1)}, f32[16]{0:T(128)S(1)}, u32[]{:S(2)}, u32[]{:S(2)}) collective-permute-start(f32[16]{0:T(128)S(1)} %add.236), channel_id=1, source_target_pairs={{0,8},{4,12},{8,0},{12,4},{16,24},{20,28},{24,16},{28,20},{1,9},{5... | collective-permute-start | bytes 200 | tf_op jit(solution)/shard_map/ppermute | solution.py:19
  78.8 2.1 %collective-permute-done.18 = f32[16]{0:T(128)S(1)} collective-permute-done((f32[16]{0:T(128)S(1)}, f32[16]{0:T(128)S(1)}, u32[]{:S(2)}, u32[]{:S(2)}) %collective-permute-start.18) | collective-permute-done | bytes 96 | tf_op jit(solution)/shard_map/ppermute | solution.py:19
  80.9 1.5 %collective-permute-start.19 = (f32[16]{0:T(128)S(1)}, f32[16]{0:T(128)S(1)}, u32[]{:S(2)}, u32[]{:S(2)}) collective-permute-start(f32[16]{0:T(128)S(1)} %add.237), channel_id=1, source_target_pairs={{0,16},{4,20},{8,24},{12,28},{16,0},{20,4},{24,8},{28,12},{1,17},{... | collective-permute-start | bytes 200 | tf_op jit(solution)/shard_map/ppermute | solution.py:19
  82.4 2.0 %collective-permute-done.19 = f32[16]{0:T(128)S(1)} collective-permute-done((f32[16]{0:T(128)S(1)}, f32[16]{0:T(128)S(1)}, u32[]{:S(2)}, u32[]{:S(2)}) %collective-permute-start.19) | collective-permute-done | bytes 96 | tf_op jit(solution)/shard_map/ppermute | solution.py:19
  84.4 0.8 multiply_subtract_fusion
  (125 shorter events, 7.4 us)
Async XLA Ops:
  0.6 1.3 %copy-start = (f32[128,2048]{1,0:T(8,128)S(1)}, f32[128,2048]{1,0:T(8,128)}, u32[]{:S(2)}) copy-start(f32[128,2048]{1,0:T(8,128)} %param.13) | copy-start | bytes 3145732
  4.1 6.9 %collective-permute-start = (f32[6,16,128]{2,1,0:T(8,128)S(1)}, f32[6,16,128]{2,1,0:T(8,128)S(1)}, u32[]{:S(2)}, u32[]{:S(2)}) collective-permute-start(f32[6,16,128]{2,1,0:T(8,128)S(1)} %pad_maximum_fusion), channel_id=1, source_target_pairs={{0,1},{1,0},{2,3},{3,2},{4,5},{5,4},{6,7},{7,6},{8,9},{9,8},{10,11... | collective-permute-start | bytes 147464 | tf_op jit(solution)/shard_map/ppermute | solution.py:19
  11.0 8.1 %collective-permute-start.1 = (f32[5,16,128]{2,1,0:T(8,128)S(1)}, f32[5,16,128]{2,1,0:T(8,128)S(1)}, u32[]{:S(2)}, u32[]{:S(2)}) collective-permute-start(f32[5,16,128]{2,1,0:T(8,128)S(1)} %slice.231), channel_id=1, source_target_pairs={{0,2},{1,3},{2,0},{3,1},{4,6},{5,7},{6,4},{7,5},{8,10},{9,11},{10,... | collective-permute-start | bytes 122888 | tf_op jit(solution)/shard_map/ppermute | solution.py:19
  14.5 4.5 %copy-start.5 = (f32[8]{0:T(128)S(1)}, f32[8]{0:T(128)}, u32[]{:S(2)}) copy-start(f32[8]{0:T(128)} %param.10) | copy-start | bytes 100
  19.2 1.3 %collective-permute-start.2 = (f32[4,16,128]{2,1,0:T(8,128)S(1)}, f32[4,16,128]{2,1,0:T(8,128)S(1)}, u32[]{:S(2)}, u32[]{:S(2)}) collective-permute-start(f32[4,16,128]{2,1,0:T(8,128)S(1)} %slice.182), channel_id=1, source_target_pairs={{0,4},{4,0},{8,12},{12,8},{16,20},{20,16},{24,28},{28,24},{1,5},{5... | collective-permute-start | bytes 98312 | tf_op jit(solution)/shard_map/ppermute | solution.py:19
  20.6 3.9 %collective-permute-start.3 = (f32[3,16,128]{2,1,0:T(8,128)S(1)}, f32[3,16,128]{2,1,0:T(8,128)S(1)}, u32[]{:S(2)}, u32[]{:S(2)}) collective-permute-start(f32[3,16,128]{2,1,0:T(8,128)S(1)} %slice.237), channel_id=1, source_target_pairs={{0,8},{4,12},{8,0},{12,4},{16,24},{20,28},{24,16},{28,20},{1,9},{5... | collective-permute-start | bytes 73736 | tf_op jit(solution)/shard_map/ppermute | solution.py:19
  22.3 6.1 %copy-start.2 = (f32[5,128,128]{2,1,0:T(8,128)S(1)}, f32[5,128,128]{2,1,0:T(8,128)}, u32[]{:S(2)}) copy-start(f32[5,128,128]{2,1,0:T(8,128)} %param.15) | copy-start | bytes 983044
  23.9 5.4 %copy-start.3 = (f32[5,2048]{1,0:T(8,128)S(1)}, f32[5,2048]{1,0:T(8,128)}, u32[]{:S(2)}) copy-start(f32[5,2048]{1,0:T(8,128)} %param.14) | copy-start | bytes 122884
  23.9 6.3 %copy-start.1 = (f32[16,2048]{1,0:T(8,128)S(1)}, f32[16,2048]{1,0:T(8,128)}, u32[]{:S(2)}) copy-start(f32[16,2048]{1,0:T(8,128)} %param.12) | copy-start | bytes 393220
  23.9 6.3 %copy-start.4 = (f32[2048]{0:T(1024)S(1)}, f32[2048]{0:T(1024)}, u32[]{:S(2)}) copy-start(f32[2048]{0:T(1024)} %param.11) | copy-start | bytes 24580
  24.5 3.8 %collective-permute-start.4 = (f32[2,16,128]{2,1,0:T(8,128)S(1)}, f32[2,16,128]{2,1,0:T(8,128)S(1)}, u32[]{:S(2)}, u32[]{:S(2)}) collective-permute-start(f32[2,16,128]{2,1,0:T(8,128)S(1)} %slice.188), channel_id=1, source_target_pairs={{0,16},{4,20},{8,24},{12,28},{16,0},{20,4},{24,8},{28,12},{1,17},{... | collective-permute-start | bytes 49160 | tf_op jit(solution)/shard_map/ppermute | solution.py:19
  30.4 3.6 %collective-permute-start.5 = (f32[16]{0:T(128)S(1)}, f32[16]{0:T(128)S(1)}, u32[]{:S(2)}, u32[]{:S(2)}) collective-permute-start(f32[16]{0:T(128)S(1)} %add.198), channel_id=1, source_target_pairs={{0,1},{1,0},{2,3},{3,2},{4,5},{5,4},{6,7},{7,6},{8,9},{9,8},{10,11... | collective-permute-start | bytes 200 | tf_op jit(solution)/shard_map/ppermute | solution.py:19
  34.0 4.4 %collective-permute-start.6 = (f32[16]{0:T(128)S(1)}, f32[16]{0:T(128)S(1)}, u32[]{:S(2)}, u32[]{:S(2)}) collective-permute-start(f32[16]{0:T(128)S(1)} %add.199), channel_id=1, source_target_pairs={{0,2},{1,3},{2,0},{3,1},{4,6},{5,7},{6,4},{7,5},{8,10},{9,11},{10,... | collective-permute-start | bytes 200 | tf_op jit(solution)/shard_map/ppermute | solution.py:19
  38.4 1.2 %collective-permute-start.7 = (f32[16]{0:T(128)S(1)}, f32[16]{0:T(128)S(1)}, u32[]{:S(2)}, u32[]{:S(2)}) collective-permute-start(f32[16]{0:T(128)S(1)} %add.203), channel_id=1, source_target_pairs={{0,4},{4,0},{8,12},{12,8},{16,20},{20,16},{24,28},{28,24},{1,5},{5... | collective-permute-start | bytes 200 | tf_op jit(solution)/shard_map/ppermute | solution.py:19
  39.7 3.6 %collective-permute-start.8 = (f32[16]{0:T(128)S(1)}, f32[16]{0:T(128)S(1)}, u32[]{:S(2)}, u32[]{:S(2)}) collective-permute-start(f32[16]{0:T(128)S(1)} %add.207), channel_id=1, source_target_pairs={{0,8},{4,12},{8,0},{12,4},{16,24},{20,28},{24,16},{28,20},{1,9},{5... | collective-permute-start | bytes 200 | tf_op jit(solution)/shard_map/ppermute | solution.py:19
  43.3 3.5 %collective-permute-start.9 = (f32[16]{0:T(128)S(1)}, f32[16]{0:T(128)S(1)}, u32[]{:S(2)}, u32[]{:S(2)}) collective-permute-start(f32[16]{0:T(128)S(1)} %add.210), channel_id=1, source_target_pairs={{0,16},{4,20},{8,24},{12,28},{16,0},{20,4},{24,8},{28,12},{1,17},{... | collective-permute-start | bytes 200 | tf_op jit(solution)/shard_map/ppermute | solution.py:19
  47.2 4.1 %collective-permute-start.10 = (f32[6,16,128]{2,1,0:T(8,128)S(1)}, f32[6,16,128]{2,1,0:T(8,128)S(1)}, u32[]{:S(2)}, u32[]{:S(2)}) collective-permute-start(f32[6,16,128]{2,1,0:T(8,128)S(1)} %pad_maximum_fusion.5), channel_id=1, source_target_pairs={{0,1},{1,0},{2,3},{3,2},{4,5},{5,4},{6,7},{7,6},{8,9},{9,8},{10,11... | collective-permute-start | bytes 147464 | tf_op jit(solution)/shard_map/ppermute | solution.py:19
  51.3 5.4 %collective-permute-start.11 = (f32[5,16,128]{2,1,0:T(8,128)S(1)}, f32[5,16,128]{2,1,0:T(8,128)S(1)}, u32[]{:S(2)}, u32[]{:S(2)}) collective-permute-start(f32[5,16,128]{2,1,0:T(8,128)S(1)} %slice.206), channel_id=1, source_target_pairs={{0,2},{1,3},{2,0},{3,1},{4,6},{5,7},{6,4},{7,5},{8,10},{9,11},{10,... | collective-permute-start | bytes 122888 | tf_op jit(solution)/shard_map/ppermute | solution.py:19
  56.8 1.3 %collective-permute-start.12 = (f32[4,16,128]{2,1,0:T(8,128)S(1)}, f32[4,16,128]{2,1,0:T(8,128)S(1)}, u32[]{:S(2)}, u32[]{:S(2)}) collective-permute-start(f32[4,16,128]{2,1,0:T(8,128)S(1)} %slice.211), channel_id=1, source_target_pairs={{0,4},{4,0},{8,12},{12,8},{16,20},{20,16},{24,28},{28,24},{1,5},{5... | collective-permute-start | bytes 98312 | tf_op jit(solution)/shard_map/ppermute | solution.py:19
  58.1 3.9 %collective-permute-start.13 = (f32[3,16,128]{2,1,0:T(8,128)S(1)}, f32[3,16,128]{2,1,0:T(8,128)S(1)}, u32[]{:S(2)}, u32[]{:S(2)}) collective-permute-start(f32[3,16,128]{2,1,0:T(8,128)S(1)} %slice.252), channel_id=1, source_target_pairs={{0,8},{4,12},{8,0},{12,4},{16,24},{20,28},{24,16},{28,20},{1,9},{5... | collective-permute-start | bytes 73736 | tf_op jit(solution)/shard_map/ppermute | solution.py:19
  62.0 3.8 %collective-permute-start.14 = (f32[2,16,128]{2,1,0:T(8,128)S(1)}, f32[2,16,128]{2,1,0:T(8,128)S(1)}, u32[]{:S(2)}, u32[]{:S(2)}) collective-permute-start(f32[2,16,128]{2,1,0:T(8,128)S(1)} %slice.215), channel_id=1, source_target_pairs={{0,16},{4,20},{8,24},{12,28},{16,0},{20,4},{24,8},{28,12},{1,17},{... | collective-permute-start | bytes 49160 | tf_op jit(solution)/shard_map/ppermute | solution.py:19
  68.2 3.6 %collective-permute-start.15 = (f32[16]{0:T(128)S(1)}, f32[16]{0:T(128)S(1)}, u32[]{:S(2)}, u32[]{:S(2)}) collective-permute-start(f32[16]{0:T(128)S(1)} %add.227), channel_id=1, source_target_pairs={{0,1},{1,0},{2,3},{3,2},{4,5},{5,4},{6,7},{7,6},{8,9},{9,8},{10,11... | collective-permute-start | bytes 200 | tf_op jit(solution)/shard_map/ppermute | solution.py:19
  71.8 4.4 %collective-permute-start.16 = (f32[16]{0:T(128)S(1)}, f32[16]{0:T(128)S(1)}, u32[]{:S(2)}, u32[]{:S(2)}) collective-permute-start(f32[16]{0:T(128)S(1)} %add.228), channel_id=1, source_target_pairs={{0,2},{1,3},{2,0},{3,1},{4,6},{5,7},{6,4},{7,5},{8,10},{9,11},{10,... | collective-permute-start | bytes 200 | tf_op jit(solution)/shard_map/ppermute | solution.py:19
  76.2 1.1 %collective-permute-start.17 = (f32[16]{0:T(128)S(1)}, f32[16]{0:T(128)S(1)}, u32[]{:S(2)}, u32[]{:S(2)}) collective-permute-start(f32[16]{0:T(128)S(1)} %add.232), channel_id=1, source_target_pairs={{0,4},{4,0},{8,12},{12,8},{16,20},{20,16},{24,28},{28,24},{1,5},{5... | collective-permute-start | bytes 200 | tf_op jit(solution)/shard_map/ppermute | solution.py:19
  77.3 3.5 %collective-permute-start.18 = (f32[16]{0:T(128)S(1)}, f32[16]{0:T(128)S(1)}, u32[]{:S(2)}, u32[]{:S(2)}) collective-permute-start(f32[16]{0:T(128)S(1)} %add.236), channel_id=1, source_target_pairs={{0,8},{4,12},{8,0},{12,4},{16,24},{20,28},{24,16},{28,20},{1,9},{5... | collective-permute-start | bytes 200 | tf_op jit(solution)/shard_map/ppermute | solution.py:19
  80.9 3.5 %collective-permute-start.19 = (f32[16]{0:T(128)S(1)}, f32[16]{0:T(128)S(1)}, u32[]{:S(2)}, u32[]{:S(2)}) collective-permute-start(f32[16]{0:T(128)S(1)} %add.237), channel_id=1, source_target_pairs={{0,16},{4,20},{8,24},{12,28},{16,0},{20,4},{24,8},{28,12},{1,17},{... | collective-permute-start | bytes 200 | tf_op jit(solution)/shard_map/ppermute | solution.py:19

commit v17 on v16

--- a/solution.py
+++ b/solution.py
@@ -146,11 +146,12 @@
 
     def kernel_blocks(state):
         union_coords, direction_u = state
-        return near_kernels(union_coords), direction_u
+        product = jnp.einsum("lrs,lts->lrt", coupling, coupling, precision=highest)
+        return near_kernels(union_coords), direction_u, product * scales[:, None, None]
 
     def first_near(state):
-        kern, direction_u = state
-        return kern, direction_u, lax.optimization_barrier(near_apply(kern, direction_u))
+        kern, direction_u, product = state
+        return kern, direction_u, lax.optimization_barrier(near_apply(kern, direction_u)), product
 
     solution = jnp.zeros_like(right_side)
     residual = right_side
@@ -159,7 +160,7 @@
     for step in range(ITERATIONS):
         if step == 0:
             stages = [None, permute_inputs, None, kernel_blocks, first_near]
-            nodesum, norm_now, (kern, direction_u, near_u) = sums_with_norm(
+            nodesum, norm_now, (kern, direction_u, near_u, product) = sums_with_norm(
                 residual, residual_proj, stages, (coords, right_side)
             )
             late_u, nodesum = lax.optimization_barrier((near_u, nodesum))
@@ -178,10 +179,7 @@
             near_u = residual_near_u + ratio[None, :, None] * near_u
             carried = ratio[:, None] * near
             norm_now = norm_next
-        coupled = jnp.einsum("lcr,lrs->lcs", nodesum, coupling, precision=highest)
-        coupled = (
-            jnp.einsum("lcs,lrs->lcr", coupled, coupling, precision=highest) * scales[:, None, None]
-        )
+        coupled = jnp.einsum("lcr,lrt->lct", nodesum, product, precision=highest)
         back = jnp.einsum("lcr,rp->lcp", coupled, basis, precision=highest)
         far = jnp.sum(back * level_gain[:, None, :], axis=0)
         base = noise[None, :] * direction + far

time: 85.6 us -> 86.2 us (level)
    dot_general x4 -> x3, matrix products: 2.03 us -> 2.63 us  [the longest x1 1.86 us: kernel_blocks(): product = jnp.einsum('lrs,lts->lrt', coupling, coupling, precision=highest)]
  transfers between devices with their start and end apart: 20 -> 20, of which waited for: 17 -> 17; matrix products, arithmetic and copies ran while one was open for 32% -> 34% of each run, Pallas kernels for 0% -> 0%
where the time goes in v17:
time: 86.2 us; the launch traced here: 85.9 us
  matrix products  27.4 us (32%)
  waiting for transfers between devices  26.8 us (31%)
  starting transfers between devices  20.6 us (24%)
  other arithmetic  5.9 us (7%)
  local copies, waits for them, and re-layouts  4.03 us (5%)
  between operations  1.19 us (1%)
    ppermute x20, waiting for transfers between devices, swapped(): return lax.ppermute(value, axis, pairs)  26.8 us
    ppermute x20, starting transfers between devices, swapped(): return lax.ppermute(value, axis, pairs)  20.6 us
    dot_general x4, matrix products, from_union(): jnp.einsum('gci,gip->cp', pieces(values_u, 1), hot, preferred_element_typ...  7.26 us
    dot_general x3, matrix products, to_union(): jnp.einsum('cp,gip->gci', pieces(values, 0), hot, preferred_element_type=...  7.1 us
    dot_general x2, matrix products, near_apply(): jnp.einsum('gij,gcj->gci', kern, union_vec, precision=lax.Precision.HIGH)  3.91 us
    dot_general x2, matrix products, project(): jnp.einsum('lp,cp,rp->lcr', level_gain, values, basis, precision=highest)  3.33 us
    dot_general x1, matrix products, kernel_blocks(): product = jnp.einsum('lrs,lts->lrt', coupling, coupling, precision=highest)  1.86 us
  transfers between devices with their start and end apart: 20, of which 17 were waited for; matrix products, arithmetic and copies ran while one was open for 34% of the time, Pallas kernels for 0%

profile of v17, /device:TPU:0, one launch (start us, length us, event | category | flops | bytes accessed | tf_op | source)
XLA Modules:
  0.0 85.9 jit_solution(1175300779743418363)
XLA Ops:
  0.6 1.1 %multiply_reduce_fusion.5 = f32[16]{0:T(128)S(1)} fusion(f32[16,2048]{1,0:T(8,128)} %param.12), kind=kLoop, calls=%fused_computation.102 | loop fusion | flops 65520 | bytes 131136 | tf_op jit(solution)/shard_map/reduce_sum | solution.py:113
  1.9 2.1 %convolution_bitcast_fusion.1 = f32[5,16,128]{2,1,0:T(8,128)S(1)} fusion(f32[128,2048]{1,0:T(8,128)S(1)} %copy-done, f32[2048,5]{0,1:T(8,128)} %bitcast.68, f32[2048,16]{0,1:T(8,128)} %bitcast.67), kind=kOutput, calls=%fused_computation.33 | convolution fusion | flops 251822080 | bytes 1261568 | tf_op jit(solution)/shard_map/lp,cp,rp->lcr/dot_general | solution.py:110
  4.1 3.0 %collective-permute-start = (f32[6,16,128]{2,1,0:T(8,128)S(1)}, f32[6,16,128]{2,1,0:T(8,128)S(1)}, u32[]{:S(2)}, u32[]{:S(2)}) collective-permute-start(f32[6,16,128]{2,1,0:T(8,128)S(1)} %pad_maximum_fusion), channel_id=1, source_target_pairs={{0,1},{1,0},{2,3},{3,2},{4,5},{5,4},{6,7},{7,6},{8,9},{9,8},{10,11... | collective-permute-start | bytes 147464 | tf_op jit(solution)/shard_map/ppermute | solution.py:19
  7.7 1.4 %reduce.9 = s32[2048]{0:T(1024)S(1)} reduce(s32[1,2048]{1,0:T(1,128)} %param.16, s32[]{:T(128)} %broadcast.100), dimensions={0}, to_apply=%param.16.reduce_sub_computation.3 | reduce | bytes 16388 | tf_op args[7]
  9.1 0.8 fusion.84
  9.8 0.6 gather_fusion
  10.4 0.6 gather_fusion.1
  11.0 1.9 %convolution_multiply_fusion.2 = f32[5,128,128]{2,1,0:T(8,128)S(1)} fusion(f32[5,128,128]{2,1,0:T(8,128)} %param.15, f32[5]{0:T(128)S(1)} %multiply_power_fusion), kind=kOutput, calls=%fused_computation.29 | convolution fusion | flops 125911040 | bytes 655380 | tf_op jit(solution)/shard_map/lrs,lts->lrt/dot_general | solution.py:149
  12.9 2.7 %collective-permute-start.1 = (f32[5,16,128]{2,1,0:T(8,128)S(1)}, f32[5,16,128]{2,1,0:T(8,128)S(1)}, u32[]{:S(2)}, u32[]{:S(2)}) collective-permute-start(f32[5,16,128]{2,1,0:T(8,128)S(1)} %slice.231), channel_id=1, source_target_pairs={{0,2},{1,3},{2,0},{3,1},{4,6},{5,7},{6,4},{7,5},{8,10},{9,11},{10,... | collective-permute-start | bytes 122888 | tf_op jit(solution)/shard_map/ppermute | solution.py:19
  15.6 0.8 constant_dynamic-update-slice_fusion.3
  16.4 0.9 %constant_dynamic-update-slice_fusion.2 = f32[24,2048]{1,0:T(8,128)S(1)} fusion(f32[24,2048]{1,0:T(8,128)S(1)} %constant_dynamic-update-slice_fusion.3, f32[16,2048]{1,0:T(8,128)} %param.12), kind=kLoop, calls=%fused_computation.173 | loop fusion | bytes 262144 | tf_op jit(solution)/shard_map/concatenate | solution.py:144
  17.4 3.5 %fusion.18 = f32[4,72,512]{2,1,0:T(8,128)S(1)} fusion(s32[4,512]{1,0:T(4,128)S(1)} %constant_dynamic-update-slice_fusion, bf16[24,2048]{1,0:T(8,128)(2,1)S(1)} %get-tuple-element.153, bf16[24,2048]{1,0:T(8,128)(2,1)S(1)} %get-tuple-element.154, bf16[24,2048]{1,0:T(8,128)(2,1)S(1)} %get-tuple-element.152), kind=kOutput, calls=%fused_computation.26 | convolution fusion | flops 609058816 | bytes 892928 | tf_op jit(solution)/shard_map/cp,gip->gci/dot_general | solution.py:49
  21.2 1.2 %collective-permute-done.2 = f32[4,16,128]{2,1,0:T(8,128)S(1)} collective-permute-done((f32[4,16,128]{2,1,0:T(8,128)S(1)}, f32[4,16,128]{2,1,0:T(8,128)S(1)}, u32[]{:S(2)}, u32[]{:S(2)}) %collective-permute-start.2) | collective-permute-done | bytes 32800 | tf_op jit(solution)/shard_map/ppermute | solution.py:19
  22.4 1.6 %collective-permute-start.3 = (f32[3,16,128]{2,1,0:T(8,128)S(1)}, f32[3,16,128]{2,1,0:T(8,128)S(1)}, u32[]{:S(2)}, u32[]{:S(2)}) collective-permute-start(f32[3,16,128]{2,1,0:T(8,128)S(1)} %slice.237), channel_id=1, source_target_pairs={{0,8},{4,12},{8,0},{12,4},{16,24},{20,28},{24,16},{28,20},{1,9},{5... | collective-permute-start | bytes 73736 | tf_op jit(solution)/shard_map/ppermute | solution.py:19
  24.1 1.6 %exponential_multiply_fusion = f32[4,512,512]{2,1,0:T(8,128)S(1)} fusion(bf16[4,48,512]{2,1,0:T(8,128)(2,1)S(1)} %get-tuple-element.180, bf16[4,48,512]{2,1,0:T(8,128)(2,1)S(1)} %get-tuple-element.179, f32[4,512]{1,0:T(4,128)S(1)} %multiply_reduce_fusion.6), kind=kOutput, calls=%fused_computation.19 | convolution fusion | flops 105906176 | bytes 4595712 | tf_op jit(solution)/shard_map/gfi,gfj->gij/dot_general | solution.py:33
  25.8 0.5 collective-permute-done.3
  26.4 1.6 %collective-permute-start.4 = (f32[2,16,128]{2,1,0:T(8,128)S(1)}, f32[2,16,128]{2,1,0:T(8,128)S(1)}, u32[]{:S(2)}, u32[]{:S(2)}) collective-permute-start(f32[2,16,128]{2,1,0:T(8,128)S(1)} %slice.188), channel_id=1, source_target_pairs={{0,16},{4,20},{8,24},{12,28},{16,0},{20,4},{24,8},{28,12},{1,17},{... | collective-permute-start | bytes 49160 | tf_op jit(solution)/shard_map/ppermute | solution.py:19
  27.9 1.8 %fusion.96 = f32[4,16,512]{2,1,0:T(8,128)S(1)} fusion(f32[4,16,512]{2,1,0:T(8,128)S(1)} %slice.236, f32[4,512,512]{2,1,0:T(8,128)S(1)} %exponential_multiply_fusion), kind=kOutput, calls=%fused_computation.219 | convolution fusion | flops 100663296 | bytes 4456448 | tf_op jit(solution)/shard_map/gij,gcj->gci/dot_general | solution.py:40
  30.6 0.8 fusion.19
  32.2 1.8 %fusion.14 = f32[48,2048]{1,0:T(8,128)S(1)} fusion(s32[2,512]{1,0:T(2,128)S(1)} %get-tuple-element.184, bf16[2,16,512]{2,1,0:T(8,128)(2,1)S(1)} %get-tuple-element.171, bf16[2,16,512]{2,1,0:T(8,128)(2,1)S(1)} %get-tuple-element.172, bf16[2,16,512]{2,1,0:T(8,128)(2,1)S(1)} %get-tuple-element.170), kind=kOutput, calls=%fused_computation.22 | convolution fusion | flops 203718656 | bytes 495616 | tf_op jit(solution)/shard_map/gci,gip->cp/dot_general | solution.py:55
  34.0 1.2 %collective-permute-done.5 = f32[16]{0:T(128)S(1)} collective-permute-done((f32[16]{0:T(128)S(1)}, f32[16]{0:T(128)S(1)}, u32[]{:S(2)}, u32[]{:S(2)}) %collective-permute-start.5) | collective-permute-done | bytes 96 | tf_op jit(solution)/shard_map/ppermute | solution.py:19
  35.6 1.8 %fusion.16 = f32[48,2048]{1,0:T(8,128)S(1)} fusion(s32[2,512]{1,0:T(2,128)S(1)} %get-tuple-element.183, bf16[2,16,512]{2,1,0:T(8,128)(2,1)S(1)} %get-tuple-element.168, bf16[2,16,512]{2,1,0:T(8,128)(2,1)S(1)} %get-tuple-element.169, bf16[2,16,512]{2,1,0:T(8,128)(2,1)S(1)} %get-tuple-element.167), kind=kOutput, calls=%fused_computation.24 | convolution fusion | flops 203718656 | bytes 495616 | tf_op jit(solution)/shard_map/gci,gip->cp/dot_general | solution.py:55
  37.4 2.2 %collective-permute-done.6 = f32[16]{0:T(128)S(1)} collective-permute-done((f32[16]{0:T(128)S(1)}, f32[16]{0:T(128)S(1)}, u32[]{:S(2)}, u32[]{:S(2)}) %collective-permute-start.6) | collective-permute-done | bytes 96 | tf_op jit(solution)/shard_map/ppermute | solution.py:19
  39.7 1.2 %convolution_bitcast_fusion = f32[5,16,128]{2,1,0:T(8,128)S(1)} fusion(f32[128,2048]{1,0:T(8,128)S(1)} %copy-done, f32[2048,16]{0,1:T(8,128)S(1)} %add_bitcast_fusion, f32[2048,5]{0,1:T(8,128)S(1)} %bitcast.69), kind=kOutput, calls=%fused_computation.32 | convolution fusion | flops 251822080 | bytes 1261568 | tf_op jit(solution)/shard_map/lp,cp,rp->lcr/dot_general | solution.py:110
  40.9 1.6 %collective-permute-start.8 = (f32[16]{0:T(128)S(1)}, f32[16]{0:T(128)S(1)}, u32[]{:S(2)}, u32[]{:S(2)}) collective-permute-start(f32[16]{0:T(128)S(1)} %add.207), channel_id=1, source_target_pairs={{0,8},{4,12},{8,0},{12,4},{16,24},{20,28},{24,16},{28,20},{1,9},{5... | collective-permute-start | bytes 200 | tf_op jit(solution)/shard_map/ppermute | solution.py:19
  42.5 2.1 %collective-permute-done.8 = f32[16]{0:T(128)S(1)} collective-permute-done((f32[16]{0:T(128)S(1)}, f32[16]{0:T(128)S(1)}, u32[]{:S(2)}, u32[]{:S(2)}) %collective-permute-start.8) | collective-permute-done | bytes 96 | tf_op jit(solution)/shard_map/ppermute | solution.py:19
  44.5 1.5 %collective-permute-start.9 = (f32[16]{0:T(128)S(1)}, f32[16]{0:T(128)S(1)}, u32[]{:S(2)}, u32[]{:S(2)}) collective-permute-start(f32[16]{0:T(128)S(1)} %add.210), channel_id=1, source_target_pairs={{0,16},{4,20},{8,24},{12,28},{16,0},{20,4},{24,8},{28,12},{1,17},{... | collective-permute-start | bytes 200 | tf_op jit(solution)/shard_map/ppermute | solution.py:19
  46.2 1.9 %collective-permute-done.9 = f32[16]{0:T(128)S(1)} collective-permute-done((f32[16]{0:T(128)S(1)}, f32[16]{0:T(128)S(1)}, u32[]{:S(2)}, u32[]{:S(2)}) %collective-permute-start.9) | collective-permute-done | bytes 96 | tf_op jit(solution)/shard_map/ppermute | solution.py:19
  49.0 1.8 %fusion.21 = f32[2,48,512]{2,1,0:T(8,128)S(1)} fusion(s32[2,512]{1,0:T(2,128)S(1)} %get-tuple-element.184, bf16[16,2048]{1,0:T(8,128)(2,1)S(1)} %get-tuple-element.165, bf16[16,2048]{1,0:T(8,128)(2,1)S(1)} %get-tuple-element.166, bf16[16,2048]{1,0:T(8,128)(2,1)S(1)} %get-tuple-element.164), kind=kOutput, calls=%fused_computation.30 | convolution fusion | flops 204013568 | bytes 397312 | tf_op jit(solution)/shard_map/cp,gip->gci/dot_general | solution.py:49
  50.8 1.7 %collective-permute-done.10 = f32[6,16,128]{2,1,0:T(8,128)S(1)} collective-permute-done((f32[6,16,128]{2,1,0:T(8,128)S(1)}, f32[6,16,128]{2,1,0:T(8,128)S(1)}, u32[]{:S(2)}, u32[]{:S(2)}) %collective-permute-start.10) | collective-permute-done | bytes 49184 | tf_op jit(solution)/shard_map/ppermute | solution.py:19
  53.1 1.8 %fusion.22 = f32[2,48,512]{2,1,0:T(8,128)S(1)} fusion(s32[2,512]{1,0:T(2,128)S(1)} %get-tuple-element.183, bf16[16,2048]{1,0:T(8,128)(2,1)S(1)} %get-tuple-element.162, bf16[16,2048]{1,0:T(8,128)(2,1)S(1)} %get-tuple-element.163, bf16[16,2048]{1,0:T(8,128)(2,1)S(1)} %get-tuple-element.161), kind=kOutput, calls=%fused_computation.31 | convolution fusion | flops 204013568 | bytes 397312 | tf_op jit(solution)/shard_map/cp,gip->gci/dot_general | solution.py:49
  55.0 3.0 %collective-permute-done.11 = f32[5,16,128]{2,1,0:T(8,128)S(1)} collective-permute-done((f32[5,16,128]{2,1,0:T(8,128)S(1)}, f32[5,16,128]{2,1,0:T(8,128)S(1)}, u32[]{:S(2)}, u32[]{:S(2)}) %collective-permute-start.11) | collective-permute-done | bytes 40992 | tf_op jit(solution)/shard_map/ppermute | solution.py:19
  58.1 1.2 %collective-permute-done.12 = f32[4,16,128]{2,1,0:T(8,128)S(1)} collective-permute-done((f32[4,16,128]{2,1,0:T(8,128)S(1)}, f32[4,16,128]{2,1,0:T(8,128)S(1)}, u32[]{:S(2)}, u32[]{:S(2)}) %collective-permute-start.12) | collective-permute-done | bytes 32800 | tf_op jit(solution)/shard_map/ppermute | solution.py:19
  59.3 1.6 %collective-permute-start.13 = (f32[3,16,128]{2,1,0:T(8,128)S(1)}, f32[3,16,128]{2,1,0:T(8,128)S(1)}, u32[]{:S(2)}, u32[]{:S(2)}) collective-permute-start(f32[3,16,128]{2,1,0:T(8,128)S(1)} %slice.252), channel_id=1, source_target_pairs={{0,8},{4,12},{8,0},{12,4},{16,24},{20,28},{24,16},{28,20},{1,9},{5... | collective-permute-start | bytes 73736 | tf_op jit(solution)/shard_map/ppermute | solution.py:19
  60.9 2.1 %fusion.98 = f32[4,16,512]{2,1,0:T(8,128)S(1)} fusion(f32[4,16,512]{2,1,0:T(8,128)S(1)} %constant_dynamic-update-slice_fusion.16, f32[4,512,512]{2,1,0:T(8,128)S(1)} %exponential_multiply_fusion), kind=kOutput, calls=%fused_computation.221 | convolution fusion | flops 100663296 | bytes 4456448 | tf_op jit(solution)/shard_map/gij,gcj->gci/dot_general | solution.py:40
  63.2 1.6 %collective-permute-start.14 = (f32[2,16,128]{2,1,0:T(8,128)S(1)}, f32[2,16,128]{2,1,0:T(8,128)S(1)}, u32[]{:S(2)}, u32[]{:S(2)}) collective-permute-start(f32[2,16,128]{2,1,0:T(8,128)S(1)} %slice.215), channel_id=1, source_target_pairs={{0,16},{4,20},{8,24},{12,28},{16,0},{20,4},{24,8},{28,12},{1,17},{... | collective-permute-start | bytes 49160 | tf_op jit(solution)/shard_map/ppermute | solution.py:19
  64.8 2.2 %collective-permute-done.14 = f32[2,16,128]{2,1,0:T(8,128)S(1)} collective-permute-done((f32[2,16,128]{2,1,0:T(8,128)S(1)}, f32[2,16,128]{2,1,0:T(8,128)S(1)}, u32[]{:S(2)}, u32[]{:S(2)}) %collective-permute-start.14) | collective-permute-done | bytes 16416 | tf_op jit(solution)/shard_map/ppermute | solution.py:19
  67.6 0.8 fusion.20
  69.3 1.8 %fusion.15 = f32[48,2048]{1,0:T(8,128)S(1)} fusion(s32[2,512]{1,0:T(2,128)S(1)} %get-tuple-element.184, bf16[2,16,512]{2,1,0:T(8,128)(2,1)S(1)} %get-tuple-element.159, bf16[2,16,512]{2,1,0:T(8,128)(2,1)S(1)} %get-tuple-element.160, bf16[2,16,512]{2,1,0:T(8,128)(2,1)S(1)} %get-tuple-element.158), kind=kOutput, calls=%fused_computation.23 | convolution fusion | flops 203718656 | bytes 495616 | tf_op jit(solution)/shard_map/gci,gip->cp/dot_general | solution.py:55
  71.2 1.3 %collective-permute-done.15 = f32[16]{0:T(128)S(1)} collective-permute-done((f32[16]{0:T(128)S(1)}, f32[16]{0:T(128)S(1)}, u32[]{:S(2)}, u32[]{:S(2)}) %collective-permute-start.15) | collective-permute-done | bytes 96 | tf_op jit(solution)/shard_map/ppermute | solution.py:19
  72.5 1.8 %fusion.17 = f32[48,2048]{1,0:T(8,128)S(1)} fusion(s32[2,512]{1,0:T(2,128)S(1)} %get-tuple-element.183, bf16[2,16,512]{2,1,0:T(8,128)(2,1)S(1)} %get-tuple-element.156, bf16[2,16,512]{2,1,0:T(8,128)(2,1)S(1)} %get-tuple-element.157, bf16[2,16,512]{2,1,0:T(8,128)(2,1)S(1)} %get-tuple-element.155), kind=kOutput, calls=%fused_computation.25 | convolution fusion | flops 203718656 | bytes 495616 | tf_op jit(solution)/shard_map/gci,gip->cp/dot_general | solution.py:55
  74.3 2.5 %collective-permute-done.16 = f32[16]{0:T(128)S(1)} collective-permute-done((f32[16]{0:T(128)S(1)}, f32[16]{0:T(128)S(1)}, u32[]{:S(2)}, u32[]{:S(2)}) %collective-permute-start.16) | collective-permute-done | bytes 96 | tf_op jit(solution)/shard_map/ppermute | solution.py:19
  76.9 1.1 %collective-permute-done.17 = f32[16]{0:T(128)S(1)} collective-permute-done((f32[16]{0:T(128)S(1)}, f32[16]{0:T(128)S(1)}, u32[]{:S(2)}, u32[]{:S(2)}) %collective-permute-start.17) | collective-permute-done | bytes 96 | tf_op jit(solution)/shard_map/ppermute | solution.py:19
  78.0 1.5 %collective-permute-start.18 = (f32[16]{0:T(128)S(1)}, f32[16]{0:T(128)S(1)}, u32[]{:S(2)}, u32[]{:S(2)}) collective-permute-start(f32[16]{0:T(128)S(1)} %add.236), channel_id=1, source_target_pairs={{0,8},{4,12},{8,0},{12,4},{16,24},{20,28},{24,16},{28,20},{1,9},{5... | collective-permute-start | bytes 200 | tf_op jit(solution)/shard_map/ppermute | solution.py:19
  79.5 2.1 %collective-permute-done.18 = f32[16]{0:T(128)S(1)} collective-permute-done((f32[16]{0:T(128)S(1)}, f32[16]{0:T(128)S(1)}, u32[]{:S(2)}, u32[]{:S(2)}) %collective-permute-start.18) | collective-permute-done | bytes 96 | tf_op jit(solution)/shard_map/ppermute | solution.py:19
  81.5 1.5 %collective-permute-start.19 = (f32[16]{0:T(128)S(1)}, f32[16]{0:T(128)S(1)}, u32[]{:S(2)}, u32[]{:S(2)}) collective-permute-start(f32[16]{0:T(128)S(1)} %add.237), channel_id=1, source_target_pairs={{0,16},{4,20},{8,24},{12,28},{16,0},{20,4},{24,8},{28,12},{1,17},{... | collective-permute-start | bytes 200 | tf_op jit(solution)/shard_map/ppermute | solution.py:19
  83.0 2.0 %collective-permute-done.19 = f32[16]{0:T(128)S(1)} collective-permute-done((f32[16]{0:T(128)S(1)}, f32[16]{0:T(128)S(1)}, u32[]{:S(2)}, u32[]{:S(2)}) %collective-permute-start.19) | collective-permute-done | bytes 96 | tf_op jit(solution)/shard_map/ppermute | solution.py:19
  85.1 0.8 multiply_subtract_fusion
  (122 shorter events, 6.9 us)
Async XLA Ops:
  0.6 1.3 %copy-start = (f32[128,2048]{1,0:T(8,128)S(1)}, f32[128,2048]{1,0:T(8,128)}, u32[]{:S(2)}) copy-start(f32[128,2048]{1,0:T(8,128)} %param.13) | copy-start | bytes 3145732
  4.1 8.7 %collective-permute-start = (f32[6,16,128]{2,1,0:T(8,128)S(1)}, f32[6,16,128]{2,1,0:T(8,128)S(1)}, u32[]{:S(2)}, u32[]{:S(2)}) collective-permute-start(f32[6,16,128]{2,1,0:T(8,128)S(1)} %pad_maximum_fusion), channel_id=1, source_target_pairs={{0,1},{1,0},{2,3},{3,2},{4,5},{5,4},{6,7},{7,6},{8,9},{9,8},{10,11... | collective-permute-start | bytes 147464 | tf_op jit(solution)/shard_map/ppermute | solution.py:19
  12.9 8.1 %collective-permute-start.1 = (f32[5,16,128]{2,1,0:T(8,128)S(1)}, f32[5,16,128]{2,1,0:T(8,128)S(1)}, u32[]{:S(2)}, u32[]{:S(2)}) collective-permute-start(f32[5,16,128]{2,1,0:T(8,128)S(1)} %slice.231), channel_id=1, source_target_pairs={{0,2},{1,3},{2,0},{3,1},{4,6},{5,7},{6,4},{7,5},{8,10},{9,11},{10,... | collective-permute-start | bytes 122888 | tf_op jit(solution)/shard_map/ppermute | solution.py:19
  16.4 4.5 %copy-start.4 = (f32[8]{0:T(128)S(1)}, f32[8]{0:T(128)}, u32[]{:S(2)}) copy-start(f32[8]{0:T(128)} %param.10) | copy-start | bytes 100
  21.1 1.3 %collective-permute-start.2 = (f32[4,16,128]{2,1,0:T(8,128)S(1)}, f32[4,16,128]{2,1,0:T(8,128)S(1)}, u32[]{:S(2)}, u32[]{:S(2)}) collective-permute-start(f32[4,16,128]{2,1,0:T(8,128)S(1)} %slice.182), channel_id=1, source_target_pairs={{0,4},{4,0},{8,12},{12,8},{16,20},{20,16},{24,28},{28,24},{1,5},{5... | collective-permute-start | bytes 98312 | tf_op jit(solution)/shard_map/ppermute | solution.py:19
  22.4 3.9 %collective-permute-start.3 = (f32[3,16,128]{2,1,0:T(8,128)S(1)}, f32[3,16,128]{2,1,0:T(8,128)S(1)}, u32[]{:S(2)}, u32[]{:S(2)}) collective-permute-start(f32[3,16,128]{2,1,0:T(8,128)S(1)} %slice.237), channel_id=1, source_target_pairs={{0,8},{4,12},{8,0},{12,4},{16,24},{20,28},{24,16},{28,20},{1,9},{5... | collective-permute-start | bytes 73736 | tf_op jit(solution)/shard_map/ppermute | solution.py:19
  25.7 4.8 %copy-start.2 = (f32[5,2048]{1,0:T(8,128)S(1)}, f32[5,2048]{1,0:T(8,128)}, u32[]{:S(2)}) copy-start(f32[5,2048]{1,0:T(8,128)} %param.14) | copy-start | bytes 122884
  25.8 5.7 %copy-start.1 = (f32[16,2048]{1,0:T(8,128)S(1)}, f32[16,2048]{1,0:T(8,128)}, u32[]{:S(2)}) copy-start(f32[16,2048]{1,0:T(8,128)} %param.12) | copy-start | bytes 393220
  25.8 5.7 %copy-start.3 = (f32[2048]{0:T(1024)S(1)}, f32[2048]{0:T(1024)}, u32[]{:S(2)}) copy-start(f32[2048]{0:T(1024)} %param.11) | copy-start | bytes 24580
  26.4 3.8 %collective-permute-start.4 = (f32[2,16,128]{2,1,0:T(8,128)S(1)}, f32[2,16,128]{2,1,0:T(8,128)S(1)}, u32[]{:S(2)}, u32[]{:S(2)}) collective-permute-start(f32[2,16,128]{2,1,0:T(8,128)S(1)} %slice.188), channel_id=1, source_target_pairs={{0,16},{4,20},{8,24},{12,28},{16,0},{20,4},{24,8},{28,12},{1,17},{... | collective-permute-start | bytes 49160 | tf_op jit(solution)/shard_map/ppermute | solution.py:19
  31.6 3.6 %collective-permute-start.5 = (f32[16]{0:T(128)S(1)}, f32[16]{0:T(128)S(1)}, u32[]{:S(2)}, u32[]{:S(2)}) collective-permute-start(f32[16]{0:T(128)S(1)} %add.198), channel_id=1, source_target_pairs={{0,1},{1,0},{2,3},{3,2},{4,5},{5,4},{6,7},{7,6},{8,9},{9,8},{10,11... | collective-permute-start | bytes 200 | tf_op jit(solution)/shard_map/ppermute | solution.py:19
  35.2 4.4 %collective-permute-start.6 = (f32[16]{0:T(128)S(1)}, f32[16]{0:T(128)S(1)}, u32[]{:S(2)}, u32[]{:S(2)}) collective-permute-start(f32[16]{0:T(128)S(1)} %add.199), channel_id=1, source_target_pairs={{0,2},{1,3},{2,0},{3,1},{4,6},{5,7},{6,4},{7,5},{8,10},{9,11},{10,... | collective-permute-start | bytes 200 | tf_op jit(solution)/shard_map/ppermute | solution.py:19
  39.7 1.2 %collective-permute-start.7 = (f32[16]{0:T(128)S(1)}, f32[16]{0:T(128)S(1)}, u32[]{:S(2)}, u32[]{:S(2)}) collective-permute-start(f32[16]{0:T(128)S(1)} %add.203), channel_id=1, source_target_pairs={{0,4},{4,0},{8,12},{12,8},{16,20},{20,16},{24,28},{28,24},{1,5},{5... | collective-permute-start | bytes 200 | tf_op jit(solution)/shard_map/ppermute | solution.py:19
  40.9 3.6 %collective-permute-start.8 = (f32[16]{0:T(128)S(1)}, f32[16]{0:T(128)S(1)}, u32[]{:S(2)}, u32[]{:S(2)}) collective-permute-start(f32[16]{0:T(128)S(1)} %add.207), channel_id=1, source_target_pairs={{0,8},{4,12},{8,0},{12,4},{16,24},{20,28},{24,16},{28,20},{1,9},{5... | collective-permute-start | bytes 200 | tf_op jit(solution)/shard_map/ppermute | solution.py:19
  44.5 3.5 %collective-permute-start.9 = (f32[16]{0:T(128)S(1)}, f32[16]{0:T(128)S(1)}, u32[]{:S(2)}, u32[]{:S(2)}) collective-permute-start(f32[16]{0:T(128)S(1)} %add.210), channel_id=1, source_target_pairs={{0,16},{4,20},{8,24},{12,28},{16,0},{20,4},{24,8},{28,12},{1,17},{... | collective-permute-start | bytes 200 | tf_op jit(solution)/shard_map/ppermute | solution.py:19
  48.4 4.1 %collective-permute-start.10 = (f32[6,16,128]{2,1,0:T(8,128)S(1)}, f32[6,16,128]{2,1,0:T(8,128)S(1)}, u32[]{:S(2)}, u32[]{:S(2)}) collective-permute-start(f32[6,16,128]{2,1,0:T(8,128)S(1)} %pad_maximum_fusion.5), channel_id=1, source_target_pairs={{0,1},{1,0},{2,3},{3,2},{4,5},{5,4},{6,7},{7,6},{8,9},{9,8},{10,11... | collective-permute-start | bytes 147464 | tf_op jit(solution)/shard_map/ppermute | solution.py:19
  52.6 5.4 %collective-permute-start.11 = (f32[5,16,128]{2,1,0:T(8,128)S(1)}, f32[5,16,128]{2,1,0:T(8,128)S(1)}, u32[]{:S(2)}, u32[]{:S(2)}) collective-permute-start(f32[5,16,128]{2,1,0:T(8,128)S(1)} %slice.206), channel_id=1, source_target_pairs={{0,2},{1,3},{2,0},{3,1},{4,6},{5,7},{6,4},{7,5},{8,10},{9,11},{10,... | collective-permute-start | bytes 122888 | tf_op jit(solution)/shard_map/ppermute | solution.py:19
  58.0 1.3 %collective-permute-start.12 = (f32[4,16,128]{2,1,0:T(8,128)S(1)}, f32[4,16,128]{2,1,0:T(8,128)S(1)}, u32[]{:S(2)}, u32[]{:S(2)}) collective-permute-start(f32[4,16,128]{2,1,0:T(8,128)S(1)} %slice.211), channel_id=1, source_target_pairs={{0,4},{4,0},{8,12},{12,8},{16,20},{20,16},{24,28},{28,24},{1,5},{5... | collective-permute-start | bytes 98312 | tf_op jit(solution)/shard_map/ppermute | solution.py:19
  59.3 3.9 %collective-permute-start.13 = (f32[3,16,128]{2,1,0:T(8,128)S(1)}, f32[3,16,128]{2,1,0:T(8,128)S(1)}, u32[]{:S(2)}, u32[]{:S(2)}) collective-permute-start(f32[3,16,128]{2,1,0:T(8,128)S(1)} %slice.252), channel_id=1, source_target_pairs={{0,8},{4,12},{8,0},{12,4},{16,24},{20,28},{24,16},{28,20},{1,9},{5... | collective-permute-start | bytes 73736 | tf_op jit(solution)/shard_map/ppermute | solution.py:19
  63.2 3.8 %collective-permute-start.14 = (f32[2,16,128]{2,1,0:T(8,128)S(1)}, f32[2,16,128]{2,1,0:T(8,128)S(1)}, u32[]{:S(2)}, u32[]{:S(2)}) collective-permute-start(f32[2,16,128]{2,1,0:T(8,128)S(1)} %slice.215), channel_id=1, source_target_pairs={{0,16},{4,20},{8,24},{12,28},{16,0},{20,4},{24,8},{28,12},{1,17},{... | collective-permute-start | bytes 49160 | tf_op jit(solution)/shard_map/ppermute | solution.py:19
  68.8 3.6 %collective-permute-start.15 = (f32[16]{0:T(128)S(1)}, f32[16]{0:T(128)S(1)}, u32[]{:S(2)}, u32[]{:S(2)}) collective-permute-start(f32[16]{0:T(128)S(1)} %add.227), channel_id=1, source_target_pairs={{0,1},{1,0},{2,3},{3,2},{4,5},{5,4},{6,7},{7,6},{8,9},{9,8},{10,11... | collective-permute-start | bytes 200 | tf_op jit(solution)/shard_map/ppermute | solution.py:19
  72.4 4.4 %collective-permute-start.16 = (f32[16]{0:T(128)S(1)}, f32[16]{0:T(128)S(1)}, u32[]{:S(2)}, u32[]{:S(2)}) collective-permute-start(f32[16]{0:T(128)S(1)} %add.228), channel_id=1, source_target_pairs={{0,2},{1,3},{2,0},{3,1},{4,6},{5,7},{6,4},{7,5},{8,10},{9,11},{10,... | collective-permute-start | bytes 200 | tf_op jit(solution)/shard_map/ppermute | solution.py:19
  76.9 1.1 %collective-permute-start.17 = (f32[16]{0:T(128)S(1)}, f32[16]{0:T(128)S(1)}, u32[]{:S(2)}, u32[]{:S(2)}) collective-permute-start(f32[16]{0:T(128)S(1)} %add.232), channel_id=1, source_target_pairs={{0,4},{4,0},{8,12},{12,8},{16,20},{20,16},{24,28},{28,24},{1,5},{5... | collective-permute-start | bytes 200 | tf_op jit(solution)/shard_map/ppermute | solution.py:19
  78.0 3.5 %collective-permute-start.18 = (f32[16]{0:T(128)S(1)}, f32[16]{0:T(128)S(1)}, u32[]{:S(2)}, u32[]{:S(2)}) collective-permute-start(f32[16]{0:T(128)S(1)} %add.236), channel_id=1, source_target_pairs={{0,8},{4,12},{8,0},{12,4},{16,24},{20,28},{24,16},{28,20},{1,9},{5... | collective-permute-start | bytes 200 | tf_op jit(solution)/shard_map/ppermute | solution.py:19
  81.5 3.5 %collective-permute-start.19 = (f32[16]{0:T(128)S(1)}, f32[16]{0:T(128)S(1)}, u32[]{:S(2)}, u32[]{:S(2)}) collective-permute-start(f32[16]{0:T(128)S(1)} %add.237), channel_id=1, source_target_pairs={{0,16},{4,20},{8,24},{12,28},{16,0},{20,4},{24,8},{28,12},{1,17},{... | collective-permute-start | bytes 200 | tf_op jit(solution)/shard_map/ppermute | solution.py:19

commit v18 on v17

--- a/solution.py
+++ b/solution.py
@@ -82,14 +82,16 @@
     rounds += [("gx", bit) for bit in range(lax.axis_size("gx").bit_length() - 1)]
     for index, (axis, bit) in enumerate(rounds):
         partner = swapped(value, axis, bit)
-        if index < len(stages):
+        stage = stages[index] if index < len(stages) else None
+        if stage is not None:
             state, value = lax.optimization_barrier((state, value))
-            state = stages[index](state)
+            state = stage(state)
         value = value + partner
-        if index < len(stages):
+        if stage is not None:
             value, state = lax.optimization_barrier((value, state))
     for stage in stages[len(rounds) :]:
-        state = stage(state)
+        if stage is not None:
+            state = stage(state)
     return value, state
 
 
@@ -190,7 +192,7 @@
 
         stages = [unpermute_first, unpermute_second]
         if step + 1 < ITERATIONS:
-            stages.append(project_image)
+            stages += [None, project_image]
         curve, (late_u, near, image_proj) = butterfly(local, stages, (late_u, carried, carried))
         alpha = norm_now / curve
         solution = solution + alpha[:, None] * direction

time: 86.2 us -> 85.8 us (level)
  waiting for transfers between devices: 26.8 us -> 25.3 us
  starting transfers between devices: 20.6 us -> 21.7 us
    ppermute x20, waiting for transfers between devices: 26.8 us -> 25.3 us  [swapped(): return lax.ppermute(value, axis, pairs)]
    ppermute x20, starting transfers between devices: 20.6 us -> 21.7 us  [swapped(): return lax.ppermute(value, axis, pairs)]
where the time goes in v18:
time: 85.8 us; the launch traced here: 85.5 us
  matrix products  27.4 us (32%)
  waiting for transfers between devices  25.3 us (29%)
  starting transfers between devices  21.7 us (25%)
  other arithmetic  5.9 us (7%)
  local copies, waits for them, and re-layouts  4.03 us (5%)
  between operations  1.21 us (1%)
    ppermute x20, waiting for transfers between devices, swapped(): return lax.ppermute(value, axis, pairs)  25.3 us
    ppermute x20, starting transfers between devices, swapped(): return lax.ppermute(value, axis, pairs)  21.7 us
    dot_general x4, matrix products, from_union(): jnp.einsum('gci,gip->cp', pieces(values_u, 1), hot, preferred_element_typ...  7.26 us
    dot_general x3, matrix products, to_union(): jnp.einsum('cp,gip->gci', pieces(values, 0), hot, preferred_element_type=...  7.1 us
    dot_general x2, matrix products, near_apply(): jnp.einsum('gij,gcj->gci', kern, union_vec, precision=lax.Precision.HIGH)  3.91 us
    dot_general x2, matrix products, project(): jnp.einsum('lp,cp,rp->lcr', level_gain, values, basis, precision=highest)  3.33 us
    dot_general x1, matrix products, kernel_blocks(): product = jnp.einsum('lrs,lts->lrt', coupling, coupling, precision=highest)  1.86 us
  transfers between devices with their start and end apart: 20, of which 17 were waited for; matrix products, arithmetic and copies ran while one was open for 34% of the time, Pallas kernels for 0%

profile of v18, /device:TPU:0, one launch (start us, length us, event | category | flops | bytes accessed | tf_op | source)
XLA Modules:
  0.0 85.5 jit_solution(18015908085487113079)
XLA Ops:
  0.6 1.1 %multiply_reduce_fusion.5 = f32[16]{0:T(128)S(1)} fusion(f32[16,2048]{1,0:T(8,128)} %param.12), kind=kLoop, calls=%fused_computation.102 | loop fusion | flops 65520 | bytes 131136 | tf_op jit(solution)/shard_map/reduce_sum | solution.py:115
  1.9 2.1 %convolution_bitcast_fusion.1 = f32[5,16,128]{2,1,0:T(8,128)S(1)} fusion(f32[128,2048]{1,0:T(8,128)S(1)} %copy-done, f32[2048,5]{0,1:T(8,128)} %bitcast.68, f32[2048,16]{0,1:T(8,128)} %bitcast.67), kind=kOutput, calls=%fused_computation.33 | convolution fusion | flops 251822080 | bytes 1261568 | tf_op jit(solution)/shard_map/lp,cp,rp->lcr/dot_general | solution.py:112
  4.1 3.0 %collective-permute-start = (f32[6,16,128]{2,1,0:T(8,128)S(1)}, f32[6,16,128]{2,1,0:T(8,128)S(1)}, u32[]{:S(2)}, u32[]{:S(2)}) collective-permute-start(f32[6,16,128]{2,1,0:T(8,128)S(1)} %pad_maximum_fusion), channel_id=1, source_target_pairs={{0,1},{1,0},{2,3},{3,2},{4,5},{5,4},{6,7},{7,6},{8,9},{9,8},{10,11... | collective-permute-start | bytes 147464 | tf_op jit(solution)/shard_map/ppermute | solution.py:19
  7.7 1.4 %reduce.9 = s32[2048]{0:T(1024)S(1)} reduce(s32[1,2048]{1,0:T(1,128)} %param.16, s32[]{:T(128)} %broadcast.100), dimensions={0}, to_apply=%param.16.reduce_sub_computation.3 | reduce | bytes 16388 | tf_op args[7]
  9.1 0.8 fusion.84
  9.8 0.6 gather_fusion
  11.0 1.9 %convolution_multiply_fusion.2 = f32[5,128,128]{2,1,0:T(8,128)S(1)} fusion(f32[5,128,128]{2,1,0:T(8,128)} %param.15, f32[5]{0:T(128)S(1)} %multiply_power_fusion), kind=kOutput, calls=%fused_computation.29 | convolution fusion | flops 125911040 | bytes 655380 | tf_op jit(solution)/shard_map/lrs,lts->lrt/dot_general | solution.py:151
  12.9 2.7 %collective-permute-start.1 = (f32[5,16,128]{2,1,0:T(8,128)S(1)}, f32[5,16,128]{2,1,0:T(8,128)S(1)}, u32[]{:S(2)}, u32[]{:S(2)}) collective-permute-start(f32[5,16,128]{2,1,0:T(8,128)S(1)} %slice.231), channel_id=1, source_target_pairs={{0,2},{1,3},{2,0},{3,1},{4,6},{5,7},{6,4},{7,5},{8,10},{9,11},{10,... | collective-permute-start | bytes 122888 | tf_op jit(solution)/shard_map/ppermute | solution.py:19
  15.6 0.8 constant_dynamic-update-slice_fusion.3
  16.4 0.9 %constant_dynamic-update-slice_fusion.2 = f32[24,2048]{1,0:T(8,128)S(1)} fusion(f32[24,2048]{1,0:T(8,128)S(1)} %constant_dynamic-update-slice_fusion.3, f32[16,2048]{1,0:T(8,128)} %param.12), kind=kLoop, calls=%fused_computation.173 | loop fusion | bytes 262144 | tf_op jit(solution)/shard_map/concatenate | solution.py:146
  17.4 3.5 %fusion.18 = f32[4,72,512]{2,1,0:T(8,128)S(1)} fusion(s32[4,512]{1,0:T(4,128)S(1)} %constant_dynamic-update-slice_fusion, bf16[24,2048]{1,0:T(8,128)(2,1)S(1)} %get-tuple-element.153, bf16[24,2048]{1,0:T(8,128)(2,1)S(1)} %get-tuple-element.154, bf16[24,2048]{1,0:T(8,128)(2,1)S(1)} %get-tuple-element.152), kind=kOutput, calls=%fused_computation.26 | convolution fusion | flops 609058816 | bytes 892928 | tf_op jit(solution)/shard_map/cp,gip->gci/dot_general | solution.py:49
  21.2 1.2 %collective-permute-done.2 = f32[4,16,128]{2,1,0:T(8,128)S(1)} collective-permute-done((f32[4,16,128]{2,1,0:T(8,128)S(1)}, f32[4,16,128]{2,1,0:T(8,128)S(1)}, u32[]{:S(2)}, u32[]{:S(2)}) %collective-permute-start.2) | collective-permute-done | bytes 32800 | tf_op jit(solution)/shard_map/ppermute | solution.py:19
  22.4 1.6 %collective-permute-start.3 = (f32[3,16,128]{2,1,0:T(8,128)S(1)}, f32[3,16,128]{2,1,0:T(8,128)S(1)}, u32[]{:S(2)}, u32[]{:S(2)}) collective-permute-start(f32[3,16,128]{2,1,0:T(8,128)S(1)} %slice.237), channel_id=1, source_target_pairs={{0,8},{4,12},{8,0},{12,4},{16,24},{20,28},{24,16},{28,20},{1,9},{5... | collective-permute-start | bytes 73736 | tf_op jit(solution)/shard_map/ppermute | solution.py:19
  24.1 1.6 %exponential_multiply_fusion = f32[4,512,512]{2,1,0:T(8,128)S(1)} fusion(bf16[4,48,512]{2,1,0:T(8,128)(2,1)S(1)} %get-tuple-element.180, bf16[4,48,512]{2,1,0:T(8,128)(2,1)S(1)} %get-tuple-element.179, f32[4,512]{1,0:T(4,128)S(1)} %multiply_reduce_fusion.6), kind=kOutput, calls=%fused_computation.19 | convolution fusion | flops 105906176 | bytes 4595712 | tf_op jit(solution)/shard_map/gfi,gfj->gij/dot_general | solution.py:33
  26.4 1.6 %collective-permute-start.4 = (f32[2,16,128]{2,1,0:T(8,128)S(1)}, f32[2,16,128]{2,1,0:T(8,128)S(1)}, u32[]{:S(2)}, u32[]{:S(2)}) collective-permute-start(f32[2,16,128]{2,1,0:T(8,128)S(1)} %slice.188), channel_id=1, source_target_pairs={{0,16},{4,20},{8,24},{12,28},{16,0},{20,4},{24,8},{28,12},{1,17},{... | collective-permute-start | bytes 49160 | tf_op jit(solution)/shard_map/ppermute | solution.py:19
  27.9 1.8 %fusion.96 = f32[4,16,512]{2,1,0:T(8,128)S(1)} fusion(f32[4,16,512]{2,1,0:T(8,128)S(1)} %slice.236, f32[4,512,512]{2,1,0:T(8,128)S(1)} %exponential_multiply_fusion), kind=kOutput, calls=%fused_computation.219 | convolution fusion | flops 100663296 | bytes 4456448 | tf_op jit(solution)/shard_map/gij,gcj->gci/dot_general | solution.py:40
  30.6 0.8 fusion.19
  32.2 1.8 %fusion.14 = f32[48,2048]{1,0:T(8,128)S(1)} fusion(s32[2,512]{1,0:T(2,128)S(1)} %get-tuple-element.184, bf16[2,16,512]{2,1,0:T(8,128)(2,1)S(1)} %get-tuple-element.171, bf16[2,16,512]{2,1,0:T(8,128)(2,1)S(1)} %get-tuple-element.172, bf16[2,16,512]{2,1,0:T(8,128)(2,1)S(1)} %get-tuple-element.170), kind=kOutput, calls=%fused_computation.22 | convolution fusion | flops 203718656 | bytes 495616 | tf_op jit(solution)/shard_map/gci,gip->cp/dot_general | solution.py:55
  34.0 1.2 %collective-permute-done.5 = f32[16]{0:T(128)S(1)} collective-permute-done((f32[16]{0:T(128)S(1)}, f32[16]{0:T(128)S(1)}, u32[]{:S(2)}, u32[]{:S(2)}) %collective-permute-start.5) | collective-permute-done | bytes 96 | tf_op jit(solution)/shard_map/ppermute | solution.py:19
  35.6 1.8 %fusion.16 = f32[48,2048]{1,0:T(8,128)S(1)} fusion(s32[2,512]{1,0:T(2,128)S(1)} %get-tuple-element.183, bf16[2,16,512]{2,1,0:T(8,128)(2,1)S(1)} %get-tuple-element.168, bf16[2,16,512]{2,1,0:T(8,128)(2,1)S(1)} %get-tuple-element.169, bf16[2,16,512]{2,1,0:T(8,128)(2,1)S(1)} %get-tuple-element.167), kind=kOutput, calls=%fused_computation.24 | convolution fusion | flops 203718656 | bytes 495616 | tf_op jit(solution)/shard_map/gci,gip->cp/dot_general | solution.py:55
  37.4 2.2 %collective-permute-done.6 = f32[16]{0:T(128)S(1)} collective-permute-done((f32[16]{0:T(128)S(1)}, f32[16]{0:T(128)S(1)}, u32[]{:S(2)}, u32[]{:S(2)}) %collective-permute-start.6) | collective-permute-done | bytes 96 | tf_op jit(solution)/shard_map/ppermute | solution.py:19
  39.7 1.1 %collective-permute-done.7 = f32[16]{0:T(128)S(1)} collective-permute-done((f32[16]{0:T(128)S(1)}, f32[16]{0:T(128)S(1)}, u32[]{:S(2)}, u32[]{:S(2)}) %collective-permute-start.7) | collective-permute-done | bytes 96 | tf_op jit(solution)/shard_map/ppermute | solution.py:19
  40.8 1.5 %collective-permute-start.8 = (f32[16]{0:T(128)S(1)}, f32[16]{0:T(128)S(1)}, u32[]{:S(2)}, u32[]{:S(2)}) collective-permute-start(f32[16]{0:T(128)S(1)} %add.207), channel_id=1, source_target_pairs={{0,8},{4,12},{8,0},{12,4},{16,24},{20,28},{24,16},{28,20},{1,9},{5... | collective-permute-start | bytes 200 | tf_op jit(solution)/shard_map/ppermute | solution.py:19
  42.3 1.2 %convolution_bitcast_fusion = f32[5,16,128]{2,1,0:T(8,128)S(1)} fusion(f32[128,2048]{1,0:T(8,128)S(1)} %copy-done, f32[2048,16]{0,1:T(8,128)S(1)} %add_bitcast_fusion, f32[2048,5]{0,1:T(8,128)S(1)} %bitcast.69), kind=kOutput, calls=%fused_computation.32 | convolution fusion | flops 251822080 | bytes 1261568 | tf_op jit(solution)/shard_map/lp,cp,rp->lcr/dot_general | solution.py:112
  43.5 0.8 collective-permute-done.8
  44.3 1.5 %collective-permute-start.9 = (f32[16]{0:T(128)S(1)}, f32[16]{0:T(128)S(1)}, u32[]{:S(2)}, u32[]{:S(2)}) collective-permute-start(f32[16]{0:T(128)S(1)} %add.208), channel_id=1, source_target_pairs={{0,16},{4,20},{8,24},{12,28},{16,0},{20,4},{24,8},{28,12},{1,17},{... | collective-permute-start | bytes 200 | tf_op jit(solution)/shard_map/ppermute | solution.py:19
  46.0 1.9 %collective-permute-done.9 = f32[16]{0:T(128)S(1)} collective-permute-done((f32[16]{0:T(128)S(1)}, f32[16]{0:T(128)S(1)}, u32[]{:S(2)}, u32[]{:S(2)}) %collective-permute-start.9) | collective-permute-done | bytes 96 | tf_op jit(solution)/shard_map/ppermute | solution.py:19
  48.8 1.8 %fusion.21 = f32[2,48,512]{2,1,0:T(8,128)S(1)} fusion(s32[2,512]{1,0:T(2,128)S(1)} %get-tuple-element.184, bf16[16,2048]{1,0:T(8,128)(2,1)S(1)} %get-tuple-element.165, bf16[16,2048]{1,0:T(8,128)(2,1)S(1)} %get-tuple-element.166, bf16[16,2048]{1,0:T(8,128)(2,1)S(1)} %get-tuple-element.164), kind=kOutput, calls=%fused_computation.30 | convolution fusion | flops 204013568 | bytes 397312 | tf_op jit(solution)/shard_map/cp,gip->gci/dot_general | solution.py:49
  50.6 1.8 %collective-permute-done.10 = f32[6,16,128]{2,1,0:T(8,128)S(1)} collective-permute-done((f32[6,16,128]{2,1,0:T(8,128)S(1)}, f32[6,16,128]{2,1,0:T(8,128)S(1)}, u32[]{:S(2)}, u32[]{:S(2)}) %collective-permute-start.10) | collective-permute-done | bytes 49184 | tf_op jit(solution)/shard_map/ppermute | solution.py:19
  52.9 1.8 %fusion.22 = f32[2,48,512]{2,1,0:T(8,128)S(1)} fusion(s32[2,512]{1,0:T(2,128)S(1)} %get-tuple-element.183, bf16[16,2048]{1,0:T(8,128)(2,1)S(1)} %get-tuple-element.162, bf16[16,2048]{1,0:T(8,128)(2,1)S(1)} %get-tuple-element.163, bf16[16,2048]{1,0:T(8,128)(2,1)S(1)} %get-tuple-element.161), kind=kOutput, calls=%fused_computation.31 | convolution fusion | flops 204013568 | bytes 397312 | tf_op jit(solution)/shard_map/cp,gip->gci/dot_general | solution.py:49
  54.8 2.6 %collective-permute-done.11 = f32[5,16,128]{2,1,0:T(8,128)S(1)} collective-permute-done((f32[5,16,128]{2,1,0:T(8,128)S(1)}, f32[5,16,128]{2,1,0:T(8,128)S(1)}, u32[]{:S(2)}, u32[]{:S(2)}) %collective-permute-start.11) | collective-permute-done | bytes 40992 | tf_op jit(solution)/shard_map/ppermute | solution.py:19
  57.5 1.2 %collective-permute-done.12 = f32[4,16,128]{2,1,0:T(8,128)S(1)} collective-permute-done((f32[4,16,128]{2,1,0:T(8,128)S(1)}, f32[4,16,128]{2,1,0:T(8,128)S(1)}, u32[]{:S(2)}, u32[]{:S(2)}) %collective-permute-start.12) | collective-permute-done | bytes 32800 | tf_op jit(solution)/shard_map/ppermute | solution.py:19
  58.7 2.0 %collective-permute-start.13 = (f32[3,16,128]{2,1,0:T(8,128)S(1)}, f32[3,16,128]{2,1,0:T(8,128)S(1)}, u32[]{:S(2)}, u32[]{:S(2)}) collective-permute-start(f32[3,16,128]{2,1,0:T(8,128)S(1)} %slice.252), channel_id=1, source_target_pairs={{0,8},{4,12},{8,0},{12,4},{16,24},{20,28},{24,16},{28,20},{1,9},{5... | collective-permute-start | bytes 73736 | tf_op jit(solution)/shard_map/ppermute | solution.py:19
  60.7 2.1 %fusion.98 = f32[4,16,512]{2,1,0:T(8,128)S(1)} fusion(f32[4,16,512]{2,1,0:T(8,128)S(1)} %constant_dynamic-update-slice_fusion.16, f32[4,512,512]{2,1,0:T(8,128)S(1)} %exponential_multiply_fusion), kind=kOutput, calls=%fused_computation.221 | convolution fusion | flops 100663296 | bytes 4456448 | tf_op jit(solution)/shard_map/gij,gcj->gci/dot_general | solution.py:40
  62.8 1.6 %collective-permute-start.14 = (f32[2,16,128]{2,1,0:T(8,128)S(1)}, f32[2,16,128]{2,1,0:T(8,128)S(1)}, u32[]{:S(2)}, u32[]{:S(2)}) collective-permute-start(f32[2,16,128]{2,1,0:T(8,128)S(1)} %slice.215), channel_id=1, source_target_pairs={{0,16},{4,20},{8,24},{12,28},{16,0},{20,4},{24,8},{28,12},{1,17},{... | collective-permute-start | bytes 49160 | tf_op jit(solution)/shard_map/ppermute | solution.py:19
  64.4 2.2 %collective-permute-done.14 = f32[2,16,128]{2,1,0:T(8,128)S(1)} collective-permute-done((f32[2,16,128]{2,1,0:T(8,128)S(1)}, f32[2,16,128]{2,1,0:T(8,128)S(1)}, u32[]{:S(2)}, u32[]{:S(2)}) %collective-permute-start.14) | collective-permute-done | bytes 16416 | tf_op jit(solution)/shard_map/ppermute | solution.py:19
  67.2 0.8 fusion.20
  68.4 0.8 collective-permute-start.15
  69.3 1.8 %fusion.15 = f32[48,2048]{1,0:T(8,128)S(1)} fusion(s32[2,512]{1,0:T(2,128)S(1)} %get-tuple-element.184, bf16[2,16,512]{2,1,0:T(8,128)(2,1)S(1)} %get-tuple-element.159, bf16[2,16,512]{2,1,0:T(8,128)(2,1)S(1)} %get-tuple-element.160, bf16[2,16,512]{2,1,0:T(8,128)(2,1)S(1)} %get-tuple-element.158), kind=kOutput, calls=%fused_computation.23 | convolution fusion | flops 203718656 | bytes 495616 | tf_op jit(solution)/shard_map/gci,gip->cp/dot_general | solution.py:55
  71.1 0.9 %collective-permute-done.15 = f32[16]{0:T(128)S(1)} collective-permute-done((f32[16]{0:T(128)S(1)}, f32[16]{0:T(128)S(1)}, u32[]{:S(2)}, u32[]{:S(2)}) %collective-permute-start.15) | collective-permute-done | bytes 96 | tf_op jit(solution)/shard_map/ppermute | solution.py:19
  72.2 1.8 %fusion.17 = f32[48,2048]{1,0:T(8,128)S(1)} fusion(s32[2,512]{1,0:T(2,128)S(1)} %get-tuple-element.183, bf16[2,16,512]{2,1,0:T(8,128)(2,1)S(1)} %get-tuple-element.156, bf16[2,16,512]{2,1,0:T(8,128)(2,1)S(1)} %get-tuple-element.157, bf16[2,16,512]{2,1,0:T(8,128)(2,1)S(1)} %get-tuple-element.155), kind=kOutput, calls=%fused_computation.25 | convolution fusion | flops 203718656 | bytes 495616 | tf_op jit(solution)/shard_map/gci,gip->cp/dot_general | solution.py:55
  74.1 2.3 %collective-permute-done.16 = f32[16]{0:T(128)S(1)} collective-permute-done((f32[16]{0:T(128)S(1)}, f32[16]{0:T(128)S(1)}, u32[]{:S(2)}, u32[]{:S(2)}) %collective-permute-start.16) | collective-permute-done | bytes 96 | tf_op jit(solution)/shard_map/ppermute | solution.py:19
  76.4 1.1 %collective-permute-done.17 = f32[16]{0:T(128)S(1)} collective-permute-done((f32[16]{0:T(128)S(1)}, f32[16]{0:T(128)S(1)}, u32[]{:S(2)}, u32[]{:S(2)}) %collective-permute-start.17) | collective-permute-done | bytes 96 | tf_op jit(solution)/shard_map/ppermute | solution.py:19
  77.6 1.7 %collective-permute-start.18 = (f32[16]{0:T(128)S(1)}, f32[16]{0:T(128)S(1)}, u32[]{:S(2)}, u32[]{:S(2)}) collective-permute-start(f32[16]{0:T(128)S(1)} %add.236), channel_id=1, source_target_pairs={{0,8},{4,12},{8,0},{12,4},{16,24},{20,28},{24,16},{28,20},{1,9},{5... | collective-permute-start | bytes 200 | tf_op jit(solution)/shard_map/ppermute | solution.py:19
  79.3 1.8 %collective-permute-done.18 = f32[16]{0:T(128)S(1)} collective-permute-done((f32[16]{0:T(128)S(1)}, f32[16]{0:T(128)S(1)}, u32[]{:S(2)}, u32[]{:S(2)}) %collective-permute-start.18) | collective-permute-done | bytes 96 | tf_op jit(solution)/shard_map/ppermute | solution.py:19
  81.1 1.5 %collective-permute-start.19 = (f32[16]{0:T(128)S(1)}, f32[16]{0:T(128)S(1)}, u32[]{:S(2)}, u32[]{:S(2)}) collective-permute-start(f32[16]{0:T(128)S(1)} %add.237), channel_id=1, source_target_pairs={{0,16},{4,20},{8,24},{12,28},{16,0},{20,4},{24,8},{28,12},{1,17},{... | collective-permute-start | bytes 200 | tf_op jit(solution)/shard_map/ppermute | solution.py:19
  82.6 2.0 %collective-permute-done.19 = f32[16]{0:T(128)S(1)} collective-permute-done((f32[16]{0:T(128)S(1)}, f32[16]{0:T(128)S(1)}, u32[]{:S(2)}, u32[]{:S(2)}) %collective-permute-start.19) | collective-permute-done | bytes 96 | tf_op jit(solution)/shard_map/ppermute | solution.py:19
  84.7 0.8 multiply_subtract_fusion
  (122 shorter events, 7.4 us)
Async XLA Ops:
  0.6 1.3 %copy-start = (f32[128,2048]{1,0:T(8,128)S(1)}, f32[128,2048]{1,0:T(8,128)}, u32[]{:S(2)}) copy-start(f32[128,2048]{1,0:T(8,128)} %param.13) | copy-start | bytes 3145732
  4.1 8.7 %collective-permute-start = (f32[6,16,128]{2,1,0:T(8,128)S(1)}, f32[6,16,128]{2,1,0:T(8,128)S(1)}, u32[]{:S(2)}, u32[]{:S(2)}) collective-permute-start(f32[6,16,128]{2,1,0:T(8,128)S(1)} %pad_maximum_fusion), channel_id=1, source_target_pairs={{0,1},{1,0},{2,3},{3,2},{4,5},{5,4},{6,7},{7,6},{8,9},{9,8},{10,11... | collective-permute-start | bytes 147464 | tf_op jit(solution)/shard_map/ppermute | solution.py:19
  12.9 8.1 %collective-permute-start.1 = (f32[5,16,128]{2,1,0:T(8,128)S(1)}, f32[5,16,128]{2,1,0:T(8,128)S(1)}, u32[]{:S(2)}, u32[]{:S(2)}) collective-permute-start(f32[5,16,128]{2,1,0:T(8,128)S(1)} %slice.231), channel_id=1, source_target_pairs={{0,2},{1,3},{2,0},{3,1},{4,6},{5,7},{6,4},{7,5},{8,10},{9,11},{10,... | collective-permute-start | bytes 122888 | tf_op jit(solution)/shard_map/ppermute | solution.py:19
  16.4 4.5 %copy-start.4 = (f32[8]{0:T(128)S(1)}, f32[8]{0:T(128)}, u32[]{:S(2)}) copy-start(f32[8]{0:T(128)} %param.10) | copy-start | bytes 100
  21.1 1.3 %collective-permute-start.2 = (f32[4,16,128]{2,1,0:T(8,128)S(1)}, f32[4,16,128]{2,1,0:T(8,128)S(1)}, u32[]{:S(2)}, u32[]{:S(2)}) collective-permute-start(f32[4,16,128]{2,1,0:T(8,128)S(1)} %slice.182), channel_id=1, source_target_pairs={{0,4},{4,0},{8,12},{12,8},{16,20},{20,16},{24,28},{28,24},{1,5},{5... | collective-permute-start | bytes 98312 | tf_op jit(solution)/shard_map/ppermute | solution.py:19
  22.4 3.9 %collective-permute-start.3 = (f32[3,16,128]{2,1,0:T(8,128)S(1)}, f32[3,16,128]{2,1,0:T(8,128)S(1)}, u32[]{:S(2)}, u32[]{:S(2)}) collective-permute-start(f32[3,16,128]{2,1,0:T(8,128)S(1)} %slice.237), channel_id=1, source_target_pairs={{0,8},{4,12},{8,0},{12,4},{16,24},{20,28},{24,16},{28,20},{1,9},{5... | collective-permute-start | bytes 73736 | tf_op jit(solution)/shard_map/ppermute | solution.py:19
  25.7 4.8 %copy-start.2 = (f32[5,2048]{1,0:T(8,128)S(1)}, f32[5,2048]{1,0:T(8,128)}, u32[]{:S(2)}) copy-start(f32[5,2048]{1,0:T(8,128)} %param.14) | copy-start | bytes 122884
  25.8 5.7 %copy-start.1 = (f32[16,2048]{1,0:T(8,128)S(1)}, f32[16,2048]{1,0:T(8,128)}, u32[]{:S(2)}) copy-start(f32[16,2048]{1,0:T(8,128)} %param.12) | copy-start | bytes 393220
  25.8 5.7 %copy-start.3 = (f32[2048]{0:T(1024)S(1)}, f32[2048]{0:T(1024)}, u32[]{:S(2)}) copy-start(f32[2048]{0:T(1024)} %param.11) | copy-start | bytes 24580
  26.4 3.8 %collective-permute-start.4 = (f32[2,16,128]{2,1,0:T(8,128)S(1)}, f32[2,16,128]{2,1,0:T(8,128)S(1)}, u32[]{:S(2)}, u32[]{:S(2)}) collective-permute-start(f32[2,16,128]{2,1,0:T(8,128)S(1)} %slice.188), channel_id=1, source_target_pairs={{0,16},{4,20},{8,24},{12,28},{16,0},{20,4},{24,8},{28,12},{1,17},{... | collective-permute-start | bytes 49160 | tf_op jit(solution)/shard_map/ppermute | solution.py:19
  31.6 3.6 %collective-permute-start.5 = (f32[16]{0:T(128)S(1)}, f32[16]{0:T(128)S(1)}, u32[]{:S(2)}, u32[]{:S(2)}) collective-permute-start(f32[16]{0:T(128)S(1)} %add.198), channel_id=1, source_target_pairs={{0,1},{1,0},{2,3},{3,2},{4,5},{5,4},{6,7},{7,6},{8,9},{9,8},{10,11... | collective-permute-start | bytes 200 | tf_op jit(solution)/shard_map/ppermute | solution.py:19
  35.2 4.4 %collective-permute-start.6 = (f32[16]{0:T(128)S(1)}, f32[16]{0:T(128)S(1)}, u32[]{:S(2)}, u32[]{:S(2)}) collective-permute-start(f32[16]{0:T(128)S(1)} %add.199), channel_id=1, source_target_pairs={{0,2},{1,3},{2,0},{3,1},{4,6},{5,7},{6,4},{7,5},{8,10},{9,11},{10,... | collective-permute-start | bytes 200 | tf_op jit(solution)/shard_map/ppermute | solution.py:19
  39.7 1.1 %collective-permute-start.7 = (f32[16]{0:T(128)S(1)}, f32[16]{0:T(128)S(1)}, u32[]{:S(2)}, u32[]{:S(2)}) collective-permute-start(f32[16]{0:T(128)S(1)} %add.203), channel_id=1, source_target_pairs={{0,4},{4,0},{8,12},{12,8},{16,20},{20,16},{24,28},{28,24},{1,5},{5... | collective-permute-start | bytes 200 | tf_op jit(solution)/shard_map/ppermute | solution.py:19
  40.8 3.5 %collective-permute-start.8 = (f32[16]{0:T(128)S(1)}, f32[16]{0:T(128)S(1)}, u32[]{:S(2)}, u32[]{:S(2)}) collective-permute-start(f32[16]{0:T(128)S(1)} %add.207), channel_id=1, source_target_pairs={{0,8},{4,12},{8,0},{12,4},{16,24},{20,28},{24,16},{28,20},{1,9},{5... | collective-permute-start | bytes 200 | tf_op jit(solution)/shard_map/ppermute | solution.py:19
  44.3 3.5 %collective-permute-start.9 = (f32[16]{0:T(128)S(1)}, f32[16]{0:T(128)S(1)}, u32[]{:S(2)}, u32[]{:S(2)}) collective-permute-start(f32[16]{0:T(128)S(1)} %add.208), channel_id=1, source_target_pairs={{0,16},{4,20},{8,24},{12,28},{16,0},{20,4},{24,8},{28,12},{1,17},{... | collective-permute-start | bytes 200 | tf_op jit(solution)/shard_map/ppermute | solution.py:19
  48.2 4.1 %collective-permute-start.10 = (f32[6,16,128]{2,1,0:T(8,128)S(1)}, f32[6,16,128]{2,1,0:T(8,128)S(1)}, u32[]{:S(2)}, u32[]{:S(2)}) collective-permute-start(f32[6,16,128]{2,1,0:T(8,128)S(1)} %pad_maximum_fusion.5), channel_id=1, source_target_pairs={{0,1},{1,0},{2,3},{3,2},{4,5},{5,4},{6,7},{7,6},{8,9},{9,8},{10,11... | collective-permute-start | bytes 147464 | tf_op jit(solution)/shard_map/ppermute | solution.py:19
  52.4 5.0 %collective-permute-start.11 = (f32[5,16,128]{2,1,0:T(8,128)S(1)}, f32[5,16,128]{2,1,0:T(8,128)S(1)}, u32[]{:S(2)}, u32[]{:S(2)}) collective-permute-start(f32[5,16,128]{2,1,0:T(8,128)S(1)} %slice.206), channel_id=1, source_target_pairs={{0,2},{1,3},{2,0},{3,1},{4,6},{5,7},{6,4},{7,5},{8,10},{9,11},{10,... | collective-permute-start | bytes 122888 | tf_op jit(solution)/shard_map/ppermute | solution.py:19
  57.4 1.3 %collective-permute-start.12 = (f32[4,16,128]{2,1,0:T(8,128)S(1)}, f32[4,16,128]{2,1,0:T(8,128)S(1)}, u32[]{:S(2)}, u32[]{:S(2)}) collective-permute-start(f32[4,16,128]{2,1,0:T(8,128)S(1)} %slice.211), channel_id=1, source_target_pairs={{0,4},{4,0},{8,12},{12,8},{16,20},{20,16},{24,28},{28,24},{1,5},{5... | collective-permute-start | bytes 98312 | tf_op jit(solution)/shard_map/ppermute | solution.py:19
  58.7 4.1 %collective-permute-start.13 = (f32[3,16,128]{2,1,0:T(8,128)S(1)}, f32[3,16,128]{2,1,0:T(8,128)S(1)}, u32[]{:S(2)}, u32[]{:S(2)}) collective-permute-start(f32[3,16,128]{2,1,0:T(8,128)S(1)} %slice.252), channel_id=1, source_target_pairs={{0,8},{4,12},{8,0},{12,4},{16,24},{20,28},{24,16},{28,20},{1,9},{5... | collective-permute-start | bytes 73736 | tf_op jit(solution)/shard_map/ppermute | solution.py:19
  62.8 3.8 %collective-permute-start.14 = (f32[2,16,128]{2,1,0:T(8,128)S(1)}, f32[2,16,128]{2,1,0:T(8,128)S(1)}, u32[]{:S(2)}, u32[]{:S(2)}) collective-permute-start(f32[2,16,128]{2,1,0:T(8,128)S(1)} %slice.215), channel_id=1, source_target_pairs={{0,16},{4,20},{8,24},{12,28},{16,0},{20,4},{24,8},{28,12},{1,17},{... | collective-permute-start | bytes 49160 | tf_op jit(solution)/shard_map/ppermute | solution.py:19
  68.4 3.6 %collective-permute-start.15 = (f32[16]{0:T(128)S(1)}, f32[16]{0:T(128)S(1)}, u32[]{:S(2)}, u32[]{:S(2)}) collective-permute-start(f32[16]{0:T(128)S(1)} %add.227), channel_id=1, source_target_pairs={{0,1},{1,0},{2,3},{3,2},{4,5},{5,4},{6,7},{7,6},{8,9},{9,8},{10,11... | collective-permute-start | bytes 200 | tf_op jit(solution)/shard_map/ppermute | solution.py:19
  72.0 4.4 %collective-permute-start.16 = (f32[16]{0:T(128)S(1)}, f32[16]{0:T(128)S(1)}, u32[]{:S(2)}, u32[]{:S(2)}) collective-permute-start(f32[16]{0:T(128)S(1)} %add.228), channel_id=1, source_target_pairs={{0,2},{1,3},{2,0},{3,1},{4,6},{5,7},{6,4},{7,5},{8,10},{9,11},{10,... | collective-permute-start | bytes 200 | tf_op jit(solution)/shard_map/ppermute | solution.py:19
  76.4 1.1 %collective-permute-start.17 = (f32[16]{0:T(128)S(1)}, f32[16]{0:T(128)S(1)}, u32[]{:S(2)}, u32[]{:S(2)}) collective-permute-start(f32[16]{0:T(128)S(1)} %add.232), channel_id=1, source_target_pairs={{0,4},{4,0},{8,12},{12,8},{16,20},{20,16},{24,28},{28,24},{1,5},{5... | collective-permute-start | bytes 200 | tf_op jit(solution)/shard_map/ppermute | solution.py:19
  77.6 3.5 %collective-permute-start.18 = (f32[16]{0:T(128)S(1)}, f32[16]{0:T(128)S(1)}, u32[]{:S(2)}, u32[]{:S(2)}) collective-permute-start(f32[16]{0:T(128)S(1)} %add.236), channel_id=1, source_target_pairs={{0,8},{4,12},{8,0},{12,4},{16,24},{20,28},{24,16},{28,20},{1,9},{5... | collective-permute-start | bytes 200 | tf_op jit(solution)/shard_map/ppermute | solution.py:19
  81.1 3.5 %collective-permute-start.19 = (f32[16]{0:T(128)S(1)}, f32[16]{0:T(128)S(1)}, u32[]{:S(2)}, u32[]{:S(2)}) collective-permute-start(f32[16]{0:T(128)S(1)} %add.237), channel_id=1, source_target_pairs={{0,16},{4,20},{8,24},{12,28},{16,0},{20,4},{24,8},{28,12},{1,17},{... | collective-permute-start | bytes 200 | tf_op jit(solution)/shard_map/ppermute | solution.py:19

commit v19 on v16

--- a/solution.py
+++ b/solution.py
@@ -140,8 +140,16 @@
         late, near, extra = state
         return late, near + from_union(late[half:], hot_second), extra
 
-    def permute_inputs(state):
-        stacked = to_union(jnp.concatenate(state, axis=0), hot)
+    def permute_inputs_first(state):
+        split = pieces(jnp.concatenate(state, axis=0), 0)
+        return split, jnp.einsum("cp,gip->gci", split, hot_first, preferred_element_type=jnp.float32)
+
+    def permute_inputs_second(state):
+        split, first = state
+        second = jnp.einsum("cp,gip->gci", split, hot_second, preferred_element_type=jnp.float32)
+        stacked = jnp.concatenate([first, second], axis=0)
+        count = stacked.shape[1] // 3
+        stacked = (stacked[:, :count] + stacked[:, count : 2 * count]) + stacked[:, 2 * count :]
         return stacked[:, :features] * inv_scale[None, :, None], stacked[:, features:]
 
     def kernel_blocks(state):
@@ -158,7 +166,7 @@
     residual_proj = project(residual)
     for step in range(ITERATIONS):
         if step == 0:
-            stages = [None, permute_inputs, None, kernel_blocks, first_near]
+            stages = [None, permute_inputs_first, permute_inputs_second, kernel_blocks, first_near]
             nodesum, norm_now, (kern, direction_u, near_u) = sums_with_norm(
                 residual, residual_proj, stages, (coords, right_side)
             )

time: 85.6 us -> 84.5 us (0.987)
  waiting for transfers between devices: 26.8 us -> 23.3 us
  starting transfers between devices: 20.6 us -> 22.8 us
    dot_general x0 -> x2, matrix products: none -> 3.6 us  [the longest x1 1.8 us: permute_inputs_second(): jnp.einsum('cp,gip->gci', split, hot_second, preferred_element_type=jnp.f...]
    dot_general x3 -> x2, matrix products: 7.1 us -> 3.61 us  [to_union(): jnp.einsum('cp,gip->gci', pieces(values, 0), hot, preferred_element_type=...]
    ppermute x20, waiting for transfers between devices: 26.8 us -> 23.3 us  [swapped(): return lax.ppermute(value, axis, pairs)]
    ppermute x20, starting transfers between devices: 20.6 us -> 22.8 us  [swapped(): return lax.ppermute(value, axis, pairs)]
  transfers between devices with their start and end apart: 20 -> 20, of which waited for: 17 -> 16; matrix products, arithmetic and copies ran while one was open for 32% -> 33% of each run, Pallas kernels for 0% -> 0%
where the time goes in v19:
time: 84.5 us; the launch traced here: 84.2 us
  matrix products  26.9 us (32%)
  waiting for transfers between devices  23.3 us (28%)
  starting transfers between devices  22.8 us (27%)
  other arithmetic  5.93 us (7%)
  local copies, waits for them, and re-layouts  4.02 us (5%)
  between operations  1.24 us (1%)
    ppermute x20, waiting for transfers between devices, swapped(): return lax.ppermute(value, axis, pairs)  23.3 us
    ppermute x20, starting transfers between devices, swapped(): return lax.ppermute(value, axis, pairs)  22.8 us
    dot_general x4, matrix products, from_union(): jnp.einsum('gci,gip->cp', pieces(values_u, 1), hot, preferred_element_typ...  7.27 us
    dot_general x2, matrix products, near_apply(): jnp.einsum('gij,gcj->gci', kern, union_vec, precision=lax.Precision.HIGH)  3.91 us
    dot_general x2, matrix products, to_union(): jnp.einsum('cp,gip->gci', pieces(values, 0), hot, preferred_element_type=...  3.61 us
    dot_general x2, matrix products, project(): jnp.einsum('lp,cp,rp->lcr', level_gain, values, basis, precision=highest)  3.33 us
    dot_general x1, matrix products, permute_inputs_second(): jnp.einsum('cp,gip->gci', split, hot_second, preferred_element_type=jnp.f...  1.8 us
    dot_general x1, matrix products, permute_inputs_first(): jnp.einsum('cp,gip->gci', split, hot_first, preferred_element_type=jnp.fl...  1.8 us
  transfers between devices with their start and end apart: 20, of which 16 were waited for; matrix products, arithmetic and copies ran while one was open for 33% of the time, Pallas kernels for 0%

profile of v19, /device:TPU:0, one launch (start us, length us, event | category | flops | bytes accessed | tf_op | source)
XLA Modules:
  0.0 84.2 jit_solution(17832873706469197241)
XLA Ops:
  0.6 1.1 %multiply_reduce_fusion.5 = f32[16]{0:T(128)S(1)} fusion(f32[16,2048]{1,0:T(8,128)} %param.12), kind=kLoop, calls=%fused_computation.110 | loop fusion | flops 65520 | bytes 131136 | tf_op jit(solution)/shard_map/reduce_sum | solution.py:113
  1.9 2.1 %convolution_bitcast_fusion.1 = f32[5,16,128]{2,1,0:T(8,128)S(1)} fusion(f32[128,2048]{1,0:T(8,128)S(1)} %copy-done, f32[2048,5]{0,1:T(8,128)} %bitcast.75, f32[2048,16]{0,1:T(8,128)} %bitcast.74), kind=kOutput, calls=%fused_computation.34 | convolution fusion | flops 251822080 | bytes 1261568 | tf_op jit(solution)/shard_map/lp,cp,rp->lcr/dot_general | solution.py:110
  4.1 3.0 %collective-permute-start = (f32[6,16,128]{2,1,0:T(8,128)S(1)}, f32[6,16,128]{2,1,0:T(8,128)S(1)}, u32[]{:S(2)}, u32[]{:S(2)}) collective-permute-start(f32[6,16,128]{2,1,0:T(8,128)S(1)} %pad_maximum_fusion.2), channel_id=1, source_target_pairs={{0,1},{1,0},{2,3},{3,2},{4,5},{5,4},{6,7},{7,6},{8,9},{9,8},{10,11... | collective-permute-start | bytes 147464 | tf_op jit(solution)/shard_map/ppermute | solution.py:19
  7.7 1.4 %reduce.9 = s32[2048]{0:T(1024)S(1)} reduce(s32[1,2048]{1,0:T(1,128)} %param.16, s32[]{:T(128)} %broadcast.99), dimensions={0}, to_apply=%param.16.reduce_sub_computation.3 | reduce | bytes 16388 | tf_op args[7]
  9.1 0.8 fusion.89
  11.0 2.7 %collective-permute-start.1 = (f32[5,16,128]{2,1,0:T(8,128)S(1)}, f32[5,16,128]{2,1,0:T(8,128)S(1)}, u32[]{:S(2)}, u32[]{:S(2)}) collective-permute-start(f32[5,16,128]{2,1,0:T(8,128)S(1)} %slice.234), channel_id=1, source_target_pairs={{0,2},{1,3},{2,0},{3,1},{4,6},{5,7},{6,4},{7,5},{8,10},{9,11},{10,... | collective-permute-start | bytes 122888 | tf_op jit(solution)/shard_map/ppermute | solution.py:19
  13.7 0.8 %constant_dynamic-update-slice_fusion.1 = f32[24,2048]{1,0:T(8,128)S(1)} fusion(f32[8,2048]{1,0:T(8,128)} %param.9), kind=kLoop, calls=%fused_computation.180 | loop fusion | bytes 131072
  14.5 0.9 %constant_dynamic-update-slice_fusion = f32[24,2048]{1,0:T(8,128)S(1)} fusion(f32[24,2048]{1,0:T(8,128)S(1)} %constant_dynamic-update-slice_fusion.1, f32[16,2048]{1,0:T(8,128)} %param.12), kind=kLoop, calls=%fused_computation.179 | loop fusion | bytes 262144 | tf_op jit(solution)/shard_map/concatenate | solution.py:144
  15.5 1.8 %fusion.22 = f32[2,72,512]{2,1,0:T(8,128)S(1)} fusion(s32[2,512]{1,0:T(2,128)S(1)} %get-tuple-element.190, bf16[24,2048]{1,0:T(8,128)(2,1)S(1)} %get-tuple-element.159, bf16[24,2048]{1,0:T(8,128)(2,1)S(1)} %get-tuple-element.160, bf16[24,2048]{1,0:T(8,128)(2,1)S(1)} %get-tuple-element.158), kind=kOutput, calls=%fused_computation.29 | convolution fusion | flops 304971776 | bytes 593920 | tf_op jit(solution)/shard_map/cp,gip->gci/dot_general | solution.py:145
  17.5 1.8 %fusion.23 = f32[2,72,512]{2,1,0:T(8,128)S(1)} fusion(s32[2,512]{1,0:T(2,128)S(1)} %get-tuple-element.189, bf16[72,2048]{1,0:T(8,128)(2,1)S(1)} %pad_maximum_fusion), kind=kOutput, calls=%fused_computation.30 | convolution fusion | flops 304087040 | bytes 593920 | tf_op jit(solution)/shard_map/cp,gip->gci/dot_general | solution.py:149
  19.6 1.6 %collective-permute-start.3 = (f32[3,16,128]{2,1,0:T(8,128)S(1)}, f32[3,16,128]{2,1,0:T(8,128)S(1)}, u32[]{:S(2)}, u32[]{:S(2)}) collective-permute-start(f32[3,16,128]{2,1,0:T(8,128)S(1)} %slice.190), channel_id=1, source_target_pairs={{0,8},{4,12},{8,0},{12,4},{16,24},{20,28},{24,16},{28,20},{1,9},{5... | collective-permute-start | bytes 73736 | tf_op jit(solution)/shard_map/ppermute | solution.py:19
  21.3 1.6 %exponential_multiply_fusion = f32[4,512,512]{2,1,0:T(8,128)S(1)} fusion(bf16[4,48,512]{2,1,0:T(8,128)(2,1)S(1)} %get-tuple-element.186, bf16[4,48,512]{2,1,0:T(8,128)(2,1)S(1)} %get-tuple-element.185, f32[4,512]{1,0:T(4,128)S(1)} %multiply_reduce_fusion.6), kind=kOutput, calls=%fused_computation.12 | convolution fusion | flops 105906176 | bytes 4595712 | tf_op jit(solution)/shard_map/gfi,gfj->gij/dot_general | solution.py:33
  23.5 1.6 %collective-permute-start.4 = (f32[2,16,128]{2,1,0:T(8,128)S(1)}, f32[2,16,128]{2,1,0:T(8,128)S(1)}, u32[]{:S(2)}, u32[]{:S(2)}) collective-permute-start(f32[2,16,128]{2,1,0:T(8,128)S(1)} %slice.193), channel_id=1, source_target_pairs={{0,16},{4,20},{8,24},{12,28},{16,0},{20,4},{24,8},{28,12},{1,17},{... | collective-permute-start | bytes 49160 | tf_op jit(solution)/shard_map/ppermute | solution.py:19
  25.1 1.8 %fusion.100 = f32[4,16,512]{2,1,0:T(8,128)S(1)} fusion(f32[4,16,512]{2,1,0:T(8,128)S(1)} %slice.242, f32[4,512,512]{2,1,0:T(8,128)S(1)} %exponential_multiply_fusion), kind=kOutput, calls=%fused_computation.226 | convolution fusion | flops 100663296 | bytes 4456448 | tf_op jit(solution)/shard_map/gij,gcj->gci/dot_general | solution.py:40
  27.7 0.6 convolution_multiply_fusion.3
  28.3 0.8 fusion.20
  29.9 1.8 %fusion.16 = f32[48,2048]{1,0:T(8,128)S(1)} fusion(s32[2,512]{1,0:T(2,128)S(1)} %get-tuple-element.190, bf16[2,16,512]{2,1,0:T(8,128)(2,1)S(1)} %get-tuple-element.177, bf16[2,16,512]{2,1,0:T(8,128)(2,1)S(1)} %get-tuple-element.178, bf16[2,16,512]{2,1,0:T(8,128)(2,1)S(1)} %get-tuple-element.176), kind=kOutput, calls=%fused_computation.23 | convolution fusion | flops 203718656 | bytes 495616 | tf_op jit(solution)/shard_map/gci,gip->cp/dot_general | solution.py:55
  31.8 1.2 %collective-permute-done.5 = f32[16]{0:T(128)S(1)} collective-permute-done((f32[16]{0:T(128)S(1)}, f32[16]{0:T(128)S(1)}, u32[]{:S(2)}, u32[]{:S(2)}) %collective-permute-start.5) | collective-permute-done | bytes 96 | tf_op jit(solution)/shard_map/ppermute | solution.py:19
  33.0 1.2 %collective-permute-start.6 = (f32[16]{0:T(128)S(1)}, f32[16]{0:T(128)S(1)}, u32[]{:S(2)}, u32[]{:S(2)}) collective-permute-start(f32[16]{0:T(128)S(1)} %add.199), channel_id=1, source_target_pairs={{0,2},{1,3},{2,0},{3,1},{4,6},{5,7},{6,4},{7,5},{8,10},{9,11},{10,... | collective-permute-start | bytes 200 | tf_op jit(solution)/shard_map/ppermute | solution.py:19
  34.2 1.8 %fusion.18 = f32[48,2048]{1,0:T(8,128)S(1)} fusion(s32[2,512]{1,0:T(2,128)S(1)} %get-tuple-element.189, bf16[2,16,512]{2,1,0:T(8,128)(2,1)S(1)} %get-tuple-element.174, bf16[2,16,512]{2,1,0:T(8,128)(2,1)S(1)} %get-tuple-element.175, bf16[2,16,512]{2,1,0:T(8,128)(2,1)S(1)} %get-tuple-element.173), kind=kOutput, calls=%fused_computation.25 | convolution fusion | flops 203718656 | bytes 495616 | tf_op jit(solution)/shard_map/gci,gip->cp/dot_general | solution.py:55
  36.1 1.3 %collective-permute-done.6 = f32[16]{0:T(128)S(1)} collective-permute-done((f32[16]{0:T(128)S(1)}, f32[16]{0:T(128)S(1)}, u32[]{:S(2)}, u32[]{:S(2)}) %collective-permute-start.6) | collective-permute-done | bytes 96 | tf_op jit(solution)/shard_map/ppermute | solution.py:19
  37.5 1.2 %convolution_bitcast_fusion = f32[5,16,128]{2,1,0:T(8,128)S(1)} fusion(f32[128,2048]{1,0:T(8,128)S(1)} %copy-done, f32[2048,16]{0,1:T(8,128)S(1)} %add_bitcast_fusion, f32[2048,5]{0,1:T(8,128)S(1)} %bitcast.76), kind=kOutput, calls=%fused_computation.33 | convolution fusion | flops 251822080 | bytes 1261568 | tf_op jit(solution)/shard_map/lp,cp,rp->lcr/dot_general | solution.py:110
  38.7 1.6 %collective-permute-start.8 = (f32[16]{0:T(128)S(1)}, f32[16]{0:T(128)S(1)}, u32[]{:S(2)}, u32[]{:S(2)}) collective-permute-start(f32[16]{0:T(128)S(1)} %add.207), channel_id=1, source_target_pairs={{0,8},{4,12},{8,0},{12,4},{16,24},{20,28},{24,16},{28,20},{1,9},{5... | collective-permute-start | bytes 200 | tf_op jit(solution)/shard_map/ppermute | solution.py:19
  40.2 2.1 %collective-permute-done.8 = f32[16]{0:T(128)S(1)} collective-permute-done((f32[16]{0:T(128)S(1)}, f32[16]{0:T(128)S(1)}, u32[]{:S(2)}, u32[]{:S(2)}) %collective-permute-start.8) | collective-permute-done | bytes 96 | tf_op jit(solution)/shard_map/ppermute | solution.py:19
  42.3 1.5 %collective-permute-start.9 = (f32[16]{0:T(128)S(1)}, f32[16]{0:T(128)S(1)}, u32[]{:S(2)}, u32[]{:S(2)}) collective-permute-start(f32[16]{0:T(128)S(1)} %add.210), channel_id=1, source_target_pairs={{0,16},{4,20},{8,24},{12,28},{16,0},{20,4},{24,8},{28,12},{1,17},{... | collective-permute-start | bytes 200 | tf_op jit(solution)/shard_map/ppermute | solution.py:19
  43.9 1.9 %collective-permute-done.9 = f32[16]{0:T(128)S(1)} collective-permute-done((f32[16]{0:T(128)S(1)}, f32[16]{0:T(128)S(1)}, u32[]{:S(2)}, u32[]{:S(2)}) %collective-permute-start.9) | collective-permute-done | bytes 96 | tf_op jit(solution)/shard_map/ppermute | solution.py:19
  46.7 1.8 %fusion.24 = f32[2,48,512]{2,1,0:T(8,128)S(1)} fusion(s32[2,512]{1,0:T(2,128)S(1)} %get-tuple-element.190, bf16[16,2048]{1,0:T(8,128)(2,1)S(1)} %get-tuple-element.171, bf16[16,2048]{1,0:T(8,128)(2,1)S(1)} %get-tuple-element.172, bf16[16,2048]{1,0:T(8,128)(2,1)S(1)} %get-tuple-element.170), kind=kOutput, calls=%fused_computation.31 | convolution fusion | flops 204013568 | bytes 397312 | tf_op jit(solution)/shard_map/cp,gip->gci/dot_general | solution.py:49
  48.6 1.8 %collective-permute-done.10 = f32[6,16,128]{2,1,0:T(8,128)S(1)} collective-permute-done((f32[6,16,128]{2,1,0:T(8,128)S(1)}, f32[6,16,128]{2,1,0:T(8,128)S(1)}, u32[]{:S(2)}, u32[]{:S(2)}) %collective-permute-start.10) | collective-permute-done | bytes 49184 | tf_op jit(solution)/shard_map/ppermute | solution.py:19
  50.3 1.3 %collective-permute-start.11 = (f32[5,16,128]{2,1,0:T(8,128)S(1)}, f32[5,16,128]{2,1,0:T(8,128)S(1)}, u32[]{:S(2)}, u32[]{:S(2)}) collective-permute-start(f32[5,16,128]{2,1,0:T(8,128)S(1)} %slice.209), channel_id=1, source_target_pairs={{0,2},{1,3},{2,0},{3,1},{4,6},{5,7},{6,4},{7,5},{8,10},{9,11},{10,... | collective-permute-start | bytes 122888 | tf_op jit(solution)/shard_map/ppermute | solution.py:19
  51.6 1.8 %fusion.25 = f32[2,48,512]{2,1,0:T(8,128)S(1)} fusion(s32[2,512]{1,0:T(2,128)S(1)} %get-tuple-element.189, bf16[16,2048]{1,0:T(8,128)(2,1)S(1)} %get-tuple-element.168, bf16[16,2048]{1,0:T(8,128)(2,1)S(1)} %get-tuple-element.169, bf16[16,2048]{1,0:T(8,128)(2,1)S(1)} %get-tuple-element.167), kind=kOutput, calls=%fused_computation.32 | convolution fusion | flops 204013568 | bytes 397312 | tf_op jit(solution)/shard_map/cp,gip->gci/dot_general | solution.py:49
  53.5 2.2 %collective-permute-done.11 = f32[5,16,128]{2,1,0:T(8,128)S(1)} collective-permute-done((f32[5,16,128]{2,1,0:T(8,128)S(1)}, f32[5,16,128]{2,1,0:T(8,128)S(1)}, u32[]{:S(2)}, u32[]{:S(2)}) %collective-permute-start.11) | collective-permute-done | bytes 40992 | tf_op jit(solution)/shard_map/ppermute | solution.py:19
  55.8 1.2 %collective-permute-done.12 = f32[4,16,128]{2,1,0:T(8,128)S(1)} collective-permute-done((f32[4,16,128]{2,1,0:T(8,128)S(1)}, f32[4,16,128]{2,1,0:T(8,128)S(1)}, u32[]{:S(2)}, u32[]{:S(2)}) %collective-permute-start.12) | collective-permute-done | bytes 32800 | tf_op jit(solution)/shard_map/ppermute | solution.py:19
  57.0 1.6 %collective-permute-start.13 = (f32[3,16,128]{2,1,0:T(8,128)S(1)}, f32[3,16,128]{2,1,0:T(8,128)S(1)}, u32[]{:S(2)}, u32[]{:S(2)}) collective-permute-start(f32[3,16,128]{2,1,0:T(8,128)S(1)} %slice.255), channel_id=1, source_target_pairs={{0,8},{4,12},{8,0},{12,4},{16,24},{20,28},{24,16},{28,20},{1,9},{5... | collective-permute-start | bytes 73736 | tf_op jit(solution)/shard_map/ppermute | solution.py:19
  58.5 2.1 %fusion.102 = f32[4,16,512]{2,1,0:T(8,128)S(1)} fusion(f32[4,16,512]{2,1,0:T(8,128)S(1)} %constant_dynamic-update-slice_fusion.16, f32[4,512,512]{2,1,0:T(8,128)S(1)} %exponential_multiply_fusion), kind=kOutput, calls=%fused_computation.228 | convolution fusion | flops 100663296 | bytes 4456448 | tf_op jit(solution)/shard_map/gij,gcj->gci/dot_general | solution.py:40
  60.9 1.6 %collective-permute-start.14 = (f32[2,16,128]{2,1,0:T(8,128)S(1)}, f32[2,16,128]{2,1,0:T(8,128)S(1)}, u32[]{:S(2)}, u32[]{:S(2)}) collective-permute-start(f32[2,16,128]{2,1,0:T(8,128)S(1)} %slice.218), channel_id=1, source_target_pairs={{0,16},{4,20},{8,24},{12,28},{16,0},{20,4},{24,8},{28,12},{1,17},{... | collective-permute-start | bytes 49160 | tf_op jit(solution)/shard_map/ppermute | solution.py:19
  62.5 2.2 %collective-permute-done.14 = f32[2,16,128]{2,1,0:T(8,128)S(1)} collective-permute-done((f32[2,16,128]{2,1,0:T(8,128)S(1)}, f32[2,16,128]{2,1,0:T(8,128)S(1)}, u32[]{:S(2)}, u32[]{:S(2)}) %collective-permute-start.14) | collective-permute-done | bytes 16416 | tf_op jit(solution)/shard_map/ppermute | solution.py:19
  65.9 0.8 fusion.21
  67.3 1.8 %fusion.17 = f32[48,2048]{1,0:T(8,128)S(1)} fusion(s32[2,512]{1,0:T(2,128)S(1)} %get-tuple-element.190, bf16[2,16,512]{2,1,0:T(8,128)(2,1)S(1)} %get-tuple-element.165, bf16[2,16,512]{2,1,0:T(8,128)(2,1)S(1)} %get-tuple-element.166, bf16[2,16,512]{2,1,0:T(8,128)(2,1)S(1)} %get-tuple-element.164), kind=kOutput, calls=%fused_computation.24 | convolution fusion | flops 203718656 | bytes 495616 | tf_op jit(solution)/shard_map/gci,gip->cp/dot_general | solution.py:55
  69.2 1.5 %collective-permute-done.15 = f32[16]{0:T(128)S(1)} collective-permute-done((f32[16]{0:T(128)S(1)}, f32[16]{0:T(128)S(1)}, u32[]{:S(2)}, u32[]{:S(2)}) %collective-permute-start.15) | collective-permute-done | bytes 96 | tf_op jit(solution)/shard_map/ppermute | solution.py:19
  70.7 0.9 %collective-permute-start.16 = (f32[16]{0:T(128)S(1)}, f32[16]{0:T(128)S(1)}, u32[]{:S(2)}, u32[]{:S(2)}) collective-permute-start(f32[16]{0:T(128)S(1)} %add.228), channel_id=1, source_target_pairs={{0,2},{1,3},{2,0},{3,1},{4,6},{5,7},{6,4},{7,5},{8,10},{9,11},{10,... | collective-permute-start | bytes 200 | tf_op jit(solution)/shard_map/ppermute | solution.py:19
  71.6 1.8 %fusion.19 = f32[48,2048]{1,0:T(8,128)S(1)} fusion(s32[2,512]{1,0:T(2,128)S(1)} %get-tuple-element.189, bf16[2,16,512]{2,1,0:T(8,128)(2,1)S(1)} %get-tuple-element.162, bf16[2,16,512]{2,1,0:T(8,128)(2,1)S(1)} %get-tuple-element.163, bf16[2,16,512]{2,1,0:T(8,128)(2,1)S(1)} %get-tuple-element.161), kind=kOutput, calls=%fused_computation.26 | convolution fusion | flops 203718656 | bytes 495616 | tf_op jit(solution)/shard_map/gci,gip->cp/dot_general | solution.py:55
  73.4 1.7 %collective-permute-done.16 = f32[16]{0:T(128)S(1)} collective-permute-done((f32[16]{0:T(128)S(1)}, f32[16]{0:T(128)S(1)}, u32[]{:S(2)}, u32[]{:S(2)}) %collective-permute-start.16) | collective-permute-done | bytes 96 | tf_op jit(solution)/shard_map/ppermute | solution.py:19
  75.1 1.1 %collective-permute-done.17 = f32[16]{0:T(128)S(1)} collective-permute-done((f32[16]{0:T(128)S(1)}, f32[16]{0:T(128)S(1)}, u32[]{:S(2)}, u32[]{:S(2)}) %collective-permute-start.17) | collective-permute-done | bytes 96 | tf_op jit(solution)/shard_map/ppermute | solution.py:19
  76.3 1.5 %collective-permute-start.18 = (f32[16]{0:T(128)S(1)}, f32[16]{0:T(128)S(1)}, u32[]{:S(2)}, u32[]{:S(2)}) collective-permute-start(f32[16]{0:T(128)S(1)} %add.236), channel_id=1, source_target_pairs={{0,8},{4,12},{8,0},{12,4},{16,24},{20,28},{24,16},{28,20},{1,9},{5... | collective-permute-start | bytes 200 | tf_op jit(solution)/shard_map/ppermute | solution.py:19
  77.8 2.1 %collective-permute-done.18 = f32[16]{0:T(128)S(1)} collective-permute-done((f32[16]{0:T(128)S(1)}, f32[16]{0:T(128)S(1)}, u32[]{:S(2)}, u32[]{:S(2)}) %collective-permute-start.18) | collective-permute-done | bytes 96 | tf_op jit(solution)/shard_map/ppermute | solution.py:19
  79.8 1.5 %collective-permute-start.19 = (f32[16]{0:T(128)S(1)}, f32[16]{0:T(128)S(1)}, u32[]{:S(2)}, u32[]{:S(2)}) collective-permute-start(f32[16]{0:T(128)S(1)} %add.237), channel_id=1, source_target_pairs={{0,16},{4,20},{8,24},{12,28},{16,0},{20,4},{24,8},{28,12},{1,17},{... | collective-permute-start | bytes 200 | tf_op jit(solution)/shard_map/ppermute | solution.py:19
  81.3 2.0 %collective-permute-done.19 = f32[16]{0:T(128)S(1)} collective-permute-done((f32[16]{0:T(128)S(1)}, f32[16]{0:T(128)S(1)}, u32[]{:S(2)}, u32[]{:S(2)}) %collective-permute-start.19) | collective-permute-done | bytes 96 | tf_op jit(solution)/shard_map/ppermute | solution.py:19
  83.4 0.8 multiply_subtract_fusion
  (127 shorter events, 8.0 us)
Async XLA Ops:
  0.6 1.3 %copy-start = (f32[128,2048]{1,0:T(8,128)S(1)}, f32[128,2048]{1,0:T(8,128)}, u32[]{:S(2)}) copy-start(f32[128,2048]{1,0:T(8,128)} %param.13) | copy-start | bytes 3145732
  4.1 6.9 %collective-permute-start = (f32[6,16,128]{2,1,0:T(8,128)S(1)}, f32[6,16,128]{2,1,0:T(8,128)S(1)}, u32[]{:S(2)}, u32[]{:S(2)}) collective-permute-start(f32[6,16,128]{2,1,0:T(8,128)S(1)} %pad_maximum_fusion.2), channel_id=1, source_target_pairs={{0,1},{1,0},{2,3},{3,2},{4,5},{5,4},{6,7},{7,6},{8,9},{9,8},{10,11... | collective-permute-start | bytes 147464 | tf_op jit(solution)/shard_map/ppermute | solution.py:19
  11.0 6.3 %collective-permute-start.1 = (f32[5,16,128]{2,1,0:T(8,128)S(1)}, f32[5,16,128]{2,1,0:T(8,128)S(1)}, u32[]{:S(2)}, u32[]{:S(2)}) collective-permute-start(f32[5,16,128]{2,1,0:T(8,128)S(1)} %slice.234), channel_id=1, source_target_pairs={{0,2},{1,3},{2,0},{3,1},{4,6},{5,7},{6,4},{7,5},{8,10},{9,11},{10,... | collective-permute-start | bytes 122888 | tf_op jit(solution)/shard_map/ppermute | solution.py:19
  15.5 3.8 %copy-start.5 = (f32[8]{0:T(128)S(1)}, f32[8]{0:T(128)}, u32[]{:S(2)}) copy-start(f32[8]{0:T(128)} %param.10) | copy-start | bytes 100
  17.4 2.0 %collective-permute-start.2 = (f32[4,16,128]{2,1,0:T(8,128)S(1)}, f32[4,16,128]{2,1,0:T(8,128)S(1)}, u32[]{:S(2)}, u32[]{:S(2)}) collective-permute-start(f32[4,16,128]{2,1,0:T(8,128)S(1)} %slice.181), channel_id=1, source_target_pairs={{0,4},{4,0},{8,12},{12,8},{16,20},{20,16},{24,28},{28,24},{1,5},{5... | collective-permute-start | bytes 98312 | tf_op jit(solution)/shard_map/ppermute | solution.py:19
  19.6 3.9 %collective-permute-start.3 = (f32[3,16,128]{2,1,0:T(8,128)S(1)}, f32[3,16,128]{2,1,0:T(8,128)S(1)}, u32[]{:S(2)}, u32[]{:S(2)}) collective-permute-start(f32[3,16,128]{2,1,0:T(8,128)S(1)} %slice.190), channel_id=1, source_target_pairs={{0,8},{4,12},{8,0},{12,4},{16,24},{20,28},{24,16},{28,20},{1,9},{5... | collective-permute-start | bytes 73736 | tf_op jit(solution)/shard_map/ppermute | solution.py:19
  21.2 6.1 %copy-start.2 = (f32[5,128,128]{2,1,0:T(8,128)S(1)}, f32[5,128,128]{2,1,0:T(8,128)}, u32[]{:S(2)}) copy-start(f32[5,128,128]{2,1,0:T(8,128)} %param.15) | copy-start | bytes 983044
  22.9 5.4 %copy-start.3 = (f32[5,2048]{1,0:T(8,128)S(1)}, f32[5,2048]{1,0:T(8,128)}, u32[]{:S(2)}) copy-start(f32[5,2048]{1,0:T(8,128)} %param.14) | copy-start | bytes 122884
  22.9 6.3 %copy-start.1 = (f32[16,2048]{1,0:T(8,128)S(1)}, f32[16,2048]{1,0:T(8,128)}, u32[]{:S(2)}) copy-start(f32[16,2048]{1,0:T(8,128)} %param.12) | copy-start | bytes 393220
  22.9 6.3 %copy-start.4 = (f32[2048]{0:T(1024)S(1)}, f32[2048]{0:T(1024)}, u32[]{:S(2)}) copy-start(f32[2048]{0:T(1024)} %param.11) | copy-start | bytes 24580
  23.5 3.8 %collective-permute-start.4 = (f32[2,16,128]{2,1,0:T(8,128)S(1)}, f32[2,16,128]{2,1,0:T(8,128)S(1)}, u32[]{:S(2)}, u32[]{:S(2)}) collective-permute-start(f32[2,16,128]{2,1,0:T(8,128)S(1)} %slice.193), channel_id=1, source_target_pairs={{0,16},{4,20},{8,24},{12,28},{16,0},{20,4},{24,8},{28,12},{1,17},{... | collective-permute-start | bytes 49160 | tf_op jit(solution)/shard_map/ppermute | solution.py:19
  29.4 3.6 %collective-permute-start.5 = (f32[16]{0:T(128)S(1)}, f32[16]{0:T(128)S(1)}, u32[]{:S(2)}, u32[]{:S(2)}) collective-permute-start(f32[16]{0:T(128)S(1)} %add.198), channel_id=1, source_target_pairs={{0,1},{1,0},{2,3},{3,2},{4,5},{5,4},{6,7},{7,6},{8,9},{9,8},{10,11... | collective-permute-start | bytes 200 | tf_op jit(solution)/shard_map/ppermute | solution.py:19
  33.0 4.4 %collective-permute-start.6 = (f32[16]{0:T(128)S(1)}, f32[16]{0:T(128)S(1)}, u32[]{:S(2)}, u32[]{:S(2)}) collective-permute-start(f32[16]{0:T(128)S(1)} %add.199), channel_id=1, source_target_pairs={{0,2},{1,3},{2,0},{3,1},{4,6},{5,7},{6,4},{7,5},{8,10},{9,11},{10,... | collective-permute-start | bytes 200 | tf_op jit(solution)/shard_map/ppermute | solution.py:19
  37.4 1.2 %collective-permute-start.7 = (f32[16]{0:T(128)S(1)}, f32[16]{0:T(128)S(1)}, u32[]{:S(2)}, u32[]{:S(2)}) collective-permute-start(f32[16]{0:T(128)S(1)} %add.203), channel_id=1, source_target_pairs={{0,4},{4,0},{8,12},{12,8},{16,20},{20,16},{24,28},{28,24},{1,5},{5... | collective-permute-start | bytes 200 | tf_op jit(solution)/shard_map/ppermute | solution.py:19
  38.7 3.6 %collective-permute-start.8 = (f32[16]{0:T(128)S(1)}, f32[16]{0:T(128)S(1)}, u32[]{:S(2)}, u32[]{:S(2)}) collective-permute-start(f32[16]{0:T(128)S(1)} %add.207), channel_id=1, source_target_pairs={{0,8},{4,12},{8,0},{12,4},{16,24},{20,28},{24,16},{28,20},{1,9},{5... | collective-permute-start | bytes 200 | tf_op jit(solution)/shard_map/ppermute | solution.py:19
  42.3 3.5 %collective-permute-start.9 = (f32[16]{0:T(128)S(1)}, f32[16]{0:T(128)S(1)}, u32[]{:S(2)}, u32[]{:S(2)}) collective-permute-start(f32[16]{0:T(128)S(1)} %add.210), channel_id=1, source_target_pairs={{0,16},{4,20},{8,24},{12,28},{16,0},{20,4},{24,8},{28,12},{1,17},{... | collective-permute-start | bytes 200 | tf_op jit(solution)/shard_map/ppermute | solution.py:19
  46.2 4.1 %collective-permute-start.10 = (f32[6,16,128]{2,1,0:T(8,128)S(1)}, f32[6,16,128]{2,1,0:T(8,128)S(1)}, u32[]{:S(2)}, u32[]{:S(2)}) collective-permute-start(f32[6,16,128]{2,1,0:T(8,128)S(1)} %pad_maximum_fusion.7), channel_id=1, source_target_pairs={{0,1},{1,0},{2,3},{3,2},{4,5},{5,4},{6,7},{7,6},{8,9},{9,8},{10,11... | collective-permute-start | bytes 147464 | tf_op jit(solution)/shard_map/ppermute | solution.py:19
  50.3 5.3 %collective-permute-start.11 = (f32[5,16,128]{2,1,0:T(8,128)S(1)}, f32[5,16,128]{2,1,0:T(8,128)S(1)}, u32[]{:S(2)}, u32[]{:S(2)}) collective-permute-start(f32[5,16,128]{2,1,0:T(8,128)S(1)} %slice.209), channel_id=1, source_target_pairs={{0,2},{1,3},{2,0},{3,1},{4,6},{5,7},{6,4},{7,5},{8,10},{9,11},{10,... | collective-permute-start | bytes 122888 | tf_op jit(solution)/shard_map/ppermute | solution.py:19
  55.7 1.3 %collective-permute-start.12 = (f32[4,16,128]{2,1,0:T(8,128)S(1)}, f32[4,16,128]{2,1,0:T(8,128)S(1)}, u32[]{:S(2)}, u32[]{:S(2)}) collective-permute-start(f32[4,16,128]{2,1,0:T(8,128)S(1)} %slice.214), channel_id=1, source_target_pairs={{0,4},{4,0},{8,12},{12,8},{16,20},{20,16},{24,28},{28,24},{1,5},{5... | collective-permute-start | bytes 98312 | tf_op jit(solution)/shard_map/ppermute | solution.py:19
  57.0 3.9 %collective-permute-start.13 = (f32[3,16,128]{2,1,0:T(8,128)S(1)}, f32[3,16,128]{2,1,0:T(8,128)S(1)}, u32[]{:S(2)}, u32[]{:S(2)}) collective-permute-start(f32[3,16,128]{2,1,0:T(8,128)S(1)} %slice.255), channel_id=1, source_target_pairs={{0,8},{4,12},{8,0},{12,4},{16,24},{20,28},{24,16},{28,20},{1,9},{5... | collective-permute-start | bytes 73736 | tf_op jit(solution)/shard_map/ppermute | solution.py:19
  60.9 3.8 %collective-permute-start.14 = (f32[2,16,128]{2,1,0:T(8,128)S(1)}, f32[2,16,128]{2,1,0:T(8,128)S(1)}, u32[]{:S(2)}, u32[]{:S(2)}) collective-permute-start(f32[2,16,128]{2,1,0:T(8,128)S(1)} %slice.218), channel_id=1, source_target_pairs={{0,16},{4,20},{8,24},{12,28},{16,0},{20,4},{24,8},{28,12},{1,17},{... | collective-permute-start | bytes 49160 | tf_op jit(solution)/shard_map/ppermute | solution.py:19
  67.1 3.6 %collective-permute-start.15 = (f32[16]{0:T(128)S(1)}, f32[16]{0:T(128)S(1)}, u32[]{:S(2)}, u32[]{:S(2)}) collective-permute-start(f32[16]{0:T(128)S(1)} %add.227), channel_id=1, source_target_pairs={{0,1},{1,0},{2,3},{3,2},{4,5},{5,4},{6,7},{7,6},{8,9},{9,8},{10,11... | collective-permute-start | bytes 200 | tf_op jit(solution)/shard_map/ppermute | solution.py:19
  70.7 4.4 %collective-permute-start.16 = (f32[16]{0:T(128)S(1)}, f32[16]{0:T(128)S(1)}, u32[]{:S(2)}, u32[]{:S(2)}) collective-permute-start(f32[16]{0:T(128)S(1)} %add.228), channel_id=1, source_target_pairs={{0,2},{1,3},{2,0},{3,1},{4,6},{5,7},{6,4},{7,5},{8,10},{9,11},{10,... | collective-permute-start | bytes 200 | tf_op jit(solution)/shard_map/ppermute | solution.py:19
  75.1 1.1 %collective-permute-start.17 = (f32[16]{0:T(128)S(1)}, f32[16]{0:T(128)S(1)}, u32[]{:S(2)}, u32[]{:S(2)}) collective-permute-start(f32[16]{0:T(128)S(1)} %add.232), channel_id=1, source_target_pairs={{0,4},{4,0},{8,12},{12,8},{16,20},{20,16},{24,28},{28,24},{1,5},{5... | collective-permute-start | bytes 200 | tf_op jit(solution)/shard_map/ppermute | solution.py:19
  76.3 3.5 %collective-permute-start.18 = (f32[16]{0:T(128)S(1)}, f32[16]{0:T(128)S(1)}, u32[]{:S(2)}, u32[]{:S(2)}) collective-permute-start(f32[16]{0:T(128)S(1)} %add.236), channel_id=1, source_target_pairs={{0,8},{4,12},{8,0},{12,4},{16,24},{20,28},{24,16},{28,20},{1,9},{5... | collective-permute-start | bytes 200 | tf_op jit(solution)/shard_map/ppermute | solution.py:19
  79.8 3.5 %collective-permute-start.19 = (f32[16]{0:T(128)S(1)}, f32[16]{0:T(128)S(1)}, u32[]{:S(2)}, u32[]{:S(2)}) collective-permute-start(f32[16]{0:T(128)S(1)} %add.237), channel_id=1, source_target_pairs={{0,16},{4,20},{8,24},{12,28},{16,0},{20,4},{24,8},{28,12},{1,17},{... | collective-permute-start | bytes 200 | tf_op jit(solution)/shard_map/ppermute | solution.py:19

commit v20 on v17

--- a/solution.py
+++ b/solution.py
@@ -140,8 +140,16 @@
         late, near, extra = state
         return late, near + from_union(late[half:], hot_second), extra
 
-    def permute_inputs(state):
-        stacked = to_union(jnp.concatenate(state, axis=0), hot)
+    def permute_inputs_first(state):
+        split = pieces(jnp.concatenate(state, axis=0), 0)
+        return split, jnp.einsum("cp,gip->gci", split, hot_first, preferred_element_type=jnp.float32)
+
+    def permute_inputs_second(state):
+        split, first = state
+        second = jnp.einsum("cp,gip->gci", split, hot_second, preferred_element_type=jnp.float32)
+        stacked = jnp.concatenate([first, second], axis=0)
+        count = stacked.shape[1] // 3
+        stacked = (stacked[:, :count] + stacked[:, count : 2 * count]) + stacked[:, 2 * count :]
         return stacked[:, :features] * inv_scale[None, :, None], stacked[:, features:]
 
     def kernel_blocks(state):
@@ -159,7 +167,7 @@
     residual_proj = project(residual)
     for step in range(ITERATIONS):
         if step == 0:
-            stages = [None, permute_inputs, None, kernel_blocks, first_near]
+            stages = [None, permute_inputs_first, permute_inputs_second, kernel_blocks, first_near]
             nodesum, norm_now, (kern, direction_u, near_u, product) = sums_with_norm(
                 residual, residual_proj, stages, (coords, right_side)
             )

time: 86.2 us -> 85.1 us (0.987)
  waiting for transfers between devices: 26.8 us -> 23.4 us
  starting transfers between devices: 20.6 us -> 22.8 us
    dot_general x0 -> x2, matrix products: none -> 3.6 us  [the longest x1 1.8 us: permute_inputs_first(): jnp.einsum('cp,gip->gci', split, hot_first, preferred_element_type=jnp.fl...]
    dot_general x3 -> x2, matrix products: 7.1 us -> 3.61 us  [to_union(): jnp.einsum('cp,gip->gci', pieces(values, 0), hot, preferred_element_type=...]
    ppermute x20, waiting for transfers between devices: 26.8 us -> 23.4 us  [swapped(): return lax.ppermute(value, axis, pairs)]
    ppermute x20, starting transfers between devices: 20.6 us -> 22.8 us  [swapped(): return lax.ppermute(value, axis, pairs)]
  transfers between devices with their start and end apart: 20 -> 20, of which waited for: 17 -> 16; matrix products, arithmetic and copies ran while one was open for 34% -> 35% of each run, Pallas kernels for 0% -> 0%
where the time goes in v20:
time: 85.1 us; the launch traced here: 84.8 us
  matrix products  27.5 us (32%)
  waiting for transfers between devices  23.4 us (27%)
  starting transfers between devices  22.8 us (27%)
  other arithmetic  5.93 us (7%)
  local copies, waits for them, and re-layouts  4.02 us (5%)
  between operations  1.23 us (1%)
    ppermute x20, waiting for transfers between devices, swapped(): return lax.ppermute(value, axis, pairs)  23.4 us
    ppermute x20, starting transfers between devices, swapped(): return lax.ppermute(value, axis, pairs)  22.8 us
    dot_general x4, matrix products, from_union(): jnp.einsum('gci,gip->cp', pieces(values_u, 1), hot, preferred_element_typ...  7.27 us
    dot_general x2, matrix products, near_apply(): jnp.einsum('gij,gcj->gci', kern, union_vec, precision=lax.Precision.HIGH)  3.91 us
    dot_general x2, matrix products, to_union(): jnp.einsum('cp,gip->gci', pieces(values, 0), hot, preferred_element_type=...  3.61 us
    dot_general x2, matrix products, project(): jnp.einsum('lp,cp,rp->lcr', level_gain, values, basis, precision=highest)  3.33 us
    dot_general x1, matrix products, kernel_blocks(): product = jnp.einsum('lrs,lts->lrt', coupling, coupling, precision=highest)  1.86 us
    dot_general x1, matrix products, permute_inputs_first(): jnp.einsum('cp,gip->gci', split, hot_first, preferred_element_type=jnp.fl...  1.8 us
  transfers between devices with their start and end apart: 20, of which 16 were waited for; matrix products, arithmetic and copies ran while one was open for 35% of the time, Pallas kernels for 0%

profile of v20, /device:TPU:0, one launch (start us, length us, event | category | flops | bytes accessed | tf_op | source)
XLA Modules:
  0.0 84.8 jit_solution(3785309859410163816)
XLA Ops:
  0.6 1.1 %multiply_reduce_fusion.5 = f32[16]{0:T(128)S(1)} fusion(f32[16,2048]{1,0:T(8,128)} %param.12), kind=kLoop, calls=%fused_computation.109 | loop fusion | flops 65520 | bytes 131136 | tf_op jit(solution)/shard_map/reduce_sum | solution.py:113
  1.9 2.1 %convolution_bitcast_fusion.1 = f32[5,16,128]{2,1,0:T(8,128)S(1)} fusion(f32[128,2048]{1,0:T(8,128)S(1)} %copy-done, f32[2048,5]{0,1:T(8,128)} %bitcast.73, f32[2048,16]{0,1:T(8,128)} %bitcast.72), kind=kOutput, calls=%fused_computation.35 | convolution fusion | flops 251822080 | bytes 1261568 | tf_op jit(solution)/shard_map/lp,cp,rp->lcr/dot_general | solution.py:110
  4.1 3.0 %collective-permute-start = (f32[6,16,128]{2,1,0:T(8,128)S(1)}, f32[6,16,128]{2,1,0:T(8,128)S(1)}, u32[]{:S(2)}, u32[]{:S(2)}) collective-permute-start(f32[6,16,128]{2,1,0:T(8,128)S(1)} %pad_maximum_fusion.2), channel_id=1, source_target_pairs={{0,1},{1,0},{2,3},{3,2},{4,5},{5,4},{6,7},{7,6},{8,9},{9,8},{10,11... | collective-permute-start | bytes 147464 | tf_op jit(solution)/shard_map/ppermute | solution.py:19
  7.7 1.4 %reduce.9 = s32[2048]{0:T(1024)S(1)} reduce(s32[1,2048]{1,0:T(1,128)} %param.16, s32[]{:T(128)} %broadcast.99), dimensions={0}, to_apply=%param.16.reduce_sub_computation.3 | reduce | bytes 16388 | tf_op args[7]
  9.1 0.8 fusion.89
  11.0 1.9 %convolution_multiply_fusion.2 = f32[5,128,128]{2,1,0:T(8,128)S(1)} fusion(f32[5,128,128]{2,1,0:T(8,128)} %param.15, f32[5]{0:T(128)S(1)} %multiply_power_fusion), kind=kOutput, calls=%fused_computation.29 | convolution fusion | flops 125911040 | bytes 655380 | tf_op jit(solution)/shard_map/lrs,lts->lrt/dot_general | solution.py:157
  12.9 2.7 %collective-permute-start.1 = (f32[5,16,128]{2,1,0:T(8,128)S(1)}, f32[5,16,128]{2,1,0:T(8,128)S(1)}, u32[]{:S(2)}, u32[]{:S(2)}) collective-permute-start(f32[5,16,128]{2,1,0:T(8,128)S(1)} %slice.234), channel_id=1, source_target_pairs={{0,2},{1,3},{2,0},{3,1},{4,6},{5,7},{6,4},{7,5},{8,10},{9,11},{10,... | collective-permute-start | bytes 122888 | tf_op jit(solution)/shard_map/ppermute | solution.py:19
  15.6 0.8 constant_dynamic-update-slice_fusion.1
  16.4 0.9 %constant_dynamic-update-slice_fusion = f32[24,2048]{1,0:T(8,128)S(1)} fusion(f32[24,2048]{1,0:T(8,128)S(1)} %constant_dynamic-update-slice_fusion.1, f32[16,2048]{1,0:T(8,128)} %param.12), kind=kLoop, calls=%fused_computation.178 | loop fusion | bytes 262144 | tf_op jit(solution)/shard_map/concatenate | solution.py:144
  17.4 1.8 %fusion.22 = f32[2,72,512]{2,1,0:T(8,128)S(1)} fusion(s32[2,512]{1,0:T(2,128)S(1)} %get-tuple-element.196, bf16[24,2048]{1,0:T(8,128)(2,1)S(1)} %get-tuple-element.165, bf16[24,2048]{1,0:T(8,128)(2,1)S(1)} %get-tuple-element.166, bf16[24,2048]{1,0:T(8,128)(2,1)S(1)} %get-tuple-element.164), kind=kOutput, calls=%fused_computation.30 | convolution fusion | flops 304971776 | bytes 593920 | tf_op jit(solution)/shard_map/cp,gip->gci/dot_general | solution.py:145
  19.4 1.8 %fusion.23 = f32[2,72,512]{2,1,0:T(8,128)S(1)} fusion(s32[2,512]{1,0:T(2,128)S(1)} %get-tuple-element.195, bf16[72,2048]{1,0:T(8,128)(2,1)S(1)} %pad_maximum_fusion), kind=kOutput, calls=%fused_computation.31 | convolution fusion | flops 304087040 | bytes 593920 | tf_op jit(solution)/shard_map/cp,gip->gci/dot_general | solution.py:149
  21.4 1.6 %collective-permute-start.3 = (f32[3,16,128]{2,1,0:T(8,128)S(1)}, f32[3,16,128]{2,1,0:T(8,128)S(1)}, u32[]{:S(2)}, u32[]{:S(2)}) collective-permute-start(f32[3,16,128]{2,1,0:T(8,128)S(1)} %slice.190), channel_id=1, source_target_pairs={{0,8},{4,12},{8,0},{12,4},{16,24},{20,28},{24,16},{28,20},{1,9},{5... | collective-permute-start | bytes 73736 | tf_op jit(solution)/shard_map/ppermute | solution.py:19
  23.1 1.6 %exponential_multiply_fusion = f32[4,512,512]{2,1,0:T(8,128)S(1)} fusion(bf16[4,48,512]{2,1,0:T(8,128)(2,1)S(1)} %get-tuple-element.192, bf16[4,48,512]{2,1,0:T(8,128)(2,1)S(1)} %get-tuple-element.191, f32[4,512]{1,0:T(4,128)S(1)} %multiply_reduce_fusion.6), kind=kOutput, calls=%fused_computation.12 | convolution fusion | flops 105906176 | bytes 4595712 | tf_op jit(solution)/shard_map/gfi,gfj->gij/dot_general | solution.py:33
  25.3 1.6 %collective-permute-start.4 = (f32[2,16,128]{2,1,0:T(8,128)S(1)}, f32[2,16,128]{2,1,0:T(8,128)S(1)}, u32[]{:S(2)}, u32[]{:S(2)}) collective-permute-start(f32[2,16,128]{2,1,0:T(8,128)S(1)} %slice.193), channel_id=1, source_target_pairs={{0,16},{4,20},{8,24},{12,28},{16,0},{20,4},{24,8},{28,12},{1,17},{... | collective-permute-start | bytes 49160 | tf_op jit(solution)/shard_map/ppermute | solution.py:19
  26.9 1.8 %fusion.100 = f32[4,16,512]{2,1,0:T(8,128)S(1)} fusion(f32[4,16,512]{2,1,0:T(8,128)S(1)} %slice.242, f32[4,512,512]{2,1,0:T(8,128)S(1)} %exponential_multiply_fusion), kind=kOutput, calls=%fused_computation.225 | convolution fusion | flops 100663296 | bytes 4456448 | tf_op jit(solution)/shard_map/gij,gcj->gci/dot_general | solution.py:40
  29.5 0.8 fusion.20
  31.1 1.8 %fusion.16 = f32[48,2048]{1,0:T(8,128)S(1)} fusion(s32[2,512]{1,0:T(2,128)S(1)} %get-tuple-element.196, bf16[2,16,512]{2,1,0:T(8,128)(2,1)S(1)} %get-tuple-element.183, bf16[2,16,512]{2,1,0:T(8,128)(2,1)S(1)} %get-tuple-element.184, bf16[2,16,512]{2,1,0:T(8,128)(2,1)S(1)} %get-tuple-element.182), kind=kOutput, calls=%fused_computation.23 | convolution fusion | flops 203718656 | bytes 495616 | tf_op jit(solution)/shard_map/gci,gip->cp/dot_general | solution.py:55
  33.0 1.2 %collective-permute-done.5 = f32[16]{0:T(128)S(1)} collective-permute-done((f32[16]{0:T(128)S(1)}, f32[16]{0:T(128)S(1)}, u32[]{:S(2)}, u32[]{:S(2)}) %collective-permute-start.5) | collective-permute-done | bytes 96 | tf_op jit(solution)/shard_map/ppermute | solution.py:19
  34.2 1.2 %collective-permute-start.6 = (f32[16]{0:T(128)S(1)}, f32[16]{0:T(128)S(1)}, u32[]{:S(2)}, u32[]{:S(2)}) collective-permute-start(f32[16]{0:T(128)S(1)} %add.199), channel_id=1, source_target_pairs={{0,2},{1,3},{2,0},{3,1},{4,6},{5,7},{6,4},{7,5},{8,10},{9,11},{10,... | collective-permute-start | bytes 200 | tf_op jit(solution)/shard_map/ppermute | solution.py:19
  35.4 1.8 %fusion.18 = f32[48,2048]{1,0:T(8,128)S(1)} fusion(s32[2,512]{1,0:T(2,128)S(1)} %get-tuple-element.195, bf16[2,16,512]{2,1,0:T(8,128)(2,1)S(1)} %get-tuple-element.180, bf16[2,16,512]{2,1,0:T(8,128)(2,1)S(1)} %get-tuple-element.181, bf16[2,16,512]{2,1,0:T(8,128)(2,1)S(1)} %get-tuple-element.179), kind=kOutput, calls=%fused_computation.25 | convolution fusion | flops 203718656 | bytes 495616 | tf_op jit(solution)/shard_map/gci,gip->cp/dot_general | solution.py:55
  37.3 1.3 %collective-permute-done.6 = f32[16]{0:T(128)S(1)} collective-permute-done((f32[16]{0:T(128)S(1)}, f32[16]{0:T(128)S(1)}, u32[]{:S(2)}, u32[]{:S(2)}) %collective-permute-start.6) | collective-permute-done | bytes 96 | tf_op jit(solution)/shard_map/ppermute | solution.py:19
  38.7 1.2 %convolution_bitcast_fusion = f32[5,16,128]{2,1,0:T(8,128)S(1)} fusion(f32[128,2048]{1,0:T(8,128)S(1)} %copy-done, f32[2048,16]{0,1:T(8,128)S(1)} %add_bitcast_fusion, f32[2048,5]{0,1:T(8,128)S(1)} %bitcast.74), kind=kOutput, calls=%fused_computation.34 | convolution fusion | flops 251822080 | bytes 1261568 | tf_op jit(solution)/shard_map/lp,cp,rp->lcr/dot_general | solution.py:110
  39.9 1.6 %collective-permute-start.8 = (f32[16]{0:T(128)S(1)}, f32[16]{0:T(128)S(1)}, u32[]{:S(2)}, u32[]{:S(2)}) collective-permute-start(f32[16]{0:T(128)S(1)} %add.207), channel_id=1, source_target_pairs={{0,8},{4,12},{8,0},{12,4},{16,24},{20,28},{24,16},{28,20},{1,9},{5... | collective-permute-start | bytes 200 | tf_op jit(solution)/shard_map/ppermute | solution.py:19
  41.5 2.1 %collective-permute-done.8 = f32[16]{0:T(128)S(1)} collective-permute-done((f32[16]{0:T(128)S(1)}, f32[16]{0:T(128)S(1)}, u32[]{:S(2)}, u32[]{:S(2)}) %collective-permute-start.8) | collective-permute-done | bytes 96 | tf_op jit(solution)/shard_map/ppermute | solution.py:19
  43.5 1.5 %collective-permute-start.9 = (f32[16]{0:T(128)S(1)}, f32[16]{0:T(128)S(1)}, u32[]{:S(2)}, u32[]{:S(2)}) collective-permute-start(f32[16]{0:T(128)S(1)} %add.210), channel_id=1, source_target_pairs={{0,16},{4,20},{8,24},{12,28},{16,0},{20,4},{24,8},{28,12},{1,17},{... | collective-permute-start | bytes 200 | tf_op jit(solution)/shard_map/ppermute | solution.py:19
  45.1 1.9 %collective-permute-done.9 = f32[16]{0:T(128)S(1)} collective-permute-done((f32[16]{0:T(128)S(1)}, f32[16]{0:T(128)S(1)}, u32[]{:S(2)}, u32[]{:S(2)}) %collective-permute-start.9) | collective-permute-done | bytes 96 | tf_op jit(solution)/shard_map/ppermute | solution.py:19
  47.9 1.8 %fusion.24 = f32[2,48,512]{2,1,0:T(8,128)S(1)} fusion(s32[2,512]{1,0:T(2,128)S(1)} %get-tuple-element.196, bf16[16,2048]{1,0:T(8,128)(2,1)S(1)} %get-tuple-element.177, bf16[16,2048]{1,0:T(8,128)(2,1)S(1)} %get-tuple-element.178, bf16[16,2048]{1,0:T(8,128)(2,1)S(1)} %get-tuple-element.176), kind=kOutput, calls=%fused_computation.32 | convolution fusion | flops 204013568 | bytes 397312 | tf_op jit(solution)/shard_map/cp,gip->gci/dot_general | solution.py:49
  49.8 1.7 %collective-permute-done.10 = f32[6,16,128]{2,1,0:T(8,128)S(1)} collective-permute-done((f32[6,16,128]{2,1,0:T(8,128)S(1)}, f32[6,16,128]{2,1,0:T(8,128)S(1)}, u32[]{:S(2)}, u32[]{:S(2)}) %collective-permute-start.10) | collective-permute-done | bytes 49184 | tf_op jit(solution)/shard_map/ppermute | solution.py:19
  51.5 1.3 %collective-permute-start.11 = (f32[5,16,128]{2,1,0:T(8,128)S(1)}, f32[5,16,128]{2,1,0:T(8,128)S(1)}, u32[]{:S(2)}, u32[]{:S(2)}) collective-permute-start(f32[5,16,128]{2,1,0:T(8,128)S(1)} %slice.209), channel_id=1, source_target_pairs={{0,2},{1,3},{2,0},{3,1},{4,6},{5,7},{6,4},{7,5},{8,10},{9,11},{10,... | collective-permute-start | bytes 122888 | tf_op jit(solution)/shard_map/ppermute | solution.py:19
  52.9 1.8 %fusion.25 = f32[2,48,512]{2,1,0:T(8,128)S(1)} fusion(s32[2,512]{1,0:T(2,128)S(1)} %get-tuple-element.195, bf16[16,2048]{1,0:T(8,128)(2,1)S(1)} %get-tuple-element.174, bf16[16,2048]{1,0:T(8,128)(2,1)S(1)} %get-tuple-element.175, bf16[16,2048]{1,0:T(8,128)(2,1)S(1)} %get-tuple-element.173), kind=kOutput, calls=%fused_computation.33 | convolution fusion | flops 204013568 | bytes 397312 | tf_op jit(solution)/shard_map/cp,gip->gci/dot_general | solution.py:49
  54.7 2.1 %collective-permute-done.11 = f32[5,16,128]{2,1,0:T(8,128)S(1)} collective-permute-done((f32[5,16,128]{2,1,0:T(8,128)S(1)}, f32[5,16,128]{2,1,0:T(8,128)S(1)}, u32[]{:S(2)}, u32[]{:S(2)}) %collective-permute-start.11) | collective-permute-done | bytes 40992 | tf_op jit(solution)/shard_map/ppermute | solution.py:19
  57.0 1.2 %collective-permute-done.12 = f32[4,16,128]{2,1,0:T(8,128)S(1)} collective-permute-done((f32[4,16,128]{2,1,0:T(8,128)S(1)}, f32[4,16,128]{2,1,0:T(8,128)S(1)}, u32[]{:S(2)}, u32[]{:S(2)}) %collective-permute-start.12) | collective-permute-done | bytes 32800 | tf_op jit(solution)/shard_map/ppermute | solution.py:19
  58.2 1.6 %collective-permute-start.13 = (f32[3,16,128]{2,1,0:T(8,128)S(1)}, f32[3,16,128]{2,1,0:T(8,128)S(1)}, u32[]{:S(2)}, u32[]{:S(2)}) collective-permute-start(f32[3,16,128]{2,1,0:T(8,128)S(1)} %slice.255), channel_id=1, source_target_pairs={{0,8},{4,12},{8,0},{12,4},{16,24},{20,28},{24,16},{28,20},{1,9},{5... | collective-permute-start | bytes 73736 | tf_op jit(solution)/shard_map/ppermute | solution.py:19
  59.8 2.1 %fusion.102 = f32[4,16,512]{2,1,0:T(8,128)S(1)} fusion(f32[4,16,512]{2,1,0:T(8,128)S(1)} %constant_dynamic-update-slice_fusion.16, f32[4,512,512]{2,1,0:T(8,128)S(1)} %exponential_multiply_fusion), kind=kOutput, calls=%fused_computation.227 | convolution fusion | flops 100663296 | bytes 4456448 | tf_op jit(solution)/shard_map/gij,gcj->gci/dot_general | solution.py:40
  62.1 1.6 %collective-permute-start.14 = (f32[2,16,128]{2,1,0:T(8,128)S(1)}, f32[2,16,128]{2,1,0:T(8,128)S(1)}, u32[]{:S(2)}, u32[]{:S(2)}) collective-permute-start(f32[2,16,128]{2,1,0:T(8,128)S(1)} %slice.218), channel_id=1, source_target_pairs={{0,16},{4,20},{8,24},{12,28},{16,0},{20,4},{24,8},{28,12},{1,17},{... | collective-permute-start | bytes 49160 | tf_op jit(solution)/shard_map/ppermute | solution.py:19
  63.7 2.2 %collective-permute-done.14 = f32[2,16,128]{2,1,0:T(8,128)S(1)} collective-permute-done((f32[2,16,128]{2,1,0:T(8,128)S(1)}, f32[2,16,128]{2,1,0:T(8,128)S(1)}, u32[]{:S(2)}, u32[]{:S(2)}) %collective-permute-start.14) | collective-permute-done | bytes 16416 | tf_op jit(solution)/shard_map/ppermute | solution.py:19
  66.5 0.8 fusion.21
  67.9 1.8 %fusion.17 = f32[48,2048]{1,0:T(8,128)S(1)} fusion(s32[2,512]{1,0:T(2,128)S(1)} %get-tuple-element.196, bf16[2,16,512]{2,1,0:T(8,128)(2,1)S(1)} %get-tuple-element.171, bf16[2,16,512]{2,1,0:T(8,128)(2,1)S(1)} %get-tuple-element.172, bf16[2,16,512]{2,1,0:T(8,128)(2,1)S(1)} %get-tuple-element.170), kind=kOutput, calls=%fused_computation.24 | convolution fusion | flops 203718656 | bytes 495616 | tf_op jit(solution)/shard_map/gci,gip->cp/dot_general | solution.py:55
  69.8 1.5 %collective-permute-done.15 = f32[16]{0:T(128)S(1)} collective-permute-done((f32[16]{0:T(128)S(1)}, f32[16]{0:T(128)S(1)}, u32[]{:S(2)}, u32[]{:S(2)}) %collective-permute-start.15) | collective-permute-done | bytes 96 | tf_op jit(solution)/shard_map/ppermute | solution.py:19
  71.3 0.9 %collective-permute-start.16 = (f32[16]{0:T(128)S(1)}, f32[16]{0:T(128)S(1)}, u32[]{:S(2)}, u32[]{:S(2)}) collective-permute-start(f32[16]{0:T(128)S(1)} %add.228), channel_id=1, source_target_pairs={{0,2},{1,3},{2,0},{3,1},{4,6},{5,7},{6,4},{7,5},{8,10},{9,11},{10,... | collective-permute-start | bytes 200 | tf_op jit(solution)/shard_map/ppermute | solution.py:19
  72.2 1.8 %fusion.19 = f32[48,2048]{1,0:T(8,128)S(1)} fusion(s32[2,512]{1,0:T(2,128)S(1)} %get-tuple-element.195, bf16[2,16,512]{2,1,0:T(8,128)(2,1)S(1)} %get-tuple-element.168, bf16[2,16,512]{2,1,0:T(8,128)(2,1)S(1)} %get-tuple-element.169, bf16[2,16,512]{2,1,0:T(8,128)(2,1)S(1)} %get-tuple-element.167), kind=kOutput, calls=%fused_computation.26 | convolution fusion | flops 203718656 | bytes 495616 | tf_op jit(solution)/shard_map/gci,gip->cp/dot_general | solution.py:55
  74.0 1.7 %collective-permute-done.16 = f32[16]{0:T(128)S(1)} collective-permute-done((f32[16]{0:T(128)S(1)}, f32[16]{0:T(128)S(1)}, u32[]{:S(2)}, u32[]{:S(2)}) %collective-permute-start.16) | collective-permute-done | bytes 96 | tf_op jit(solution)/shard_map/ppermute | solution.py:19
  75.7 1.1 %collective-permute-done.17 = f32[16]{0:T(128)S(1)} collective-permute-done((f32[16]{0:T(128)S(1)}, f32[16]{0:T(128)S(1)}, u32[]{:S(2)}, u32[]{:S(2)}) %collective-permute-start.17) | collective-permute-done | bytes 96 | tf_op jit(solution)/shard_map/ppermute | solution.py:19
  76.9 1.5 %collective-permute-start.18 = (f32[16]{0:T(128)S(1)}, f32[16]{0:T(128)S(1)}, u32[]{:S(2)}, u32[]{:S(2)}) collective-permute-start(f32[16]{0:T(128)S(1)} %add.236), channel_id=1, source_target_pairs={{0,8},{4,12},{8,0},{12,4},{16,24},{20,28},{24,16},{28,20},{1,9},{5... | collective-permute-start | bytes 200 | tf_op jit(solution)/shard_map/ppermute | solution.py:19
  78.4 2.1 %collective-permute-done.18 = f32[16]{0:T(128)S(1)} collective-permute-done((f32[16]{0:T(128)S(1)}, f32[16]{0:T(128)S(1)}, u32[]{:S(2)}, u32[]{:S(2)}) %collective-permute-start.18) | collective-permute-done | bytes 96 | tf_op jit(solution)/shard_map/ppermute | solution.py:19
  80.4 1.5 %collective-permute-start.19 = (f32[16]{0:T(128)S(1)}, f32[16]{0:T(128)S(1)}, u32[]{:S(2)}, u32[]{:S(2)}) collective-permute-start(f32[16]{0:T(128)S(1)} %add.237), channel_id=1, source_target_pairs={{0,16},{4,20},{8,24},{12,28},{16,0},{20,4},{24,8},{28,12},{1,17},{... | collective-permute-start | bytes 200 | tf_op jit(solution)/shard_map/ppermute | solution.py:19
  81.9 2.0 %collective-permute-done.19 = f32[16]{0:T(128)S(1)} collective-permute-done((f32[16]{0:T(128)S(1)}, f32[16]{0:T(128)S(1)}, u32[]{:S(2)}, u32[]{:S(2)}) %collective-permute-start.19) | collective-permute-done | bytes 96 | tf_op jit(solution)/shard_map/ppermute | solution.py:19
  84.0 0.8 multiply_subtract_fusion
  (124 shorter events, 7.4 us)
Async XLA Ops:
  0.6 1.3 %copy-start = (f32[128,2048]{1,0:T(8,128)S(1)}, f32[128,2048]{1,0:T(8,128)}, u32[]{:S(2)}) copy-start(f32[128,2048]{1,0:T(8,128)} %param.13) | copy-start | bytes 3145732
  4.1 8.7 %collective-permute-start = (f32[6,16,128]{2,1,0:T(8,128)S(1)}, f32[6,16,128]{2,1,0:T(8,128)S(1)}, u32[]{:S(2)}, u32[]{:S(2)}) collective-permute-start(f32[6,16,128]{2,1,0:T(8,128)S(1)} %pad_maximum_fusion.2), channel_id=1, source_target_pairs={{0,1},{1,0},{2,3},{3,2},{4,5},{5,4},{6,7},{7,6},{8,9},{9,8},{10,11... | collective-permute-start | bytes 147464 | tf_op jit(solution)/shard_map/ppermute | solution.py:19
  12.9 6.3 %collective-permute-start.1 = (f32[5,16,128]{2,1,0:T(8,128)S(1)}, f32[5,16,128]{2,1,0:T(8,128)S(1)}, u32[]{:S(2)}, u32[]{:S(2)}) collective-permute-start(f32[5,16,128]{2,1,0:T(8,128)S(1)} %slice.234), channel_id=1, source_target_pairs={{0,2},{1,3},{2,0},{3,1},{4,6},{5,7},{6,4},{7,5},{8,10},{9,11},{10,... | collective-permute-start | bytes 122888 | tf_op jit(solution)/shard_map/ppermute | solution.py:19
  17.4 3.8 %copy-start.4 = (f32[8]{0:T(128)S(1)}, f32[8]{0:T(128)}, u32[]{:S(2)}) copy-start(f32[8]{0:T(128)} %param.10) | copy-start | bytes 100
  19.3 2.0 %collective-permute-start.2 = (f32[4,16,128]{2,1,0:T(8,128)S(1)}, f32[4,16,128]{2,1,0:T(8,128)S(1)}, u32[]{:S(2)}, u32[]{:S(2)}) collective-permute-start(f32[4,16,128]{2,1,0:T(8,128)S(1)} %slice.181), channel_id=1, source_target_pairs={{0,4},{4,0},{8,12},{12,8},{16,20},{20,16},{24,28},{28,24},{1,5},{5... | collective-permute-start | bytes 98312 | tf_op jit(solution)/shard_map/ppermute | solution.py:19
  21.4 3.9 %collective-permute-start.3 = (f32[3,16,128]{2,1,0:T(8,128)S(1)}, f32[3,16,128]{2,1,0:T(8,128)S(1)}, u32[]{:S(2)}, u32[]{:S(2)}) collective-permute-start(f32[3,16,128]{2,1,0:T(8,128)S(1)} %slice.190), channel_id=1, source_target_pairs={{0,8},{4,12},{8,0},{12,4},{16,24},{20,28},{24,16},{28,20},{1,9},{5... | collective-permute-start | bytes 73736 | tf_op jit(solution)/shard_map/ppermute | solution.py:19
  24.7 4.8 %copy-start.2 = (f32[5,2048]{1,0:T(8,128)S(1)}, f32[5,2048]{1,0:T(8,128)}, u32[]{:S(2)}) copy-start(f32[5,2048]{1,0:T(8,128)} %param.14) | copy-start | bytes 122884
  24.7 5.7 %copy-start.1 = (f32[16,2048]{1,0:T(8,128)S(1)}, f32[16,2048]{1,0:T(8,128)}, u32[]{:S(2)}) copy-start(f32[16,2048]{1,0:T(8,128)} %param.12) | copy-start | bytes 393220
  24.8 5.7 %copy-start.3 = (f32[2048]{0:T(1024)S(1)}, f32[2048]{0:T(1024)}, u32[]{:S(2)}) copy-start(f32[2048]{0:T(1024)} %param.11) | copy-start | bytes 24580
  25.3 3.8 %collective-permute-start.4 = (f32[2,16,128]{2,1,0:T(8,128)S(1)}, f32[2,16,128]{2,1,0:T(8,128)S(1)}, u32[]{:S(2)}, u32[]{:S(2)}) collective-permute-start(f32[2,16,128]{2,1,0:T(8,128)S(1)} %slice.193), channel_id=1, source_target_pairs={{0,16},{4,20},{8,24},{12,28},{16,0},{20,4},{24,8},{28,12},{1,17},{... | collective-permute-start | bytes 49160 | tf_op jit(solution)/shard_map/ppermute | solution.py:19
  30.6 3.6 %collective-permute-start.5 = (f32[16]{0:T(128)S(1)}, f32[16]{0:T(128)S(1)}, u32[]{:S(2)}, u32[]{:S(2)}) collective-permute-start(f32[16]{0:T(128)S(1)} %add.198), channel_id=1, source_target_pairs={{0,1},{1,0},{2,3},{3,2},{4,5},{5,4},{6,7},{7,6},{8,9},{9,8},{10,11... | collective-permute-start | bytes 200 | tf_op jit(solution)/shard_map/ppermute | solution.py:19
  34.2 4.4 %collective-permute-start.6 = (f32[16]{0:T(128)S(1)}, f32[16]{0:T(128)S(1)}, u32[]{:S(2)}, u32[]{:S(2)}) collective-permute-start(f32[16]{0:T(128)S(1)} %add.199), channel_id=1, source_target_pairs={{0,2},{1,3},{2,0},{3,1},{4,6},{5,7},{6,4},{7,5},{8,10},{9,11},{10,... | collective-permute-start | bytes 200 | tf_op jit(solution)/shard_map/ppermute | solution.py:19
  38.7 1.2 %collective-permute-start.7 = (f32[16]{0:T(128)S(1)}, f32[16]{0:T(128)S(1)}, u32[]{:S(2)}, u32[]{:S(2)}) collective-permute-start(f32[16]{0:T(128)S(1)} %add.203), channel_id=1, source_target_pairs={{0,4},{4,0},{8,12},{12,8},{16,20},{20,16},{24,28},{28,24},{1,5},{5... | collective-permute-start | bytes 200 | tf_op jit(solution)/shard_map/ppermute | solution.py:19
  39.9 3.6 %collective-permute-start.8 = (f32[16]{0:T(128)S(1)}, f32[16]{0:T(128)S(1)}, u32[]{:S(2)}, u32[]{:S(2)}) collective-permute-start(f32[16]{0:T(128)S(1)} %add.207), channel_id=1, source_target_pairs={{0,8},{4,12},{8,0},{12,4},{16,24},{20,28},{24,16},{28,20},{1,9},{5... | collective-permute-start | bytes 200 | tf_op jit(solution)/shard_map/ppermute | solution.py:19
  43.5 3.5 %collective-permute-start.9 = (f32[16]{0:T(128)S(1)}, f32[16]{0:T(128)S(1)}, u32[]{:S(2)}, u32[]{:S(2)}) collective-permute-start(f32[16]{0:T(128)S(1)} %add.210), channel_id=1, source_target_pairs={{0,16},{4,20},{8,24},{12,28},{16,0},{20,4},{24,8},{28,12},{1,17},{... | collective-permute-start | bytes 200 | tf_op jit(solution)/shard_map/ppermute | solution.py:19
  47.4 4.1 %collective-permute-start.10 = (f32[6,16,128]{2,1,0:T(8,128)S(1)}, f32[6,16,128]{2,1,0:T(8,128)S(1)}, u32[]{:S(2)}, u32[]{:S(2)}) collective-permute-start(f32[6,16,128]{2,1,0:T(8,128)S(1)} %pad_maximum_fusion.7), channel_id=1, source_target_pairs={{0,1},{1,0},{2,3},{3,2},{4,5},{5,4},{6,7},{7,6},{8,9},{9,8},{10,11... | collective-permute-start | bytes 147464 | tf_op jit(solution)/shard_map/ppermute | solution.py:19
  51.5 5.3 %collective-permute-start.11 = (f32[5,16,128]{2,1,0:T(8,128)S(1)}, f32[5,16,128]{2,1,0:T(8,128)S(1)}, u32[]{:S(2)}, u32[]{:S(2)}) collective-permute-start(f32[5,16,128]{2,1,0:T(8,128)S(1)} %slice.209), channel_id=1, source_target_pairs={{0,2},{1,3},{2,0},{3,1},{4,6},{5,7},{6,4},{7,5},{8,10},{9,11},{10,... | collective-permute-start | bytes 122888 | tf_op jit(solution)/shard_map/ppermute | solution.py:19
  56.9 1.3 %collective-permute-start.12 = (f32[4,16,128]{2,1,0:T(8,128)S(1)}, f32[4,16,128]{2,1,0:T(8,128)S(1)}, u32[]{:S(2)}, u32[]{:S(2)}) collective-permute-start(f32[4,16,128]{2,1,0:T(8,128)S(1)} %slice.214), channel_id=1, source_target_pairs={{0,4},{4,0},{8,12},{12,8},{16,20},{20,16},{24,28},{28,24},{1,5},{5... | collective-permute-start | bytes 98312 | tf_op jit(solution)/shard_map/ppermute | solution.py:19
  58.2 3.9 %collective-permute-start.13 = (f32[3,16,128]{2,1,0:T(8,128)S(1)}, f32[3,16,128]{2,1,0:T(8,128)S(1)}, u32[]{:S(2)}, u32[]{:S(2)}) collective-permute-start(f32[3,16,128]{2,1,0:T(8,128)S(1)} %slice.255), channel_id=1, source_target_pairs={{0,8},{4,12},{8,0},{12,4},{16,24},{20,28},{24,16},{28,20},{1,9},{5... | collective-permute-start | bytes 73736 | tf_op jit(solution)/shard_map/ppermute | solution.py:19
  62.1 3.8 %collective-permute-start.14 = (f32[2,16,128]{2,1,0:T(8,128)S(1)}, f32[2,16,128]{2,1,0:T(8,128)S(1)}, u32[]{:S(2)}, u32[]{:S(2)}) collective-permute-start(f32[2,16,128]{2,1,0:T(8,128)S(1)} %slice.218), channel_id=1, source_target_pairs={{0,16},{4,20},{8,24},{12,28},{16,0},{20,4},{24,8},{28,12},{1,17},{... | collective-permute-start | bytes 49160 | tf_op jit(solution)/shard_map/ppermute | solution.py:19
  67.7 3.6 %collective-permute-start.15 = (f32[16]{0:T(128)S(1)}, f32[16]{0:T(128)S(1)}, u32[]{:S(2)}, u32[]{:S(2)}) collective-permute-start(f32[16]{0:T(128)S(1)} %add.227), channel_id=1, source_target_pairs={{0,1},{1,0},{2,3},{3,2},{4,5},{5,4},{6,7},{7,6},{8,9},{9,8},{10,11... | collective-permute-start | bytes 200 | tf_op jit(solution)/shard_map/ppermute | solution.py:19
  71.3 4.4 %collective-permute-start.16 = (f32[16]{0:T(128)S(1)}, f32[16]{0:T(128)S(1)}, u32[]{:S(2)}, u32[]{:S(2)}) collective-permute-start(f32[16]{0:T(128)S(1)} %add.228), channel_id=1, source_target_pairs={{0,2},{1,3},{2,0},{3,1},{4,6},{5,7},{6,4},{7,5},{8,10},{9,11},{10,... | collective-permute-start | bytes 200 | tf_op jit(solution)/shard_map/ppermute | solution.py:19
  75.7 1.1 %collective-permute-start.17 = (f32[16]{0:T(128)S(1)}, f32[16]{0:T(128)S(1)}, u32[]{:S(2)}, u32[]{:S(2)}) collective-permute-start(f32[16]{0:T(128)S(1)} %add.232), channel_id=1, source_target_pairs={{0,4},{4,0},{8,12},{12,8},{16,20},{20,16},{24,28},{28,24},{1,5},{5... | collective-permute-start | bytes 200 | tf_op jit(solution)/shard_map/ppermute | solution.py:19
  76.9 3.5 %collective-permute-start.18 = (f32[16]{0:T(128)S(1)}, f32[16]{0:T(128)S(1)}, u32[]{:S(2)}, u32[]{:S(2)}) collective-permute-start(f32[16]{0:T(128)S(1)} %add.236), channel_id=1, source_target_pairs={{0,8},{4,12},{8,0},{12,4},{16,24},{20,28},{24,16},{28,20},{1,9},{5... | collective-permute-start | bytes 200 | tf_op jit(solution)/shard_map/ppermute | solution.py:19
  80.4 3.5 %collective-permute-start.19 = (f32[16]{0:T(128)S(1)}, f32[16]{0:T(128)S(1)}, u32[]{:S(2)}, u32[]{:S(2)}) collective-permute-start(f32[16]{0:T(128)S(1)} %add.237), channel_id=1, source_target_pairs={{0,16},{4,20},{8,24},{12,28},{16,0},{20,4},{24,8},{28,12},{1,17},{... | collective-permute-start | bytes 200 | tf_op jit(solution)/shard_map/ppermute | solution.py:19

commit v21 on v19

--- a/solution.py
+++ b/solution.py
@@ -115,6 +115,9 @@
         running, state = tree_sums(jnp.concatenate([proj, extra], axis=0), stages, state)
         return running[:levels], running[levels, :, 0], state
 
+    def sums_alone(proj, stages, state):
+        return tree_sums(proj, stages, state)
+
     def permute_first(state):
         values, first, second = state
         return values, to_union(values, hot_first), second
@@ -167,9 +170,10 @@
     for step in range(ITERATIONS):
         if step == 0:
             stages = [None, permute_inputs_first, permute_inputs_second, kernel_blocks, first_near]
-            nodesum, norm_now, (kern, direction_u, near_u) = sums_with_norm(
-                residual, residual_proj, stages, (coords, right_side)
+            nodesum, (kern, direction_u, near_u) = sums_alone(
+                residual_proj, stages, (coords, right_side)
             )
+            norm_now = None
             late_u, nodesum = lax.optimization_barrier((near_u, nodesum))
             carried = jnp.zeros_like(right_side)
         else:
@@ -194,6 +198,8 @@
         far = jnp.sum(back * level_gain[:, None, :], axis=0)
         base = noise[None, :] * direction + far
         local = jnp.sum(direction * base, axis=1) + jnp.sum(direction_u * near_u, axis=(0, 2))
+        if norm_now is None:
+            local = jnp.concatenate([local, jnp.sum(residual * residual, axis=1)])
         def project_image(state, base=base):
             late, near, extra = state
             return late, near, project(base + near)
@@ -202,6 +208,8 @@
         if step + 1 < ITERATIONS:
             stages.append(project_image)
         curve, (late_u, near, image_proj) = butterfly(local, stages, (late_u, carried, carried))
+        if norm_now is None:
+            curve, norm_now = curve[:columns], curve[columns:]
         alpha = norm_now / curve
         solution = solution + alpha[:, None] * direction
         residual = residual - alpha[:, None] * (base + near)

time: 84.5 us -> 84.3 us (level)
  other arithmetic: 5.93 us -> 4.91 us
  local copies, waits for them, and re-layouts: 4.02 us -> 5 us
    reduce_sum x2 -> x1, other arithmetic: 1.33 us -> 0.2 us  [sums_with_norm(): norm = jnp.sum(values * values, axis=1)]
    unnamed x21, local copies, waits for them, and re-layouts: 1.6 us -> 2.65 us
where the time goes in v21:
time: 84.3 us; the launch traced here: 84 us
  matrix products  26.9 us (32%)
  waiting for transfers between devices  23.5 us (28%)
  starting transfers between devices  22.5 us (27%)
  local copies, waits for them, and re-layouts  5 us (6%)
  other arithmetic  4.91 us (6%)
  between operations  1.24 us (1%)
    ppermute x20, waiting for transfers between devices, swapped(): return lax.ppermute(value, axis, pairs)  23.5 us
    ppermute x20, starting transfers between devices, swapped(): return lax.ppermute(value, axis, pairs)  22.5 us
    dot_general x4, matrix products, from_union(): jnp.einsum('gci,gip->cp', pieces(values_u, 1), hot, preferred_element_typ...  7.26 us
    dot_general x2, matrix products, near_apply(): jnp.einsum('gij,gcj->gci', kern, union_vec, precision=lax.Precision.HIGH)  3.91 us
    dot_general x2, matrix products, to_union(): jnp.einsum('cp,gip->gci', pieces(values, 0), hot, preferred_element_type=...  3.61 us
    dot_general x2, matrix products, project(): jnp.einsum('lp,cp,rp->lcr', level_gain, values, basis, precision=highest)  3.34 us
    unnamed x21, local copies, waits for them, and re-layouts  2.65 us
    dot_general x1, matrix products, permute_inputs_first(): jnp.einsum('cp,gip->gci', split, hot_first, preferred_element_type=jnp.fl...  1.8 us
  transfers between devices with their start and end apart: 20, of which 16 were waited for; matrix products, arithmetic and copies ran while one was open for 33% of the time, Pallas kernels for 0%

profile of v21, /device:TPU:0, one launch (start us, length us, event | category | flops | bytes accessed | tf_op | source)
XLA Modules:
  0.0 84.0 jit_solution(12143880339722605545)
XLA Ops:
  0.6 1.2 %copy-done = f32[128,2048]{1,0:T(8,128)S(1)} copy-done((f32[128,2048]{1,0:T(8,128)S(1)}, f32[128,2048]{1,0:T(8,128)}, u32[]{:S(2)}) %copy-start) | copy-done | bytes 1048600
  1.9 2.1 %convolution_bitcast_fusion.1 = f32[5,16,128]{2,1,0:T(8,128)S(1)} fusion(f32[128,2048]{1,0:T(8,128)S(1)} %copy-done, f32[2048,5]{0,1:T(8,128)} %bitcast.75, f32[2048,16]{0,1:T(8,128)} %bitcast.74), kind=kOutput, calls=%fused_computation.34 | convolution fusion | flops 251822080 | bytes 1261568 | tf_op jit(solution)/shard_map/lp,cp,rp->lcr/dot_general | solution.py:110
  4.0 3.1 %collective-permute-start = (f32[5,16,128]{2,1,0:T(8,128)S(1)}, f32[5,16,128]{2,1,0:T(8,128)S(1)}, u32[]{:S(2)}, u32[]{:S(2)}) collective-permute-start(f32[5,16,128]{2,1,0:T(8,128)S(1)} %convolution_bitcast_fusion.1), channel_id=1, source_target_pairs={{0,1},{1,0},{2,3},{3,2},{4,5},{5,4},{6,7},{7,6},{8,9},{9,8},{10,11... | collective-permute-start | bytes 122888 | tf_op jit(solution)/shard_map/ppermute | solution.py:19
  7.1 0.8 fusion.89
  8.3 1.4 %reduce.5 = s32[2048]{0:T(1024)S(1)} reduce(s32[1,2048]{1,0:T(1,128)} %param.16, s32[]{:T(128)} %broadcast.97), dimensions={0}, to_apply=%param.16.reduce_sub_computation.3 | reduce | bytes 16388 | tf_op args[7]
  11.0 2.7 %collective-permute-start.1 = (f32[4,16,128]{2,1,0:T(8,128)S(1)}, f32[4,16,128]{2,1,0:T(8,128)S(1)}, u32[]{:S(2)}, u32[]{:S(2)}) collective-permute-start(f32[4,16,128]{2,1,0:T(8,128)S(1)} %slice.234), channel_id=1, source_target_pairs={{0,2},{1,3},{2,0},{3,1},{4,6},{5,7},{6,4},{7,5},{8,10},{9,11},{10,... | collective-permute-start | bytes 98312 | tf_op jit(solution)/shard_map/ppermute | solution.py:19
  13.6 0.8 %constant_dynamic-update-slice_fusion.1 = f32[24,2048]{1,0:T(8,128)S(1)} fusion(f32[8,2048]{1,0:T(8,128)} %param.9), kind=kLoop, calls=%fused_computation.178 | loop fusion | bytes 131072
  14.5 0.9 %constant_dynamic-update-slice_fusion = f32[24,2048]{1,0:T(8,128)S(1)} fusion(f32[24,2048]{1,0:T(8,128)S(1)} %constant_dynamic-update-slice_fusion.1, f32[16,2048]{1,0:T(8,128)} %param.12), kind=kLoop, calls=%fused_computation.177 | loop fusion | bytes 262144 | tf_op jit(solution)/shard_map/concatenate | solution.py:147
  15.4 1.8 %fusion.22 = f32[2,72,512]{2,1,0:T(8,128)S(1)} fusion(s32[2,512]{1,0:T(2,128)S(1)} %get-tuple-element.188, bf16[24,2048]{1,0:T(8,128)(2,1)S(1)} %get-tuple-element.159, bf16[24,2048]{1,0:T(8,128)(2,1)S(1)} %get-tuple-element.160, bf16[24,2048]{1,0:T(8,128)(2,1)S(1)} %get-tuple-element.158), kind=kOutput, calls=%fused_computation.29 | convolution fusion | flops 304971776 | bytes 593920 | tf_op jit(solution)/shard_map/cp,gip->gci/dot_general | solution.py:148
  17.4 1.8 %fusion.23 = f32[2,72,512]{2,1,0:T(8,128)S(1)} fusion(s32[2,512]{1,0:T(2,128)S(1)} %get-tuple-element.187, bf16[72,2048]{1,0:T(8,128)(2,1)S(1)} %pad_maximum_fusion), kind=kOutput, calls=%fused_computation.30 | convolution fusion | flops 304087040 | bytes 593920 | tf_op jit(solution)/shard_map/cp,gip->gci/dot_general | solution.py:152
  19.5 1.6 %collective-permute-start.3 = (f32[2,16,128]{2,1,0:T(8,128)S(1)}, f32[2,16,128]{2,1,0:T(8,128)S(1)}, u32[]{:S(2)}, u32[]{:S(2)}) collective-permute-start(f32[2,16,128]{2,1,0:T(8,128)S(1)} %slice.190), channel_id=1, source_target_pairs={{0,8},{4,12},{8,0},{12,4},{16,24},{20,28},{24,16},{28,20},{1,9},{5... | collective-permute-start | bytes 49160 | tf_op jit(solution)/shard_map/ppermute | solution.py:19
  21.2 1.6 %exponential_multiply_fusion = f32[4,512,512]{2,1,0:T(8,128)S(1)} fusion(bf16[4,48,512]{2,1,0:T(8,128)(2,1)S(1)} %get-tuple-element.184, bf16[4,48,512]{2,1,0:T(8,128)(2,1)S(1)} %get-tuple-element.183, f32[4,512]{1,0:T(4,128)S(1)} %multiply_reduce_fusion.6), kind=kOutput, calls=%fused_computation.12 | convolution fusion | flops 105906176 | bytes 4595712 | tf_op jit(solution)/shard_map/gfi,gfj->gij/dot_general | solution.py:33
  23.3 1.6 %collective-permute-start.4 = (f32[1,16,128]{2,1,0:T(8,128)S(1)}, f32[1,16,128]{2,1,0:T(8,128)S(1)}, u32[]{:S(2)}, u32[]{:S(2)}) collective-permute-start(f32[1,16,128]{2,1,0:T(8,128)S(1)} %slice.193), channel_id=1, source_target_pairs={{0,16},{4,20},{8,24},{12,28},{16,0},{20,4},{24,8},{28,12},{1,17},{... | collective-permute-start | bytes 24584 | tf_op jit(solution)/shard_map/ppermute | solution.py:19
  24.9 1.8 %fusion.98 = f32[4,16,512]{2,1,0:T(8,128)S(1)} fusion(f32[4,16,512]{2,1,0:T(8,128)S(1)} %slice.242, f32[4,512,512]{2,1,0:T(8,128)S(1)} %exponential_multiply_fusion), kind=kOutput, calls=%fused_computation.223 | convolution fusion | flops 100663296 | bytes 4456448 | tf_op jit(solution)/shard_map/gij,gcj->gci/dot_general | solution.py:40
  27.5 0.6 convolution_multiply_fusion.3
  28.2 0.8 fusion.20
  29.7 1.8 %fusion.16 = f32[48,2048]{1,0:T(8,128)S(1)} fusion(s32[2,512]{1,0:T(2,128)S(1)} %get-tuple-element.188, bf16[2,16,512]{2,1,0:T(8,128)(2,1)S(1)} %get-tuple-element.177, bf16[2,16,512]{2,1,0:T(8,128)(2,1)S(1)} %get-tuple-element.178, bf16[2,16,512]{2,1,0:T(8,128)(2,1)S(1)} %get-tuple-element.176), kind=kOutput, calls=%fused_computation.23 | convolution fusion | flops 203718656 | bytes 495616 | tf_op jit(solution)/shard_map/gci,gip->cp/dot_general | solution.py:55
  31.5 1.2 %collective-permute-done.5 = f32[32]{0:T(128)S(1)} collective-permute-done((f32[32]{0:T(128)S(1)}, f32[32]{0:T(128)S(1)}, u32[]{:S(2)}, u32[]{:S(2)}) %collective-permute-start.5) | collective-permute-done | bytes 160 | tf_op jit(solution)/shard_map/ppermute | solution.py:19
  32.7 1.1 %collective-permute-start.6 = (f32[32]{0:T(128)S(1)}, f32[32]{0:T(128)S(1)}, u32[]{:S(2)}, u32[]{:S(2)}) collective-permute-start(f32[32]{0:T(128)S(1)} %add.199), channel_id=1, source_target_pairs={{0,2},{1,3},{2,0},{3,1},{4,6},{5,7},{6,4},{7,5},{8,10},{9,11},{10,... | collective-permute-start | bytes 392 | tf_op jit(solution)/shard_map/ppermute | solution.py:19
  33.9 1.8 %fusion.18 = f32[48,2048]{1,0:T(8,128)S(1)} fusion(s32[2,512]{1,0:T(2,128)S(1)} %get-tuple-element.187, bf16[2,16,512]{2,1,0:T(8,128)(2,1)S(1)} %get-tuple-element.174, bf16[2,16,512]{2,1,0:T(8,128)(2,1)S(1)} %get-tuple-element.175, bf16[2,16,512]{2,1,0:T(8,128)(2,1)S(1)} %get-tuple-element.173), kind=kOutput, calls=%fused_computation.25 | convolution fusion | flops 203718656 | bytes 495616 | tf_op jit(solution)/shard_map/gci,gip->cp/dot_general | solution.py:55
  35.7 1.4 %collective-permute-done.6 = f32[32]{0:T(128)S(1)} collective-permute-done((f32[32]{0:T(128)S(1)}, f32[32]{0:T(128)S(1)}, u32[]{:S(2)}, u32[]{:S(2)}) %collective-permute-start.6) | collective-permute-done | bytes 160 | tf_op jit(solution)/shard_map/ppermute | solution.py:19
  37.2 1.2 %convolution_bitcast_fusion = f32[5,16,128]{2,1,0:T(8,128)S(1)} fusion(f32[128,2048]{1,0:T(8,128)S(1)} %copy-done, f32[2048,16]{0,1:T(8,128)S(1)} %add_bitcast_fusion, f32[2048,5]{0,1:T(8,128)S(1)} %bitcast.76), kind=kOutput, calls=%fused_computation.33 | convolution fusion | flops 251822080 | bytes 1261568 | tf_op jit(solution)/shard_map/lp,cp,rp->lcr/dot_general | solution.py:110
  38.4 1.6 %collective-permute-start.8 = (f32[32]{0:T(128)S(1)}, f32[32]{0:T(128)S(1)}, u32[]{:S(2)}, u32[]{:S(2)}) collective-permute-start(f32[32]{0:T(128)S(1)} %add.207), channel_id=1, source_target_pairs={{0,8},{4,12},{8,0},{12,4},{16,24},{20,28},{24,16},{28,20},{1,9},{5... | collective-permute-start | bytes 392 | tf_op jit(solution)/shard_map/ppermute | solution.py:19
  40.0 2.1 %collective-permute-done.8 = f32[32]{0:T(128)S(1)} collective-permute-done((f32[32]{0:T(128)S(1)}, f32[32]{0:T(128)S(1)}, u32[]{:S(2)}, u32[]{:S(2)}) %collective-permute-start.8) | collective-permute-done | bytes 160 | tf_op jit(solution)/shard_map/ppermute | solution.py:19
  42.0 1.5 %collective-permute-start.9 = (f32[32]{0:T(128)S(1)}, f32[32]{0:T(128)S(1)}, u32[]{:S(2)}, u32[]{:S(2)}) collective-permute-start(f32[32]{0:T(128)S(1)} %add.210), channel_id=1, source_target_pairs={{0,16},{4,20},{8,24},{12,28},{16,0},{20,4},{24,8},{28,12},{1,17},{... | collective-permute-start | bytes 392 | tf_op jit(solution)/shard_map/ppermute | solution.py:19
  43.5 2.0 %collective-permute-done.9 = f32[32]{0:T(128)S(1)} collective-permute-done((f32[32]{0:T(128)S(1)}, f32[32]{0:T(128)S(1)}, u32[]{:S(2)}, u32[]{:S(2)}) %collective-permute-start.9) | collective-permute-done | bytes 160 | tf_op jit(solution)/shard_map/ppermute | solution.py:19
  46.5 1.8 %fusion.24 = f32[2,48,512]{2,1,0:T(8,128)S(1)} fusion(s32[2,512]{1,0:T(2,128)S(1)} %get-tuple-element.188, bf16[16,2048]{1,0:T(8,128)(2,1)S(1)} %get-tuple-element.171, bf16[16,2048]{1,0:T(8,128)(2,1)S(1)} %get-tuple-element.172, bf16[16,2048]{1,0:T(8,128)(2,1)S(1)} %get-tuple-element.170), kind=kOutput, calls=%fused_computation.31 | convolution fusion | flops 204013568 | bytes 397312 | tf_op jit(solution)/shard_map/cp,gip->gci/dot_general | solution.py:49
  48.4 1.8 %collective-permute-done.10 = f32[6,16,128]{2,1,0:T(8,128)S(1)} collective-permute-done((f32[6,16,128]{2,1,0:T(8,128)S(1)}, f32[6,16,128]{2,1,0:T(8,128)S(1)}, u32[]{:S(2)}, u32[]{:S(2)}) %collective-permute-start.10) | collective-permute-done | bytes 49184 | tf_op jit(solution)/shard_map/ppermute | solution.py:19
  50.1 1.2 %collective-permute-start.11 = (f32[5,16,128]{2,1,0:T(8,128)S(1)}, f32[5,16,128]{2,1,0:T(8,128)S(1)}, u32[]{:S(2)}, u32[]{:S(2)}) collective-permute-start(f32[5,16,128]{2,1,0:T(8,128)S(1)} %slice.209), channel_id=1, source_target_pairs={{0,2},{1,3},{2,0},{3,1},{4,6},{5,7},{6,4},{7,5},{8,10},{9,11},{10,... | collective-permute-start | bytes 122888 | tf_op jit(solution)/shard_map/ppermute | solution.py:19
  51.4 1.8 %fusion.25 = f32[2,48,512]{2,1,0:T(8,128)S(1)} fusion(s32[2,512]{1,0:T(2,128)S(1)} %get-tuple-element.187, bf16[16,2048]{1,0:T(8,128)(2,1)S(1)} %get-tuple-element.168, bf16[16,2048]{1,0:T(8,128)(2,1)S(1)} %get-tuple-element.169, bf16[16,2048]{1,0:T(8,128)(2,1)S(1)} %get-tuple-element.167), kind=kOutput, calls=%fused_computation.32 | convolution fusion | flops 204013568 | bytes 397312 | tf_op jit(solution)/shard_map/cp,gip->gci/dot_general | solution.py:49
  53.2 2.2 %collective-permute-done.11 = f32[5,16,128]{2,1,0:T(8,128)S(1)} collective-permute-done((f32[5,16,128]{2,1,0:T(8,128)S(1)}, f32[5,16,128]{2,1,0:T(8,128)S(1)}, u32[]{:S(2)}, u32[]{:S(2)}) %collective-permute-start.11) | collective-permute-done | bytes 40992 | tf_op jit(solution)/shard_map/ppermute | solution.py:19
  55.6 1.2 %collective-permute-done.12 = f32[4,16,128]{2,1,0:T(8,128)S(1)} collective-permute-done((f32[4,16,128]{2,1,0:T(8,128)S(1)}, f32[4,16,128]{2,1,0:T(8,128)S(1)}, u32[]{:S(2)}, u32[]{:S(2)}) %collective-permute-start.12) | collective-permute-done | bytes 32800 | tf_op jit(solution)/shard_map/ppermute | solution.py:19
  56.8 1.6 %collective-permute-start.13 = (f32[3,16,128]{2,1,0:T(8,128)S(1)}, f32[3,16,128]{2,1,0:T(8,128)S(1)}, u32[]{:S(2)}, u32[]{:S(2)}) collective-permute-start(f32[3,16,128]{2,1,0:T(8,128)S(1)} %slice.255), channel_id=1, source_target_pairs={{0,8},{4,12},{8,0},{12,4},{16,24},{20,28},{24,16},{28,20},{1,9},{5... | collective-permute-start | bytes 73736 | tf_op jit(solution)/shard_map/ppermute | solution.py:19
  58.3 2.1 %fusion.100 = f32[4,16,512]{2,1,0:T(8,128)S(1)} fusion(f32[4,16,512]{2,1,0:T(8,128)S(1)} %constant_dynamic-update-slice_fusion.16, f32[4,512,512]{2,1,0:T(8,128)S(1)} %exponential_multiply_fusion), kind=kOutput, calls=%fused_computation.225 | convolution fusion | flops 100663296 | bytes 4456448 | tf_op jit(solution)/shard_map/gij,gcj->gci/dot_general | solution.py:40
  60.7 1.6 %collective-permute-start.14 = (f32[2,16,128]{2,1,0:T(8,128)S(1)}, f32[2,16,128]{2,1,0:T(8,128)S(1)}, u32[]{:S(2)}, u32[]{:S(2)}) collective-permute-start(f32[2,16,128]{2,1,0:T(8,128)S(1)} %slice.218), channel_id=1, source_target_pairs={{0,16},{4,20},{8,24},{12,28},{16,0},{20,4},{24,8},{28,12},{1,17},{... | collective-permute-start | bytes 49160 | tf_op jit(solution)/shard_map/ppermute | solution.py:19
  62.3 2.2 %collective-permute-done.14 = f32[2,16,128]{2,1,0:T(8,128)S(1)} collective-permute-done((f32[2,16,128]{2,1,0:T(8,128)S(1)}, f32[2,16,128]{2,1,0:T(8,128)S(1)}, u32[]{:S(2)}, u32[]{:S(2)}) %collective-permute-start.14) | collective-permute-done | bytes 16416 | tf_op jit(solution)/shard_map/ppermute | solution.py:19
  66.0 0.8 fusion.21
  67.2 1.8 %fusion.17 = f32[48,2048]{1,0:T(8,128)S(1)} fusion(s32[2,512]{1,0:T(2,128)S(1)} %get-tuple-element.188, bf16[2,16,512]{2,1,0:T(8,128)(2,1)S(1)} %get-tuple-element.165, bf16[2,16,512]{2,1,0:T(8,128)(2,1)S(1)} %get-tuple-element.166, bf16[2,16,512]{2,1,0:T(8,128)(2,1)S(1)} %get-tuple-element.164), kind=kOutput, calls=%fused_computation.24 | convolution fusion | flops 203718656 | bytes 495616 | tf_op jit(solution)/shard_map/gci,gip->cp/dot_general | solution.py:55
  69.0 1.5 %collective-permute-done.15 = f32[16]{0:T(128)S(1)} collective-permute-done((f32[16]{0:T(128)S(1)}, f32[16]{0:T(128)S(1)}, u32[]{:S(2)}, u32[]{:S(2)}) %collective-permute-start.15) | collective-permute-done | bytes 96 | tf_op jit(solution)/shard_map/ppermute | solution.py:19
  70.6 0.8 collective-permute-start.16
  71.4 1.8 %fusion.19 = f32[48,2048]{1,0:T(8,128)S(1)} fusion(s32[2,512]{1,0:T(2,128)S(1)} %get-tuple-element.187, bf16[2,16,512]{2,1,0:T(8,128)(2,1)S(1)} %get-tuple-element.162, bf16[2,16,512]{2,1,0:T(8,128)(2,1)S(1)} %get-tuple-element.163, bf16[2,16,512]{2,1,0:T(8,128)(2,1)S(1)} %get-tuple-element.161), kind=kOutput, calls=%fused_computation.26 | convolution fusion | flops 203718656 | bytes 495616 | tf_op jit(solution)/shard_map/gci,gip->cp/dot_general | solution.py:55
  73.2 1.8 %collective-permute-done.16 = f32[16]{0:T(128)S(1)} collective-permute-done((f32[16]{0:T(128)S(1)}, f32[16]{0:T(128)S(1)}, u32[]{:S(2)}, u32[]{:S(2)}) %collective-permute-start.16) | collective-permute-done | bytes 96 | tf_op jit(solution)/shard_map/ppermute | solution.py:19
  75.0 1.1 %collective-permute-done.17 = f32[16]{0:T(128)S(1)} collective-permute-done((f32[16]{0:T(128)S(1)}, f32[16]{0:T(128)S(1)}, u32[]{:S(2)}, u32[]{:S(2)}) %collective-permute-start.17) | collective-permute-done | bytes 96 | tf_op jit(solution)/shard_map/ppermute | solution.py:19
  76.1 1.5 %collective-permute-start.18 = (f32[16]{0:T(128)S(1)}, f32[16]{0:T(128)S(1)}, u32[]{:S(2)}, u32[]{:S(2)}) collective-permute-start(f32[16]{0:T(128)S(1)} %add.236), channel_id=1, source_target_pairs={{0,8},{4,12},{8,0},{12,4},{16,24},{20,28},{24,16},{28,20},{1,9},{5... | collective-permute-start | bytes 200 | tf_op jit(solution)/shard_map/ppermute | solution.py:19
  77.6 2.1 %collective-permute-done.18 = f32[16]{0:T(128)S(1)} collective-permute-done((f32[16]{0:T(128)S(1)}, f32[16]{0:T(128)S(1)}, u32[]{:S(2)}, u32[]{:S(2)}) %collective-permute-start.18) | collective-permute-done | bytes 96 | tf_op jit(solution)/shard_map/ppermute | solution.py:19
  79.7 1.5 %collective-permute-start.19 = (f32[16]{0:T(128)S(1)}, f32[16]{0:T(128)S(1)}, u32[]{:S(2)}, u32[]{:S(2)}) collective-permute-start(f32[16]{0:T(128)S(1)} %add.237), channel_id=1, source_target_pairs={{0,16},{4,20},{8,24},{12,28},{16,0},{20,4},{24,8},{28,12},{1,17},{... | collective-permute-start | bytes 200 | tf_op jit(solution)/shard_map/ppermute | solution.py:19
  81.2 2.0 %collective-permute-done.19 = f32[16]{0:T(128)S(1)} collective-permute-done((f32[16]{0:T(128)S(1)}, f32[16]{0:T(128)S(1)}, u32[]{:S(2)}, u32[]{:S(2)}) %collective-permute-start.19) | collective-permute-done | bytes 96 | tf_op jit(solution)/shard_map/ppermute | solution.py:19
  83.2 0.8 multiply_subtract_fusion
  (125 shorter events, 7.7 us)
Async XLA Ops:
  0.6 1.2 %copy-start = (f32[128,2048]{1,0:T(8,128)S(1)}, f32[128,2048]{1,0:T(8,128)}, u32[]{:S(2)}) copy-start(f32[128,2048]{1,0:T(8,128)} %param.13) | copy-start | bytes 3145732
  4.0 6.9 %collective-permute-start = (f32[5,16,128]{2,1,0:T(8,128)S(1)}, f32[5,16,128]{2,1,0:T(8,128)S(1)}, u32[]{:S(2)}, u32[]{:S(2)}) collective-permute-start(f32[5,16,128]{2,1,0:T(8,128)S(1)} %convolution_bitcast_fusion.1), channel_id=1, source_target_pairs={{0,1},{1,0},{2,3},{3,2},{4,5},{5,4},{6,7},{7,6},{8,9},{9,8},{10,11... | collective-permute-start | bytes 122888 | tf_op jit(solution)/shard_map/ppermute | solution.py:19
  11.0 6.3 %collective-permute-start.1 = (f32[4,16,128]{2,1,0:T(8,128)S(1)}, f32[4,16,128]{2,1,0:T(8,128)S(1)}, u32[]{:S(2)}, u32[]{:S(2)}) collective-permute-start(f32[4,16,128]{2,1,0:T(8,128)S(1)} %slice.234), channel_id=1, source_target_pairs={{0,2},{1,3},{2,0},{3,1},{4,6},{5,7},{6,4},{7,5},{8,10},{9,11},{10,... | collective-permute-start | bytes 98312 | tf_op jit(solution)/shard_map/ppermute | solution.py:19
  15.4 3.8 %copy-start.5 = (f32[8]{0:T(128)S(1)}, f32[8]{0:T(128)}, u32[]{:S(2)}) copy-start(f32[8]{0:T(128)} %param.10) | copy-start | bytes 100
  17.3 2.0 %collective-permute-start.2 = (f32[3,16,128]{2,1,0:T(8,128)S(1)}, f32[3,16,128]{2,1,0:T(8,128)S(1)}, u32[]{:S(2)}, u32[]{:S(2)}) collective-permute-start(f32[3,16,128]{2,1,0:T(8,128)S(1)} %slice.181), channel_id=1, source_target_pairs={{0,4},{4,0},{8,12},{12,8},{16,20},{20,16},{24,28},{28,24},{1,5},{5... | collective-permute-start | bytes 73736 | tf_op jit(solution)/shard_map/ppermute | solution.py:19
  19.5 3.8 %collective-permute-start.3 = (f32[2,16,128]{2,1,0:T(8,128)S(1)}, f32[2,16,128]{2,1,0:T(8,128)S(1)}, u32[]{:S(2)}, u32[]{:S(2)}) collective-permute-start(f32[2,16,128]{2,1,0:T(8,128)S(1)} %slice.190), channel_id=1, source_target_pairs={{0,8},{4,12},{8,0},{12,4},{16,24},{20,28},{24,16},{28,20},{1,9},{5... | collective-permute-start | bytes 49160 | tf_op jit(solution)/shard_map/ppermute | solution.py:19
  21.2 6.0 %copy-start.2 = (f32[5,128,128]{2,1,0:T(8,128)S(1)}, f32[5,128,128]{2,1,0:T(8,128)}, u32[]{:S(2)}) copy-start(f32[5,128,128]{2,1,0:T(8,128)} %param.15) | copy-start | bytes 983044
  22.8 5.4 %copy-start.3 = (f32[5,2048]{1,0:T(8,128)S(1)}, f32[5,2048]{1,0:T(8,128)}, u32[]{:S(2)}) copy-start(f32[5,2048]{1,0:T(8,128)} %param.14) | copy-start | bytes 122884
  22.8 6.1 %copy-start.1 = (f32[16,2048]{1,0:T(8,128)S(1)}, f32[16,2048]{1,0:T(8,128)}, u32[]{:S(2)}) copy-start(f32[16,2048]{1,0:T(8,128)} %param.12) | copy-start | bytes 393220
  22.8 6.1 %copy-start.4 = (f32[2048]{0:T(1024)S(1)}, f32[2048]{0:T(1024)}, u32[]{:S(2)}) copy-start(f32[2048]{0:T(1024)} %param.11) | copy-start | bytes 24580
  23.3 3.7 %collective-permute-start.4 = (f32[1,16,128]{2,1,0:T(8,128)S(1)}, f32[1,16,128]{2,1,0:T(8,128)S(1)}, u32[]{:S(2)}, u32[]{:S(2)}) collective-permute-start(f32[1,16,128]{2,1,0:T(8,128)S(1)} %slice.193), channel_id=1, source_target_pairs={{0,16},{4,20},{8,24},{12,28},{16,0},{20,4},{24,8},{28,12},{1,17},{... | collective-permute-start | bytes 24584 | tf_op jit(solution)/shard_map/ppermute | solution.py:19
  29.2 3.5 %collective-permute-start.5 = (f32[32]{0:T(128)S(1)}, f32[32]{0:T(128)S(1)}, u32[]{:S(2)}, u32[]{:S(2)}) collective-permute-start(f32[32]{0:T(128)S(1)} %pad_maximum_fusion.11), channel_id=1, source_target_pairs={{0,1},{1,0},{2,3},{3,2},{4,5},{5,4},{6,7},{7,6},{8,9},{9,8},{10,11... | collective-permute-start | bytes 392 | tf_op jit(solution)/shard_map/ppermute | solution.py:19
  32.7 4.4 %collective-permute-start.6 = (f32[32]{0:T(128)S(1)}, f32[32]{0:T(128)S(1)}, u32[]{:S(2)}, u32[]{:S(2)}) collective-permute-start(f32[32]{0:T(128)S(1)} %add.199), channel_id=1, source_target_pairs={{0,2},{1,3},{2,0},{3,1},{4,6},{5,7},{6,4},{7,5},{8,10},{9,11},{10,... | collective-permute-start | bytes 392 | tf_op jit(solution)/shard_map/ppermute | solution.py:19
  37.2 1.2 %collective-permute-start.7 = (f32[32]{0:T(128)S(1)}, f32[32]{0:T(128)S(1)}, u32[]{:S(2)}, u32[]{:S(2)}) collective-permute-start(f32[32]{0:T(128)S(1)} %add.203), channel_id=1, source_target_pairs={{0,4},{4,0},{8,12},{12,8},{16,20},{20,16},{24,28},{28,24},{1,5},{5... | collective-permute-start | bytes 392 | tf_op jit(solution)/shard_map/ppermute | solution.py:19
  38.4 3.6 %collective-permute-start.8 = (f32[32]{0:T(128)S(1)}, f32[32]{0:T(128)S(1)}, u32[]{:S(2)}, u32[]{:S(2)}) collective-permute-start(f32[32]{0:T(128)S(1)} %add.207), channel_id=1, source_target_pairs={{0,8},{4,12},{8,0},{12,4},{16,24},{20,28},{24,16},{28,20},{1,9},{5... | collective-permute-start | bytes 392 | tf_op jit(solution)/shard_map/ppermute | solution.py:19
  42.0 3.5 %collective-permute-start.9 = (f32[32]{0:T(128)S(1)}, f32[32]{0:T(128)S(1)}, u32[]{:S(2)}, u32[]{:S(2)}) collective-permute-start(f32[32]{0:T(128)S(1)} %add.210), channel_id=1, source_target_pairs={{0,16},{4,20},{8,24},{12,28},{16,0},{20,4},{24,8},{28,12},{1,17},{... | collective-permute-start | bytes 392 | tf_op jit(solution)/shard_map/ppermute | solution.py:19
  46.0 4.1 %collective-permute-start.10 = (f32[6,16,128]{2,1,0:T(8,128)S(1)}, f32[6,16,128]{2,1,0:T(8,128)S(1)}, u32[]{:S(2)}, u32[]{:S(2)}) collective-permute-start(f32[6,16,128]{2,1,0:T(8,128)S(1)} %pad_maximum_fusion.2), channel_id=1, source_target_pairs={{0,1},{1,0},{2,3},{3,2},{4,5},{5,4},{6,7},{7,6},{8,9},{9,8},{10,11... | collective-permute-start | bytes 147464 | tf_op jit(solution)/shard_map/ppermute | solution.py:19
  50.1 5.3 %collective-permute-start.11 = (f32[5,16,128]{2,1,0:T(8,128)S(1)}, f32[5,16,128]{2,1,0:T(8,128)S(1)}, u32[]{:S(2)}, u32[]{:S(2)}) collective-permute-start(f32[5,16,128]{2,1,0:T(8,128)S(1)} %slice.209), channel_id=1, source_target_pairs={{0,2},{1,3},{2,0},{3,1},{4,6},{5,7},{6,4},{7,5},{8,10},{9,11},{10,... | collective-permute-start | bytes 122888 | tf_op jit(solution)/shard_map/ppermute | solution.py:19
  55.5 1.3 %collective-permute-start.12 = (f32[4,16,128]{2,1,0:T(8,128)S(1)}, f32[4,16,128]{2,1,0:T(8,128)S(1)}, u32[]{:S(2)}, u32[]{:S(2)}) collective-permute-start(f32[4,16,128]{2,1,0:T(8,128)S(1)} %slice.214), channel_id=1, source_target_pairs={{0,4},{4,0},{8,12},{12,8},{16,20},{20,16},{24,28},{28,24},{1,5},{5... | collective-permute-start | bytes 98312 | tf_op jit(solution)/shard_map/ppermute | solution.py:19
  56.8 3.9 %collective-permute-start.13 = (f32[3,16,128]{2,1,0:T(8,128)S(1)}, f32[3,16,128]{2,1,0:T(8,128)S(1)}, u32[]{:S(2)}, u32[]{:S(2)}) collective-permute-start(f32[3,16,128]{2,1,0:T(8,128)S(1)} %slice.255), channel_id=1, source_target_pairs={{0,8},{4,12},{8,0},{12,4},{16,24},{20,28},{24,16},{28,20},{1,9},{5... | collective-permute-start | bytes 73736 | tf_op jit(solution)/shard_map/ppermute | solution.py:19
  60.7 3.8 %collective-permute-start.14 = (f32[2,16,128]{2,1,0:T(8,128)S(1)}, f32[2,16,128]{2,1,0:T(8,128)S(1)}, u32[]{:S(2)}, u32[]{:S(2)}) collective-permute-start(f32[2,16,128]{2,1,0:T(8,128)S(1)} %slice.218), channel_id=1, source_target_pairs={{0,16},{4,20},{8,24},{12,28},{16,0},{20,4},{24,8},{28,12},{1,17},{... | collective-permute-start | bytes 49160 | tf_op jit(solution)/shard_map/ppermute | solution.py:19
  66.9 3.6 %collective-permute-start.15 = (f32[16]{0:T(128)S(1)}, f32[16]{0:T(128)S(1)}, u32[]{:S(2)}, u32[]{:S(2)}) collective-permute-start(f32[16]{0:T(128)S(1)} %add.227), channel_id=1, source_target_pairs={{0,1},{1,0},{2,3},{3,2},{4,5},{5,4},{6,7},{7,6},{8,9},{9,8},{10,11... | collective-permute-start | bytes 200 | tf_op jit(solution)/shard_map/ppermute | solution.py:19
  70.6 4.4 %collective-permute-start.16 = (f32[16]{0:T(128)S(1)}, f32[16]{0:T(128)S(1)}, u32[]{:S(2)}, u32[]{:S(2)}) collective-permute-start(f32[16]{0:T(128)S(1)} %add.228), channel_id=1, source_target_pairs={{0,2},{1,3},{2,0},{3,1},{4,6},{5,7},{6,4},{7,5},{8,10},{9,11},{10,... | collective-permute-start | bytes 200 | tf_op jit(solution)/shard_map/ppermute | solution.py:19
  75.0 1.1 %collective-permute-start.17 = (f32[16]{0:T(128)S(1)}, f32[16]{0:T(128)S(1)}, u32[]{:S(2)}, u32[]{:S(2)}) collective-permute-start(f32[16]{0:T(128)S(1)} %add.232), channel_id=1, source_target_pairs={{0,4},{4,0},{8,12},{12,8},{16,20},{20,16},{24,28},{28,24},{1,5},{5... | collective-permute-start | bytes 200 | tf_op jit(solution)/shard_map/ppermute | solution.py:19
  76.1 3.5 %collective-permute-start.18 = (f32[16]{0:T(128)S(1)}, f32[16]{0:T(128)S(1)}, u32[]{:S(2)}, u32[]{:S(2)}) collective-permute-start(f32[16]{0:T(128)S(1)} %add.236), channel_id=1, source_target_pairs={{0,8},{4,12},{8,0},{12,4},{16,24},{20,28},{24,16},{28,20},{1,9},{5... | collective-permute-start | bytes 200 | tf_op jit(solution)/shard_map/ppermute | solution.py:19
  79.7 3.5 %collective-permute-start.19 = (f32[16]{0:T(128)S(1)}, f32[16]{0:T(128)S(1)}, u32[]{:S(2)}, u32[]{:S(2)}) collective-permute-start(f32[16]{0:T(128)S(1)} %add.237), channel_id=1, source_target_pairs={{0,16},{4,20},{8,24},{12,28},{16,0},{20,4},{24,8},{28,12},{1,17},{... | collective-permute-start | bytes 200 | tf_op jit(solution)/shard_map/ppermute | solution.py:19
